TPU v7x, 32 devices: a whole 2x2x4 slice. The times are simulated.
32 devices in a mesh: gx: 4 (over z), gy: 2 (over y), gz: 4 (over x, core).
Axes of the slice: x: 2, y: 2, z: 4, core: 2. Of those that a mesh axis runs over, the one named last changes fastest.
Arguments:
- residuals: bfloat16 [32, 16, 32, 512], P('gx', 'gy', 'gz'), may hold values from -6 to 6
- patch_box: int32 [3, 2, 512], replicated, may hold values from 0 to 32, as said below
- tile_pairs: int32 [4, 2], replicated, may hold values from 0 to 3, as said below
- inv_tiles: float32 [4, 128, 128], P('gx')
Outputs:
- mixed: bfloat16 [32, 16, 32, 512], P('gx', 'gy', 'gz')
Inputs may be any that keep to these rules, and one draw needn't show every extreme that they name: patch_box[a, 0, k] < patch_box[a, 1, k], the box spans at least a quarter and at most three quarters of dimension a's cells, and ends within the grid. `tile_pairs`: rows are distinct pairs of blocks, and every (b, b) is among them.
All inputs are finite; a program needn't handle non-finite values.
Results may differ from a plain program's by a relative error of at most 0.001.
Values sent between devices are 32-bit elements; how exact they have to be, the bound alone decides.
No kernel may reach another device: no remote copies, remote signals or barrier semaphores. Data moves between devices by JAX's collectives and lax.ppermute only.
A program may use at most 64 MiB of HBM per device.

v0:
```python
import jax
import jax.numpy as jnp
from jax import lax
from jax.sharding import PartitionSpec as P

LEVELS = 4
COARSE = 4


omega = 0.8
shift_sigma = 0.01


def with_halo(block, sides, width):
    for axis, dim in sides:
        count = lax.axis_size(axis)
        forward = [(i, i + 1) for i in range(count - 1)]
        forward.append((count - 1, 0))
        backward = [(target, source) for source, target in forward]
        low = lax.ppermute(
            lax.slice_in_dim(block, block.shape[dim] - width, None, axis=dim), axis, forward
        )
        high = lax.ppermute(lax.slice_in_dim(block, 0, width, axis=dim), axis, backward)
        block = jnp.concatenate([low, block, high], axis=dim)
    return block


def level_coeffs(level_id):
    coupling = 0.5 / 4.0**level_id
    return (6.0 * coupling + shift_sigma, coupling)


def stencil(padded, level_id):
    center, coupling = level_coeffs(level_id)
    middle = padded[1:-1, 1:-1, 1:-1]
    beside = padded[2:, 1:-1, 1:-1] + padded[:-2, 1:-1, 1:-1]
    beside = beside + padded[1:-1, 2:, 1:-1] + padded[1:-1, :-2, 1:-1]
    beside = beside + padded[1:-1, 1:-1, 2:] + padded[1:-1, 1:-1, :-2]
    return center * middle - coupling * beside


def restrict(field):
    size_a, size_b, size_c, width = field.shape
    return field.reshape(size_a // 2, 2, size_b // 2, 2, size_c // 2, 2, width).mean(axis=(1, 3, 5))


def prolong(field):
    return jnp.repeat(jnp.repeat(jnp.repeat(field, 2, 0), 2, 1), 2, 2)


def dim_mask(box_part, offset, extent):
    cells = offset + jnp.arange(extent, dtype=jnp.int32)[:, None]
    return ((box_part[0][None, :] <= cells) & (cells < box_part[1][None, :])).astype(jnp.float32)


def body(residuals, patch_box, tile_pairs, inv_tiles):
    current = residuals.astype(jnp.float32)
    rhs_list = []
    corr_list = []
    pad_list = []
    for level_id in range(LEVELS - 1):
        center, coupling = level_coeffs(level_id)
        correct = omega * current / center
        padded = with_halo(correct, (("gx", 0), ("gy", 1), ("gz", 2)), 1)
        remain = current - stencil(padded, level_id)
        rhs_list.append(current)
        corr_list.append(correct)
        pad_list.append(padded)
        current = restrict(remain)
    top_level = LEVELS - 1
    center, coupling = level_coeffs(top_level)
    correct = omega * current / center
    for sweep_id in range(COARSE - 1):
        padded = with_halo(correct, (("gx", 0), ("gy", 1), ("gz", 2)), 1)
        correct = correct + omega * (current - stencil(padded, top_level)) / center
    for level_id in reversed(range(LEVELS - 1)):
        center, coupling = level_coeffs(level_id)
        updated = corr_list[level_id] + prolong(correct)
        padded = with_halo(updated, (("gx", 0), ("gy", 1), ("gz", 2)), 1)
        correct = updated + omega * (rhs_list[level_id] - stencil(padded, level_id)) / center
    size_a, size_b, size_c, orb_count = correct.shape
    mask_first = dim_mask(patch_box[0], lax.axis_index("gx") * size_a, size_a)
    mask_second = dim_mask(patch_box[1], lax.axis_index("gy") * size_b, size_b)
    mask_third = dim_mask(patch_box[2], lax.axis_index("gz") * size_c, size_c)
    precond = correct * (
        mask_first[:, None, None, :] * mask_second[None, :, None, :] * mask_third[None, None, :, :]
    )
    tile_edge = inv_tiles.shape[1]
    block_count = orb_count // tile_edge
    cell_count = size_a * size_b * size_c
    pre_rows = precond.reshape(cell_count, block_count, tile_edge)
    block_ids = jnp.arange(block_count, dtype=jnp.int32)
    start_val = jnp.zeros((cell_count, block_count, tile_edge), jnp.float32)
    total = start_val
    piece = lax.all_gather(inv_tiles, "gx", axis=0, tiled=True)
    number = piece.shape[0]
    for first in range(0, number, 8):
        tile_group = piece[first : first + 8]
        pair_group = tile_pairs[first : first + 8]
        picked = jnp.take(pre_rows, pair_group[:, 0], axis=1)
        product = jnp.einsum("cnk,nkj->cnj", picked, tile_group, precision=lax.Precision.HIGHEST)
        onehot = (pair_group[:, 1][:, None] == block_ids[None, :]).astype(jnp.float32)
        total = total + jnp.einsum("cnj,nb->cbj", product, onehot, precision=lax.Precision.HIGHEST)
    return total.reshape(size_a, size_b, size_c, orb_count).astype(jnp.bfloat16)


def solution(mesh):
    return jax.shard_map(
        body,
        mesh=mesh,
        in_specs=(P("gx", "gy", "gz", None), P(), P(), P("gx", None, None)),
        out_specs=P("gx", "gy", "gz", None),
        check_vma=False,
    )
```

profile of v0, /device:TPU:0, one launch (start us, length us, event | category | flops | bytes accessed | tf_op | source)
XLA Modules:
  0.0 177.9 jit_solution(16156711588720346992)
XLA Ops:
  1.2 5.1 %collective-permute-start = (f32[1,8,8,512]{3,2,1,0:T(8,128)S(1)}, f32[1,8,8,512]{3,2,1,0:T(8,128)S(1)}, u32[]{:S(2)}, u32[]{:S(2)}) collective-permute-start(f32[1,8,8,512]{3,2,1,0:T(8,128)S(1)} %get-tuple-element.16), channel_id=1, source_target_pairs={{8,0},{16,8},{24,16},{0,24},{9,1},{17,9},{25,17},{1,25},{10,2},{18... | collective-permute-start | bytes 393224 | tf_op jit(solution)/shard_map/ppermute | solution.py:23
  6.3 3.9 %collective-permute-done = f32[1,8,8,512]{3,2,1,0:T(8,128)S(1)} collective-permute-done((f32[1,8,8,512]{3,2,1,0:T(8,128)S(1)}, f32[1,8,8,512]{3,2,1,0:T(8,128)S(1)}, u32[]{:S(2)}, u32[]{:S(2)}) %collective-permute-start) | collective-permute-done | bytes 131104 | tf_op jit(solution)/shard_map/ppermute | solution.py:23
  10.2 2.9 %collective-permute-done.1 = f32[1,8,8,512]{3,2,1,0:T(8,128)S(1)} collective-permute-done((f32[1,8,8,512]{3,2,1,0:T(8,128)S(1)}, f32[1,8,8,512]{3,2,1,0:T(8,128)S(1)}, u32[]{:S(2)}, u32[]{:S(2)}) %collective-permute-start.1) | collective-permute-done | bytes 131104 | tf_op jit(solution)/shard_map/ppermute | solution.py:20
  13.1 1.6 collective-permute-start.2
  15.2 4.2 %collective-permute-done.2 = f32[10,1,8,512]{3,2,1,0:T(8,128)S(1)} collective-permute-done((f32[10,1,8,512]{3,2,1,0:T(8,128)S(1)}, f32[10,1,8,512]{3,2,1,0:T(8,128)S(1)}, u32[]{:S(2)}, u32[]{:S(2)}) %collective-permute-start.2) | collective-permute-done | bytes 163872 | tf_op jit(solution)/shard_map/ppermute | solution.py:23
  19.5 1.8 collective-permute-done.3
  22.2 6.5 %collective-permute-done.4 = f32[10,10,1,512]{3,1,2,0:T(8,128)S(1)} collective-permute-done((f32[10,10,1,512]{3,1,2,0:T(8,128)S(1)}, f32[10,10,1,512]{3,1,2,0:T(8,128)S(1)}, u32[]{:S(2)}, u32[]{:S(2)}) %collective-permute-start.4) | collective-permute-done | bytes 204832 | tf_op jit(solution)/shard_map/ppermute | solution.py:23
  28.9 2.8 %collective-permute-done.5 = f32[10,10,1,512]{3,1,2,0:T(8,128)S(1)} collective-permute-done((f32[10,10,1,512]{3,1,2,0:T(8,128)S(1)}, f32[10,10,1,512]{3,1,2,0:T(8,128)S(1)}, u32[]{:S(2)}, u32[]{:S(2)}) %collective-permute-start.5) | collective-permute-done | bytes 204832 | tf_op jit(solution)/shard_map/ppermute | solution.py:20
  36.3 1.9 %collective-permute-done.6 = f32[1,4,4,512]{3,2,1,0:T(4,128)S(1)} collective-permute-done((f32[1,4,4,512]{3,2,1,0:T(4,128)S(1)}, f32[1,4,4,512]{3,2,1,0:T(4,128)S(1)}, u32[]{:S(2)}, u32[]{:S(2)}) %collective-permute-start.6) | collective-permute-done | bytes 32800 | tf_op jit(solution)/shard_map/ppermute | solution.py:23
  38.2 2.7 %collective-permute-done.7 = f32[1,4,4,512]{3,2,1,0:T(4,128)S(1)} collective-permute-done((f32[1,4,4,512]{3,2,1,0:T(4,128)S(1)}, f32[1,4,4,512]{3,2,1,0:T(4,128)S(1)}, u32[]{:S(2)}, u32[]{:S(2)}) %collective-permute-start.7) | collective-permute-done | bytes 32800 | tf_op jit(solution)/shard_map/ppermute | solution.py:20
  40.9 1.6 collective-permute-start.8
  43.0 2.1 %collective-permute-done.8 = f32[6,1,4,512]{3,2,1,0:T(4,128)S(1)} collective-permute-done((f32[6,1,4,512]{3,2,1,0:T(4,128)S(1)}, f32[6,1,4,512]{3,2,1,0:T(4,128)S(1)}, u32[]{:S(2)}, u32[]{:S(2)}) %collective-permute-start.8) | collective-permute-done | bytes 49184 | tf_op jit(solution)/shard_map/ppermute | solution.py:23
  47.3 2.1 %collective-permute-done.10 = f32[6,6,1,512]{3,2,1,0:T(1,128)S(1)} collective-permute-done((f32[6,6,1,512]{3,2,1,0:T(1,128)S(1)}, f32[6,6,1,512]{3,2,1,0:T(1,128)S(1)}, u32[]{:S(2)}, u32[]{:S(2)}) %collective-permute-start.10) | collective-permute-done | bytes 73760 | tf_op jit(solution)/shard_map/ppermute | solution.py:23
  51.5 1.7 collective-permute-start.13
  53.1 1.6 collective-permute-done.12
  54.8 2.1 %collective-permute-done.13 = f32[1,2,2,512]{3,2,1,0:T(2,128)S(1)} collective-permute-done((f32[1,2,2,512]{3,2,1,0:T(2,128)S(1)}, f32[1,2,2,512]{3,2,1,0:T(2,128)S(1)}, u32[]{:S(2)}, u32[]{:S(2)}) %collective-permute-start.13) | collective-permute-done | bytes 8224 | tf_op jit(solution)/shard_map/ppermute | solution.py:20
  59.0 1.7 collective-permute-done.14
  63.0 1.9 %collective-permute-done.17 = f32[4,4,1,512]{3,2,1,0:T(1,128)S(1)} collective-permute-done((f32[4,4,1,512]{3,2,1,0:T(1,128)S(1)}, f32[4,4,1,512]{3,2,1,0:T(1,128)S(1)}, u32[]{:S(2)}, u32[]{:S(2)}) %collective-permute-start.17) | collective-permute-done | bytes 32800 | tf_op jit(solution)/shard_map/ppermute | solution.py:20
  65.2 2.0 %collective-permute-start.19 = (f32[1,1,1,512]{3,2,1,0:T(1,128)S(1)}, f32[1,1,1,512]{3,2,1,0:T(1,128)S(1)}, u32[]{:S(2)}, u32[]{:S(2)}) collective-permute-start(f32[1,1,1,512]{3,2,1,0:T(1,128)S(1)} %bitcast.43), channel_id=1, source_target_pairs={{0,8},{8,16},{16,24},{24,0},{1,9},{9,17},{17,25},{25,1},{2,10},{10... | collective-permute-start | bytes 6152 | tf_op jit(solution)/shard_map/ppermute | solution.py:20
  68.7 1.9 %collective-permute-done.19 = f32[1,1,1,512]{3,2,1,0:T(1,128)S(1)} collective-permute-done((f32[1,1,1,512]{3,2,1,0:T(1,128)S(1)}, f32[1,1,1,512]{3,2,1,0:T(1,128)S(1)}, u32[]{:S(2)}, u32[]{:S(2)}) %collective-permute-start.19) | collective-permute-done | bytes 2080 | tf_op jit(solution)/shard_map/ppermute | solution.py:20
  70.6 1.6 collective-permute-start.20
  72.7 1.6 collective-permute-done.20
  77.3 1.8 %collective-permute-done.23 = f32[3,3,1,512]{3,2,1,0:T(1,128)S(1)} collective-permute-done((f32[3,3,1,512]{3,2,1,0:T(1,128)S(1)}, f32[3,3,1,512]{3,2,1,0:T(1,128)S(1)}, u32[]{:S(2)}, u32[]{:S(2)}) %collective-permute-start.23) | collective-permute-done | bytes 18464 | tf_op jit(solution)/shard_map/ppermute | solution.py:20
  79.2 2.0 %collective-permute-start.25 = (f32[1,1,1,512]{3,2,1,0:T(1,128)S(1)}, f32[1,1,1,512]{3,2,1,0:T(1,128)S(1)}, u32[]{:S(2)}, u32[]{:S(2)}) collective-permute-start(f32[1,1,1,512]{3,2,1,0:T(1,128)S(1)} %multiply_add_fusion.3), channel_id=1, source_target_pairs={{0,8},{8,16},{16,24},{24,0},{1,9},{9,17},{17,25},{25,1},{2,10},{10... | collective-permute-start | bytes 6152 | tf_op jit(solution)/shard_map/ppermute | solution.py:20
  82.7 1.9 %collective-permute-done.25 = f32[1,1,1,512]{3,2,1,0:T(1,128)S(1)} collective-permute-done((f32[1,1,1,512]{3,2,1,0:T(1,128)S(1)}, f32[1,1,1,512]{3,2,1,0:T(1,128)S(1)}, u32[]{:S(2)}, u32[]{:S(2)}) %collective-permute-start.25) | collective-permute-done | bytes 2080 | tf_op jit(solution)/shard_map/ppermute | solution.py:20
  86.7 1.6 collective-permute-done.26
  90.4 1.8 %collective-permute-done.29 = f32[3,3,1,512]{3,2,1,0:T(1,128)S(1)} collective-permute-done((f32[3,3,1,512]{3,2,1,0:T(1,128)S(1)}, f32[3,3,1,512]{3,2,1,0:T(1,128)S(1)}, u32[]{:S(2)}, u32[]{:S(2)}) %collective-permute-start.29) | collective-permute-done | bytes 18464 | tf_op jit(solution)/shard_map/ppermute | solution.py:20
  92.2 2.0 %collective-permute-start.31 = (f32[1,1,1,512]{3,2,1,0:T(1,128)S(1)}, f32[1,1,1,512]{3,2,1,0:T(1,128)S(1)}, u32[]{:S(2)}, u32[]{:S(2)}) collective-permute-start(f32[1,1,1,512]{3,2,1,0:T(1,128)S(1)} %multiply_add_fusion.2), channel_id=1, source_target_pairs={{0,8},{8,16},{16,24},{24,0},{1,9},{9,17},{17,25},{25,1},{2,10},{10... | collective-permute-start | bytes 6152 | tf_op jit(solution)/shard_map/ppermute | solution.py:20
  95.8 1.9 %collective-permute-done.31 = f32[1,1,1,512]{3,2,1,0:T(1,128)S(1)} collective-permute-done((f32[1,1,1,512]{3,2,1,0:T(1,128)S(1)}, f32[1,1,1,512]{3,2,1,0:T(1,128)S(1)}, u32[]{:S(2)}, u32[]{:S(2)}) %collective-permute-start.31) | collective-permute-done | bytes 2080 | tf_op jit(solution)/shard_map/ppermute | solution.py:20
  97.7 1.6 collective-permute-start.32
  99.8 1.6 collective-permute-done.32
  104.4 1.8 %collective-permute-done.35 = f32[3,3,1,512]{3,2,1,0:T(1,128)S(1)} collective-permute-done((f32[3,3,1,512]{3,2,1,0:T(1,128)S(1)}, f32[3,3,1,512]{3,2,1,0:T(1,128)S(1)}, u32[]{:S(2)}, u32[]{:S(2)}) %collective-permute-start.35) | collective-permute-done | bytes 18464 | tf_op jit(solution)/shard_map/ppermute | solution.py:20
  106.3 2.0 %collective-permute-start.37 = (f32[1,2,2,512]{3,2,1,0:T(2,128)S(1)}, f32[1,2,2,512]{3,2,1,0:T(2,128)S(1)}, u32[]{:S(2)}, u32[]{:S(2)}) collective-permute-start(f32[1,2,2,512]{3,2,1,0:T(2,128)S(1)} %get-tuple-element.37), channel_id=1, source_target_pairs={{0,8},{8,16},{16,24},{24,0},{1,9},{9,17},{17,25},{25,1},{2,10},{10... | collective-permute-start | bytes 24584 | tf_op jit(solution)/shard_map/ppermute | solution.py:20
  108.3 1.6 collective-permute-done.36
  110.0 1.9 %collective-permute-done.37 = f32[1,2,2,512]{3,2,1,0:T(2,128)S(1)} collective-permute-done((f32[1,2,2,512]{3,2,1,0:T(2,128)S(1)}, f32[1,2,2,512]{3,2,1,0:T(2,128)S(1)}, u32[]{:S(2)}, u32[]{:S(2)}) %collective-permute-start.37) | collective-permute-done | bytes 8224 | tf_op jit(solution)/shard_map/ppermute | solution.py:20
  114.0 1.7 collective-permute-done.38
  117.9 1.8 %collective-permute-done.41 = f32[4,4,1,512]{3,2,1,0:T(1,128)S(1)} collective-permute-done((f32[4,4,1,512]{3,2,1,0:T(1,128)S(1)}, f32[4,4,1,512]{3,2,1,0:T(1,128)S(1)}, u32[]{:S(2)}, u32[]{:S(2)}) %collective-permute-start.41) | collective-permute-done | bytes 32800 | tf_op jit(solution)/shard_map/ppermute | solution.py:20
  120.2 2.0 %collective-permute-start.43 = (f32[1,4,4,512]{3,2,1,0:T(4,128)S(1)}, f32[1,4,4,512]{3,2,1,0:T(4,128)S(1)}, u32[]{:S(2)}, u32[]{:S(2)}) collective-permute-start(f32[1,4,4,512]{3,2,1,0:T(4,128)S(1)} %get-tuple-element.25), channel_id=1, source_target_pairs={{0,8},{8,16},{16,24},{24,0},{1,9},{9,17},{17,25},{25,1},{2,10},{10... | collective-permute-start | bytes 98312 | tf_op jit(solution)/shard_map/ppermute | solution.py:20
  122.2 1.9 %collective-permute-done.42 = f32[1,4,4,512]{3,2,1,0:T(4,128)S(1)} collective-permute-done((f32[1,4,4,512]{3,2,1,0:T(4,128)S(1)}, f32[1,4,4,512]{3,2,1,0:T(4,128)S(1)}, u32[]{:S(2)}, u32[]{:S(2)}) %collective-permute-start.42) | collective-permute-done | bytes 32800 | tf_op jit(solution)/shard_map/ppermute | solution.py:23
  124.1 1.9 %collective-permute-done.43 = f32[1,4,4,512]{3,2,1,0:T(4,128)S(1)} collective-permute-done((f32[1,4,4,512]{3,2,1,0:T(4,128)S(1)}, f32[1,4,4,512]{3,2,1,0:T(4,128)S(1)}, u32[]{:S(2)}, u32[]{:S(2)}) %collective-permute-start.43) | collective-permute-done | bytes 32800 | tf_op jit(solution)/shard_map/ppermute | solution.py:20
  126.0 1.6 collective-permute-start.44
  128.1 2.1 %collective-permute-done.44 = f32[6,1,4,512]{3,2,1,0:T(4,128)S(1)} collective-permute-done((f32[6,1,4,512]{3,2,1,0:T(4,128)S(1)}, f32[6,1,4,512]{3,2,1,0:T(4,128)S(1)}, u32[]{:S(2)}, u32[]{:S(2)}) %collective-permute-start.44) | collective-permute-done | bytes 49184 | tf_op jit(solution)/shard_map/ppermute | solution.py:23
  133.8 2.3 %collective-permute-done.47 = f32[6,6,1,512]{3,2,1,0:T(1,128)S(1)} collective-permute-done((f32[6,6,1,512]{3,2,1,0:T(1,128)S(1)}, f32[6,6,1,512]{3,2,1,0:T(1,128)S(1)}, u32[]{:S(2)}, u32[]{:S(2)}) %collective-permute-start.47) | collective-permute-done | bytes 73760 | tf_op jit(solution)/shard_map/ppermute | solution.py:20
  138.2 1.8 %collective-permute-start.49 = (f32[1,8,8,512]{3,2,1,0:T(8,128)S(1)}, f32[1,8,8,512]{3,2,1,0:T(8,128)S(1)}, u32[]{:S(2)}, u32[]{:S(2)}) collective-permute-start(f32[1,8,8,512]{3,2,1,0:T(8,128)S(1)} %get-tuple-element.13), channel_id=1, source_target_pairs={{0,8},{8,16},{16,24},{24,0},{1,9},{9,17},{17,25},{25,1},{2,10},{10... | collective-permute-start | bytes 393224 | tf_op jit(solution)/shard_map/ppermute | solution.py:20
  140.0 5.9 %collective-permute-done.48 = f32[1,8,8,512]{3,2,1,0:T(8,128)S(1)} collective-permute-done((f32[1,8,8,512]{3,2,1,0:T(8,128)S(1)}, f32[1,8,8,512]{3,2,1,0:T(8,128)S(1)}, u32[]{:S(2)}, u32[]{:S(2)}) %collective-permute-start.48) | collective-permute-done | bytes 131104 | tf_op jit(solution)/shard_map/ppermute | solution.py:23
  148.1 13.8 %all_gather.3 = f32[4,128,128]{2,1,0:T(8,128)S(1)} all-gather(f32[1,128,128]{2,1,0:T(8,128)S(1)} %copy-done.1), channel_id=1, replica_groups=mesh['gx'=4,'gy'=2,'gz'=4] {'gx'}, dimensions={0}, use_global_device_ids=true | all-gather | bytes 327680 | tf_op jit(solution)/shard_map/all_gather | solution.py:95
  163.0 7.3 %collective-permute-done.52 = f32[10,10,1,512]{3,1,2,0:T(8,128)S(1)} collective-permute-done((f32[10,10,1,512]{3,1,2,0:T(8,128)S(1)}, f32[10,10,1,512]{3,1,2,0:T(8,128)S(1)}, u32[]{:S(2)}, u32[]{:S(2)}) %collective-permute-start.52) | collective-permute-done | bytes 204832 | tf_op jit(solution)/shard_map/ppermute | solution.py:23
  175.2 1.7 fusion
  (149 shorter events, 53.2 us)
Async XLA Ops:
  1.2 9.0 %collective-permute-start = (f32[1,8,8,512]{3,2,1,0:T(8,128)S(1)}, f32[1,8,8,512]{3,2,1,0:T(8,128)S(1)}, u32[]{:S(2)}, u32[]{:S(2)}) collective-permute-start(f32[1,8,8,512]{3,2,1,0:T(8,128)S(1)} %get-tuple-element.16), channel_id=1, source_target_pairs={{8,0},{16,8},{24,16},{0,24},{9,1},{17,9},{25,17},{1,25},{10,2},{18... | collective-permute-start | bytes 393224 | tf_op jit(solution)/shard_map/ppermute | solution.py:23
  6.3 6.8 %collective-permute-start.1 = (f32[1,8,8,512]{3,2,1,0:T(8,128)S(1)}, f32[1,8,8,512]{3,2,1,0:T(8,128)S(1)}, u32[]{:S(2)}, u32[]{:S(2)}) collective-permute-start(f32[1,8,8,512]{3,2,1,0:T(8,128)S(1)} %get-tuple-element.15), channel_id=1, source_target_pairs={{0,8},{8,16},{16,24},{24,0},{1,9},{9,17},{17,25},{25,1},{2,10},{10... | collective-permute-start | bytes 393224 | tf_op jit(solution)/shard_map/ppermute | solution.py:20
  13.1 6.3 %collective-permute-start.2 = (f32[10,1,8,512]{3,2,1,0:T(8,128)S(1)}, f32[10,1,8,512]{3,2,1,0:T(8,128)S(1)}, u32[]{:S(2)}, u32[]{:S(2)}) collective-permute-start(f32[10,1,8,512]{3,2,1,0:T(8,128)S(1)} %get-tuple-element.12), channel_id=1, source_target_pairs={{4,0},{0,4},{5,1},{1,5},{6,2},{2,6},{7,3},{3,7},{12,8},{8,12},{13,... | collective-permute-start | bytes 491528 | tf_op jit(solution)/shard_map/ppermute | solution.py:23
  14.7 6.5 %collective-permute-start.3 = (f32[10,1,8,512]{3,2,1,0:T(8,128)S(1)}, f32[10,1,8,512]{3,2,1,0:T(8,128)S(1)}, u32[]{:S(2)}, u32[]{:S(2)}) collective-permute-start(f32[10,1,8,512]{3,2,1,0:T(8,128)S(1)} %get-tuple-element.11), channel_id=1, source_target_pairs={{0,4},{4,0},{1,5},{5,1},{2,6},{6,2},{3,7},{7,3},{8,12},{12,8},{9,1... | collective-permute-start | bytes 491528 | tf_op jit(solution)/shard_map/ppermute | solution.py:20
  21.5 7.1 %collective-permute-start.4 = (f32[10,10,1,512]{3,1,2,0:T(8,128)S(1)}, f32[10,10,1,512]{3,1,2,0:T(8,128)S(1)}, u32[]{:S(2)}, u32[]{:S(2)}) collective-permute-start(f32[10,10,1,512]{3,1,2,0:T(8,128)S(1)} %copy.11), channel_id=1, source_target_pairs={{1,0},{2,1},{3,2},{0,3},{5,4},{6,5},{7,6},{4,7},{9,8},{10,9},{11,1... | collective-permute-start | bytes 614408 | tf_op jit(solution)/shard_map/ppermute | solution.py:23
  21.6 10.0 %collective-permute-start.5 = (f32[10,10,1,512]{3,1,2,0:T(8,128)S(1)}, f32[10,10,1,512]{3,1,2,0:T(8,128)S(1)}, u32[]{:S(2)}, u32[]{:S(2)}) collective-permute-start(f32[10,10,1,512]{3,1,2,0:T(8,128)S(1)} %copy.13), channel_id=1, source_target_pairs={{0,1},{1,2},{2,3},{3,0},{4,5},{5,6},{6,7},{7,4},{8,9},{9,10},{10,1... | collective-permute-start | bytes 614408 | tf_op jit(solution)/shard_map/ppermute | solution.py:20
  34.2 4.0 %collective-permute-start.6 = (f32[1,4,4,512]{3,2,1,0:T(4,128)S(1)}, f32[1,4,4,512]{3,2,1,0:T(4,128)S(1)}, u32[]{:S(2)}, u32[]{:S(2)}) collective-permute-start(f32[1,4,4,512]{3,2,1,0:T(4,128)S(1)} %get-tuple-element.28), channel_id=1, source_target_pairs={{8,0},{16,8},{24,16},{0,24},{9,1},{17,9},{25,17},{1,25},{10,2},{18... | collective-permute-start | bytes 98312 | tf_op jit(solution)/shard_map/ppermute | solution.py:23
  35.2 5.7 %collective-permute-start.7 = (f32[1,4,4,512]{3,2,1,0:T(4,128)S(1)}, f32[1,4,4,512]{3,2,1,0:T(4,128)S(1)}, u32[]{:S(2)}, u32[]{:S(2)}) collective-permute-start(f32[1,4,4,512]{3,2,1,0:T(4,128)S(1)} %get-tuple-element.27), channel_id=1, source_target_pairs={{0,8},{8,16},{16,24},{24,0},{1,9},{9,17},{17,25},{25,1},{2,10},{10... | collective-permute-start | bytes 98312 | tf_op jit(solution)/shard_map/ppermute | solution.py:20
  40.9 4.2 %collective-permute-start.8 = (f32[6,1,4,512]{3,2,1,0:T(4,128)S(1)}, f32[6,1,4,512]{3,2,1,0:T(4,128)S(1)}, u32[]{:S(2)}, u32[]{:S(2)}) collective-permute-start(f32[6,1,4,512]{3,2,1,0:T(4,128)S(1)} %get-tuple-element.24), channel_id=1, source_target_pairs={{4,0},{0,4},{5,1},{1,5},{6,2},{2,6},{7,3},{3,7},{12,8},{8,12},{13,... | collective-permute-start | bytes 147464 | tf_op jit(solution)/shard_map/ppermute | solution.py:23
  42.5 4.1 %collective-permute-start.9 = (f32[6,1,4,512]{3,2,1,0:T(4,128)S(1)}, f32[6,1,4,512]{3,2,1,0:T(4,128)S(1)}, u32[]{:S(2)}, u32[]{:S(2)}) collective-permute-start(f32[6,1,4,512]{3,2,1,0:T(4,128)S(1)} %get-tuple-element.23), channel_id=1, source_target_pairs={{0,4},{4,0},{1,5},{5,1},{2,6},{6,2},{3,7},{7,3},{8,12},{12,8},{9,1... | collective-permute-start | bytes 147464 | tf_op jit(solution)/shard_map/ppermute | solution.py:20
  46.7 2.7 %collective-permute-start.10 = (f32[6,6,1,512]{3,2,1,0:T(1,128)S(1)}, f32[6,6,1,512]{3,2,1,0:T(1,128)S(1)}, u32[]{:S(2)}, u32[]{:S(2)}) collective-permute-start(f32[6,6,1,512]{3,2,1,0:T(1,128)S(1)} %get-tuple-element.19), channel_id=1, source_target_pairs={{1,0},{2,1},{3,2},{0,3},{5,4},{6,5},{7,6},{4,7},{9,8},{10,9},{11,1... | collective-permute-start | bytes 221192 | tf_op jit(solution)/shard_map/ppermute | solution.py:23
  46.8 3.8 %collective-permute-start.11 = (f32[6,6,1,512]{3,2,1,0:T(1,128)S(1)}, f32[6,6,1,512]{3,2,1,0:T(1,128)S(1)}, u32[]{:S(2)}, u32[]{:S(2)}) collective-permute-start(f32[6,6,1,512]{3,2,1,0:T(1,128)S(1)} %get-tuple-element.20), channel_id=1, source_target_pairs={{0,1},{1,2},{2,3},{3,0},{4,5},{5,6},{6,7},{7,4},{8,9},{9,10},{10,1... | collective-permute-start | bytes 221192 | tf_op jit(solution)/shard_map/ppermute | solution.py:20
  51.0 3.7 %collective-permute-start.12 = (f32[1,2,2,512]{3,2,1,0:T(2,128)S(1)}, f32[1,2,2,512]{3,2,1,0:T(2,128)S(1)}, u32[]{:S(2)}, u32[]{:S(2)}) collective-permute-start(f32[1,2,2,512]{3,2,1,0:T(2,128)S(1)} %get-tuple-element.40), channel_id=1, source_target_pairs={{8,0},{16,8},{24,16},{0,24},{9,1},{17,9},{25,17},{1,25},{10,2},{18... | collective-permute-start | bytes 24584 | tf_op jit(solution)/shard_map/ppermute | solution.py:23
  51.5 5.4 %collective-permute-start.13 = (f32[1,2,2,512]{3,2,1,0:T(2,128)S(1)}, f32[1,2,2,512]{3,2,1,0:T(2,128)S(1)}, u32[]{:S(2)}, u32[]{:S(2)}) collective-permute-start(f32[1,2,2,512]{3,2,1,0:T(2,128)S(1)} %get-tuple-element.39), channel_id=1, source_target_pairs={{0,8},{8,16},{16,24},{24,0},{1,9},{9,17},{17,25},{25,1},{2,10},{10... | collective-permute-start | bytes 24584 | tf_op jit(solution)/shard_map/ppermute | solution.py:20
  56.9 3.8 %collective-permute-start.14 = (f32[4,1,2,512]{3,2,1,0:T(2,128)S(1)}, f32[4,1,2,512]{3,2,1,0:T(2,128)S(1)}, u32[]{:S(2)}, u32[]{:S(2)}) collective-permute-start(f32[4,1,2,512]{3,2,1,0:T(2,128)S(1)} %get-tuple-element.36), channel_id=1, source_target_pairs={{4,0},{0,4},{5,1},{1,5},{6,2},{2,6},{7,3},{3,7},{12,8},{8,12},{13,... | collective-permute-start | bytes 49160 | tf_op jit(solution)/shard_map/ppermute | solution.py:23
  57.5 3.7 %collective-permute-start.15 = (f32[4,1,2,512]{3,2,1,0:T(2,128)S(1)}, f32[4,1,2,512]{3,2,1,0:T(2,128)S(1)}, u32[]{:S(2)}, u32[]{:S(2)}) collective-permute-start(f32[4,1,2,512]{3,2,1,0:T(2,128)S(1)} %get-tuple-element.35), channel_id=1, source_target_pairs={{0,4},{4,0},{1,5},{5,1},{2,6},{6,2},{3,7},{7,3},{8,12},{12,8},{9,1... | collective-permute-start | bytes 49160 | tf_op jit(solution)/shard_map/ppermute | solution.py:20
  61.4 3.5 %collective-permute-start.17 = (f32[4,4,1,512]{3,2,1,0:T(1,128)S(1)}, f32[4,4,1,512]{3,2,1,0:T(1,128)S(1)}, u32[]{:S(2)}, u32[]{:S(2)}) collective-permute-start(f32[4,4,1,512]{3,2,1,0:T(1,128)S(1)} %get-tuple-element.32), channel_id=1, source_target_pairs={{0,1},{1,2},{2,3},{3,0},{4,5},{5,6},{6,7},{7,4},{8,9},{9,10},{10,1... | collective-permute-start | bytes 98312 | tf_op jit(solution)/shard_map/ppermute | solution.py:20
  65.1 3.6 %collective-permute-start.18 = (f32[1,1,1,512]{3,2,1,0:T(1,128)S(1)}, f32[1,1,1,512]{3,2,1,0:T(1,128)S(1)}, u32[]{:S(2)}, u32[]{:S(2)}) collective-permute-start(f32[1,1,1,512]{3,2,1,0:T(1,128)S(1)} %bitcast.42), channel_id=1, source_target_pairs={{8,0},{16,8},{24,16},{0,24},{9,1},{17,9},{25,17},{1,25},{10,2},{18... | collective-permute-start | bytes 6152 | tf_op jit(solution)/shard_map/ppermute | solution.py:23
  65.2 5.4 %collective-permute-start.19 = (f32[1,1,1,512]{3,2,1,0:T(1,128)S(1)}, f32[1,1,1,512]{3,2,1,0:T(1,128)S(1)}, u32[]{:S(2)}, u32[]{:S(2)}) collective-permute-start(f32[1,1,1,512]{3,2,1,0:T(1,128)S(1)} %bitcast.43), channel_id=1, source_target_pairs={{0,8},{8,16},{16,24},{24,0},{1,9},{9,17},{17,25},{25,1},{2,10},{10... | collective-permute-start | bytes 6152 | tf_op jit(solution)/shard_map/ppermute | solution.py:20
  70.6 3.7 %collective-permute-start.20 = (f32[3,1,1,512]{3,2,1,0:T(1,128)S(1)}, f32[3,1,1,512]{3,2,1,0:T(1,128)S(1)}, u32[]{:S(2)}, u32[]{:S(2)}) collective-permute-start(f32[3,1,1,512]{3,2,1,0:T(1,128)S(1)} %pad_maximum_fusion.147), channel_id=1, source_target_pairs={{4,0},{0,4},{5,1},{1,5},{6,2},{2,6},{7,3},{3,7},{12,8},{8,12},{13,... | collective-permute-start | bytes 18440 | tf_op jit(solution)/shard_map/ppermute | solution.py:23
  72.1 3.6 %collective-permute-start.21 = (f32[3,1,1,512]{3,2,1,0:T(1,128)S(1)}, f32[3,1,1,512]{3,2,1,0:T(1,128)S(1)}, u32[]{:S(2)}, u32[]{:S(2)}) collective-permute-start(f32[3,1,1,512]{3,2,1,0:T(1,128)S(1)} %pad_maximum_fusion.147), channel_id=1, source_target_pairs={{0,4},{4,0},{1,5},{5,1},{2,6},{6,2},{3,7},{7,3},{8,12},{12,8},{9,1... | collective-permute-start | bytes 18440 | tf_op jit(solution)/shard_map/ppermute | solution.py:20
  75.8 3.2 %collective-permute-start.23 = (f32[3,3,1,512]{3,2,1,0:T(1,128)S(1)}, f32[3,3,1,512]{3,2,1,0:T(1,128)S(1)}, u32[]{:S(2)}, u32[]{:S(2)}) collective-permute-start(f32[3,3,1,512]{3,2,1,0:T(1,128)S(1)} %pad_maximum_fusion.108), channel_id=1, source_target_pairs={{0,1},{1,2},{2,3},{3,0},{4,5},{5,6},{6,7},{7,4},{8,9},{9,10},{10,1... | collective-permute-start | bytes 55304 | tf_op jit(solution)/shard_map/ppermute | solution.py:20
  79.1 3.6 %collective-permute-start.24 = (f32[1,1,1,512]{3,2,1,0:T(1,128)S(1)}, f32[1,1,1,512]{3,2,1,0:T(1,128)S(1)}, u32[]{:S(2)}, u32[]{:S(2)}) collective-permute-start(f32[1,1,1,512]{3,2,1,0:T(1,128)S(1)} %multiply_add_fusion.3), channel_id=1, source_target_pairs={{8,0},{16,8},{24,16},{0,24},{9,1},{17,9},{25,17},{1,25},{10,2},{18... | collective-permute-start | bytes 6152 | tf_op jit(solution)/shard_map/ppermute | solution.py:23
  79.2 5.4 %collective-permute-start.25 = (f32[1,1,1,512]{3,2,1,0:T(1,128)S(1)}, f32[1,1,1,512]{3,2,1,0:T(1,128)S(1)}, u32[]{:S(2)}, u32[]{:S(2)}) collective-permute-start(f32[1,1,1,512]{3,2,1,0:T(1,128)S(1)} %multiply_add_fusion.3), channel_id=1, source_target_pairs={{0,8},{8,16},{16,24},{24,0},{1,9},{9,17},{17,25},{25,1},{2,10},{10... | collective-permute-start | bytes 6152 | tf_op jit(solution)/shard_map/ppermute | solution.py:20
  84.6 3.7 %collective-permute-start.26 = (f32[3,1,1,512]{3,2,1,0:T(1,128)S(1)}, f32[3,1,1,512]{3,2,1,0:T(1,128)S(1)}, u32[]{:S(2)}, u32[]{:S(2)}) collective-permute-start(f32[3,1,1,512]{3,2,1,0:T(1,128)S(1)} %pad_maximum_fusion.148), channel_id=1, source_target_pairs={{4,0},{0,4},{5,1},{1,5},{6,2},{2,6},{7,3},{3,7},{12,8},{8,12},{13,... | collective-permute-start | bytes 18440 | tf_op jit(solution)/shard_map/ppermute | solution.py:23
  85.2 3.6 %collective-permute-start.27 = (f32[3,1,1,512]{3,2,1,0:T(1,128)S(1)}, f32[3,1,1,512]{3,2,1,0:T(1,128)S(1)}, u32[]{:S(2)}, u32[]{:S(2)}) collective-permute-start(f32[3,1,1,512]{3,2,1,0:T(1,128)S(1)} %pad_maximum_fusion.148), channel_id=1, source_target_pairs={{0,4},{4,0},{1,5},{5,1},{2,6},{6,2},{3,7},{7,3},{8,12},{12,8},{9,1... | collective-permute-start | bytes 18440 | tf_op jit(solution)/shard_map/ppermute | solution.py:20
  88.9 3.2 %collective-permute-start.29 = (f32[3,3,1,512]{3,2,1,0:T(1,128)S(1)}, f32[3,3,1,512]{3,2,1,0:T(1,128)S(1)}, u32[]{:S(2)}, u32[]{:S(2)}) collective-permute-start(f32[3,3,1,512]{3,2,1,0:T(1,128)S(1)} %pad_maximum_fusion.109), channel_id=1, source_target_pairs={{0,1},{1,2},{2,3},{3,0},{4,5},{5,6},{6,7},{7,4},{8,9},{9,10},{10,1... | collective-permute-start | bytes 55304 | tf_op jit(solution)/shard_map/ppermute | solution.py:20
  92.2 3.6 %collective-permute-start.30 = (f32[1,1,1,512]{3,2,1,0:T(1,128)S(1)}, f32[1,1,1,512]{3,2,1,0:T(1,128)S(1)}, u32[]{:S(2)}, u32[]{:S(2)}) collective-permute-start(f32[1,1,1,512]{3,2,1,0:T(1,128)S(1)} %multiply_add_fusion.2), channel_id=1, source_target_pairs={{8,0},{16,8},{24,16},{0,24},{9,1},{17,9},{25,17},{1,25},{10,2},{18... | collective-permute-start | bytes 6152 | tf_op jit(solution)/shard_map/ppermute | solution.py:23
  92.2 5.4 %collective-permute-start.31 = (f32[1,1,1,512]{3,2,1,0:T(1,128)S(1)}, f32[1,1,1,512]{3,2,1,0:T(1,128)S(1)}, u32[]{:S(2)}, u32[]{:S(2)}) collective-permute-start(f32[1,1,1,512]{3,2,1,0:T(1,128)S(1)} %multiply_add_fusion.2), channel_id=1, source_target_pairs={{0,8},{8,16},{16,24},{24,0},{1,9},{9,17},{17,25},{25,1},{2,10},{10... | collective-permute-start | bytes 6152 | tf_op jit(solution)/shard_map/ppermute | solution.py:20
  97.7 3.7 %collective-permute-start.32 = (f32[3,1,1,512]{3,2,1,0:T(1,128)S(1)}, f32[3,1,1,512]{3,2,1,0:T(1,128)S(1)}, u32[]{:S(2)}, u32[]{:S(2)}) collective-permute-start(f32[3,1,1,512]{3,2,1,0:T(1,128)S(1)} %pad_maximum_fusion.149), channel_id=1, source_target_pairs={{4,0},{0,4},{5,1},{1,5},{6,2},{2,6},{7,3},{3,7},{12,8},{8,12},{13,... | collective-permute-start | bytes 18440 | tf_op jit(solution)/shard_map/ppermute | solution.py:23
  99.3 3.6 %collective-permute-start.33 = (f32[3,1,1,512]{3,2,1,0:T(1,128)S(1)}, f32[3,1,1,512]{3,2,1,0:T(1,128)S(1)}, u32[]{:S(2)}, u32[]{:S(2)}) collective-permute-start(f32[3,1,1,512]{3,2,1,0:T(1,128)S(1)} %pad_maximum_fusion.149), channel_id=1, source_target_pairs={{0,4},{4,0},{1,5},{5,1},{2,6},{6,2},{3,7},{7,3},{8,12},{12,8},{9,1... | collective-permute-start | bytes 18440 | tf_op jit(solution)/shard_map/ppermute | solution.py:20
  103.0 3.2 %collective-permute-start.35 = (f32[3,3,1,512]{3,2,1,0:T(1,128)S(1)}, f32[3,3,1,512]{3,2,1,0:T(1,128)S(1)}, u32[]{:S(2)}, u32[]{:S(2)}) collective-permute-start(f32[3,3,1,512]{3,2,1,0:T(1,128)S(1)} %pad_maximum_fusion.110), channel_id=1, source_target_pairs={{0,1},{1,2},{2,3},{3,0},{4,5},{5,6},{6,7},{7,4},{8,9},{9,10},{10,1... | collective-permute-start | bytes 55304 | tf_op jit(solution)/shard_map/ppermute | solution.py:20
  106.3 3.7 %collective-permute-start.36 = (f32[1,2,2,512]{3,2,1,0:T(2,128)S(1)}, f32[1,2,2,512]{3,2,1,0:T(2,128)S(1)}, u32[]{:S(2)}, u32[]{:S(2)}) collective-permute-start(f32[1,2,2,512]{3,2,1,0:T(2,128)S(1)} %get-tuple-element.38), channel_id=1, source_target_pairs={{8,0},{16,8},{24,16},{0,24},{9,1},{17,9},{25,17},{1,25},{10,2},{18... | collective-permute-start | bytes 24584 | tf_op jit(solution)/shard_map/ppermute | solution.py:23
  106.3 5.5 %collective-permute-start.37 = (f32[1,2,2,512]{3,2,1,0:T(2,128)S(1)}, f32[1,2,2,512]{3,2,1,0:T(2,128)S(1)}, u32[]{:S(2)}, u32[]{:S(2)}) collective-permute-start(f32[1,2,2,512]{3,2,1,0:T(2,128)S(1)} %get-tuple-element.37), channel_id=1, source_target_pairs={{0,8},{8,16},{16,24},{24,0},{1,9},{9,17},{17,25},{25,1},{2,10},{10... | collective-permute-start | bytes 24584 | tf_op jit(solution)/shard_map/ppermute | solution.py:20
  111.9 3.8 %collective-permute-start.38 = (f32[4,1,2,512]{3,2,1,0:T(2,128)S(1)}, f32[4,1,2,512]{3,2,1,0:T(2,128)S(1)}, u32[]{:S(2)}, u32[]{:S(2)}) collective-permute-start(f32[4,1,2,512]{3,2,1,0:T(2,128)S(1)} %get-tuple-element.34), channel_id=1, source_target_pairs={{4,0},{0,4},{5,1},{1,5},{6,2},{2,6},{7,3},{3,7},{12,8},{8,12},{13,... | collective-permute-start | bytes 49160 | tf_op jit(solution)/shard_map/ppermute | solution.py:23
  112.5 3.7 %collective-permute-start.39 = (f32[4,1,2,512]{3,2,1,0:T(2,128)S(1)}, f32[4,1,2,512]{3,2,1,0:T(2,128)S(1)}, u32[]{:S(2)}, u32[]{:S(2)}) collective-permute-start(f32[4,1,2,512]{3,2,1,0:T(2,128)S(1)} %get-tuple-element.33), channel_id=1, source_target_pairs={{0,4},{4,0},{1,5},{5,1},{2,6},{6,2},{3,7},{7,3},{8,12},{12,8},{9,1... | collective-permute-start | bytes 49160 | tf_op jit(solution)/shard_map/ppermute | solution.py:20
  116.4 3.4 %collective-permute-start.41 = (f32[4,4,1,512]{3,2,1,0:T(1,128)S(1)}, f32[4,4,1,512]{3,2,1,0:T(1,128)S(1)}, u32[]{:S(2)}, u32[]{:S(2)}) collective-permute-start(f32[4,4,1,512]{3,2,1,0:T(1,128)S(1)} %get-tuple-element.30), channel_id=1, source_target_pairs={{0,1},{1,2},{2,3},{3,0},{4,5},{5,6},{6,7},{7,4},{8,9},{9,10},{10,1... | collective-permute-start | bytes 98312 | tf_op jit(solution)/shard_map/ppermute | solution.py:20
  120.1 4.0 %collective-permute-start.42 = (f32[1,4,4,512]{3,2,1,0:T(4,128)S(1)}, f32[1,4,4,512]{3,2,1,0:T(4,128)S(1)}, u32[]{:S(2)}, u32[]{:S(2)}) collective-permute-start(f32[1,4,4,512]{3,2,1,0:T(4,128)S(1)} %get-tuple-element.26), channel_id=1, source_target_pairs={{8,0},{16,8},{24,16},{0,24},{9,1},{17,9},{25,17},{1,25},{10,2},{18... | collective-permute-start | bytes 98312 | tf_op jit(solution)/shard_map/ppermute | solution.py:23
  120.2 5.8 %collective-permute-start.43 = (f32[1,4,4,512]{3,2,1,0:T(4,128)S(1)}, f32[1,4,4,512]{3,2,1,0:T(4,128)S(1)}, u32[]{:S(2)}, u32[]{:S(2)}) collective-permute-start(f32[1,4,4,512]{3,2,1,0:T(4,128)S(1)} %get-tuple-element.25), channel_id=1, source_target_pairs={{0,8},{8,16},{16,24},{24,0},{1,9},{9,17},{17,25},{25,1},{2,10},{10... | collective-permute-start | bytes 98312 | tf_op jit(solution)/shard_map/ppermute | solution.py:20
  126.0 4.2 %collective-permute-start.44 = (f32[6,1,4,512]{3,2,1,0:T(4,128)S(1)}, f32[6,1,4,512]{3,2,1,0:T(4,128)S(1)}, u32[]{:S(2)}, u32[]{:S(2)}) collective-permute-start(f32[6,1,4,512]{3,2,1,0:T(4,128)S(1)} %get-tuple-element.22), channel_id=1, source_target_pairs={{4,0},{0,4},{5,1},{1,5},{6,2},{2,6},{7,3},{3,7},{12,8},{8,12},{13,... | collective-permute-start | bytes 147464 | tf_op jit(solution)/shard_map/ppermute | solution.py:23
  127.5 4.1 %collective-permute-start.45 = (f32[6,1,4,512]{3,2,1,0:T(4,128)S(1)}, f32[6,1,4,512]{3,2,1,0:T(4,128)S(1)}, u32[]{:S(2)}, u32[]{:S(2)}) collective-permute-start(f32[6,1,4,512]{3,2,1,0:T(4,128)S(1)} %get-tuple-element.21), channel_id=1, source_target_pairs={{0,4},{4,0},{1,5},{5,1},{2,6},{6,2},{3,7},{7,3},{8,12},{12,8},{9,1... | collective-permute-start | bytes 147464 | tf_op jit(solution)/shard_map/ppermute | solution.py:20
  131.8 4.3 %collective-permute-start.47 = (f32[6,6,1,512]{3,2,1,0:T(1,128)S(1)}, f32[6,6,1,512]{3,2,1,0:T(1,128)S(1)}, u32[]{:S(2)}, u32[]{:S(2)}) collective-permute-start(f32[6,6,1,512]{3,2,1,0:T(1,128)S(1)} %get-tuple-element.18), channel_id=1, source_target_pairs={{0,1},{1,2},{2,3},{3,0},{4,5},{5,6},{6,7},{7,4},{8,9},{9,10},{10,1... | collective-permute-start | bytes 221192 | tf_op jit(solution)/shard_map/ppermute | solution.py:20
  137.9 8.0 %collective-permute-start.48 = (f32[1,8,8,512]{3,2,1,0:T(8,128)S(1)}, f32[1,8,8,512]{3,2,1,0:T(8,128)S(1)}, u32[]{:S(2)}, u32[]{:S(2)}) collective-permute-start(f32[1,8,8,512]{3,2,1,0:T(8,128)S(1)} %get-tuple-element.14), channel_id=1, source_target_pairs={{8,0},{16,8},{24,16},{0,24},{9,1},{17,9},{25,17},{1,25},{10,2},{18... | collective-permute-start | bytes 393224 | tf_op jit(solution)/shard_map/ppermute | solution.py:23
  138.2 7.7 %collective-permute-start.49 = (f32[1,8,8,512]{3,2,1,0:T(8,128)S(1)}, f32[1,8,8,512]{3,2,1,0:T(8,128)S(1)}, u32[]{:S(2)}, u32[]{:S(2)}) collective-permute-start(f32[1,8,8,512]{3,2,1,0:T(8,128)S(1)} %get-tuple-element.13), channel_id=1, source_target_pairs={{0,8},{8,16},{16,24},{24,0},{1,9},{9,17},{17,25},{25,1},{2,10},{10... | collective-permute-start | bytes 393224 | tf_op jit(solution)/shard_map/ppermute | solution.py:20
  146.0 15.9 %collective-permute-start.50 = (f32[10,1,8,512]{3,2,1,0:T(8,128)S(1)}, f32[10,1,8,512]{3,2,1,0:T(8,128)S(1)}, u32[]{:S(2)}, u32[]{:S(2)}) collective-permute-start(f32[10,1,8,512]{3,2,1,0:T(8,128)S(1)} %get-tuple-element.10), channel_id=1, source_target_pairs={{4,0},{0,4},{5,1},{1,5},{6,2},{2,6},{7,3},{3,7},{12,8},{8,12},{13,... | collective-permute-start | bytes 491528 | tf_op jit(solution)/shard_map/ppermute | solution.py:23
  146.6 15.3 %collective-permute-start.51 = (f32[10,1,8,512]{3,2,1,0:T(8,128)S(1)}, f32[10,1,8,512]{3,2,1,0:T(8,128)S(1)}, u32[]{:S(2)}, u32[]{:S(2)}) collective-permute-start(f32[10,1,8,512]{3,2,1,0:T(8,128)S(1)} %get-tuple-element.9), channel_id=1, source_target_pairs={{0,4},{4,0},{1,5},{5,1},{2,6},{6,2},{3,7},{7,3},{8,12},{12,8},{9,1... | collective-permute-start | bytes 491528 | tf_op jit(solution)/shard_map/ppermute | solution.py:20
  162.2 8.1 %collective-permute-start.52 = (f32[10,10,1,512]{3,1,2,0:T(8,128)S(1)}, f32[10,10,1,512]{3,1,2,0:T(8,128)S(1)}, u32[]{:S(2)}, u32[]{:S(2)}) collective-permute-start(f32[10,10,1,512]{3,1,2,0:T(8,128)S(1)} %copy.15), channel_id=1, source_target_pairs={{1,0},{2,1},{3,2},{0,3},{5,4},{6,5},{7,6},{4,7},{9,8},{10,9},{11,1... | collective-permute-start | bytes 614408 | tf_op jit(solution)/shard_map/ppermute | solution.py:23
  162.5 9.2 %collective-permute-start.53 = (f32[10,10,1,512]{3,1,2,0:T(8,128)S(1)}, f32[10,10,1,512]{3,1,2,0:T(8,128)S(1)}, u32[]{:S(2)}, u32[]{:S(2)}) collective-permute-start(f32[10,10,1,512]{3,1,2,0:T(8,128)S(1)} %copy.17), channel_id=1, source_target_pairs={{0,1},{1,2},{2,3},{3,0},{4,5},{5,6},{6,7},{7,4},{8,9},{9,10},{10,1... | collective-permute-start | bytes 614408 | tf_op jit(solution)/shard_map/ppermute | solution.py:20
  (10 other events, 36.1 us)
where the time goes:
time: 178 us
  waiting for transfers between devices  103 us (58%)
  starting transfers between devices  45.8 us (26%)
  blocking collectives  13.8 us (8%)
  other arithmetic  6.08 us (3%)
  local copies, waits for them, and re-layouts  5.52 us (3%)
  matrix products  2.79 us (2%)
    ppermute x27, waiting for transfers between devices, with_halo(): lax.ppermute(lax.slice_in_dim(block, 0, width, axis=dim), axis, backward)  60.4 us
    ppermute x27, waiting for transfers between devices, with_halo(): lax.ppermute(lax.slice_in_dim(block, block.shape[dim] - width, None, axis...  43 us
    ppermute x27, starting transfers between devices, with_halo(): lax.ppermute(lax.slice_in_dim(block, block.shape[dim] - width, None, axis...  27.7 us
    ppermute x27, starting transfers between devices, with_halo(): lax.ppermute(lax.slice_in_dim(block, 0, width, axis=dim), axis, backward)  18.1 us
    all_gather x1, blocking collectives, body(): piece = lax.all_gather(inv_tiles, 'gx', axis=0, tiled=True)  13.8 us
  transfers between devices with their start and end apart: 54, of which 51 were waited for; matrix products, arithmetic and copies ran while one was open for 0% of the time, Pallas kernels for 0%

commit v1 on v0

v1 whole, which is shorter than its diff:
```python
import jax
import jax.numpy as jnp
from jax import lax
from jax.sharding import PartitionSpec as P

LEVELS = 4
COARSE = 4


omega = 0.8
shift_sigma = 0.01

GRID_AXES = (("gx", 0), ("gy", 1), ("gz", 2))


def axis_faces(block, axis, dim):
    count = lax.axis_size(axis)
    first = lax.slice_in_dim(block, 0, 1, axis=dim)
    last = lax.slice_in_dim(block, block.shape[dim] - 1, None, axis=dim)
    if count == 1:
        return last, first
    if count == 2:
        both = lax.ppermute(jnp.concatenate([first, last], axis=dim), axis, [(0, 1), (1, 0)])
        hi = lax.slice_in_dim(both, 0, 1, axis=dim)
        lo = lax.slice_in_dim(both, 1, 2, axis=dim)
        return lo, hi
    forward = [(i, (i + 1) % count) for i in range(count)]
    backward = [((i + 1) % count, i) for i in range(count)]
    lo = lax.ppermute(last, axis, forward)
    hi = lax.ppermute(first, axis, backward)
    return lo, hi


def all_faces(block):
    return [axis_faces(block, axis, dim) for axis, dim in GRID_AXES]


def level_coeffs(level_id):
    coupling = 0.5 / 4.0**level_id
    return (6.0 * coupling + shift_sigma, coupling)


def stencil(block, faces, level_id):
    center, coupling = level_coeffs(level_id)
    beside = None
    for dim, (lo, hi) in enumerate(faces):
        size = block.shape[dim]
        plus = jnp.concatenate([lax.slice_in_dim(block, 1, size, axis=dim), hi], axis=dim)
        minus = jnp.concatenate([lo, lax.slice_in_dim(block, 0, size - 1, axis=dim)], axis=dim)
        pair = plus + minus
        beside = pair if beside is None else beside + pair
    return center * block - coupling * beside


def restrict(field):
    size_a, size_b, size_c, width = field.shape
    return field.reshape(size_a // 2, 2, size_b // 2, 2, size_c // 2, 2, width).mean(axis=(1, 3, 5))


def prolong(field):
    return jnp.repeat(jnp.repeat(jnp.repeat(field, 2, 0), 2, 1), 2, 2)


def dim_mask(box_part, offset, extent):
    cells = offset + jnp.arange(extent, dtype=jnp.int32)[:, None]
    return ((box_part[0][None, :] <= cells) & (cells < box_part[1][None, :])).astype(jnp.float32)


def gram_matrix(inv_tiles, tile_pairs, orb_count):
    count = lax.axis_size("gx")
    local = inv_tiles.shape[0]
    tile_edge = inv_tiles.shape[1]
    me = lax.axis_index("gx")
    total = jnp.zeros((orb_count, orb_count), jnp.float32)
    for shift in range(count):
        if shift == 0:
            piece = inv_tiles
        else:
            piece = lax.ppermute(inv_tiles, "gx", [(i, (i + shift) % count) for i in range(count)])
        owner = (me - shift) % count
        for slot in range(local):
            tile_id = owner * local + slot
            row = tile_pairs[tile_id, 0] * tile_edge
            col = tile_pairs[tile_id, 1] * tile_edge
            total = lax.dynamic_update_slice(total, piece[slot], (row, col))
    return total


def body(residuals, patch_box, tile_pairs, inv_tiles):
    size_a, size_b, size_c, orb_count = residuals.shape
    gram = gram_matrix(inv_tiles, tile_pairs, orb_count)
    current = residuals.astype(jnp.float32)
    rhs_list = []
    corr_list = []
    for level_id in range(LEVELS - 1):
        center, coupling = level_coeffs(level_id)
        correct = omega * current / center
        faces = all_faces(correct)
        remain = current - stencil(correct, faces, level_id)
        rhs_list.append(current)
        corr_list.append(correct)
        current = restrict(remain)
    top_level = LEVELS - 1
    center, coupling = level_coeffs(top_level)
    correct = omega * current / center
    for sweep_id in range(COARSE - 1):
        faces = all_faces(correct)
        correct = correct + omega * (current - stencil(correct, faces, top_level)) / center
    for level_id in reversed(range(LEVELS - 1)):
        center, coupling = level_coeffs(level_id)
        updated = corr_list[level_id] + prolong(correct)
        faces = all_faces(updated)
        correct = updated + omega * (rhs_list[level_id] - stencil(updated, faces, level_id)) / center
    mask_first = dim_mask(patch_box[0], lax.axis_index("gx") * size_a, size_a)
    mask_second = dim_mask(patch_box[1], lax.axis_index("gy") * size_b, size_b)
    mask_third = dim_mask(patch_box[2], lax.axis_index("gz") * size_c, size_c)
    precond = correct * (
        mask_first[:, None, None, :] * mask_second[None, :, None, :] * mask_third[None, None, :, :]
    )
    cell_count = size_a * size_b * size_c
    rows = precond.reshape(cell_count, orb_count)
    mixed = jnp.dot(rows, gram, precision=lax.Precision.HIGHEST, preferred_element_type=jnp.float32)
    return mixed.reshape(size_a, size_b, size_c, orb_count).astype(jnp.bfloat16)


def solution(mesh):
    return jax.shard_map(
        body,
        mesh=mesh,
        in_specs=(P("gx", "gy", "gz", None), P(), P(), P("gx", None, None)),
        out_specs=P("gx", "gy", "gz", None),
        check_vma=False,
    )
```

time: 178 us -> 109 us (0.61)
  waiting for transfers between devices: 103 us -> 35.1 us
  blocking collectives: 13.8 us -> 0 us
  local copies, waits for them, and re-layouts: 5.52 us -> 14.6 us
  between operations: 0.59 us -> 5.83 us
  starting transfers between devices: 45.8 us -> 41.2 us
  other arithmetic: 6.08 us -> 8.62 us
    ppermute x54 -> x48, waiting for transfers between devices: 103 us -> 35.1 us  [the longest x18 26.3 us: axis_faces(): lo = lax.ppermute(last, axis, forward)]
    all_gather x1 -> x0, blocking collectives: 13.8 us -> none  [body(): piece = lax.all_gather(inv_tiles, 'gx', axis=0, tiled=True)]
    slice x14 -> x44, local copies, waits for them, and re-layouts: 0.3 us -> 7.82 us  [the longest x12 3.95 us: stencil(): lax.slice_in_dim(block, 0, size - 1, axis=dim)]
    ppermute x54 -> x48, starting transfers between devices: 45.8 us -> 41.2 us  [the longest x18 21.6 us: axis_faces(): hi = lax.ppermute(first, axis, backward)]
    sub x2, other arithmetic: 1.15 us -> 3.21 us  [body(): remain = current - stencil(correct, faces, level_id)]
  transfers between devices with their start and end apart: 54 -> 48, of which waited for: 51 -> 19; matrix products, arithmetic and copies ran while one was open for 0% -> 15% of each run, Pallas kernels for 0% -> 0%
where the time goes in v1:
time: 109 us
  starting transfers between devices  41.2 us (38%)
  waiting for transfers between devices  35.1 us (32%)
  local copies, waits for them, and re-layouts  14.6 us (13%)
  other arithmetic  8.62 us (8%)
  between operations  5.83 us (5%)
  matrix products  3.2 us (3%)
    ppermute x18, waiting for transfers between devices, axis_faces(): lo = lax.ppermute(last, axis, forward)  26.3 us
    ppermute x18, starting transfers between devices, axis_faces(): hi = lax.ppermute(first, axis, backward)  21.6 us
    ppermute x9, starting transfers between devices, axis_faces(): lax.ppermute(jnp.concatenate([first, last], axis=dim), axis, [(0, 1), (1,...  10.7 us
    ppermute x18, starting transfers between devices, axis_faces(): lo = lax.ppermute(last, axis, forward)  6.4 us
    ppermute x18, waiting for transfers between devices, axis_faces(): hi = lax.ppermute(first, axis, backward)  4.39 us
    slice x12, local copies, waits for them, and re-layouts, stencil(): lax.slice_in_dim(block, 0, size - 1, axis=dim)  3.95 us
    ppermute x9, waiting for transfers between devices, axis_faces(): lax.ppermute(jnp.concatenate([first, last], axis=dim), axis, [(0, 1), (1,...  3.42 us
    sub x2, other arithmetic, body(): remain = current - stencil(correct, faces, level_id)  3.21 us
  transfers between devices with their start and end apart: 48, of which 19 were waited for; matrix products, arithmetic and copies ran while one was open for 15% of the time, Pallas kernels for 0%

profile of v1, /device:TPU:0, one launch (start us, length us, event | category | flops | bytes accessed | tf_op | source)
XLA Modules:
  0.0 108.6 jit_solution(13997019546285248822)
XLA Ops:
  0.0 1.3 %convert_multiply_fusion.1 = f32[8,8,8,512]{3,1,2,0:T(8,128)S(1)} fusion(bf16[8,8,8,512]{3,2,1,0:T(8,128)(2,1)} %param.4), kind=kLoop, calls=%fused_computation.3 | loop fusion | flops 524288 | bytes 1572864 | tf_op jit(solution)/shard_map/div | solution.py:97
  1.6 3.1 %collective-permute-start.2 = (f32[8,2,8,512]{3,2,1,0:T(8,128)S(1)}, f32[8,2,8,512]{3,2,1,0:T(8,128)S(1)}, u32[]{:S(2)}, u32[]{:S(2)}) collective-permute-start(f32[8,2,8,512]{3,2,1,0:T(8,128)S(1)} %pad_maximum_fusion), channel_id=1, source_target_pairs={{0,4},{4,0},{1,5},{5,1},{2,6},{6,2},{3,7},{7,3},{8,12},{12,8},{9,1... | collective-permute-start | bytes 786440 | tf_op jit(solution)/shard_map/ppermute | solution.py:23
  4.6 0.7 fusion.54
  5.4 3.6 %collective-permute-start = (f32[1,8,8,512]{3,1,2,0:T(8,128)}, f32[1,8,8,512]{3,1,2,0:T(8,128)}, u32[]{:S(2)}, u32[]{:S(2)}) collective-permute-start(f32[1,8,8,512]{3,1,2,0:T(8,128)} %get-tuple-element.26), channel_id=1, source_target_pairs={{8,0},{16,8},{24,16},{0,24},{9,1},{17,9},{25,17},{1,25},{10,2},{18... | collective-permute-start | bytes 393224 | tf_op jit(solution)/shard_map/ppermute | solution.py:30
  9.0 0.7 fusion.50
  10.1 1.6 %fusion.52 = (f32[8,7,8,512]{3,1,2,0:T(8,128)}, f32[8,7,8,512]{3,1,2,0:T(8,128)}) fusion(f32[8,8,8,512]{3,1,2,0:T(8,128)S(1)} %convert_multiply_fusion.1), kind=kLoop, calls=%fused_computation.114 | loop fusion | bytes 3670016 | tf_op jit(solution)/shard_map/slice | solution.py:49
  11.7 1.2 %fusion.51 = (f32[8,8,7,512]{3,1,2,0:T(8,128)S(1)}, f32[8,8,7,512]{3,1,2,0:T(8,128)}) fusion(f32[8,8,8,512]{3,1,2,0:T(8,128)S(1)} %convert_multiply_fusion.1), kind=kLoop, calls=%fused_computation.113 | loop fusion | bytes 3670016 | tf_op jit(solution)/shard_map/slice | solution.py:49
  12.9 0.7 copy-done.7
  13.6 0.7 constant_dynamic-slice_fusion
  19.6 0.7 broadcast_multiply_fusion
  20.5 0.9 bitcast_dynamic-update-slice_fusion.3
  21.6 0.7 copy-done.5
  22.4 1.1 %fusion.57 = (f32[8,1,8,512]{3,2,1,0:T(8,128)S(1)}, f32[8,1,8,512]{3,2,1,0:T(8,128)S(1)}) fusion(f32[8,2,8,512]{3,2,1,0:T(8,128)} %copy-done.5), kind=kLoop, calls=%fused_computation.119 | loop fusion | bytes 524288 | tf_op jit(solution)/shard_map/slice | solution.py:25
  23.8 2.8 %collective-permute-done.4 = f32[8,8,1,512]{3,1,2,0:T(8,128)S(1)} collective-permute-done((f32[8,8,1,512]{3,1,2,0:T(8,128)S(1)}, f32[8,8,1,512]{3,1,2,0:T(8,128)S(1)}, u32[]{:S(2)}, u32[]{:S(2)}) %collective-permute-start.4) | collective-permute-done | bytes 131104 | tf_op jit(solution)/shard_map/ppermute | solution.py:29
  26.7 3.0 %convert_subtract_fusion.1 = f32[8,8,8,512]{3,1,2,0:T(8,128)} fusion(f32[1,8,8,512]{3,1,2,0:T(8,128)} %collective-permute-done, f32[7,8,8,512]{3,1,2,0:T(8,128)S(1)} %get-tuple-element.28, f32[7,8,8,512]{3,1,2,0:T(8,128)S(1)} %get-tuple-element.27, f32[1,8,8,512]{3,1,2,0:T(8,128)} %collective-permute-done.1, f32[8,1,8,512]{3,1,2,0:T(1,128)S(1)} %copy.10, ...), kind=kLoop, calls=%fused_computation.1 | loop fusion | flops 4194304 | bytes 7864320 | tf_op jit(solution)/shard_map/sub | solution.py:99
  29.7 1.8 %reshape.338 = f32[4,2,4,2,4,2,512]{6,3,2,5,4,1,0:T(2,128)S(1)} reshape(f32[8,8,8,512]{3,1,2,0:T(8,128)} %convert_subtract_fusion.1) | data formatting | bytes 2097152 | tf_op jit(solution)/shard_map/reshape | solution.py:57
  31.5 0.7 reduce_sum.27
  33.1 3.8 %collective-permute-start.5 = (f32[1,4,4,512]{3,1,2,0:T(4,128)S(1)}, f32[1,4,4,512]{3,1,2,0:T(4,128)S(1)}, u32[]{:S(2)}, u32[]{:S(2)}) collective-permute-start(f32[1,4,4,512]{3,1,2,0:T(4,128)S(1)} %get-tuple-element.54), channel_id=1, source_target_pairs={{8,0},{16,8},{24,16},{0,24},{9,1},{17,9},{25,17},{1,25},{10,2},{18... | collective-permute-start | bytes 98312 | tf_op jit(solution)/shard_map/ppermute | solution.py:30
  37.5 1.0 collective-permute-done.5
  38.6 4.1 %collective-permute-done.6 = f32[1,4,4,512]{3,1,2,0:T(4,128)S(1)} collective-permute-done((f32[1,4,4,512]{3,1,2,0:T(4,128)S(1)}, f32[1,4,4,512]{3,1,2,0:T(4,128)S(1)}, u32[]{:S(2)}, u32[]{:S(2)}) %collective-permute-start.6) | collective-permute-done | bytes 32800 | tf_op jit(solution)/shard_map/ppermute | solution.py:29
  43.1 1.6 %collective-permute-start.12 = (f32[2,2,2,512]{3,1,2,0:T(2,128)S(1)}, f32[2,2,2,512]{3,1,2,0:T(2,128)S(1)}, u32[]{:S(2)}, u32[]{:S(2)}) collective-permute-start(f32[2,2,2,512]{3,1,2,0:T(2,128)S(1)} %broadcast_multiply_fusion.2), channel_id=1, source_target_pairs={{0,4},{4,0},{1,5},{5,1},{2,6},{6,2},{3,7},{7,3},{8,12},{12,8},{9,1... | collective-permute-start | bytes 49160 | tf_op jit(solution)/shard_map/ppermute | solution.py:23
  44.7 1.5 %collective-permute-start.10 = (f32[1,2,2,512]{3,1,2,0:T(2,128)S(1)}, f32[1,2,2,512]{3,1,2,0:T(2,128)S(1)}, u32[]{:S(2)}, u32[]{:S(2)}) collective-permute-start(f32[1,2,2,512]{3,1,2,0:T(2,128)S(1)} %get-tuple-element.70), channel_id=1, source_target_pairs={{8,0},{16,8},{24,16},{0,24},{9,1},{17,9},{25,17},{1,25},{10,2},{18... | collective-permute-start | bytes 24584 | tf_op jit(solution)/shard_map/ppermute | solution.py:30
  47.3 1.1 %collective-permute-done.10 = f32[1,2,2,512]{3,1,2,0:T(2,128)S(1)} collective-permute-done((f32[1,2,2,512]{3,1,2,0:T(2,128)S(1)}, f32[1,2,2,512]{3,1,2,0:T(2,128)S(1)}, u32[]{:S(2)}, u32[]{:S(2)}) %collective-permute-start.10) | collective-permute-done | bytes 8224 | tf_op jit(solution)/shard_map/ppermute | solution.py:30
  48.4 3.3 %collective-permute-done.11 = f32[1,2,2,512]{3,1,2,0:T(2,128)S(1)} collective-permute-done((f32[1,2,2,512]{3,1,2,0:T(2,128)S(1)}, f32[1,2,2,512]{3,1,2,0:T(2,128)S(1)}, u32[]{:S(2)}, u32[]{:S(2)}) %collective-permute-start.11) | collective-permute-done | bytes 8224 | tf_op jit(solution)/shard_map/ppermute | solution.py:29
  51.8 1.5 %collective-permute-start.15 = (f32[1,1,1,512]{3,2,1,0:T(1,128)S(1)}, f32[1,1,1,512]{3,2,1,0:T(1,128)S(1)}, u32[]{:S(2)}, u32[]{:S(2)}) collective-permute-start(f32[1,1,1,512]{3,2,1,0:T(1,128)S(1)} %bitcast.56), channel_id=1, source_target_pairs={{8,0},{16,8},{24,16},{0,24},{9,1},{17,9},{25,17},{1,25},{10,2},{18... | collective-permute-start | bytes 6152 | tf_op jit(solution)/shard_map/ppermute | solution.py:30
  55.0 0.8 bitcast_dynamic-update-slice_fusion.2
  55.9 2.7 %collective-permute-done.16 = f32[1,1,1,512]{3,2,1,0:T(1,128)S(1)} collective-permute-done((f32[1,1,1,512]{3,2,1,0:T(1,128)S(1)}, f32[1,1,1,512]{3,2,1,0:T(1,128)S(1)}, u32[]{:S(2)}, u32[]{:S(2)}) %collective-permute-start.16) | collective-permute-done | bytes 2080 | tf_op jit(solution)/shard_map/ppermute | solution.py:29
  58.7 2.7 %collective-permute-start.20 = (f32[1,1,1,512]{3,2,1,0:T(1,128)S(1)}, f32[1,1,1,512]{3,2,1,0:T(1,128)S(1)}, u32[]{:S(2)}, u32[]{:S(2)}) collective-permute-start(f32[1,1,1,512]{3,2,1,0:T(1,128)S(1)} %multiply_add_fusion.3), channel_id=1, source_target_pairs={{8,0},{16,8},{24,16},{0,24},{9,1},{17,9},{25,17},{1,25},{10,2},{18... | collective-permute-start | bytes 6152 | tf_op jit(solution)/shard_map/ppermute | solution.py:30
  61.9 1.0 collective-permute-done.46
  62.9 1.5 %collective-permute-start.22 = (f32[1,2,1,512]{3,2,1,0:T(1,128)S(1)}, f32[1,2,1,512]{3,2,1,0:T(1,128)S(1)}, u32[]{:S(2)}, u32[]{:S(2)}) collective-permute-start(f32[1,2,1,512]{3,2,1,0:T(1,128)S(1)} %pad_maximum_fusion.5), channel_id=1, source_target_pairs={{0,4},{4,0},{1,5},{5,1},{2,6},{6,2},{3,7},{7,3},{8,12},{12,8},{9,1... | collective-permute-start | bytes 12296 | tf_op jit(solution)/shard_map/ppermute | solution.py:23
  64.4 2.4 %collective-permute-start.47 = (f32[1,128,128]{2,1,0:T(8,128)}, f32[1,128,128]{2,1,0:T(8,128)S(1)}, u32[]{:S(2)}, u32[]{:S(2)}) collective-permute-start(f32[1,128,128]{2,1,0:T(8,128)} %param.7), channel_id=1, source_target_pairs={{0,24},{8,0},{16,8},{24,16},{1,25},{9,1},{17,9},{25,17},{2,26},{10... | collective-permute-start | bytes 196616 | tf_op jit(solution)/shard_map/ppermute | solution.py:79
  66.9 2.6 %collective-permute-start.25 = (f32[1,1,1,512]{3,2,1,0:T(1,128)S(1)}, f32[1,1,1,512]{3,2,1,0:T(1,128)S(1)}, u32[]{:S(2)}, u32[]{:S(2)}) collective-permute-start(f32[1,1,1,512]{3,2,1,0:T(1,128)S(1)} %multiply_add_fusion.2), channel_id=1, source_target_pairs={{8,0},{16,8},{24,16},{0,24},{9,1},{17,9},{25,17},{1,25},{10,2},{18... | collective-permute-start | bytes 6152 | tf_op jit(solution)/shard_map/ppermute | solution.py:30
  70.0 0.7 collective-permute-start.27
  70.8 4.1 %collective-permute-done.26 = f32[1,1,1,512]{3,2,1,0:T(1,128)S(1)} collective-permute-done((f32[1,1,1,512]{3,2,1,0:T(1,128)S(1)}, f32[1,1,1,512]{3,2,1,0:T(1,128)S(1)}, u32[]{:S(2)}, u32[]{:S(2)}) %collective-permute-start.26) | collective-permute-done | bytes 2080 | tf_op jit(solution)/shard_map/ppermute | solution.py:29
  75.5 2.7 %collective-permute-start.30 = (f32[1,2,2,512]{3,1,2,0:T(2,128)S(1)}, f32[1,2,2,512]{3,1,2,0:T(2,128)S(1)}, u32[]{:S(2)}, u32[]{:S(2)}) collective-permute-start(f32[1,2,2,512]{3,1,2,0:T(2,128)S(1)} %get-tuple-element.62), channel_id=1, source_target_pairs={{8,0},{16,8},{24,16},{0,24},{9,1},{17,9},{25,17},{1,25},{10,2},{18... | collective-permute-start | bytes 24584 | tf_op jit(solution)/shard_map/ppermute | solution.py:30
  78.7 0.8 collective-permute-done.30
  79.6 4.1 %collective-permute-done.31 = f32[1,2,2,512]{3,1,2,0:T(2,128)S(1)} collective-permute-done((f32[1,2,2,512]{3,1,2,0:T(2,128)S(1)}, f32[1,2,2,512]{3,1,2,0:T(2,128)S(1)}, u32[]{:S(2)}, u32[]{:S(2)}) %collective-permute-start.31) | collective-permute-done | bytes 8224 | tf_op jit(solution)/shard_map/ppermute | solution.py:29
  84.2 1.6 %collective-permute-start.37 = (f32[4,2,4,512]{3,1,2,0:T(2,128)S(1)}, f32[4,2,4,512]{3,1,2,0:T(2,128)S(1)}, u32[]{:S(2)}, u32[]{:S(2)}) collective-permute-start(f32[4,2,4,512]{3,1,2,0:T(2,128)S(1)} %pad_maximum_fusion.3), channel_id=1, source_target_pairs={{0,4},{4,0},{1,5},{5,1},{2,6},{6,2},{3,7},{7,3},{8,12},{12,8},{9,1... | collective-permute-start | bytes 196616 | tf_op jit(solution)/shard_map/ppermute | solution.py:23
  85.8 1.4 %collective-permute-start.35 = (f32[1,4,4,512]{3,1,2,0:T(4,128)S(1)}, f32[1,4,4,512]{3,1,2,0:T(4,128)S(1)}, u32[]{:S(2)}, u32[]{:S(2)}) collective-permute-start(f32[1,4,4,512]{3,1,2,0:T(4,128)S(1)} %get-tuple-element.42), channel_id=1, source_target_pairs={{8,0},{16,8},{24,16},{0,24},{9,1},{17,9},{25,17},{1,25},{10,2},{18... | collective-permute-start | bytes 98312 | tf_op jit(solution)/shard_map/ppermute | solution.py:30
  87.2 0.6 collective-permute-start.36
  88.6 1.1 %collective-permute-done.35 = f32[1,4,4,512]{3,1,2,0:T(4,128)S(1)} collective-permute-done((f32[1,4,4,512]{3,1,2,0:T(4,128)S(1)}, f32[1,4,4,512]{3,1,2,0:T(4,128)S(1)}, u32[]{:S(2)}, u32[]{:S(2)}) %collective-permute-start.35) | collective-permute-done | bytes 32800 | tf_op jit(solution)/shard_map/ppermute | solution.py:30
  89.7 3.2 %collective-permute-done.36 = f32[1,4,4,512]{3,1,2,0:T(4,128)S(1)} collective-permute-done((f32[1,4,4,512]{3,1,2,0:T(4,128)S(1)}, f32[1,4,4,512]{3,1,2,0:T(4,128)S(1)}, u32[]{:S(2)}, u32[]{:S(2)}) %collective-permute-start.36) | collective-permute-done | bytes 32800 | tf_op jit(solution)/shard_map/ppermute | solution.py:29
  95.2 0.6 collective-permute-start.42
  95.8 1.4 %collective-permute-start.40 = (f32[1,8,8,512]{3,1,2,0:T(8,128)S(1)}, f32[1,8,8,512]{3,1,2,0:T(8,128)S(1)}, u32[]{:S(2)}, u32[]{:S(2)}) collective-permute-start(f32[1,8,8,512]{3,1,2,0:T(8,128)S(1)} %get-tuple-element.14), channel_id=1, source_target_pairs={{8,0},{16,8},{24,16},{0,24},{9,1},{17,9},{25,17},{1,25},{10,2},{18... | collective-permute-start | bytes 393224 | tf_op jit(solution)/shard_map/ppermute | solution.py:30
  98.6 3.1 %collective-permute-done.42 = f32[8,2,8,512]{3,2,1,0:T(8,128)S(1)} collective-permute-done((f32[8,2,8,512]{3,2,1,0:T(8,128)S(1)}, f32[8,2,8,512]{3,2,1,0:T(8,128)S(1)}, u32[]{:S(2)}, u32[]{:S(2)}) %collective-permute-start.42) | collective-permute-done | bytes 262176 | tf_op jit(solution)/shard_map/ppermute | solution.py:23
  102.2 1.8 %collective-permute-done.41 = f32[1,8,8,512]{3,1,2,0:T(8,128)S(1)} collective-permute-done((f32[1,8,8,512]{3,1,2,0:T(8,128)S(1)}, f32[1,8,8,512]{3,1,2,0:T(8,128)S(1)}, u32[]{:S(2)}, u32[]{:S(2)}) %collective-permute-start.41) | collective-permute-done | bytes 131104 | tf_op jit(solution)/shard_map/ppermute | solution.py:29
  104.1 1.3 %fusion.3 = f32[8,8,8,512]{3,1,2,0:T(8,128)S(1)} fusion(f32[1,8,8,512]{3,1,2,0:T(8,128)S(1)} %collective-permute-done.40, f32[7,8,8,512]{3,1,2,0:T(8,128)S(1)} %get-tuple-element.16, f32[7,8,8,512]{3,1,2,0:T(8,128)S(1)} %get-tuple-element.15, f32[1,8,8,512]{3,1,2,0:T(8,128)S(1)} %collective-permute-done.41, f32[8,1,8,512]{3,1,2,0:T(1,128)S(1)} %copy.14, ...), kind=kLoop, calls=%fused_computation.8 | loop fusion | flops 5767168 | bytes 9060352 | tf_op jit(solution)/shard_map/mul | solution.py:117
  105.4 3.2 %convolution_convert_fusion = bf16[8,8,8,512]{3,2,1,0:T(8,128)(2,1)} fusion(f32[512,512]{1,0:T(8,128)S(1)} %bitcast_dynamic-update-slice_fusion, f32[8,8,8,512]{3,1,2,0:T(8,128)S(1)} %fusion.3), kind=kOutput, calls=%fused_computation.4 | convolution fusion | flops 1610874880 | bytes 2621440 | tf_op jit(solution)/shard_map/dot_general | solution.py:122
  (159 shorter events, 14.1 us)
Async XLA Ops:
  1.6 20.0 %collective-permute-start.2 = (f32[8,2,8,512]{3,2,1,0:T(8,128)S(1)}, f32[8,2,8,512]{3,2,1,0:T(8,128)S(1)}, u32[]{:S(2)}, u32[]{:S(2)}) collective-permute-start(f32[8,2,8,512]{3,2,1,0:T(8,128)S(1)} %pad_maximum_fusion), channel_id=1, source_target_pairs={{0,4},{4,0},{1,5},{5,1},{2,6},{6,2},{3,7},{7,3},{8,12},{12,8},{9,1... | collective-permute-start | bytes 786440 | tf_op jit(solution)/shard_map/ppermute | solution.py:23
  5.4 18.4 %collective-permute-start = (f32[1,8,8,512]{3,1,2,0:T(8,128)}, f32[1,8,8,512]{3,1,2,0:T(8,128)}, u32[]{:S(2)}, u32[]{:S(2)}) collective-permute-start(f32[1,8,8,512]{3,1,2,0:T(8,128)} %get-tuple-element.26), channel_id=1, source_target_pairs={{8,0},{16,8},{24,16},{0,24},{9,1},{17,9},{25,17},{1,25},{10,2},{18... | collective-permute-start | bytes 393224 | tf_op jit(solution)/shard_map/ppermute | solution.py:30
  9.0 14.8 %collective-permute-start.1 = (f32[1,8,8,512]{3,1,2,0:T(8,128)}, f32[1,8,8,512]{3,1,2,0:T(8,128)}, u32[]{:S(2)}, u32[]{:S(2)}) collective-permute-start(f32[1,8,8,512]{3,1,2,0:T(8,128)} %get-tuple-element.25), channel_id=1, source_target_pairs={{0,8},{8,16},{16,24},{24,0},{1,9},{9,17},{17,25},{25,1},{2,10},{10... | collective-permute-start | bytes 393224 | tf_op jit(solution)/shard_map/ppermute | solution.py:29
  9.7 14.1 %collective-permute-start.3 = (f32[8,8,1,512]{3,1,2,0:T(8,128)}, f32[8,8,1,512]{3,1,2,0:T(8,128)}, u32[]{:S(2)}, u32[]{:S(2)}) collective-permute-start(f32[8,8,1,512]{3,1,2,0:T(8,128)} %get-tuple-element.18), channel_id=1, source_target_pairs={{1,0},{2,1},{3,2},{0,3},{5,4},{6,5},{7,6},{4,7},{9,8},{10,9},{11,1... | collective-permute-start | bytes 393224 | tf_op jit(solution)/shard_map/ppermute | solution.py:30
  10.1 44.3 %collective-permute-start.45 = (f32[1,128,128]{2,1,0:T(8,128)}, f32[1,128,128]{2,1,0:T(8,128)}, u32[]{:S(2)}, u32[]{:S(2)}) collective-permute-start(f32[1,128,128]{2,1,0:T(8,128)} %param.7), channel_id=1, source_target_pairs={{0,8},{8,16},{16,24},{24,0},{1,9},{9,17},{17,25},{25,1},{2,10},{10... | collective-permute-start | bytes 196616 | tf_op jit(solution)/shard_map/ppermute | solution.py:79
  22.3 4.4 %collective-permute-start.4 = (f32[8,8,1,512]{3,1,2,0:T(8,128)S(1)}, f32[8,8,1,512]{3,1,2,0:T(8,128)S(1)}, u32[]{:S(2)}, u32[]{:S(2)}) collective-permute-start(f32[8,8,1,512]{3,1,2,0:T(8,128)S(1)} %copy-done.6), channel_id=1, source_target_pairs={{0,1},{1,2},{2,3},{3,0},{4,5},{5,6},{6,7},{7,4},{8,9},{9,10},{10,1... | collective-permute-start | bytes 393224 | tf_op jit(solution)/shard_map/ppermute | solution.py:29
  32.6 4.4 %collective-permute-start.7 = (f32[4,2,4,512]{3,1,2,0:T(2,128)S(1)}, f32[4,2,4,512]{3,1,2,0:T(2,128)S(1)}, u32[]{:S(2)}, u32[]{:S(2)}) collective-permute-start(f32[4,2,4,512]{3,1,2,0:T(2,128)S(1)} %pad_maximum_fusion.2), channel_id=1, source_target_pairs={{0,4},{4,0},{1,5},{5,1},{2,6},{6,2},{3,7},{7,3},{8,12},{12,8},{9,1... | collective-permute-start | bytes 196616 | tf_op jit(solution)/shard_map/ppermute | solution.py:23
  33.1 5.4 %collective-permute-start.5 = (f32[1,4,4,512]{3,1,2,0:T(4,128)S(1)}, f32[1,4,4,512]{3,1,2,0:T(4,128)S(1)}, u32[]{:S(2)}, u32[]{:S(2)}) collective-permute-start(f32[1,4,4,512]{3,1,2,0:T(4,128)S(1)} %get-tuple-element.54), channel_id=1, source_target_pairs={{8,0},{16,8},{24,16},{0,24},{9,1},{17,9},{25,17},{1,25},{10,2},{18... | collective-permute-start | bytes 98312 | tf_op jit(solution)/shard_map/ppermute | solution.py:30
  37.0 5.7 %collective-permute-start.6 = (f32[1,4,4,512]{3,1,2,0:T(4,128)S(1)}, f32[1,4,4,512]{3,1,2,0:T(4,128)S(1)}, u32[]{:S(2)}, u32[]{:S(2)}) collective-permute-start(f32[1,4,4,512]{3,1,2,0:T(4,128)S(1)} %get-tuple-element.53), channel_id=1, source_target_pairs={{0,8},{8,16},{16,24},{24,0},{1,9},{9,17},{17,25},{25,1},{2,10},{10... | collective-permute-start | bytes 98312 | tf_op jit(solution)/shard_map/ppermute | solution.py:29
  37.0 5.7 %collective-permute-start.8 = (f32[4,4,1,512]{3,1,2,0:T(4,128)S(1)}, f32[4,4,1,512]{3,1,2,0:T(4,128)S(1)}, u32[]{:S(2)}, u32[]{:S(2)}) collective-permute-start(f32[4,4,1,512]{3,1,2,0:T(4,128)S(1)} %get-tuple-element.46), channel_id=1, source_target_pairs={{1,0},{2,1},{3,2},{0,3},{5,4},{6,5},{7,6},{4,7},{9,8},{10,9},{11,1... | collective-permute-start | bytes 98312 | tf_op jit(solution)/shard_map/ppermute | solution.py:30
  37.0 5.7 %collective-permute-start.9 = (f32[4,4,1,512]{3,1,2,0:T(4,128)S(1)}, f32[4,4,1,512]{3,1,2,0:T(4,128)S(1)}, u32[]{:S(2)}, u32[]{:S(2)}) collective-permute-start(f32[4,4,1,512]{3,1,2,0:T(4,128)S(1)} %get-tuple-element.45), channel_id=1, source_target_pairs={{0,1},{1,2},{2,3},{3,0},{4,5},{5,6},{6,7},{7,4},{8,9},{9,10},{10,1... | collective-permute-start | bytes 98312 | tf_op jit(solution)/shard_map/ppermute | solution.py:29
  43.1 3.8 %collective-permute-start.12 = (f32[2,2,2,512]{3,1,2,0:T(2,128)S(1)}, f32[2,2,2,512]{3,1,2,0:T(2,128)S(1)}, u32[]{:S(2)}, u32[]{:S(2)}) collective-permute-start(f32[2,2,2,512]{3,1,2,0:T(2,128)S(1)} %broadcast_multiply_fusion.2), channel_id=1, source_target_pairs={{0,4},{4,0},{1,5},{5,1},{2,6},{6,2},{3,7},{7,3},{8,12},{12,8},{9,1... | collective-permute-start | bytes 49160 | tf_op jit(solution)/shard_map/ppermute | solution.py:23
  44.7 3.7 %collective-permute-start.10 = (f32[1,2,2,512]{3,1,2,0:T(2,128)S(1)}, f32[1,2,2,512]{3,1,2,0:T(2,128)S(1)}, u32[]{:S(2)}, u32[]{:S(2)}) collective-permute-start(f32[1,2,2,512]{3,1,2,0:T(2,128)S(1)} %get-tuple-element.70), channel_id=1, source_target_pairs={{8,0},{16,8},{24,16},{0,24},{9,1},{17,9},{25,17},{1,25},{10,2},{18... | collective-permute-start | bytes 24584 | tf_op jit(solution)/shard_map/ppermute | solution.py:30
  46.3 5.4 %collective-permute-start.11 = (f32[1,2,2,512]{3,1,2,0:T(2,128)S(1)}, f32[1,2,2,512]{3,1,2,0:T(2,128)S(1)}, u32[]{:S(2)}, u32[]{:S(2)}) collective-permute-start(f32[1,2,2,512]{3,1,2,0:T(2,128)S(1)} %get-tuple-element.69), channel_id=1, source_target_pairs={{0,8},{8,16},{16,24},{24,0},{1,9},{9,17},{17,25},{25,1},{2,10},{10... | collective-permute-start | bytes 24584 | tf_op jit(solution)/shard_map/ppermute | solution.py:29
  46.8 4.9 %collective-permute-start.13 = (f32[2,2,1,512]{3,1,2,0:T(2,128)S(1)}, f32[2,2,1,512]{3,1,2,0:T(2,128)S(1)}, u32[]{:S(2)}, u32[]{:S(2)}) collective-permute-start(f32[2,2,1,512]{3,1,2,0:T(2,128)S(1)} %get-tuple-element.76), channel_id=1, source_target_pairs={{1,0},{2,1},{3,2},{0,3},{5,4},{6,5},{7,6},{4,7},{9,8},{10,9},{11,1... | collective-permute-start | bytes 24584 | tf_op jit(solution)/shard_map/ppermute | solution.py:30
  46.9 4.8 %collective-permute-start.14 = (f32[2,2,1,512]{3,1,2,0:T(2,128)S(1)}, f32[2,2,1,512]{3,1,2,0:T(2,128)S(1)}, u32[]{:S(2)}, u32[]{:S(2)}) collective-permute-start(f32[2,2,1,512]{3,1,2,0:T(2,128)S(1)} %get-tuple-element.75), channel_id=1, source_target_pairs={{0,1},{1,2},{2,3},{3,0},{4,5},{5,6},{6,7},{7,4},{8,9},{9,10},{10,1... | collective-permute-start | bytes 24584 | tf_op jit(solution)/shard_map/ppermute | solution.py:29
  51.8 4.0 %collective-permute-start.15 = (f32[1,1,1,512]{3,2,1,0:T(1,128)S(1)}, f32[1,1,1,512]{3,2,1,0:T(1,128)S(1)}, u32[]{:S(2)}, u32[]{:S(2)}) collective-permute-start(f32[1,1,1,512]{3,2,1,0:T(1,128)S(1)} %bitcast.56), channel_id=1, source_target_pairs={{8,0},{16,8},{24,16},{0,24},{9,1},{17,9},{25,17},{1,25},{10,2},{18... | collective-permute-start | bytes 6152 | tf_op jit(solution)/shard_map/ppermute | solution.py:30
  53.3 5.4 %collective-permute-start.16 = (f32[1,1,1,512]{3,2,1,0:T(1,128)S(1)}, f32[1,1,1,512]{3,2,1,0:T(1,128)S(1)}, u32[]{:S(2)}, u32[]{:S(2)}) collective-permute-start(f32[1,1,1,512]{3,2,1,0:T(1,128)S(1)} %bitcast.57), channel_id=1, source_target_pairs={{0,8},{8,16},{16,24},{24,0},{1,9},{9,17},{17,25},{25,1},{2,10},{10... | collective-permute-start | bytes 6152 | tf_op jit(solution)/shard_map/ppermute | solution.py:29
  53.9 4.8 %collective-permute-start.18 = (f32[1,1,1,512]{3,2,1,0:T(1,128)S(1)}, f32[1,1,1,512]{3,2,1,0:T(1,128)S(1)}, u32[]{:S(2)}, u32[]{:S(2)}) collective-permute-start(f32[1,1,1,512]{3,2,1,0:T(1,128)S(1)} %bitcast.58), channel_id=1, source_target_pairs={{1,0},{2,1},{3,2},{0,3},{5,4},{6,5},{7,6},{4,7},{9,8},{10,9},{11,1... | collective-permute-start | bytes 6152 | tf_op jit(solution)/shard_map/ppermute | solution.py:30
  53.9 4.8 %collective-permute-start.19 = (f32[1,1,1,512]{3,2,1,0:T(1,128)S(1)}, f32[1,1,1,512]{3,2,1,0:T(1,128)S(1)}, u32[]{:S(2)}, u32[]{:S(2)}) collective-permute-start(f32[1,1,1,512]{3,2,1,0:T(1,128)S(1)} %bitcast.59), channel_id=1, source_target_pairs={{0,1},{1,2},{2,3},{3,0},{4,5},{5,6},{6,7},{7,4},{8,9},{9,10},{10,1... | collective-permute-start | bytes 6152 | tf_op jit(solution)/shard_map/ppermute | solution.py:29
  54.4 4.3 %collective-permute-start.17 = (f32[1,2,1,512]{3,2,1,0:T(1,128)S(1)}, f32[1,2,1,512]{3,2,1,0:T(1,128)S(1)}, u32[]{:S(2)}, u32[]{:S(2)}) collective-permute-start(f32[1,2,1,512]{3,2,1,0:T(1,128)S(1)} %pad_maximum_fusion.4), channel_id=1, source_target_pairs={{0,4},{4,0},{1,5},{5,1},{2,6},{6,2},{3,7},{7,3},{8,12},{12,8},{9,1... | collective-permute-start | bytes 12296 | tf_op jit(solution)/shard_map/ppermute | solution.py:23
  55.8 7.1 %collective-permute-start.46 = (f32[1,128,128]{2,1,0:T(8,128)}, f32[1,128,128]{2,1,0:T(8,128)S(1)}, u32[]{:S(2)}, u32[]{:S(2)}) collective-permute-start(f32[1,128,128]{2,1,0:T(8,128)} %param.7), channel_id=1, source_target_pairs={{0,16},{8,24},{16,0},{24,8},{1,17},{9,25},{17,1},{25,9},{2,18},{10... | collective-permute-start | bytes 196616 | tf_op jit(solution)/shard_map/ppermute | solution.py:79
  58.7 5.7 %collective-permute-start.20 = (f32[1,1,1,512]{3,2,1,0:T(1,128)S(1)}, f32[1,1,1,512]{3,2,1,0:T(1,128)S(1)}, u32[]{:S(2)}, u32[]{:S(2)}) collective-permute-start(f32[1,1,1,512]{3,2,1,0:T(1,128)S(1)} %multiply_add_fusion.3), channel_id=1, source_target_pairs={{8,0},{16,8},{24,16},{0,24},{9,1},{17,9},{25,17},{1,25},{10,2},{18... | collective-permute-start | bytes 6152 | tf_op jit(solution)/shard_map/ppermute | solution.py:30
  61.4 5.5 %collective-permute-start.21 = (f32[1,1,1,512]{3,2,1,0:T(1,128)S(1)}, f32[1,1,1,512]{3,2,1,0:T(1,128)S(1)}, u32[]{:S(2)}, u32[]{:S(2)}) collective-permute-start(f32[1,1,1,512]{3,2,1,0:T(1,128)S(1)} %multiply_add_fusion.3), channel_id=1, source_target_pairs={{0,8},{8,16},{16,24},{24,0},{1,9},{9,17},{17,25},{25,1},{2,10},{10... | collective-permute-start | bytes 6152 | tf_op jit(solution)/shard_map/ppermute | solution.py:29
  61.4 5.5 %collective-permute-start.23 = (f32[1,1,1,512]{3,2,1,0:T(1,128)S(1)}, f32[1,1,1,512]{3,2,1,0:T(1,128)S(1)}, u32[]{:S(2)}, u32[]{:S(2)}) collective-permute-start(f32[1,1,1,512]{3,2,1,0:T(1,128)S(1)} %multiply_add_fusion.3), channel_id=1, source_target_pairs={{1,0},{2,1},{3,2},{0,3},{5,4},{6,5},{7,6},{4,7},{9,8},{10,9},{11,1... | collective-permute-start | bytes 6152 | tf_op jit(solution)/shard_map/ppermute | solution.py:30
  61.4 5.5 %collective-permute-start.24 = (f32[1,1,1,512]{3,2,1,0:T(1,128)S(1)}, f32[1,1,1,512]{3,2,1,0:T(1,128)S(1)}, u32[]{:S(2)}, u32[]{:S(2)}) collective-permute-start(f32[1,1,1,512]{3,2,1,0:T(1,128)S(1)} %multiply_add_fusion.3), channel_id=1, source_target_pairs={{0,1},{1,2},{2,3},{3,0},{4,5},{5,6},{6,7},{7,4},{8,9},{9,10},{10,1... | collective-permute-start | bytes 6152 | tf_op jit(solution)/shard_map/ppermute | solution.py:29
  62.9 4.0 %collective-permute-start.22 = (f32[1,2,1,512]{3,2,1,0:T(1,128)S(1)}, f32[1,2,1,512]{3,2,1,0:T(1,128)S(1)}, u32[]{:S(2)}, u32[]{:S(2)}) collective-permute-start(f32[1,2,1,512]{3,2,1,0:T(1,128)S(1)} %pad_maximum_fusion.5), channel_id=1, source_target_pairs={{0,4},{4,0},{1,5},{5,1},{2,6},{6,2},{3,7},{7,3},{8,12},{12,8},{9,1... | collective-permute-start | bytes 12296 | tf_op jit(solution)/shard_map/ppermute | solution.py:23
  64.4 5.6 %collective-permute-start.47 = (f32[1,128,128]{2,1,0:T(8,128)}, f32[1,128,128]{2,1,0:T(8,128)S(1)}, u32[]{:S(2)}, u32[]{:S(2)}) collective-permute-start(f32[1,128,128]{2,1,0:T(8,128)} %param.7), channel_id=1, source_target_pairs={{0,24},{8,0},{16,8},{24,16},{1,25},{9,1},{17,9},{25,17},{2,26},{10... | collective-permute-start | bytes 196616 | tf_op jit(solution)/shard_map/ppermute | solution.py:79
  66.9 3.9 %collective-permute-start.25 = (f32[1,1,1,512]{3,2,1,0:T(1,128)S(1)}, f32[1,1,1,512]{3,2,1,0:T(1,128)S(1)}, u32[]{:S(2)}, u32[]{:S(2)}) collective-permute-start(f32[1,1,1,512]{3,2,1,0:T(1,128)S(1)} %multiply_add_fusion.2), channel_id=1, source_target_pairs={{8,0},{16,8},{24,16},{0,24},{9,1},{17,9},{25,17},{1,25},{10,2},{18... | collective-permute-start | bytes 6152 | tf_op jit(solution)/shard_map/ppermute | solution.py:30
  69.5 5.4 %collective-permute-start.26 = (f32[1,1,1,512]{3,2,1,0:T(1,128)S(1)}, f32[1,1,1,512]{3,2,1,0:T(1,128)S(1)}, u32[]{:S(2)}, u32[]{:S(2)}) collective-permute-start(f32[1,1,1,512]{3,2,1,0:T(1,128)S(1)} %multiply_add_fusion.2), channel_id=1, source_target_pairs={{0,8},{8,16},{16,24},{24,0},{1,9},{9,17},{17,25},{25,1},{2,10},{10... | collective-permute-start | bytes 6152 | tf_op jit(solution)/shard_map/ppermute | solution.py:29
  69.5 5.4 %collective-permute-start.28 = (f32[1,1,1,512]{3,2,1,0:T(1,128)S(1)}, f32[1,1,1,512]{3,2,1,0:T(1,128)S(1)}, u32[]{:S(2)}, u32[]{:S(2)}) collective-permute-start(f32[1,1,1,512]{3,2,1,0:T(1,128)S(1)} %multiply_add_fusion.2), channel_id=1, source_target_pairs={{1,0},{2,1},{3,2},{0,3},{5,4},{6,5},{7,6},{4,7},{9,8},{10,9},{11,1... | collective-permute-start | bytes 6152 | tf_op jit(solution)/shard_map/ppermute | solution.py:30
  69.5 5.4 %collective-permute-start.29 = (f32[1,1,1,512]{3,2,1,0:T(1,128)S(1)}, f32[1,1,1,512]{3,2,1,0:T(1,128)S(1)}, u32[]{:S(2)}, u32[]{:S(2)}) collective-permute-start(f32[1,1,1,512]{3,2,1,0:T(1,128)S(1)} %multiply_add_fusion.2), channel_id=1, source_target_pairs={{0,1},{1,2},{2,3},{3,0},{4,5},{5,6},{6,7},{7,4},{8,9},{9,10},{10,1... | collective-permute-start | bytes 6152 | tf_op jit(solution)/shard_map/ppermute | solution.py:29
  70.0 4.9 %collective-permute-start.27 = (f32[1,2,1,512]{3,2,1,0:T(1,128)S(1)}, f32[1,2,1,512]{3,2,1,0:T(1,128)S(1)}, u32[]{:S(2)}, u32[]{:S(2)}) collective-permute-start(f32[1,2,1,512]{3,2,1,0:T(1,128)S(1)} %pad_maximum_fusion.6), channel_id=1, source_target_pairs={{0,4},{4,0},{1,5},{5,1},{2,6},{6,2},{3,7},{7,3},{8,12},{12,8},{9,1... | collective-permute-start | bytes 12296 | tf_op jit(solution)/shard_map/ppermute | solution.py:23
  74.9 3.8 %collective-permute-start.32 = (f32[2,2,2,512]{3,1,2,0:T(2,128)S(1)}, f32[2,2,2,512]{3,1,2,0:T(2,128)S(1)}, u32[]{:S(2)}, u32[]{:S(2)}) collective-permute-start(f32[2,2,2,512]{3,1,2,0:T(2,128)S(1)} %broadcast_add_fusion), channel_id=1, source_target_pairs={{0,4},{4,0},{1,5},{5,1},{2,6},{6,2},{3,7},{7,3},{8,12},{12,8},{9,1... | collective-permute-start | bytes 49160 | tf_op jit(solution)/shard_map/ppermute | solution.py:23
  75.5 4.0 %collective-permute-start.30 = (f32[1,2,2,512]{3,1,2,0:T(2,128)S(1)}, f32[1,2,2,512]{3,1,2,0:T(2,128)S(1)}, u32[]{:S(2)}, u32[]{:S(2)}) collective-permute-start(f32[1,2,2,512]{3,1,2,0:T(2,128)S(1)} %get-tuple-element.62), channel_id=1, source_target_pairs={{8,0},{16,8},{24,16},{0,24},{9,1},{17,9},{25,17},{1,25},{10,2},{18... | collective-permute-start | bytes 24584 | tf_op jit(solution)/shard_map/ppermute | solution.py:30
  78.2 5.4 %collective-permute-start.31 = (f32[1,2,2,512]{3,1,2,0:T(2,128)S(1)}, f32[1,2,2,512]{3,1,2,0:T(2,128)S(1)}, u32[]{:S(2)}, u32[]{:S(2)}) collective-permute-start(f32[1,2,2,512]{3,1,2,0:T(2,128)S(1)} %get-tuple-element.61), channel_id=1, source_target_pairs={{0,8},{8,16},{16,24},{24,0},{1,9},{9,17},{17,25},{25,1},{2,10},{10... | collective-permute-start | bytes 24584 | tf_op jit(solution)/shard_map/ppermute | solution.py:29
  78.2 5.4 %collective-permute-start.33 = (f32[2,2,1,512]{3,1,2,0:T(2,128)S(1)}, f32[2,2,1,512]{3,1,2,0:T(2,128)S(1)}, u32[]{:S(2)}, u32[]{:S(2)}) collective-permute-start(f32[2,2,1,512]{3,1,2,0:T(2,128)S(1)} %get-tuple-element.68), channel_id=1, source_target_pairs={{1,0},{2,1},{3,2},{0,3},{5,4},{6,5},{7,6},{4,7},{9,8},{10,9},{11,1... | collective-permute-start | bytes 24584 | tf_op jit(solution)/shard_map/ppermute | solution.py:30
  78.2 5.4 %collective-permute-start.34 = (f32[2,2,1,512]{3,1,2,0:T(2,128)S(1)}, f32[2,2,1,512]{3,1,2,0:T(2,128)S(1)}, u32[]{:S(2)}, u32[]{:S(2)}) collective-permute-start(f32[2,2,1,512]{3,1,2,0:T(2,128)S(1)} %get-tuple-element.67), channel_id=1, source_target_pairs={{0,1},{1,2},{2,3},{3,0},{4,5},{5,6},{6,7},{7,4},{8,9},{9,10},{10,1... | collective-permute-start | bytes 24584 | tf_op jit(solution)/shard_map/ppermute | solution.py:29
  84.2 4.3 %collective-permute-start.37 = (f32[4,2,4,512]{3,1,2,0:T(2,128)S(1)}, f32[4,2,4,512]{3,1,2,0:T(2,128)S(1)}, u32[]{:S(2)}, u32[]{:S(2)}) collective-permute-start(f32[4,2,4,512]{3,1,2,0:T(2,128)S(1)} %pad_maximum_fusion.3), channel_id=1, source_target_pairs={{0,4},{4,0},{1,5},{5,1},{2,6},{6,2},{3,7},{7,3},{8,12},{12,8},{9,1... | collective-permute-start | bytes 196616 | tf_op jit(solution)/shard_map/ppermute | solution.py:23
  85.8 3.9 %collective-permute-start.35 = (f32[1,4,4,512]{3,1,2,0:T(4,128)S(1)}, f32[1,4,4,512]{3,1,2,0:T(4,128)S(1)}, u32[]{:S(2)}, u32[]{:S(2)}) collective-permute-start(f32[1,4,4,512]{3,1,2,0:T(4,128)S(1)} %get-tuple-element.42), channel_id=1, source_target_pairs={{8,0},{16,8},{24,16},{0,24},{9,1},{17,9},{25,17},{1,25},{10,2},{18... | collective-permute-start | bytes 98312 | tf_op jit(solution)/shard_map/ppermute | solution.py:30
  87.2 5.7 %collective-permute-start.36 = (f32[1,4,4,512]{3,1,2,0:T(4,128)S(1)}, f32[1,4,4,512]{3,1,2,0:T(4,128)S(1)}, u32[]{:S(2)}, u32[]{:S(2)}) collective-permute-start(f32[1,4,4,512]{3,1,2,0:T(4,128)S(1)} %get-tuple-element.41), channel_id=1, source_target_pairs={{0,8},{8,16},{16,24},{24,0},{1,9},{9,17},{17,25},{25,1},{2,10},{10... | collective-permute-start | bytes 98312 | tf_op jit(solution)/shard_map/ppermute | solution.py:29
  87.8 5.1 %collective-permute-start.38 = (f32[4,4,1,512]{3,1,2,0:T(4,128)S(1)}, f32[4,4,1,512]{3,1,2,0:T(4,128)S(1)}, u32[]{:S(2)}, u32[]{:S(2)}) collective-permute-start(f32[4,4,1,512]{3,1,2,0:T(4,128)S(1)} %get-tuple-element.34), channel_id=1, source_target_pairs={{1,0},{2,1},{3,2},{0,3},{5,4},{6,5},{7,6},{4,7},{9,8},{10,9},{11,1... | collective-permute-start | bytes 98312 | tf_op jit(solution)/shard_map/ppermute | solution.py:30
  87.8 5.1 %collective-permute-start.39 = (f32[4,4,1,512]{3,1,2,0:T(4,128)S(1)}, f32[4,4,1,512]{3,1,2,0:T(4,128)S(1)}, u32[]{:S(2)}, u32[]{:S(2)}) collective-permute-start(f32[4,4,1,512]{3,1,2,0:T(4,128)S(1)} %get-tuple-element.33), channel_id=1, source_target_pairs={{0,1},{1,2},{2,3},{3,0},{4,5},{5,6},{6,7},{7,4},{8,9},{9,10},{10,1... | collective-permute-start | bytes 98312 | tf_op jit(solution)/shard_map/ppermute | solution.py:29
  95.2 6.4 %collective-permute-start.42 = (f32[8,2,8,512]{3,2,1,0:T(8,128)S(1)}, f32[8,2,8,512]{3,2,1,0:T(8,128)S(1)}, u32[]{:S(2)}, u32[]{:S(2)}) collective-permute-start(f32[8,2,8,512]{3,2,1,0:T(8,128)S(1)} %pad_maximum_fusion.1), channel_id=1, source_target_pairs={{0,4},{4,0},{1,5},{5,1},{2,6},{6,2},{3,7},{7,3},{8,12},{12,8},{9,1... | collective-permute-start | bytes 786440 | tf_op jit(solution)/shard_map/ppermute | solution.py:23
  95.8 6.4 %collective-permute-start.40 = (f32[1,8,8,512]{3,1,2,0:T(8,128)S(1)}, f32[1,8,8,512]{3,1,2,0:T(8,128)S(1)}, u32[]{:S(2)}, u32[]{:S(2)}) collective-permute-start(f32[1,8,8,512]{3,1,2,0:T(8,128)S(1)} %get-tuple-element.14), channel_id=1, source_target_pairs={{8,0},{16,8},{24,16},{0,24},{9,1},{17,9},{25,17},{1,25},{10,2},{18... | collective-permute-start | bytes 393224 | tf_op jit(solution)/shard_map/ppermute | solution.py:30
  97.3 6.8 %collective-permute-start.41 = (f32[1,8,8,512]{3,1,2,0:T(8,128)S(1)}, f32[1,8,8,512]{3,1,2,0:T(8,128)S(1)}, u32[]{:S(2)}, u32[]{:S(2)}) collective-permute-start(f32[1,8,8,512]{3,1,2,0:T(8,128)S(1)} %get-tuple-element.13), channel_id=1, source_target_pairs={{0,8},{8,16},{16,24},{24,0},{1,9},{9,17},{17,25},{25,1},{2,10},{10... | collective-permute-start | bytes 393224 | tf_op jit(solution)/shard_map/ppermute | solution.py:29
  97.9 6.2 %collective-permute-start.43 = (f32[8,8,1,512]{3,1,2,0:T(8,128)S(1)}, f32[8,8,1,512]{3,1,2,0:T(8,128)S(1)}, u32[]{:S(2)}, u32[]{:S(2)}) collective-permute-start(f32[8,8,1,512]{3,1,2,0:T(8,128)S(1)} %get-tuple-element.6), channel_id=1, source_target_pairs={{1,0},{2,1},{3,2},{0,3},{5,4},{6,5},{7,6},{4,7},{9,8},{10,9},{11,1... | collective-permute-start | bytes 393224 | tf_op jit(solution)/shard_map/ppermute | solution.py:30
  97.9 6.2 %collective-permute-start.44 = (f32[8,8,1,512]{3,1,2,0:T(8,128)S(1)}, f32[8,8,1,512]{3,1,2,0:T(8,128)S(1)}, u32[]{:S(2)}, u32[]{:S(2)}) collective-permute-start(f32[8,8,1,512]{3,1,2,0:T(8,128)S(1)} %get-tuple-element.5), channel_id=1, source_target_pairs={{0,1},{1,2},{2,3},{3,0},{4,5},{5,6},{6,7},{7,4},{8,9},{9,10},{10,1... | collective-permute-start | bytes 393224 | tf_op jit(solution)/shard_map/ppermute | solution.py:29
  (9 other events, 26.4 us)

commit v2 on v1

--- a/solution.py
+++ b/solution.py
@@ -11,6 +11,16 @@
 shift_sigma = 0.01
 
 GRID_AXES = (("gx", 0), ("gy", 1), ("gz", 2))
+COARSE_HALO = 10
+CHUNK_BYTES = 1 << 21
+
+
+def shifted(block, axis, offset):
+    count = lax.axis_size(axis)
+    step = offset % count
+    if step == 0:
+        return block
+    return lax.ppermute(block, axis, [(j, (j - step) % count) for j in range(count)])
 
 
 def axis_faces(block, axis, dim):
@@ -24,15 +34,33 @@
         hi = lax.slice_in_dim(both, 0, 1, axis=dim)
         lo = lax.slice_in_dim(both, 1, 2, axis=dim)
         return lo, hi
-    forward = [(i, (i + 1) % count) for i in range(count)]
-    backward = [((i + 1) % count, i) for i in range(count)]
-    lo = lax.ppermute(last, axis, forward)
-    hi = lax.ppermute(first, axis, backward)
+    lo = shifted(last, axis, -1)
+    hi = shifted(first, axis, 1)
     return lo, hi
 
 
 def all_faces(block):
     return [axis_faces(block, axis, dim) for axis, dim in GRID_AXES]
+
+
+def extend_axis(block, axis, dim, halo):
+    count = lax.axis_size(axis)
+    size = block.shape[dim]
+    reach = -(-halo // size)
+    if 2 * reach + 1 >= count:
+        offsets = list(range(count))
+        start = 0
+    else:
+        offsets = list(range(-reach, reach + 1))
+        start = reach * size
+    cache = {}
+    pieces = []
+    for offset in offsets:
+        step = offset % count
+        if step not in cache:
+            cache[step] = shifted(block, axis, step)
+        pieces.append(cache[step])
+    return jnp.concatenate(pieces, axis=dim), start
 
 
 def level_coeffs(level_id):
@@ -52,6 +80,16 @@
     return center * block - coupling * beside
 
 
+def wrap_faces(block):
+    faces = []
+    for dim in range(3):
+        size = block.shape[dim]
+        faces.append(
+            (lax.slice_in_dim(block, size - 1, size, axis=dim), lax.slice_in_dim(block, 0, 1, axis=dim))
+        )
+    return faces
+
+
 def restrict(field):
     size_a, size_b, size_c, width = field.shape
     return field.reshape(size_a // 2, 2, size_b // 2, 2, size_c // 2, 2, width).mean(axis=(1, 3, 5))
@@ -59,6 +97,83 @@
 
 def prolong(field):
     return jnp.repeat(jnp.repeat(jnp.repeat(field, 2, 0), 2, 1), 2, 2)
+
+
+def periodic_take(field, dim, first, count):
+    size = field.shape[dim]
+    index = [(first + k) % size for k in range(count)]
+    parts = [lax.slice_in_dim(field, i, i + 1, axis=dim) for i in index]
+    return jnp.concatenate(parts, axis=dim)
+
+
+def coarse_solve(rhs_two):
+    extended = rhs_two
+    starts = []
+    for axis, dim in GRID_AXES:
+        extended, start = extend_axis(extended, axis, dim, COARSE_HALO)
+        starts.append(start)
+    width = extended.shape[3]
+    chunks = 1
+    while extended.size * 4 // chunks > CHUNK_BYTES and width % (2 * chunks * 128) == 0:
+        chunks *= 2
+    if chunks == 1:
+        return coarse_levels(extended, starts, rhs_two.shape)
+    part = width // chunks
+
+    def one_chunk(k):
+        piece = lax.dynamic_slice_in_dim(extended, k * part, part, axis=3)
+        return coarse_levels(piece, starts, rhs_two.shape)
+
+    outs = lax.map(one_chunk, jnp.arange(chunks))
+    outs = jnp.moveaxis(outs, 0, 3)
+    return outs.reshape(outs.shape[:3] + (width,))
+
+
+def coarse_levels(extended, starts, block_shape):
+    level_two = LEVELS - 2
+    center, coupling = level_coeffs(level_two)
+    correct_two = omega * extended / center
+    remain = extended - stencil(correct_two, wrap_faces(correct_two), level_two)
+    current = restrict(remain)
+    top_level = LEVELS - 1
+    center_top, coupling_top = level_coeffs(top_level)
+    correct = omega * current / center_top
+    for sweep_id in range(COARSE - 1):
+        correct = correct + omega * (current - stencil(correct, wrap_faces(correct), top_level)) / center_top
+    updated = correct_two + prolong(correct)
+    post = updated + omega * (extended - stencil(updated, wrap_faces(updated), level_two)) / center
+    for dim, start in enumerate(starts):
+        post = periodic_take(post, dim, start - 1, block_shape[dim] + 2)
+    return post
+
+
+def prolong_face(face, dim):
+    for other in range(3):
+        if other != dim:
+            face = jnp.repeat(face, 2, other)
+    return face
+
+
+def coarse_faces(halo_block, dim):
+    inner = halo_block
+    for other in range(3):
+        if other != dim:
+            inner = lax.slice_in_dim(inner, 1, inner.shape[other] - 1, axis=other)
+    size = inner.shape[dim]
+    lo = lax.slice_in_dim(inner, 0, 1, axis=dim)
+    hi = lax.slice_in_dim(inner, size - 1, size, axis=dim)
+    return lo, hi
+
+
+def post_smooth(level_id, corr, corr_faces, rhs, coarse_inner, coarse_face_list):
+    center, coupling = level_coeffs(level_id)
+    updated = corr + prolong(coarse_inner)
+    faces = []
+    for dim in range(3):
+        lo = corr_faces[dim][0] + prolong_face(coarse_face_list[dim][0], dim)
+        hi = corr_faces[dim][1] + prolong_face(coarse_face_list[dim][1], dim)
+        faces.append((lo, hi))
+    return updated + omega * (rhs - stencil(updated, faces, level_id)) / center
 
 
 def dim_mask(box_part, offset, extent):
@@ -73,10 +188,7 @@
     me = lax.axis_index("gx")
     total = jnp.zeros((orb_count, orb_count), jnp.float32)
     for shift in range(count):
-        if shift == 0:
-            piece = inv_tiles
-        else:
-            piece = lax.ppermute(inv_tiles, "gx", [(i, (i + shift) % count) for i in range(count)])
+        piece = shifted(inv_tiles, "gx", -shift)
         owner = (me - shift) % count
         for slot in range(local):
             tile_id = owner * local + slot
@@ -86,31 +198,28 @@
     return total
 
 
+def vcycle(residuals):
+    rhs_zero = residuals.astype(jnp.float32)
+    center, coupling = level_coeffs(0)
+    corr_zero = omega * rhs_zero / center
+    faces_zero = all_faces(corr_zero)
+    rhs_one = restrict(rhs_zero - stencil(corr_zero, faces_zero, 0))
+    center, coupling = level_coeffs(1)
+    corr_one = omega * rhs_one / center
+    faces_one = all_faces(corr_one)
+    rhs_two = restrict(rhs_one - stencil(corr_one, faces_one, 1))
+    post_two = coarse_solve(rhs_two)
+    inner_two = post_two[1:-1, 1:-1, 1:-1]
+    post_one = post_smooth(
+        1, corr_one, faces_one, rhs_one, inner_two, [coarse_faces(post_two, dim) for dim in range(3)]
+    )
+    return post_smooth(0, corr_zero, faces_zero, rhs_zero, post_one, all_faces(post_one))
+
+
 def body(residuals, patch_box, tile_pairs, inv_tiles):
     size_a, size_b, size_c, orb_count = residuals.shape
     gram = gram_matrix(inv_tiles, tile_pairs, orb_count)
-    current = residuals.astype(jnp.float32)
-    rhs_list = []
-    corr_list = []
-    for level_id in range(LEVELS - 1):
-        center, coupling = level_coeffs(level_id)
-        correct = omega * current / center
-        faces = all_faces(correct)
-        remain = current - stencil(correct, faces, level_id)
-        rhs_list.append(current)
-        corr_list.append(correct)
-        current = restrict(remain)
-    top_level = LEVELS - 1
-    center, coupling = level_coeffs(top_level)
-    correct = omega * current / center
-    for sweep_id in range(COARSE - 1):
-        faces = all_faces(correct)
-        correct = correct + omega * (current - stencil(correct, faces, top_level)) / center
-    for level_id in reversed(range(LEVELS - 1)):
-        center, coupling = level_coeffs(level_id)
-        updated = corr_list[level_id] + prolong(correct)
-        faces = all_faces(updated)
-        correct = updated + omega * (rhs_list[level_id] - stencil(updated, faces, level_id)) / center
+    correct = vcycle(residuals)
     mask_first = dim_mask(patch_box[0], lax.axis_index("gx") * size_a, size_a)
     mask_second = dim_mask(patch_box[1], lax.axis_index("gy") * size_b, size_b)
     mask_third = dim_mask(patch_box[2], lax.axis_index("gz") * size_c, size_c)

time: 109 us -> 107 us (0.982)
  waiting for transfers between devices: 35.1 us -> 19.4 us
  local copies, waits for them, and re-layouts: 14.6 us -> 29.5 us
  starting transfers between devices: 41.2 us -> 29 us
  other arithmetic: 8.62 us -> 18.8 us
    ppermute x39 -> x22, waiting for transfers between devices: 31.7 us -> 19.4 us  [shifted(): lax.ppermute(block, axis, [(j, (j - step) % count) for j in range(count)])]
    broadcast_in_dim x0 -> x32, local copies, waits for them, and re-layouts: none -> 7.88 us  [prolong_face(): face = jnp.repeat(face, 2, other)]
    ppermute x39 -> x22, starting transfers between devices: 30.5 us -> 23.8 us  [shifted(): lax.ppermute(block, axis, [(j, (j - step) % count) for j in range(count)])]
    add x8 -> x17, other arithmetic: 0.82 us -> 6.66 us  [the longest x3 2.7 us: post_smooth(): hi = corr_faces[dim][1] + prolong_face(coarse_face_list[dim][1], dim)]
    ppermute x9 -> x3, starting transfers between devices: 10.7 us -> 5.19 us  [axis_faces(): lax.ppermute(jnp.concatenate([first, last], axis=dim), axis, [(0, 1), (1,...]
    ppermute x9 -> x3, waiting for transfers between devices: 3.42 us -> 0.01 us  [axis_faces(): lax.ppermute(jnp.concatenate([first, last], axis=dim), axis, [(0, 1), (1,...]
    slice x12 -> x24, local copies, waits for them, and re-layouts: 3.95 us -> 7.15 us  [stencil(): lax.slice_in_dim(block, 0, size - 1, axis=dim)]
    mul x1, other arithmetic: 1.32 us -> 3.21 us  [body(): correct * (mask_first[:, None, None, :] * mask_second[None, :, None, :] *...]
  transfers between devices with their start and end apart: 48 -> 25, of which waited for: 19 -> 9; matrix products, arithmetic and copies ran while one was open for 15% -> 22% of each run, Pallas kernels for 0% -> 0%
where the time goes in v2:
time: 107 us; the launch traced here: 106 us
  local copies, waits for them, and re-layouts  29.5 us (28%)
  starting transfers between devices  29 us (27%)
  waiting for transfers between devices  19.4 us (18%)
  other arithmetic  18.8 us (18%)
  between operations  6.1 us (6%)
  matrix products  3.15 us (3%)
    ppermute x22, starting transfers between devices, shifted(): lax.ppermute(block, axis, [(j, (j - step) % count) for j in range(count)])  23.8 us
    ppermute x22, waiting for transfers between devices, shifted(): lax.ppermute(block, axis, [(j, (j - step) % count) for j in range(count)])  19.4 us
    broadcast_in_dim x32, local copies, waits for them, and re-layouts, prolong_face(): face = jnp.repeat(face, 2, other)  7.88 us
    slice x24, local copies, waits for them, and re-layouts, stencil(): lax.slice_in_dim(block, 0, size - 1, axis=dim)  7.15 us
    ppermute x3, starting transfers between devices, axis_faces(): lax.ppermute(jnp.concatenate([first, last], axis=dim), axis, [(0, 1), (1,...  5.19 us
    mul x1, other arithmetic, body(): correct * (mask_first[:, None, None, :] * mask_second[None, :, None, :] *...  3.21 us
    dot_general x1, matrix products, body(): jnp.dot(rows, gram, precision=lax.Precision.HIGHEST, preferred_element_ty...  3.15 us
    slice x6, local copies, waits for them, and re-layouts, axis_faces(): last = lax.slice_in_dim(block, block.shape[dim] - 1, None, axis=dim)  3 us
  transfers between devices with their start and end apart: 25, of which 9 were waited for; matrix products, arithmetic and copies ran while one was open for 22% of the time, Pallas kernels for 0%

profile of v2, /device:TPU:0, one launch (start us, length us, event | category | flops | bytes accessed | tf_op | source)
XLA Modules:
  0.0 106.0 jit_solution(18445690668720911508)
XLA Ops:
  0.0 1.4 %convert_multiply_fusion.1 = f32[8,8,8,512]{3,0,1,2:T(8,128)S(1)} fusion(bf16[8,8,8,512]{3,2,1,0:T(8,128)(2,1)} %param.4), kind=kLoop, calls=%fused_computation.3 | loop fusion | flops 524288 | bytes 1572864 | tf_op jit(solution)/shard_map/div | solution.py:204
  1.5 0.7 pad_maximum_fusion.1
  2.2 3.0 %collective-permute-start.2 = (f32[8,2,8,512]{3,0,1,2:T(8,128)}, f32[8,2,8,512]{3,0,1,2:T(8,128)}, u32[]{:S(2)}, u32[]{:S(2)}) collective-permute-start(f32[8,2,8,512]{3,0,1,2:T(8,128)} %pad_maximum_fusion.1), channel_id=1, source_target_pairs={{0,4},{4,0},{1,5},{5,1},{2,6},{6,2},{3,7},{7,3},{8,12},{12,8},{9,1... | collective-permute-start | bytes 786440 | tf_op jit(solution)/shard_map/ppermute | solution.py:33
  5.2 0.9 fusion.63
  6.1 3.6 %collective-permute-start = (f32[1,8,8,512]{3,0,1,2:T(1,128)}, f32[1,8,8,512]{3,0,1,2:T(1,128)}, u32[]{:S(2)}, u32[]{:S(2)}) collective-permute-start(f32[1,8,8,512]{3,0,1,2:T(1,128)} %get-tuple-element.20), channel_id=1, source_target_pairs={{0,24},{8,0},{16,8},{24,16},{1,25},{9,1},{17,9},{25,17},{2,26},{10... | collective-permute-start | bytes 393224 | tf_op jit(solution)/shard_map/ppermute | solution.py:23
  9.7 0.7 fusion.59
  10.8 1.6 %fusion.64 = (f32[7,8,8,512]{3,0,1,2:T(8,128)}, f32[7,8,8,512]{3,0,1,2:T(8,128)}) fusion(f32[8,8,8,512]{3,0,1,2:T(8,128)S(1)} %convert_multiply_fusion.1), kind=kLoop, calls=%fused_computation.147 | loop fusion | bytes 3670016 | tf_op jit(solution)/shard_map/slice | solution.py:77
  12.4 1.2 %fusion.60 = (f32[8,8,7,512]{3,0,1,2:T(8,128)S(1)}, f32[8,8,7,512]{3,0,1,2:T(8,128)}) fusion(f32[8,8,8,512]{3,0,1,2:T(8,128)S(1)} %convert_multiply_fusion.1), kind=kLoop, calls=%fused_computation.143 | loop fusion | bytes 3670016 | tf_op jit(solution)/shard_map/slice | solution.py:77
  13.6 0.7 copy-done.14
  14.3 0.7 constant_dynamic-slice_fusion
  21.1 0.9 bitcast_dynamic-update-slice_fusion.3
  23.0 1.1 %fusion.78 = (f32[8,1,8,512]{3,0,1,2:T(8,128)S(1)}, f32[8,1,8,512]{3,0,1,2:T(8,128)S(1)}) fusion(f32[8,2,8,512]{3,0,1,2:T(8,128)} %collective-permute-done.2), kind=kLoop, calls=%fused_computation.161 | loop fusion | bytes 524288 | tf_op jit(solution)/shard_map/slice | solution.py:35
  24.1 3.2 %collective-permute-done.4 = f32[8,8,1,512]{3,0,1,2:T(8,128)S(1)} collective-permute-done((f32[8,8,1,512]{3,0,1,2:T(8,128)S(1)}, f32[8,8,1,512]{3,0,1,2:T(8,128)S(1)}, u32[]{:S(2)}, u32[]{:S(2)}) %collective-permute-start.4) | collective-permute-done | bytes 131104 | tf_op jit(solution)/shard_map/ppermute | solution.py:23
  27.9 3.0 %convert_subtract_fusion.1 = f32[8,8,8,512]{3,0,1,2:T(8,128)} fusion(f32[1,8,8,512]{3,0,1,2:T(1,128)} %collective-permute-done, f32[7,8,8,512]{3,0,1,2:T(8,128)S(1)} %copy-done.4, f32[7,8,8,512]{3,0,1,2:T(8,128)S(1)} %copy-done.3, f32[1,8,8,512]{3,0,1,2:T(1,128)} %collective-permute-done.1, f32[8,1,8,512]{3,0,1,2:T(8,128)S(1)} %get-tuple-element.58, ...), kind=kLoop, calls=%fused_computation.1 | loop fusion | flops 4194304 | bytes 7864320 | tf_op jit(solution)/shard_map/sub | solution.py:206
  30.8 1.8 %reshape.395 = f32[4,2,4,2,4,2,512]{6,1,0,3,2,5,4:T(2,128)S(1)} reshape(f32[8,8,8,512]{3,0,1,2:T(8,128)} %convert_subtract_fusion.1) | data formatting | bytes 2097152 | tf_op jit(solution)/shard_map/reshape | solution.py:95
  32.7 0.7 reduce_sum.27
  34.2 3.8 %collective-permute-start.5 = (f32[1,4,4,512]{3,0,1,2:T(1,128)S(1)}, f32[1,4,4,512]{3,0,1,2:T(1,128)S(1)}, u32[]{:S(2)}, u32[]{:S(2)}) collective-permute-start(f32[1,4,4,512]{3,0,1,2:T(1,128)S(1)} %get-tuple-element.80), channel_id=1, source_target_pairs={{0,24},{8,0},{16,8},{24,16},{1,25},{9,1},{17,9},{25,17},{2,26},{10... | collective-permute-start | bytes 98312 | tf_op jit(solution)/shard_map/ppermute | solution.py:23
  38.6 1.1 %collective-permute-done.5 = f32[1,4,4,512]{3,0,1,2:T(1,128)S(1)} collective-permute-done((f32[1,4,4,512]{3,0,1,2:T(1,128)S(1)}, f32[1,4,4,512]{3,0,1,2:T(1,128)S(1)}, u32[]{:S(2)}, u32[]{:S(2)}) %collective-permute-start.5) | collective-permute-done | bytes 32800 | tf_op jit(solution)/shard_map/ppermute | solution.py:23
  39.7 2.6 %collective-permute-start.23 = (f32[1,128,128]{2,1,0:T(8,128)}, f32[1,128,128]{2,1,0:T(8,128)S(1)}, u32[]{:S(2)}, u32[]{:S(2)}) collective-permute-start(f32[1,128,128]{2,1,0:T(8,128)} %param.7), channel_id=1, source_target_pairs={{0,16},{8,24},{16,0},{24,8},{1,17},{9,25},{17,1},{25,9},{2,18},{10... | collective-permute-start | bytes 196616 | tf_op jit(solution)/shard_map/ppermute | solution.py:23
  42.3 1.5 %collective-permute-done.6 = f32[1,4,4,512]{3,0,1,2:T(1,128)S(1)} collective-permute-done((f32[1,4,4,512]{3,0,1,2:T(1,128)S(1)}, f32[1,4,4,512]{3,0,1,2:T(1,128)S(1)}, u32[]{:S(2)}, u32[]{:S(2)}) %collective-permute-start.6) | collective-permute-done | bytes 32800 | tf_op jit(solution)/shard_map/ppermute | solution.py:23
  44.5 1.2 %collective-permute-start.10 = (f32[2,2,2,512]{3,0,1,2:T(2,128)S(1)}, f32[2,2,2,512]{3,0,1,2:T(2,128)S(1)}, u32[]{:S(2)}, u32[]{:S(2)}) collective-permute-start(f32[2,2,2,512]{3,0,1,2:T(2,128)S(1)} %broadcast_multiply_fusion.4), channel_id=1, source_target_pairs={{0,24},{8,0},{16,8},{24,16},{1,25},{9,1},{17,9},{25,17},{2,26},{10... | collective-permute-start | bytes 49160 | tf_op jit(solution)/shard_map/ppermute | solution.py:23
  45.7 2.0 %collective-permute-start.11 = (f32[2,2,2,512]{3,0,1,2:T(2,128)S(1)}, f32[2,2,2,512]{3,0,1,2:T(2,128)S(1)}, u32[]{:S(2)}, u32[]{:S(2)}) collective-permute-start(f32[2,2,2,512]{3,0,1,2:T(2,128)S(1)} %broadcast_multiply_fusion.4), channel_id=1, source_target_pairs={{0,16},{8,24},{16,0},{24,8},{1,17},{9,25},{17,1},{25,9},{2,18},{10... | collective-permute-start | bytes 49160 | tf_op jit(solution)/shard_map/ppermute | solution.py:23
  48.4 0.8 bitcast_dynamic-update-slice_fusion.2
  49.3 1.1 %collective-permute-done.11 = f32[2,2,2,512]{3,0,1,2:T(2,128)S(1)} collective-permute-done((f32[2,2,2,512]{3,0,1,2:T(2,128)S(1)}, f32[2,2,2,512]{3,0,1,2:T(2,128)S(1)}, u32[]{:S(2)}, u32[]{:S(2)}) %collective-permute-start.11) | collective-permute-done | bytes 16416 | tf_op jit(solution)/shard_map/ppermute | solution.py:23
  50.4 2.9 %collective-permute-done.12 = f32[2,2,2,512]{3,0,1,2:T(2,128)S(1)} collective-permute-done((f32[2,2,2,512]{3,0,1,2:T(2,128)S(1)}, f32[2,2,2,512]{3,0,1,2:T(2,128)S(1)}, u32[]{:S(2)}, u32[]{:S(2)}) %collective-permute-start.12) | collective-permute-done | bytes 16416 | tf_op jit(solution)/shard_map/ppermute | solution.py:23
  53.3 1.6 %collective-permute-start.13 = (f32[8,2,2,512]{3,0,1,2:T(8,128)S(1)}, f32[8,2,2,512]{3,0,1,2:T(8,128)S(1)}, u32[]{:S(2)}, u32[]{:S(2)}) collective-permute-start(f32[8,2,2,512]{3,0,1,2:T(8,128)S(1)} %pad_maximum_fusion.4), channel_id=1, source_target_pairs={{0,4},{4,0},{1,5},{5,1},{2,6},{6,2},{3,7},{7,3},{8,12},{12,8},{9,1... | collective-permute-start | bytes 196616 | tf_op jit(solution)/shard_map/ppermute | solution.py:23
  54.9 2.7 %collective-permute-done.13 = f32[8,2,2,512]{3,0,1,2:T(8,128)S(1)} collective-permute-done((f32[8,2,2,512]{3,0,1,2:T(8,128)S(1)}, f32[8,2,2,512]{3,0,1,2:T(8,128)S(1)}, u32[]{:S(2)}, u32[]{:S(2)}) %collective-permute-start.13) | collective-permute-done | bytes 65568 | tf_op jit(solution)/shard_map/ppermute | solution.py:23
  57.8 1.2 %collective-permute-start.15 = (f32[8,4,2,512]{3,0,1,2:T(8,128)S(1)}, f32[8,4,2,512]{3,0,1,2:T(8,128)S(1)}, u32[]{:S(2)}, u32[]{:S(2)}) collective-permute-start(f32[8,4,2,512]{3,0,1,2:T(8,128)S(1)} %pad_maximum_fusion.2), channel_id=1, source_target_pairs={{0,2},{1,3},{2,0},{3,1},{4,6},{5,7},{6,4},{7,5},{8,10},{9,11},{10,... | collective-permute-start | bytes 393224 | tf_op jit(solution)/shard_map/ppermute | solution.py:23
  59.1 1.9 %collective-permute-done.14 = f32[8,4,2,512]{3,0,1,2:T(8,128)S(1)} collective-permute-done((f32[8,4,2,512]{3,0,1,2:T(8,128)S(1)}, f32[8,4,2,512]{3,0,1,2:T(8,128)S(1)}, u32[]{:S(2)}, u32[]{:S(2)}) %collective-permute-start.14) | collective-permute-done | bytes 131104 | tf_op jit(solution)/shard_map/ppermute | solution.py:23
  61.0 4.6 %collective-permute-done.15 = f32[8,4,2,512]{3,0,1,2:T(8,128)S(1)} collective-permute-done((f32[8,4,2,512]{3,0,1,2:T(8,128)S(1)}, f32[8,4,2,512]{3,0,1,2:T(8,128)S(1)}, u32[]{:S(2)}, u32[]{:S(2)}) %collective-permute-start.15) | collective-permute-done | bytes 131104 | tf_op jit(solution)/shard_map/ppermute | solution.py:23
  72.5 1.5 %fusion.56 = (f32[8,8,7,512]{3,0,1,2:T(8,128)}, f32[8,8,7,512]{3,0,1,2:T(8,128)}) fusion(f32[8,8,8,512]{3,0,1,2:T(8,128)S(1)} %bitcast_add_fusion), kind=kLoop, calls=%fused_computation.139 | loop fusion | bytes 3670016 | tf_op jit(solution)/shard_map/slice | solution.py:77
  76.0 1.6 %collective-permute-start.19 = (f32[4,2,4,512]{3,0,1,2:T(4,128)}, f32[4,2,4,512]{3,0,1,2:T(4,128)}, u32[]{:S(2)}, u32[]{:S(2)}) collective-permute-start(f32[4,2,4,512]{3,0,1,2:T(4,128)} %pad_maximum_fusion.5), channel_id=1, source_target_pairs={{0,4},{4,0},{1,5},{5,1},{2,6},{6,2},{3,7},{7,3},{8,12},{12,8},{9,1... | collective-permute-start | bytes 196616 | tf_op jit(solution)/shard_map/ppermute | solution.py:33
  77.6 1.7 %collective-permute-start.20 = (f32[4,4,1,512]{3,0,1,2:T(4,128)}, f32[4,4,1,512]{3,0,1,2:T(4,128)S(1)}, u32[]{:S(2)}, u32[]{:S(2)}) collective-permute-start(f32[4,4,1,512]{3,0,1,2:T(4,128)} %get-tuple-element.60), channel_id=1, source_target_pairs={{0,3},{1,0},{2,1},{3,2},{4,7},{5,4},{6,5},{7,6},{8,11},{9,8},{10,9... | collective-permute-start | bytes 98312 | tf_op jit(solution)/shard_map/ppermute | solution.py:23
  79.4 3.8 %collective-permute-start.17 = (f32[1,4,4,512]{3,0,1,2:T(1,128)}, f32[1,4,4,512]{3,0,1,2:T(1,128)S(1)}, u32[]{:S(2)}, u32[]{:S(2)}) collective-permute-start(f32[1,4,4,512]{3,0,1,2:T(1,128)} %get-tuple-element.64), channel_id=1, source_target_pairs={{0,24},{8,0},{16,8},{24,16},{1,25},{9,1},{17,9},{25,17},{2,26},{10... | collective-permute-start | bytes 98312 | tf_op jit(solution)/shard_map/ppermute | solution.py:23
  83.2 1.5 %fusion.57 = (f32[8,7,8,512]{3,0,1,2:T(8,128)}, f32[8,7,8,512]{3,0,1,2:T(8,128)}) fusion(f32[8,8,8,512]{3,0,1,2:T(8,128)S(1)} %bitcast_add_fusion), kind=kLoop, calls=%fused_computation.140 | loop fusion | bytes 3670016 | tf_op jit(solution)/shard_map/slice | solution.py:77
  85.0 0.7 broadcast_in_dim.210
  86.5 0.8 broadcast_in_dim.192
  87.3 1.1 %add.362 = f32[1,8,8,512]{3,0,1,2:T(1,128)S(1)} add(f32[1,8,8,512]{3,0,1,2:T(1,128)} %collective-permute-done.1, f32[1,8,8,512]{3,0,1,2:T(1,128)S(1)} %broadcast_in_dim.196) | non-fusion elementwise | flops 32768 | bytes 393216 | tf_op jit(solution)/shard_map/add | solution.py:173
  88.5 0.8 copy-done.12
  89.3 1.6 %bitcast_add_fusion.3 = f32[8,8,1,512]{3,0,1,2:T(8,128)} fusion(f32[8,8,1,512]{3,0,1,2:T(8,128)} %collective-permute-done.3, f32[8,4,512]{2,0,1:T(8,128)S(1)} %copy-done.12), kind=kLoop, calls=%fused_computation.66 | loop fusion | flops 32768 | bytes 327680 | tf_op jit(solution)/shard_map/add | solution.py:174
  90.9 1.1 add.361
  92.0 1.4 %slice_bitcast_fusion = (f32[4,4,512]{2,0,1:T(4,128)}, f32[4,4,512]{2,0,1:T(4,128)S(1)}) fusion(f32[4,2,4,512]{3,0,1,2:T(4,128)} %collective-permute-done.19), kind=kLoop, calls=%fused_computation.109 | loop fusion | bytes 131072 | tf_op jit(solution)/shard_map/slice | solution.py:35
  94.0 1.5 %broadcast_in_dim.198 = f32[8,4,512]{2,0,1:T(8,128)} reshape(f32[4,2,4,512]{3,1,0,2:T(2,128)} %broadcast_in_dim.197) | data formatting | bytes 131072 | tf_op jit(solution)/shard_map/broadcast_in_dim | solution.py:153
  95.5 1.4 %broadcast_in_dim.201 = f32[4,2,4,512]{3,1,0,2:T(2,128)} broadcast(f32[4,4,512]{2,0,1:T(4,128)} %get-tuple-element.83), dimensions={0,2,3} | broadcast | bytes 98304 | tf_op jit(solution)/shard_map/broadcast_in_dim | solution.py:153
  96.9 1.5 %broadcast_in_dim.202 = f32[8,4,512]{2,0,1:T(8,128)} reshape(f32[4,2,4,512]{3,1,0,2:T(2,128)} %broadcast_in_dim.201) | data formatting | bytes 131072 | tf_op jit(solution)/shard_map/broadcast_in_dim | solution.py:153
  98.4 1.1 %bitcast_add_fusion.4 = (f32[8,1,8,512]{3,0,1,2:T(8,128)S(1)}, f32[8,1,8,512]{3,0,1,2:T(8,128)S(1)}) fusion(f32[8,4,512]{2,0,1:T(8,128)} %broadcast_in_dim.202, f32[8,2,8,512]{3,0,1,2:T(8,128)} %collective-permute-done.2, f32[8,4,512]{2,0,1:T(8,128)} %broadcast_in_dim.198), kind=kLoop, calls=%fused_computation.67 | loop fusion | flops 65536 | bytes 655360 | tf_op jit(solution)/shard_map/add | solution.py:173
  99.6 3.2 %fusion.3 = f32[8,8,8,512]{3,0,1,2:T(8,128)S(1)} fusion(f32[1,8,8,512]{3,0,1,2:T(1,128)S(1)} %add.361, f32[7,8,8,512]{3,0,1,2:T(8,128)S(1)} %get-tuple-element.10, f32[7,8,8,512]{3,0,1,2:T(8,128)S(1)} %get-tuple-element.9, f32[1,8,8,512]{3,0,1,2:T(1,128)S(1)} %add.362, f32[8,1,8,512]{3,0,1,2:T(8,128)S(1)} %get-tuple-element.56, ...), kind=kLoop, calls=%fused_computation.8 | loop fusion | flops 5767168 | bytes 8536064 | tf_op jit(solution)/shard_map/mul | solution.py:226
  102.8 3.2 %convolution_convert_fusion = bf16[8,8,8,512]{3,2,1,0:T(8,128)(2,1)} fusion(f32[512,512]{1,0:T(8,128)S(1)} %copy-done.2, f32[8,8,8,512]{3,0,1,2:T(8,128)S(1)} %fusion.3), kind=kOutput, calls=%fused_computation.4 | convolution fusion | flops 1610874880 | bytes 2621440 | tf_op jit(solution)/shard_map/dot_general | solution.py:231
  (185 shorter events, 16.2 us)
Async XLA Ops:
  2.2 20.0 %collective-permute-start.2 = (f32[8,2,8,512]{3,0,1,2:T(8,128)}, f32[8,2,8,512]{3,0,1,2:T(8,128)}, u32[]{:S(2)}, u32[]{:S(2)}) collective-permute-start(f32[8,2,8,512]{3,0,1,2:T(8,128)} %pad_maximum_fusion.1), channel_id=1, source_target_pairs={{0,4},{4,0},{1,5},{5,1},{2,6},{6,2},{3,7},{7,3},{8,12},{12,8},{9,1... | collective-permute-start | bytes 786440 | tf_op jit(solution)/shard_map/ppermute | solution.py:33
  6.1 17.9 %collective-permute-start = (f32[1,8,8,512]{3,0,1,2:T(1,128)}, f32[1,8,8,512]{3,0,1,2:T(1,128)}, u32[]{:S(2)}, u32[]{:S(2)}) collective-permute-start(f32[1,8,8,512]{3,0,1,2:T(1,128)} %get-tuple-element.20), channel_id=1, source_target_pairs={{0,24},{8,0},{16,8},{24,16},{1,25},{9,1},{17,9},{25,17},{2,26},{10... | collective-permute-start | bytes 393224 | tf_op jit(solution)/shard_map/ppermute | solution.py:23
  9.7 14.3 %collective-permute-start.1 = (f32[1,8,8,512]{3,0,1,2:T(1,128)}, f32[1,8,8,512]{3,0,1,2:T(1,128)}, u32[]{:S(2)}, u32[]{:S(2)}) collective-permute-start(f32[1,8,8,512]{3,0,1,2:T(1,128)} %get-tuple-element.19), channel_id=1, source_target_pairs={{0,8},{8,16},{16,24},{24,0},{1,9},{9,17},{17,25},{25,1},{2,10},{10... | collective-permute-start | bytes 393224 | tf_op jit(solution)/shard_map/ppermute | solution.py:23
  10.4 13.6 %collective-permute-start.3 = (f32[8,8,1,512]{3,0,1,2:T(8,128)}, f32[8,8,1,512]{3,0,1,2:T(8,128)}, u32[]{:S(2)}, u32[]{:S(2)}) collective-permute-start(f32[8,8,1,512]{3,0,1,2:T(8,128)} %get-tuple-element.12), channel_id=1, source_target_pairs={{0,3},{1,0},{2,1},{3,2},{4,7},{5,4},{6,5},{7,6},{8,11},{9,8},{10,9... | collective-permute-start | bytes 393224 | tf_op jit(solution)/shard_map/ppermute | solution.py:23
  10.8 37.0 %collective-permute-start.22 = (f32[1,128,128]{2,1,0:T(8,128)}, f32[1,128,128]{2,1,0:T(8,128)}, u32[]{:S(2)}, u32[]{:S(2)}) collective-permute-start(f32[1,128,128]{2,1,0:T(8,128)} %param.7), channel_id=1, source_target_pairs={{0,8},{8,16},{16,24},{24,0},{1,9},{9,17},{17,25},{25,1},{2,10},{10... | collective-permute-start | bytes 196616 | tf_op jit(solution)/shard_map/ppermute | solution.py:23
  13.6 0.7 copy-start.14
  18.7 1.3 %copy-start.15 = (s32[3,2,512]{2,1,0:T(2,128)S(1)}, s32[3,2,512]{2,1,0:T(2,128)}, u32[]{:S(2)}) copy-start(s32[3,2,512]{2,1,0:T(2,128)} %param.5) | copy-start | bytes 36868
  21.9 0.9 copy-start.13
  21.9 5.9 %copy-start.3 = (f32[7,8,8,512]{3,0,1,2:T(8,128)S(1)}, f32[7,8,8,512]{3,0,1,2:T(8,128)}, u32[]{:S(2)}) copy-start(f32[7,8,8,512]{3,0,1,2:T(8,128)} %get-tuple-element.21) | copy-start | bytes 2752516
  21.9 5.9 %copy-start.4 = (f32[7,8,8,512]{3,0,1,2:T(8,128)S(1)}, f32[7,8,8,512]{3,0,1,2:T(8,128)}, u32[]{:S(2)}) copy-start(f32[7,8,8,512]{3,0,1,2:T(8,128)} %get-tuple-element.22) | copy-start | bytes 2752516
  21.9 5.9 %copy-start.5 = (f32[8,8,7,512]{3,0,1,2:T(8,128)S(1)}, f32[8,8,7,512]{3,0,1,2:T(8,128)}, u32[]{:S(2)}) copy-start(f32[8,8,7,512]{3,0,1,2:T(8,128)} %get-tuple-element.14) | copy-start | bytes 2752516
  22.2 5.7 %copy-start = (bf16[8,8,8,512]{3,2,1,0:T(8,128)(2,1)S(1)}, bf16[8,8,8,512]{3,2,1,0:T(8,128)(2,1)}, u32[]{:S(2)}) copy-start(bf16[8,8,8,512]{3,2,1,0:T(8,128)(2,1)} %param.4) | copy-start | bytes 1572868
  22.8 4.4 %collective-permute-start.4 = (f32[8,8,1,512]{3,0,1,2:T(8,128)S(1)}, f32[8,8,1,512]{3,0,1,2:T(8,128)S(1)}, u32[]{:S(2)}, u32[]{:S(2)}) collective-permute-start(f32[8,8,1,512]{3,0,1,2:T(8,128)S(1)} %copy-done.13), channel_id=1, source_target_pairs={{0,1},{1,2},{2,3},{3,0},{4,5},{5,6},{6,7},{7,4},{8,9},{9,10},{10,1... | collective-permute-start | bytes 393224 | tf_op jit(solution)/shard_map/ppermute | solution.py:23
  27.2 0.6 copy-start.7
  33.7 4.4 %collective-permute-start.7 = (f32[4,2,4,512]{3,0,1,2:T(4,128)S(1)}, f32[4,2,4,512]{3,0,1,2:T(4,128)S(1)}, u32[]{:S(2)}, u32[]{:S(2)}) collective-permute-start(f32[4,2,4,512]{3,0,1,2:T(4,128)S(1)} %pad_maximum_fusion.3), channel_id=1, source_target_pairs={{0,4},{4,0},{1,5},{5,1},{2,6},{6,2},{3,7},{7,3},{8,12},{12,8},{9,1... | collective-permute-start | bytes 196616 | tf_op jit(solution)/shard_map/ppermute | solution.py:33
  34.2 5.4 %collective-permute-start.5 = (f32[1,4,4,512]{3,0,1,2:T(1,128)S(1)}, f32[1,4,4,512]{3,0,1,2:T(1,128)S(1)}, u32[]{:S(2)}, u32[]{:S(2)}) collective-permute-start(f32[1,4,4,512]{3,0,1,2:T(1,128)S(1)} %get-tuple-element.80), channel_id=1, source_target_pairs={{0,24},{8,0},{16,8},{24,16},{1,25},{9,1},{17,9},{25,17},{2,26},{10... | collective-permute-start | bytes 98312 | tf_op jit(solution)/shard_map/ppermute | solution.py:23
  38.1 5.7 %collective-permute-start.6 = (f32[1,4,4,512]{3,0,1,2:T(1,128)S(1)}, f32[1,4,4,512]{3,0,1,2:T(1,128)S(1)}, u32[]{:S(2)}, u32[]{:S(2)}) collective-permute-start(f32[1,4,4,512]{3,0,1,2:T(1,128)S(1)} %get-tuple-element.79), channel_id=1, source_target_pairs={{0,8},{8,16},{16,24},{24,0},{1,9},{9,17},{17,25},{25,1},{2,10},{10... | collective-permute-start | bytes 98312 | tf_op jit(solution)/shard_map/ppermute | solution.py:23
  38.1 6.0 %collective-permute-start.8 = (f32[4,4,1,512]{3,0,1,2:T(4,128)S(1)}, f32[4,4,1,512]{3,0,1,2:T(4,128)S(1)}, u32[]{:S(2)}, u32[]{:S(2)}) collective-permute-start(f32[4,4,1,512]{3,0,1,2:T(4,128)S(1)} %get-tuple-element.72), channel_id=1, source_target_pairs={{0,3},{1,0},{2,1},{3,2},{4,7},{5,4},{6,5},{7,6},{8,11},{9,8},{10,9... | collective-permute-start | bytes 98312 | tf_op jit(solution)/shard_map/ppermute | solution.py:23
  38.1 6.0 %collective-permute-start.9 = (f32[4,4,1,512]{3,0,1,2:T(4,128)S(1)}, f32[4,4,1,512]{3,0,1,2:T(4,128)S(1)}, u32[]{:S(2)}, u32[]{:S(2)}) collective-permute-start(f32[4,4,1,512]{3,0,1,2:T(4,128)S(1)} %get-tuple-element.71), channel_id=1, source_target_pairs={{0,1},{1,2},{2,3},{3,0},{4,5},{5,6},{6,7},{7,4},{8,9},{9,10},{10,1... | collective-permute-start | bytes 98312 | tf_op jit(solution)/shard_map/ppermute | solution.py:23
  39.7 15.3 %collective-permute-start.23 = (f32[1,128,128]{2,1,0:T(8,128)}, f32[1,128,128]{2,1,0:T(8,128)S(1)}, u32[]{:S(2)}, u32[]{:S(2)}) collective-permute-start(f32[1,128,128]{2,1,0:T(8,128)} %param.7), channel_id=1, source_target_pairs={{0,16},{8,24},{16,0},{24,8},{1,17},{9,25},{17,1},{25,9},{2,18},{10... | collective-permute-start | bytes 196616 | tf_op jit(solution)/shard_map/ppermute | solution.py:23
  43.8 15.3 %collective-permute-start.24 = (f32[1,128,128]{2,1,0:T(8,128)}, f32[1,128,128]{2,1,0:T(8,128)S(1)}, u32[]{:S(2)}, u32[]{:S(2)}) collective-permute-start(f32[1,128,128]{2,1,0:T(8,128)} %param.7), channel_id=1, source_target_pairs={{0,24},{8,0},{16,8},{24,16},{1,25},{9,1},{17,9},{25,17},{2,26},{10... | collective-permute-start | bytes 196616 | tf_op jit(solution)/shard_map/ppermute | solution.py:23
  44.5 4.8 %collective-permute-start.10 = (f32[2,2,2,512]{3,0,1,2:T(2,128)S(1)}, f32[2,2,2,512]{3,0,1,2:T(2,128)S(1)}, u32[]{:S(2)}, u32[]{:S(2)}) collective-permute-start(f32[2,2,2,512]{3,0,1,2:T(2,128)S(1)} %broadcast_multiply_fusion.4), channel_id=1, source_target_pairs={{0,24},{8,0},{16,8},{24,16},{1,25},{9,1},{17,9},{25,17},{2,26},{10... | collective-permute-start | bytes 49160 | tf_op jit(solution)/shard_map/ppermute | solution.py:23
  45.7 4.6 %collective-permute-start.11 = (f32[2,2,2,512]{3,0,1,2:T(2,128)S(1)}, f32[2,2,2,512]{3,0,1,2:T(2,128)S(1)}, u32[]{:S(2)}, u32[]{:S(2)}) collective-permute-start(f32[2,2,2,512]{3,0,1,2:T(2,128)S(1)} %broadcast_multiply_fusion.4), channel_id=1, source_target_pairs={{0,16},{8,24},{16,0},{24,8},{1,17},{9,25},{17,1},{25,9},{2,18},{10... | collective-permute-start | bytes 49160 | tf_op jit(solution)/shard_map/ppermute | solution.py:23
  47.8 5.5 %collective-permute-start.12 = (f32[2,2,2,512]{3,0,1,2:T(2,128)S(1)}, f32[2,2,2,512]{3,0,1,2:T(2,128)S(1)}, u32[]{:S(2)}, u32[]{:S(2)}) collective-permute-start(f32[2,2,2,512]{3,0,1,2:T(2,128)S(1)} %broadcast_multiply_fusion.4), channel_id=1, source_target_pairs={{0,8},{8,16},{16,24},{24,0},{1,9},{9,17},{17,25},{25,1},{2,10},{10... | collective-permute-start | bytes 49160 | tf_op jit(solution)/shard_map/ppermute | solution.py:23
  53.3 4.3 %collective-permute-start.13 = (f32[8,2,2,512]{3,0,1,2:T(8,128)S(1)}, f32[8,2,2,512]{3,0,1,2:T(8,128)S(1)}, u32[]{:S(2)}, u32[]{:S(2)}) collective-permute-start(f32[8,2,2,512]{3,0,1,2:T(8,128)S(1)} %pad_maximum_fusion.4), channel_id=1, source_target_pairs={{0,4},{4,0},{1,5},{5,1},{2,6},{6,2},{3,7},{7,3},{8,12},{12,8},{9,1... | collective-permute-start | bytes 196616 | tf_op jit(solution)/shard_map/ppermute | solution.py:23
  57.7 3.3 %collective-permute-start.14 = (f32[8,4,2,512]{3,0,1,2:T(8,128)S(1)}, f32[8,4,2,512]{3,0,1,2:T(8,128)S(1)}, u32[]{:S(2)}, u32[]{:S(2)}) collective-permute-start(f32[8,4,2,512]{3,0,1,2:T(8,128)S(1)} %pad_maximum_fusion.2), channel_id=1, source_target_pairs={{0,3},{1,0},{2,1},{3,2},{4,7},{5,4},{6,5},{7,6},{8,11},{9,8},{10,9... | collective-permute-start | bytes 393224 | tf_op jit(solution)/shard_map/ppermute | solution.py:23
  57.8 7.8 %collective-permute-start.15 = (f32[8,4,2,512]{3,0,1,2:T(8,128)S(1)}, f32[8,4,2,512]{3,0,1,2:T(8,128)S(1)}, u32[]{:S(2)}, u32[]{:S(2)}) collective-permute-start(f32[8,4,2,512]{3,0,1,2:T(8,128)S(1)} %pad_maximum_fusion.2), channel_id=1, source_target_pairs={{0,2},{1,3},{2,0},{3,1},{4,6},{5,7},{6,4},{7,5},{8,10},{9,11},{10,... | collective-permute-start | bytes 393224 | tf_op jit(solution)/shard_map/ppermute | solution.py:23
  59.0 7.1 %collective-permute-start.16 = (f32[8,4,2,512]{3,0,1,2:T(8,128)S(1)}, f32[8,4,2,512]{3,0,1,2:T(8,128)S(1)}, u32[]{:S(2)}, u32[]{:S(2)}) collective-permute-start(f32[8,4,2,512]{3,0,1,2:T(8,128)S(1)} %pad_maximum_fusion.2), channel_id=1, source_target_pairs={{0,1},{1,2},{2,3},{3,0},{4,5},{5,6},{6,7},{7,4},{8,9},{9,10},{10,1... | collective-permute-start | bytes 393224 | tf_op jit(solution)/shard_map/ppermute | solution.py:23
  59.1 7.2 %copy-start.1 = (f32[512,512]{1,0:T(8,128)}, f32[512,512]{1,0:T(8,128)S(1)}, u32[]{:S(2)}) copy-start(f32[512,512]{1,0:T(8,128)S(1)} %bitcast_dynamic-update-slice_fusion) | copy-start | bytes 3145732
  76.0 15.9 %collective-permute-start.19 = (f32[4,2,4,512]{3,0,1,2:T(4,128)}, f32[4,2,4,512]{3,0,1,2:T(4,128)}, u32[]{:S(2)}, u32[]{:S(2)}) collective-permute-start(f32[4,2,4,512]{3,0,1,2:T(4,128)} %pad_maximum_fusion.5), channel_id=1, source_target_pairs={{0,4},{4,0},{1,5},{5,1},{2,6},{6,2},{3,7},{7,3},{8,12},{12,8},{9,1... | collective-permute-start | bytes 196616 | tf_op jit(solution)/shard_map/ppermute | solution.py:33
  77.6 7.1 %collective-permute-start.18 = (f32[1,4,4,512]{3,0,1,2:T(1,128)S(1)}, f32[1,4,4,512]{3,0,1,2:T(1,128)S(1)}, u32[]{:S(2)}, u32[]{:S(2)}) collective-permute-start(f32[1,4,4,512]{3,0,1,2:T(1,128)S(1)} %get-tuple-element.63), channel_id=1, source_target_pairs={{0,8},{8,16},{16,24},{24,0},{1,9},{9,17},{17,25},{25,1},{2,10},{10... | collective-permute-start | bytes 98312 | tf_op jit(solution)/shard_map/ppermute | solution.py:23
  77.6 7.4 %collective-permute-start.21 = (f32[4,4,1,512]{3,0,1,2:T(4,128)}, f32[4,4,1,512]{3,0,1,2:T(4,128)S(1)}, u32[]{:S(2)}, u32[]{:S(2)}) collective-permute-start(f32[4,4,1,512]{3,0,1,2:T(4,128)} %get-tuple-element.59), channel_id=1, source_target_pairs={{0,1},{1,2},{2,3},{3,0},{4,5},{5,6},{6,7},{7,4},{8,9},{9,10},{10,1... | collective-permute-start | bytes 98312 | tf_op jit(solution)/shard_map/ppermute | solution.py:23
  77.6 8.1 %collective-permute-start.20 = (f32[4,4,1,512]{3,0,1,2:T(4,128)}, f32[4,4,1,512]{3,0,1,2:T(4,128)S(1)}, u32[]{:S(2)}, u32[]{:S(2)}) collective-permute-start(f32[4,4,1,512]{3,0,1,2:T(4,128)} %get-tuple-element.60), channel_id=1, source_target_pairs={{0,3},{1,0},{2,1},{3,2},{4,7},{5,4},{6,5},{7,6},{8,11},{9,8},{10,9... | collective-permute-start | bytes 98312 | tf_op jit(solution)/shard_map/ppermute | solution.py:23
  79.4 7.0 %collective-permute-start.17 = (f32[1,4,4,512]{3,0,1,2:T(1,128)}, f32[1,4,4,512]{3,0,1,2:T(1,128)S(1)}, u32[]{:S(2)}, u32[]{:S(2)}) collective-permute-start(f32[1,4,4,512]{3,0,1,2:T(1,128)} %get-tuple-element.64), channel_id=1, source_target_pairs={{0,24},{8,0},{16,8},{24,16},{1,25},{9,1},{17,9},{25,17},{2,26},{10... | collective-permute-start | bytes 98312 | tf_op jit(solution)/shard_map/ppermute | solution.py:23
  87.3 1.1 %copy-start.8 = (f32[8,8,1,512]{3,0,1,2:T(8,128)S(1)}, f32[8,8,1,512]{3,0,1,2:T(8,128)}, u32[]{:S(2)}) copy-start(f32[8,8,1,512]{3,0,1,2:T(8,128)} %copy-done.7) | copy-start | bytes 393220
  87.3 1.1 %copy-start.11 = (f32[8,4,512]{2,0,1:T(8,128)S(1)}, f32[8,4,512]{2,0,1:T(8,128)}, u32[]{:S(2)}) copy-start(f32[8,4,512]{2,0,1:T(8,128)} %broadcast_in_dim.210) | copy-start | bytes 196612
  88.4 0.8 copy-start.12
  89.3 1.6 %copy-start.10 = (f32[1,8,8,512]{3,0,1,2:T(1,128)S(1)}, f32[1,8,8,512]{3,0,1,2:T(1,128)}, u32[]{:S(2)}) copy-start(f32[1,8,8,512]{3,0,1,2:T(1,128)} %broadcast_in_dim.192) | copy-start | bytes 393220
  98.4 1.1 %copy-start.6 = (f32[8,8,512]{2,0,1:T(8,128)S(1)}, f32[8,8,512]{2,0,1:T(8,128)}, u32[]{:S(2)}) copy-start(f32[8,8,512]{2,0,1:T(8,128)} %broadcast_multiply_fusion.1) | copy-start | bytes 393220
  98.4 1.2 %copy-start.9 = (f32[8,8,1,512]{3,0,1,2:T(8,128)S(1)}, f32[8,8,1,512]{3,0,1,2:T(8,128)}, u32[]{:S(2)}) copy-start(f32[8,8,1,512]{3,0,1,2:T(8,128)} %bitcast_add_fusion.3) | copy-start | bytes 393220
  99.6 3.2 %copy-start.2 = (f32[512,512]{1,0:T(8,128)S(1)}, f32[512,512]{1,0:T(8,128)}, u32[]{:S(2)}) copy-start(f32[512,512]{1,0:T(8,128)} %copy-done.1) | copy-start | bytes 3145732

commit v3 on v2

--- a/solution.py
+++ b/solution.py
@@ -68,16 +68,26 @@
     return (6.0 * coupling + shift_sigma, coupling)
 
 
+def pad_with(block, faces):
+    padded = block
+    for dim, (lo, hi) in enumerate(faces):
+        widths = [(0, 0)] * 4
+        for other in range(dim):
+            widths[other] = (1, 1)
+        lo = jnp.pad(lo, widths)
+        hi = jnp.pad(hi, widths)
+        padded = jnp.concatenate([lo, padded, hi], axis=dim)
+    return padded
+
+
 def stencil(block, faces, level_id):
     center, coupling = level_coeffs(level_id)
-    beside = None
-    for dim, (lo, hi) in enumerate(faces):
-        size = block.shape[dim]
-        plus = jnp.concatenate([lax.slice_in_dim(block, 1, size, axis=dim), hi], axis=dim)
-        minus = jnp.concatenate([lo, lax.slice_in_dim(block, 0, size - 1, axis=dim)], axis=dim)
-        pair = plus + minus
-        beside = pair if beside is None else beside + pair
-    return center * block - coupling * beside
+    padded = pad_with(block, faces)
+    middle = padded[1:-1, 1:-1, 1:-1]
+    beside = padded[2:, 1:-1, 1:-1] + padded[:-2, 1:-1, 1:-1]
+    beside = beside + padded[1:-1, 2:, 1:-1] + padded[1:-1, :-2, 1:-1]
+    beside = beside + padded[1:-1, 1:-1, 2:] + padded[1:-1, 1:-1, :-2]
+    return center * middle - coupling * beside
 
 
 def wrap_faces(block):

time: 107 us -> 82.7 us (0.77)
  local copies, waits for them, and re-layouts: 29.5 us -> 15.4 us
  other arithmetic: 18.8 us -> 11.9 us
  waiting for transfers between devices: 19.4 us -> 15.5 us
    slice x27 -> x6, local copies, waits for them, and re-layouts: 7.17 us -> 0.04 us  [the longest x5 0.04 us: wrap_faces(): lax.slice_in_dim(block, 0, 1, axis=dim)]
    broadcast_in_dim x32, local copies, waits for them, and re-layouts: 7.88 us -> 1.04 us  [prolong_face(): face = jnp.repeat(face, 2, other)]
    unnamed x35 -> x55, local copies, waits for them, and re-layouts: 2.9 us -> 6.96 us
    ppermute x22, waiting for transfers between devices: 19.4 us -> 15.5 us  [shifted(): lax.ppermute(block, axis, [(j, (j - step) % count) for j in range(count)])]
    slice x6 -> x3, local copies, waits for them, and re-layouts: 3 us -> 0.29 us  [axis_faces(): last = lax.slice_in_dim(block, block.shape[dim] - 1, None, axis=dim)]
    add x3, other arithmetic: 2.7 us -> 0.83 us  [post_smooth(): hi = corr_faces[dim][1] + prolong_face(coarse_face_list[dim][1], dim)]
    slice x3, local copies, waits for them, and re-layouts: 2.47 us -> 0.81 us  [axis_faces(): lo = lax.slice_in_dim(both, 1, 2, axis=dim)]
    mul x1, other arithmetic: 3.21 us -> 1.66 us  [body(): correct * (mask_first[:, None, None, :] * mask_second[None, :, None, :] *...]
  transfers between devices with their start and end apart: 25 -> 25, of which waited for: 9 -> 9; matrix products, arithmetic and copies ran while one was open for 22% -> 20% of each run, Pallas kernels for 0% -> 0%
where the time goes in v3:
time: 82.7 us; the launch traced here: 81.9 us
  starting transfers between devices  29.8 us (36%)
  waiting for transfers between devices  15.5 us (19%)
  local copies, waits for them, and re-layouts  15.4 us (19%)
  other arithmetic  11.9 us (14%)
  between operations  6.1 us (7%)
  matrix products  3.19 us (4%)
    ppermute x22, starting transfers between devices, shifted(): lax.ppermute(block, axis, [(j, (j - step) % count) for j in range(count)])  24.6 us
    ppermute x22, waiting for transfers between devices, shifted(): lax.ppermute(block, axis, [(j, (j - step) % count) for j in range(count)])  15.5 us
    unnamed x55, local copies, waits for them, and re-layouts  6.96 us
    ppermute x3, starting transfers between devices, axis_faces(): lax.ppermute(jnp.concatenate([first, last], axis=dim), axis, [(0, 1), (1,...  5.15 us
    dot_general x1, matrix products, body(): jnp.dot(rows, gram, precision=lax.Precision.HIGHEST, preferred_element_ty...  3.19 us
    dynamic_update_slice x4, local copies, waits for them, and re-layouts, gram_matrix(): total = lax.dynamic_update_slice(total, piece[slot], (row, col))  2.55 us
    mul x1, other arithmetic, body(): correct * (mask_first[:, None, None, :] * mask_second[None, :, None, :] *...  1.66 us
  transfers between devices with their start and end apart: 25, of which 9 were waited for; matrix products, arithmetic and copies ran while one was open for 20% of the time, Pallas kernels for 0%

profile of v3, /device:TPU:0, one launch (start us, length us, event | category | flops | bytes accessed | tf_op | source)
XLA Modules:
  0.0 81.9 jit_solution(13926341591744458277)
XLA Ops:
  0.0 1.4 %convert_multiply_fusion.1 = f32[8,8,8,512]{3,0,1,2:T(8,128)S(1)} fusion(bf16[8,8,8,512]{3,2,1,0:T(8,128)(2,1)} %param.4), kind=kLoop, calls=%fused_computation.3 | loop fusion | flops 524288 | bytes 1572864 | tf_op jit(solution)/shard_map/div | solution.py:214
  1.5 3.1 %collective-permute-start.2 = (f32[8,2,8,512]{3,0,1,2:T(8,128)S(1)}, f32[8,2,8,512]{3,0,1,2:T(8,128)S(1)}, u32[]{:S(2)}, u32[]{:S(2)}) collective-permute-start(f32[8,2,8,512]{3,0,1,2:T(8,128)S(1)} %pad_maximum_fusion.65), channel_id=1, source_target_pairs={{0,4},{4,0},{1,5},{5,1},{2,6},{6,2},{3,7},{7,3},{8,12},{12,8},{9,1... | collective-permute-start | bytes 786440 | tf_op jit(solution)/shard_map/ppermute | solution.py:33
  4.8 3.7 %collective-permute-start = (f32[1,8,8,512]{3,0,1,2:T(1,128)S(1)}, f32[1,8,8,512]{3,0,1,2:T(1,128)S(1)}, u32[]{:S(2)}, u32[]{:S(2)}) collective-permute-start(f32[1,8,8,512]{3,0,1,2:T(1,128)S(1)} %get-tuple-element.8), channel_id=1, source_target_pairs={{0,24},{8,0},{16,8},{24,16},{1,25},{9,1},{17,9},{25,17},{2,26},{10... | collective-permute-start | bytes 393224 | tf_op jit(solution)/shard_map/ppermute | solution.py:23
  8.9 0.7 copy-done.24
  9.5 0.7 constant_dynamic-slice_fusion
  11.7 0.9 %bitcast_dynamic-update-slice_fusion.3 = f32[512,512]{1,0:T(8,128)S(1)} fusion(f32[512,512]{1,0:T(8,128)S(1)} %broadcast_in_dim.213, s32[]{:T(128)S(6)} %select_n.61, s32[]{:T(128)S(6)} %select_n.62, f32[1,128,128]{2,1,0:T(8,128)} %param.7), kind=kLoop, calls=%fused_computation.295 | loop fusion | bytes 131080 | tf_op jit(solution)/shard_map/dynamic_update_slice | solution.py:207
  12.6 0.8 broadcast_multiply_fusion.1
  13.6 2.2 %collective-permute-done.1 = f32[1,8,8,512]{3,0,1,2:T(1,128)S(1)} collective-permute-done((f32[1,8,8,512]{3,0,1,2:T(1,128)S(1)}, f32[1,8,8,512]{3,0,1,2:T(1,128)S(1)}, u32[]{:S(2)}, u32[]{:S(2)}) %collective-permute-start.1) | collective-permute-done | bytes 131104 | tf_op jit(solution)/shard_map/ppermute | solution.py:23
  15.9 1.9 %collective-permute-done.4 = f32[8,8,1,512]{3,0,1,2:T(8,128)S(1)} collective-permute-done((f32[8,8,1,512]{3,0,1,2:T(8,128)S(1)}, f32[8,8,1,512]{3,0,1,2:T(8,128)S(1)}, u32[]{:S(2)}, u32[]{:S(2)}) %collective-permute-start.4) | collective-permute-done | bytes 131104 | tf_op jit(solution)/shard_map/ppermute | solution.py:23
  17.8 1.5 %convert_subtract_fusion.1 = f32[8,8,8,512]{3,0,1,2:T(8,128)S(1)} fusion(f32[8,8,1,512]{3,0,1,2:T(8,128)S(1)} %collective-permute-done.4, f32[10,1,8,512]{3,0,1,2:T(8,128)S(1)} %pad.114, f32[10,1,8,512]{3,0,1,2:T(8,128)S(1)} %pad.115, f32[1,8,8,512]{3,0,1,2:T(1,128)S(1)} %collective-permute-done, f32[8,8,8,512]{3,0,1,2:T(8,128)S(1)} %convert_multiply_fusion.1, ...), kind=kLoop, calls=%fused_computation.1 | loop fusion | flops 8912896 | bytes 3473408 | tf_op jit(solution)/shard_map/sub | solution.py:216
  19.4 0.6 reshape.367
  20.0 0.7 reduce_sum.27
  20.9 0.6 collective-permute-start.7
  21.5 3.8 %collective-permute-start.5 = (f32[1,4,4,512]{3,0,1,2:T(1,128)S(1)}, f32[1,4,4,512]{3,0,1,2:T(1,128)S(1)}, u32[]{:S(2)}, u32[]{:S(2)}) collective-permute-start(f32[1,4,4,512]{3,0,1,2:T(1,128)S(1)} %get-tuple-element.42), channel_id=1, source_target_pairs={{0,24},{8,0},{16,8},{24,16},{1,25},{9,1},{17,9},{25,17},{2,26},{10... | collective-permute-start | bytes 98312 | tf_op jit(solution)/shard_map/ppermute | solution.py:23
  25.9 0.9 %collective-permute-done.5 = f32[1,4,4,512]{3,0,1,2:T(1,128)S(1)} collective-permute-done((f32[1,4,4,512]{3,0,1,2:T(1,128)S(1)}, f32[1,4,4,512]{3,0,1,2:T(1,128)S(1)}, u32[]{:S(2)}, u32[]{:S(2)}) %collective-permute-start.5) | collective-permute-done | bytes 32800 | tf_op jit(solution)/shard_map/ppermute | solution.py:23
  26.9 3.2 %collective-permute-start.23 = (f32[1,128,128]{2,1,0:T(8,128)}, f32[1,128,128]{2,1,0:T(8,128)S(1)}, u32[]{:S(2)}, u32[]{:S(2)}) collective-permute-start(f32[1,128,128]{2,1,0:T(8,128)} %param.7), channel_id=1, source_target_pairs={{0,16},{8,24},{16,0},{24,8},{1,17},{9,25},{17,1},{25,9},{2,18},{10... | collective-permute-start | bytes 196616 | tf_op jit(solution)/shard_map/ppermute | solution.py:23
  30.1 0.9 %collective-permute-done.6 = f32[1,4,4,512]{3,0,1,2:T(1,128)S(1)} collective-permute-done((f32[1,4,4,512]{3,0,1,2:T(1,128)S(1)}, f32[1,4,4,512]{3,0,1,2:T(1,128)S(1)}, u32[]{:S(2)}, u32[]{:S(2)}) %collective-permute-start.6) | collective-permute-done | bytes 32800 | tf_op jit(solution)/shard_map/ppermute | solution.py:23
  31.8 1.7 %collective-permute-start.10 = (f32[2,2,2,512]{3,0,1,2:T(2,128)S(1)}, f32[2,2,2,512]{3,0,1,2:T(2,128)S(1)}, u32[]{:S(2)}, u32[]{:S(2)}) collective-permute-start(f32[2,2,2,512]{3,0,1,2:T(2,128)S(1)} %broadcast_multiply_fusion.4), channel_id=1, source_target_pairs={{0,24},{8,0},{16,8},{24,16},{1,25},{9,1},{17,9},{25,17},{2,26},{10... | collective-permute-start | bytes 49160 | tf_op jit(solution)/shard_map/ppermute | solution.py:23
  33.5 0.5 collective-permute-start.11
  34.0 1.5 %collective-permute-start.12 = (f32[2,2,2,512]{3,0,1,2:T(2,128)S(1)}, f32[2,2,2,512]{3,0,1,2:T(2,128)S(1)}, u32[]{:S(2)}, u32[]{:S(2)}) collective-permute-start(f32[2,2,2,512]{3,0,1,2:T(2,128)S(1)} %broadcast_multiply_fusion.4), channel_id=1, source_target_pairs={{0,8},{8,16},{16,24},{24,0},{1,9},{9,17},{17,25},{25,1},{2,10},{10... | collective-permute-start | bytes 49160 | tf_op jit(solution)/shard_map/ppermute | solution.py:23
  39.4 2.4 %collective-permute-start.24 = (f32[1,128,128]{2,1,0:T(8,128)}, f32[1,128,128]{2,1,0:T(8,128)}, u32[]{:S(2)}, u32[]{:S(2)}) collective-permute-start(f32[1,128,128]{2,1,0:T(8,128)} %param.7), channel_id=1, source_target_pairs={{0,24},{8,0},{16,8},{24,16},{1,25},{9,1},{17,9},{25,17},{2,26},{10... | collective-permute-start | bytes 196616 | tf_op jit(solution)/shard_map/ppermute | solution.py:23
  41.8 1.6 %collective-permute-start.13 = (f32[8,2,2,512]{3,0,1,2:T(8,128)S(1)}, f32[8,2,2,512]{3,0,1,2:T(8,128)S(1)}, u32[]{:S(2)}, u32[]{:S(2)}) collective-permute-start(f32[8,2,2,512]{3,0,1,2:T(8,128)S(1)} %pad_maximum_fusion.148), channel_id=1, source_target_pairs={{0,4},{4,0},{1,5},{5,1},{2,6},{6,2},{3,7},{7,3},{8,12},{12,8},{9,1... | collective-permute-start | bytes 196616 | tf_op jit(solution)/shard_map/ppermute | solution.py:23
  43.3 0.8 %bitcast_dynamic-update-slice_fusion.2 = f32[512,512]{1,0:T(8,128)S(1)} fusion(f32[512,512]{1,0:T(8,128)S(1)} %copy-done.2, s32[]{:T(128)S(6)} %select_n.65, s32[]{:T(128)S(6)} %select_n.66, f32[1,128,128]{2,1,0:T(8,128)} %collective-permute-done.22), kind=kLoop, calls=%fused_computation.294 | loop fusion | bytes 131080 | tf_op jit(solution)/shard_map/dynamic_update_slice | solution.py:207
  44.2 1.9 %collective-permute-done.13 = f32[8,2,2,512]{3,0,1,2:T(8,128)S(1)} collective-permute-done((f32[8,2,2,512]{3,0,1,2:T(8,128)S(1)}, f32[8,2,2,512]{3,0,1,2:T(8,128)S(1)}, u32[]{:S(2)}, u32[]{:S(2)}) %collective-permute-start.13) | collective-permute-done | bytes 65568 | tf_op jit(solution)/shard_map/ppermute | solution.py:23
  46.2 1.3 %collective-permute-start.15 = (f32[8,4,2,512]{3,0,1,2:T(8,128)S(1)}, f32[8,4,2,512]{3,0,1,2:T(8,128)S(1)}, u32[]{:S(2)}, u32[]{:S(2)}) collective-permute-start(f32[8,4,2,512]{3,0,1,2:T(8,128)S(1)} %pad_maximum_fusion.98), channel_id=1, source_target_pairs={{0,2},{1,3},{2,0},{3,1},{4,6},{5,7},{6,4},{7,5},{8,10},{9,11},{10,... | collective-permute-start | bytes 393224 | tf_op jit(solution)/shard_map/ppermute | solution.py:23
  47.6 1.7 %collective-permute-done.14 = f32[8,4,2,512]{3,0,1,2:T(8,128)S(1)} collective-permute-done((f32[8,4,2,512]{3,0,1,2:T(8,128)S(1)}, f32[8,4,2,512]{3,0,1,2:T(8,128)S(1)}, u32[]{:S(2)}, u32[]{:S(2)}) %collective-permute-start.14) | collective-permute-done | bytes 131104 | tf_op jit(solution)/shard_map/ppermute | solution.py:23
  49.3 4.9 %collective-permute-done.15 = f32[8,4,2,512]{3,0,1,2:T(8,128)S(1)} collective-permute-done((f32[8,4,2,512]{3,0,1,2:T(8,128)S(1)}, f32[8,4,2,512]{3,0,1,2:T(8,128)S(1)}, u32[]{:S(2)}, u32[]{:S(2)}) %collective-permute-start.15) | collective-permute-done | bytes 131104 | tf_op jit(solution)/shard_map/ppermute | solution.py:23
  57.3 0.5 fusion.29
  58.2 0.7 copy-done.15
  59.2 0.7 copy-done.21
  59.9 0.7 copy-done.17
  60.7 0.7 copy-done.19
  61.9 0.6 fusion.114
  62.5 0.6 pad_maximum_fusion.149
  63.1 1.5 %collective-permute-start.19 = (f32[4,2,4,512]{3,0,1,2:T(4,128)}, f32[4,2,4,512]{3,0,1,2:T(4,128)}, u32[]{:S(2)}, u32[]{:S(2)}) collective-permute-start(f32[4,2,4,512]{3,0,1,2:T(4,128)} %pad_maximum_fusion.149), channel_id=1, source_target_pairs={{0,4},{4,0},{1,5},{5,1},{2,6},{6,2},{3,7},{7,3},{8,12},{12,8},{9,1... | collective-permute-start | bytes 196616 | tf_op jit(solution)/shard_map/ppermute | solution.py:33
  64.6 0.6 collective-permute-start.17
  65.3 1.4 %collective-permute-start.18 = (f32[1,4,4,512]{3,0,1,2:T(1,128)S(1)}, f32[1,4,4,512]{3,0,1,2:T(1,128)S(1)}, u32[]{:S(2)}, u32[]{:S(2)}) collective-permute-start(f32[1,4,4,512]{3,0,1,2:T(1,128)S(1)} %get-tuple-element.35), channel_id=1, source_target_pairs={{0,8},{8,16},{16,24},{24,0},{1,9},{9,17},{17,25},{25,1},{2,10},{10... | collective-permute-start | bytes 98312 | tf_op jit(solution)/shard_map/ppermute | solution.py:23
  66.7 1.7 %collective-permute-start.20 = (f32[4,4,1,512]{3,0,1,2:T(4,128)}, f32[4,4,1,512]{3,0,1,2:T(4,128)S(1)}, u32[]{:S(2)}, u32[]{:S(2)}) collective-permute-start(f32[4,4,1,512]{3,0,1,2:T(4,128)} %get-tuple-element.33), channel_id=1, source_target_pairs={{0,3},{1,0},{2,1},{3,2},{4,7},{5,4},{6,5},{7,6},{8,11},{9,8},{10,9... | collective-permute-start | bytes 98312 | tf_op jit(solution)/shard_map/ppermute | solution.py:23
  68.4 0.8 %bitcast_dynamic-update-slice_fusion = f32[512,512]{1,0:T(8,128)S(1)} fusion(f32[512,512]{1,0:T(8,128)S(1)} %bitcast_dynamic-update-slice_fusion.1, s32[]{:T(128)S(6)} %select_n.73, s32[]{:T(128)S(6)} %select_n.74, f32[1,128,128]{2,1,0:T(8,128)} %collective-permute-done.24), kind=kLoop, calls=%fused_computation.292 | loop fusion | bytes 131080 | tf_op jit(solution)/shard_map/dynamic_update_slice | solution.py:207
  70.3 0.7 collective-permute-done.18
  71.5 0.8 copy-done.4
  72.3 0.8 add.413
  73.2 0.8 add.414
  74.1 0.9 %copy-done.8 = f32[8,8,1,512]{3,0,1,2:T(8,128)S(1)} copy-done((f32[8,8,1,512]{3,0,1,2:T(8,128)S(1)}, f32[8,8,1,512]{3,0,1,2:T(8,128)}, u32[]{:S(2)}) %copy-start.8) | copy-done | bytes 131096
  75.0 0.8 slice_bitcast_fusion
  76.1 0.8 %copy-done.11 = f32[1,8,8,512]{3,0,1,2:T(1,128)S(1)} copy-done((f32[1,8,8,512]{3,0,1,2:T(1,128)S(1)}, f32[1,8,8,512]{3,0,1,2:T(1,128)}, u32[]{:S(2)}) %copy-start.11) | copy-done | bytes 131096
  77.0 1.7 %fusion.3 = f32[8,8,8,512]{3,0,1,2:T(8,128)S(1)} fusion(f32[8,8,8,512]{3,0,1,2:T(8,128)S(1)} %bitcast_add_fusion, f32[8,8,1,512]{3,0,1,2:T(8,128)S(1)} %bitcast_add_fusion.2, f32[10,1,8,512]{3,0,1,2:T(8,128)S(1)} %pad.146, f32[10,1,8,512]{3,0,1,2:T(8,128)S(1)} %pad.147, f32[1,8,8,512]{3,0,1,2:T(1,128)S(1)} %copy-done.11, f32[1,8,8,512]{3,0,1,2:T(1,128)S(1)} %copy-done.12, ...), kind=kLoop, calls=%fused_computation.8 | loop fusion | flops 9961472 | bytes 3620864 | tf_op jit(solution)/shard_map/mul | solution.py:236
  78.7 3.2 %convolution_convert_fusion = bf16[8,8,8,512]{3,2,1,0:T(8,128)(2,1)} fusion(f32[512,512]{1,0:T(8,128)S(1)} %bitcast_dynamic-update-slice_fusion, f32[8,8,8,512]{3,0,1,2:T(8,128)S(1)} %fusion.3), kind=kOutput, calls=%fused_computation.4 | convolution fusion | flops 1610874880 | bytes 2621440 | tf_op jit(solution)/shard_map/dot_general | solution.py:241
  (198 shorter events, 8.8 us)
Async XLA Ops:
  1.5 11.9 %collective-permute-start.2 = (f32[8,2,8,512]{3,0,1,2:T(8,128)S(1)}, f32[8,2,8,512]{3,0,1,2:T(8,128)S(1)}, u32[]{:S(2)}, u32[]{:S(2)}) collective-permute-start(f32[8,2,8,512]{3,0,1,2:T(8,128)S(1)} %pad_maximum_fusion.65), channel_id=1, source_target_pairs={{0,4},{4,0},{1,5},{5,1},{2,6},{6,2},{3,7},{7,3},{8,12},{12,8},{9,1... | collective-permute-start | bytes 786440 | tf_op jit(solution)/shard_map/ppermute | solution.py:33
  4.8 8.9 %collective-permute-start = (f32[1,8,8,512]{3,0,1,2:T(1,128)S(1)}, f32[1,8,8,512]{3,0,1,2:T(1,128)S(1)}, u32[]{:S(2)}, u32[]{:S(2)}) collective-permute-start(f32[1,8,8,512]{3,0,1,2:T(1,128)S(1)} %get-tuple-element.8), channel_id=1, source_target_pairs={{0,24},{8,0},{16,8},{24,16},{1,25},{9,1},{17,9},{25,17},{2,26},{10... | collective-permute-start | bytes 393224 | tf_op jit(solution)/shard_map/ppermute | solution.py:23
  8.4 7.5 %collective-permute-start.1 = (f32[1,8,8,512]{3,0,1,2:T(1,128)S(1)}, f32[1,8,8,512]{3,0,1,2:T(1,128)S(1)}, u32[]{:S(2)}, u32[]{:S(2)}) collective-permute-start(f32[1,8,8,512]{3,0,1,2:T(1,128)S(1)} %get-tuple-element.7), channel_id=1, source_target_pairs={{0,8},{8,16},{16,24},{24,0},{1,9},{9,17},{17,25},{25,1},{2,10},{10... | collective-permute-start | bytes 393224 | tf_op jit(solution)/shard_map/ppermute | solution.py:23
  8.4 7.4 %collective-permute-start.3 = (f32[8,8,1,512]{3,0,1,2:T(8,128)S(1)}, f32[8,8,1,512]{3,0,1,2:T(8,128)S(1)}, u32[]{:S(2)}, u32[]{:S(2)}) collective-permute-start(f32[8,8,1,512]{3,0,1,2:T(8,128)S(1)} %get-tuple-element.5), channel_id=1, source_target_pairs={{0,3},{1,0},{2,1},{3,2},{4,7},{5,4},{6,5},{7,6},{8,11},{9,8},{10,9... | collective-permute-start | bytes 393224 | tf_op jit(solution)/shard_map/ppermute | solution.py:23
  8.9 34.5 %collective-permute-start.22 = (f32[1,128,128]{2,1,0:T(8,128)}, f32[1,128,128]{2,1,0:T(8,128)}, u32[]{:S(2)}, u32[]{:S(2)}) collective-permute-start(f32[1,128,128]{2,1,0:T(8,128)} %param.7), channel_id=1, source_target_pairs={{0,8},{8,16},{16,24},{24,0},{1,9},{9,17},{17,25},{25,1},{2,10},{10... | collective-permute-start | bytes 196616 | tf_op jit(solution)/shard_map/ppermute | solution.py:23
  8.9 0.7 copy-start.24
  10.2 1.3 %copy-start.25 = (s32[3,2,512]{2,1,0:T(2,128)S(1)}, s32[3,2,512]{2,1,0:T(2,128)}, u32[]{:S(2)}) copy-start(s32[3,2,512]{2,1,0:T(2,128)} %param.5) | copy-start | bytes 36868
  12.5 3.4 %copy-start.1 = (f32[512,512]{1,0:T(8,128)}, f32[512,512]{1,0:T(8,128)S(1)}, u32[]{:S(2)}) copy-start(f32[512,512]{1,0:T(8,128)S(1)} %bitcast_dynamic-update-slice_fusion.3) | copy-start | bytes 3145732
  13.4 4.4 %collective-permute-start.4 = (f32[8,8,1,512]{3,0,1,2:T(8,128)S(1)}, f32[8,8,1,512]{3,0,1,2:T(8,128)S(1)}, u32[]{:S(2)}, u32[]{:S(2)}) collective-permute-start(f32[8,8,1,512]{3,0,1,2:T(8,128)S(1)} %get-tuple-element.6), channel_id=1, source_target_pairs={{0,1},{1,2},{2,3},{3,0},{4,5},{5,6},{6,7},{7,4},{8,9},{9,10},{10,1... | collective-permute-start | bytes 393224 | tf_op jit(solution)/shard_map/ppermute | solution.py:23
  13.5 4.2 %copy-start = (bf16[8,8,8,512]{3,2,1,0:T(8,128)(2,1)S(1)}, bf16[8,8,8,512]{3,2,1,0:T(8,128)(2,1)}, u32[]{:S(2)}) copy-start(bf16[8,8,8,512]{3,2,1,0:T(8,128)(2,1)} %param.4) | copy-start | bytes 1572868
  13.6 5.7 %copy-start.3 = (f32[1,8,8,512]{3,0,1,2:T(1,128)}, f32[1,8,8,512]{3,0,1,2:T(1,128)S(1)}, u32[]{:S(2)}) copy-start(f32[1,8,8,512]{3,0,1,2:T(1,128)S(1)} %collective-permute-done) | copy-start | bytes 393220
  15.9 3.5 %copy-start.5 = (f32[1,8,8,512]{3,0,1,2:T(1,128)}, f32[1,8,8,512]{3,0,1,2:T(1,128)S(1)}, u32[]{:S(2)}) copy-start(f32[1,8,8,512]{3,0,1,2:T(1,128)S(1)} %collective-permute-done.1) | copy-start | bytes 393220
  15.9 3.5 %copy-start.7 = (f32[8,8,1,512]{3,0,1,2:T(8,128)}, f32[8,8,1,512]{3,0,1,2:T(8,128)S(1)}, u32[]{:S(2)}) copy-start(f32[8,8,1,512]{3,0,1,2:T(8,128)S(1)} %collective-permute-done.3) | copy-start | bytes 393220
  17.8 1.6 %copy-start.9 = (f32[8,8,1,512]{3,0,1,2:T(8,128)}, f32[8,8,1,512]{3,0,1,2:T(8,128)S(1)}, u32[]{:S(2)}) copy-start(f32[8,8,1,512]{3,0,1,2:T(8,128)S(1)} %collective-permute-done.4) | copy-start | bytes 393220
  20.8 22.6 %copy-start.2 = (f32[512,512]{1,0:T(8,128)S(1)}, f32[512,512]{1,0:T(8,128)}, u32[]{:S(2)}) copy-start(f32[512,512]{1,0:T(8,128)} %copy-done.1) | copy-start | bytes 3145732
  20.9 4.4 %collective-permute-start.7 = (f32[4,2,4,512]{3,0,1,2:T(4,128)S(1)}, f32[4,2,4,512]{3,0,1,2:T(4,128)S(1)}, u32[]{:S(2)}, u32[]{:S(2)}) collective-permute-start(f32[4,2,4,512]{3,0,1,2:T(4,128)S(1)} %pad_maximum_fusion.147), channel_id=1, source_target_pairs={{0,4},{4,0},{1,5},{5,1},{2,6},{6,2},{3,7},{7,3},{8,12},{12,8},{9,1... | collective-permute-start | bytes 196616 | tf_op jit(solution)/shard_map/ppermute | solution.py:33
  21.5 5.4 %collective-permute-start.5 = (f32[1,4,4,512]{3,0,1,2:T(1,128)S(1)}, f32[1,4,4,512]{3,0,1,2:T(1,128)S(1)}, u32[]{:S(2)}, u32[]{:S(2)}) collective-permute-start(f32[1,4,4,512]{3,0,1,2:T(1,128)S(1)} %get-tuple-element.42), channel_id=1, source_target_pairs={{0,24},{8,0},{16,8},{24,16},{1,25},{9,1},{17,9},{25,17},{2,26},{10... | collective-permute-start | bytes 98312 | tf_op jit(solution)/shard_map/ppermute | solution.py:23
  25.3 5.7 %collective-permute-start.6 = (f32[1,4,4,512]{3,0,1,2:T(1,128)S(1)}, f32[1,4,4,512]{3,0,1,2:T(1,128)S(1)}, u32[]{:S(2)}, u32[]{:S(2)}) collective-permute-start(f32[1,4,4,512]{3,0,1,2:T(1,128)S(1)} %get-tuple-element.41), channel_id=1, source_target_pairs={{0,8},{8,16},{16,24},{24,0},{1,9},{9,17},{17,25},{25,1},{2,10},{10... | collective-permute-start | bytes 98312 | tf_op jit(solution)/shard_map/ppermute | solution.py:23
  25.3 5.7 %collective-permute-start.8 = (f32[4,4,1,512]{3,0,1,2:T(4,128)S(1)}, f32[4,4,1,512]{3,0,1,2:T(4,128)S(1)}, u32[]{:S(2)}, u32[]{:S(2)}) collective-permute-start(f32[4,4,1,512]{3,0,1,2:T(4,128)S(1)} %get-tuple-element.39), channel_id=1, source_target_pairs={{0,3},{1,0},{2,1},{3,2},{4,7},{5,4},{6,5},{7,6},{8,11},{9,8},{10,9... | collective-permute-start | bytes 98312 | tf_op jit(solution)/shard_map/ppermute | solution.py:23
  25.3 5.7 %collective-permute-start.9 = (f32[4,4,1,512]{3,0,1,2:T(4,128)S(1)}, f32[4,4,1,512]{3,0,1,2:T(4,128)S(1)}, u32[]{:S(2)}, u32[]{:S(2)}) collective-permute-start(f32[4,4,1,512]{3,0,1,2:T(4,128)S(1)} %get-tuple-element.40), channel_id=1, source_target_pairs={{0,1},{1,2},{2,3},{3,0},{4,5},{5,6},{6,7},{7,4},{8,9},{9,10},{10,1... | collective-permute-start | bytes 98312 | tf_op jit(solution)/shard_map/ppermute | solution.py:23
  26.9 4.4 %copy-start.16 = (f32[1,4,4,512]{3,0,1,2:T(1,128)}, f32[1,4,4,512]{3,0,1,2:T(1,128)S(1)}, u32[]{:S(2)}) copy-start(f32[1,4,4,512]{3,0,1,2:T(1,128)S(1)} %collective-permute-done.5) | copy-start | bytes 98308
  26.9 20.7 %collective-permute-start.23 = (f32[1,128,128]{2,1,0:T(8,128)}, f32[1,128,128]{2,1,0:T(8,128)S(1)}, u32[]{:S(2)}, u32[]{:S(2)}) collective-permute-start(f32[1,128,128]{2,1,0:T(8,128)} %param.7), channel_id=1, source_target_pairs={{0,16},{8,24},{16,0},{24,8},{1,17},{9,25},{17,1},{25,9},{2,18},{10... | collective-permute-start | bytes 196616 | tf_op jit(solution)/shard_map/ppermute | solution.py:23
  31.0 0.6 copy-start.22
  31.8 7.5 %collective-permute-start.10 = (f32[2,2,2,512]{3,0,1,2:T(2,128)S(1)}, f32[2,2,2,512]{3,0,1,2:T(2,128)S(1)}, u32[]{:S(2)}, u32[]{:S(2)}) collective-permute-start(f32[2,2,2,512]{3,0,1,2:T(2,128)S(1)} %broadcast_multiply_fusion.4), channel_id=1, source_target_pairs={{0,24},{8,0},{16,8},{24,16},{1,25},{9,1},{17,9},{25,17},{2,26},{10... | collective-permute-start | bytes 49160 | tf_op jit(solution)/shard_map/ppermute | solution.py:23
  33.5 8.2 %collective-permute-start.11 = (f32[2,2,2,512]{3,0,1,2:T(2,128)S(1)}, f32[2,2,2,512]{3,0,1,2:T(2,128)S(1)}, u32[]{:S(2)}, u32[]{:S(2)}) collective-permute-start(f32[2,2,2,512]{3,0,1,2:T(2,128)S(1)} %broadcast_multiply_fusion.4), channel_id=1, source_target_pairs={{0,16},{8,24},{16,0},{24,8},{1,17},{9,25},{17,1},{25,9},{2,18},{10... | collective-permute-start | bytes 49160 | tf_op jit(solution)/shard_map/ppermute | solution.py:23
  34.0 7.7 %collective-permute-start.12 = (f32[2,2,2,512]{3,0,1,2:T(2,128)S(1)}, f32[2,2,2,512]{3,0,1,2:T(2,128)S(1)}, u32[]{:S(2)}, u32[]{:S(2)}) collective-permute-start(f32[2,2,2,512]{3,0,1,2:T(2,128)S(1)} %broadcast_multiply_fusion.4), channel_id=1, source_target_pairs={{0,8},{8,16},{16,24},{24,0},{1,9},{9,17},{17,25},{25,1},{2,10},{10... | collective-permute-start | bytes 49160 | tf_op jit(solution)/shard_map/ppermute | solution.py:23
  39.4 27.3 %collective-permute-start.24 = (f32[1,128,128]{2,1,0:T(8,128)}, f32[1,128,128]{2,1,0:T(8,128)}, u32[]{:S(2)}, u32[]{:S(2)}) collective-permute-start(f32[1,128,128]{2,1,0:T(8,128)} %param.7), channel_id=1, source_target_pairs={{0,24},{8,0},{16,8},{24,16},{1,25},{9,1},{17,9},{25,17},{2,26},{10... | collective-permute-start | bytes 196616 | tf_op jit(solution)/shard_map/ppermute | solution.py:23
  41.8 4.3 %collective-permute-start.13 = (f32[8,2,2,512]{3,0,1,2:T(8,128)S(1)}, f32[8,2,2,512]{3,0,1,2:T(8,128)S(1)}, u32[]{:S(2)}, u32[]{:S(2)}) collective-permute-start(f32[8,2,2,512]{3,0,1,2:T(8,128)S(1)} %pad_maximum_fusion.148), channel_id=1, source_target_pairs={{0,4},{4,0},{1,5},{5,1},{2,6},{6,2},{3,7},{7,3},{8,12},{12,8},{9,1... | collective-permute-start | bytes 196616 | tf_op jit(solution)/shard_map/ppermute | solution.py:23
  46.1 3.2 %collective-permute-start.14 = (f32[8,4,2,512]{3,0,1,2:T(8,128)S(1)}, f32[8,4,2,512]{3,0,1,2:T(8,128)S(1)}, u32[]{:S(2)}, u32[]{:S(2)}) collective-permute-start(f32[8,4,2,512]{3,0,1,2:T(8,128)S(1)} %pad_maximum_fusion.98), channel_id=1, source_target_pairs={{0,3},{1,0},{2,1},{3,2},{4,7},{5,4},{6,5},{7,6},{8,11},{9,8},{10,9... | collective-permute-start | bytes 393224 | tf_op jit(solution)/shard_map/ppermute | solution.py:23
  46.2 8.0 %collective-permute-start.15 = (f32[8,4,2,512]{3,0,1,2:T(8,128)S(1)}, f32[8,4,2,512]{3,0,1,2:T(8,128)S(1)}, u32[]{:S(2)}, u32[]{:S(2)}) collective-permute-start(f32[8,4,2,512]{3,0,1,2:T(8,128)S(1)} %pad_maximum_fusion.98), channel_id=1, source_target_pairs={{0,2},{1,3},{2,0},{3,1},{4,6},{5,7},{6,4},{7,5},{8,10},{9,11},{10,... | collective-permute-start | bytes 393224 | tf_op jit(solution)/shard_map/ppermute | solution.py:23
  47.5 7.1 %collective-permute-start.16 = (f32[8,4,2,512]{3,0,1,2:T(8,128)S(1)}, f32[8,4,2,512]{3,0,1,2:T(8,128)S(1)}, u32[]{:S(2)}, u32[]{:S(2)}) collective-permute-start(f32[8,4,2,512]{3,0,1,2:T(8,128)S(1)} %pad_maximum_fusion.98), channel_id=1, source_target_pairs={{0,1},{1,2},{2,3},{3,0},{4,5},{5,6},{6,7},{7,4},{8,9},{9,10},{10,1... | collective-permute-start | bytes 393224 | tf_op jit(solution)/shard_map/ppermute | solution.py:23
  58.1 0.8 %copy-start.15 = (f32[4,2,4,512]{3,0,1,2:T(4,128)S(1)}, f32[4,2,4,512]{3,0,1,2:T(4,128)}, u32[]{:S(2)}) copy-start(f32[4,2,4,512]{3,0,1,2:T(4,128)} %copy-done.14) | copy-start | bytes 196612
  59.1 0.8 copy-start.21
  59.9 0.8 copy-start.17
  60.7 0.8 copy-start.19
  60.7 0.8 copy-start.23
  63.1 11.9 %collective-permute-start.19 = (f32[4,2,4,512]{3,0,1,2:T(4,128)}, f32[4,2,4,512]{3,0,1,2:T(4,128)}, u32[]{:S(2)}, u32[]{:S(2)}) collective-permute-start(f32[4,2,4,512]{3,0,1,2:T(4,128)} %pad_maximum_fusion.149), channel_id=1, source_target_pairs={{0,4},{4,0},{1,5},{5,1},{2,6},{6,2},{3,7},{7,3},{8,12},{12,8},{9,1... | collective-permute-start | bytes 196616 | tf_op jit(solution)/shard_map/ppermute | solution.py:33
  64.6 5.4 %collective-permute-start.17 = (f32[1,4,4,512]{3,0,1,2:T(1,128)S(1)}, f32[1,4,4,512]{3,0,1,2:T(1,128)S(1)}, u32[]{:S(2)}, u32[]{:S(2)}) collective-permute-start(f32[1,4,4,512]{3,0,1,2:T(1,128)S(1)} %get-tuple-element.36), channel_id=1, source_target_pairs={{0,24},{8,0},{16,8},{24,16},{1,25},{9,1},{17,9},{25,17},{2,26},{10... | collective-permute-start | bytes 98312 | tf_op jit(solution)/shard_map/ppermute | solution.py:23
  65.3 5.7 %collective-permute-start.18 = (f32[1,4,4,512]{3,0,1,2:T(1,128)S(1)}, f32[1,4,4,512]{3,0,1,2:T(1,128)S(1)}, u32[]{:S(2)}, u32[]{:S(2)}) collective-permute-start(f32[1,4,4,512]{3,0,1,2:T(1,128)S(1)} %get-tuple-element.35), channel_id=1, source_target_pairs={{0,8},{8,16},{16,24},{24,0},{1,9},{9,17},{17,25},{25,1},{2,10},{10... | collective-permute-start | bytes 98312 | tf_op jit(solution)/shard_map/ppermute | solution.py:23
  66.6 4.6 %collective-permute-start.21 = (f32[4,4,1,512]{3,0,1,2:T(4,128)}, f32[4,4,1,512]{3,0,1,2:T(4,128)S(1)}, u32[]{:S(2)}, u32[]{:S(2)}) collective-permute-start(f32[4,4,1,512]{3,0,1,2:T(4,128)} %get-tuple-element.34), channel_id=1, source_target_pairs={{0,1},{1,2},{2,3},{3,0},{4,5},{5,6},{6,7},{7,4},{8,9},{9,10},{10,1... | collective-permute-start | bytes 98312 | tf_op jit(solution)/shard_map/ppermute | solution.py:23
  66.7 4.7 %collective-permute-start.20 = (f32[4,4,1,512]{3,0,1,2:T(4,128)}, f32[4,4,1,512]{3,0,1,2:T(4,128)S(1)}, u32[]{:S(2)}, u32[]{:S(2)}) collective-permute-start(f32[4,4,1,512]{3,0,1,2:T(4,128)} %get-tuple-element.33), channel_id=1, source_target_pairs={{0,3},{1,0},{2,1},{3,2},{4,7},{5,4},{6,5},{7,6},{8,11},{9,8},{10,9... | collective-permute-start | bytes 98312 | tf_op jit(solution)/shard_map/ppermute | solution.py:23
  71.3 0.9 %copy-start.4 = (f32[1,8,8,512]{3,0,1,2:T(1,128)S(1)}, f32[1,8,8,512]{3,0,1,2:T(1,128)}, u32[]{:S(2)}) copy-start(f32[1,8,8,512]{3,0,1,2:T(1,128)} %copy-done.3) | copy-start | bytes 393220
  72.2 0.9 %copy-start.6 = (f32[1,8,8,512]{3,0,1,2:T(1,128)S(1)}, f32[1,8,8,512]{3,0,1,2:T(1,128)}, u32[]{:S(2)}) copy-start(f32[1,8,8,512]{3,0,1,2:T(1,128)} %copy-done.5) | copy-start | bytes 393220
  73.2 0.9 %copy-start.10 = (f32[8,8,1,512]{3,0,1,2:T(8,128)S(1)}, f32[8,8,1,512]{3,0,1,2:T(8,128)}, u32[]{:S(2)}) copy-start(f32[8,8,1,512]{3,0,1,2:T(8,128)} %copy-done.9) | copy-start | bytes 393220
  74.1 0.9 %copy-start.8 = (f32[8,8,1,512]{3,0,1,2:T(8,128)S(1)}, f32[8,8,1,512]{3,0,1,2:T(8,128)}, u32[]{:S(2)}) copy-start(f32[8,8,1,512]{3,0,1,2:T(8,128)} %copy-done.7) | copy-start | bytes 393220
  76.0 0.9 %copy-start.11 = (f32[1,8,8,512]{3,0,1,2:T(1,128)S(1)}, f32[1,8,8,512]{3,0,1,2:T(1,128)}, u32[]{:S(2)}) copy-start(f32[1,8,8,512]{3,0,1,2:T(1,128)} %add.413) | copy-start | bytes 393220
  76.0 1.0 %copy-start.12 = (f32[1,8,8,512]{3,0,1,2:T(1,128)S(1)}, f32[1,8,8,512]{3,0,1,2:T(1,128)}, u32[]{:S(2)}) copy-start(f32[1,8,8,512]{3,0,1,2:T(1,128)} %add.414) | copy-start | bytes 393220
  76.0 1.0 %copy-start.13 = (f32[8,8,512]{2,0,1:T(8,128)S(1)}, f32[8,8,512]{2,0,1:T(8,128)}, u32[]{:S(2)}) copy-start(f32[8,8,512]{2,0,1:T(8,128)} %broadcast_multiply_fusion.1) | copy-start | bytes 393220
  (3 other events, 1.8 us)

commit v4 on v3

--- a/solution.py
+++ b/solution.py
@@ -43,7 +43,7 @@
     return [axis_faces(block, axis, dim) for axis, dim in GRID_AXES]
 
 
-def extend_axis(block, axis, dim, halo):
+def extend_axis(block, axis, dim, halo, extra=None):
     count = lax.axis_size(axis)
     size = block.shape[dim]
     reach = -(-halo // size)
@@ -54,13 +54,21 @@
         offsets = list(range(-reach, reach + 1))
         start = reach * size
     cache = {}
+    extras = {}
     pieces = []
     for offset in offsets:
         step = offset % count
         if step not in cache:
-            cache[step] = shifted(block, axis, step)
+            if extra is None or step == 0:
+                cache[step] = shifted(block, axis, step)
+                extras[step] = extra
+            else:
+                both = jnp.concatenate([block.reshape(-1), extra.reshape(-1)])
+                both = shifted(both, axis, step)
+                cache[step] = both[: block.size].reshape(block.shape)
+                extras[step] = both[block.size :].reshape(extra.shape)
         pieces.append(cache[step])
-    return jnp.concatenate(pieces, axis=dim), start
+    return jnp.concatenate(pieces, axis=dim), start, extras
 
 
 def level_coeffs(level_id):
@@ -116,18 +124,22 @@
     return jnp.concatenate(parts, axis=dim)
 
 
-def coarse_solve(rhs_two):
+def coarse_solve(rhs_two, tiles):
     extended = rhs_two
     starts = []
+    tiles_by_step = {}
     for axis, dim in GRID_AXES:
-        extended, start = extend_axis(extended, axis, dim, COARSE_HALO)
+        extra = tiles if axis == "gx" else None
+        extended, start, extras = extend_axis(extended, axis, dim, COARSE_HALO, extra)
+        if axis == "gx":
+            tiles_by_step = extras
         starts.append(start)
     width = extended.shape[3]
     chunks = 1
     while extended.size * 4 // chunks > CHUNK_BYTES and width % (2 * chunks * 128) == 0:
         chunks *= 2
     if chunks == 1:
-        return coarse_levels(extended, starts, rhs_two.shape)
+        return coarse_levels(extended, starts, rhs_two.shape), tiles_by_step
     part = width // chunks
 
     def one_chunk(k):
@@ -136,7 +148,7 @@
 
     outs = lax.map(one_chunk, jnp.arange(chunks))
     outs = jnp.moveaxis(outs, 0, 3)
-    return outs.reshape(outs.shape[:3] + (width,))
+    return outs.reshape(outs.shape[:3] + (width,)), tiles_by_step
 
 
 def coarse_levels(extended, starts, block_shape):
@@ -191,15 +203,17 @@
     return ((box_part[0][None, :] <= cells) & (cells < box_part[1][None, :])).astype(jnp.float32)
 
 
-def gram_matrix(inv_tiles, tile_pairs, orb_count):
+def gram_matrix(tiles_by_step, inv_tiles, tile_pairs, orb_count):
     count = lax.axis_size("gx")
     local = inv_tiles.shape[0]
     tile_edge = inv_tiles.shape[1]
     me = lax.axis_index("gx")
     total = jnp.zeros((orb_count, orb_count), jnp.float32)
-    for shift in range(count):
-        piece = shifted(inv_tiles, "gx", -shift)
-        owner = (me - shift) % count
+    for step in range(count):
+        piece = tiles_by_step.get(step)
+        if piece is None:
+            piece = inv_tiles if step == 0 else shifted(inv_tiles, "gx", step)
+        owner = (me + step) % count
         for slot in range(local):
             tile_id = owner * local + slot
             row = tile_pairs[tile_id, 0] * tile_edge
@@ -208,7 +222,7 @@
     return total
 
 
-def vcycle(residuals):
+def vcycle(residuals, inv_tiles):
     rhs_zero = residuals.astype(jnp.float32)
     center, coupling = level_coeffs(0)
     corr_zero = omega * rhs_zero / center
@@ -218,18 +232,18 @@
     corr_one = omega * rhs_one / center
     faces_one = all_faces(corr_one)
     rhs_two = restrict(rhs_one - stencil(corr_one, faces_one, 1))
-    post_two = coarse_solve(rhs_two)
+    post_two, tiles_by_step = coarse_solve(rhs_two, inv_tiles)
     inner_two = post_two[1:-1, 1:-1, 1:-1]
     post_one = post_smooth(
         1, corr_one, faces_one, rhs_one, inner_two, [coarse_faces(post_two, dim) for dim in range(3)]
     )
-    return post_smooth(0, corr_zero, faces_zero, rhs_zero, post_one, all_faces(post_one))
+    return post_smooth(0, corr_zero, faces_zero, rhs_zero, post_one, all_faces(post_one)), tiles_by_step
 
 
 def body(residuals, patch_box, tile_pairs, inv_tiles):
     size_a, size_b, size_c, orb_count = residuals.shape
-    gram = gram_matrix(inv_tiles, tile_pairs, orb_count)
-    correct = vcycle(residuals)
+    correct, tiles_by_step = vcycle(residuals, inv_tiles)
+    gram = gram_matrix(tiles_by_step, inv_tiles, tile_pairs, orb_count)
     mask_first = dim_mask(patch_box[0], lax.axis_index("gx") * size_a, size_a)
     mask_second = dim_mask(patch_box[1], lax.axis_index("gy") * size_b, size_b)
     mask_third = dim_mask(patch_box[2], lax.axis_index("gz") * size_c, size_c)
@@ -238,7 +252,7 @@
     )
     cell_count = size_a * size_b * size_c
     rows = precond.reshape(cell_count, orb_count)
-    mixed = jnp.dot(rows, gram, precision=lax.Precision.HIGHEST, preferred_element_type=jnp.float32)
+    mixed = jnp.dot(rows, gram, precision=lax.Precision.HIGH, preferred_element_type=jnp.float32)
     return mixed.reshape(size_a, size_b, size_c, orb_count).astype(jnp.bfloat16)
 
 

time: 82.7 us -> 79.7 us (0.964)
  starting transfers between devices: 29.8 us -> 22.1 us
  waiting for transfers between devices: 15.5 us -> 21.2 us
  matrix products: 3.19 us -> 2.25 us
    ppermute x22 -> x19, starting transfers between devices: 24.6 us -> 16.9 us  [shifted(): lax.ppermute(block, axis, [(j, (j - step) % count) for j in range(count)])]
    ppermute x22 -> x19, waiting for transfers between devices: 15.5 us -> 21.1 us  [shifted(): lax.ppermute(block, axis, [(j, (j - step) % count) for j in range(count)])]
    dynamic_update_slice x4, local copies, waits for them, and re-layouts: 2.55 us -> 0.03 us  [gram_matrix(): total = lax.dynamic_update_slice(total, piece[slot], (row, col))]
    unnamed x55 -> x64, local copies, waits for them, and re-layouts: 6.96 us -> 8.69 us
    dot_general x1, matrix products: 3.19 us -> 2.25 us  [body(): jnp.dot(rows, gram, precision=lax.Precision.HIGH, preferred_element_type=...]
  transfers between devices with their start and end apart: 25 -> 22, of which waited for: 9 -> 9; matrix products, arithmetic and copies ran while one was open for 20% -> 7% of each run, Pallas kernels for 0% -> 0%
where the time goes in v4:
time: 79.7 us; the launch traced here: 78.9 us
  starting transfers between devices  22.1 us (28%)
  waiting for transfers between devices  21.2 us (27%)
  local copies, waits for them, and re-layouts  14.7 us (18%)
  other arithmetic  12.6 us (16%)
  between operations  6.08 us (8%)
  matrix products  2.25 us (3%)
    ppermute x19, waiting for transfers between devices, shifted(): lax.ppermute(block, axis, [(j, (j - step) % count) for j in range(count)])  21.1 us
    ppermute x19, starting transfers between devices, shifted(): lax.ppermute(block, axis, [(j, (j - step) % count) for j in range(count)])  16.9 us
    unnamed x64, local copies, waits for them, and re-layouts  8.69 us
    ppermute x3, starting transfers between devices, axis_faces(): lax.ppermute(jnp.concatenate([first, last], axis=dim), axis, [(0, 1), (1,...  5.15 us
    dot_general x1, matrix products, body(): jnp.dot(rows, gram, precision=lax.Precision.HIGH, preferred_element_type=...  2.25 us
    mul x1, other arithmetic, body(): correct * (mask_first[:, None, None, :] * mask_second[None, :, None, :] *...  1.66 us
  transfers between devices with their start and end apart: 22, of which 9 were waited for; matrix products, arithmetic and copies ran while one was open for 7% of the time, Pallas kernels for 0%

profile of v4, /device:TPU:0, one launch (start us, length us, event | category | flops | bytes accessed | tf_op | source)
XLA Modules:
  0.0 78.9 jit_solution(17665251316406396512)
XLA Ops:
  0.0 1.4 %convert_multiply_fusion.1 = f32[8,8,8,512]{3,0,1,2:T(8,128)S(1)} fusion(bf16[8,8,8,512]{3,2,1,0:T(8,128)(2,1)} %param.4), kind=kLoop, calls=%fused_computation.3 | loop fusion | flops 524288 | bytes 1572864 | tf_op jit(solution)/shard_map/div | solution.py:228
  1.5 3.1 %collective-permute-start.2 = (f32[8,2,8,512]{3,0,1,2:T(8,128)S(1)}, f32[8,2,8,512]{3,0,1,2:T(8,128)S(1)}, u32[]{:S(2)}, u32[]{:S(2)}) collective-permute-start(f32[8,2,8,512]{3,0,1,2:T(8,128)S(1)} %pad_maximum_fusion.65), channel_id=1, source_target_pairs={{0,4},{4,0},{1,5},{5,1},{2,6},{6,2},{3,7},{7,3},{8,12},{12,8},{9,1... | collective-permute-start | bytes 786440 | tf_op jit(solution)/shard_map/ppermute | solution.py:33
  4.8 3.7 %collective-permute-start = (f32[1,8,8,512]{3,0,1,2:T(1,128)S(1)}, f32[1,8,8,512]{3,0,1,2:T(1,128)S(1)}, u32[]{:S(2)}, u32[]{:S(2)}) collective-permute-start(f32[1,8,8,512]{3,0,1,2:T(1,128)S(1)} %get-tuple-element.8), channel_id=1, source_target_pairs={{0,24},{8,0},{16,8},{24,16},{1,25},{9,1},{17,9},{25,17},{2,26},{10... | collective-permute-start | bytes 393224 | tf_op jit(solution)/shard_map/ppermute | solution.py:23
  9.0 0.7 copy-done.28
  9.7 0.7 constant_dynamic-slice_fusion
  11.8 0.7 copy-done.14
  12.6 0.8 %broadcast_multiply_fusion.1 = f32[8,8,512]{2,0,1:T(8,128)} fusion(f32[8,512]{1,0:T(8,128)S(1)} %get-tuple-element.87, f32[8,512]{1,0:T(8,128)S(1)} %get-tuple-element.88), kind=kLoop, calls=%fused_computation.300 | loop fusion | flops 32768 | bytes 163840 | tf_op jit(solution)/shard_map/mul | solution.py:251
  13.5 1.7 %collective-permute-done.1 = f32[1,8,8,512]{3,0,1,2:T(1,128)S(1)} collective-permute-done((f32[1,8,8,512]{3,0,1,2:T(1,128)S(1)}, f32[1,8,8,512]{3,0,1,2:T(1,128)S(1)}, u32[]{:S(2)}, u32[]{:S(2)}) %collective-permute-start.1) | collective-permute-done | bytes 131104 | tf_op jit(solution)/shard_map/ppermute | solution.py:23
  15.2 1.6 %convert_subtract_fusion.1 = f32[8,8,8,512]{3,0,1,2:T(8,128)S(1)} fusion(f32[8,8,1,512]{3,0,1,2:T(8,128)S(1)} %collective-permute-done.4, f32[10,1,8,512]{3,0,1,2:T(8,128)S(1)} %pad.114, f32[10,1,8,512]{3,0,1,2:T(8,128)S(1)} %pad.115, f32[1,8,8,512]{3,0,1,2:T(1,128)S(1)} %collective-permute-done, f32[8,8,8,512]{3,0,1,2:T(8,128)S(1)} %convert_multiply_fusion.1, ...), kind=kLoop, calls=%fused_computation.1 | loop fusion | flops 8912896 | bytes 3473408 | tf_op jit(solution)/shard_map/sub | solution.py:230
  16.9 0.6 reshape.429
  17.5 0.7 reduce_sum.27
  18.3 0.6 collective-permute-start.7
  18.9 3.2 %collective-permute-start.5 = (f32[1,4,4,512]{3,0,1,2:T(1,128)S(1)}, f32[1,4,4,512]{3,0,1,2:T(1,128)S(1)}, u32[]{:S(2)}, u32[]{:S(2)}) collective-permute-start(f32[1,4,4,512]{3,0,1,2:T(1,128)S(1)} %get-tuple-element.42), channel_id=1, source_target_pairs={{0,24},{8,0},{16,8},{24,16},{1,25},{9,1},{17,9},{25,17},{2,26},{10... | collective-permute-start | bytes 98312 | tf_op jit(solution)/shard_map/ppermute | solution.py:23
  22.1 0.8 collective-permute-start.8
  22.9 0.6 copy-done.15
  23.9 3.9 %collective-permute-done.6 = f32[1,4,4,512]{3,0,1,2:T(1,128)S(1)} collective-permute-done((f32[1,4,4,512]{3,0,1,2:T(1,128)S(1)}, f32[1,4,4,512]{3,0,1,2:T(1,128)S(1)}, u32[]{:S(2)}, u32[]{:S(2)}) %collective-permute-start.6) | collective-permute-done | bytes 32800 | tf_op jit(solution)/shard_map/ppermute | solution.py:23
  28.7 2.3 %collective-permute-start.10 = (f32[20480]{0:T(1024)S(1)}, f32[20480]{0:T(1024)S(1)}, u32[]{:S(2)}, u32[]{:S(2)}) collective-permute-start(f32[20480]{0:T(1024)S(1)} %pad_maximum_fusion.99), channel_id=1, source_target_pairs={{0,24},{8,0},{16,8},{24,16},{1,25},{9,1},{17,9},{25,17},{2,26},{10... | collective-permute-start | bytes 245768 | tf_op jit(solution)/shard_map/ppermute | solution.py:23
  31.0 0.6 collective-permute-start.12
  31.6 0.7 and_convert_fusion
  36.0 3.0 %collective-permute-done.11 = f32[20480]{0:T(1024)S(1)} collective-permute-done((f32[20480]{0:T(1024)S(1)}, f32[20480]{0:T(1024)S(1)}, u32[]{:S(2)}, u32[]{:S(2)}) %collective-permute-start.11) | collective-permute-done | bytes 81952 | tf_op jit(solution)/shard_map/ppermute | solution.py:23
  39.1 0.5 copy-done.25
  39.7 1.5 %collective-permute-start.13 = (f32[8,2,2,512]{3,0,1,2:T(8,128)S(1)}, f32[8,2,2,512]{3,0,1,2:T(8,128)S(1)}, u32[]{:S(2)}, u32[]{:S(2)}) collective-permute-start(f32[8,2,2,512]{3,0,1,2:T(8,128)S(1)} %pad_maximum_fusion.149), channel_id=1, source_target_pairs={{0,4},{4,0},{1,5},{5,1},{2,6},{6,2},{3,7},{7,3},{8,12},{12,8},{9,1... | collective-permute-start | bytes 196616 | tf_op jit(solution)/shard_map/ppermute | solution.py:23
  41.2 2.7 %collective-permute-done.13 = f32[8,2,2,512]{3,0,1,2:T(8,128)S(1)} collective-permute-done((f32[8,2,2,512]{3,0,1,2:T(8,128)S(1)}, f32[8,2,2,512]{3,0,1,2:T(8,128)S(1)}, u32[]{:S(2)}, u32[]{:S(2)}) %collective-permute-start.13) | collective-permute-done | bytes 65568 | tf_op jit(solution)/shard_map/ppermute | solution.py:23
  44.0 0.5 collective-permute-start.15
  44.5 3.4 %collective-permute-done.14 = f32[8,4,2,512]{3,0,1,2:T(8,128)S(1)} collective-permute-done((f32[8,4,2,512]{3,0,1,2:T(8,128)S(1)}, f32[8,4,2,512]{3,0,1,2:T(8,128)S(1)}, u32[]{:S(2)}, u32[]{:S(2)}) %collective-permute-start.14) | collective-permute-done | bytes 131104 | tf_op jit(solution)/shard_map/ppermute | solution.py:23
  47.9 2.7 %collective-permute-done.15 = f32[8,4,2,512]{3,0,1,2:T(8,128)S(1)} collective-permute-done((f32[8,4,2,512]{3,0,1,2:T(8,128)S(1)}, f32[8,4,2,512]{3,0,1,2:T(8,128)S(1)}, u32[]{:S(2)}, u32[]{:S(2)}) %collective-permute-start.15) | collective-permute-done | bytes 131104 | tf_op jit(solution)/shard_map/ppermute | solution.py:23
  50.6 1.1 %collective-permute-done.16 = f32[8,4,2,512]{3,0,1,2:T(8,128)S(1)} collective-permute-done((f32[8,4,2,512]{3,0,1,2:T(8,128)S(1)}, f32[8,4,2,512]{3,0,1,2:T(8,128)S(1)}, u32[]{:S(2)}, u32[]{:S(2)}) %collective-permute-start.16) | collective-permute-done | bytes 131104 | tf_op jit(solution)/shard_map/ppermute | solution.py:23
  51.9 0.5 fusion.39
  54.4 0.5 fusion.29
  55.3 0.7 copy-done.16
  56.3 0.7 copy-done.22
  57.1 0.7 copy-done.18
  57.8 0.7 copy-done.20
  59.0 0.6 fusion.117
  59.6 0.6 pad_maximum_fusion.150
  60.2 1.5 %collective-permute-start.19 = (f32[4,2,4,512]{3,0,1,2:T(4,128)}, f32[4,2,4,512]{3,0,1,2:T(4,128)}, u32[]{:S(2)}, u32[]{:S(2)}) collective-permute-start(f32[4,2,4,512]{3,0,1,2:T(4,128)} %pad_maximum_fusion.150), channel_id=1, source_target_pairs={{0,4},{4,0},{1,5},{5,1},{2,6},{6,2},{3,7},{7,3},{8,12},{12,8},{9,1... | collective-permute-start | bytes 196616 | tf_op jit(solution)/shard_map/ppermute | solution.py:33
  61.8 1.5 %collective-permute-start.17 = (f32[1,4,4,512]{3,0,1,2:T(1,128)S(1)}, f32[1,4,4,512]{3,0,1,2:T(1,128)S(1)}, u32[]{:S(2)}, u32[]{:S(2)}) collective-permute-start(f32[1,4,4,512]{3,0,1,2:T(1,128)S(1)} %get-tuple-element.36), channel_id=1, source_target_pairs={{0,24},{8,0},{16,8},{24,16},{1,25},{9,1},{17,9},{25,17},{2,26},{10... | collective-permute-start | bytes 98312 | tf_op jit(solution)/shard_map/ppermute | solution.py:23
  63.2 0.6 collective-permute-start.18
  63.8 1.7 %collective-permute-start.20 = (f32[4,4,1,512]{3,0,1,2:T(4,128)}, f32[4,4,1,512]{3,0,1,2:T(4,128)S(1)}, u32[]{:S(2)}, u32[]{:S(2)}) collective-permute-start(f32[4,4,1,512]{3,0,1,2:T(4,128)} %get-tuple-element.33), channel_id=1, source_target_pairs={{0,3},{1,0},{2,1},{3,2},{4,7},{5,4},{6,5},{7,6},{8,11},{9,8},{10,9... | collective-permute-start | bytes 98312 | tf_op jit(solution)/shard_map/ppermute | solution.py:23
  66.6 2.3 %collective-permute-done.18 = f32[1,4,4,512]{3,0,1,2:T(1,128)S(1)} collective-permute-done((f32[1,4,4,512]{3,0,1,2:T(1,128)S(1)}, f32[1,4,4,512]{3,0,1,2:T(1,128)S(1)}, u32[]{:S(2)}, u32[]{:S(2)}) %collective-permute-start.18) | collective-permute-done | bytes 32800 | tf_op jit(solution)/shard_map/ppermute | solution.py:23
  69.4 0.8 %copy-done.4 = f32[1,8,8,512]{3,0,1,2:T(1,128)S(1)} copy-done((f32[1,8,8,512]{3,0,1,2:T(1,128)S(1)}, f32[1,8,8,512]{3,0,1,2:T(1,128)}, u32[]{:S(2)}) %copy-start.4) | copy-done | bytes 131096
  70.2 0.8 %add.419 = f32[1,8,8,512]{3,0,1,2:T(1,128)} add(f32[1,8,8,512]{3,0,1,2:T(1,128)S(1)} %copy-done.4, f32[1,8,8,512]{3,0,1,2:T(1,128)S(1)} %broadcast_in_dim.192) | non-fusion elementwise | flops 32768 | bytes 393216 | tf_op jit(solution)/shard_map/add | solution.py:196
  71.1 0.8 %add.420 = f32[1,8,8,512]{3,0,1,2:T(1,128)} add(f32[1,8,8,512]{3,0,1,2:T(1,128)S(1)} %copy-done.6, f32[1,8,8,512]{3,0,1,2:T(1,128)S(1)} %broadcast_in_dim.196) | non-fusion elementwise | flops 32768 | bytes 393216 | tf_op jit(solution)/shard_map/add | solution.py:195
  72.0 0.9 %copy-done.8 = f32[8,8,1,512]{3,0,1,2:T(8,128)S(1)} copy-done((f32[8,8,1,512]{3,0,1,2:T(8,128)S(1)}, f32[8,8,1,512]{3,0,1,2:T(8,128)}, u32[]{:S(2)}) %copy-start.8) | copy-done | bytes 131096
  72.9 0.8 slice_bitcast_fusion.3
  74.0 0.6 copy-done.27
  75.0 1.7 %fusion.3 = f32[8,8,8,512]{3,0,1,2:T(8,128)S(1)} fusion(f32[8,8,8,512]{3,0,1,2:T(8,128)S(1)} %bitcast_add_fusion, f32[8,8,1,512]{3,0,1,2:T(8,128)S(1)} %bitcast_add_fusion.2, f32[10,1,8,512]{3,0,1,2:T(8,128)S(1)} %pad.146, f32[10,1,8,512]{3,0,1,2:T(8,128)S(1)} %pad.147, f32[1,8,8,512]{3,0,1,2:T(1,128)S(1)} %copy-done.11, f32[1,8,8,512]{3,0,1,2:T(1,128)S(1)} %copy-done.12, ...), kind=kLoop, calls=%fused_computation.8 | loop fusion | flops 9961472 | bytes 3620864 | tf_op jit(solution)/shard_map/mul | solution.py:250
  76.7 2.3 %convolution_convert_fusion = bf16[8,8,8,512]{3,2,1,0:T(8,128)(2,1)} fusion(f32[512,512]{1,0:T(8,128)S(1)} %fusion.67, f32[8,8,8,512]{3,0,1,2:T(8,128)S(1)} %fusion.3), kind=kOutput, calls=%fused_computation.4 | convolution fusion | flops 805568512 | bytes 2621440 | tf_op jit(solution)/shard_map/dot_general | solution.py:255
  (212 shorter events, 7.8 us)
Async XLA Ops:
  1.5 11.9 %collective-permute-start.2 = (f32[8,2,8,512]{3,0,1,2:T(8,128)S(1)}, f32[8,2,8,512]{3,0,1,2:T(8,128)S(1)}, u32[]{:S(2)}, u32[]{:S(2)}) collective-permute-start(f32[8,2,8,512]{3,0,1,2:T(8,128)S(1)} %pad_maximum_fusion.65), channel_id=1, source_target_pairs={{0,4},{4,0},{1,5},{5,1},{2,6},{6,2},{3,7},{7,3},{8,12},{12,8},{9,1... | collective-permute-start | bytes 786440 | tf_op jit(solution)/shard_map/ppermute | solution.py:33
  4.8 8.7 %collective-permute-start = (f32[1,8,8,512]{3,0,1,2:T(1,128)S(1)}, f32[1,8,8,512]{3,0,1,2:T(1,128)S(1)}, u32[]{:S(2)}, u32[]{:S(2)}) collective-permute-start(f32[1,8,8,512]{3,0,1,2:T(1,128)S(1)} %get-tuple-element.8), channel_id=1, source_target_pairs={{0,24},{8,0},{16,8},{24,16},{1,25},{9,1},{17,9},{25,17},{2,26},{10... | collective-permute-start | bytes 393224 | tf_op jit(solution)/shard_map/ppermute | solution.py:23
  8.4 6.8 %collective-permute-start.1 = (f32[1,8,8,512]{3,0,1,2:T(1,128)S(1)}, f32[1,8,8,512]{3,0,1,2:T(1,128)S(1)}, u32[]{:S(2)}, u32[]{:S(2)}) collective-permute-start(f32[1,8,8,512]{3,0,1,2:T(1,128)S(1)} %get-tuple-element.7), channel_id=1, source_target_pairs={{0,8},{8,16},{16,24},{24,0},{1,9},{9,17},{17,25},{25,1},{2,10},{10... | collective-permute-start | bytes 393224 | tf_op jit(solution)/shard_map/ppermute | solution.py:23
  8.4 6.7 %collective-permute-start.3 = (f32[8,8,1,512]{3,0,1,2:T(8,128)S(1)}, f32[8,8,1,512]{3,0,1,2:T(8,128)S(1)}, u32[]{:S(2)}, u32[]{:S(2)}) collective-permute-start(f32[8,8,1,512]{3,0,1,2:T(8,128)S(1)} %get-tuple-element.5), channel_id=1, source_target_pairs={{0,3},{1,0},{2,1},{3,2},{4,7},{5,4},{6,5},{7,6},{8,11},{9,8},{10,9... | collective-permute-start | bytes 393224 | tf_op jit(solution)/shard_map/ppermute | solution.py:23
  8.9 6.3 %collective-permute-start.4 = (f32[8,8,1,512]{3,0,1,2:T(8,128)S(1)}, f32[8,8,1,512]{3,0,1,2:T(8,128)S(1)}, u32[]{:S(2)}, u32[]{:S(2)}) collective-permute-start(f32[8,8,1,512]{3,0,1,2:T(8,128)S(1)} %get-tuple-element.6), channel_id=1, source_target_pairs={{0,1},{1,2},{2,3},{3,0},{4,5},{5,6},{6,7},{7,4},{8,9},{9,10},{10,1... | collective-permute-start | bytes 393224 | tf_op jit(solution)/shard_map/ppermute | solution.py:23
  9.0 0.7 copy-start.28
  10.3 1.2 %copy-start.29 = (s32[3,2,512]{2,1,0:T(2,128)S(1)}, s32[3,2,512]{2,1,0:T(2,128)}, u32[]{:S(2)}) copy-start(s32[3,2,512]{2,1,0:T(2,128)} %param.5) | copy-start | bytes 36868
  11.6 0.8 %copy-start.14 = (f32[1,128,128]{2,1,0:T(8,128)S(1)}, f32[1,128,128]{2,1,0:T(8,128)}, u32[]{:S(2)}) copy-start(f32[1,128,128]{2,1,0:T(8,128)} %param.7) | copy-start | bytes 196612
  12.5 2.7 %copy-start.1 = (f32[512,512]{1,0:T(8,128)}, f32[512,512]{1,0:T(8,128)S(1)}, u32[]{:S(2)}) copy-start(f32[512,512]{1,0:T(8,128)S(1)} %bitcast_dynamic-update-slice_fusion) | copy-start | bytes 3145732
  13.4 1.8 %copy-start = (bf16[8,8,8,512]{3,2,1,0:T(8,128)(2,1)S(1)}, bf16[8,8,8,512]{3,2,1,0:T(8,128)(2,1)}, u32[]{:S(2)}) copy-start(bf16[8,8,8,512]{3,2,1,0:T(8,128)(2,1)} %param.4) | copy-start | bytes 1572868
  13.5 3.3 %copy-start.3 = (f32[1,8,8,512]{3,0,1,2:T(1,128)}, f32[1,8,8,512]{3,0,1,2:T(1,128)S(1)}, u32[]{:S(2)}) copy-start(f32[1,8,8,512]{3,0,1,2:T(1,128)S(1)} %collective-permute-done) | copy-start | bytes 393220
  15.2 1.6 %copy-start.5 = (f32[1,8,8,512]{3,0,1,2:T(1,128)}, f32[1,8,8,512]{3,0,1,2:T(1,128)S(1)}, u32[]{:S(2)}) copy-start(f32[1,8,8,512]{3,0,1,2:T(1,128)S(1)} %collective-permute-done.1) | copy-start | bytes 393220
  15.2 1.6 %copy-start.7 = (f32[8,8,1,512]{3,0,1,2:T(8,128)}, f32[8,8,1,512]{3,0,1,2:T(8,128)S(1)}, u32[]{:S(2)}) copy-start(f32[8,8,1,512]{3,0,1,2:T(8,128)S(1)} %collective-permute-done.3) | copy-start | bytes 393220
  15.2 1.6 %copy-start.9 = (f32[8,8,1,512]{3,0,1,2:T(8,128)}, f32[8,8,1,512]{3,0,1,2:T(8,128)S(1)}, u32[]{:S(2)}) copy-start(f32[8,8,1,512]{3,0,1,2:T(8,128)S(1)} %collective-permute-done.4) | copy-start | bytes 393220
  18.3 4.6 %collective-permute-start.7 = (f32[4,2,4,512]{3,0,1,2:T(4,128)S(1)}, f32[4,2,4,512]{3,0,1,2:T(4,128)S(1)}, u32[]{:S(2)}, u32[]{:S(2)}) collective-permute-start(f32[4,2,4,512]{3,0,1,2:T(4,128)S(1)} %pad_maximum_fusion.148), channel_id=1, source_target_pairs={{0,4},{4,0},{1,5},{5,1},{2,6},{6,2},{3,7},{7,3},{8,12},{12,8},{9,1... | collective-permute-start | bytes 196616 | tf_op jit(solution)/shard_map/ppermute | solution.py:33
  18.9 5.0 %collective-permute-start.5 = (f32[1,4,4,512]{3,0,1,2:T(1,128)S(1)}, f32[1,4,4,512]{3,0,1,2:T(1,128)S(1)}, u32[]{:S(2)}, u32[]{:S(2)}) collective-permute-start(f32[1,4,4,512]{3,0,1,2:T(1,128)S(1)} %get-tuple-element.42), channel_id=1, source_target_pairs={{0,24},{8,0},{16,8},{24,16},{1,25},{9,1},{17,9},{25,17},{2,26},{10... | collective-permute-start | bytes 98312 | tf_op jit(solution)/shard_map/ppermute | solution.py:23
  22.1 5.7 %collective-permute-start.6 = (f32[1,4,4,512]{3,0,1,2:T(1,128)S(1)}, f32[1,4,4,512]{3,0,1,2:T(1,128)S(1)}, u32[]{:S(2)}, u32[]{:S(2)}) collective-permute-start(f32[1,4,4,512]{3,0,1,2:T(1,128)S(1)} %get-tuple-element.41), channel_id=1, source_target_pairs={{0,8},{8,16},{16,24},{24,0},{1,9},{9,17},{17,25},{25,1},{2,10},{10... | collective-permute-start | bytes 98312 | tf_op jit(solution)/shard_map/ppermute | solution.py:23
  22.1 5.7 %collective-permute-start.8 = (f32[4,4,1,512]{3,0,1,2:T(4,128)S(1)}, f32[4,4,1,512]{3,0,1,2:T(4,128)S(1)}, u32[]{:S(2)}, u32[]{:S(2)}) collective-permute-start(f32[4,4,1,512]{3,0,1,2:T(4,128)S(1)} %get-tuple-element.39), channel_id=1, source_target_pairs={{0,3},{1,0},{2,1},{3,2},{4,7},{5,4},{6,5},{7,6},{8,11},{9,8},{10,9... | collective-permute-start | bytes 98312 | tf_op jit(solution)/shard_map/ppermute | solution.py:23
  22.9 5.0 %collective-permute-start.9 = (f32[4,4,1,512]{3,0,1,2:T(4,128)S(1)}, f32[4,4,1,512]{3,0,1,2:T(4,128)S(1)}, u32[]{:S(2)}, u32[]{:S(2)}) collective-permute-start(f32[4,4,1,512]{3,0,1,2:T(4,128)S(1)} %get-tuple-element.40), channel_id=1, source_target_pairs={{0,1},{1,2},{2,3},{3,0},{4,5},{5,6},{6,7},{7,4},{8,9},{9,10},{10,1... | collective-permute-start | bytes 98312 | tf_op jit(solution)/shard_map/ppermute | solution.py:23
  23.5 17.6 %copy-start.2 = (f32[512,512]{1,0:T(8,128)S(1)}, f32[512,512]{1,0:T(8,128)}, u32[]{:S(2)}) copy-start(f32[512,512]{1,0:T(8,128)} %copy-done.1) | copy-start | bytes 3145732
  23.9 4.3 %copy-start.17 = (f32[1,4,4,512]{3,0,1,2:T(1,128)}, f32[1,4,4,512]{3,0,1,2:T(1,128)S(1)}, u32[]{:S(2)}) copy-start(f32[1,4,4,512]{3,0,1,2:T(1,128)S(1)} %collective-permute-done.5) | copy-start | bytes 98308
  28.7 7.2 %collective-permute-start.10 = (f32[20480]{0:T(1024)S(1)}, f32[20480]{0:T(1024)S(1)}, u32[]{:S(2)}, u32[]{:S(2)}) collective-permute-start(f32[20480]{0:T(1024)S(1)} %pad_maximum_fusion.99), channel_id=1, source_target_pairs={{0,24},{8,0},{16,8},{24,16},{1,25},{9,1},{17,9},{25,17},{2,26},{10... | collective-permute-start | bytes 245768 | tf_op jit(solution)/shard_map/ppermute | solution.py:23
  31.0 8.0 %collective-permute-start.11 = (f32[20480]{0:T(1024)S(1)}, f32[20480]{0:T(1024)S(1)}, u32[]{:S(2)}, u32[]{:S(2)}) collective-permute-start(f32[20480]{0:T(1024)S(1)} %pad_maximum_fusion.99), channel_id=1, source_target_pairs={{0,16},{8,24},{16,0},{24,8},{1,17},{9,25},{17,1},{25,9},{2,18},{10... | collective-permute-start | bytes 245768 | tf_op jit(solution)/shard_map/ppermute | solution.py:23
  31.0 8.0 %collective-permute-start.12 = (f32[20480]{0:T(1024)S(1)}, f32[20480]{0:T(1024)S(1)}, u32[]{:S(2)}, u32[]{:S(2)}) collective-permute-start(f32[20480]{0:T(1024)S(1)} %pad_maximum_fusion.99), channel_id=1, source_target_pairs={{0,8},{8,16},{16,24},{24,0},{1,9},{9,17},{17,25},{25,1},{2,10},{10... | collective-permute-start | bytes 245768 | tf_op jit(solution)/shard_map/ppermute | solution.py:23
  39.0 0.6 copy-start.25
  39.7 4.3 %collective-permute-start.13 = (f32[8,2,2,512]{3,0,1,2:T(8,128)S(1)}, f32[8,2,2,512]{3,0,1,2:T(8,128)S(1)}, u32[]{:S(2)}, u32[]{:S(2)}) collective-permute-start(f32[8,2,2,512]{3,0,1,2:T(8,128)S(1)} %pad_maximum_fusion.149), channel_id=1, source_target_pairs={{0,4},{4,0},{1,5},{5,1},{2,6},{6,2},{3,7},{7,3},{8,12},{12,8},{9,1... | collective-permute-start | bytes 196616 | tf_op jit(solution)/shard_map/ppermute | solution.py:23
  44.0 3.9 %collective-permute-start.14 = (f32[8,4,2,512]{3,0,1,2:T(8,128)S(1)}, f32[8,4,2,512]{3,0,1,2:T(8,128)S(1)}, u32[]{:S(2)}, u32[]{:S(2)}) collective-permute-start(f32[8,4,2,512]{3,0,1,2:T(8,128)S(1)} %pad_maximum_fusion.98), channel_id=1, source_target_pairs={{0,3},{1,0},{2,1},{3,2},{4,7},{5,4},{6,5},{7,6},{8,11},{9,8},{10,9... | collective-permute-start | bytes 393224 | tf_op jit(solution)/shard_map/ppermute | solution.py:23
  44.0 6.6 %collective-permute-start.15 = (f32[8,4,2,512]{3,0,1,2:T(8,128)S(1)}, f32[8,4,2,512]{3,0,1,2:T(8,128)S(1)}, u32[]{:S(2)}, u32[]{:S(2)}) collective-permute-start(f32[8,4,2,512]{3,0,1,2:T(8,128)S(1)} %pad_maximum_fusion.98), channel_id=1, source_target_pairs={{0,2},{1,3},{2,0},{3,1},{4,6},{5,7},{6,4},{7,5},{8,10},{9,11},{10,... | collective-permute-start | bytes 393224 | tf_op jit(solution)/shard_map/ppermute | solution.py:23
  44.5 7.2 %collective-permute-start.16 = (f32[8,4,2,512]{3,0,1,2:T(8,128)S(1)}, f32[8,4,2,512]{3,0,1,2:T(8,128)S(1)}, u32[]{:S(2)}, u32[]{:S(2)}) collective-permute-start(f32[8,4,2,512]{3,0,1,2:T(8,128)S(1)} %pad_maximum_fusion.98), channel_id=1, source_target_pairs={{0,1},{1,2},{2,3},{3,0},{4,5},{5,6},{6,7},{7,4},{8,9},{9,10},{10,1... | collective-permute-start | bytes 393224 | tf_op jit(solution)/shard_map/ppermute | solution.py:23
  55.2 0.8 %copy-start.16 = (f32[4,2,4,512]{3,0,1,2:T(4,128)S(1)}, f32[4,2,4,512]{3,0,1,2:T(4,128)}, u32[]{:S(2)}) copy-start(f32[4,2,4,512]{3,0,1,2:T(4,128)} %copy-done.15) | copy-start | bytes 196612
  56.3 0.8 copy-start.22
  57.0 0.8 copy-start.18
  57.8 0.8 copy-start.20
  57.8 0.8 copy-start.24
  59.6 5.9 %copy-start.26 = (f32[20480]{0:T(1024)S(1)}, f32[20480]{0:T(1024)}, u32[]{:S(2)}) copy-start(f32[20480]{0:T(1024)} %copy-done.25) | copy-start | bytes 245764
  60.2 12.7 %collective-permute-start.19 = (f32[4,2,4,512]{3,0,1,2:T(4,128)}, f32[4,2,4,512]{3,0,1,2:T(4,128)}, u32[]{:S(2)}, u32[]{:S(2)}) collective-permute-start(f32[4,2,4,512]{3,0,1,2:T(4,128)} %pad_maximum_fusion.150), channel_id=1, source_target_pairs={{0,4},{4,0},{1,5},{5,1},{2,6},{6,2},{3,7},{7,3},{8,12},{12,8},{9,1... | collective-permute-start | bytes 196616 | tf_op jit(solution)/shard_map/ppermute | solution.py:33
  61.8 4.6 %collective-permute-start.17 = (f32[1,4,4,512]{3,0,1,2:T(1,128)S(1)}, f32[1,4,4,512]{3,0,1,2:T(1,128)S(1)}, u32[]{:S(2)}, u32[]{:S(2)}) collective-permute-start(f32[1,4,4,512]{3,0,1,2:T(1,128)S(1)} %get-tuple-element.36), channel_id=1, source_target_pairs={{0,24},{8,0},{16,8},{24,16},{1,25},{9,1},{17,9},{25,17},{2,26},{10... | collective-permute-start | bytes 98312 | tf_op jit(solution)/shard_map/ppermute | solution.py:23
  63.2 5.7 %collective-permute-start.18 = (f32[1,4,4,512]{3,0,1,2:T(1,128)S(1)}, f32[1,4,4,512]{3,0,1,2:T(1,128)S(1)}, u32[]{:S(2)}, u32[]{:S(2)}) collective-permute-start(f32[1,4,4,512]{3,0,1,2:T(1,128)S(1)} %get-tuple-element.35), channel_id=1, source_target_pairs={{0,8},{8,16},{16,24},{24,0},{1,9},{9,17},{17,25},{25,1},{2,10},{10... | collective-permute-start | bytes 98312 | tf_op jit(solution)/shard_map/ppermute | solution.py:23
  63.8 5.4 %collective-permute-start.21 = (f32[4,4,1,512]{3,0,1,2:T(4,128)}, f32[4,4,1,512]{3,0,1,2:T(4,128)S(1)}, u32[]{:S(2)}, u32[]{:S(2)}) collective-permute-start(f32[4,4,1,512]{3,0,1,2:T(4,128)} %get-tuple-element.34), channel_id=1, source_target_pairs={{0,1},{1,2},{2,3},{3,0},{4,5},{5,6},{6,7},{7,4},{8,9},{9,10},{10,1... | collective-permute-start | bytes 98312 | tf_op jit(solution)/shard_map/ppermute | solution.py:23
  63.8 5.5 %collective-permute-start.20 = (f32[4,4,1,512]{3,0,1,2:T(4,128)}, f32[4,4,1,512]{3,0,1,2:T(4,128)S(1)}, u32[]{:S(2)}, u32[]{:S(2)}) collective-permute-start(f32[4,4,1,512]{3,0,1,2:T(4,128)} %get-tuple-element.33), channel_id=1, source_target_pairs={{0,3},{1,0},{2,1},{3,2},{4,7},{5,4},{6,5},{7,6},{8,11},{9,8},{10,9... | collective-permute-start | bytes 98312 | tf_op jit(solution)/shard_map/ppermute | solution.py:23
  69.3 0.9 %copy-start.4 = (f32[1,8,8,512]{3,0,1,2:T(1,128)S(1)}, f32[1,8,8,512]{3,0,1,2:T(1,128)}, u32[]{:S(2)}) copy-start(f32[1,8,8,512]{3,0,1,2:T(1,128)} %copy-done.3) | copy-start | bytes 393220
  70.2 0.9 %copy-start.6 = (f32[1,8,8,512]{3,0,1,2:T(1,128)S(1)}, f32[1,8,8,512]{3,0,1,2:T(1,128)}, u32[]{:S(2)}) copy-start(f32[1,8,8,512]{3,0,1,2:T(1,128)} %copy-done.5) | copy-start | bytes 393220
  71.1 0.9 %copy-start.10 = (f32[8,8,1,512]{3,0,1,2:T(8,128)S(1)}, f32[8,8,1,512]{3,0,1,2:T(8,128)}, u32[]{:S(2)}) copy-start(f32[8,8,1,512]{3,0,1,2:T(8,128)} %copy-done.9) | copy-start | bytes 393220
  72.0 0.9 %copy-start.8 = (f32[8,8,1,512]{3,0,1,2:T(8,128)S(1)}, f32[8,8,1,512]{3,0,1,2:T(8,128)}, u32[]{:S(2)}) copy-start(f32[8,8,1,512]{3,0,1,2:T(8,128)} %copy-done.7) | copy-start | bytes 393220
  73.9 0.7 copy-start.27
  74.0 0.9 %copy-start.11 = (f32[1,8,8,512]{3,0,1,2:T(1,128)S(1)}, f32[1,8,8,512]{3,0,1,2:T(1,128)}, u32[]{:S(2)}) copy-start(f32[1,8,8,512]{3,0,1,2:T(1,128)} %add.419) | copy-start | bytes 393220
  74.0 1.0 %copy-start.12 = (f32[1,8,8,512]{3,0,1,2:T(1,128)S(1)}, f32[1,8,8,512]{3,0,1,2:T(1,128)}, u32[]{:S(2)}) copy-start(f32[1,8,8,512]{3,0,1,2:T(1,128)} %add.420) | copy-start | bytes 393220
  74.0 1.0 %copy-start.13 = (f32[8,8,512]{2,0,1:T(8,128)S(1)}, f32[8,8,512]{2,0,1:T(8,128)}, u32[]{:S(2)}) copy-start(f32[8,8,512]{2,0,1:T(8,128)} %broadcast_multiply_fusion.1) | copy-start | bytes 393220
  (4 other events, 2.4 us)

commit v5 on v4

--- a/solution.py
+++ b/solution.py
@@ -71,6 +71,65 @@
     return jnp.concatenate(pieces, axis=dim), start, extras
 
 
+def axis_offsets(count, size, halo):
+    reach = -(-halo // size)
+    if 2 * reach + 1 >= count:
+        return list(range(count)), 0
+    return list(range(-reach, reach + 1)), reach * size
+
+
+def extend_joint(block, axes, dims, halo):
+    counts = [lax.axis_size(axis) for axis in axes]
+    plans = [axis_offsets(count, block.shape[dim], halo) for count, dim in zip(counts, dims)]
+    cache = {}
+
+    def fetch(offset):
+        steps = tuple(o % c for o, c in zip(offset, counts))
+        if steps not in cache:
+            if not any(steps):
+                cache[steps] = block
+            else:
+                pairs = []
+                for target in range(_prod(counts)):
+                    coords = _unravel(target, counts)
+                    source = _ravel([(c + s) % n for c, s, n in zip(coords, steps, counts)], counts)
+                    pairs.append((source, target))
+                cache[steps] = lax.ppermute(block, tuple(axes), pairs)
+        return cache[steps]
+
+    def assemble(level, prefix):
+        offsets, start = plans[level]
+        if level == len(axes) - 1:
+            pieces = [fetch(prefix + (o,)) for o in offsets]
+        else:
+            pieces = [assemble(level + 1, prefix + (o,)) for o in offsets]
+        return jnp.concatenate(pieces, axis=dims[level])
+
+    return assemble(0, ()), [start for offsets, start in plans]
+
+
+def _prod(values):
+    total = 1
+    for v in values:
+        total *= v
+    return total
+
+
+def _unravel(index, counts):
+    coords = []
+    for n in reversed(counts):
+        coords.append(index % n)
+        index //= n
+    return list(reversed(coords))
+
+
+def _ravel(coords, counts):
+    index = 0
+    for c, n in zip(coords, counts):
+        index = index * n + c
+    return index
+
+
 def level_coeffs(level_id):
     coupling = 0.5 / 4.0**level_id
     return (6.0 * coupling + shift_sigma, coupling)
@@ -128,12 +187,10 @@
     extended = rhs_two
     starts = []
     tiles_by_step = {}
-    for axis, dim in GRID_AXES:
-        extra = tiles if axis == "gx" else None
-        extended, start, extras = extend_axis(extended, axis, dim, COARSE_HALO, extra)
-        if axis == "gx":
-            tiles_by_step = extras
-        starts.append(start)
+    extended, start, tiles_by_step = extend_axis(extended, "gx", 0, COARSE_HALO, tiles)
+    starts.append(start)
+    extended, joint_starts = extend_joint(extended, ("gy", "gz"), (1, 2), COARSE_HALO)
+    starts.extend(joint_starts)
     width = extended.shape[3]
     chunks = 1
     while extended.size * 4 // chunks > CHUNK_BYTES and width % (2 * chunks * 128) == 0:

time: 79.7 us -> 77.8 us (0.976)
  waiting for transfers between devices: 21.2 us -> 15.9 us
  starting transfers between devices: 22.1 us -> 26.1 us
    ppermute x19 -> x15, waiting for transfers between devices: 21.1 us -> 11.2 us  [shifted(): lax.ppermute(block, axis, [(j, (j - step) % count) for j in range(count)])]
    ppermute x0 -> x7, starting transfers between devices: none -> 5.98 us  [fetch(): cache[steps] = lax.ppermute(block, tuple(axes), pairs)]
    ppermute x0 -> x7, waiting for transfers between devices: none -> 4.57 us  [fetch(): cache[steps] = lax.ppermute(block, tuple(axes), pairs)]
    ppermute x19 -> x15, starting transfers between devices: 16.9 us -> 14.9 us  [shifted(): lax.ppermute(block, axis, [(j, (j - step) % count) for j in range(count)])]
    unnamed x64 -> x62, local copies, waits for them, and re-layouts: 8.69 us -> 8.73 us
  transfers between devices with their start and end apart: 22 -> 25, of which waited for: 9 -> 9; matrix products, arithmetic and copies ran while one was open for 7% -> 7% of each run, Pallas kernels for 0% -> 0%
where the time goes in v5:
time: 77.8 us; the launch traced here: 77 us
  starting transfers between devices  26.1 us (34%)
  waiting for transfers between devices  15.9 us (20%)
  local copies, waits for them, and re-layouts  14.8 us (19%)
  other arithmetic  11.9 us (15%)
  between operations  6.12 us (8%)
  matrix products  2.25 us (3%)
    ppermute x15, starting transfers between devices, shifted(): lax.ppermute(block, axis, [(j, (j - step) % count) for j in range(count)])  14.9 us
    ppermute x15, waiting for transfers between devices, shifted(): lax.ppermute(block, axis, [(j, (j - step) % count) for j in range(count)])  11.2 us
    unnamed x62, local copies, waits for them, and re-layouts  8.73 us
    ppermute x7, starting transfers between devices, fetch(): cache[steps] = lax.ppermute(block, tuple(axes), pairs)  5.98 us
    ppermute x3, starting transfers between devices, axis_faces(): lax.ppermute(jnp.concatenate([first, last], axis=dim), axis, [(0, 1), (1,...  5.18 us
    ppermute x7, waiting for transfers between devices, fetch(): cache[steps] = lax.ppermute(block, tuple(axes), pairs)  4.57 us
    dot_general x1, matrix products, body(): jnp.dot(rows, gram, precision=lax.Precision.HIGH, preferred_element_type=...  2.25 us
    mul x1, other arithmetic, body(): correct * (mask_first[:, None, None, :] * mask_second[None, :, None, :] *...  1.66 us
  transfers between devices with their start and end apart: 25, of which 9 were waited for; matrix products, arithmetic and copies ran while one was open for 7% of the time, Pallas kernels for 0%

profile of v5, /device:TPU:0, one launch (start us, length us, event | category | flops | bytes accessed | tf_op | source)
XLA Modules:
  0.0 77.0 jit_solution(2263010223633361555)
XLA Ops:
  0.0 1.4 %convert_multiply_fusion.1 = f32[8,8,8,512]{3,0,1,2:T(8,128)S(1)} fusion(bf16[8,8,8,512]{3,2,1,0:T(8,128)(2,1)} %param.4), kind=kLoop, calls=%fused_computation.3 | loop fusion | flops 524288 | bytes 1572864 | tf_op jit(solution)/shard_map/div | solution.py:285
  1.5 3.1 %collective-permute-start.2 = (f32[8,2,8,512]{3,0,1,2:T(8,128)S(1)}, f32[8,2,8,512]{3,0,1,2:T(8,128)S(1)}, u32[]{:S(2)}, u32[]{:S(2)}) collective-permute-start(f32[8,2,8,512]{3,0,1,2:T(8,128)S(1)} %pad_maximum_fusion.64), channel_id=1, source_target_pairs={{0,4},{4,0},{1,5},{5,1},{2,6},{6,2},{3,7},{7,3},{8,12},{12,8},{9,1... | collective-permute-start | bytes 786440 | tf_op jit(solution)/shard_map/ppermute | solution.py:33
  4.8 3.7 %collective-permute-start = (f32[1,8,8,512]{3,0,1,2:T(1,128)S(1)}, f32[1,8,8,512]{3,0,1,2:T(1,128)S(1)}, u32[]{:S(2)}, u32[]{:S(2)}) collective-permute-start(f32[1,8,8,512]{3,0,1,2:T(1,128)S(1)} %get-tuple-element.8), channel_id=1, source_target_pairs={{0,24},{8,0},{16,8},{24,16},{1,25},{9,1},{17,9},{25,17},{2,26},{10... | collective-permute-start | bytes 393224 | tf_op jit(solution)/shard_map/ppermute | solution.py:23
  9.0 0.7 copy-done.27
  9.7 0.7 constant_dynamic-slice_fusion
  11.9 0.7 copy-done.14
  12.7 0.8 %broadcast_multiply_fusion.1 = f32[8,8,512]{2,0,1:T(8,128)} fusion(f32[8,512]{1,0:T(8,128)S(1)} %get-tuple-element.87, f32[8,512]{1,0:T(8,128)S(1)} %get-tuple-element.88), kind=kLoop, calls=%fused_computation.299 | loop fusion | flops 32768 | bytes 163840 | tf_op jit(solution)/shard_map/mul | solution.py:308
  13.6 1.6 %collective-permute-done.1 = f32[1,8,8,512]{3,0,1,2:T(1,128)S(1)} collective-permute-done((f32[1,8,8,512]{3,0,1,2:T(1,128)S(1)}, f32[1,8,8,512]{3,0,1,2:T(1,128)S(1)}, u32[]{:S(2)}, u32[]{:S(2)}) %collective-permute-start.1) | collective-permute-done | bytes 131104 | tf_op jit(solution)/shard_map/ppermute | solution.py:23
  15.2 1.6 %convert_subtract_fusion.1 = f32[8,8,8,512]{3,0,1,2:T(8,128)S(1)} fusion(f32[8,8,1,512]{3,0,1,2:T(8,128)S(1)} %collective-permute-done.4, f32[10,1,8,512]{3,0,1,2:T(8,128)S(1)} %pad.114, f32[10,1,8,512]{3,0,1,2:T(8,128)S(1)} %pad.115, f32[1,8,8,512]{3,0,1,2:T(1,128)S(1)} %collective-permute-done, f32[8,8,8,512]{3,0,1,2:T(8,128)S(1)} %convert_multiply_fusion.1, ...), kind=kLoop, calls=%fused_computation.1 | loop fusion | flops 8912896 | bytes 3473408 | tf_op jit(solution)/shard_map/sub | solution.py:287
  16.9 0.6 reshape.429
  17.5 0.7 reduce_sum.27
  18.3 0.6 collective-permute-start.7
  18.9 3.2 %collective-permute-start.5 = (f32[1,4,4,512]{3,0,1,2:T(1,128)S(1)}, f32[1,4,4,512]{3,0,1,2:T(1,128)S(1)}, u32[]{:S(2)}, u32[]{:S(2)}) collective-permute-start(f32[1,4,4,512]{3,0,1,2:T(1,128)S(1)} %get-tuple-element.42), channel_id=1, source_target_pairs={{0,24},{8,0},{16,8},{24,16},{1,25},{9,1},{17,9},{25,17},{2,26},{10... | collective-permute-start | bytes 98312 | tf_op jit(solution)/shard_map/ppermute | solution.py:23
  22.1 0.8 collective-permute-start.8
  23.0 0.6 copy-done.15
  23.9 3.9 %collective-permute-done.6 = f32[1,4,4,512]{3,0,1,2:T(1,128)S(1)} collective-permute-done((f32[1,4,4,512]{3,0,1,2:T(1,128)S(1)}, f32[1,4,4,512]{3,0,1,2:T(1,128)S(1)}, u32[]{:S(2)}, u32[]{:S(2)}) %collective-permute-start.6) | collective-permute-done | bytes 32800 | tf_op jit(solution)/shard_map/ppermute | solution.py:23
  28.7 2.3 %collective-permute-start.10 = (f32[20480]{0:T(1024)S(1)}, f32[20480]{0:T(1024)S(1)}, u32[]{:S(2)}, u32[]{:S(2)}) collective-permute-start(f32[20480]{0:T(1024)S(1)} %pad_maximum_fusion.97), channel_id=1, source_target_pairs={{0,24},{8,0},{16,8},{24,16},{1,25},{9,1},{17,9},{25,17},{2,26},{10... | collective-permute-start | bytes 245768 | tf_op jit(solution)/shard_map/ppermute | solution.py:23
  31.0 0.6 collective-permute-start.12
  35.4 3.7 %collective-permute-done.11 = f32[20480]{0:T(1024)S(1)} collective-permute-done((f32[20480]{0:T(1024)S(1)}, f32[20480]{0:T(1024)S(1)}, u32[]{:S(2)}, u32[]{:S(2)}) %collective-permute-start.11) | collective-permute-done | bytes 81952 | tf_op jit(solution)/shard_map/ppermute | solution.py:23
  39.2 0.5 copy-done.25
  39.7 1.6 %collective-permute-start.14 = (f32[8,2,2,512]{3,0,1,2:T(8,128)S(1)}, f32[8,2,2,512]{3,0,1,2:T(8,128)S(1)}, u32[]{:S(2)}, u32[]{:S(2)}) collective-permute-start(f32[8,2,2,512]{3,0,1,2:T(8,128)S(1)} %pad_maximum_fusion.147), channel_id=1, source_target_pairs={{2,0},{3,1},{0,2},{1,3},{6,4},{7,5},{4,6},{5,7},{10,8},{11,9},{8,1... | collective-permute-start | bytes 196616 | tf_op jit(solution)/shard_map/ppermute | solution.py:97
  41.4 1.5 %collective-permute-start.16 = (f32[8,2,2,512]{3,0,1,2:T(8,128)S(1)}, f32[8,2,2,512]{3,0,1,2:T(8,128)S(1)}, u32[]{:S(2)}, u32[]{:S(2)}) collective-permute-start(f32[8,2,2,512]{3,0,1,2:T(8,128)S(1)} %pad_maximum_fusion.147), channel_id=1, source_target_pairs={{4,0},{5,1},{6,2},{7,3},{0,4},{1,5},{2,6},{3,7},{12,8},{13,9},{14,... | collective-permute-start | bytes 196616 | tf_op jit(solution)/shard_map/ppermute | solution.py:97
  42.9 1.4 %collective-permute-start.17 = (f32[8,2,2,512]{3,0,1,2:T(8,128)S(1)}, f32[8,2,2,512]{3,0,1,2:T(8,128)S(1)}, u32[]{:S(2)}, u32[]{:S(2)}) collective-permute-start(f32[8,2,2,512]{3,0,1,2:T(8,128)S(1)} %pad_maximum_fusion.147), channel_id=1, source_target_pairs={{5,0},{6,1},{7,2},{4,3},{1,4},{2,5},{3,6},{0,7},{13,8},{14,9},{15,... | collective-permute-start | bytes 196616 | tf_op jit(solution)/shard_map/ppermute | solution.py:97
  44.3 1.4 %collective-permute-start.18 = (f32[8,2,2,512]{3,0,1,2:T(8,128)S(1)}, f32[8,2,2,512]{3,0,1,2:T(8,128)S(1)}, u32[]{:S(2)}, u32[]{:S(2)}) collective-permute-start(f32[8,2,2,512]{3,0,1,2:T(8,128)S(1)} %pad_maximum_fusion.147), channel_id=1, source_target_pairs={{6,0},{7,1},{4,2},{5,3},{2,4},{3,5},{0,6},{1,7},{14,8},{15,9},{12,... | collective-permute-start | bytes 196616 | tf_op jit(solution)/shard_map/ppermute | solution.py:97
  45.9 0.9 %collective-permute-done.17 = f32[8,2,2,512]{3,0,1,2:T(8,128)S(1)} collective-permute-done((f32[8,2,2,512]{3,0,1,2:T(8,128)S(1)}, f32[8,2,2,512]{3,0,1,2:T(8,128)S(1)}, u32[]{:S(2)}, u32[]{:S(2)}) %collective-permute-start.17) | collective-permute-done | bytes 65568 | tf_op jit(solution)/shard_map/ppermute | solution.py:97
  46.8 2.8 %collective-permute-done.18 = f32[8,2,2,512]{3,0,1,2:T(8,128)S(1)} collective-permute-done((f32[8,2,2,512]{3,0,1,2:T(8,128)S(1)}, f32[8,2,2,512]{3,0,1,2:T(8,128)S(1)}, u32[]{:S(2)}, u32[]{:S(2)}) %collective-permute-start.18) | collective-permute-done | bytes 65568 | tf_op jit(solution)/shard_map/ppermute | solution.py:97
  49.5 0.8 collective-permute-done.19
  50.6 0.5 fusion.39
  53.0 0.5 fusion.29
  53.9 0.7 copy-done.16
  55.0 0.7 copy-done.22
  55.7 0.7 copy-done.18
  56.5 0.7 copy-done.20
  57.6 0.6 fusion.117
  58.3 0.6 pad_maximum_fusion.148
  58.9 1.5 %collective-permute-start.22 = (f32[4,2,4,512]{3,0,1,2:T(4,128)}, f32[4,2,4,512]{3,0,1,2:T(4,128)}, u32[]{:S(2)}, u32[]{:S(2)}) collective-permute-start(f32[4,2,4,512]{3,0,1,2:T(4,128)} %pad_maximum_fusion.148), channel_id=1, source_target_pairs={{0,4},{4,0},{1,5},{5,1},{2,6},{6,2},{3,7},{7,3},{8,12},{12,8},{9,1... | collective-permute-start | bytes 196616 | tf_op jit(solution)/shard_map/ppermute | solution.py:33
  60.4 0.8 %collective-permute-start.20 = (f32[1,4,4,512]{3,0,1,2:T(1,128)S(1)}, f32[1,4,4,512]{3,0,1,2:T(1,128)S(1)}, u32[]{:S(2)}, u32[]{:S(2)}) collective-permute-start(f32[1,4,4,512]{3,0,1,2:T(1,128)S(1)} %get-tuple-element.36), channel_id=1, source_target_pairs={{0,24},{8,0},{16,8},{24,16},{1,25},{9,1},{17,9},{25,17},{2,26},{10... | collective-permute-start | bytes 98312 | tf_op jit(solution)/shard_map/ppermute | solution.py:23
  61.3 1.2 %collective-permute-start.21 = (f32[1,4,4,512]{3,0,1,2:T(1,128)S(1)}, f32[1,4,4,512]{3,0,1,2:T(1,128)S(1)}, u32[]{:S(2)}, u32[]{:S(2)}) collective-permute-start(f32[1,4,4,512]{3,0,1,2:T(1,128)S(1)} %get-tuple-element.35), channel_id=1, source_target_pairs={{0,8},{8,16},{16,24},{24,0},{1,9},{9,17},{17,25},{25,1},{2,10},{10... | collective-permute-start | bytes 98312 | tf_op jit(solution)/shard_map/ppermute | solution.py:23
  62.5 1.7 %collective-permute-start.23 = (f32[4,4,1,512]{3,0,1,2:T(4,128)}, f32[4,4,1,512]{3,0,1,2:T(4,128)S(1)}, u32[]{:S(2)}, u32[]{:S(2)}) collective-permute-start(f32[4,4,1,512]{3,0,1,2:T(4,128)} %get-tuple-element.33), channel_id=1, source_target_pairs={{0,3},{1,0},{2,1},{3,2},{4,7},{5,4},{6,5},{7,6},{8,11},{9,8},{10,9... | collective-permute-start | bytes 98312 | tf_op jit(solution)/shard_map/ppermute | solution.py:23
  65.3 1.7 %collective-permute-done.21 = f32[1,4,4,512]{3,0,1,2:T(1,128)S(1)} collective-permute-done((f32[1,4,4,512]{3,0,1,2:T(1,128)S(1)}, f32[1,4,4,512]{3,0,1,2:T(1,128)S(1)}, u32[]{:S(2)}, u32[]{:S(2)}) %collective-permute-start.21) | collective-permute-done | bytes 32800 | tf_op jit(solution)/shard_map/ppermute | solution.py:23
  67.5 0.8 %copy-done.4 = f32[1,8,8,512]{3,0,1,2:T(1,128)S(1)} copy-done((f32[1,8,8,512]{3,0,1,2:T(1,128)S(1)}, f32[1,8,8,512]{3,0,1,2:T(1,128)}, u32[]{:S(2)}) %copy-start.4) | copy-done | bytes 131096
  68.3 0.8 %add.419 = f32[1,8,8,512]{3,0,1,2:T(1,128)} add(f32[1,8,8,512]{3,0,1,2:T(1,128)S(1)} %copy-done.4, f32[1,8,8,512]{3,0,1,2:T(1,128)S(1)} %broadcast_in_dim.192) | non-fusion elementwise | flops 32768 | bytes 393216 | tf_op jit(solution)/shard_map/add | solution.py:253
  69.2 0.8 %add.420 = f32[1,8,8,512]{3,0,1,2:T(1,128)} add(f32[1,8,8,512]{3,0,1,2:T(1,128)S(1)} %copy-done.6, f32[1,8,8,512]{3,0,1,2:T(1,128)S(1)} %broadcast_in_dim.196) | non-fusion elementwise | flops 32768 | bytes 393216 | tf_op jit(solution)/shard_map/add | solution.py:252
  70.1 0.9 %copy-done.8 = f32[8,8,1,512]{3,0,1,2:T(8,128)S(1)} copy-done((f32[8,8,1,512]{3,0,1,2:T(8,128)S(1)}, f32[8,8,1,512]{3,0,1,2:T(8,128)}, u32[]{:S(2)}) %copy-start.8) | copy-done | bytes 131096
  71.0 0.8 %slice_bitcast_fusion.3 = (f32[4,4,512]{2,0,1:T(4,128)S(1)}, f32[4,4,512]{2,0,1:T(4,128)S(1)}) fusion(f32[4,2,4,512]{3,0,1,2:T(4,128)} %collective-permute-done.22), kind=kLoop, calls=%fused_computation.301 | loop fusion | bytes 131072 | tf_op jit(solution)/shard_map/slice | solution.py:35
  72.1 0.8 %copy-done.11 = f32[1,8,8,512]{3,0,1,2:T(1,128)S(1)} copy-done((f32[1,8,8,512]{3,0,1,2:T(1,128)S(1)}, f32[1,8,8,512]{3,0,1,2:T(1,128)}, u32[]{:S(2)}) %copy-start.11) | copy-done | bytes 131096
  73.1 1.7 %fusion.3 = f32[8,8,8,512]{3,0,1,2:T(8,128)S(1)} fusion(f32[8,8,8,512]{3,0,1,2:T(8,128)S(1)} %bitcast_add_fusion, f32[8,8,1,512]{3,0,1,2:T(8,128)S(1)} %bitcast_add_fusion.2, f32[10,1,8,512]{3,0,1,2:T(8,128)S(1)} %pad.146, f32[10,1,8,512]{3,0,1,2:T(8,128)S(1)} %pad.147, f32[1,8,8,512]{3,0,1,2:T(1,128)S(1)} %copy-done.11, f32[1,8,8,512]{3,0,1,2:T(1,128)S(1)} %copy-done.12, ...), kind=kLoop, calls=%fused_computation.8 | loop fusion | flops 9961472 | bytes 3620864 | tf_op jit(solution)/shard_map/mul | solution.py:307
  74.8 2.3 %convolution_convert_fusion = bf16[8,8,8,512]{3,2,1,0:T(8,128)(2,1)} fusion(f32[512,512]{1,0:T(8,128)S(1)} %fusion.67, f32[8,8,8,512]{3,0,1,2:T(8,128)S(1)} %fusion.3), kind=kOutput, calls=%fused_computation.4 | convolution fusion | flops 805568512 | bytes 2621440 | tf_op jit(solution)/shard_map/dot_general | solution.py:312
  (215 shorter events, 7.7 us)
Async XLA Ops:
  1.5 11.9 %collective-permute-start.2 = (f32[8,2,8,512]{3,0,1,2:T(8,128)S(1)}, f32[8,2,8,512]{3,0,1,2:T(8,128)S(1)}, u32[]{:S(2)}, u32[]{:S(2)}) collective-permute-start(f32[8,2,8,512]{3,0,1,2:T(8,128)S(1)} %pad_maximum_fusion.64), channel_id=1, source_target_pairs={{0,4},{4,0},{1,5},{5,1},{2,6},{6,2},{3,7},{7,3},{8,12},{12,8},{9,1... | collective-permute-start | bytes 786440 | tf_op jit(solution)/shard_map/ppermute | solution.py:33
  4.8 8.8 %collective-permute-start = (f32[1,8,8,512]{3,0,1,2:T(1,128)S(1)}, f32[1,8,8,512]{3,0,1,2:T(1,128)S(1)}, u32[]{:S(2)}, u32[]{:S(2)}) collective-permute-start(f32[1,8,8,512]{3,0,1,2:T(1,128)S(1)} %get-tuple-element.8), channel_id=1, source_target_pairs={{0,24},{8,0},{16,8},{24,16},{1,25},{9,1},{17,9},{25,17},{2,26},{10... | collective-permute-start | bytes 393224 | tf_op jit(solution)/shard_map/ppermute | solution.py:23
  8.4 6.8 %collective-permute-start.1 = (f32[1,8,8,512]{3,0,1,2:T(1,128)S(1)}, f32[1,8,8,512]{3,0,1,2:T(1,128)S(1)}, u32[]{:S(2)}, u32[]{:S(2)}) collective-permute-start(f32[1,8,8,512]{3,0,1,2:T(1,128)S(1)} %get-tuple-element.7), channel_id=1, source_target_pairs={{0,8},{8,16},{16,24},{24,0},{1,9},{9,17},{17,25},{25,1},{2,10},{10... | collective-permute-start | bytes 393224 | tf_op jit(solution)/shard_map/ppermute | solution.py:23
  8.4 6.7 %collective-permute-start.3 = (f32[8,8,1,512]{3,0,1,2:T(8,128)S(1)}, f32[8,8,1,512]{3,0,1,2:T(8,128)S(1)}, u32[]{:S(2)}, u32[]{:S(2)}) collective-permute-start(f32[8,8,1,512]{3,0,1,2:T(8,128)S(1)} %get-tuple-element.5), channel_id=1, source_target_pairs={{0,3},{1,0},{2,1},{3,2},{4,7},{5,4},{6,5},{7,6},{8,11},{9,8},{10,9... | collective-permute-start | bytes 393224 | tf_op jit(solution)/shard_map/ppermute | solution.py:23
  8.9 6.3 %collective-permute-start.4 = (f32[8,8,1,512]{3,0,1,2:T(8,128)S(1)}, f32[8,8,1,512]{3,0,1,2:T(8,128)S(1)}, u32[]{:S(2)}, u32[]{:S(2)}) collective-permute-start(f32[8,8,1,512]{3,0,1,2:T(8,128)S(1)} %get-tuple-element.6), channel_id=1, source_target_pairs={{0,1},{1,2},{2,3},{3,0},{4,5},{5,6},{6,7},{7,4},{8,9},{9,10},{10,1... | collective-permute-start | bytes 393224 | tf_op jit(solution)/shard_map/ppermute | solution.py:23
  10.3 1.3 %copy-start.28 = (s32[3,2,512]{2,1,0:T(2,128)S(1)}, s32[3,2,512]{2,1,0:T(2,128)}, u32[]{:S(2)}) copy-start(s32[3,2,512]{2,1,0:T(2,128)} %param.5) | copy-start | bytes 36868
  11.7 0.8 %copy-start.14 = (f32[1,128,128]{2,1,0:T(8,128)S(1)}, f32[1,128,128]{2,1,0:T(8,128)}, u32[]{:S(2)}) copy-start(f32[1,128,128]{2,1,0:T(8,128)} %param.7) | copy-start | bytes 196612
  12.6 2.6 %copy-start.1 = (f32[512,512]{1,0:T(8,128)}, f32[512,512]{1,0:T(8,128)S(1)}, u32[]{:S(2)}) copy-start(f32[512,512]{1,0:T(8,128)S(1)} %bitcast_dynamic-update-slice_fusion) | copy-start | bytes 3145732
  13.5 1.7 %copy-start = (bf16[8,8,8,512]{3,2,1,0:T(8,128)(2,1)S(1)}, bf16[8,8,8,512]{3,2,1,0:T(8,128)(2,1)}, u32[]{:S(2)}) copy-start(bf16[8,8,8,512]{3,2,1,0:T(8,128)(2,1)} %param.4) | copy-start | bytes 1572868
  13.6 3.3 %copy-start.3 = (f32[1,8,8,512]{3,0,1,2:T(1,128)}, f32[1,8,8,512]{3,0,1,2:T(1,128)S(1)}, u32[]{:S(2)}) copy-start(f32[1,8,8,512]{3,0,1,2:T(1,128)S(1)} %collective-permute-done) | copy-start | bytes 393220
  15.2 1.6 %copy-start.5 = (f32[1,8,8,512]{3,0,1,2:T(1,128)}, f32[1,8,8,512]{3,0,1,2:T(1,128)S(1)}, u32[]{:S(2)}) copy-start(f32[1,8,8,512]{3,0,1,2:T(1,128)S(1)} %collective-permute-done.1) | copy-start | bytes 393220
  15.2 1.6 %copy-start.7 = (f32[8,8,1,512]{3,0,1,2:T(8,128)}, f32[8,8,1,512]{3,0,1,2:T(8,128)S(1)}, u32[]{:S(2)}) copy-start(f32[8,8,1,512]{3,0,1,2:T(8,128)S(1)} %collective-permute-done.3) | copy-start | bytes 393220
  15.2 1.6 %copy-start.9 = (f32[8,8,1,512]{3,0,1,2:T(8,128)}, f32[8,8,1,512]{3,0,1,2:T(8,128)S(1)}, u32[]{:S(2)}) copy-start(f32[8,8,1,512]{3,0,1,2:T(8,128)S(1)} %collective-permute-done.4) | copy-start | bytes 393220
  18.3 4.6 %collective-permute-start.7 = (f32[4,2,4,512]{3,0,1,2:T(4,128)S(1)}, f32[4,2,4,512]{3,0,1,2:T(4,128)S(1)}, u32[]{:S(2)}, u32[]{:S(2)}) collective-permute-start(f32[4,2,4,512]{3,0,1,2:T(4,128)S(1)} %pad_maximum_fusion.146), channel_id=1, source_target_pairs={{0,4},{4,0},{1,5},{5,1},{2,6},{6,2},{3,7},{7,3},{8,12},{12,8},{9,1... | collective-permute-start | bytes 196616 | tf_op jit(solution)/shard_map/ppermute | solution.py:33
  18.9 5.0 %collective-permute-start.5 = (f32[1,4,4,512]{3,0,1,2:T(1,128)S(1)}, f32[1,4,4,512]{3,0,1,2:T(1,128)S(1)}, u32[]{:S(2)}, u32[]{:S(2)}) collective-permute-start(f32[1,4,4,512]{3,0,1,2:T(1,128)S(1)} %get-tuple-element.42), channel_id=1, source_target_pairs={{0,24},{8,0},{16,8},{24,16},{1,25},{9,1},{17,9},{25,17},{2,26},{10... | collective-permute-start | bytes 98312 | tf_op jit(solution)/shard_map/ppermute | solution.py:23
  22.1 5.7 %collective-permute-start.6 = (f32[1,4,4,512]{3,0,1,2:T(1,128)S(1)}, f32[1,4,4,512]{3,0,1,2:T(1,128)S(1)}, u32[]{:S(2)}, u32[]{:S(2)}) collective-permute-start(f32[1,4,4,512]{3,0,1,2:T(1,128)S(1)} %get-tuple-element.41), channel_id=1, source_target_pairs={{0,8},{8,16},{16,24},{24,0},{1,9},{9,17},{17,25},{25,1},{2,10},{10... | collective-permute-start | bytes 98312 | tf_op jit(solution)/shard_map/ppermute | solution.py:23
  22.1 5.7 %collective-permute-start.8 = (f32[4,4,1,512]{3,0,1,2:T(4,128)S(1)}, f32[4,4,1,512]{3,0,1,2:T(4,128)S(1)}, u32[]{:S(2)}, u32[]{:S(2)}) collective-permute-start(f32[4,4,1,512]{3,0,1,2:T(4,128)S(1)} %get-tuple-element.39), channel_id=1, source_target_pairs={{0,3},{1,0},{2,1},{3,2},{4,7},{5,4},{6,5},{7,6},{8,11},{9,8},{10,9... | collective-permute-start | bytes 98312 | tf_op jit(solution)/shard_map/ppermute | solution.py:23
  22.9 5.0 %collective-permute-start.9 = (f32[4,4,1,512]{3,0,1,2:T(4,128)S(1)}, f32[4,4,1,512]{3,0,1,2:T(4,128)S(1)}, u32[]{:S(2)}, u32[]{:S(2)}) collective-permute-start(f32[4,4,1,512]{3,0,1,2:T(4,128)S(1)} %get-tuple-element.40), channel_id=1, source_target_pairs={{0,1},{1,2},{2,3},{3,0},{4,5},{5,6},{6,7},{7,4},{8,9},{9,10},{10,1... | collective-permute-start | bytes 98312 | tf_op jit(solution)/shard_map/ppermute | solution.py:23
  23.6 20.7 %copy-start.2 = (f32[512,512]{1,0:T(8,128)S(1)}, f32[512,512]{1,0:T(8,128)}, u32[]{:S(2)}) copy-start(f32[512,512]{1,0:T(8,128)} %copy-done.1) | copy-start | bytes 3145732
  23.9 4.3 %copy-start.17 = (f32[1,4,4,512]{3,0,1,2:T(1,128)}, f32[1,4,4,512]{3,0,1,2:T(1,128)S(1)}, u32[]{:S(2)}) copy-start(f32[1,4,4,512]{3,0,1,2:T(1,128)S(1)} %collective-permute-done.5) | copy-start | bytes 98308
  28.7 6.6 %collective-permute-start.10 = (f32[20480]{0:T(1024)S(1)}, f32[20480]{0:T(1024)S(1)}, u32[]{:S(2)}, u32[]{:S(2)}) collective-permute-start(f32[20480]{0:T(1024)S(1)} %pad_maximum_fusion.97), channel_id=1, source_target_pairs={{0,24},{8,0},{16,8},{24,16},{1,25},{9,1},{17,9},{25,17},{2,26},{10... | collective-permute-start | bytes 245768 | tf_op jit(solution)/shard_map/ppermute | solution.py:23
  31.0 8.0 %collective-permute-start.11 = (f32[20480]{0:T(1024)S(1)}, f32[20480]{0:T(1024)S(1)}, u32[]{:S(2)}, u32[]{:S(2)}) collective-permute-start(f32[20480]{0:T(1024)S(1)} %pad_maximum_fusion.97), channel_id=1, source_target_pairs={{0,16},{8,24},{16,0},{24,8},{1,17},{9,25},{17,1},{25,9},{2,18},{10... | collective-permute-start | bytes 245768 | tf_op jit(solution)/shard_map/ppermute | solution.py:23
  31.0 8.0 %collective-permute-start.12 = (f32[20480]{0:T(1024)S(1)}, f32[20480]{0:T(1024)S(1)}, u32[]{:S(2)}, u32[]{:S(2)}) collective-permute-start(f32[20480]{0:T(1024)S(1)} %pad_maximum_fusion.97), channel_id=1, source_target_pairs={{0,8},{8,16},{16,24},{24,0},{1,9},{9,17},{17,25},{25,1},{2,10},{10... | collective-permute-start | bytes 245768 | tf_op jit(solution)/shard_map/ppermute | solution.py:23
  39.7 4.6 %collective-permute-start.13 = (f32[8,2,2,512]{3,0,1,2:T(8,128)S(1)}, f32[8,2,2,512]{3,0,1,2:T(8,128)S(1)}, u32[]{:S(2)}, u32[]{:S(2)}) collective-permute-start(f32[8,2,2,512]{3,0,1,2:T(8,128)S(1)} %pad_maximum_fusion.147), channel_id=1, source_target_pairs={{1,0},{2,1},{3,2},{0,3},{5,4},{6,5},{7,6},{4,7},{9,8},{10,9},{11,1... | collective-permute-start | bytes 196616 | tf_op jit(solution)/shard_map/ppermute | solution.py:97
  39.7 6.0 %collective-permute-start.14 = (f32[8,2,2,512]{3,0,1,2:T(8,128)S(1)}, f32[8,2,2,512]{3,0,1,2:T(8,128)S(1)}, u32[]{:S(2)}, u32[]{:S(2)}) collective-permute-start(f32[8,2,2,512]{3,0,1,2:T(8,128)S(1)} %pad_maximum_fusion.147), channel_id=1, source_target_pairs={{2,0},{3,1},{0,2},{1,3},{6,4},{7,5},{4,6},{5,7},{10,8},{11,9},{8,1... | collective-permute-start | bytes 196616 | tf_op jit(solution)/shard_map/ppermute | solution.py:97
  41.4 4.4 %collective-permute-start.15 = (f32[8,2,2,512]{3,0,1,2:T(8,128)S(1)}, f32[8,2,2,512]{3,0,1,2:T(8,128)S(1)}, u32[]{:S(2)}, u32[]{:S(2)}) collective-permute-start(f32[8,2,2,512]{3,0,1,2:T(8,128)S(1)} %pad_maximum_fusion.147), channel_id=1, source_target_pairs={{3,0},{0,1},{1,2},{2,3},{7,4},{4,5},{5,6},{6,7},{11,8},{8,9},{9,10... | collective-permute-start | bytes 196616 | tf_op jit(solution)/shard_map/ppermute | solution.py:97
  41.4 4.5 %collective-permute-start.16 = (f32[8,2,2,512]{3,0,1,2:T(8,128)S(1)}, f32[8,2,2,512]{3,0,1,2:T(8,128)S(1)}, u32[]{:S(2)}, u32[]{:S(2)}) collective-permute-start(f32[8,2,2,512]{3,0,1,2:T(8,128)S(1)} %pad_maximum_fusion.147), channel_id=1, source_target_pairs={{4,0},{5,1},{6,2},{7,3},{0,4},{1,5},{2,6},{3,7},{12,8},{13,9},{14,... | collective-permute-start | bytes 196616 | tf_op jit(solution)/shard_map/ppermute | solution.py:97
  42.9 3.9 %collective-permute-start.17 = (f32[8,2,2,512]{3,0,1,2:T(8,128)S(1)}, f32[8,2,2,512]{3,0,1,2:T(8,128)S(1)}, u32[]{:S(2)}, u32[]{:S(2)}) collective-permute-start(f32[8,2,2,512]{3,0,1,2:T(8,128)S(1)} %pad_maximum_fusion.147), channel_id=1, source_target_pairs={{5,0},{6,1},{7,2},{4,3},{1,4},{2,5},{3,6},{0,7},{13,8},{14,9},{15,... | collective-permute-start | bytes 196616 | tf_op jit(solution)/shard_map/ppermute | solution.py:97
  44.3 5.2 %collective-permute-start.18 = (f32[8,2,2,512]{3,0,1,2:T(8,128)S(1)}, f32[8,2,2,512]{3,0,1,2:T(8,128)S(1)}, u32[]{:S(2)}, u32[]{:S(2)}) collective-permute-start(f32[8,2,2,512]{3,0,1,2:T(8,128)S(1)} %pad_maximum_fusion.147), channel_id=1, source_target_pairs={{6,0},{7,1},{4,2},{5,3},{2,4},{3,5},{0,6},{1,7},{14,8},{15,9},{12,... | collective-permute-start | bytes 196616 | tf_op jit(solution)/shard_map/ppermute | solution.py:97
  45.7 4.6 %collective-permute-start.19 = (f32[8,2,2,512]{3,0,1,2:T(8,128)S(1)}, f32[8,2,2,512]{3,0,1,2:T(8,128)S(1)}, u32[]{:S(2)}, u32[]{:S(2)}) collective-permute-start(f32[8,2,2,512]{3,0,1,2:T(8,128)S(1)} %pad_maximum_fusion.147), channel_id=1, source_target_pairs={{7,0},{4,1},{5,2},{6,3},{3,4},{0,5},{1,6},{2,7},{15,8},{12,9},{13,... | collective-permute-start | bytes 196616 | tf_op jit(solution)/shard_map/ppermute | solution.py:97
  53.9 0.8 %copy-start.16 = (f32[4,2,4,512]{3,0,1,2:T(4,128)S(1)}, f32[4,2,4,512]{3,0,1,2:T(4,128)}, u32[]{:S(2)}) copy-start(f32[4,2,4,512]{3,0,1,2:T(4,128)} %copy-done.15) | copy-start | bytes 196612
  54.9 0.8 copy-start.22
  55.7 0.8 copy-start.18
  56.4 0.8 copy-start.20
  56.4 0.8 %copy-start.24 = (f32[4,4,1,512]{3,0,1,2:T(4,128)S(1)}, f32[4,4,1,512]{3,0,1,2:T(4,128)}, u32[]{:S(2)}) copy-start(f32[4,4,1,512]{3,0,1,2:T(4,128)} %copy-done.23) | copy-start | bytes 98308
  58.3 6.0 %copy-start.26 = (f32[20480]{0:T(1024)S(1)}, f32[20480]{0:T(1024)}, u32[]{:S(2)}) copy-start(f32[20480]{0:T(1024)} %copy-done.25) | copy-start | bytes 245764
  58.9 12.1 %collective-permute-start.22 = (f32[4,2,4,512]{3,0,1,2:T(4,128)}, f32[4,2,4,512]{3,0,1,2:T(4,128)}, u32[]{:S(2)}, u32[]{:S(2)}) collective-permute-start(f32[4,2,4,512]{3,0,1,2:T(4,128)} %pad_maximum_fusion.148), channel_id=1, source_target_pairs={{0,4},{4,0},{1,5},{5,1},{2,6},{6,2},{3,7},{7,3},{8,12},{12,8},{9,1... | collective-permute-start | bytes 196616 | tf_op jit(solution)/shard_map/ppermute | solution.py:33
  60.4 4.6 %collective-permute-start.20 = (f32[1,4,4,512]{3,0,1,2:T(1,128)S(1)}, f32[1,4,4,512]{3,0,1,2:T(1,128)S(1)}, u32[]{:S(2)}, u32[]{:S(2)}) collective-permute-start(f32[1,4,4,512]{3,0,1,2:T(1,128)S(1)} %get-tuple-element.36), channel_id=1, source_target_pairs={{0,24},{8,0},{16,8},{24,16},{1,25},{9,1},{17,9},{25,17},{2,26},{10... | collective-permute-start | bytes 98312 | tf_op jit(solution)/shard_map/ppermute | solution.py:23
  61.3 5.7 %collective-permute-start.21 = (f32[1,4,4,512]{3,0,1,2:T(1,128)S(1)}, f32[1,4,4,512]{3,0,1,2:T(1,128)S(1)}, u32[]{:S(2)}, u32[]{:S(2)}) collective-permute-start(f32[1,4,4,512]{3,0,1,2:T(1,128)S(1)} %get-tuple-element.35), channel_id=1, source_target_pairs={{0,8},{8,16},{16,24},{24,0},{1,9},{9,17},{17,25},{25,1},{2,10},{10... | collective-permute-start | bytes 98312 | tf_op jit(solution)/shard_map/ppermute | solution.py:23
  62.5 4.8 %collective-permute-start.24 = (f32[4,4,1,512]{3,0,1,2:T(4,128)}, f32[4,4,1,512]{3,0,1,2:T(4,128)S(1)}, u32[]{:S(2)}, u32[]{:S(2)}) collective-permute-start(f32[4,4,1,512]{3,0,1,2:T(4,128)} %get-tuple-element.34), channel_id=1, source_target_pairs={{0,1},{1,2},{2,3},{3,0},{4,5},{5,6},{6,7},{7,4},{8,9},{9,10},{10,1... | collective-permute-start | bytes 98312 | tf_op jit(solution)/shard_map/ppermute | solution.py:23
  62.5 4.9 %collective-permute-start.23 = (f32[4,4,1,512]{3,0,1,2:T(4,128)}, f32[4,4,1,512]{3,0,1,2:T(4,128)S(1)}, u32[]{:S(2)}, u32[]{:S(2)}) collective-permute-start(f32[4,4,1,512]{3,0,1,2:T(4,128)} %get-tuple-element.33), channel_id=1, source_target_pairs={{0,3},{1,0},{2,1},{3,2},{4,7},{5,4},{6,5},{7,6},{8,11},{9,8},{10,9... | collective-permute-start | bytes 98312 | tf_op jit(solution)/shard_map/ppermute | solution.py:23
  67.4 0.9 %copy-start.4 = (f32[1,8,8,512]{3,0,1,2:T(1,128)S(1)}, f32[1,8,8,512]{3,0,1,2:T(1,128)}, u32[]{:S(2)}) copy-start(f32[1,8,8,512]{3,0,1,2:T(1,128)} %copy-done.3) | copy-start | bytes 393220
  68.3 0.9 %copy-start.6 = (f32[1,8,8,512]{3,0,1,2:T(1,128)S(1)}, f32[1,8,8,512]{3,0,1,2:T(1,128)}, u32[]{:S(2)}) copy-start(f32[1,8,8,512]{3,0,1,2:T(1,128)} %copy-done.5) | copy-start | bytes 393220
  69.2 0.9 %copy-start.10 = (f32[8,8,1,512]{3,0,1,2:T(8,128)S(1)}, f32[8,8,1,512]{3,0,1,2:T(8,128)}, u32[]{:S(2)}) copy-start(f32[8,8,1,512]{3,0,1,2:T(8,128)} %copy-done.9) | copy-start | bytes 393220
  70.1 0.9 %copy-start.8 = (f32[8,8,1,512]{3,0,1,2:T(8,128)S(1)}, f32[8,8,1,512]{3,0,1,2:T(8,128)}, u32[]{:S(2)}) copy-start(f32[8,8,1,512]{3,0,1,2:T(8,128)} %copy-done.7) | copy-start | bytes 393220
  72.1 0.9 %copy-start.11 = (f32[1,8,8,512]{3,0,1,2:T(1,128)S(1)}, f32[1,8,8,512]{3,0,1,2:T(1,128)}, u32[]{:S(2)}) copy-start(f32[1,8,8,512]{3,0,1,2:T(1,128)} %add.419) | copy-start | bytes 393220
  72.1 1.0 %copy-start.12 = (f32[1,8,8,512]{3,0,1,2:T(1,128)S(1)}, f32[1,8,8,512]{3,0,1,2:T(1,128)}, u32[]{:S(2)}) copy-start(f32[1,8,8,512]{3,0,1,2:T(1,128)} %add.420) | copy-start | bytes 393220
  72.1 1.0 %copy-start.13 = (f32[8,8,512]{2,0,1:T(8,128)S(1)}, f32[8,8,512]{2,0,1:T(8,128)}, u32[]{:S(2)}) copy-start(f32[8,8,512]{2,0,1:T(8,128)} %broadcast_multiply_fusion.1) | copy-start | bytes 393220
  (6 other events, 3.8 us)

commit v6 on v5

--- a/solution.py
+++ b/solution.py
@@ -13,6 +13,7 @@
 GRID_AXES = (("gx", 0), ("gy", 1), ("gz", 2))
 COARSE_HALO = 10
 CHUNK_BYTES = 1 << 21
+LANES = 128
 
 
 def shifted(block, axis, offset):
@@ -138,7 +139,7 @@
 def pad_with(block, faces):
     padded = block
     for dim, (lo, hi) in enumerate(faces):
-        widths = [(0, 0)] * 4
+        widths = [(0, 0)] * block.ndim
         for other in range(dim):
             widths[other] = (1, 1)
         lo = jnp.pad(lo, widths)
@@ -168,8 +169,9 @@
 
 
 def restrict(field):
-    size_a, size_b, size_c, width = field.shape
-    return field.reshape(size_a // 2, 2, size_b // 2, 2, size_c // 2, 2, width).mean(axis=(1, 3, 5))
+    size_a, size_b, size_c = field.shape[:3]
+    rest = field.shape[3:]
+    return field.reshape((size_a // 2, 2, size_b // 2, 2, size_c // 2, 2) + rest).mean(axis=(1, 3, 5))
 
 
 def prolong(field):
@@ -191,7 +193,7 @@
     starts.append(start)
     extended, joint_starts = extend_joint(extended, ("gy", "gz"), (1, 2), COARSE_HALO)
     starts.extend(joint_starts)
-    width = extended.shape[3]
+    width = extended.shape[3] * extended.shape[4]
     chunks = 1
     while extended.size * 4 // chunks > CHUNK_BYTES and width % (2 * chunks * 128) == 0:
         chunks *= 2
@@ -199,13 +201,15 @@
         return coarse_levels(extended, starts, rhs_two.shape), tiles_by_step
     part = width // chunks
 
+    groups = extended.shape[3] // chunks
+
     def one_chunk(k):
-        piece = lax.dynamic_slice_in_dim(extended, k * part, part, axis=3)
+        piece = lax.dynamic_slice_in_dim(extended, k * groups, groups, axis=3)
         return coarse_levels(piece, starts, rhs_two.shape)
 
     outs = lax.map(one_chunk, jnp.arange(chunks))
     outs = jnp.moveaxis(outs, 0, 3)
-    return outs.reshape(outs.shape[:3] + (width,)), tiles_by_step
+    return outs.reshape(outs.shape[:3] + (extended.shape[3], extended.shape[4])), tiles_by_step
 
 
 def coarse_levels(extended, starts, block_shape):
@@ -299,7 +303,10 @@
 
 def body(residuals, patch_box, tile_pairs, inv_tiles):
     size_a, size_b, size_c, orb_count = residuals.shape
-    correct, tiles_by_step = vcycle(residuals, inv_tiles)
+    lanes = LANES if orb_count % LANES == 0 else orb_count
+    grouped = residuals.reshape(size_a, size_b, size_c, orb_count // lanes, lanes)
+    correct, tiles_by_step = vcycle(grouped, inv_tiles)
+    correct = correct.reshape(size_a, size_b, size_c, orb_count)
     gram = gram_matrix(tiles_by_step, inv_tiles, tile_pairs, orb_count)
     mask_first = dim_mask(patch_box[0], lax.axis_index("gx") * size_a, size_a)
     mask_second = dim_mask(patch_box[1], lax.axis_index("gy") * size_b, size_b)

time: 77.8 us -> 74.9 us (0.963)
  other arithmetic: 11.9 us -> 9.28 us
  waiting for transfers between devices: 15.9 us -> 14.3 us
  starting transfers between devices: 26.1 us -> 27.3 us
  matrix products: 2.25 us -> 3.38 us
  local copies, waits for them, and re-layouts: 14.8 us -> 13.7 us
    ppermute x7, waiting for transfers between devices: 4.57 us -> 1.26 us  [fetch(): cache[steps] = lax.ppermute(block, tuple(axes), pairs)]
    dynamic_update_slice x4, local copies, waits for them, and re-layouts: 0.03 us -> 1.92 us  [gram_matrix(): total = lax.dynamic_update_slice(total, piece[slot], (row, col))]
    ppermute x15, waiting for transfers between devices: 11.2 us -> 13 us  [shifted(): lax.ppermute(block, axis, [(j, (j - step) % count) for j in range(count)])]
    mul x1 -> x0, other arithmetic: 1.66 us -> none  [body(): correct * (mask_first[:, None, None, :] * mask_second[None, :, None, :] *...]
    ppermute x7, starting transfers between devices: 5.98 us -> 7.37 us  [fetch(): cache[steps] = lax.ppermute(block, tuple(axes), pairs)]
    reshape x6 -> x0, local copies, waits for them, and re-layouts: 1.33 us -> none  [the longest x3 1.03 us: restrict(): field.reshape(size_a // 2, 2, size_b // 2, 2, size_c // 2, 2, width)]
    unnamed x62 -> x38, local copies, waits for them, and re-layouts: 8.73 us -> 7.5 us
    dot_general x1, matrix products: 2.25 us -> 3.38 us  [body(): jnp.dot(rows, gram, precision=lax.Precision.HIGH, preferred_element_type=...]
  transfers between devices with their start and end apart: 25 -> 25, of which waited for: 9 -> 8; matrix products, arithmetic and copies ran while one was open for 7% -> 9% of each run, Pallas kernels for 0% -> 0%
where the time goes in v6:
time: 74.9 us; the launch traced here: 74.2 us
  starting transfers between devices  27.3 us (36%)
  waiting for transfers between devices  14.3 us (19%)
  local copies, waits for them, and re-layouts  13.7 us (18%)
  other arithmetic  9.28 us (12%)
  between operations  6.2 us (8%)
  matrix products  3.38 us (5%)
    ppermute x15, starting transfers between devices, shifted(): lax.ppermute(block, axis, [(j, (j - step) % count) for j in range(count)])  15.2 us
    ppermute x15, waiting for transfers between devices, shifted(): lax.ppermute(block, axis, [(j, (j - step) % count) for j in range(count)])  13 us
    unnamed x38, local copies, waits for them, and re-layouts  7.5 us
    ppermute x7, starting transfers between devices, fetch(): cache[steps] = lax.ppermute(block, tuple(axes), pairs)  7.37 us
    ppermute x3, starting transfers between devices, axis_faces(): lax.ppermute(jnp.concatenate([first, last], axis=dim), axis, [(0, 1), (1,...  4.74 us
    dot_general x1, matrix products, body(): jnp.dot(rows, gram, precision=lax.Precision.HIGH, preferred_element_type=...  3.38 us
    dynamic_update_slice x4, local copies, waits for them, and re-layouts, gram_matrix(): total = lax.dynamic_update_slice(total, piece[slot], (row, col))  1.92 us
  transfers between devices with their start and end apart: 25, of which 8 were waited for; matrix products, arithmetic and copies ran while one was open for 9% of the time, Pallas kernels for 0%

profile of v6, /device:TPU:0, one launch (start us, length us, event | category | flops | bytes accessed | tf_op | source)
XLA Modules:
  0.0 74.2 jit_solution(13726425635034849402)
XLA Ops:
  0.0 1.2 %convert_multiply_fusion.1 = f32[8,8,8,4,128]{4,2,3,1,0:T(8,128)S(1)} fusion(bf16[8,8,8,512]{3,2,1,0:T(8,128)(2,1)} %param.4), kind=kLoop, calls=%fused_computation.3 | loop fusion | flops 524288 | bytes 1572864 | tf_op jit(solution)/shard_map/div | solution.py:289
  1.4 0.5 collective-permute-start.4
  2.0 2.6 %collective-permute-start.2 = (f32[8,2,8,4,128]{4,2,3,1,0:T(8,128)S(1)}, f32[8,2,8,4,128]{4,2,3,1,0:T(8,128)S(1)}, u32[]{:S(2)}, u32[]{:S(2)}) collective-permute-start(f32[8,2,8,4,128]{4,2,3,1,0:T(8,128)S(1)} %pad_maximum_fusion.77), channel_id=1, source_target_pairs={{0,4},{4,0},{1,5},{5,1},{2,6},{6,2},{3,7},{7,3},{8,12},{12,8},{9,1... | collective-permute-start | bytes 786440 | tf_op jit(solution)/shard_map/ppermute | solution.py:34
  4.6 0.7 fusion.141
  5.3 3.6 %collective-permute-start = (f32[1,8,8,4,128]{4,2,3,1,0:T(8,128)}, f32[1,8,8,4,128]{4,2,3,1,0:T(8,128)S(1)}, u32[]{:S(2)}, u32[]{:S(2)}) collective-permute-start(f32[1,8,8,4,128]{4,2,3,1,0:T(8,128)} %get-tuple-element.10), channel_id=1, source_target_pairs={{0,24},{8,0},{16,8},{24,16},{1,25},{9,1},{17,9},{25,17},{2,26},{10... | collective-permute-start | bytes 393224 | tf_op jit(solution)/shard_map/ppermute | solution.py:24
  8.9 1.2 %collective-permute-start.3 = (f32[8,8,1,4,128]{4,2,3,1,0:T(1,128)S(1)}, f32[8,8,1,4,128]{4,2,3,1,0:T(1,128)S(1)}, u32[]{:S(2)}, u32[]{:S(2)}) collective-permute-start(f32[8,8,1,4,128]{4,2,3,1,0:T(1,128)S(1)} %get-tuple-element.7), channel_id=1, source_target_pairs={{0,3},{1,0},{2,1},{3,2},{4,7},{5,4},{6,5},{7,6},{8,11},{9,8},{10,9... | collective-permute-start | bytes 393224 | tf_op jit(solution)/shard_map/ppermute | solution.py:24
  10.0 0.7 copy-done.14
  10.7 0.7 constant_dynamic-slice_fusion
  12.8 0.6 fusion.166
  13.5 0.7 copy-done.3
  14.3 0.6 iota_add_fusion
  15.3 0.7 broadcast_multiply_fusion.1
  16.0 1.2 %collective-permute-done.1 = f32[1,8,8,4,128]{4,2,3,1,0:T(8,128)S(1)} collective-permute-done((f32[1,8,8,4,128]{4,2,3,1,0:T(8,128)}, f32[1,8,8,4,128]{4,2,3,1,0:T(8,128)S(1)}, u32[]{:S(2)}, u32[]{:S(2)}) %collective-permute-start.1) | collective-permute-done | bytes 131104 | tf_op jit(solution)/shard_map/ppermute | solution.py:24
  17.2 0.9 %convert_subtract_fusion.1 = f32[8,8,8,4,128]{4,2,3,1,0:T(8,128)S(1)} fusion(f32[8,8,1,4,128]{4,2,3,1,0:T(1,128)S(1)} %collective-permute-done.4, f32[10,1,8,4,128]{4,2,3,1,0:T(8,128)S(1)} %pad.114, f32[10,1,8,4,128]{4,2,3,1,0:T(8,128)S(1)} %pad.115, f32[1,8,8,4,128]{4,2,3,1,0:T(8,128)S(1)} %collective-permute-done, ...), kind=kLoop, calls=%fused_computation.1 | loop fusion | flops 8912896 | bytes 3473408 | tf_op jit(solution)/shard_map/sub | solution.py:291
  18.2 0.7 reduce_sum.27
  19.0 0.6 collective-permute-start.7
  19.6 3.4 %collective-permute-start.5 = (f32[1,4,4,4,128]{4,2,3,1,0:T(4,128)S(1)}, f32[1,4,4,4,128]{4,2,3,1,0:T(4,128)S(1)}, u32[]{:S(2)}, u32[]{:S(2)}) collective-permute-start(f32[1,4,4,4,128]{4,2,3,1,0:T(4,128)S(1)} %get-tuple-element.44), channel_id=1, source_target_pairs={{0,24},{8,0},{16,8},{24,16},{1,25},{9,1},{17,9},{25,17},{2,26},{10... | collective-permute-start | bytes 98312 | tf_op jit(solution)/shard_map/ppermute | solution.py:24
  23.0 1.4 %collective-permute-start.8 = (f32[4,4,1,4,128]{4,2,3,1,0:T(1,128)S(1)}, f32[4,4,1,4,128]{4,2,3,1,0:T(1,128)S(1)}, u32[]{:S(2)}, u32[]{:S(2)}) collective-permute-start(f32[4,4,1,4,128]{4,2,3,1,0:T(1,128)S(1)} %get-tuple-element.41), channel_id=1, source_target_pairs={{0,3},{1,0},{2,1},{3,2},{4,7},{5,4},{6,5},{7,6},{8,11},{9,8},{10,9... | collective-permute-start | bytes 98312 | tf_op jit(solution)/shard_map/ppermute | solution.py:24
  24.6 4.2 %collective-permute-done.6 = f32[1,4,4,4,128]{4,2,3,1,0:T(4,128)S(1)} collective-permute-done((f32[1,4,4,4,128]{4,2,3,1,0:T(4,128)S(1)}, f32[1,4,4,4,128]{4,2,3,1,0:T(4,128)S(1)}, u32[]{:S(2)}, u32[]{:S(2)}) %collective-permute-start.6) | collective-permute-done | bytes 32800 | tf_op jit(solution)/shard_map/ppermute | solution.py:24
  29.5 0.8 %copy-done.4 = f32[1,128,128]{2,1,0:T(8,128)S(1)} copy-done((f32[1,128,128]{2,1,0:T(8,128)S(1)}, f32[1,128,128]{2,1,0:T(8,128)}, u32[]{:S(2)}) %copy-start.4) | copy-done | bytes 65560
  30.3 0.8 %collective-permute-start.10 = (f32[20480]{0:T(1024)S(1)}, f32[20480]{0:T(1024)S(1)}, u32[]{:S(2)}, u32[]{:S(2)}) collective-permute-start(f32[20480]{0:T(1024)S(1)} %pad_maximum_fusion.110), channel_id=1, source_target_pairs={{0,24},{8,0},{16,8},{24,16},{1,25},{9,1},{17,9},{25,17},{2,26},{10... | collective-permute-start | bytes 245768 | tf_op jit(solution)/shard_map/ppermute | solution.py:24
  31.0 1.3 %collective-permute-start.12 = (f32[20480]{0:T(1024)S(1)}, f32[20480]{0:T(1024)S(1)}, u32[]{:S(2)}, u32[]{:S(2)}) collective-permute-start(f32[20480]{0:T(1024)S(1)} %pad_maximum_fusion.110), channel_id=1, source_target_pairs={{0,8},{8,16},{16,24},{24,0},{1,9},{9,17},{17,25},{25,1},{2,10},{10... | collective-permute-start | bytes 245768 | tf_op jit(solution)/shard_map/ppermute | solution.py:24
  32.3 0.7 copy-done.17
  36.9 3.4 %collective-permute-done.11 = f32[20480]{0:T(1024)S(1)} collective-permute-done((f32[20480]{0:T(1024)S(1)}, f32[20480]{0:T(1024)S(1)}, u32[]{:S(2)}, u32[]{:S(2)}) %collective-permute-start.11) | collective-permute-done | bytes 81952 | tf_op jit(solution)/shard_map/ppermute | solution.py:24
  40.3 1.3 %collective-permute-start.19 = (f32[8,2,2,4,128]{4,3,1,0,2:T(4,128)S(1)}, f32[8,2,2,4,128]{4,3,1,0,2:T(4,128)S(1)}, u32[]{:S(2)}, u32[]{:S(2)}) collective-permute-start(f32[8,2,2,4,128]{4,3,1,0,2:T(4,128)S(1)} %pad_maximum_fusion.160), channel_id=1, source_target_pairs={{7,0},{4,1},{5,2},{6,3},{3,4},{0,5},{1,6},{2,7},{15,8},{12,9},{13,... | collective-permute-start | bytes 196616 | tf_op jit(solution)/shard_map/ppermute | solution.py:98
  41.6 0.5 collective-permute-start.18
  42.2 2.3 %collective-permute-start.17 = (f32[8,2,2,4,128]{4,3,1,0,2:T(4,128)S(1)}, f32[8,2,2,4,128]{4,3,1,0,2:T(4,128)S(1)}, u32[]{:S(2)}, u32[]{:S(2)}) collective-permute-start(f32[8,2,2,4,128]{4,3,1,0,2:T(4,128)S(1)} %pad_maximum_fusion.160), channel_id=1, source_target_pairs={{5,0},{6,1},{7,2},{4,3},{1,4},{2,5},{3,6},{0,7},{13,8},{14,9},{15,... | collective-permute-start | bytes 196616 | tf_op jit(solution)/shard_map/ppermute | solution.py:98
  44.5 0.5 collective-permute-start.16
  45.0 0.6 fusion.94
  45.6 0.7 fusion.93
  46.2 1.3 %collective-permute-start.14 = (f32[8,2,2,4,128]{4,3,1,0,2:T(4,128)S(1)}, f32[8,2,2,4,128]{4,3,1,0,2:T(4,128)S(1)}, u32[]{:S(2)}, u32[]{:S(2)}) collective-permute-start(f32[8,2,2,4,128]{4,3,1,0,2:T(4,128)S(1)} %pad_maximum_fusion.160), channel_id=1, source_target_pairs={{2,0},{3,1},{0,2},{1,3},{6,4},{7,5},{4,6},{5,7},{10,8},{11,9},{8,1... | collective-permute-start | bytes 196616 | tf_op jit(solution)/shard_map/ppermute | solution.py:98
  47.5 1.5 %collective-permute-start.13 = (f32[8,2,2,4,128]{4,3,1,0,2:T(4,128)S(1)}, f32[8,2,2,4,128]{4,3,1,0,2:T(4,128)S(1)}, u32[]{:S(2)}, u32[]{:S(2)}) collective-permute-start(f32[8,2,2,4,128]{4,3,1,0,2:T(4,128)S(1)} %pad_maximum_fusion.160), channel_id=1, source_target_pairs={{1,0},{2,1},{3,2},{0,3},{5,4},{6,5},{7,6},{4,7},{9,8},{10,9},{11,1... | collective-permute-start | bytes 196616 | tf_op jit(solution)/shard_map/ppermute | solution.py:98
  49.0 0.6 fusion.92
  49.6 1.1 %collective-permute-done.14 = f32[8,2,2,4,128]{4,3,1,0,2:T(4,128)S(1)} collective-permute-done((f32[8,2,2,4,128]{4,3,1,0,2:T(4,128)S(1)}, f32[8,2,2,4,128]{4,3,1,0,2:T(4,128)S(1)}, u32[]{:S(2)}, u32[]{:S(2)}) %collective-permute-start.14) | collective-permute-done | bytes 65568 | tf_op jit(solution)/shard_map/ppermute | solution.py:98
  51.3 1.4 %fusion.53 = f32[8,4,8,4,128]{4,3,1,0,2:T(4,128)S(1)} fusion(f32[8,4,8,4,128]{4,3,1,0,2:T(4,128)S(1)} %get-tuple-element.6, f32[8,4,1,4,128]{4,3,1,0,2:T(4,128)S(1)} %get-tuple-element.26, f32[10,1,8,4,128]{4,3,1,0,2:T(4,128)S(1)} %pad.122, f32[10,1,8,4,128]{4,3,1,0,2:T(4,128)S(1)} %pad.123, f32[1,4,8,4,128]{4,3,1,0,2:T(4,128)S(1)} %get-tuple-element.28, ...), kind=kLoop, calls=%fused_computation.109 | loop fusion | flops 4325376 | bytes 2162688 | tf_op jit(solution)/shard_map/sub | solution.py:219
  53.8 1.5 %fusion.43 = f32[8,4,8,4,128]{4,3,1,0,2:T(4,128)S(1)} fusion(f32[8,4,8,4,128]{4,3,1,0,2:T(4,128)S(1)} %bitcast_add_fusion, f32[8,4,8,4,128]{4,3,1,0,2:T(4,128)S(1)} %get-tuple-element.6, f32[8,4,1,4,128]{4,3,1,0,2:T(4,128)S(1)} %get-tuple-element.20, f32[10,1,8,4,128]{4,3,1,0,2:T(4,128)S(1)} %pad.138, f32[10,1,8,4,128]{4,3,1,0,2:T(4,128)S(1)} %pad.139, ...), kind=kLoop, calls=%fused_computation.81 | loop fusion | flops 4587520 | bytes 2162688 | tf_op jit(solution)/shard_map/add | solution.py:227
  55.7 0.7 copy-done.12
  56.6 0.7 copy-done.10
  57.3 0.7 copy-done.8
  58.1 0.7 copy-done.6
  59.2 0.9 %collective-permute-start.24 = (f32[4,4,1,4,128]{4,2,3,1,0:T(1,128)S(1)}, f32[4,4,1,4,128]{4,2,3,1,0:T(1,128)S(1)}, u32[]{:S(2)}, u32[]{:S(2)}) collective-permute-start(f32[4,4,1,4,128]{4,2,3,1,0:T(1,128)S(1)} %get-tuple-element.36), channel_id=1, source_target_pairs={{0,1},{1,2},{2,3},{3,0},{4,5},{5,6},{6,7},{7,4},{8,9},{9,10},{10,1... | collective-permute-start | bytes 98312 | tf_op jit(solution)/shard_map/ppermute | solution.py:24
  60.1 1.6 %collective-permute-start.22 = (f32[4,2,4,4,128]{4,2,3,1,0:T(4,128)S(1)}, f32[4,2,4,4,128]{4,2,3,1,0:T(4,128)S(1)}, u32[]{:S(2)}, u32[]{:S(2)}) collective-permute-start(f32[4,2,4,4,128]{4,2,3,1,0:T(4,128)S(1)} %pad_maximum_fusion.161), channel_id=1, source_target_pairs={{0,4},{4,0},{1,5},{5,1},{2,6},{6,2},{3,7},{7,3},{8,12},{12,8},{9,1... | collective-permute-start | bytes 196616 | tf_op jit(solution)/shard_map/ppermute | solution.py:34
  61.7 1.8 %collective-permute-start.20 = (f32[1,4,4,4,128]{4,2,3,1,0:T(4,128)S(1)}, f32[1,4,4,4,128]{4,2,3,1,0:T(4,128)S(1)}, u32[]{:S(2)}, u32[]{:S(2)}) collective-permute-start(f32[1,4,4,4,128]{4,2,3,1,0:T(4,128)S(1)} %get-tuple-element.38), channel_id=1, source_target_pairs={{0,24},{8,0},{16,8},{24,16},{1,25},{9,1},{17,9},{25,17},{2,26},{10... | collective-permute-start | bytes 98312 | tf_op jit(solution)/shard_map/ppermute | solution.py:24
  64.0 0.6 broadcast_in_dim.188
  65.0 0.7 collective-permute-done.20
  65.7 3.5 %collective-permute-done.21 = f32[1,4,4,4,128]{4,2,3,1,0:T(4,128)S(1)} collective-permute-done((f32[1,4,4,4,128]{4,2,3,1,0:T(4,128)S(1)}, f32[1,4,4,4,128]{4,2,3,1,0:T(4,128)S(1)}, u32[]{:S(2)}, u32[]{:S(2)}) %collective-permute-start.21) | collective-permute-done | bytes 32800 | tf_op jit(solution)/shard_map/ppermute | solution.py:24
  69.8 0.9 %copy-done.2 = f32[512,512]{1,0:T(8,128)S(1)} copy-done((f32[512,512]{1,0:T(8,128)S(1)}, f32[512,512]{1,0:T(8,128)}, u32[]{:S(2)}) %copy-start.2) | copy-done | bytes 1048600
  70.8 3.4 %convolution_convert_fusion = bf16[8,8,8,512]{3,2,1,0:T(8,128)(2,1)} fusion(f32[8,8,8,4,128]{4,2,3,1,0:T(8,128)S(1)} %fusion.69, f32[8,8,1,4,128]{4,2,3,1,0:T(1,128)S(1)} %add.428, f32[10,1,8,4,128]{4,2,3,1,0:T(8,128)S(1)} %pad.146, f32[10,1,8,4,128]{4,2,3,1,0:T(8,128)S(1)} %pad.147, f32[1,8,8,4,128]{4,2,3,1,0:T(8,128)S(1)} %add.419, ...), kind=kOutput, calls=%fused_computation.4 | convolution fusion | flops 815529984 | bytes 4145152 | tf_op jit(solution)/shard_map/dot_general | solution.py:319
  (178 shorter events, 5.5 us)
Async XLA Ops:
  1.4 14.6 %collective-permute-start.4 = (f32[8,8,1,4,128]{4,2,3,1,0:T(1,128)S(1)}, f32[8,8,1,4,128]{4,2,3,1,0:T(1,128)S(1)}, u32[]{:S(2)}, u32[]{:S(2)}) collective-permute-start(f32[8,8,1,4,128]{4,2,3,1,0:T(1,128)S(1)} %get-tuple-element.8), channel_id=1, source_target_pairs={{0,1},{1,2},{2,3},{3,0},{4,5},{5,6},{6,7},{7,4},{8,9},{9,10},{10,1... | collective-permute-start | bytes 393224 | tf_op jit(solution)/shard_map/ppermute | solution.py:24
  2.0 13.9 %collective-permute-start.2 = (f32[8,2,8,4,128]{4,2,3,1,0:T(8,128)S(1)}, f32[8,2,8,4,128]{4,2,3,1,0:T(8,128)S(1)}, u32[]{:S(2)}, u32[]{:S(2)}) collective-permute-start(f32[8,2,8,4,128]{4,2,3,1,0:T(8,128)S(1)} %pad_maximum_fusion.77), channel_id=1, source_target_pairs={{0,4},{4,0},{1,5},{5,1},{2,6},{6,2},{3,7},{7,3},{8,12},{12,8},{9,1... | collective-permute-start | bytes 786440 | tf_op jit(solution)/shard_map/ppermute | solution.py:34
  5.3 10.7 %collective-permute-start = (f32[1,8,8,4,128]{4,2,3,1,0:T(8,128)}, f32[1,8,8,4,128]{4,2,3,1,0:T(8,128)S(1)}, u32[]{:S(2)}, u32[]{:S(2)}) collective-permute-start(f32[1,8,8,4,128]{4,2,3,1,0:T(8,128)} %get-tuple-element.10), channel_id=1, source_target_pairs={{0,24},{8,0},{16,8},{24,16},{1,25},{9,1},{17,9},{25,17},{2,26},{10... | collective-permute-start | bytes 393224 | tf_op jit(solution)/shard_map/ppermute | solution.py:24
  8.9 8.3 %collective-permute-start.1 = (f32[1,8,8,4,128]{4,2,3,1,0:T(8,128)}, f32[1,8,8,4,128]{4,2,3,1,0:T(8,128)S(1)}, u32[]{:S(2)}, u32[]{:S(2)}) collective-permute-start(f32[1,8,8,4,128]{4,2,3,1,0:T(8,128)} %get-tuple-element.9), channel_id=1, source_target_pairs={{0,8},{8,16},{16,24},{24,0},{1,9},{9,17},{17,25},{25,1},{2,10},{10... | collective-permute-start | bytes 393224 | tf_op jit(solution)/shard_map/ppermute | solution.py:24
  8.9 8.3 %collective-permute-start.3 = (f32[8,8,1,4,128]{4,2,3,1,0:T(1,128)S(1)}, f32[8,8,1,4,128]{4,2,3,1,0:T(1,128)S(1)}, u32[]{:S(2)}, u32[]{:S(2)}) collective-permute-start(f32[8,8,1,4,128]{4,2,3,1,0:T(1,128)S(1)} %get-tuple-element.7), channel_id=1, source_target_pairs={{0,3},{1,0},{2,1},{3,2},{4,7},{5,4},{6,5},{7,6},{8,11},{9,8},{10,9... | collective-permute-start | bytes 393224 | tf_op jit(solution)/shard_map/ppermute | solution.py:24
  10.0 0.7 copy-start.14
  11.4 1.3 %copy-start.15 = (s32[3,2,512]{2,1,0:T(2,128)S(1)}, s32[3,2,512]{2,1,0:T(2,128)}, u32[]{:S(2)}) copy-start(s32[3,2,512]{2,1,0:T(2,128)} %param.5) | copy-start | bytes 36868
  13.4 0.8 %copy-start.3 = (f32[1,128,128]{2,1,0:T(8,128)S(1)}, f32[1,128,128]{2,1,0:T(8,128)}, u32[]{:S(2)}) copy-start(f32[1,128,128]{2,1,0:T(8,128)} %param.7) | copy-start | bytes 196612
  14.2 1.0 %copy-start.1 = (f32[512,512]{1,0:T(8,128)}, f32[512,512]{1,0:T(8,128)S(1)}, u32[]{:S(2)}) copy-start(f32[512,512]{1,0:T(8,128)S(1)} %bitcast_dynamic-update-slice_fusion) | copy-start | bytes 3145732
  15.9 1.3 %copy-start = (bf16[8,8,8,512]{3,2,1,0:T(8,128)(2,1)S(1)}, bf16[8,8,8,512]{3,2,1,0:T(8,128)(2,1)}, u32[]{:S(2)}) copy-start(bf16[8,8,8,512]{3,2,1,0:T(8,128)(2,1)} %param.4) | copy-start | bytes 1572868
  19.0 5.3 %collective-permute-start.7 = (f32[4,2,4,4,128]{4,2,3,1,0:T(4,128)S(1)}, f32[4,2,4,4,128]{4,2,3,1,0:T(4,128)S(1)}, u32[]{:S(2)}, u32[]{:S(2)}) collective-permute-start(f32[4,2,4,4,128]{4,2,3,1,0:T(4,128)S(1)} %pad_maximum_fusion.159), channel_id=1, source_target_pairs={{0,4},{4,0},{1,5},{5,1},{2,6},{6,2},{3,7},{7,3},{8,12},{12,8},{9,1... | collective-permute-start | bytes 196616 | tf_op jit(solution)/shard_map/ppermute | solution.py:34
  19.6 4.8 %collective-permute-start.9 = (f32[4,4,1,4,128]{4,2,3,1,0:T(1,128)S(1)}, f32[4,4,1,4,128]{4,2,3,1,0:T(1,128)S(1)}, u32[]{:S(2)}, u32[]{:S(2)}) collective-permute-start(f32[4,4,1,4,128]{4,2,3,1,0:T(1,128)S(1)} %get-tuple-element.42), channel_id=1, source_target_pairs={{0,1},{1,2},{2,3},{3,0},{4,5},{5,6},{6,7},{7,4},{8,9},{9,10},{10,1... | collective-permute-start | bytes 98312 | tf_op jit(solution)/shard_map/ppermute | solution.py:24
  19.6 4.9 %collective-permute-start.5 = (f32[1,4,4,4,128]{4,2,3,1,0:T(4,128)S(1)}, f32[1,4,4,4,128]{4,2,3,1,0:T(4,128)S(1)}, u32[]{:S(2)}, u32[]{:S(2)}) collective-permute-start(f32[1,4,4,4,128]{4,2,3,1,0:T(4,128)S(1)} %get-tuple-element.44), channel_id=1, source_target_pairs={{0,24},{8,0},{16,8},{24,16},{1,25},{9,1},{17,9},{25,17},{2,26},{10... | collective-permute-start | bytes 98312 | tf_op jit(solution)/shard_map/ppermute | solution.py:24
  23.0 5.8 %collective-permute-start.6 = (f32[1,4,4,4,128]{4,2,3,1,0:T(4,128)S(1)}, f32[1,4,4,4,128]{4,2,3,1,0:T(4,128)S(1)}, u32[]{:S(2)}, u32[]{:S(2)}) collective-permute-start(f32[1,4,4,4,128]{4,2,3,1,0:T(4,128)S(1)} %get-tuple-element.43), channel_id=1, source_target_pairs={{0,8},{8,16},{16,24},{24,0},{1,9},{9,17},{17,25},{25,1},{2,10},{10... | collective-permute-start | bytes 98312 | tf_op jit(solution)/shard_map/ppermute | solution.py:24
  23.0 5.8 %collective-permute-start.8 = (f32[4,4,1,4,128]{4,2,3,1,0:T(1,128)S(1)}, f32[4,4,1,4,128]{4,2,3,1,0:T(1,128)S(1)}, u32[]{:S(2)}, u32[]{:S(2)}) collective-permute-start(f32[4,4,1,4,128]{4,2,3,1,0:T(1,128)S(1)} %get-tuple-element.41), channel_id=1, source_target_pairs={{0,3},{1,0},{2,1},{3,2},{4,7},{5,4},{6,5},{7,6},{8,11},{9,8},{10,9... | collective-permute-start | bytes 98312 | tf_op jit(solution)/shard_map/ppermute | solution.py:24
  24.4 4.5 %copy-start.11 = (f32[4,4,1,4,128]{4,2,3,1,0:T(1,128)}, f32[4,4,1,4,128]{4,2,3,1,0:T(1,128)S(1)}, u32[]{:S(2)}) copy-start(f32[4,4,1,4,128]{4,2,3,1,0:T(1,128)S(1)} %collective-permute-done.9) | copy-start | bytes 98308
  24.6 4.4 %copy-start.9 = (f32[1,4,4,4,128]{4,2,3,1,0:T(4,128)}, f32[1,4,4,4,128]{4,2,3,1,0:T(4,128)S(1)}, u32[]{:S(2)}) copy-start(f32[1,4,4,4,128]{4,2,3,1,0:T(4,128)S(1)} %collective-permute-done.5) | copy-start | bytes 98308
  28.7 0.6 copy-start.7
  28.7 0.6 copy-start.5
  29.4 0.8 %copy-start.4 = (f32[1,128,128]{2,1,0:T(8,128)S(1)}, f32[1,128,128]{2,1,0:T(8,128)}, u32[]{:S(2)}) copy-start(f32[1,128,128]{2,1,0:T(8,128)} %param.7) | copy-start | bytes 196612
  30.3 6.6 %collective-permute-start.10 = (f32[20480]{0:T(1024)S(1)}, f32[20480]{0:T(1024)S(1)}, u32[]{:S(2)}, u32[]{:S(2)}) collective-permute-start(f32[20480]{0:T(1024)S(1)} %pad_maximum_fusion.110), channel_id=1, source_target_pairs={{0,24},{8,0},{16,8},{24,16},{1,25},{9,1},{17,9},{25,17},{2,26},{10... | collective-permute-start | bytes 245768 | tf_op jit(solution)/shard_map/ppermute | solution.py:24
  31.0 9.3 %collective-permute-start.11 = (f32[20480]{0:T(1024)S(1)}, f32[20480]{0:T(1024)S(1)}, u32[]{:S(2)}, u32[]{:S(2)}) collective-permute-start(f32[20480]{0:T(1024)S(1)} %pad_maximum_fusion.110), channel_id=1, source_target_pairs={{0,16},{8,24},{16,0},{24,8},{1,17},{9,25},{17,1},{25,9},{2,18},{10... | collective-permute-start | bytes 245768 | tf_op jit(solution)/shard_map/ppermute | solution.py:24
  31.0 9.3 %collective-permute-start.12 = (f32[20480]{0:T(1024)S(1)}, f32[20480]{0:T(1024)S(1)}, u32[]{:S(2)}, u32[]{:S(2)}) collective-permute-start(f32[20480]{0:T(1024)S(1)} %pad_maximum_fusion.110), channel_id=1, source_target_pairs={{0,8},{8,16},{16,24},{24,0},{1,9},{9,17},{17,25},{25,1},{2,10},{10... | collective-permute-start | bytes 245768 | tf_op jit(solution)/shard_map/ppermute | solution.py:24
  32.3 0.7 copy-start.17
  32.3 0.7 copy-start.16
  32.3 0.7 copy-start.18
  40.3 5.9 %collective-permute-start.19 = (f32[8,2,2,4,128]{4,3,1,0,2:T(4,128)S(1)}, f32[8,2,2,4,128]{4,3,1,0,2:T(4,128)S(1)}, u32[]{:S(2)}, u32[]{:S(2)}) collective-permute-start(f32[8,2,2,4,128]{4,3,1,0,2:T(4,128)S(1)} %pad_maximum_fusion.160), channel_id=1, source_target_pairs={{7,0},{4,1},{5,2},{6,3},{3,4},{0,5},{1,6},{2,7},{15,8},{12,9},{13,... | collective-permute-start | bytes 196616 | tf_op jit(solution)/shard_map/ppermute | solution.py:98
  41.6 5.9 %collective-permute-start.18 = (f32[8,2,2,4,128]{4,3,1,0,2:T(4,128)S(1)}, f32[8,2,2,4,128]{4,3,1,0,2:T(4,128)S(1)}, u32[]{:S(2)}, u32[]{:S(2)}) collective-permute-start(f32[8,2,2,4,128]{4,3,1,0,2:T(4,128)S(1)} %pad_maximum_fusion.160), channel_id=1, source_target_pairs={{6,0},{7,1},{4,2},{5,3},{2,4},{3,5},{0,6},{1,7},{14,8},{15,9},{12,... | collective-permute-start | bytes 196616 | tf_op jit(solution)/shard_map/ppermute | solution.py:98
  42.2 7.5 %collective-permute-start.17 = (f32[8,2,2,4,128]{4,3,1,0,2:T(4,128)S(1)}, f32[8,2,2,4,128]{4,3,1,0,2:T(4,128)S(1)}, u32[]{:S(2)}, u32[]{:S(2)}) collective-permute-start(f32[8,2,2,4,128]{4,3,1,0,2:T(4,128)S(1)} %pad_maximum_fusion.160), channel_id=1, source_target_pairs={{5,0},{6,1},{7,2},{4,3},{1,4},{2,5},{3,6},{0,7},{13,8},{14,9},{15,... | collective-permute-start | bytes 196616 | tf_op jit(solution)/shard_map/ppermute | solution.py:98
  44.5 5.2 %collective-permute-start.16 = (f32[8,2,2,4,128]{4,3,1,0,2:T(4,128)S(1)}, f32[8,2,2,4,128]{4,3,1,0,2:T(4,128)S(1)}, u32[]{:S(2)}, u32[]{:S(2)}) collective-permute-start(f32[8,2,2,4,128]{4,3,1,0,2:T(4,128)S(1)} %pad_maximum_fusion.160), channel_id=1, source_target_pairs={{4,0},{5,1},{6,2},{7,3},{0,4},{1,5},{2,6},{3,7},{12,8},{13,9},{14,... | collective-permute-start | bytes 196616 | tf_op jit(solution)/shard_map/ppermute | solution.py:98
  45.0 4.7 %collective-permute-start.15 = (f32[8,2,2,4,128]{4,3,1,0,2:T(4,128)S(1)}, f32[8,2,2,4,128]{4,3,1,0,2:T(4,128)S(1)}, u32[]{:S(2)}, u32[]{:S(2)}) collective-permute-start(f32[8,2,2,4,128]{4,3,1,0,2:T(4,128)S(1)} %pad_maximum_fusion.160), channel_id=1, source_target_pairs={{3,0},{0,1},{1,2},{2,3},{7,4},{4,5},{5,6},{6,7},{11,8},{8,9},{9,10... | collective-permute-start | bytes 196616 | tf_op jit(solution)/shard_map/ppermute | solution.py:98
  46.2 4.5 %collective-permute-start.14 = (f32[8,2,2,4,128]{4,3,1,0,2:T(4,128)S(1)}, f32[8,2,2,4,128]{4,3,1,0,2:T(4,128)S(1)}, u32[]{:S(2)}, u32[]{:S(2)}) collective-permute-start(f32[8,2,2,4,128]{4,3,1,0,2:T(4,128)S(1)} %pad_maximum_fusion.160), channel_id=1, source_target_pairs={{2,0},{3,1},{0,2},{1,3},{6,4},{7,5},{4,6},{5,7},{10,8},{11,9},{8,1... | collective-permute-start | bytes 196616 | tf_op jit(solution)/shard_map/ppermute | solution.py:98
  47.5 3.4 %collective-permute-start.13 = (f32[8,2,2,4,128]{4,3,1,0,2:T(4,128)S(1)}, f32[8,2,2,4,128]{4,3,1,0,2:T(4,128)S(1)}, u32[]{:S(2)}, u32[]{:S(2)}) collective-permute-start(f32[8,2,2,4,128]{4,3,1,0,2:T(4,128)S(1)} %pad_maximum_fusion.160), channel_id=1, source_target_pairs={{1,0},{2,1},{3,2},{0,3},{5,4},{6,5},{7,6},{4,7},{9,8},{10,9},{11,1... | collective-permute-start | bytes 196616 | tf_op jit(solution)/shard_map/ppermute | solution.py:98
  55.7 0.8 %copy-start.12 = (f32[4,4,1,4,128]{4,2,3,1,0:T(1,128)S(1)}, f32[4,4,1,4,128]{4,2,3,1,0:T(1,128)}, u32[]{:S(2)}) copy-start(f32[4,4,1,4,128]{4,2,3,1,0:T(1,128)} %copy-done.11) | copy-start | bytes 98308
  56.5 0.8 %copy-start.10 = (f32[1,4,4,4,128]{4,2,3,1,0:T(4,128)S(1)}, f32[1,4,4,4,128]{4,2,3,1,0:T(4,128)}, u32[]{:S(2)}) copy-start(f32[1,4,4,4,128]{4,2,3,1,0:T(4,128)} %copy-done.9) | copy-start | bytes 98308
  57.3 0.8 %copy-start.8 = (f32[1,4,4,4,128]{4,2,3,1,0:T(4,128)S(1)}, f32[1,4,4,4,128]{4,2,3,1,0:T(4,128)}, u32[]{:S(2)}) copy-start(f32[1,4,4,4,128]{4,2,3,1,0:T(4,128)} %copy-done.7) | copy-start | bytes 98308
  58.1 0.8 %copy-start.6 = (f32[4,4,1,4,128]{4,2,3,1,0:T(1,128)S(1)}, f32[4,4,1,4,128]{4,2,3,1,0:T(1,128)}, u32[]{:S(2)}) copy-start(f32[4,4,1,4,128]{4,2,3,1,0:T(1,128)} %copy-done.5) | copy-start | bytes 98308
  59.2 5.6 %collective-permute-start.24 = (f32[4,4,1,4,128]{4,2,3,1,0:T(1,128)S(1)}, f32[4,4,1,4,128]{4,2,3,1,0:T(1,128)S(1)}, u32[]{:S(2)}, u32[]{:S(2)}) collective-permute-start(f32[4,4,1,4,128]{4,2,3,1,0:T(1,128)S(1)} %get-tuple-element.36), channel_id=1, source_target_pairs={{0,1},{1,2},{2,3},{3,0},{4,5},{5,6},{6,7},{7,4},{8,9},{9,10},{10,1... | collective-permute-start | bytes 98312 | tf_op jit(solution)/shard_map/ppermute | solution.py:24
  60.1 9.4 %collective-permute-start.22 = (f32[4,2,4,4,128]{4,2,3,1,0:T(4,128)S(1)}, f32[4,2,4,4,128]{4,2,3,1,0:T(4,128)S(1)}, u32[]{:S(2)}, u32[]{:S(2)}) collective-permute-start(f32[4,2,4,4,128]{4,2,3,1,0:T(4,128)S(1)} %pad_maximum_fusion.161), channel_id=1, source_target_pairs={{0,4},{4,0},{1,5},{5,1},{2,6},{6,2},{3,7},{7,3},{8,12},{12,8},{9,1... | collective-permute-start | bytes 196616 | tf_op jit(solution)/shard_map/ppermute | solution.py:34
  61.7 3.9 %collective-permute-start.20 = (f32[1,4,4,4,128]{4,2,3,1,0:T(4,128)S(1)}, f32[1,4,4,4,128]{4,2,3,1,0:T(4,128)S(1)}, u32[]{:S(2)}, u32[]{:S(2)}) collective-permute-start(f32[1,4,4,4,128]{4,2,3,1,0:T(4,128)S(1)} %get-tuple-element.38), channel_id=1, source_target_pairs={{0,24},{8,0},{16,8},{24,16},{1,25},{9,1},{17,9},{25,17},{2,26},{10... | collective-permute-start | bytes 98312 | tf_op jit(solution)/shard_map/ppermute | solution.py:24
  63.5 5.7 %collective-permute-start.21 = (f32[1,4,4,4,128]{4,2,3,1,0:T(4,128)S(1)}, f32[1,4,4,4,128]{4,2,3,1,0:T(4,128)S(1)}, u32[]{:S(2)}, u32[]{:S(2)}) collective-permute-start(f32[1,4,4,4,128]{4,2,3,1,0:T(4,128)S(1)} %get-tuple-element.37), channel_id=1, source_target_pairs={{0,8},{8,16},{16,24},{24,0},{1,9},{9,17},{17,25},{25,1},{2,10},{10... | collective-permute-start | bytes 98312 | tf_op jit(solution)/shard_map/ppermute | solution.py:24
  63.8 5.6 %collective-permute-start.23 = (f32[4,4,1,4,128]{4,2,3,1,0:T(1,128)S(1)}, f32[4,4,1,4,128]{4,2,3,1,0:T(1,128)S(1)}, u32[]{:S(2)}, u32[]{:S(2)}) collective-permute-start(f32[4,4,1,4,128]{4,2,3,1,0:T(1,128)S(1)} %get-tuple-element.35), channel_id=1, source_target_pairs={{0,3},{1,0},{2,1},{3,2},{4,7},{5,4},{6,5},{7,6},{8,11},{9,8},{10,9... | collective-permute-start | bytes 98312 | tf_op jit(solution)/shard_map/ppermute | solution.py:24
  69.5 1.2 %copy-start.2 = (f32[512,512]{1,0:T(8,128)S(1)}, f32[512,512]{1,0:T(8,128)}, u32[]{:S(2)}) copy-start(f32[512,512]{1,0:T(8,128)} %fusion.92) | copy-start | bytes 3145732
  69.8 1.0 %copy-start.13 = (f32[8,8,512]{2,1,0:T(8,128)S(1)}, f32[8,8,512]{2,1,0:T(8,128)}, u32[]{:S(2)}) copy-start(f32[8,8,512]{2,1,0:T(8,128)} %broadcast_multiply_fusion.1) | copy-start | bytes 393220

commit v7 on v6

--- a/solution.py
+++ b/solution.py
@@ -149,8 +149,11 @@
 
 
 def stencil(block, faces, level_id):
+    return padded_stencil(pad_with(block, faces), level_id)
+
+
+def padded_stencil(padded, level_id):
     center, coupling = level_coeffs(level_id)
-    padded = pad_with(block, faces)
     middle = padded[1:-1, 1:-1, 1:-1]
     beside = padded[2:, 1:-1, 1:-1] + padded[:-2, 1:-1, 1:-1]
     beside = beside + padded[1:-1, 2:, 1:-1] + padded[1:-1, :-2, 1:-1]
@@ -257,6 +260,14 @@
         hi = corr_faces[dim][1] + prolong_face(coarse_face_list[dim][1], dim)
         faces.append((lo, hi))
     return updated + omega * (rhs - stencil(updated, faces, level_id)) / center
+
+
+def post_smooth_padded(level_id, corr_padded, rhs, coarse_inner, coarse_face_list):
+    center, coupling = level_coeffs(level_id)
+    faces = [(prolong_face(lo, dim), prolong_face(hi, dim)) for dim, (lo, hi) in enumerate(coarse_face_list)]
+    updated_padded = corr_padded + pad_with(prolong(coarse_inner), faces)
+    updated = updated_padded[1:-1, 1:-1, 1:-1]
+    return updated + omega * (rhs - padded_stencil(updated_padded, level_id)) / center
 
 
 def dim_mask(box_part, offset, extent):
@@ -291,12 +302,12 @@
     rhs_one = restrict(rhs_zero - stencil(corr_zero, faces_zero, 0))
     center, coupling = level_coeffs(1)
     corr_one = omega * rhs_one / center
-    faces_one = all_faces(corr_one)
-    rhs_two = restrict(rhs_one - stencil(corr_one, faces_one, 1))
+    padded_one = pad_with(corr_one, all_faces(corr_one))
+    rhs_two = restrict(rhs_one - padded_stencil(padded_one, 1))
     post_two, tiles_by_step = coarse_solve(rhs_two, inv_tiles)
     inner_two = post_two[1:-1, 1:-1, 1:-1]
-    post_one = post_smooth(
-        1, corr_one, faces_one, rhs_one, inner_two, [coarse_faces(post_two, dim) for dim in range(3)]
+    post_one = post_smooth_padded(
+        1, padded_one, rhs_one, inner_two, [coarse_faces(post_two, dim) for dim in range(3)]
     )
     return post_smooth(0, corr_zero, faces_zero, rhs_zero, post_one, all_faces(post_one)), tiles_by_step
 

time: 74.9 us -> 72.1 us (0.963)
  local copies, waits for them, and re-layouts: 13.7 us -> 11.5 us
    unnamed x38 -> x34, local copies, waits for them, and re-layouts: 7.5 us -> 5.35 us
    ppermute x15, waiting for transfers between devices: 13 us -> 12 us  [shifted(): lax.ppermute(block, axis, [(j, (j - step) % count) for j in range(count)])]
    ppermute x7, waiting for transfers between devices: 1.26 us -> 2.02 us  [fetch(): cache[steps] = lax.ppermute(block, tuple(axes), pairs)]
  transfers between devices with their start and end apart: 25 -> 25, of which waited for: 8 -> 7; matrix products, arithmetic and copies ran while one was open for 9% -> 10% of each run, Pallas kernels for 0% -> 0%
where the time goes in v7:
time: 72.1 us; the launch traced here: 71.6 us
  starting transfers between devices  27.1 us (38%)
  waiting for transfers between devices  14.1 us (20%)
  local copies, waits for them, and re-layouts  11.5 us (16%)
  other arithmetic  9.39 us (13%)
  between operations  6.12 us (8%)
  matrix products  3.39 us (5%)
    ppermute x15, starting transfers between devices, shifted(): lax.ppermute(block, axis, [(j, (j - step) % count) for j in range(count)])  15 us
    ppermute x15, waiting for transfers between devices, shifted(): lax.ppermute(block, axis, [(j, (j - step) % count) for j in range(count)])  12 us
    ppermute x7, starting transfers between devices, fetch(): cache[steps] = lax.ppermute(block, tuple(axes), pairs)  7.36 us
    unnamed x34, local copies, waits for them, and re-layouts  5.35 us
    ppermute x3, starting transfers between devices, axis_faces(): lax.ppermute(jnp.concatenate([first, last], axis=dim), axis, [(0, 1), (1,...  4.74 us
    dot_general x1, matrix products, body(): jnp.dot(rows, gram, precision=lax.Precision.HIGH, preferred_element_type=...  3.39 us
    ppermute x7, waiting for transfers between devices, fetch(): cache[steps] = lax.ppermute(block, tuple(axes), pairs)  2.02 us
    dynamic_update_slice x4, local copies, waits for them, and re-layouts, gram_matrix(): total = lax.dynamic_update_slice(total, piece[slot], (row, col))  1.9 us
  transfers between devices with their start and end apart: 25, of which 7 were waited for; matrix products, arithmetic and copies ran while one was open for 10% of the time, Pallas kernels for 0%

profile of v7, /device:TPU:0, one launch (start us, length us, event | category | flops | bytes accessed | tf_op | source)
XLA Modules:
  0.0 71.6 jit_solution(5685952414228042251)
XLA Ops:
  0.0 1.2 %convert_multiply_fusion.1 = f32[8,8,8,4,128]{4,2,3,1,0:T(8,128)S(1)} fusion(bf16[8,8,8,512]{3,2,1,0:T(8,128)(2,1)} %param.4), kind=kLoop, calls=%fused_computation.3 | loop fusion | flops 524288 | bytes 1572864 | tf_op jit(solution)/shard_map/div | solution.py:300
  1.4 0.5 collective-permute-start.4
  2.0 2.6 %collective-permute-start.2 = (f32[8,2,8,4,128]{4,2,3,1,0:T(8,128)S(1)}, f32[8,2,8,4,128]{4,2,3,1,0:T(8,128)S(1)}, u32[]{:S(2)}, u32[]{:S(2)}) collective-permute-start(f32[8,2,8,4,128]{4,2,3,1,0:T(8,128)S(1)} %pad_maximum_fusion.77), channel_id=1, source_target_pairs={{0,4},{4,0},{1,5},{5,1},{2,6},{6,2},{3,7},{7,3},{8,12},{12,8},{9,1... | collective-permute-start | bytes 786440 | tf_op jit(solution)/shard_map/ppermute | solution.py:34
  4.6 0.7 fusion.137
  5.3 3.6 %collective-permute-start = (f32[1,8,8,4,128]{4,2,3,1,0:T(8,128)}, f32[1,8,8,4,128]{4,2,3,1,0:T(8,128)S(1)}, u32[]{:S(2)}, u32[]{:S(2)}) collective-permute-start(f32[1,8,8,4,128]{4,2,3,1,0:T(8,128)} %get-tuple-element.10), channel_id=1, source_target_pairs={{0,24},{8,0},{16,8},{24,16},{1,25},{9,1},{17,9},{25,17},{2,26},{10... | collective-permute-start | bytes 393224 | tf_op jit(solution)/shard_map/ppermute | solution.py:24
  8.9 1.2 %collective-permute-start.3 = (f32[8,8,1,4,128]{4,2,3,1,0:T(1,128)S(1)}, f32[8,8,1,4,128]{4,2,3,1,0:T(1,128)S(1)}, u32[]{:S(2)}, u32[]{:S(2)}) collective-permute-start(f32[8,8,1,4,128]{4,2,3,1,0:T(1,128)S(1)} %get-tuple-element.7), channel_id=1, source_target_pairs={{0,3},{1,0},{2,1},{3,2},{4,7},{5,4},{6,5},{7,6},{8,11},{9,8},{10,9... | collective-permute-start | bytes 393224 | tf_op jit(solution)/shard_map/ppermute | solution.py:24
  10.0 0.7 copy-done.12
  10.7 0.7 constant_dynamic-slice_fusion
  12.6 0.6 fusion.162
  13.4 0.7 copy-done.5
  14.2 0.6 iota_add_fusion
  14.8 0.3 copy-done.1
  15.1 0.7 broadcast_multiply_fusion.1
  15.9 1.3 %collective-permute-done.1 = f32[1,8,8,4,128]{4,2,3,1,0:T(8,128)S(1)} collective-permute-done((f32[1,8,8,4,128]{4,2,3,1,0:T(8,128)}, f32[1,8,8,4,128]{4,2,3,1,0:T(8,128)S(1)}, u32[]{:S(2)}, u32[]{:S(2)}) %collective-permute-start.1) | collective-permute-done | bytes 131104 | tf_op jit(solution)/shard_map/ppermute | solution.py:24
  17.2 0.9 %convert_subtract_fusion.1 = f32[8,8,8,4,128]{4,2,3,1,0:T(8,128)S(1)} fusion(f32[8,8,1,4,128]{4,2,3,1,0:T(1,128)S(1)} %collective-permute-done.4, f32[10,1,8,4,128]{4,2,3,1,0:T(8,128)S(1)} %pad.114, f32[10,1,8,4,128]{4,2,3,1,0:T(8,128)S(1)} %pad.115, f32[1,8,8,4,128]{4,2,3,1,0:T(8,128)S(1)} %collective-permute-done, ...), kind=kLoop, calls=%fused_computation.1 | loop fusion | flops 8912896 | bytes 3473408 | tf_op jit(solution)/shard_map/sub | solution.py:302
  18.2 0.7 %reduce_sum.27 = f32[4,4,4,4,128]{4,2,3,1,0:T(4,128)S(1)} reduce(f32[4,2,4,2,4,2,4,128]{7,5,4,6,3,2,1,0:T(2,128)S(1)} %bitcast.110, f32[]{:T(128)} %constant.96.clone.1), dimensions={1,3,5}, to_apply=%region_0.1 | reduce | flops 229376 | bytes 1179652 | tf_op jit(solution)/shard_map/reduce_sum | solution.py:177
  19.2 0.6 collective-permute-start.6
  19.8 1.4 %collective-permute-start.9 = (f32[4,4,1,4,128]{4,2,3,1,0:T(1,128)S(1)}, f32[4,4,1,4,128]{4,2,3,1,0:T(1,128)S(1)}, u32[]{:S(2)}, u32[]{:S(2)}) collective-permute-start(f32[4,4,1,4,128]{4,2,3,1,0:T(1,128)S(1)} %get-tuple-element.41), channel_id=1, source_target_pairs={{0,3},{1,0},{2,1},{3,2},{4,7},{5,4},{6,5},{7,6},{8,11},{9,8},{10,9... | collective-permute-start | bytes 98312 | tf_op jit(solution)/shard_map/ppermute | solution.py:24
  21.1 3.1 %collective-permute-start.8 = (f32[1,4,4,4,128]{4,2,3,1,0:T(4,128)S(1)}, f32[1,4,4,4,128]{4,2,3,1,0:T(4,128)S(1)}, u32[]{:S(2)}, u32[]{:S(2)}) collective-permute-start(f32[1,4,4,4,128]{4,2,3,1,0:T(4,128)S(1)} %get-tuple-element.44), channel_id=1, source_target_pairs={{0,24},{8,0},{16,8},{24,16},{1,25},{9,1},{17,9},{25,17},{2,26},{10... | collective-permute-start | bytes 98312 | tf_op jit(solution)/shard_map/ppermute | solution.py:24
  24.4 1.4 %collective-permute-done.8 = f32[1,4,4,4,128]{4,2,3,1,0:T(4,128)S(1)} collective-permute-done((f32[1,4,4,4,128]{4,2,3,1,0:T(4,128)S(1)}, f32[1,4,4,4,128]{4,2,3,1,0:T(4,128)S(1)}, u32[]{:S(2)}, u32[]{:S(2)}) %collective-permute-start.8) | collective-permute-done | bytes 32800 | tf_op jit(solution)/shard_map/ppermute | solution.py:24
  25.9 4.1 %collective-permute-done.7 = f32[1,4,4,4,128]{4,2,3,1,0:T(4,128)S(1)} collective-permute-done((f32[1,4,4,4,128]{4,2,3,1,0:T(4,128)S(1)}, f32[1,4,4,4,128]{4,2,3,1,0:T(4,128)S(1)}, u32[]{:S(2)}, u32[]{:S(2)}) %collective-permute-start.7) | collective-permute-done | bytes 32800 | tf_op jit(solution)/shard_map/ppermute | solution.py:24
  30.2 0.4 copy-done.9
  30.7 0.8 %copy-done.6 = f32[1,128,128]{2,1,0:T(8,128)S(1)} copy-done((f32[1,128,128]{2,1,0:T(8,128)S(1)}, f32[1,128,128]{2,1,0:T(8,128)}, u32[]{:S(2)}) %copy-start.6) | copy-done | bytes 65560
  31.6 1.9 %collective-permute-start.12 = (f32[20480]{0:T(1024)S(1)}, f32[20480]{0:T(1024)S(1)}, u32[]{:S(2)}, u32[]{:S(2)}) collective-permute-start(f32[20480]{0:T(1024)S(1)} %pad_maximum_fusion.96), channel_id=1, source_target_pairs={{0,8},{8,16},{16,24},{24,0},{1,9},{9,17},{17,25},{25,1},{2,10},{10... | collective-permute-start | bytes 245768 | tf_op jit(solution)/shard_map/ppermute | solution.py:24
  33.5 0.7 copy-done.15
  38.2 1.1 %collective-permute-done.12 = f32[20480]{0:T(1024)S(1)} collective-permute-done((f32[20480]{0:T(1024)S(1)}, f32[20480]{0:T(1024)S(1)}, u32[]{:S(2)}, u32[]{:S(2)}) %collective-permute-start.12) | collective-permute-done | bytes 81952 | tf_op jit(solution)/shard_map/ppermute | solution.py:24
  39.3 2.4 %collective-permute-start.18 = (f32[8,2,2,4,128]{4,3,1,0,2:T(4,128)S(1)}, f32[8,2,2,4,128]{4,3,1,0,2:T(4,128)S(1)}, u32[]{:S(2)}, u32[]{:S(2)}) collective-permute-start(f32[8,2,2,4,128]{4,3,1,0,2:T(4,128)S(1)} %pad_maximum_fusion.146), channel_id=1, source_target_pairs={{6,0},{7,1},{4,2},{5,3},{2,4},{3,5},{0,6},{1,7},{14,8},{15,9},{12,... | collective-permute-start | bytes 196616 | tf_op jit(solution)/shard_map/ppermute | solution.py:98
  41.8 2.3 %collective-permute-start.17 = (f32[8,2,2,4,128]{4,3,1,0,2:T(4,128)S(1)}, f32[8,2,2,4,128]{4,3,1,0,2:T(4,128)S(1)}, u32[]{:S(2)}, u32[]{:S(2)}) collective-permute-start(f32[8,2,2,4,128]{4,3,1,0,2:T(4,128)S(1)} %pad_maximum_fusion.146), channel_id=1, source_target_pairs={{5,0},{6,1},{7,2},{4,3},{1,4},{2,5},{3,6},{0,7},{13,8},{14,9},{15,... | collective-permute-start | bytes 196616 | tf_op jit(solution)/shard_map/ppermute | solution.py:98
  44.1 0.5 collective-permute-start.16
  44.6 0.6 fusion.91
  45.2 0.6 fusion.90
  45.9 0.6 collective-permute-start.14
  46.5 1.5 %collective-permute-start.13 = (f32[8,2,2,4,128]{4,3,1,0,2:T(4,128)S(1)}, f32[8,2,2,4,128]{4,3,1,0,2:T(4,128)S(1)}, u32[]{:S(2)}, u32[]{:S(2)}) collective-permute-start(f32[8,2,2,4,128]{4,3,1,0,2:T(4,128)S(1)} %pad_maximum_fusion.146), channel_id=1, source_target_pairs={{1,0},{2,1},{3,2},{0,3},{5,4},{6,5},{7,6},{4,7},{9,8},{10,9},{11,1... | collective-permute-start | bytes 196616 | tf_op jit(solution)/shard_map/ppermute | solution.py:98
  47.9 0.6 fusion.89
  48.6 2.0 %collective-permute-done.14 = f32[8,2,2,4,128]{4,3,1,0,2:T(4,128)S(1)} collective-permute-done((f32[8,2,2,4,128]{4,3,1,0,2:T(4,128)S(1)}, f32[8,2,2,4,128]{4,3,1,0,2:T(4,128)S(1)}, u32[]{:S(2)}, u32[]{:S(2)}) %collective-permute-start.14) | collective-permute-done | bytes 65568 | tf_op jit(solution)/shard_map/ppermute | solution.py:98
  51.0 1.4 %fusion.59 = f32[8,4,8,4,128]{4,3,1,0,2:T(4,128)S(1)} fusion(f32[8,4,8,4,128]{4,3,1,0,2:T(4,128)S(1)} %get-tuple-element.6, f32[8,4,1,4,128]{4,3,1,0,2:T(4,128)S(1)} %get-tuple-element.26, f32[10,1,8,4,128]{4,3,1,0,2:T(4,128)S(1)} %pad.122, f32[10,1,8,4,128]{4,3,1,0,2:T(4,128)S(1)} %pad.123, f32[1,4,8,4,128]{4,3,1,0,2:T(4,128)S(1)} %get-tuple-element.28, ...), kind=kLoop, calls=%fused_computation.124 | loop fusion | flops 4325376 | bytes 2162688 | tf_op jit(solution)/shard_map/sub | solution.py:222
  53.5 1.5 %fusion.49 = f32[8,4,8,4,128]{4,3,1,0,2:T(4,128)S(1)} fusion(f32[8,4,8,4,128]{4,3,1,0,2:T(4,128)S(1)} %bitcast_add_fusion, f32[8,4,8,4,128]{4,3,1,0,2:T(4,128)S(1)} %get-tuple-element.6, f32[8,4,1,4,128]{4,3,1,0,2:T(4,128)S(1)} %get-tuple-element.20, f32[10,1,8,4,128]{4,3,1,0,2:T(4,128)S(1)} %pad.138, f32[10,1,8,4,128]{4,3,1,0,2:T(4,128)S(1)} %pad.139, ...), kind=kLoop, calls=%fused_computation.96 | loop fusion | flops 4587520 | bytes 2162688 | tf_op jit(solution)/shard_map/add | solution.py:230
  55.4 0.6 copy-done.8
  56.2 0.3 fusion.41
  56.8 0.9 %collective-permute-start.24 = (f32[4,4,1,4,128]{4,2,3,1,0:T(1,128)S(1)}, f32[4,4,1,4,128]{4,2,3,1,0:T(1,128)S(1)}, u32[]{:S(2)}, u32[]{:S(2)}) collective-permute-start(f32[4,4,1,4,128]{4,2,3,1,0:T(1,128)S(1)} %get-tuple-element.36), channel_id=1, source_target_pairs={{0,1},{1,2},{2,3},{3,0},{4,5},{5,6},{6,7},{7,4},{8,9},{9,10},{10,1... | collective-permute-start | bytes 98312 | tf_op jit(solution)/shard_map/ppermute | solution.py:24
  57.7 1.6 %collective-permute-start.22 = (f32[4,2,4,4,128]{4,2,3,1,0:T(4,128)S(1)}, f32[4,2,4,4,128]{4,2,3,1,0:T(4,128)S(1)}, u32[]{:S(2)}, u32[]{:S(2)}) collective-permute-start(f32[4,2,4,4,128]{4,2,3,1,0:T(4,128)S(1)} %pad_maximum_fusion.147), channel_id=1, source_target_pairs={{0,4},{4,0},{1,5},{5,1},{2,6},{6,2},{3,7},{7,3},{8,12},{12,8},{9,1... | collective-permute-start | bytes 196616 | tf_op jit(solution)/shard_map/ppermute | solution.py:34
  59.3 1.7 %collective-permute-start.20 = (f32[1,4,4,4,128]{4,2,3,1,0:T(4,128)S(1)}, f32[1,4,4,4,128]{4,2,3,1,0:T(4,128)S(1)}, u32[]{:S(2)}, u32[]{:S(2)}) collective-permute-start(f32[1,4,4,4,128]{4,2,3,1,0:T(4,128)S(1)} %get-tuple-element.38), channel_id=1, source_target_pairs={{0,24},{8,0},{16,8},{24,16},{1,25},{9,1},{17,9},{25,17},{2,26},{10... | collective-permute-start | bytes 98312 | tf_op jit(solution)/shard_map/ppermute | solution.py:24
  60.9 0.4 collective-permute-start.21
  61.5 0.6 broadcast_in_dim.188
  62.5 0.7 %collective-permute-done.20 = f32[1,4,4,4,128]{4,2,3,1,0:T(4,128)S(1)} collective-permute-done((f32[1,4,4,4,128]{4,2,3,1,0:T(4,128)S(1)}, f32[1,4,4,4,128]{4,2,3,1,0:T(4,128)S(1)}, u32[]{:S(2)}, u32[]{:S(2)}) %collective-permute-start.20) | collective-permute-done | bytes 32800 | tf_op jit(solution)/shard_map/ppermute | solution.py:24
  63.3 3.4 %collective-permute-done.21 = f32[1,4,4,4,128]{4,2,3,1,0:T(4,128)S(1)} collective-permute-done((f32[1,4,4,4,128]{4,2,3,1,0:T(4,128)S(1)}, f32[1,4,4,4,128]{4,2,3,1,0:T(4,128)S(1)}, u32[]{:S(2)}, u32[]{:S(2)}) %collective-permute-start.21) | collective-permute-done | bytes 32800 | tf_op jit(solution)/shard_map/ppermute | solution.py:24
  67.2 0.9 %copy-done.2 = f32[512,512]{1,0:T(8,128)S(1)} copy-done((f32[512,512]{1,0:T(8,128)S(1)}, f32[512,512]{1,0:T(8,128)}, u32[]{:S(2)}) %copy-start.2) | copy-done | bytes 1048600
  68.2 3.4 %convolution_convert_fusion = bf16[8,8,8,512]{3,2,1,0:T(8,128)(2,1)} fusion(f32[8,8,8,4,128]{4,2,3,1,0:T(8,128)S(1)} %fusion.75, f32[8,8,1,4,128]{4,2,3,1,0:T(1,128)S(1)} %add.404, f32[10,1,8,4,128]{4,2,3,1,0:T(8,128)S(1)} %pad.146, f32[10,1,8,4,128]{4,2,3,1,0:T(8,128)S(1)} %pad.147, f32[1,8,8,4,128]{4,2,3,1,0:T(8,128)S(1)} %add.395, ...), kind=kOutput, calls=%fused_computation.4 | convolution fusion | flops 815529984 | bytes 4145152 | tf_op jit(solution)/shard_map/dot_general | solution.py:330
  (169 shorter events, 4.4 us)
Async XLA Ops:
  1.4 14.4 %collective-permute-start.4 = (f32[8,8,1,4,128]{4,2,3,1,0:T(1,128)S(1)}, f32[8,8,1,4,128]{4,2,3,1,0:T(1,128)S(1)}, u32[]{:S(2)}, u32[]{:S(2)}) collective-permute-start(f32[8,8,1,4,128]{4,2,3,1,0:T(1,128)S(1)} %get-tuple-element.8), channel_id=1, source_target_pairs={{0,1},{1,2},{2,3},{3,0},{4,5},{5,6},{6,7},{7,4},{8,9},{9,10},{10,1... | collective-permute-start | bytes 393224 | tf_op jit(solution)/shard_map/ppermute | solution.py:24
  2.0 13.8 %collective-permute-start.2 = (f32[8,2,8,4,128]{4,2,3,1,0:T(8,128)S(1)}, f32[8,2,8,4,128]{4,2,3,1,0:T(8,128)S(1)}, u32[]{:S(2)}, u32[]{:S(2)}) collective-permute-start(f32[8,2,8,4,128]{4,2,3,1,0:T(8,128)S(1)} %pad_maximum_fusion.77), channel_id=1, source_target_pairs={{0,4},{4,0},{1,5},{5,1},{2,6},{6,2},{3,7},{7,3},{8,12},{12,8},{9,1... | collective-permute-start | bytes 786440 | tf_op jit(solution)/shard_map/ppermute | solution.py:34
  5.3 10.6 %collective-permute-start = (f32[1,8,8,4,128]{4,2,3,1,0:T(8,128)}, f32[1,8,8,4,128]{4,2,3,1,0:T(8,128)S(1)}, u32[]{:S(2)}, u32[]{:S(2)}) collective-permute-start(f32[1,8,8,4,128]{4,2,3,1,0:T(8,128)} %get-tuple-element.10), channel_id=1, source_target_pairs={{0,24},{8,0},{16,8},{24,16},{1,25},{9,1},{17,9},{25,17},{2,26},{10... | collective-permute-start | bytes 393224 | tf_op jit(solution)/shard_map/ppermute | solution.py:24
  8.9 8.3 %collective-permute-start.1 = (f32[1,8,8,4,128]{4,2,3,1,0:T(8,128)}, f32[1,8,8,4,128]{4,2,3,1,0:T(8,128)S(1)}, u32[]{:S(2)}, u32[]{:S(2)}) collective-permute-start(f32[1,8,8,4,128]{4,2,3,1,0:T(8,128)} %get-tuple-element.9), channel_id=1, source_target_pairs={{0,8},{8,16},{16,24},{24,0},{1,9},{9,17},{17,25},{25,1},{2,10},{10... | collective-permute-start | bytes 393224 | tf_op jit(solution)/shard_map/ppermute | solution.py:24
  8.9 8.3 %collective-permute-start.3 = (f32[8,8,1,4,128]{4,2,3,1,0:T(1,128)S(1)}, f32[8,8,1,4,128]{4,2,3,1,0:T(1,128)S(1)}, u32[]{:S(2)}, u32[]{:S(2)}) collective-permute-start(f32[8,8,1,4,128]{4,2,3,1,0:T(1,128)S(1)} %get-tuple-element.7), channel_id=1, source_target_pairs={{0,3},{1,0},{2,1},{3,2},{4,7},{5,4},{6,5},{7,6},{8,11},{9,8},{10,9... | collective-permute-start | bytes 393224 | tf_op jit(solution)/shard_map/ppermute | solution.py:24
  10.0 0.7 copy-start.12
  11.4 1.2 %copy-start.13 = (s32[3,2,512]{2,1,0:T(2,128)S(1)}, s32[3,2,512]{2,1,0:T(2,128)}, u32[]{:S(2)}) copy-start(s32[3,2,512]{2,1,0:T(2,128)} %param.5) | copy-start | bytes 36868
  13.2 0.8 %copy-start.5 = (f32[1,128,128]{2,1,0:T(8,128)S(1)}, f32[1,128,128]{2,1,0:T(8,128)}, u32[]{:S(2)}) copy-start(f32[1,128,128]{2,1,0:T(8,128)} %param.7) | copy-start | bytes 196612
  14.1 1.0 %copy-start.1 = (f32[512,512]{1,0:T(8,128)}, f32[512,512]{1,0:T(8,128)S(1)}, u32[]{:S(2)}) copy-start(f32[512,512]{1,0:T(8,128)S(1)} %bitcast_dynamic-update-slice_fusion) | copy-start | bytes 3145732
  15.8 1.4 %copy-start = (bf16[8,8,8,512]{3,2,1,0:T(8,128)(2,1)S(1)}, bf16[8,8,8,512]{3,2,1,0:T(8,128)(2,1)}, u32[]{:S(2)}) copy-start(bf16[8,8,8,512]{3,2,1,0:T(8,128)(2,1)} %param.4) | copy-start | bytes 1572868
  19.0 5.3 %collective-permute-start.5 = (f32[4,4,1,4,128]{4,2,3,1,0:T(1,128)S(1)}, f32[4,4,1,4,128]{4,2,3,1,0:T(1,128)S(1)}, u32[]{:S(2)}, u32[]{:S(2)}) collective-permute-start(f32[4,4,1,4,128]{4,2,3,1,0:T(1,128)S(1)} %get-tuple-element.42), channel_id=1, source_target_pairs={{0,1},{1,2},{2,3},{3,0},{4,5},{5,6},{6,7},{7,4},{8,9},{9,10},{10,1... | collective-permute-start | bytes 98312 | tf_op jit(solution)/shard_map/ppermute | solution.py:24
  19.2 5.2 %collective-permute-start.6 = (f32[4,2,4,4,128]{4,2,3,1,0:T(4,128)S(1)}, f32[4,2,4,4,128]{4,2,3,1,0:T(4,128)S(1)}, u32[]{:S(2)}, u32[]{:S(2)}) collective-permute-start(f32[4,2,4,4,128]{4,2,3,1,0:T(4,128)S(1)} %pad_maximum_fusion.145), channel_id=1, source_target_pairs={{0,4},{4,0},{1,5},{5,1},{2,6},{6,2},{3,7},{7,3},{8,12},{12,8},{9,1... | collective-permute-start | bytes 196616 | tf_op jit(solution)/shard_map/ppermute | solution.py:34
  19.8 4.6 %collective-permute-start.9 = (f32[4,4,1,4,128]{4,2,3,1,0:T(1,128)S(1)}, f32[4,4,1,4,128]{4,2,3,1,0:T(1,128)S(1)}, u32[]{:S(2)}, u32[]{:S(2)}) collective-permute-start(f32[4,4,1,4,128]{4,2,3,1,0:T(1,128)S(1)} %get-tuple-element.41), channel_id=1, source_target_pairs={{0,3},{1,0},{2,1},{3,2},{4,7},{5,4},{6,5},{7,6},{8,11},{9,8},{10,9... | collective-permute-start | bytes 98312 | tf_op jit(solution)/shard_map/ppermute | solution.py:24
  21.1 4.7 %collective-permute-start.8 = (f32[1,4,4,4,128]{4,2,3,1,0:T(4,128)S(1)}, f32[1,4,4,4,128]{4,2,3,1,0:T(4,128)S(1)}, u32[]{:S(2)}, u32[]{:S(2)}) collective-permute-start(f32[1,4,4,4,128]{4,2,3,1,0:T(4,128)S(1)} %get-tuple-element.44), channel_id=1, source_target_pairs={{0,24},{8,0},{16,8},{24,16},{1,25},{9,1},{17,9},{25,17},{2,26},{10... | collective-permute-start | bytes 98312 | tf_op jit(solution)/shard_map/ppermute | solution.py:24
  24.3 5.7 %collective-permute-start.7 = (f32[1,4,4,4,128]{4,2,3,1,0:T(4,128)S(1)}, f32[1,4,4,4,128]{4,2,3,1,0:T(4,128)S(1)}, u32[]{:S(2)}, u32[]{:S(2)}) collective-permute-start(f32[1,4,4,4,128]{4,2,3,1,0:T(4,128)S(1)} %get-tuple-element.43), channel_id=1, source_target_pairs={{0,8},{8,16},{16,24},{24,0},{1,9},{9,17},{17,25},{25,1},{2,10},{10... | collective-permute-start | bytes 98312 | tf_op jit(solution)/shard_map/ppermute | solution.py:24
  24.4 5.8 %copy-start.3 = (f32[6,1,4,4,128]{4,2,3,1,0:T(4,128)}, f32[6,1,4,4,128]{4,2,3,1,0:T(4,128)S(1)}, u32[]{:S(2)}) copy-start(f32[6,1,4,4,128]{4,2,3,1,0:T(4,128)S(1)} %pad.119) | copy-start | bytes 147460
  25.9 4.3 %copy-start.7 = (f32[1,4,4,4,128]{4,2,3,1,0:T(4,128)}, f32[1,4,4,4,128]{4,2,3,1,0:T(4,128)S(1)}, u32[]{:S(2)}) copy-start(f32[1,4,4,4,128]{4,2,3,1,0:T(4,128)S(1)} %collective-permute-done.8) | copy-start | bytes 98308
  30.0 0.6 copy-start.9
  30.7 0.8 %copy-start.6 = (f32[1,128,128]{2,1,0:T(8,128)S(1)}, f32[1,128,128]{2,1,0:T(8,128)}, u32[]{:S(2)}) copy-start(f32[1,128,128]{2,1,0:T(8,128)} %param.7) | copy-start | bytes 196612
  31.5 6.6 %collective-permute-start.10 = (f32[20480]{0:T(1024)S(1)}, f32[20480]{0:T(1024)S(1)}, u32[]{:S(2)}, u32[]{:S(2)}) collective-permute-start(f32[20480]{0:T(1024)S(1)} %pad_maximum_fusion.96), channel_id=1, source_target_pairs={{0,24},{8,0},{16,8},{24,16},{1,25},{9,1},{17,9},{25,17},{2,26},{10... | collective-permute-start | bytes 245768 | tf_op jit(solution)/shard_map/ppermute | solution.py:24
  31.5 6.7 %collective-permute-start.11 = (f32[20480]{0:T(1024)S(1)}, f32[20480]{0:T(1024)S(1)}, u32[]{:S(2)}, u32[]{:S(2)}) collective-permute-start(f32[20480]{0:T(1024)S(1)} %pad_maximum_fusion.96), channel_id=1, source_target_pairs={{0,16},{8,24},{16,0},{24,8},{1,17},{9,25},{17,1},{25,9},{2,18},{10... | collective-permute-start | bytes 245768 | tf_op jit(solution)/shard_map/ppermute | solution.py:24
  31.6 7.7 %collective-permute-start.12 = (f32[20480]{0:T(1024)S(1)}, f32[20480]{0:T(1024)S(1)}, u32[]{:S(2)}, u32[]{:S(2)}) collective-permute-start(f32[20480]{0:T(1024)S(1)} %pad_maximum_fusion.96), channel_id=1, source_target_pairs={{0,8},{8,16},{16,24},{24,0},{1,9},{9,17},{17,25},{25,1},{2,10},{10... | collective-permute-start | bytes 245768 | tf_op jit(solution)/shard_map/ppermute | solution.py:24
  33.5 0.7 copy-start.15
  33.5 0.7 copy-start.14
  33.5 0.7 copy-start.16
  39.3 6.6 %collective-permute-start.19 = (f32[8,2,2,4,128]{4,3,1,0,2:T(4,128)S(1)}, f32[8,2,2,4,128]{4,3,1,0,2:T(4,128)S(1)}, u32[]{:S(2)}, u32[]{:S(2)}) collective-permute-start(f32[8,2,2,4,128]{4,3,1,0,2:T(4,128)S(1)} %pad_maximum_fusion.146), channel_id=1, source_target_pairs={{7,0},{4,1},{5,2},{6,3},{3,4},{0,5},{1,6},{2,7},{15,8},{12,9},{13,... | collective-permute-start | bytes 196616 | tf_op jit(solution)/shard_map/ppermute | solution.py:98
  39.3 7.1 %collective-permute-start.18 = (f32[8,2,2,4,128]{4,3,1,0,2:T(4,128)S(1)}, f32[8,2,2,4,128]{4,3,1,0,2:T(4,128)S(1)}, u32[]{:S(2)}, u32[]{:S(2)}) collective-permute-start(f32[8,2,2,4,128]{4,3,1,0,2:T(4,128)S(1)} %pad_maximum_fusion.146), channel_id=1, source_target_pairs={{6,0},{7,1},{4,2},{5,3},{2,4},{3,5},{0,6},{1,7},{14,8},{15,9},{12,... | collective-permute-start | bytes 196616 | tf_op jit(solution)/shard_map/ppermute | solution.py:98
  41.8 6.8 %collective-permute-start.17 = (f32[8,2,2,4,128]{4,3,1,0,2:T(4,128)S(1)}, f32[8,2,2,4,128]{4,3,1,0,2:T(4,128)S(1)}, u32[]{:S(2)}, u32[]{:S(2)}) collective-permute-start(f32[8,2,2,4,128]{4,3,1,0,2:T(4,128)S(1)} %pad_maximum_fusion.146), channel_id=1, source_target_pairs={{5,0},{6,1},{7,2},{4,3},{1,4},{2,5},{3,6},{0,7},{13,8},{14,9},{15,... | collective-permute-start | bytes 196616 | tf_op jit(solution)/shard_map/ppermute | solution.py:98
  44.1 4.5 %collective-permute-start.16 = (f32[8,2,2,4,128]{4,3,1,0,2:T(4,128)S(1)}, f32[8,2,2,4,128]{4,3,1,0,2:T(4,128)S(1)}, u32[]{:S(2)}, u32[]{:S(2)}) collective-permute-start(f32[8,2,2,4,128]{4,3,1,0,2:T(4,128)S(1)} %pad_maximum_fusion.146), channel_id=1, source_target_pairs={{4,0},{5,1},{6,2},{7,3},{0,4},{1,5},{2,6},{3,7},{12,8},{13,9},{14,... | collective-permute-start | bytes 196616 | tf_op jit(solution)/shard_map/ppermute | solution.py:98
  44.6 4.0 %collective-permute-start.15 = (f32[8,2,2,4,128]{4,3,1,0,2:T(4,128)S(1)}, f32[8,2,2,4,128]{4,3,1,0,2:T(4,128)S(1)}, u32[]{:S(2)}, u32[]{:S(2)}) collective-permute-start(f32[8,2,2,4,128]{4,3,1,0,2:T(4,128)S(1)} %pad_maximum_fusion.146), channel_id=1, source_target_pairs={{3,0},{0,1},{1,2},{2,3},{7,4},{4,5},{5,6},{6,7},{11,8},{8,9},{9,10... | collective-permute-start | bytes 196616 | tf_op jit(solution)/shard_map/ppermute | solution.py:98
  45.9 4.7 %collective-permute-start.14 = (f32[8,2,2,4,128]{4,3,1,0,2:T(4,128)S(1)}, f32[8,2,2,4,128]{4,3,1,0,2:T(4,128)S(1)}, u32[]{:S(2)}, u32[]{:S(2)}) collective-permute-start(f32[8,2,2,4,128]{4,3,1,0,2:T(4,128)S(1)} %pad_maximum_fusion.146), channel_id=1, source_target_pairs={{2,0},{3,1},{0,2},{1,3},{6,4},{7,5},{4,6},{5,7},{10,8},{11,9},{8,1... | collective-permute-start | bytes 196616 | tf_op jit(solution)/shard_map/ppermute | solution.py:98
  46.5 4.1 %collective-permute-start.13 = (f32[8,2,2,4,128]{4,3,1,0,2:T(4,128)S(1)}, f32[8,2,2,4,128]{4,3,1,0,2:T(4,128)S(1)}, u32[]{:S(2)}, u32[]{:S(2)}) collective-permute-start(f32[8,2,2,4,128]{4,3,1,0,2:T(4,128)S(1)} %pad_maximum_fusion.146), channel_id=1, source_target_pairs={{1,0},{2,1},{3,2},{0,3},{5,4},{6,5},{7,6},{4,7},{9,8},{10,9},{11,1... | collective-permute-start | bytes 196616 | tf_op jit(solution)/shard_map/ppermute | solution.py:98
  55.3 0.8 %copy-start.8 = (f32[1,4,4,4,128]{4,2,3,1,0:T(4,128)S(1)}, f32[1,4,4,4,128]{4,2,3,1,0:T(4,128)}, u32[]{:S(2)}) copy-start(f32[1,4,4,4,128]{4,2,3,1,0:T(4,128)} %copy-done.7) | copy-start | bytes 98308
  55.3 0.8 %copy-start.10 = (f32[1,4,4,4,128]{4,2,3,1,0:T(4,128)S(1)}, f32[1,4,4,4,128]{4,2,3,1,0:T(4,128)}, u32[]{:S(2)}) copy-start(f32[1,4,4,4,128]{4,2,3,1,0:T(4,128)} %copy-done.9) | copy-start | bytes 98308
  55.4 0.8 %copy-start.4 = (f32[6,1,4,4,128]{4,2,3,1,0:T(4,128)S(1)}, f32[6,1,4,4,128]{4,2,3,1,0:T(4,128)}, u32[]{:S(2)}) copy-start(f32[6,1,4,4,128]{4,2,3,1,0:T(4,128)} %copy-done.3) | copy-start | bytes 147460
  56.8 5.5 %collective-permute-start.24 = (f32[4,4,1,4,128]{4,2,3,1,0:T(1,128)S(1)}, f32[4,4,1,4,128]{4,2,3,1,0:T(1,128)S(1)}, u32[]{:S(2)}, u32[]{:S(2)}) collective-permute-start(f32[4,4,1,4,128]{4,2,3,1,0:T(1,128)S(1)} %get-tuple-element.36), channel_id=1, source_target_pairs={{0,1},{1,2},{2,3},{3,0},{4,5},{5,6},{6,7},{7,4},{8,9},{9,10},{10,1... | collective-permute-start | bytes 98312 | tf_op jit(solution)/shard_map/ppermute | solution.py:24
  57.7 9.3 %collective-permute-start.22 = (f32[4,2,4,4,128]{4,2,3,1,0:T(4,128)S(1)}, f32[4,2,4,4,128]{4,2,3,1,0:T(4,128)S(1)}, u32[]{:S(2)}, u32[]{:S(2)}) collective-permute-start(f32[4,2,4,4,128]{4,2,3,1,0:T(4,128)S(1)} %pad_maximum_fusion.147), channel_id=1, source_target_pairs={{0,4},{4,0},{1,5},{5,1},{2,6},{6,2},{3,7},{7,3},{8,12},{12,8},{9,1... | collective-permute-start | bytes 196616 | tf_op jit(solution)/shard_map/ppermute | solution.py:34
  59.3 3.9 %collective-permute-start.20 = (f32[1,4,4,4,128]{4,2,3,1,0:T(4,128)S(1)}, f32[1,4,4,4,128]{4,2,3,1,0:T(4,128)S(1)}, u32[]{:S(2)}, u32[]{:S(2)}) collective-permute-start(f32[1,4,4,4,128]{4,2,3,1,0:T(4,128)S(1)} %get-tuple-element.38), channel_id=1, source_target_pairs={{0,24},{8,0},{16,8},{24,16},{1,25},{9,1},{17,9},{25,17},{2,26},{10... | collective-permute-start | bytes 98312 | tf_op jit(solution)/shard_map/ppermute | solution.py:24
  60.9 5.7 %collective-permute-start.21 = (f32[1,4,4,4,128]{4,2,3,1,0:T(4,128)S(1)}, f32[1,4,4,4,128]{4,2,3,1,0:T(4,128)S(1)}, u32[]{:S(2)}, u32[]{:S(2)}) collective-permute-start(f32[1,4,4,4,128]{4,2,3,1,0:T(4,128)S(1)} %get-tuple-element.37), channel_id=1, source_target_pairs={{0,8},{8,16},{16,24},{24,0},{1,9},{9,17},{17,25},{25,1},{2,10},{10... | collective-permute-start | bytes 98312 | tf_op jit(solution)/shard_map/ppermute | solution.py:24
  61.3 5.4 %collective-permute-start.23 = (f32[4,4,1,4,128]{4,2,3,1,0:T(1,128)S(1)}, f32[4,4,1,4,128]{4,2,3,1,0:T(1,128)S(1)}, u32[]{:S(2)}, u32[]{:S(2)}) collective-permute-start(f32[4,4,1,4,128]{4,2,3,1,0:T(1,128)S(1)} %get-tuple-element.35), channel_id=1, source_target_pairs={{0,3},{1,0},{2,1},{3,2},{4,7},{5,4},{6,5},{7,6},{8,11},{9,8},{10,9... | collective-permute-start | bytes 98312 | tf_op jit(solution)/shard_map/ppermute | solution.py:24
  66.9 1.2 %copy-start.2 = (f32[512,512]{1,0:T(8,128)S(1)}, f32[512,512]{1,0:T(8,128)}, u32[]{:S(2)}) copy-start(f32[512,512]{1,0:T(8,128)} %fusion.89) | copy-start | bytes 3145732
  67.2 1.0 %copy-start.11 = (f32[8,8,512]{2,1,0:T(8,128)S(1)}, f32[8,8,512]{2,1,0:T(8,128)}, u32[]{:S(2)}) copy-start(f32[8,8,512]{2,1,0:T(8,128)} %broadcast_multiply_fusion.1) | copy-start | bytes 393220

commit v8 on v7

--- a/solution.py
+++ b/solution.py
@@ -24,10 +24,13 @@
     return lax.ppermute(block, axis, [(j, (j - step) % count) for j in range(count)])
 
 
-def axis_faces(block, axis, dim):
+def axis_faces(block, axis, dim, prepare=None):
     count = lax.axis_size(axis)
     first = lax.slice_in_dim(block, 0, 1, axis=dim)
     last = lax.slice_in_dim(block, block.shape[dim] - 1, None, axis=dim)
+    if prepare is not None:
+        first = prepare(first)
+        last = prepare(last)
     if count == 1:
         return last, first
     if count == 2:
@@ -40,8 +43,8 @@
     return lo, hi
 
 
-def all_faces(block):
-    return [axis_faces(block, axis, dim) for axis, dim in GRID_AXES]
+def all_faces(block, prepare=None):
+    return [axis_faces(block, axis, dim, prepare) for axis, dim in GRID_AXES]
 
 
 def extend_axis(block, axis, dim, halo, extra=None):
@@ -295,10 +298,10 @@
 
 
 def vcycle(residuals, inv_tiles):
+    center, coupling = level_coeffs(0)
+    faces_zero = all_faces(residuals, lambda part: omega * part.astype(jnp.float32) / center)
     rhs_zero = residuals.astype(jnp.float32)
-    center, coupling = level_coeffs(0)
     corr_zero = omega * rhs_zero / center
-    faces_zero = all_faces(corr_zero)
     rhs_one = restrict(rhs_zero - stencil(corr_zero, faces_zero, 0))
     center, coupling = level_coeffs(1)
     corr_one = omega * rhs_one / center
@@ -326,7 +329,7 @@
         mask_first[:, None, None, :] * mask_second[None, :, None, :] * mask_third[None, None, :, :]
     )
     cell_count = size_a * size_b * size_c
-    rows = precond.reshape(cell_count, orb_count)
+    rows = lax.optimization_barrier(precond.reshape(cell_count, orb_count))
     mixed = jnp.dot(rows, gram, precision=lax.Precision.HIGH, preferred_element_type=jnp.float32)
     return mixed.reshape(size_a, size_b, size_c, orb_count).astype(jnp.bfloat16)
 

time: 72.1 us -> 71.9 us (level)
  other arithmetic: 9.39 us -> 13.6 us
  local copies, waits for them, and re-layouts: 11.5 us -> 9.6 us
  matrix products: 3.39 us -> 1.8 us
  starting transfers between devices: 27.1 us -> 25.8 us
    dynamic_update_slice x4, local copies, waits for them, and re-layouts: 1.9 us -> 0.04 us  [gram_matrix(): total = lax.dynamic_update_slice(total, piece[slot], (row, col))]
    dot_general x1, matrix products: 3.39 us -> 1.8 us  [body(): jnp.dot(rows, gram, precision=lax.Precision.HIGH, preferred_element_type=...]
    div x0 -> x3, other arithmetic: none -> 1.58 us  [vcycle(): omega * part.astype(jnp.float32) / center]
    unnamed x34 -> x44, local copies, waits for them, and re-layouts: 5.35 us -> 6.78 us
    ppermute x15, starting transfers between devices: 15 us -> 13.8 us  [shifted(): lax.ppermute(block, axis, [(j, (j - step) % count) for j in range(count)])]
    reduce_sum x3, other arithmetic: 0.9 us -> 1.95 us  [restrict(): field.reshape((size_a // 2, 2, size_b // 2, 2, size_c // 2, 2) + rest)]
    div x1, other arithmetic: 1.18 us -> 0.13 us  [vcycle(): corr_zero = omega * rhs_zero / center]
    add x0 -> x1, other arithmetic: none -> 1.03 us  [post_smooth(): return updated + omega * (rhs - stencil(updated, faces, level_id)) / center]
  transfers between devices with their start and end apart: 25 -> 25, of which waited for: 7 -> 9; matrix products, arithmetic and copies ran while one was open for 10% -> 5% of each run, Pallas kernels for 0% -> 0%
where the time goes in v8:
time: 71.9 us; the launch traced here: 71.3 us
  starting transfers between devices  25.8 us (36%)
  waiting for transfers between devices  14.2 us (20%)
  other arithmetic  13.6 us (19%)
  local copies, waits for them, and re-layouts  9.6 us (13%)
  between operations  6.26 us (9%)
  matrix products  1.8 us (3%)
    ppermute x15, starting transfers between devices, shifted(): lax.ppermute(block, axis, [(j, (j - step) % count) for j in range(count)])  13.8 us
    ppermute x15, waiting for transfers between devices, shifted(): lax.ppermute(block, axis, [(j, (j - step) % count) for j in range(count)])  11.3 us
    ppermute x7, starting transfers between devices, fetch(): cache[steps] = lax.ppermute(block, tuple(axes), pairs)  7.43 us
    unnamed x44, local copies, waits for them, and re-layouts  6.78 us
    ppermute x3, starting transfers between devices, axis_faces(): lax.ppermute(jnp.concatenate([first, last], axis=dim), axis, [(0, 1), (1,...  4.56 us
    ppermute x7, waiting for transfers between devices, fetch(): cache[steps] = lax.ppermute(block, tuple(axes), pairs)  2.31 us
    sub x1, other arithmetic, coarse_levels(): remain = extended - stencil(correct_two, wrap_faces(correct_two), level_two)  2.11 us
    reduce_sum x3, other arithmetic, restrict(): field.reshape((size_a // 2, 2, size_b // 2, 2, size_c // 2, 2) + rest)  1.95 us
  transfers between devices with their start and end apart: 25, of which 9 were waited for; matrix products, arithmetic and copies ran while one was open for 5% of the time, Pallas kernels for 0%

profile of v8, /device:TPU:0, one launch (start us, length us, event | category | flops | bytes accessed | tf_op | source)
XLA Modules:
  0.0 71.3 jit_solution(12102907105458549686)
XLA Ops:
  0.0 1.5 %fusion.63 = (f32[8,8,1,4,128]{4,2,3,1,0:T(1,128)S(1)}, f32[8,8,1,4,128]{4,2,3,1,0:T(1,128)S(1)}) fusion(bf16[8,8,8,4,128]{4,2,3,1,0:T(8,128)(2,1)} %bitcast.105), kind=kLoop, calls=%fused_computation.184 | loop fusion | flops 131072 | bytes 393216 | tf_op jit(solution)/shard_map/div | solution.py:302
  1.5 0.5 collective-permute-start.4
  2.2 2.6 %collective-permute-start.2 = (f32[8,2,8,4,128]{4,2,3,1,0:T(8,128)S(1)}, f32[8,2,8,4,128]{4,2,3,1,0:T(8,128)S(1)}, u32[]{:S(2)}, u32[]{:S(2)}) collective-permute-start(f32[8,2,8,4,128]{4,2,3,1,0:T(8,128)S(1)} %pad_maximum_fusion.64), channel_id=1, source_target_pairs={{0,4},{4,0},{1,5},{5,1},{2,6},{6,2},{3,7},{7,3},{8,12},{12,8},{9,1... | collective-permute-start | bytes 786440 | tf_op jit(solution)/shard_map/ppermute | solution.py:37
  4.8 3.7 %collective-permute-start = (f32[1,8,8,4,128]{4,2,3,1,0:T(8,128)S(1)}, f32[1,8,8,4,128]{4,2,3,1,0:T(8,128)}, u32[]{:S(2)}, u32[]{:S(2)}) collective-permute-start(f32[1,8,8,4,128]{4,2,3,1,0:T(8,128)S(1)} %get-tuple-element.28), channel_id=1, source_target_pairs={{0,24},{8,0},{16,8},{24,16},{1,25},{9,1},{17,9},{25,17},{2,26},{10... | collective-permute-start | bytes 393224 | tf_op jit(solution)/shard_map/ppermute | solution.py:24
  8.4 1.2 %collective-permute-start.3 = (f32[8,8,1,4,128]{4,2,3,1,0:T(1,128)S(1)}, f32[8,8,1,4,128]{4,2,3,1,0:T(1,128)S(1)}, u32[]{:S(2)}, u32[]{:S(2)}) collective-permute-start(f32[8,8,1,4,128]{4,2,3,1,0:T(1,128)S(1)} %get-tuple-element.25), channel_id=1, source_target_pairs={{0,3},{1,0},{2,1},{3,2},{4,7},{5,4},{6,5},{7,6},{8,11},{9,8},{10,9... | collective-permute-start | bytes 393224 | tf_op jit(solution)/shard_map/ppermute | solution.py:24
  9.6 0.7 copy-done.20
  10.3 0.7 constant_dynamic-slice_fusion
  12.8 0.7 copy-done.1
  13.5 3.0 %collective-permute-done.1 = f32[1,8,8,4,128]{4,2,3,1,0:T(8,128)S(1)} collective-permute-done((f32[1,8,8,4,128]{4,2,3,1,0:T(8,128)S(1)}, f32[1,8,8,4,128]{4,2,3,1,0:T(8,128)S(1)}, u32[]{:S(2)}, u32[]{:S(2)}) %collective-permute-start.1) | collective-permute-done | bytes 131104 | tf_op jit(solution)/shard_map/ppermute | solution.py:24
  16.6 1.9 %convert_subtract_fusion.1 = f32[8,8,8,4,128]{4,2,3,1,0:T(8,128)S(1)} fusion(f32[8,8,1,4,128]{4,2,3,1,0:T(1,128)S(1)} %collective-permute-done.4, f32[10,1,8,4,128]{4,2,3,1,0:T(8,128)S(1)} %pad.114, f32[10,1,8,4,128]{4,2,3,1,0:T(8,128)S(1)} %pad.115, f32[1,8,8,4,128]{4,2,3,1,0:T(8,128)} %collective-permute-done, ...), kind=kLoop, calls=%fused_computation.1 | loop fusion | flops 8912896 | bytes 3473408 | tf_op jit(solution)/shard_map/sub | solution.py:305
  18.5 0.7 %reduce_sum.27 = f32[4,4,4,4,128]{4,2,3,1,0:T(4,128)S(1)} reduce(f32[4,2,4,2,4,2,4,128]{7,5,4,6,3,2,1,0:T(2,128)S(1)} %bitcast.108, f32[]{:T(128)} %constant.114.clone.1), dimensions={1,3,5}, to_apply=%region_0.1 | reduce | flops 229376 | bytes 1179652 | tf_op jit(solution)/shard_map/reduce_sum | solution.py:180
  19.5 0.6 collective-permute-start.6
  20.1 1.4 %collective-permute-start.9 = (f32[4,4,1,4,128]{4,2,3,1,0:T(1,128)S(1)}, f32[4,4,1,4,128]{4,2,3,1,0:T(1,128)S(1)}, u32[]{:S(2)}, u32[]{:S(2)}) collective-permute-start(f32[4,4,1,4,128]{4,2,3,1,0:T(1,128)S(1)} %get-tuple-element.41), channel_id=1, source_target_pairs={{0,3},{1,0},{2,1},{3,2},{4,7},{5,4},{6,5},{7,6},{8,11},{9,8},{10,9... | collective-permute-start | bytes 98312 | tf_op jit(solution)/shard_map/ppermute | solution.py:24
  21.4 1.5 %collective-permute-start.8 = (f32[1,4,4,4,128]{4,2,3,1,0:T(4,128)S(1)}, f32[1,4,4,4,128]{4,2,3,1,0:T(4,128)S(1)}, u32[]{:S(2)}, u32[]{:S(2)}) collective-permute-start(f32[1,4,4,4,128]{4,2,3,1,0:T(4,128)S(1)} %get-tuple-element.44), channel_id=1, source_target_pairs={{0,24},{8,0},{16,8},{24,16},{1,25},{9,1},{17,9},{25,17},{2,26},{10... | collective-permute-start | bytes 98312 | tf_op jit(solution)/shard_map/ppermute | solution.py:24
  22.9 0.6 collective-permute-start.7
  23.6 0.6 collective-permute-done.6
  24.3 1.1 %collective-permute-done.8 = f32[1,4,4,4,128]{4,2,3,1,0:T(4,128)S(1)} collective-permute-done((f32[1,4,4,4,128]{4,2,3,1,0:T(4,128)S(1)}, f32[1,4,4,4,128]{4,2,3,1,0:T(4,128)S(1)}, u32[]{:S(2)}, u32[]{:S(2)}) %collective-permute-start.8) | collective-permute-done | bytes 32800 | tf_op jit(solution)/shard_map/ppermute | solution.py:24
  25.4 3.3 %collective-permute-done.7 = f32[1,4,4,4,128]{4,2,3,1,0:T(4,128)S(1)} collective-permute-done((f32[1,4,4,4,128]{4,2,3,1,0:T(4,128)S(1)}, f32[1,4,4,4,128]{4,2,3,1,0:T(4,128)S(1)}, u32[]{:S(2)}, u32[]{:S(2)}) %collective-permute-start.7) | collective-permute-done | bytes 32800 | tf_op jit(solution)/shard_map/ppermute | solution.py:24
  28.9 0.4 copy-done.18
  29.3 0.8 %copy-done.15 = f32[1,128,128]{2,1,0:T(8,128)S(1)} copy-done((f32[1,128,128]{2,1,0:T(8,128)S(1)}, f32[1,128,128]{2,1,0:T(8,128)}, u32[]{:S(2)}) %copy-start.15) | copy-done | bytes 65560
  30.4 1.8 %collective-permute-start.12 = (f32[20480]{0:T(1024)S(1)}, f32[20480]{0:T(1024)S(1)}, u32[]{:S(2)}, u32[]{:S(2)}) collective-permute-start(f32[20480]{0:T(1024)S(1)} %pad_maximum_fusion.83), channel_id=1, source_target_pairs={{0,8},{8,16},{16,24},{24,0},{1,9},{9,17},{17,25},{25,1},{2,10},{10... | collective-permute-start | bytes 245768 | tf_op jit(solution)/shard_map/ppermute | solution.py:24
  36.1 0.3 collective-permute-done.10
  36.4 1.5 %collective-permute-done.12 = f32[20480]{0:T(1024)S(1)} collective-permute-done((f32[20480]{0:T(1024)S(1)}, f32[20480]{0:T(1024)S(1)}, u32[]{:S(2)}, u32[]{:S(2)}) %collective-permute-start.12) | collective-permute-done | bytes 81952 | tf_op jit(solution)/shard_map/ppermute | solution.py:24
  38.0 1.8 %collective-permute-start.18 = (f32[8,2,2,4,128]{4,3,1,0,2:T(4,128)S(1)}, f32[8,2,2,4,128]{4,3,1,0,2:T(4,128)S(1)}, u32[]{:S(2)}, u32[]{:S(2)}) collective-permute-start(f32[8,2,2,4,128]{4,3,1,0,2:T(4,128)S(1)} %pad_maximum_fusion.133), channel_id=1, source_target_pairs={{6,0},{7,1},{4,2},{5,3},{2,4},{3,5},{0,6},{1,7},{14,8},{15,9},{12,... | collective-permute-start | bytes 196616 | tf_op jit(solution)/shard_map/ppermute | solution.py:101
  39.8 2.3 %collective-permute-start.17 = (f32[8,2,2,4,128]{4,3,1,0,2:T(4,128)S(1)}, f32[8,2,2,4,128]{4,3,1,0,2:T(4,128)S(1)}, u32[]{:S(2)}, u32[]{:S(2)}) collective-permute-start(f32[8,2,2,4,128]{4,3,1,0,2:T(4,128)S(1)} %pad_maximum_fusion.133), channel_id=1, source_target_pairs={{5,0},{6,1},{7,2},{4,3},{1,4},{2,5},{3,6},{0,7},{13,8},{14,9},{15,... | collective-permute-start | bytes 196616 | tf_op jit(solution)/shard_map/ppermute | solution.py:101
  42.1 0.7 collective-permute-start.16
  42.9 1.1 %collective-permute-start.14 = (f32[8,2,2,4,128]{4,3,1,0,2:T(4,128)S(1)}, f32[8,2,2,4,128]{4,3,1,0,2:T(4,128)S(1)}, u32[]{:S(2)}, u32[]{:S(2)}) collective-permute-start(f32[8,2,2,4,128]{4,3,1,0,2:T(4,128)S(1)} %pad_maximum_fusion.133), channel_id=1, source_target_pairs={{2,0},{3,1},{0,2},{1,3},{6,4},{7,5},{4,6},{5,7},{10,8},{11,9},{8,1... | collective-permute-start | bytes 196616 | tf_op jit(solution)/shard_map/ppermute | solution.py:101
  44.0 1.5 %collective-permute-start.13 = (f32[8,2,2,4,128]{4,3,1,0,2:T(4,128)S(1)}, f32[8,2,2,4,128]{4,3,1,0,2:T(4,128)S(1)}, u32[]{:S(2)}, u32[]{:S(2)}) collective-permute-start(f32[8,2,2,4,128]{4,3,1,0,2:T(4,128)S(1)} %pad_maximum_fusion.133), channel_id=1, source_target_pairs={{1,0},{2,1},{3,2},{0,3},{5,4},{6,5},{7,6},{4,7},{9,8},{10,9},{11,1... | collective-permute-start | bytes 196616 | tf_op jit(solution)/shard_map/ppermute | solution.py:101
  45.4 1.3 %collective-permute-done.16 = f32[8,2,2,4,128]{4,3,1,0,2:T(4,128)S(1)} collective-permute-done((f32[8,2,2,4,128]{4,3,1,0,2:T(4,128)S(1)}, f32[8,2,2,4,128]{4,3,1,0,2:T(4,128)S(1)}, u32[]{:S(2)}, u32[]{:S(2)}) %collective-permute-start.16) | collective-permute-done | bytes 65568 | tf_op jit(solution)/shard_map/ppermute | solution.py:101
  46.8 1.0 %collective-permute-done.14 = f32[8,2,2,4,128]{4,3,1,0,2:T(4,128)S(1)} collective-permute-done((f32[8,2,2,4,128]{4,3,1,0,2:T(4,128)S(1)}, f32[8,2,2,4,128]{4,3,1,0,2:T(4,128)S(1)}, u32[]{:S(2)}, u32[]{:S(2)}) %collective-permute-start.14) | collective-permute-done | bytes 65568 | tf_op jit(solution)/shard_map/ppermute | solution.py:101
  48.2 2.1 %fusion.42 = f32[8,4,8,4,128]{4,3,1,0,2:T(4,128)} fusion(f32[8,4,8,4,128]{4,3,1,0,2:T(4,128)S(1)} %get-tuple-element.6, f32[8,4,1,4,128]{4,3,1,0,2:T(4,128)S(1)} %get-tuple-element.20, f32[10,1,8,4,128]{4,3,1,0,2:T(4,128)S(1)} %pad.122, f32[10,1,8,4,128]{4,3,1,0,2:T(4,128)S(1)} %pad.123, f32[1,4,8,4,128]{4,3,1,0,2:T(4,128)S(1)} %get-tuple-element.22, ...), kind=kLoop, calls=%fused_computation.114 | loop fusion | flops 4325376 | bytes 2162688 | tf_op jit(solution)/shard_map/sub | solution.py:225
  50.3 1.1 %reduce_sum.29 = f32[4,2,4,4,128]{4,3,1,0,2:T(4,128)S(1)} reduce(f32[4,2,2,2,4,2,4,128]{7,6,3,2,1,0,5,4:T(4,128)} %bitcast.111, f32[]{:T(128)} %constant.114.clone.1), dimensions={1,3,5}, to_apply=%region_2.3 | reduce | flops 114688 | bytes 589828 | tf_op jit(solution)/shard_map/reduce_sum | solution.py:180
  52.4 1.5 %fusion.32 = f32[8,4,8,4,128]{4,3,1,0,2:T(4,128)S(1)} fusion(f32[8,4,8,4,128]{4,3,1,0,2:T(4,128)S(1)} %bitcast_add_fusion, f32[8,4,8,4,128]{4,3,1,0,2:T(4,128)S(1)} %get-tuple-element.6, f32[8,4,1,4,128]{4,3,1,0,2:T(4,128)S(1)} %get-tuple-element.14, f32[10,1,8,4,128]{4,3,1,0,2:T(4,128)S(1)} %pad.138, f32[10,1,8,4,128]{4,3,1,0,2:T(4,128)S(1)} %pad.139, ...), kind=kLoop, calls=%fused_computation.86 | loop fusion | flops 4587520 | bytes 2162688 | tf_op jit(solution)/shard_map/add | solution.py:233
  54.3 0.7 copy-done.12
  55.2 0.3 fusion.24
  55.8 0.8 %collective-permute-start.24 = (f32[4,4,1,4,128]{4,2,3,1,0:T(1,128)S(1)}, f32[4,4,1,4,128]{4,2,3,1,0:T(1,128)S(1)}, u32[]{:S(2)}, u32[]{:S(2)}) collective-permute-start(f32[4,4,1,4,128]{4,2,3,1,0:T(1,128)S(1)} %get-tuple-element.36), channel_id=1, source_target_pairs={{0,1},{1,2},{2,3},{3,0},{4,5},{5,6},{6,7},{7,4},{8,9},{9,10},{10,1... | collective-permute-start | bytes 98312 | tf_op jit(solution)/shard_map/ppermute | solution.py:24
  56.6 1.4 %collective-permute-start.22 = (f32[4,2,4,4,128]{4,2,3,1,0:T(4,128)S(1)}, f32[4,2,4,4,128]{4,2,3,1,0:T(4,128)S(1)}, u32[]{:S(2)}, u32[]{:S(2)}) collective-permute-start(f32[4,2,4,4,128]{4,2,3,1,0:T(4,128)S(1)} %pad_maximum_fusion.134), channel_id=1, source_target_pairs={{0,4},{4,0},{1,5},{5,1},{2,6},{6,2},{3,7},{7,3},{8,12},{12,8},{9,1... | collective-permute-start | bytes 196616 | tf_op jit(solution)/shard_map/ppermute | solution.py:37
  58.0 1.5 %collective-permute-start.20 = (f32[1,4,4,4,128]{4,2,3,1,0:T(4,128)S(1)}, f32[1,4,4,4,128]{4,2,3,1,0:T(4,128)S(1)}, u32[]{:S(2)}, u32[]{:S(2)}) collective-permute-start(f32[1,4,4,4,128]{4,2,3,1,0:T(4,128)S(1)} %get-tuple-element.38), channel_id=1, source_target_pairs={{0,24},{8,0},{16,8},{24,16},{1,25},{9,1},{17,9},{25,17},{2,26},{10... | collective-permute-start | bytes 98312 | tf_op jit(solution)/shard_map/ppermute | solution.py:24
  59.5 0.5 collective-permute-start.21
  60.2 0.6 broadcast_in_dim.188
  61.0 0.8 %copy-done.8 = f32[8,8,1,4,128]{4,2,3,1,0:T(1,128)S(1)} copy-done((f32[8,8,1,4,128]{4,2,3,1,0:T(1,128)S(1)}, f32[8,8,1,4,128]{4,2,3,1,0:T(1,128)}, u32[]{:S(2)}) %copy-start.8) | copy-done | bytes 131096
  62.1 0.9 %add.395 = f32[1,8,8,4,128]{4,2,3,1,0:T(8,128)S(1)} add(f32[1,8,8,4,128]{4,2,3,1,0:T(8,128)} %collective-permute-done, f32[1,8,8,4,128]{4,2,3,1,0:T(8,128)S(1)} %bitcast.115) | non-fusion elementwise | flops 32768 | bytes 393216 | tf_op jit(solution)/shard_map/add | solution.py:263
  63.0 2.2 %collective-permute-done.21 = f32[1,4,4,4,128]{4,2,3,1,0:T(4,128)S(1)} collective-permute-done((f32[1,4,4,4,128]{4,2,3,1,0:T(4,128)S(1)}, f32[1,4,4,4,128]{4,2,3,1,0:T(4,128)S(1)}, u32[]{:S(2)}, u32[]{:S(2)}) %collective-permute-start.21) | collective-permute-done | bytes 32800 | tf_op jit(solution)/shard_map/ppermute | solution.py:24
  65.3 0.8 %copy-done.10 = f32[1,8,8,4,128]{4,2,3,1,0:T(8,128)S(1)} copy-done((f32[1,8,8,4,128]{4,2,3,1,0:T(8,128)S(1)}, f32[1,8,8,4,128]{4,2,3,1,0:T(8,128)}, u32[]{:S(2)}) %copy-start.10) | copy-done | bytes 131096
  66.2 0.8 %copy-done.6 = f32[8,8,1,4,128]{4,2,3,1,0:T(1,128)S(1)} copy-done((f32[8,8,1,4,128]{4,2,3,1,0:T(1,128)S(1)}, f32[8,8,1,4,128]{4,2,3,1,0:T(1,128)}, u32[]{:S(2)}) %copy-start.6) | copy-done | bytes 131096
  67.4 0.8 %copy-done.2 = f32[8,2,8,4,128]{4,2,3,1,0:T(8,128)S(1)} copy-done((f32[8,2,8,4,128]{4,2,3,1,0:T(8,128)S(1)}, f32[8,2,8,4,128]{4,2,3,1,0:T(8,128)}, u32[]{:S(2)}) %copy-start.2) | copy-done | bytes 262168
  68.3 1.0 %fusion.2 = f32[8,8,8,4,128]{4,2,3,1,0:T(8,128)S(1)} fusion(f32[8,8,8,4,128]{4,2,3,1,0:T(8,128)S(1)} %fusion.48, f32[8,8,1,4,128]{4,2,3,1,0:T(1,128)S(1)} %add.404, f32[10,1,8,4,128]{4,2,3,1,0:T(8,128)S(1)} %pad.146, f32[10,1,8,4,128]{4,2,3,1,0:T(8,128)S(1)} %pad.147, f32[1,8,8,4,128]{4,2,3,1,0:T(8,128)S(1)} %add.395, f32[1,8,8,4,128]{4,2,3,1,0:T(8,128)S(1)} %add.396, ...), kind=kLoop, calls=%fused_computation.7 | loop fusion | flops 9437184 | bytes 3473408 | tf_op jit(solution)/shard_map/add | solution.py:265
  69.5 1.8 %convolution_convert_fusion = bf16[512,512]{1,0:T(8,128)(2,1)} fusion(f32[512,512]{1,0:T(8,128)S(1)} %bitcast_multiply_fusion, f32[512,512]{1,0:T(8,128)S(1)} %fusion.64), kind=kOutput, calls=%fused_computation.4 | convolution fusion | flops 805568512 | bytes 2621440 | tf_op jit(solution)/shard_map/dot_general | solution.py:333
  (182 shorter events, 4.9 us)
Async XLA Ops:
  0.0 2.1 %copy-start = (bf16[8,8,8,512]{3,2,1,0:T(8,128)(2,1)S(1)}, bf16[8,8,8,512]{3,2,1,0:T(8,128)(2,1)}, u32[]{:S(2)}) copy-start(bf16[8,8,8,512]{3,2,1,0:T(8,128)(2,1)} %param.4) | copy-start | bytes 1572868
  1.5 12.0 %collective-permute-start.4 = (f32[8,8,1,4,128]{4,2,3,1,0:T(1,128)S(1)}, f32[8,8,1,4,128]{4,2,3,1,0:T(1,128)S(1)}, u32[]{:S(2)}, u32[]{:S(2)}) collective-permute-start(f32[8,8,1,4,128]{4,2,3,1,0:T(1,128)S(1)} %get-tuple-element.26), channel_id=1, source_target_pairs={{0,1},{1,2},{2,3},{3,0},{4,5},{5,6},{6,7},{7,4},{8,9},{9,10},{10,1... | collective-permute-start | bytes 393224 | tf_op jit(solution)/shard_map/ppermute | solution.py:24
  2.2 10.6 %collective-permute-start.2 = (f32[8,2,8,4,128]{4,2,3,1,0:T(8,128)S(1)}, f32[8,2,8,4,128]{4,2,3,1,0:T(8,128)S(1)}, u32[]{:S(2)}, u32[]{:S(2)}) collective-permute-start(f32[8,2,8,4,128]{4,2,3,1,0:T(8,128)S(1)} %pad_maximum_fusion.64), channel_id=1, source_target_pairs={{0,4},{4,0},{1,5},{5,1},{2,6},{6,2},{3,7},{7,3},{8,12},{12,8},{9,1... | collective-permute-start | bytes 786440 | tf_op jit(solution)/shard_map/ppermute | solution.py:37
  4.8 8.8 %collective-permute-start = (f32[1,8,8,4,128]{4,2,3,1,0:T(8,128)S(1)}, f32[1,8,8,4,128]{4,2,3,1,0:T(8,128)}, u32[]{:S(2)}, u32[]{:S(2)}) collective-permute-start(f32[1,8,8,4,128]{4,2,3,1,0:T(8,128)S(1)} %get-tuple-element.28), channel_id=1, source_target_pairs={{0,24},{8,0},{16,8},{24,16},{1,25},{9,1},{17,9},{25,17},{2,26},{10... | collective-permute-start | bytes 393224 | tf_op jit(solution)/shard_map/ppermute | solution.py:24
  8.4 8.1 %collective-permute-start.1 = (f32[1,8,8,4,128]{4,2,3,1,0:T(8,128)S(1)}, f32[1,8,8,4,128]{4,2,3,1,0:T(8,128)S(1)}, u32[]{:S(2)}, u32[]{:S(2)}) collective-permute-start(f32[1,8,8,4,128]{4,2,3,1,0:T(8,128)S(1)} %get-tuple-element.27), channel_id=1, source_target_pairs={{0,8},{8,16},{16,24},{24,0},{1,9},{9,17},{17,25},{25,1},{2,10},{10... | collective-permute-start | bytes 393224 | tf_op jit(solution)/shard_map/ppermute | solution.py:24
  8.4 8.1 %collective-permute-start.3 = (f32[8,8,1,4,128]{4,2,3,1,0:T(1,128)S(1)}, f32[8,8,1,4,128]{4,2,3,1,0:T(1,128)S(1)}, u32[]{:S(2)}, u32[]{:S(2)}) collective-permute-start(f32[8,8,1,4,128]{4,2,3,1,0:T(1,128)S(1)} %get-tuple-element.25), channel_id=1, source_target_pairs={{0,3},{1,0},{2,1},{3,2},{4,7},{5,4},{6,5},{7,6},{8,11},{9,8},{10,9... | collective-permute-start | bytes 393224 | tf_op jit(solution)/shard_map/ppermute | solution.py:24
  9.6 0.7 copy-start.20
  10.3 1.9 %copy-start.21 = (s32[3,2,512]{2,1,0:T(2,128)S(1)}, s32[3,2,512]{2,1,0:T(2,128)}, u32[]{:S(2)}) copy-start(s32[3,2,512]{2,1,0:T(2,128)} %param.5) | copy-start | bytes 36868
  12.8 0.7 copy-start.1
  13.5 4.9 %copy-start.7 = (f32[8,8,1,4,128]{4,2,3,1,0:T(1,128)}, f32[8,8,1,4,128]{4,2,3,1,0:T(1,128)S(1)}, u32[]{:S(2)}) copy-start(f32[8,8,1,4,128]{4,2,3,1,0:T(1,128)S(1)} %collective-permute-done.4) | copy-start | bytes 393220
  16.5 1.9 %copy-start.9 = (f32[1,8,8,4,128]{4,2,3,1,0:T(8,128)}, f32[1,8,8,4,128]{4,2,3,1,0:T(8,128)S(1)}, u32[]{:S(2)}) copy-start(f32[1,8,8,4,128]{4,2,3,1,0:T(8,128)S(1)} %collective-permute-done.1) | copy-start | bytes 393220
  16.6 1.9 %copy-start.5 = (f32[8,8,1,4,128]{4,2,3,1,0:T(1,128)}, f32[8,8,1,4,128]{4,2,3,1,0:T(1,128)S(1)}, u32[]{:S(2)}) copy-start(f32[8,8,1,4,128]{4,2,3,1,0:T(1,128)S(1)} %collective-permute-done.3) | copy-start | bytes 393220
  19.3 4.1 %collective-permute-start.5 = (f32[4,4,1,4,128]{4,2,3,1,0:T(1,128)S(1)}, f32[4,4,1,4,128]{4,2,3,1,0:T(1,128)S(1)}, u32[]{:S(2)}, u32[]{:S(2)}) collective-permute-start(f32[4,4,1,4,128]{4,2,3,1,0:T(1,128)S(1)} %get-tuple-element.42), channel_id=1, source_target_pairs={{0,1},{1,2},{2,3},{3,0},{4,5},{5,6},{6,7},{7,4},{8,9},{9,10},{10,1... | collective-permute-start | bytes 98312 | tf_op jit(solution)/shard_map/ppermute | solution.py:24
  19.5 4.7 %collective-permute-start.6 = (f32[4,2,4,4,128]{4,2,3,1,0:T(4,128)S(1)}, f32[4,2,4,4,128]{4,2,3,1,0:T(4,128)S(1)}, u32[]{:S(2)}, u32[]{:S(2)}) collective-permute-start(f32[4,2,4,4,128]{4,2,3,1,0:T(4,128)S(1)} %pad_maximum_fusion.132), channel_id=1, source_target_pairs={{0,4},{4,0},{1,5},{5,1},{2,6},{6,2},{3,7},{7,3},{8,12},{12,8},{9,1... | collective-permute-start | bytes 196616 | tf_op jit(solution)/shard_map/ppermute | solution.py:37
  20.1 3.4 %collective-permute-start.9 = (f32[4,4,1,4,128]{4,2,3,1,0:T(1,128)S(1)}, f32[4,4,1,4,128]{4,2,3,1,0:T(1,128)S(1)}, u32[]{:S(2)}, u32[]{:S(2)}) collective-permute-start(f32[4,4,1,4,128]{4,2,3,1,0:T(1,128)S(1)} %get-tuple-element.41), channel_id=1, source_target_pairs={{0,3},{1,0},{2,1},{3,2},{4,7},{5,4},{6,5},{7,6},{8,11},{9,8},{10,9... | collective-permute-start | bytes 98312 | tf_op jit(solution)/shard_map/ppermute | solution.py:24
  21.4 3.9 %collective-permute-start.8 = (f32[1,4,4,4,128]{4,2,3,1,0:T(4,128)S(1)}, f32[1,4,4,4,128]{4,2,3,1,0:T(4,128)S(1)}, u32[]{:S(2)}, u32[]{:S(2)}) collective-permute-start(f32[1,4,4,4,128]{4,2,3,1,0:T(4,128)S(1)} %get-tuple-element.44), channel_id=1, source_target_pairs={{0,24},{8,0},{16,8},{24,16},{1,25},{9,1},{17,9},{25,17},{2,26},{10... | collective-permute-start | bytes 98312 | tf_op jit(solution)/shard_map/ppermute | solution.py:24
  22.9 5.7 %collective-permute-start.7 = (f32[1,4,4,4,128]{4,2,3,1,0:T(4,128)S(1)}, f32[1,4,4,4,128]{4,2,3,1,0:T(4,128)S(1)}, u32[]{:S(2)}, u32[]{:S(2)}) collective-permute-start(f32[1,4,4,4,128]{4,2,3,1,0:T(4,128)S(1)} %get-tuple-element.43), channel_id=1, source_target_pairs={{0,8},{8,16},{16,24},{24,0},{1,9},{9,17},{17,25},{25,1},{2,10},{10... | collective-permute-start | bytes 98312 | tf_op jit(solution)/shard_map/ppermute | solution.py:24
  23.6 5.0 %copy-start.3 = (f32[6,6,1,4,128]{4,2,3,1,0:T(1,128)}, f32[6,6,1,4,128]{4,2,3,1,0:T(1,128)S(1)}, u32[]{:S(2)}) copy-start(f32[6,6,1,4,128]{4,2,3,1,0:T(1,128)S(1)} %pad.121) | copy-start | bytes 221188
  24.2 4.6 %copy-start.11 = (f32[6,1,4,4,128]{4,2,3,1,0:T(4,128)}, f32[6,1,4,4,128]{4,2,3,1,0:T(4,128)S(1)}, u32[]{:S(2)}) copy-start(f32[6,1,4,4,128]{4,2,3,1,0:T(4,128)S(1)} %pad.120) | copy-start | bytes 147460
  24.3 4.6 %copy-start.13 = (f32[6,1,4,4,128]{4,2,3,1,0:T(4,128)}, f32[6,1,4,4,128]{4,2,3,1,0:T(4,128)S(1)}, u32[]{:S(2)}) copy-start(f32[6,1,4,4,128]{4,2,3,1,0:T(4,128)S(1)} %pad.119) | copy-start | bytes 147460
  25.3 3.5 %copy-start.16 = (f32[1,4,4,4,128]{4,2,3,1,0:T(4,128)}, f32[1,4,4,4,128]{4,2,3,1,0:T(4,128)S(1)}, u32[]{:S(2)}) copy-start(f32[1,4,4,4,128]{4,2,3,1,0:T(4,128)S(1)} %collective-permute-done.8) | copy-start | bytes 98308
  28.6 0.6 copy-start.18
  29.3 0.8 %copy-start.15 = (f32[1,128,128]{2,1,0:T(8,128)S(1)}, f32[1,128,128]{2,1,0:T(8,128)}, u32[]{:S(2)}) copy-start(f32[1,128,128]{2,1,0:T(8,128)} %param.7) | copy-start | bytes 196612
  30.2 6.3 %collective-permute-start.10 = (f32[20480]{0:T(1024)S(1)}, f32[20480]{0:T(1024)S(1)}, u32[]{:S(2)}, u32[]{:S(2)}) collective-permute-start(f32[20480]{0:T(1024)S(1)} %pad_maximum_fusion.83), channel_id=1, source_target_pairs={{0,24},{8,0},{16,8},{24,16},{1,25},{9,1},{17,9},{25,17},{2,26},{10... | collective-permute-start | bytes 245768 | tf_op jit(solution)/shard_map/ppermute | solution.py:24
  30.3 6.1 %collective-permute-start.11 = (f32[20480]{0:T(1024)S(1)}, f32[20480]{0:T(1024)S(1)}, u32[]{:S(2)}, u32[]{:S(2)}) collective-permute-start(f32[20480]{0:T(1024)S(1)} %pad_maximum_fusion.83), channel_id=1, source_target_pairs={{0,16},{8,24},{16,0},{24,8},{1,17},{9,25},{17,1},{25,9},{2,18},{10... | collective-permute-start | bytes 245768 | tf_op jit(solution)/shard_map/ppermute | solution.py:24
  30.4 7.5 %collective-permute-start.12 = (f32[20480]{0:T(1024)S(1)}, f32[20480]{0:T(1024)S(1)}, u32[]{:S(2)}, u32[]{:S(2)}) collective-permute-start(f32[20480]{0:T(1024)S(1)} %pad_maximum_fusion.83), channel_id=1, source_target_pairs={{0,8},{8,16},{16,24},{24,0},{1,9},{9,17},{17,25},{25,1},{2,10},{10... | collective-permute-start | bytes 245768 | tf_op jit(solution)/shard_map/ppermute | solution.py:24
  37.9 4.9 %collective-permute-start.19 = (f32[8,2,2,4,128]{4,3,1,0,2:T(4,128)S(1)}, f32[8,2,2,4,128]{4,3,1,0,2:T(4,128)S(1)}, u32[]{:S(2)}, u32[]{:S(2)}) collective-permute-start(f32[8,2,2,4,128]{4,3,1,0,2:T(4,128)S(1)} %pad_maximum_fusion.133), channel_id=1, source_target_pairs={{7,0},{4,1},{5,2},{6,3},{3,4},{0,5},{1,6},{2,7},{15,8},{12,9},{13,... | collective-permute-start | bytes 196616 | tf_op jit(solution)/shard_map/ppermute | solution.py:101
  38.0 6.0 %collective-permute-start.18 = (f32[8,2,2,4,128]{4,3,1,0,2:T(4,128)S(1)}, f32[8,2,2,4,128]{4,3,1,0,2:T(4,128)S(1)}, u32[]{:S(2)}, u32[]{:S(2)}) collective-permute-start(f32[8,2,2,4,128]{4,3,1,0,2:T(4,128)S(1)} %pad_maximum_fusion.133), channel_id=1, source_target_pairs={{6,0},{7,1},{4,2},{5,3},{2,4},{3,5},{0,6},{1,7},{14,8},{15,9},{12,... | collective-permute-start | bytes 196616 | tf_op jit(solution)/shard_map/ppermute | solution.py:101
  39.8 5.6 %collective-permute-start.17 = (f32[8,2,2,4,128]{4,3,1,0,2:T(4,128)S(1)}, f32[8,2,2,4,128]{4,3,1,0,2:T(4,128)S(1)}, u32[]{:S(2)}, u32[]{:S(2)}) collective-permute-start(f32[8,2,2,4,128]{4,3,1,0,2:T(4,128)S(1)} %pad_maximum_fusion.133), channel_id=1, source_target_pairs={{5,0},{6,1},{7,2},{4,3},{1,4},{2,5},{3,6},{0,7},{13,8},{14,9},{15,... | collective-permute-start | bytes 196616 | tf_op jit(solution)/shard_map/ppermute | solution.py:101
  42.1 4.7 %collective-permute-start.16 = (f32[8,2,2,4,128]{4,3,1,0,2:T(4,128)S(1)}, f32[8,2,2,4,128]{4,3,1,0,2:T(4,128)S(1)}, u32[]{:S(2)}, u32[]{:S(2)}) collective-permute-start(f32[8,2,2,4,128]{4,3,1,0,2:T(4,128)S(1)} %pad_maximum_fusion.133), channel_id=1, source_target_pairs={{4,0},{5,1},{6,2},{7,3},{0,4},{1,5},{2,6},{3,7},{12,8},{13,9},{14,... | collective-permute-start | bytes 196616 | tf_op jit(solution)/shard_map/ppermute | solution.py:101
  42.8 4.0 %collective-permute-start.15 = (f32[8,2,2,4,128]{4,3,1,0,2:T(4,128)S(1)}, f32[8,2,2,4,128]{4,3,1,0,2:T(4,128)S(1)}, u32[]{:S(2)}, u32[]{:S(2)}) collective-permute-start(f32[8,2,2,4,128]{4,3,1,0,2:T(4,128)S(1)} %pad_maximum_fusion.133), channel_id=1, source_target_pairs={{3,0},{0,1},{1,2},{2,3},{7,4},{4,5},{5,6},{6,7},{11,8},{8,9},{9,10... | collective-permute-start | bytes 196616 | tf_op jit(solution)/shard_map/ppermute | solution.py:101
  42.9 4.9 %collective-permute-start.14 = (f32[8,2,2,4,128]{4,3,1,0,2:T(4,128)S(1)}, f32[8,2,2,4,128]{4,3,1,0,2:T(4,128)S(1)}, u32[]{:S(2)}, u32[]{:S(2)}) collective-permute-start(f32[8,2,2,4,128]{4,3,1,0,2:T(4,128)S(1)} %pad_maximum_fusion.133), channel_id=1, source_target_pairs={{2,0},{3,1},{0,2},{1,3},{6,4},{7,5},{4,6},{5,7},{10,8},{11,9},{8,1... | collective-permute-start | bytes 196616 | tf_op jit(solution)/shard_map/ppermute | solution.py:101
  44.0 3.8 %collective-permute-start.13 = (f32[8,2,2,4,128]{4,3,1,0,2:T(4,128)S(1)}, f32[8,2,2,4,128]{4,3,1,0,2:T(4,128)S(1)}, u32[]{:S(2)}, u32[]{:S(2)}) collective-permute-start(f32[8,2,2,4,128]{4,3,1,0,2:T(4,128)S(1)} %pad_maximum_fusion.133), channel_id=1, source_target_pairs={{1,0},{2,1},{3,2},{0,3},{5,4},{6,5},{7,6},{4,7},{9,8},{10,9},{11,1... | collective-permute-start | bytes 196616 | tf_op jit(solution)/shard_map/ppermute | solution.py:101
  54.2 0.8 %copy-start.12 = (f32[6,1,4,4,128]{4,2,3,1,0:T(4,128)S(1)}, f32[6,1,4,4,128]{4,2,3,1,0:T(4,128)}, u32[]{:S(2)}) copy-start(f32[6,1,4,4,128]{4,2,3,1,0:T(4,128)} %copy-done.11) | copy-start | bytes 147460
  54.2 0.8 %copy-start.14 = (f32[6,1,4,4,128]{4,2,3,1,0:T(4,128)S(1)}, f32[6,1,4,4,128]{4,2,3,1,0:T(4,128)}, u32[]{:S(2)}) copy-start(f32[6,1,4,4,128]{4,2,3,1,0:T(4,128)} %copy-done.13) | copy-start | bytes 147460
  54.2 0.8 %copy-start.17 = (f32[1,4,4,4,128]{4,2,3,1,0:T(4,128)S(1)}, f32[1,4,4,4,128]{4,2,3,1,0:T(4,128)}, u32[]{:S(2)}) copy-start(f32[1,4,4,4,128]{4,2,3,1,0:T(4,128)} %copy-done.16) | copy-start | bytes 98308
  54.2 0.8 %copy-start.19 = (f32[1,4,4,4,128]{4,2,3,1,0:T(4,128)S(1)}, f32[1,4,4,4,128]{4,2,3,1,0:T(4,128)}, u32[]{:S(2)}) copy-start(f32[1,4,4,4,128]{4,2,3,1,0:T(4,128)} %copy-done.18) | copy-start | bytes 98308
  54.3 0.9 %copy-start.4 = (f32[6,6,1,4,128]{4,2,3,1,0:T(1,128)S(1)}, f32[6,6,1,4,128]{4,2,3,1,0:T(1,128)}, u32[]{:S(2)}) copy-start(f32[6,6,1,4,128]{4,2,3,1,0:T(1,128)} %copy-done.3) | copy-start | bytes 221188
  55.8 5.2 %collective-permute-start.24 = (f32[4,4,1,4,128]{4,2,3,1,0:T(1,128)S(1)}, f32[4,4,1,4,128]{4,2,3,1,0:T(1,128)S(1)}, u32[]{:S(2)}, u32[]{:S(2)}) collective-permute-start(f32[4,4,1,4,128]{4,2,3,1,0:T(1,128)S(1)} %get-tuple-element.36), channel_id=1, source_target_pairs={{0,1},{1,2},{2,3},{3,0},{4,5},{5,6},{6,7},{7,4},{8,9},{9,10},{10,1... | collective-permute-start | bytes 98312 | tf_op jit(solution)/shard_map/ppermute | solution.py:24
  56.6 10.6 %collective-permute-start.22 = (f32[4,2,4,4,128]{4,2,3,1,0:T(4,128)S(1)}, f32[4,2,4,4,128]{4,2,3,1,0:T(4,128)S(1)}, u32[]{:S(2)}, u32[]{:S(2)}) collective-permute-start(f32[4,2,4,4,128]{4,2,3,1,0:T(4,128)S(1)} %pad_maximum_fusion.134), channel_id=1, source_target_pairs={{0,4},{4,0},{1,5},{5,1},{2,6},{6,2},{3,7},{7,3},{8,12},{12,8},{9,1... | collective-permute-start | bytes 196616 | tf_op jit(solution)/shard_map/ppermute | solution.py:37
  58.0 4.1 %collective-permute-start.20 = (f32[1,4,4,4,128]{4,2,3,1,0:T(4,128)S(1)}, f32[1,4,4,4,128]{4,2,3,1,0:T(4,128)S(1)}, u32[]{:S(2)}, u32[]{:S(2)}) collective-permute-start(f32[1,4,4,4,128]{4,2,3,1,0:T(4,128)S(1)} %get-tuple-element.38), channel_id=1, source_target_pairs={{0,24},{8,0},{16,8},{24,16},{1,25},{9,1},{17,9},{25,17},{2,26},{10... | collective-permute-start | bytes 98312 | tf_op jit(solution)/shard_map/ppermute | solution.py:24
  59.5 5.7 %collective-permute-start.21 = (f32[1,4,4,4,128]{4,2,3,1,0:T(4,128)S(1)}, f32[1,4,4,4,128]{4,2,3,1,0:T(4,128)S(1)}, u32[]{:S(2)}, u32[]{:S(2)}) collective-permute-start(f32[1,4,4,4,128]{4,2,3,1,0:T(4,128)S(1)} %get-tuple-element.37), channel_id=1, source_target_pairs={{0,8},{8,16},{16,24},{24,0},{1,9},{9,17},{17,25},{25,1},{2,10},{10... | collective-permute-start | bytes 98312 | tf_op jit(solution)/shard_map/ppermute | solution.py:24
  60.0 6.1 %collective-permute-start.23 = (f32[4,4,1,4,128]{4,2,3,1,0:T(1,128)S(1)}, f32[4,4,1,4,128]{4,2,3,1,0:T(1,128)S(1)}, u32[]{:S(2)}, u32[]{:S(2)}) collective-permute-start(f32[4,4,1,4,128]{4,2,3,1,0:T(1,128)S(1)} %get-tuple-element.35), channel_id=1, source_target_pairs={{0,3},{1,0},{2,1},{3,2},{4,7},{5,4},{6,5},{7,6},{8,11},{9,8},{10,9... | collective-permute-start | bytes 98312 | tf_op jit(solution)/shard_map/ppermute | solution.py:24
  61.0 0.9 %copy-start.8 = (f32[8,8,1,4,128]{4,2,3,1,0:T(1,128)S(1)}, f32[8,8,1,4,128]{4,2,3,1,0:T(1,128)}, u32[]{:S(2)}) copy-start(f32[8,8,1,4,128]{4,2,3,1,0:T(1,128)} %copy-done.7) | copy-start | bytes 393220
  65.2 0.9 %copy-start.10 = (f32[1,8,8,4,128]{4,2,3,1,0:T(8,128)S(1)}, f32[1,8,8,4,128]{4,2,3,1,0:T(8,128)}, u32[]{:S(2)}) copy-start(f32[1,8,8,4,128]{4,2,3,1,0:T(8,128)} %copy-done.9) | copy-start | bytes 393220
  66.1 0.9 %copy-start.6 = (f32[8,8,1,4,128]{4,2,3,1,0:T(1,128)S(1)}, f32[8,8,1,4,128]{4,2,3,1,0:T(1,128)}, u32[]{:S(2)}) copy-start(f32[8,8,1,4,128]{4,2,3,1,0:T(1,128)} %copy-done.5) | copy-start | bytes 393220
  67.2 1.0 %copy-start.2 = (f32[8,2,8,4,128]{4,2,3,1,0:T(8,128)S(1)}, f32[8,2,8,4,128]{4,2,3,1,0:T(8,128)}, u32[]{:S(2)}) copy-start(f32[8,2,8,4,128]{4,2,3,1,0:T(8,128)} %copy-done.1) | copy-start | bytes 786436

commit v9 on v8

--- a/solution.py
+++ b/solution.py
@@ -1,5 +1,6 @@
 import jax
 import jax.numpy as jnp
+import numpy as np
 from jax import lax
 from jax.sharding import PartitionSpec as P
 
@@ -12,7 +13,6 @@
 
 GRID_AXES = (("gx", 0), ("gy", 1), ("gz", 2))
 COARSE_HALO = 10
-CHUNK_BYTES = 1 << 21
 LANES = 128
 
 
@@ -164,16 +164,6 @@
     return center * middle - coupling * beside
 
 
-def wrap_faces(block):
-    faces = []
-    for dim in range(3):
-        size = block.shape[dim]
-        faces.append(
-            (lax.slice_in_dim(block, size - 1, size, axis=dim), lax.slice_in_dim(block, 0, 1, axis=dim))
-        )
-    return faces
-
-
 def restrict(field):
     size_a, size_b, size_c = field.shape[:3]
     rest = field.shape[3:]
@@ -184,56 +174,54 @@
     return jnp.repeat(jnp.repeat(jnp.repeat(field, 2, 0), 2, 1), 2, 2)
 
 
-def periodic_take(field, dim, first, count):
-    size = field.shape[dim]
-    index = [(first + k) % size for k in range(count)]
-    parts = [lax.slice_in_dim(field, i, i + 1, axis=dim) for i in index]
-    return jnp.concatenate(parts, axis=dim)
-
-
 def coarse_solve(rhs_two, tiles):
     extended = rhs_two
     starts = []
-    tiles_by_step = {}
     extended, start, tiles_by_step = extend_axis(extended, "gx", 0, COARSE_HALO, tiles)
     starts.append(start)
     extended, joint_starts = extend_joint(extended, ("gy", "gz"), (1, 2), COARSE_HALO)
     starts.extend(joint_starts)
-    width = extended.shape[3] * extended.shape[4]
-    chunks = 1
-    while extended.size * 4 // chunks > CHUNK_BYTES and width % (2 * chunks * 128) == 0:
-        chunks *= 2
-    if chunks == 1:
-        return coarse_levels(extended, starts, rhs_two.shape), tiles_by_step
-    part = width // chunks
-
-    groups = extended.shape[3] // chunks
-
-    def one_chunk(k):
-        piece = lax.dynamic_slice_in_dim(extended, k * groups, groups, axis=3)
-        return coarse_levels(piece, starts, rhs_two.shape)
-
-    outs = lax.map(one_chunk, jnp.arange(chunks))
-    outs = jnp.moveaxis(outs, 0, 3)
-    return outs.reshape(outs.shape[:3] + (extended.shape[3], extended.shape[4])), tiles_by_step
-
-
-def coarse_levels(extended, starts, block_shape):
+    grid = extended.shape[:3]
+    orbs = extended.shape[3:]
+    operator = jnp.asarray(coarse_matrix(grid, tuple(starts), rhs_two.shape[:3]))
+    flat = extended.reshape((-1,) + (int(np.prod(orbs)),))
+    post = jnp.dot(operator, flat, precision=lax.Precision.HIGHEST, preferred_element_type=jnp.float32)
+    return post.reshape(tuple(size + 2 for size in rhs_two.shape[:3]) + orbs), tiles_by_step
+
+
+def coarse_matrix(grid, starts, block):
+    cells = int(np.prod(grid))
+    field = np.eye(cells).reshape(tuple(grid) + (cells,))
+
+    def apply(v, level_id):
+        center, coupling = level_coeffs(level_id)
+        beside = 0.0
+        for dim in range(3):
+            beside = beside + np.roll(v, -1, dim) + np.roll(v, 1, dim)
+        return center * v - coupling * beside
+
+    def shrink(v):
+        a, b, c = v.shape[:3]
+        return v.reshape(a // 2, 2, b // 2, 2, c // 2, 2, -1).mean(axis=(1, 3, 5))
+
+    def grow(v):
+        return np.repeat(np.repeat(np.repeat(v, 2, 0), 2, 1), 2, 2)
+
     level_two = LEVELS - 2
     center, coupling = level_coeffs(level_two)
-    correct_two = omega * extended / center
-    remain = extended - stencil(correct_two, wrap_faces(correct_two), level_two)
-    current = restrict(remain)
+    correct_two = omega * field / center
+    current = shrink(field - apply(correct_two, level_two))
     top_level = LEVELS - 1
     center_top, coupling_top = level_coeffs(top_level)
     correct = omega * current / center_top
     for sweep_id in range(COARSE - 1):
-        correct = correct + omega * (current - stencil(correct, wrap_faces(correct), top_level)) / center_top
-    updated = correct_two + prolong(correct)
-    post = updated + omega * (extended - stencil(updated, wrap_faces(updated), level_two)) / center
+        correct = correct + omega * (current - apply(correct, top_level)) / center_top
+    updated = correct_two + grow(correct)
+    post = updated + omega * (field - apply(updated, level_two)) / center
     for dim, start in enumerate(starts):
-        post = periodic_take(post, dim, start - 1, block_shape[dim] + 2)
-    return post
+        index = [(start - 1 + k) % grid[dim] for k in range(block[dim] + 2)]
+        post = np.take(post, index, axis=dim)
+    return post.reshape(-1, cells).astype(np.float32)
 
 
 def prolong_face(face, dim):

time: 71.9 us -> 78.6 us (1.093)
  local copies, waits for them, and re-layouts: 9.6 us -> 21.1 us
  other arithmetic: 13.6 us -> 8.99 us
  waiting for transfers between devices: 14.2 us -> 13 us
    slice x5, local copies, waits for them, and re-layouts: 0.02 us -> 3.35 us  [coarse_faces(): lo = lax.slice_in_dim(inner, 0, 1, axis=dim)]
    dynamic_update_slice x4, local copies, waits for them, and re-layouts: 0.04 us -> 2.55 us  [gram_matrix(): total = lax.dynamic_update_slice(total, piece[slot], (row, col))]
    slice x3, local copies, waits for them, and re-layouts: 0.01 us -> 2.16 us  [extend_axis(): cache[step] = both[:block.size].reshape(block.shape)]
    sub x1 -> x0, other arithmetic: 2.11 us -> none  [coarse_levels(): remain = extended - stencil(correct_two, wrap_faces(correct_two), level_two)]
    slice x15 -> x2, local copies, waits for them, and re-layouts: 0.23 us -> 2.11 us  [coarse_faces(): inner = lax.slice_in_dim(inner, 1, inner.shape[other] - 1, axis=other)]
    add x5 -> x0, other arithmetic: 1.88 us -> none  [the longest x1 1.48 us: coarse_levels(): updated + omega * (extended - stencil(updated, wrap_faces(updated), level...]
    reduce_sum x3 -> x2, other arithmetic: 1.95 us -> 0.8 us  [restrict(): field.reshape((size_a // 2, 2, size_b // 2, 2, size_c // 2, 2) + rest)]
    unnamed x44 -> x42, local copies, waits for them, and re-layouts: 6.78 us -> 6.91 us
  transfers between devices with their start and end apart: 25 -> 25, of which waited for: 9 -> 7; matrix products, arithmetic and copies ran while one was open for 5% -> 10% of each run, Pallas kernels for 0% -> 0%
where the time goes in v9:
time: 78.6 us; the launch traced here: 77.5 us
  starting transfers between devices  26.2 us (33%)
  local copies, waits for them, and re-layouts  21.1 us (27%)
  waiting for transfers between devices  13 us (17%)
  other arithmetic  8.99 us (11%)
  between operations  5.92 us (8%)
  matrix products  2.24 us (3%)
    ppermute x15, starting transfers between devices, shifted(): lax.ppermute(block, axis, [(j, (j - step) % count) for j in range(count)])  14 us
    ppermute x15, waiting for transfers between devices, shifted(): lax.ppermute(block, axis, [(j, (j - step) % count) for j in range(count)])  10.6 us
    ppermute x7, starting transfers between devices, fetch(): cache[steps] = lax.ppermute(block, tuple(axes), pairs)  7.43 us
    unnamed x42, local copies, waits for them, and re-layouts  6.91 us
    ppermute x3, starting transfers between devices, axis_faces(): lax.ppermute(jnp.concatenate([first, last], axis=dim), axis, [(0, 1), (1,...  4.75 us
    slice x5, local copies, waits for them, and re-layouts, coarse_faces(): lo = lax.slice_in_dim(inner, 0, 1, axis=dim)  3.35 us
    dynamic_update_slice x4, local copies, waits for them, and re-layouts, gram_matrix(): total = lax.dynamic_update_slice(total, piece[slot], (row, col))  2.55 us
    slice x3, local copies, waits for them, and re-layouts, extend_axis(): cache[step] = both[:block.size].reshape(block.shape)  2.16 us
  transfers between devices with their start and end apart: 25, of which 7 were waited for; matrix products, arithmetic and copies ran while one was open for 10% of the time, Pallas kernels for 0%

profile of v9, /device:TPU:0, one launch (start us, length us, event | category | flops | bytes accessed | tf_op | source)
XLA Modules:
  0.0 77.5 jit_solution(12213794528561678181)
XLA Ops:
  0.0 1.5 %fusion.41 = (f32[8,8,1,4,128]{4,2,3,1,0:T(1,128)S(1)}, f32[8,8,1,4,128]{4,2,3,1,0:T(1,128)S(1)}) fusion(bf16[8,8,8,4,128]{4,2,3,1,0:T(8,128)(2,1)} %bitcast.103), kind=kLoop, calls=%fused_computation.122 | loop fusion | flops 131072 | bytes 393216 | tf_op jit(solution)/shard_map/div | solution.py:290
  2.2 2.6 %collective-permute-start.2 = (f32[8,2,8,4,128]{4,2,3,1,0:T(8,128)S(1)}, f32[8,2,8,4,128]{4,2,3,1,0:T(8,128)S(1)}, u32[]{:S(2)}, u32[]{:S(2)}) collective-permute-start(f32[8,2,8,4,128]{4,2,3,1,0:T(8,128)S(1)} %pad_maximum_fusion.32), channel_id=1, source_target_pairs={{0,4},{4,0},{1,5},{5,1},{2,6},{6,2},{3,7},{7,3},{8,12},{12,8},{9,1... | collective-permute-start | bytes 786440 | tf_op jit(solution)/shard_map/ppermute | solution.py:37
  4.8 3.7 %collective-permute-start = (f32[1,8,8,4,128]{4,2,3,1,0:T(8,128)S(1)}, f32[1,8,8,4,128]{4,2,3,1,0:T(8,128)}, u32[]{:S(2)}, u32[]{:S(2)}) collective-permute-start(f32[1,8,8,4,128]{4,2,3,1,0:T(8,128)S(1)} %get-tuple-element.8), channel_id=1, source_target_pairs={{0,24},{8,0},{16,8},{24,16},{1,25},{9,1},{17,9},{25,17},{2,26},{10... | collective-permute-start | bytes 393224 | tf_op jit(solution)/shard_map/ppermute | solution.py:24
  8.4 1.2 %collective-permute-start.3 = (f32[8,8,1,4,128]{4,2,3,1,0:T(1,128)S(1)}, f32[8,8,1,4,128]{4,2,3,1,0:T(1,128)S(1)}, u32[]{:S(2)}, u32[]{:S(2)}) collective-permute-start(f32[8,8,1,4,128]{4,2,3,1,0:T(1,128)S(1)} %get-tuple-element.5), channel_id=1, source_target_pairs={{0,3},{1,0},{2,1},{3,2},{4,7},{5,4},{6,5},{7,6},{8,11},{9,8},{10,9... | collective-permute-start | bytes 393224 | tf_op jit(solution)/shard_map/ppermute | solution.py:24
  9.6 0.7 copy-done.19
  10.3 0.7 constant_dynamic-slice_fusion
  12.9 3.7 %collective-permute-done.1 = f32[1,8,8,4,128]{4,2,3,1,0:T(8,128)S(1)} collective-permute-done((f32[1,8,8,4,128]{4,2,3,1,0:T(8,128)S(1)}, f32[1,8,8,4,128]{4,2,3,1,0:T(8,128)S(1)}, u32[]{:S(2)}, u32[]{:S(2)}) %collective-permute-start.1) | collective-permute-done | bytes 131104 | tf_op jit(solution)/shard_map/ppermute | solution.py:24
  16.6 1.9 %convert_subtract_fusion.1 = f32[8,8,8,4,128]{4,2,3,1,0:T(8,128)S(1)} fusion(f32[8,8,1,4,128]{4,2,3,1,0:T(1,128)S(1)} %collective-permute-done.4, f32[10,1,8,4,128]{4,2,3,1,0:T(8,128)S(1)} %pad.52, f32[10,1,8,4,128]{4,2,3,1,0:T(8,128)S(1)} %pad.53, f32[1,8,8,4,128]{4,2,3,1,0:T(8,128)} %collective-permute-done, ...), kind=kLoop, calls=%fused_computation.1 | loop fusion | flops 8912896 | bytes 3473408 | tf_op jit(solution)/shard_map/sub | solution.py:293
  18.4 0.7 reduce_sum.18
  20.0 1.4 %collective-permute-start.9 = (f32[4,4,1,4,128]{4,2,3,1,0:T(1,128)S(1)}, f32[4,4,1,4,128]{4,2,3,1,0:T(1,128)S(1)}, u32[]{:S(2)}, u32[]{:S(2)}) collective-permute-start(f32[4,4,1,4,128]{4,2,3,1,0:T(1,128)S(1)} %get-tuple-element.23), channel_id=1, source_target_pairs={{0,3},{1,0},{2,1},{3,2},{4,7},{5,4},{6,5},{7,6},{8,11},{9,8},{10,9... | collective-permute-start | bytes 98312 | tf_op jit(solution)/shard_map/ppermute | solution.py:24
  21.4 1.5 %collective-permute-start.8 = (f32[1,4,4,4,128]{4,2,3,1,0:T(4,128)S(1)}, f32[1,4,4,4,128]{4,2,3,1,0:T(4,128)S(1)}, u32[]{:S(2)}, u32[]{:S(2)}) collective-permute-start(f32[1,4,4,4,128]{4,2,3,1,0:T(4,128)S(1)} %get-tuple-element.26), channel_id=1, source_target_pairs={{0,24},{8,0},{16,8},{24,16},{1,25},{9,1},{17,9},{25,17},{2,26},{10... | collective-permute-start | bytes 98312 | tf_op jit(solution)/shard_map/ppermute | solution.py:24
  23.5 0.6 collective-permute-done.6
  24.2 1.1 %collective-permute-done.8 = f32[1,4,4,4,128]{4,2,3,1,0:T(4,128)S(1)} collective-permute-done((f32[1,4,4,4,128]{4,2,3,1,0:T(4,128)S(1)}, f32[1,4,4,4,128]{4,2,3,1,0:T(4,128)S(1)}, u32[]{:S(2)}, u32[]{:S(2)}) %collective-permute-start.8) | collective-permute-done | bytes 32800 | tf_op jit(solution)/shard_map/ppermute | solution.py:24
  25.3 3.3 %collective-permute-done.7 = f32[1,4,4,4,128]{4,2,3,1,0:T(4,128)S(1)} collective-permute-done((f32[1,4,4,4,128]{4,2,3,1,0:T(4,128)S(1)}, f32[1,4,4,4,128]{4,2,3,1,0:T(4,128)S(1)}, u32[]{:S(2)}, u32[]{:S(2)}) %collective-permute-start.7) | collective-permute-done | bytes 32800 | tf_op jit(solution)/shard_map/ppermute | solution.py:24
  29.3 0.8 %copy-done.9 = f32[1,128,128]{2,1,0:T(8,128)S(1)} copy-done((f32[1,128,128]{2,1,0:T(8,128)S(1)}, f32[1,128,128]{2,1,0:T(8,128)}, u32[]{:S(2)}) %copy-start.9) | copy-done | bytes 65560
  30.1 0.6 pad_maximum_fusion.51
  31.0 1.8 %collective-permute-start.12 = (f32[20480]{0:T(1024)}, f32[20480]{0:T(1024)}, u32[]{:S(2)}, u32[]{:S(2)}) collective-permute-start(f32[20480]{0:T(1024)} %pad_maximum_fusion.51), channel_id=1, source_target_pairs={{0,8},{8,16},{16,24},{24,0},{1,9},{9,17},{17,25},{25,1},{2,10},{10... | collective-permute-start | bytes 245768 | tf_op jit(solution)/shard_map/ppermute | solution.py:24
  37.3 0.7 slice.432
  38.0 0.7 slice.433
  38.7 0.7 slice.434
  39.5 2.6 %collective-permute-start.18 = (f32[8,2,2,4,128]{4,3,1,0,2:T(4,128)S(1)}, f32[8,2,2,4,128]{4,3,1,0,2:T(4,128)S(1)}, u32[]{:S(2)}, u32[]{:S(2)}) collective-permute-start(f32[8,2,2,4,128]{4,3,1,0,2:T(4,128)S(1)} %pad_maximum_fusion.53), channel_id=1, source_target_pairs={{6,0},{7,1},{4,2},{5,3},{2,4},{3,5},{0,6},{1,7},{14,8},{15,9},{12,... | collective-permute-start | bytes 196616 | tf_op jit(solution)/shard_map/ppermute | solution.py:101
  42.2 2.3 %collective-permute-start.17 = (f32[8,2,2,4,128]{4,3,1,0,2:T(4,128)S(1)}, f32[8,2,2,4,128]{4,3,1,0,2:T(4,128)S(1)}, u32[]{:S(2)}, u32[]{:S(2)}) collective-permute-start(f32[8,2,2,4,128]{4,3,1,0,2:T(4,128)S(1)} %pad_maximum_fusion.53), channel_id=1, source_target_pairs={{5,0},{6,1},{7,2},{4,3},{1,4},{2,5},{3,6},{0,7},{13,8},{14,9},{15,... | collective-permute-start | bytes 196616 | tf_op jit(solution)/shard_map/ppermute | solution.py:101
  45.0 0.8 %fusion.44 = f32[512,512]{1,0:T(8,128)S(1)} fusion(f32[512,512]{1,0:T(8,128)S(1)} %bitcast_dynamic-update-slice_fusion, s32[]{:T(128)S(6)} %select_n.65, s32[]{:T(128)S(6)} %select_n.66, f32[20480]{0:T(1024)} %collective-permute-done.10), kind=kLoop, calls=%fused_computation.133 | loop fusion | bytes 131080 | tf_op jit(solution)/shard_map/dynamic_update_slice | solution.py:284
  45.8 0.8 %fusion.43 = f32[512,512]{1,0:T(8,128)S(1)} fusion(f32[512,512]{1,0:T(8,128)S(1)} %fusion.44, s32[]{:T(128)S(6)} %select_n.69, s32[]{:T(128)S(6)} %select_n.70, f32[20480]{0:T(1024)} %collective-permute-done.11), kind=kLoop, calls=%fused_computation.131 | loop fusion | bytes 131080 | tf_op jit(solution)/shard_map/dynamic_update_slice | solution.py:284
  47.2 1.5 %collective-permute-start.13 = (f32[8,2,2,4,128]{4,3,1,0,2:T(4,128)S(1)}, f32[8,2,2,4,128]{4,3,1,0,2:T(4,128)S(1)}, u32[]{:S(2)}, u32[]{:S(2)}) collective-permute-start(f32[8,2,2,4,128]{4,3,1,0,2:T(4,128)S(1)} %pad_maximum_fusion.53), channel_id=1, source_target_pairs={{1,0},{2,1},{3,2},{0,3},{5,4},{6,5},{7,6},{4,7},{9,8},{10,9},{11,1... | collective-permute-start | bytes 196616 | tf_op jit(solution)/shard_map/ppermute | solution.py:101
  48.6 0.8 %fusion.42 = f32[512,512]{1,0:T(8,128)S(1)} fusion(f32[512,512]{1,0:T(8,128)S(1)} %fusion.43, s32[]{:T(128)S(6)} %select_n.73, s32[]{:T(128)S(6)} %select_n.74, f32[20480]{0:T(1024)} %collective-permute-done.12), kind=kLoop, calls=%fused_computation.129 | loop fusion | bytes 131080 | tf_op jit(solution)/shard_map/dynamic_update_slice | solution.py:284
  49.5 1.8 %collective-permute-done.14 = f32[8,2,2,4,128]{4,3,1,0,2:T(4,128)S(1)} collective-permute-done((f32[8,2,2,4,128]{4,3,1,0,2:T(4,128)S(1)}, f32[8,2,2,4,128]{4,3,1,0,2:T(4,128)S(1)}, u32[]{:S(2)}, u32[]{:S(2)}) %collective-permute-start.14) | collective-permute-done | bytes 65568 | tf_op jit(solution)/shard_map/ppermute | solution.py:101
  52.7 0.6 slice.435
  53.3 1.5 %slice.369 = f32[2,4,4,4,128]{4,3,2,1,0:T(4,128)} reshape(f32[32,512]{1,0:T(8,128)} %slice.435) | data formatting | bytes 131072 | tf_op jit(solution)/shard_map/slice | solution.py:238
  54.8 1.3 %slice_bitcast_fusion.10 = (f32[2,2,4,128]{3,2,1,0:T(4,128)}, f32[2,2,4,128]{3,2,1,0:T(4,128)}) fusion(f32[2,4,4,4,128]{4,3,2,1,0:T(4,128)} %slice.369), kind=kLoop, calls=%fused_computation.151 | loop fusion | bytes 32768 | tf_op jit(solution)/shard_map/slice | solution.py:240
  56.1 1.3 %slice_bitcast_fusion.9 = (f32[2,2,4,128]{3,2,1,0:T(4,128)}, f32[2,2,4,128]{3,2,1,0:T(4,128)}) fusion(f32[2,4,4,4,128]{4,3,2,1,0:T(4,128)} %slice.369), kind=kLoop, calls=%fused_computation.150 | loop fusion | bytes 32768 | tf_op jit(solution)/shard_map/slice | solution.py:240
  57.4 0.7 reshape.480
  58.1 0.7 slice_bitcast_fusion.8
  58.8 0.7 slice.439
  59.6 0.7 copy-done.17
  60.3 0.7 copy-done.16
  61.1 0.7 copy-done.15
  62.0 0.7 copy-done.8
  63.4 1.1 %collective-permute-start.24 = (f32[4,4,1,4,128]{4,2,3,1,0:T(1,128)S(1)}, f32[4,4,1,4,128]{4,2,3,1,0:T(1,128)S(1)}, u32[]{:S(2)}, u32[]{:S(2)}) collective-permute-start(f32[4,4,1,4,128]{4,2,3,1,0:T(1,128)S(1)} %get-tuple-element.16), channel_id=1, source_target_pairs={{0,1},{1,2},{2,3},{3,0},{4,5},{5,6},{6,7},{7,4},{8,9},{9,10},{10,1... | collective-permute-start | bytes 98312 | tf_op jit(solution)/shard_map/ppermute | solution.py:24
  64.4 1.6 %collective-permute-start.22 = (f32[4,2,4,4,128]{4,2,3,1,0:T(4,128)S(1)}, f32[4,2,4,4,128]{4,2,3,1,0:T(4,128)S(1)}, u32[]{:S(2)}, u32[]{:S(2)}) collective-permute-start(f32[4,2,4,4,128]{4,2,3,1,0:T(4,128)S(1)} %pad_maximum_fusion.54), channel_id=1, source_target_pairs={{0,4},{4,0},{1,5},{5,1},{2,6},{6,2},{3,7},{7,3},{8,12},{12,8},{9,1... | collective-permute-start | bytes 196616 | tf_op jit(solution)/shard_map/ppermute | solution.py:37
  66.0 1.3 %collective-permute-start.20 = (f32[1,4,4,4,128]{4,2,3,1,0:T(4,128)S(1)}, f32[1,4,4,4,128]{4,2,3,1,0:T(4,128)S(1)}, u32[]{:S(2)}, u32[]{:S(2)}) collective-permute-start(f32[1,4,4,4,128]{4,2,3,1,0:T(4,128)S(1)} %get-tuple-element.18), channel_id=1, source_target_pairs={{0,24},{8,0},{16,8},{24,16},{1,25},{9,1},{17,9},{25,17},{2,26},{10... | collective-permute-start | bytes 98312 | tf_op jit(solution)/shard_map/ppermute | solution.py:24
  67.3 0.7 collective-permute-start.21
  69.0 0.8 %copy-done.2 = f32[8,8,1,4,128]{4,2,3,1,0:T(1,128)S(1)} copy-done((f32[8,8,1,4,128]{4,2,3,1,0:T(1,128)S(1)}, f32[8,8,1,4,128]{4,2,3,1,0:T(1,128)}, u32[]{:S(2)}) %copy-start.2) | copy-done | bytes 131096
  70.1 0.9 %add.235 = f32[1,8,8,4,128]{4,2,3,1,0:T(8,128)S(1)} add(f32[1,8,8,4,128]{4,2,3,1,0:T(8,128)} %collective-permute-done, f32[1,8,8,4,128]{4,2,3,1,0:T(8,128)S(1)} %bitcast.112) | non-fusion elementwise | flops 32768 | bytes 393216 | tf_op jit(solution)/shard_map/add | solution.py:251
  71.0 2.0 %collective-permute-done.21 = f32[1,4,4,4,128]{4,2,3,1,0:T(4,128)S(1)} collective-permute-done((f32[1,4,4,4,128]{4,2,3,1,0:T(4,128)S(1)}, f32[1,4,4,4,128]{4,2,3,1,0:T(4,128)S(1)}, u32[]{:S(2)}, u32[]{:S(2)}) %collective-permute-start.21) | collective-permute-done | bytes 32800 | tf_op jit(solution)/shard_map/ppermute | solution.py:24
  73.1 0.8 %copy-done.4 = f32[1,8,8,4,128]{4,2,3,1,0:T(8,128)S(1)} copy-done((f32[1,8,8,4,128]{4,2,3,1,0:T(8,128)S(1)}, f32[1,8,8,4,128]{4,2,3,1,0:T(8,128)}, u32[]{:S(2)}) %copy-start.4) | copy-done | bytes 131096
  74.4 1.0 %fusion.2 = f32[8,8,8,4,128]{4,2,3,1,0:T(8,128)S(1)} fusion(f32[8,8,8,4,128]{4,2,3,1,0:T(8,128)S(1)} %fusion.26, f32[8,8,1,4,128]{4,2,3,1,0:T(1,128)S(1)} %add.244, f32[10,1,8,4,128]{4,2,3,1,0:T(8,128)S(1)} %pad.64, f32[10,1,8,4,128]{4,2,3,1,0:T(8,128)S(1)} %pad.65, f32[1,8,8,4,128]{4,2,3,1,0:T(8,128)S(1)} %add.235, f32[1,8,8,4,128]{4,2,3,1,0:T(8,128)S(1)} %add.236, ...), kind=kLoop, calls=%fused_computation.7 | loop fusion | flops 9437184 | bytes 3473408 | tf_op jit(solution)/shard_map/add | solution.py:253
  75.7 1.8 %convolution_convert_fusion = bf16[512,512]{1,0:T(8,128)(2,1)} fusion(f32[512,512]{1,0:T(8,128)S(1)} %bitcast_multiply_fusion, f32[512,512]{1,0:T(8,128)S(1)} %fusion.42), kind=kOutput, calls=%fused_computation.4 | convolution fusion | flops 805568512 | bytes 2621440 | tf_op jit(solution)/shard_map/dot_general | solution.py:321
  (150 shorter events, 9.4 us)
Async XLA Ops:
  0.0 2.1 %copy-start = (bf16[8,8,8,512]{3,2,1,0:T(8,128)(2,1)S(1)}, bf16[8,8,8,512]{3,2,1,0:T(8,128)(2,1)}, u32[]{:S(2)}) copy-start(bf16[8,8,8,512]{3,2,1,0:T(8,128)(2,1)} %param.5) | copy-start | bytes 1572868
  1.5 11.3 %collective-permute-start.4 = (f32[8,8,1,4,128]{4,2,3,1,0:T(1,128)S(1)}, f32[8,8,1,4,128]{4,2,3,1,0:T(1,128)S(1)}, u32[]{:S(2)}, u32[]{:S(2)}) collective-permute-start(f32[8,8,1,4,128]{4,2,3,1,0:T(1,128)S(1)} %get-tuple-element.6), channel_id=1, source_target_pairs={{0,1},{1,2},{2,3},{3,0},{4,5},{5,6},{6,7},{7,4},{8,9},{9,10},{10,1... | collective-permute-start | bytes 393224 | tf_op jit(solution)/shard_map/ppermute | solution.py:24
  2.2 10.6 %collective-permute-start.2 = (f32[8,2,8,4,128]{4,2,3,1,0:T(8,128)S(1)}, f32[8,2,8,4,128]{4,2,3,1,0:T(8,128)S(1)}, u32[]{:S(2)}, u32[]{:S(2)}) collective-permute-start(f32[8,2,8,4,128]{4,2,3,1,0:T(8,128)S(1)} %pad_maximum_fusion.32), channel_id=1, source_target_pairs={{0,4},{4,0},{1,5},{5,1},{2,6},{6,2},{3,7},{7,3},{8,12},{12,8},{9,1... | collective-permute-start | bytes 786440 | tf_op jit(solution)/shard_map/ppermute | solution.py:37
  4.8 8.1 %collective-permute-start = (f32[1,8,8,4,128]{4,2,3,1,0:T(8,128)S(1)}, f32[1,8,8,4,128]{4,2,3,1,0:T(8,128)}, u32[]{:S(2)}, u32[]{:S(2)}) collective-permute-start(f32[1,8,8,4,128]{4,2,3,1,0:T(8,128)S(1)} %get-tuple-element.8), channel_id=1, source_target_pairs={{0,24},{8,0},{16,8},{24,16},{1,25},{9,1},{17,9},{25,17},{2,26},{10... | collective-permute-start | bytes 393224 | tf_op jit(solution)/shard_map/ppermute | solution.py:24
  8.4 8.1 %collective-permute-start.1 = (f32[1,8,8,4,128]{4,2,3,1,0:T(8,128)S(1)}, f32[1,8,8,4,128]{4,2,3,1,0:T(8,128)S(1)}, u32[]{:S(2)}, u32[]{:S(2)}) collective-permute-start(f32[1,8,8,4,128]{4,2,3,1,0:T(8,128)S(1)} %get-tuple-element.7), channel_id=1, source_target_pairs={{0,8},{8,16},{16,24},{24,0},{1,9},{9,17},{17,25},{25,1},{2,10},{10... | collective-permute-start | bytes 393224 | tf_op jit(solution)/shard_map/ppermute | solution.py:24
  8.4 8.1 %collective-permute-start.3 = (f32[8,8,1,4,128]{4,2,3,1,0:T(1,128)S(1)}, f32[8,8,1,4,128]{4,2,3,1,0:T(1,128)S(1)}, u32[]{:S(2)}, u32[]{:S(2)}) collective-permute-start(f32[8,8,1,4,128]{4,2,3,1,0:T(1,128)S(1)} %get-tuple-element.5), channel_id=1, source_target_pairs={{0,3},{1,0},{2,1},{3,2},{4,7},{5,4},{6,5},{7,6},{8,11},{9,8},{10,9... | collective-permute-start | bytes 393224 | tf_op jit(solution)/shard_map/ppermute | solution.py:24
  9.6 0.7 copy-start.19
  10.3 1.9 %copy-start.20 = (s32[3,2,512]{2,1,0:T(2,128)S(1)}, s32[3,2,512]{2,1,0:T(2,128)}, u32[]{:S(2)}) copy-start(s32[3,2,512]{2,1,0:T(2,128)} %param.6) | copy-start | bytes 36868
  12.8 5.6 %copy-start.1 = (f32[8,8,1,4,128]{4,2,3,1,0:T(1,128)}, f32[8,8,1,4,128]{4,2,3,1,0:T(1,128)S(1)}, u32[]{:S(2)}) copy-start(f32[8,8,1,4,128]{4,2,3,1,0:T(1,128)S(1)} %collective-permute-done.4) | copy-start | bytes 393220
  16.5 1.9 %copy-start.3 = (f32[1,8,8,4,128]{4,2,3,1,0:T(8,128)}, f32[1,8,8,4,128]{4,2,3,1,0:T(8,128)S(1)}, u32[]{:S(2)}) copy-start(f32[1,8,8,4,128]{4,2,3,1,0:T(8,128)S(1)} %collective-permute-done.1) | copy-start | bytes 393220
  19.3 4.1 %collective-permute-start.5 = (f32[4,4,1,4,128]{4,2,3,1,0:T(1,128)S(1)}, f32[4,4,1,4,128]{4,2,3,1,0:T(1,128)S(1)}, u32[]{:S(2)}, u32[]{:S(2)}) collective-permute-start(f32[4,4,1,4,128]{4,2,3,1,0:T(1,128)S(1)} %get-tuple-element.24), channel_id=1, source_target_pairs={{0,1},{1,2},{2,3},{3,0},{4,5},{5,6},{6,7},{7,4},{8,9},{9,10},{10,1... | collective-permute-start | bytes 98312 | tf_op jit(solution)/shard_map/ppermute | solution.py:24
  19.5 4.7 %collective-permute-start.6 = (f32[4,2,4,4,128]{4,2,3,1,0:T(4,128)S(1)}, f32[4,2,4,4,128]{4,2,3,1,0:T(4,128)S(1)}, u32[]{:S(2)}, u32[]{:S(2)}) collective-permute-start(f32[4,2,4,4,128]{4,2,3,1,0:T(4,128)S(1)} %pad_maximum_fusion.52), channel_id=1, source_target_pairs={{0,4},{4,0},{1,5},{5,1},{2,6},{6,2},{3,7},{7,3},{8,12},{12,8},{9,1... | collective-permute-start | bytes 196616 | tf_op jit(solution)/shard_map/ppermute | solution.py:37
  20.0 3.4 %collective-permute-start.9 = (f32[4,4,1,4,128]{4,2,3,1,0:T(1,128)S(1)}, f32[4,4,1,4,128]{4,2,3,1,0:T(1,128)S(1)}, u32[]{:S(2)}, u32[]{:S(2)}) collective-permute-start(f32[4,4,1,4,128]{4,2,3,1,0:T(1,128)S(1)} %get-tuple-element.23), channel_id=1, source_target_pairs={{0,3},{1,0},{2,1},{3,2},{4,7},{5,4},{6,5},{7,6},{8,11},{9,8},{10,9... | collective-permute-start | bytes 98312 | tf_op jit(solution)/shard_map/ppermute | solution.py:24
  21.4 3.9 %collective-permute-start.8 = (f32[1,4,4,4,128]{4,2,3,1,0:T(4,128)S(1)}, f32[1,4,4,4,128]{4,2,3,1,0:T(4,128)S(1)}, u32[]{:S(2)}, u32[]{:S(2)}) collective-permute-start(f32[1,4,4,4,128]{4,2,3,1,0:T(4,128)S(1)} %get-tuple-element.26), channel_id=1, source_target_pairs={{0,24},{8,0},{16,8},{24,16},{1,25},{9,1},{17,9},{25,17},{2,26},{10... | collective-permute-start | bytes 98312 | tf_op jit(solution)/shard_map/ppermute | solution.py:24
  22.9 5.7 %collective-permute-start.7 = (f32[1,4,4,4,128]{4,2,3,1,0:T(4,128)S(1)}, f32[1,4,4,4,128]{4,2,3,1,0:T(4,128)S(1)}, u32[]{:S(2)}, u32[]{:S(2)}) collective-permute-start(f32[1,4,4,4,128]{4,2,3,1,0:T(4,128)S(1)} %get-tuple-element.25), channel_id=1, source_target_pairs={{0,8},{8,16},{16,24},{24,0},{1,9},{9,17},{17,25},{25,1},{2,10},{10... | collective-permute-start | bytes 98312 | tf_op jit(solution)/shard_map/ppermute | solution.py:24
  24.2 4.6 %copy-start.5 = (f32[6,1,4,4,128]{4,2,3,1,0:T(4,128)}, f32[6,1,4,4,128]{4,2,3,1,0:T(4,128)S(1)}, u32[]{:S(2)}) copy-start(f32[6,1,4,4,128]{4,2,3,1,0:T(4,128)S(1)} %pad.58) | copy-start | bytes 147460
  24.2 4.6 %copy-start.7 = (f32[6,1,4,4,128]{4,2,3,1,0:T(4,128)}, f32[6,1,4,4,128]{4,2,3,1,0:T(4,128)S(1)}, u32[]{:S(2)}) copy-start(f32[6,1,4,4,128]{4,2,3,1,0:T(4,128)S(1)} %pad.57) | copy-start | bytes 147460
  25.3 3.5 %copy-start.10 = (f32[1,4,4,4,128]{4,2,3,1,0:T(4,128)}, f32[1,4,4,4,128]{4,2,3,1,0:T(4,128)S(1)}, u32[]{:S(2)}) copy-start(f32[1,4,4,4,128]{4,2,3,1,0:T(4,128)S(1)} %collective-permute-done.8) | copy-start | bytes 98308
  28.6 0.6 copy-start.12
  29.3 0.8 %copy-start.9 = (f32[1,128,128]{2,1,0:T(8,128)S(1)}, f32[1,128,128]{2,1,0:T(8,128)}, u32[]{:S(2)}) copy-start(f32[1,128,128]{2,1,0:T(8,128)} %param.8) | copy-start | bytes 196612
  30.7 6.5 %collective-permute-start.10 = (f32[20480]{0:T(1024)}, f32[20480]{0:T(1024)}, u32[]{:S(2)}, u32[]{:S(2)}) collective-permute-start(f32[20480]{0:T(1024)} %pad_maximum_fusion.51), channel_id=1, source_target_pairs={{0,24},{8,0},{16,8},{24,16},{1,25},{9,1},{17,9},{25,17},{2,26},{10... | collective-permute-start | bytes 245768 | tf_op jit(solution)/shard_map/ppermute | solution.py:24
  30.9 7.1 %collective-permute-start.11 = (f32[20480]{0:T(1024)}, f32[20480]{0:T(1024)}, u32[]{:S(2)}, u32[]{:S(2)}) collective-permute-start(f32[20480]{0:T(1024)} %pad_maximum_fusion.51), channel_id=1, source_target_pairs={{0,16},{8,24},{16,0},{24,8},{1,17},{9,25},{17,1},{25,9},{2,18},{10... | collective-permute-start | bytes 245768 | tf_op jit(solution)/shard_map/ppermute | solution.py:24
  31.0 7.8 %collective-permute-start.12 = (f32[20480]{0:T(1024)}, f32[20480]{0:T(1024)}, u32[]{:S(2)}, u32[]{:S(2)}) collective-permute-start(f32[20480]{0:T(1024)} %pad_maximum_fusion.51), channel_id=1, source_target_pairs={{0,8},{8,16},{16,24},{24,0},{1,9},{9,17},{17,25},{25,1},{2,10},{10... | collective-permute-start | bytes 245768 | tf_op jit(solution)/shard_map/ppermute | solution.py:24
  39.5 7.2 %collective-permute-start.19 = (f32[8,2,2,4,128]{4,3,1,0,2:T(4,128)S(1)}, f32[8,2,2,4,128]{4,3,1,0,2:T(4,128)S(1)}, u32[]{:S(2)}, u32[]{:S(2)}) collective-permute-start(f32[8,2,2,4,128]{4,3,1,0,2:T(4,128)S(1)} %pad_maximum_fusion.53), channel_id=1, source_target_pairs={{7,0},{4,1},{5,2},{6,3},{3,4},{0,5},{1,6},{2,7},{15,8},{12,9},{13,... | collective-permute-start | bytes 196616 | tf_op jit(solution)/shard_map/ppermute | solution.py:101
  39.5 7.6 %collective-permute-start.18 = (f32[8,2,2,4,128]{4,3,1,0,2:T(4,128)S(1)}, f32[8,2,2,4,128]{4,3,1,0,2:T(4,128)S(1)}, u32[]{:S(2)}, u32[]{:S(2)}) collective-permute-start(f32[8,2,2,4,128]{4,3,1,0,2:T(4,128)S(1)} %pad_maximum_fusion.53), channel_id=1, source_target_pairs={{6,0},{7,1},{4,2},{5,3},{2,4},{3,5},{0,6},{1,7},{14,8},{15,9},{12,... | collective-permute-start | bytes 196616 | tf_op jit(solution)/shard_map/ppermute | solution.py:101
  42.2 7.3 %collective-permute-start.17 = (f32[8,2,2,4,128]{4,3,1,0,2:T(4,128)S(1)}, f32[8,2,2,4,128]{4,3,1,0,2:T(4,128)S(1)}, u32[]{:S(2)}, u32[]{:S(2)}) collective-permute-start(f32[8,2,2,4,128]{4,3,1,0,2:T(4,128)S(1)} %pad_maximum_fusion.53), channel_id=1, source_target_pairs={{5,0},{6,1},{7,2},{4,3},{1,4},{2,5},{3,6},{0,7},{13,8},{14,9},{15,... | collective-permute-start | bytes 196616 | tf_op jit(solution)/shard_map/ppermute | solution.py:101
  44.5 5.0 %collective-permute-start.16 = (f32[8,2,2,4,128]{4,3,1,0,2:T(4,128)S(1)}, f32[8,2,2,4,128]{4,3,1,0,2:T(4,128)S(1)}, u32[]{:S(2)}, u32[]{:S(2)}) collective-permute-start(f32[8,2,2,4,128]{4,3,1,0,2:T(4,128)S(1)} %pad_maximum_fusion.53), channel_id=1, source_target_pairs={{4,0},{5,1},{6,2},{7,3},{0,4},{1,5},{2,6},{3,7},{12,8},{13,9},{14,... | collective-permute-start | bytes 196616 | tf_op jit(solution)/shard_map/ppermute | solution.py:101
  45.0 4.5 %collective-permute-start.15 = (f32[8,2,2,4,128]{4,3,1,0,2:T(4,128)S(1)}, f32[8,2,2,4,128]{4,3,1,0,2:T(4,128)S(1)}, u32[]{:S(2)}, u32[]{:S(2)}) collective-permute-start(f32[8,2,2,4,128]{4,3,1,0,2:T(4,128)S(1)} %pad_maximum_fusion.53), channel_id=1, source_target_pairs={{3,0},{0,1},{1,2},{2,3},{7,4},{4,5},{5,6},{6,7},{11,8},{8,9},{9,10... | collective-permute-start | bytes 196616 | tf_op jit(solution)/shard_map/ppermute | solution.py:101
  46.7 4.6 %collective-permute-start.14 = (f32[8,2,2,4,128]{4,3,1,0,2:T(4,128)S(1)}, f32[8,2,2,4,128]{4,3,1,0,2:T(4,128)S(1)}, u32[]{:S(2)}, u32[]{:S(2)}) collective-permute-start(f32[8,2,2,4,128]{4,3,1,0,2:T(4,128)S(1)} %pad_maximum_fusion.53), channel_id=1, source_target_pairs={{2,0},{3,1},{0,2},{1,3},{6,4},{7,5},{4,6},{5,7},{10,8},{11,9},{8,1... | collective-permute-start | bytes 196616 | tf_op jit(solution)/shard_map/ppermute | solution.py:101
  47.2 4.1 %collective-permute-start.13 = (f32[8,2,2,4,128]{4,3,1,0,2:T(4,128)S(1)}, f32[8,2,2,4,128]{4,3,1,0,2:T(4,128)S(1)}, u32[]{:S(2)}, u32[]{:S(2)}) collective-permute-start(f32[8,2,2,4,128]{4,3,1,0,2:T(4,128)S(1)} %pad_maximum_fusion.53), channel_id=1, source_target_pairs={{1,0},{2,1},{3,2},{0,3},{5,4},{6,5},{7,6},{4,7},{9,8},{10,9},{11,1... | collective-permute-start | bytes 196616 | tf_op jit(solution)/shard_map/ppermute | solution.py:101
  51.4 0.8 %copy-start.14 = (f32[64,256]{1,0:T(8,128)S(1)}, f32[64,256]{1,0:T(8,128)}, u32[]{:S(2)}) copy-start(f32[64,256]{1,0:T(8,128)} %constant.111.clone) | copy-start | bytes 196612
  58.8 0.7 copy-start.18
  59.6 0.7 copy-start.17
  60.3 0.7 copy-start.16
  61.1 0.7 copy-start.15
  61.9 0.8 %copy-start.8 = (f32[6,1,4,4,128]{4,2,3,1,0:T(4,128)S(1)}, f32[6,1,4,4,128]{4,2,3,1,0:T(4,128)}, u32[]{:S(2)}) copy-start(f32[6,1,4,4,128]{4,2,3,1,0:T(4,128)} %copy-done.7) | copy-start | bytes 147460
  61.9 0.8 %copy-start.11 = (f32[1,4,4,4,128]{4,2,3,1,0:T(4,128)S(1)}, f32[1,4,4,4,128]{4,2,3,1,0:T(4,128)}, u32[]{:S(2)}) copy-start(f32[1,4,4,4,128]{4,2,3,1,0:T(4,128)} %copy-done.10) | copy-start | bytes 98308
  61.9 0.8 %copy-start.13 = (f32[1,4,4,4,128]{4,2,3,1,0:T(4,128)S(1)}, f32[1,4,4,4,128]{4,2,3,1,0:T(4,128)}, u32[]{:S(2)}) copy-start(f32[1,4,4,4,128]{4,2,3,1,0:T(4,128)} %copy-done.12) | copy-start | bytes 98308
  61.9 0.8 %copy-start.6 = (f32[6,1,4,4,128]{4,2,3,1,0:T(4,128)S(1)}, f32[6,1,4,4,128]{4,2,3,1,0:T(4,128)}, u32[]{:S(2)}) copy-start(f32[6,1,4,4,128]{4,2,3,1,0:T(4,128)} %copy-done.5) | copy-start | bytes 147460
  63.4 5.6 %collective-permute-start.24 = (f32[4,4,1,4,128]{4,2,3,1,0:T(1,128)S(1)}, f32[4,4,1,4,128]{4,2,3,1,0:T(1,128)S(1)}, u32[]{:S(2)}, u32[]{:S(2)}) collective-permute-start(f32[4,4,1,4,128]{4,2,3,1,0:T(1,128)S(1)} %get-tuple-element.16), channel_id=1, source_target_pairs={{0,1},{1,2},{2,3},{3,0},{4,5},{5,6},{6,7},{7,4},{8,9},{9,10},{10,1... | collective-permute-start | bytes 98312 | tf_op jit(solution)/shard_map/ppermute | solution.py:24
  64.4 9.7 %collective-permute-start.22 = (f32[4,2,4,4,128]{4,2,3,1,0:T(4,128)S(1)}, f32[4,2,4,4,128]{4,2,3,1,0:T(4,128)S(1)}, u32[]{:S(2)}, u32[]{:S(2)}) collective-permute-start(f32[4,2,4,4,128]{4,2,3,1,0:T(4,128)S(1)} %pad_maximum_fusion.54), channel_id=1, source_target_pairs={{0,4},{4,0},{1,5},{5,1},{2,6},{6,2},{3,7},{7,3},{8,12},{12,8},{9,1... | collective-permute-start | bytes 196616 | tf_op jit(solution)/shard_map/ppermute | solution.py:37
  66.0 4.0 %collective-permute-start.20 = (f32[1,4,4,4,128]{4,2,3,1,0:T(4,128)S(1)}, f32[1,4,4,4,128]{4,2,3,1,0:T(4,128)S(1)}, u32[]{:S(2)}, u32[]{:S(2)}) collective-permute-start(f32[1,4,4,4,128]{4,2,3,1,0:T(4,128)S(1)} %get-tuple-element.18), channel_id=1, source_target_pairs={{0,24},{8,0},{16,8},{24,16},{1,25},{9,1},{17,9},{25,17},{2,26},{10... | collective-permute-start | bytes 98312 | tf_op jit(solution)/shard_map/ppermute | solution.py:24
  67.3 5.7 %collective-permute-start.21 = (f32[1,4,4,4,128]{4,2,3,1,0:T(4,128)S(1)}, f32[1,4,4,4,128]{4,2,3,1,0:T(4,128)S(1)}, u32[]{:S(2)}, u32[]{:S(2)}) collective-permute-start(f32[1,4,4,4,128]{4,2,3,1,0:T(4,128)S(1)} %get-tuple-element.17), channel_id=1, source_target_pairs={{0,8},{8,16},{16,24},{24,0},{1,9},{9,17},{17,25},{25,1},{2,10},{10... | collective-permute-start | bytes 98312 | tf_op jit(solution)/shard_map/ppermute | solution.py:24
  68.0 5.9 %collective-permute-start.23 = (f32[4,4,1,4,128]{4,2,3,1,0:T(1,128)S(1)}, f32[4,4,1,4,128]{4,2,3,1,0:T(1,128)S(1)}, u32[]{:S(2)}, u32[]{:S(2)}) collective-permute-start(f32[4,4,1,4,128]{4,2,3,1,0:T(1,128)S(1)} %get-tuple-element.15), channel_id=1, source_target_pairs={{0,3},{1,0},{2,1},{3,2},{4,7},{5,4},{6,5},{7,6},{8,11},{9,8},{10,9... | collective-permute-start | bytes 98312 | tf_op jit(solution)/shard_map/ppermute | solution.py:24
  69.0 0.9 %copy-start.2 = (f32[8,8,1,4,128]{4,2,3,1,0:T(1,128)S(1)}, f32[8,8,1,4,128]{4,2,3,1,0:T(1,128)}, u32[]{:S(2)}) copy-start(f32[8,8,1,4,128]{4,2,3,1,0:T(1,128)} %copy-done.1) | copy-start | bytes 393220
  73.0 0.9 %copy-start.4 = (f32[1,8,8,4,128]{4,2,3,1,0:T(8,128)S(1)}, f32[1,8,8,4,128]{4,2,3,1,0:T(8,128)}, u32[]{:S(2)}) copy-start(f32[1,8,8,4,128]{4,2,3,1,0:T(8,128)} %copy-done.3) | copy-start | bytes 393220

commit v10 on v9

--- a/solution.py
+++ b/solution.py
@@ -175,23 +175,59 @@
 
 
 def coarse_solve(rhs_two, tiles):
-    extended = rhs_two
-    starts = []
-    extended, start, tiles_by_step = extend_axis(extended, "gx", 0, COARSE_HALO, tiles)
-    starts.append(start)
-    extended, joint_starts = extend_joint(extended, ("gy", "gz"), (1, 2), COARSE_HALO)
-    starts.extend(joint_starts)
-    grid = extended.shape[:3]
-    orbs = extended.shape[3:]
-    operator = jnp.asarray(coarse_matrix(grid, tuple(starts), rhs_two.shape[:3]))
-    flat = extended.reshape((-1,) + (int(np.prod(orbs)),))
-    post = jnp.dot(operator, flat, precision=lax.Precision.HIGHEST, preferred_element_type=jnp.float32)
-    return post.reshape(tuple(size + 2 for size in rhs_two.shape[:3]) + orbs), tiles_by_step
-
-
-def coarse_matrix(grid, starts, block):
+    block = rhs_two.shape[:3]
+    orbs = rhs_two.shape[3:]
+    width = int(np.prod(orbs))
+    rows = rhs_two.reshape(-1, width)
+    tile_rows = tiles.reshape(-1, width)
+    count_x = lax.axis_size("gx")
+    offsets_x, start_x = axis_offsets(count_x, block[0], COARSE_HALO)
+    cache = {}
+    tiles_by_step = {0: tiles}
+    for offset in offsets_x:
+        step = offset % count_x
+        if step in cache:
+            continue
+        if step == 0:
+            cache[step] = rows
+            continue
+        both = shifted(jnp.concatenate([rows, tile_rows], axis=0), "gx", step)
+        cache[step] = both[: rows.shape[0]]
+        tiles_by_step[step] = both[rows.shape[0] :].reshape(tiles.shape)
+    line = jnp.concatenate([cache[offset % count_x] for offset in offsets_x], axis=0)
+    axes = ("gy", "gz")
+    counts = [lax.axis_size(axis) for axis in axes]
+    plans = [axis_offsets(count, block[dim], COARSE_HALO) for count, dim in zip(counts, (1, 2))]
+    moved = {}
+    pieces = []
+    for offset_y in plans[0][0]:
+        for offset_z in plans[1][0]:
+            steps = (offset_y % counts[0], offset_z % counts[1])
+            if steps not in moved:
+                if steps == (0, 0):
+                    moved[steps] = line
+                else:
+                    pairs = []
+                    for target in range(counts[0] * counts[1]):
+                        ty, tz = divmod(target, counts[1])
+                        source = ((ty + steps[0]) % counts[0]) * counts[1] + (tz + steps[1]) % counts[1]
+                        pairs.append((source, target))
+                    moved[steps] = lax.ppermute(line, axes, pairs)
+            pieces.append(moved[steps])
+    gathered = jnp.concatenate(pieces, axis=0)
+    operator = coarse_matrix(
+        block, (offsets_x, plans[0][0], plans[1][0]), (start_x, plans[0][1], plans[1][1])
+    )
+    post = jnp.dot(
+        jnp.asarray(operator), gathered, precision=lax.Precision.HIGHEST, preferred_element_type=jnp.float32
+    )
+    return post.reshape(tuple(2 * size + 2 for size in block) + orbs), tiles_by_step
+
+
+def coarse_matrix(block, offsets, starts):
+    grid = tuple(len(offs) * size for offs, size in zip(offsets, block))
     cells = int(np.prod(grid))
-    field = np.eye(cells).reshape(tuple(grid) + (cells,))
+    field = np.eye(cells).reshape(grid + (cells,))
 
     def apply(v, level_id):
         center, coupling = level_coeffs(level_id)
@@ -218,10 +254,29 @@
         correct = correct + omega * (current - apply(correct, top_level)) / center_top
     updated = correct_two + grow(correct)
     post = updated + omega * (field - apply(updated, level_two)) / center
-    for dim, start in enumerate(starts):
-        index = [(start - 1 + k) % grid[dim] for k in range(block[dim] + 2)]
+    padded = [2 * size + 2 for size in block]
+    for dim in range(3):
+        index = [(starts[dim] + (p - 1) // 2) % grid[dim] for p in range(padded[dim])]
         post = np.take(post, index, axis=dim)
-    return post.reshape(-1, cells).astype(np.float32)
+    rim = np.zeros(padded, np.int32)
+    for dim in range(3):
+        edge = np.zeros(padded[dim], np.int32)
+        edge[0] = edge[-1] = 1
+        rim = rim + edge.reshape([-1 if d == dim else 1 for d in range(3)])
+    post = post * (rim <= 1)[..., None]
+    order = []
+    for iy in range(len(offsets[1])):
+        for iz in range(len(offsets[2])):
+            for ix in range(len(offsets[0])):
+                for lx in range(block[0]):
+                    for ly in range(block[1]):
+                        for lz in range(block[2]):
+                            x = ix * block[0] + lx
+                            y = iy * block[1] + ly
+                            z = iz * block[2] + lz
+                            order.append((x * grid[1] + y) * grid[2] + z)
+    post = post.reshape(-1, cells)[:, np.array(order)]
+    return post.astype(np.float32)
 
 
 def prolong_face(face, dim):
@@ -295,11 +350,11 @@
     corr_one = omega * rhs_one / center
     padded_one = pad_with(corr_one, all_faces(corr_one))
     rhs_two = restrict(rhs_one - padded_stencil(padded_one, 1))
-    post_two, tiles_by_step = coarse_solve(rhs_two, inv_tiles)
-    inner_two = post_two[1:-1, 1:-1, 1:-1]
-    post_one = post_smooth_padded(
-        1, padded_one, rhs_one, inner_two, [coarse_faces(post_two, dim) for dim in range(3)]
-    )
+    coarse_padded, tiles_by_step = coarse_solve(rhs_two, inv_tiles)
+    center, coupling = level_coeffs(1)
+    updated_padded = padded_one + coarse_padded
+    updated = updated_padded[1:-1, 1:-1, 1:-1]
+    post_one = updated + omega * (rhs_one - padded_stencil(updated_padded, 1)) / center
     return post_smooth(0, corr_zero, faces_zero, rhs_zero, post_one, all_faces(post_one)), tiles_by_step
 
 

time: 78.6 us -> 93.9 us (1.19)
  matrix products: 2.24 us -> 13.8 us
  starting transfers between devices: 26.2 us -> 29.3 us
  local copies, waits for them, and re-layouts: 21.1 us -> 23.6 us
  other arithmetic: 8.99 us -> 7.79 us
    dot_general x1 -> x11, matrix products: 0.43 us -> 12 us  [coarse_solve(): jnp.dot(jnp.asarray(operator), gathered, precision=lax.Precision.HIGHEST,...]
    slice x14 -> x6, local copies, waits for them, and re-layouts: 8.38 us -> 3.55 us  [the longest x3 3.54 us: coarse_solve(): tiles_by_step[step] = both[rows.shape[0]:].reshape(tiles.shape)]
    another operation x0 -> x3, local copies, waits for them, and re-layouts: none -> 4.38 us  [gram_matrix(): total = lax.dynamic_update_slice(total, piece[slot], (row, col))]
    ppermute x15, starting transfers between devices: 14 us -> 16.8 us  [shifted(): lax.ppermute(block, axis, [(j, (j - step) % count) for j in range(count)])]
    dynamic_update_slice x4, local copies, waits for them, and re-layouts: 2.55 us -> 4.99 us  [gram_matrix(): total = lax.dynamic_update_slice(total, piece[slot], (row, col))]
    ppermute x7, waiting for transfers between devices: 1.79 us -> 0.02 us  [coarse_solve(): moved[steps] = lax.ppermute(line, axes, pairs)]
    ppermute x15, waiting for transfers between devices: 10.6 us -> 12.2 us  [shifted(): lax.ppermute(block, axis, [(j, (j - step) % count) for j in range(count)])]
    unnamed x42 -> x70, local copies, waits for them, and re-layouts: 6.91 us -> 7.45 us
  transfers between devices with their start and end apart: 25 -> 25, of which waited for: 7 -> 5; matrix products, arithmetic and copies ran while one was open for 10% -> 27% of each run, Pallas kernels for 0% -> 0%
where the time goes in v10:
time: 93.9 us; the launch traced here: 92.9 us
  starting transfers between devices  29.3 us (31%)
  local copies, waits for them, and re-layouts  23.6 us (25%)
  matrix products  13.8 us (15%)
  waiting for transfers between devices  12.2 us (13%)
  other arithmetic  7.79 us (8%)
  between operations  6.11 us (7%)
    ppermute x15, starting transfers between devices, shifted(): lax.ppermute(block, axis, [(j, (j - step) % count) for j in range(count)])  16.8 us
    ppermute x15, waiting for transfers between devices, shifted(): lax.ppermute(block, axis, [(j, (j - step) % count) for j in range(count)])  12.2 us
    dot_general x11, matrix products, coarse_solve(): jnp.dot(jnp.asarray(operator), gathered, precision=lax.Precision.HIGHEST,...  12 us
    ppermute x7, starting transfers between devices, coarse_solve(): moved[steps] = lax.ppermute(line, axes, pairs)  7.71 us
    unnamed x70, local copies, waits for them, and re-layouts  7.45 us
    dynamic_update_slice x4, local copies, waits for them, and re-layouts, gram_matrix(): total = lax.dynamic_update_slice(total, piece[slot], (row, col))  4.99 us
    ppermute x3, starting transfers between devices, axis_faces(): lax.ppermute(jnp.concatenate([first, last], axis=dim), axis, [(0, 1), (1,...  4.75 us
    another operation x3, local copies, waits for them, and re-layouts, gram_matrix(): total = lax.dynamic_update_slice(total, piece[slot], (row, col))  4.38 us
  transfers between devices with their start and end apart: 25, of which 5 were waited for; matrix products, arithmetic and copies ran while one was open for 27% of the time, Pallas kernels for 0%

profile of v10, /device:TPU:0, one launch (start us, length us, event | category | flops | bytes accessed | tf_op | source)
XLA Modules:
  0.0 92.9 jit_solution(17291611564913108152)
XLA Ops:
  0.0 1.6 %fusion.44 = (f32[8,8,1,4,128]{4,2,3,1,0:T(1,128)S(1)}, f32[8,8,1,4,128]{4,2,3,1,0:T(1,128)S(1)}) fusion(bf16[8,8,8,4,128]{4,2,3,1,0:T(8,128)(2,1)} %bitcast.84), kind=kLoop, calls=%fused_computation.118 | loop fusion | flops 131072 | bytes 393216 | tf_op jit(solution)/shard_map/div | solution.py:345
  2.2 2.6 %collective-permute-start.2 = (f32[8,2,8,4,128]{4,2,3,1,0:T(8,128)S(1)}, f32[8,2,8,4,128]{4,2,3,1,0:T(8,128)S(1)}, u32[]{:S(2)}, u32[]{:S(2)}) collective-permute-start(f32[8,2,8,4,128]{4,2,3,1,0:T(8,128)S(1)} %pad_maximum_fusion.32), channel_id=1, source_target_pairs={{0,4},{4,0},{1,5},{5,1},{2,6},{6,2},{3,7},{7,3},{8,12},{12,8},{9,1... | collective-permute-start | bytes 786440 | tf_op jit(solution)/shard_map/ppermute | solution.py:37
  4.8 3.7 %collective-permute-start = (f32[1,8,8,4,128]{4,2,3,1,0:T(8,128)S(1)}, f32[1,8,8,4,128]{4,2,3,1,0:T(8,128)S(1)}, u32[]{:S(2)}, u32[]{:S(2)}) collective-permute-start(f32[1,8,8,4,128]{4,2,3,1,0:T(8,128)S(1)} %get-tuple-element.8), channel_id=1, source_target_pairs={{0,24},{8,0},{16,8},{24,16},{1,25},{9,1},{17,9},{25,17},{2,26},{10... | collective-permute-start | bytes 393224 | tf_op jit(solution)/shard_map/ppermute | solution.py:24
  8.5 1.2 %collective-permute-start.3 = (f32[8,8,1,4,128]{4,2,3,1,0:T(1,128)S(1)}, f32[8,8,1,4,128]{4,2,3,1,0:T(1,128)S(1)}, u32[]{:S(2)}, u32[]{:S(2)}) collective-permute-start(f32[8,8,1,4,128]{4,2,3,1,0:T(1,128)S(1)} %get-tuple-element.5), channel_id=1, source_target_pairs={{0,3},{1,0},{2,1},{3,2},{4,7},{5,4},{6,5},{7,6},{8,11},{9,8},{10,9... | collective-permute-start | bytes 393224 | tf_op jit(solution)/shard_map/ppermute | solution.py:24
  9.6 0.7 copy-done.32
  10.3 0.7 constant_dynamic-slice_fusion
  16.1 0.7 copy-done.33
  17.5 0.8 copy-done.1
  18.5 1.0 %convert_subtract_fusion.1 = f32[8,8,8,4,128]{4,2,3,1,0:T(8,128)S(1)} fusion(f32[8,8,1,4,128]{4,2,3,1,0:T(1,128)S(1)} %collective-permute-done.4, f32[10,1,8,4,128]{4,2,3,1,0:T(8,128)S(1)} %pad.40, f32[10,1,8,4,128]{4,2,3,1,0:T(8,128)S(1)} %pad.41, f32[1,8,8,4,128]{4,2,3,1,0:T(8,128)S(1)} %collective-permute-done, ...), kind=kLoop, calls=%fused_computation.1 | loop fusion | flops 8912896 | bytes 3473408 | tf_op jit(solution)/shard_map/sub | solution.py:348
  19.5 0.7 reduce_sum.18
  21.5 3.9 %collective-permute-start.8 = (f32[1,4,4,4,128]{4,2,3,1,0:T(4,128)S(1)}, f32[1,4,4,4,128]{4,2,3,1,0:T(4,128)S(1)}, u32[]{:S(2)}, u32[]{:S(2)}) collective-permute-start(f32[1,4,4,4,128]{4,2,3,1,0:T(4,128)S(1)} %get-tuple-element.24), channel_id=1, source_target_pairs={{0,24},{8,0},{16,8},{24,16},{1,25},{9,1},{17,9},{25,17},{2,26},{10... | collective-permute-start | bytes 98312 | tf_op jit(solution)/shard_map/ppermute | solution.py:24
  25.5 1.6 %collective-permute-done.8 = f32[1,4,4,4,128]{4,2,3,1,0:T(4,128)S(1)} collective-permute-done((f32[1,4,4,4,128]{4,2,3,1,0:T(4,128)S(1)}, f32[1,4,4,4,128]{4,2,3,1,0:T(4,128)S(1)}, u32[]{:S(2)}, u32[]{:S(2)}) %collective-permute-start.8) | collective-permute-done | bytes 32800 | tf_op jit(solution)/shard_map/ppermute | solution.py:24
  27.1 3.9 %collective-permute-done.7 = f32[1,4,4,4,128]{4,2,3,1,0:T(4,128)S(1)} collective-permute-done((f32[1,4,4,4,128]{4,2,3,1,0:T(4,128)S(1)}, f32[1,4,4,4,128]{4,2,3,1,0:T(4,128)S(1)}, u32[]{:S(2)}, u32[]{:S(2)}) %collective-permute-start.7) | collective-permute-done | bytes 32800 | tf_op jit(solution)/shard_map/ppermute | solution.py:24
  31.9 0.9 collective-permute-start.11
  32.8 2.9 %collective-permute-start.10 = (f32[40,512]{1,0:T(8,128)S(1)}, f32[40,512]{1,0:T(8,128)S(1)}, u32[]{:S(2)}, u32[]{:S(2)}) collective-permute-start(f32[40,512]{1,0:T(8,128)S(1)} %constant_dynamic-update-slice_fusion), channel_id=1, source_target_pairs={{0,24},{8,0},{16,8},{24,16},{1,25},{9,1},{17,9},{25,17},{2,26},{10... | collective-permute-start | bytes 245768 | tf_op jit(solution)/shard_map/ppermute | solution.py:24
  36.2 2.8 %collective-permute-done.12 = f32[40,512]{1,0:T(8,128)S(1)} collective-permute-done((f32[40,512]{1,0:T(8,128)S(1)}, f32[40,512]{1,0:T(8,128)S(1)}, u32[]{:S(2)}, u32[]{:S(2)}) %collective-permute-start.12) | collective-permute-done | bytes 81952 | tf_op jit(solution)/shard_map/ppermute | solution.py:24
  39.0 1.9 %collective-permute-done.11 = f32[40,512]{1,0:T(8,128)S(1)} collective-permute-done((f32[40,512]{1,0:T(8,128)S(1)}, f32[40,512]{1,0:T(8,128)S(1)}, u32[]{:S(2)}, u32[]{:S(2)}) %collective-permute-start.11) | collective-permute-done | bytes 81952 | tf_op jit(solution)/shard_map/ppermute | solution.py:24
  41.6 2.8 %collective-permute-start.18 = (f32[32,512]{1,0:T(8,128)}, f32[32,512]{1,0:T(8,128)}, u32[]{:S(2)}, u32[]{:S(2)}) collective-permute-start(f32[32,512]{1,0:T(8,128)} %pad_maximum_fusion.52), channel_id=1, source_target_pairs={{6,0},{7,1},{4,2},{5,3},{2,4},{3,5},{0,6},{1,7},{14,8},{15,9},{12,... | collective-permute-start | bytes 196616 | tf_op jit(solution)/shard_map/ppermute | solution.py:215
  44.4 2.3 %collective-permute-start.17 = (f32[32,512]{1,0:T(8,128)}, f32[32,512]{1,0:T(8,128)}, u32[]{:S(2)}, u32[]{:S(2)}) collective-permute-start(f32[32,512]{1,0:T(8,128)} %pad_maximum_fusion.52), channel_id=1, source_target_pairs={{5,0},{6,1},{7,2},{4,3},{1,4},{2,5},{3,6},{0,7},{13,8},{14,9},{15,... | collective-permute-start | bytes 196616 | tf_op jit(solution)/shard_map/ppermute | solution.py:215
  47.2 1.2 %convolution_add_fusion.1 = f32[512,216]{0,1:T(8,128)} fusion(f32[512,216]{0,1:T(8,128)S(1)} %fusion.49, f32[216,8]{1,0:T(8,128)S(1)} %copy-done.30, f32[40,512]{1,0:T(8,128)S(1)} %collective-permute-done.10), kind=kOutput, calls=%fused_computation.6 | convolution fusion | flops 10727424 | bytes 1011712 | tf_op jit(solution)/shard_map/dot_general | solution.py:221
  49.6 1.5 %squeeze_reshape.9 = f32[128,128]{1,0:T(8,128)} reshape(f32[32,512]{1,0:T(8,128)} %slice.329) | data formatting | bytes 131072 | tf_op jit(solution)/shard_map/squeeze;reshape | solution.py:339
  51.0 1.5 %slice.330 = f32[32,512]{1,0:T(8,128)} slice(f32[40,512]{1,0:T(8,128)} %copy-done.20), slice={[8:40], [0:512]} | slice | bytes 131072 | tf_op jit(solution)/shard_map/slice | solution.py:196
  52.5 1.5 %squeeze_reshape.10 = f32[128,128]{1,0:T(8,128)} reshape(f32[32,512]{1,0:T(8,128)} %slice.330) | data formatting | bytes 131072 | tf_op jit(solution)/shard_map/squeeze;reshape | solution.py:339
  53.9 1.5 %slice.331 = f32[32,512]{1,0:T(8,128)} slice(f32[40,512]{1,0:T(8,128)} %copy-done.19), slice={[8:40], [0:512]} | slice | bytes 131072 | tf_op jit(solution)/shard_map/slice | solution.py:196
  55.4 1.5 %squeeze_reshape.11 = f32[128,128]{1,0:T(8,128)} reshape(f32[32,512]{1,0:T(8,128)} %slice.331) | data formatting | bytes 131072 | tf_op jit(solution)/shard_map/squeeze;reshape | solution.py:339
  56.9 2.4 %dynamic_update_slice.13 = f32[512,512]{1,0:T(8,128)S(1)} dynamic-update-slice(f32[512,512]{1,0:T(8,128)S(1)} %copy-done.2, f32[128,128]{1,0:T(8,128)} %squeeze_reshape.9, s32[]{:T(128)S(6)} %select_n.65, s32[]{:T(128)S(6)} %select_n.66) | dynamic-update-slice | bytes 131076 | tf_op jit(solution)/shard_map/dynamic_update_slice | solution.py:339
  59.3 0.9 dynamic_update_slice.14
  60.2 1.7 %dynamic_update_slice.15 = f32[512,512]{1,0:T(8,128)S(1)} dynamic-update-slice(f32[512,512]{1,0:T(8,128)S(1)} %dynamic_update_slice.14, f32[128,128]{1,0:T(8,128)S(1)} %copy-done.16, s32[]{:T(128)S(6)} %select_n.73, s32[]{:T(128)S(6)} %select_n.74) | dynamic-update-slice | bytes 131076 | tf_op jit(solution)/shard_map/dynamic_update_slice | solution.py:339
  62.3 1.3 %fusion.65 = f32[512,216]{0,1:T(8,128)S(1)} fusion(f32[32,512]{1,0:T(8,128)} %collective-permute-done.19, f32[216,32]{1,0:T(8,128)S(1)} %copy-done.27), kind=kOutput, calls=%fused_computation.171 | convolution fusion | flops 42467328 | bytes 535552 | tf_op jit(solution)/shard_map/dot_general | solution.py:221
  63.7 1.7 %collective-permute-start.13 = (f32[32,512]{1,0:T(8,128)}, f32[32,512]{1,0:T(8,128)S(1)}, u32[]{:S(2)}, u32[]{:S(2)}) collective-permute-start(f32[32,512]{1,0:T(8,128)} %pad_maximum_fusion.52), channel_id=1, source_target_pairs={{1,0},{2,1},{3,2},{0,3},{5,4},{6,5},{7,6},{4,7},{9,8},{10,9},{11,1... | collective-permute-start | bytes 196616 | tf_op jit(solution)/shard_map/ppermute | solution.py:215
  65.4 1.3 %fusion.64 = f32[512,216]{0,1:T(8,128)S(1)} fusion(f32[32,512]{1,0:T(8,128)} %collective-permute-done.18, f32[216,32]{1,0:T(8,128)S(1)} %copy-done.26), kind=kOutput, calls=%fused_computation.170 | convolution fusion | flops 42467328 | bytes 535552 | tf_op jit(solution)/shard_map/dot_general | solution.py:221
  66.8 1.4 %fusion.63 = f32[512,216]{0,1:T(8,128)S(1)} fusion(f32[32,512]{1,0:T(8,128)} %collective-permute-done.17, f32[216,32]{1,0:T(8,128)S(1)} %copy-done.25), kind=kOutput, calls=%fused_computation.169 | convolution fusion | flops 42467328 | bytes 535552 | tf_op jit(solution)/shard_map/dot_general | solution.py:221
  68.2 1.4 %fusion.62 = f32[512,216]{0,1:T(8,128)S(1)} fusion(f32[32,512]{1,0:T(8,128)} %collective-permute-done.16, f32[216,32]{1,0:T(8,128)S(1)} %copy-done.24), kind=kOutput, calls=%fused_computation.168 | convolution fusion | flops 42467328 | bytes 535552 | tf_op jit(solution)/shard_map/dot_general | solution.py:221
  69.6 1.4 %fusion.61 = f32[512,216]{0,1:T(8,128)S(1)} fusion(f32[32,512]{1,0:T(8,128)} %collective-permute-done.15, f32[216,32]{1,0:T(8,128)S(1)} %copy-done.23), kind=kOutput, calls=%fused_computation.167 | convolution fusion | flops 42467328 | bytes 535552 | tf_op jit(solution)/shard_map/dot_general | solution.py:221
  72.5 2.1 %fusion.8 = f32[216,512]{1,0:T(8,128)} fusion(f32[512,216]{0,1:T(8,128)S(1)} %fusion.65, f32[512,216]{0,1:T(8,128)S(1)} %fusion.64, f32[512,216]{0,1:T(8,128)S(1)} %fusion.63, f32[512,216]{0,1:T(8,128)S(1)} %fusion.62, f32[512,216]{0,1:T(8,128)S(1)} %fusion.61, f32[512,216]{0,1:T(8,128)S(1)} %fusion.60, f32[512,216]{0,1:T(8,128)S(1)} %fusion.59, ...), kind=kOutput, calls=%fused_computation.15 | convolution fusion | flops 11612160 | bytes 4446976 | tf_op jit(solution)/shard_map/dot_general | solution.py:221
  74.6 1.2 %reshape.357 = f32[6,6,6,4,128]{4,3,2,1,0:T(4,128)S(1)} reshape(f32[216,512]{1,0:T(8,128)} %fusion.8) | data formatting | bytes 884736 | tf_op jit(solution)/shard_map/reshape | solution.py:224
  75.8 1.1 %maximum_add_fusion = f32[6,6,6,4,128]{4,2,3,1,0:T(8,128)S(1)} fusion(f32[6,6,1,4,128]{4,2,3,1,0:T(1,128)S(1)} %pad.47, f32[6,1,4,4,128]{4,2,3,1,0:T(4,128)S(1)} %pad.46, f32[1,4,4,4,128]{4,2,3,1,0:T(4,128)S(1)} %collective-permute-done.8, f32[4,4,4,4,128]{4,2,3,1,0:T(4,128)S(1)} %broadcast_multiply_fusion.2, f32[1,4,4,4,128]{4,2,3,1,0:T(4,128)} %copy-done.18, ...), kind=kLoop, calls=%fused_computation.75 | loop fusion | flops 774144 | bytes 1327104 | tf_op jit(solution)/shard_map/add | solution.py:355
  77.3 1.6 %collective-permute-start.22 = (f32[4,2,4,4,128]{4,2,3,1,0:T(4,128)S(1)}, f32[4,2,4,4,128]{4,2,3,1,0:T(4,128)S(1)}, u32[]{:S(2)}, u32[]{:S(2)}) collective-permute-start(f32[4,2,4,4,128]{4,2,3,1,0:T(4,128)S(1)} %pad_maximum_fusion.53), channel_id=1, source_target_pairs={{0,4},{4,0},{1,5},{5,1},{2,6},{6,2},{3,7},{7,3},{8,12},{12,8},{9,1... | collective-permute-start | bytes 196616 | tf_op jit(solution)/shard_map/ppermute | solution.py:37
  78.8 2.0 %collective-permute-start.20 = (f32[1,4,4,4,128]{4,2,3,1,0:T(4,128)S(1)}, f32[1,4,4,4,128]{4,2,3,1,0:T(4,128)S(1)}, u32[]{:S(2)}, u32[]{:S(2)}) collective-permute-start(f32[1,4,4,4,128]{4,2,3,1,0:T(4,128)S(1)} %get-tuple-element.18), channel_id=1, source_target_pairs={{0,24},{8,0},{16,8},{24,16},{1,25},{9,1},{17,9},{25,17},{2,26},{10... | collective-permute-start | bytes 98312 | tf_op jit(solution)/shard_map/ppermute | solution.py:24
  80.9 1.0 %collective-permute-start.23 = (f32[4,4,1,4,128]{4,2,3,1,0:T(1,128)S(1)}, f32[4,4,1,4,128]{4,2,3,1,0:T(1,128)S(1)}, u32[]{:S(2)}, u32[]{:S(2)}) collective-permute-start(f32[4,4,1,4,128]{4,2,3,1,0:T(1,128)S(1)} %get-tuple-element.15), channel_id=1, source_target_pairs={{0,3},{1,0},{2,1},{3,2},{4,7},{5,4},{6,5},{7,6},{8,11},{9,8},{10,9... | collective-permute-start | bytes 98312 | tf_op jit(solution)/shard_map/ppermute | solution.py:24
  82.9 0.8 copy-done.9
  84.0 0.8 copy-done.13
  84.8 1.9 %collective-permute-done.21 = f32[1,4,4,4,128]{4,2,3,1,0:T(4,128)S(1)} collective-permute-done((f32[1,4,4,4,128]{4,2,3,1,0:T(4,128)S(1)}, f32[1,4,4,4,128]{4,2,3,1,0:T(4,128)S(1)}, u32[]{:S(2)}, u32[]{:S(2)}) %collective-permute-start.21) | collective-permute-done | bytes 32800 | tf_op jit(solution)/shard_map/ppermute | solution.py:24
  86.8 0.8 copy-done.11
  87.7 0.8 copy-done.7
  88.9 0.8 copy-done.5
  89.8 1.0 %fusion.11 = f32[8,8,8,4,128]{4,2,3,1,0:T(8,128)S(1)} fusion(f32[8,8,8,4,128]{4,2,3,1,0:T(8,128)S(1)} %fusion.29, f32[8,8,1,4,128]{4,2,3,1,0:T(1,128)S(1)} %add.236, f32[10,1,8,4,128]{4,2,3,1,0:T(8,128)S(1)} %pad.48, f32[10,1,8,4,128]{4,2,3,1,0:T(8,128)S(1)} %pad.49, f32[1,8,8,4,128]{4,2,3,1,0:T(8,128)S(1)} %add.227, f32[1,8,8,4,128]{4,2,3,1,0:T(8,128)S(1)} %add.228, ...), kind=kLoop, calls=%fused_computation.18 | loop fusion | flops 9437184 | bytes 3473408 | tf_op jit(solution)/shard_map/add | solution.py:308
  91.0 1.8 %convolution_convert_fusion = bf16[512,512]{1,0:T(8,128)(2,1)} fusion(f32[512,512]{1,0:T(8,128)S(1)} %bitcast_multiply_fusion, f32[512,512]{1,0:T(8,128)S(1)} %dynamic_update_slice.15), kind=kOutput, calls=%fused_computation.4 | convolution fusion | flops 805568512 | bytes 2621440 | tf_op jit(solution)/shard_map/dot_general | solution.py:376
  (166 shorter events, 10.3 us)
Async XLA Ops:
  0.0 2.1 %copy-start = (bf16[8,8,8,512]{3,2,1,0:T(8,128)(2,1)S(1)}, bf16[8,8,8,512]{3,2,1,0:T(8,128)(2,1)}, u32[]{:S(2)}) copy-start(bf16[8,8,8,512]{3,2,1,0:T(8,128)(2,1)} %param.5) | copy-start | bytes 1572868
  1.6 16.8 %collective-permute-start.4 = (f32[8,8,1,4,128]{4,2,3,1,0:T(1,128)S(1)}, f32[8,8,1,4,128]{4,2,3,1,0:T(1,128)S(1)}, u32[]{:S(2)}, u32[]{:S(2)}) collective-permute-start(f32[8,8,1,4,128]{4,2,3,1,0:T(1,128)S(1)} %get-tuple-element.6), channel_id=1, source_target_pairs={{0,1},{1,2},{2,3},{3,0},{4,5},{5,6},{6,7},{7,4},{8,9},{9,10},{10,1... | collective-permute-start | bytes 393224 | tf_op jit(solution)/shard_map/ppermute | solution.py:24
  2.2 15.3 %collective-permute-start.2 = (f32[8,2,8,4,128]{4,2,3,1,0:T(8,128)S(1)}, f32[8,2,8,4,128]{4,2,3,1,0:T(8,128)S(1)}, u32[]{:S(2)}, u32[]{:S(2)}) collective-permute-start(f32[8,2,8,4,128]{4,2,3,1,0:T(8,128)S(1)} %pad_maximum_fusion.32), channel_id=1, source_target_pairs={{0,4},{4,0},{1,5},{5,1},{2,6},{6,2},{3,7},{7,3},{8,12},{12,8},{9,1... | collective-permute-start | bytes 786440 | tf_op jit(solution)/shard_map/ppermute | solution.py:37
  4.8 13.6 %collective-permute-start = (f32[1,8,8,4,128]{4,2,3,1,0:T(8,128)S(1)}, f32[1,8,8,4,128]{4,2,3,1,0:T(8,128)S(1)}, u32[]{:S(2)}, u32[]{:S(2)}) collective-permute-start(f32[1,8,8,4,128]{4,2,3,1,0:T(8,128)S(1)} %get-tuple-element.8), channel_id=1, source_target_pairs={{0,24},{8,0},{16,8},{24,16},{1,25},{9,1},{17,9},{25,17},{2,26},{10... | collective-permute-start | bytes 393224 | tf_op jit(solution)/shard_map/ppermute | solution.py:24
  8.5 10.0 %collective-permute-start.1 = (f32[1,8,8,4,128]{4,2,3,1,0:T(8,128)S(1)}, f32[1,8,8,4,128]{4,2,3,1,0:T(8,128)S(1)}, u32[]{:S(2)}, u32[]{:S(2)}) collective-permute-start(f32[1,8,8,4,128]{4,2,3,1,0:T(8,128)S(1)} %get-tuple-element.7), channel_id=1, source_target_pairs={{0,8},{8,16},{16,24},{24,0},{1,9},{9,17},{17,25},{25,1},{2,10},{10... | collective-permute-start | bytes 393224 | tf_op jit(solution)/shard_map/ppermute | solution.py:24
  8.5 10.0 %collective-permute-start.3 = (f32[8,8,1,4,128]{4,2,3,1,0:T(1,128)S(1)}, f32[8,8,1,4,128]{4,2,3,1,0:T(1,128)S(1)}, u32[]{:S(2)}, u32[]{:S(2)}) collective-permute-start(f32[8,8,1,4,128]{4,2,3,1,0:T(1,128)S(1)} %get-tuple-element.5), channel_id=1, source_target_pairs={{0,3},{1,0},{2,1},{3,2},{4,7},{5,4},{6,5},{7,6},{8,11},{9,8},{10,9... | collective-permute-start | bytes 393224 | tf_op jit(solution)/shard_map/ppermute | solution.py:24
  9.6 6.4 %copy-start.15 = (f32[1,128,128]{2,1,0:T(8,128)S(1)}, f32[1,128,128]{2,1,0:T(8,128)}, u32[]{:S(2)}) copy-start(f32[1,128,128]{2,1,0:T(8,128)} %param.8) | copy-start | bytes 196612
  17.3 1.0 %copy-start.1 = (f32[512,512]{1,0:T(8,128)}, f32[512,512]{1,0:T(8,128)S(1)}, u32[]{:S(2)}) copy-start(f32[512,512]{1,0:T(8,128)S(1)} %bitcast_dynamic-update-slice_fusion) | copy-start | bytes 3145732
  18.4 1.0 %copy-start.8 = (f32[8,8,1,4,128]{4,2,3,1,0:T(1,128)}, f32[8,8,1,4,128]{4,2,3,1,0:T(1,128)S(1)}, u32[]{:S(2)}) copy-start(f32[8,8,1,4,128]{4,2,3,1,0:T(1,128)S(1)} %collective-permute-done.4) | copy-start | bytes 393220
  18.5 1.0 %copy-start.12 = (f32[1,8,8,4,128]{4,2,3,1,0:T(8,128)}, f32[1,8,8,4,128]{4,2,3,1,0:T(8,128)S(1)}, u32[]{:S(2)}) copy-start(f32[1,8,8,4,128]{4,2,3,1,0:T(8,128)S(1)} %collective-permute-done) | copy-start | bytes 393220
  18.5 1.0 %copy-start.10 = (f32[1,8,8,4,128]{4,2,3,1,0:T(8,128)}, f32[1,8,8,4,128]{4,2,3,1,0:T(8,128)S(1)}, u32[]{:S(2)}) copy-start(f32[1,8,8,4,128]{4,2,3,1,0:T(8,128)S(1)} %collective-permute-done.1) | copy-start | bytes 393220
  18.5 1.0 %copy-start.6 = (f32[8,8,1,4,128]{4,2,3,1,0:T(1,128)}, f32[8,8,1,4,128]{4,2,3,1,0:T(1,128)S(1)}, u32[]{:S(2)}) copy-start(f32[8,8,1,4,128]{4,2,3,1,0:T(1,128)S(1)} %collective-permute-done.3) | copy-start | bytes 393220
  20.4 5.0 %collective-permute-start.9 = (f32[4,4,1,4,128]{4,2,3,1,0:T(1,128)S(1)}, f32[4,4,1,4,128]{4,2,3,1,0:T(1,128)S(1)}, u32[]{:S(2)}, u32[]{:S(2)}) collective-permute-start(f32[4,4,1,4,128]{4,2,3,1,0:T(1,128)S(1)} %get-tuple-element.22), channel_id=1, source_target_pairs={{0,3},{1,0},{2,1},{3,2},{4,7},{5,4},{6,5},{7,6},{8,11},{9,8},{10,9... | collective-permute-start | bytes 98312 | tf_op jit(solution)/shard_map/ppermute | solution.py:24
  20.9 4.6 %collective-permute-start.6 = (f32[4,2,4,4,128]{4,2,3,1,0:T(4,128)S(1)}, f32[4,2,4,4,128]{4,2,3,1,0:T(4,128)S(1)}, u32[]{:S(2)}, u32[]{:S(2)}) collective-permute-start(f32[4,2,4,4,128]{4,2,3,1,0:T(4,128)S(1)} %pad_maximum_fusion.51), channel_id=1, source_target_pairs={{0,4},{4,0},{1,5},{5,1},{2,6},{6,2},{3,7},{7,3},{8,12},{12,8},{9,1... | collective-permute-start | bytes 196616 | tf_op jit(solution)/shard_map/ppermute | solution.py:37
  21.4 3.9 %collective-permute-start.5 = (f32[4,4,1,4,128]{4,2,3,1,0:T(1,128)S(1)}, f32[4,4,1,4,128]{4,2,3,1,0:T(1,128)S(1)}, u32[]{:S(2)}, u32[]{:S(2)}) collective-permute-start(f32[4,4,1,4,128]{4,2,3,1,0:T(1,128)S(1)} %get-tuple-element.21), channel_id=1, source_target_pairs={{0,1},{1,2},{2,3},{3,0},{4,5},{5,6},{6,7},{7,4},{8,9},{9,10},{10,1... | collective-permute-start | bytes 98312 | tf_op jit(solution)/shard_map/ppermute | solution.py:24
  21.5 5.7 %collective-permute-start.8 = (f32[1,4,4,4,128]{4,2,3,1,0:T(4,128)S(1)}, f32[1,4,4,4,128]{4,2,3,1,0:T(4,128)S(1)}, u32[]{:S(2)}, u32[]{:S(2)}) collective-permute-start(f32[1,4,4,4,128]{4,2,3,1,0:T(4,128)S(1)} %get-tuple-element.24), channel_id=1, source_target_pairs={{0,24},{8,0},{16,8},{24,16},{1,25},{9,1},{17,9},{25,17},{2,26},{10... | collective-permute-start | bytes 98312 | tf_op jit(solution)/shard_map/ppermute | solution.py:24
  25.3 5.7 %collective-permute-start.7 = (f32[1,4,4,4,128]{4,2,3,1,0:T(4,128)S(1)}, f32[1,4,4,4,128]{4,2,3,1,0:T(4,128)S(1)}, u32[]{:S(2)}, u32[]{:S(2)}) collective-permute-start(f32[1,4,4,4,128]{4,2,3,1,0:T(4,128)S(1)} %get-tuple-element.23), channel_id=1, source_target_pairs={{0,8},{8,16},{16,24},{24,0},{1,9},{9,17},{17,25},{25,1},{2,10},{10... | collective-permute-start | bytes 98312 | tf_op jit(solution)/shard_map/ppermute | solution.py:24
  25.5 5.8 %copy-start.14 = (f32[6,1,4,4,128]{4,2,3,1,0:T(4,128)}, f32[6,1,4,4,128]{4,2,3,1,0:T(4,128)S(1)}, u32[]{:S(2)}) copy-start(f32[6,1,4,4,128]{4,2,3,1,0:T(4,128)S(1)} %pad.45) | copy-start | bytes 147460
  31.7 3.9 %copy-start.31 = (f32[216,8]{1,0:T(8,128)S(1)}, f32[216,8]{1,0:T(8,128)}, u32[]{:S(2)}) copy-start(f32[216,8]{1,0:T(8,128)} %constant.137) | copy-start | bytes 20740
  31.8 7.2 %collective-permute-start.12 = (f32[40,512]{1,0:T(8,128)S(1)}, f32[40,512]{1,0:T(8,128)S(1)}, u32[]{:S(2)}, u32[]{:S(2)}) collective-permute-start(f32[40,512]{1,0:T(8,128)S(1)} %constant_dynamic-update-slice_fusion), channel_id=1, source_target_pairs={{0,8},{8,16},{16,24},{24,0},{1,9},{9,17},{17,25},{25,1},{2,10},{10... | collective-permute-start | bytes 245768 | tf_op jit(solution)/shard_map/ppermute | solution.py:24
  31.9 9.1 %collective-permute-start.11 = (f32[40,512]{1,0:T(8,128)S(1)}, f32[40,512]{1,0:T(8,128)S(1)}, u32[]{:S(2)}, u32[]{:S(2)}) collective-permute-start(f32[40,512]{1,0:T(8,128)S(1)} %constant_dynamic-update-slice_fusion), channel_id=1, source_target_pairs={{0,16},{8,24},{16,0},{24,8},{1,17},{9,25},{17,1},{25,9},{2,18},{10... | collective-permute-start | bytes 245768 | tf_op jit(solution)/shard_map/ppermute | solution.py:24
  32.8 8.2 %collective-permute-start.10 = (f32[40,512]{1,0:T(8,128)S(1)}, f32[40,512]{1,0:T(8,128)S(1)}, u32[]{:S(2)}, u32[]{:S(2)}) collective-permute-start(f32[40,512]{1,0:T(8,128)S(1)} %constant_dynamic-update-slice_fusion), channel_id=1, source_target_pairs={{0,24},{8,0},{16,8},{24,16},{1,25},{9,1},{17,9},{25,17},{2,26},{10... | collective-permute-start | bytes 245768 | tf_op jit(solution)/shard_map/ppermute | solution.py:24
  36.2 11.0 %copy-start.30 = (f32[216,8]{1,0:T(8,128)S(1)}, f32[216,8]{1,0:T(8,128)}, u32[]{:S(2)}) copy-start(f32[216,8]{1,0:T(8,128)} %constant.138) | copy-start | bytes 20740
  39.0 9.5 %copy-start.19 = (f32[40,512]{1,0:T(8,128)}, f32[40,512]{1,0:T(8,128)S(1)}, u32[]{:S(2)}) copy-start(f32[40,512]{1,0:T(8,128)S(1)} %collective-permute-done.12) | copy-start | bytes 245764
  41.0 7.5 %copy-start.29 = (f32[216,8]{1,0:T(8,128)S(1)}, f32[216,8]{1,0:T(8,128)}, u32[]{:S(2)}) copy-start(f32[216,8]{1,0:T(8,128)} %constant.140) | copy-start | bytes 20740
  41.6 15.3 %copy-start.2 = (f32[512,512]{1,0:T(8,128)S(1)}, f32[512,512]{1,0:T(8,128)}, u32[]{:S(2)}) copy-start(f32[512,512]{1,0:T(8,128)} %copy-done.1) | copy-start | bytes 3145732
  41.6 20.3 %collective-permute-start.19 = (f32[32,512]{1,0:T(8,128)}, f32[32,512]{1,0:T(8,128)}, u32[]{:S(2)}, u32[]{:S(2)}) collective-permute-start(f32[32,512]{1,0:T(8,128)} %pad_maximum_fusion.52), channel_id=1, source_target_pairs={{7,0},{4,1},{5,2},{6,3},{3,4},{0,5},{1,6},{2,7},{15,8},{12,9},{13,... | collective-permute-start | bytes 196616 | tf_op jit(solution)/shard_map/ppermute | solution.py:215
  41.6 22.1 %collective-permute-start.18 = (f32[32,512]{1,0:T(8,128)}, f32[32,512]{1,0:T(8,128)}, u32[]{:S(2)}, u32[]{:S(2)}) collective-permute-start(f32[32,512]{1,0:T(8,128)} %pad_maximum_fusion.52), channel_id=1, source_target_pairs={{6,0},{7,1},{4,2},{5,3},{2,4},{3,5},{0,6},{1,7},{14,8},{15,9},{12,... | collective-permute-start | bytes 196616 | tf_op jit(solution)/shard_map/ppermute | solution.py:215
  44.4 22.4 %collective-permute-start.17 = (f32[32,512]{1,0:T(8,128)}, f32[32,512]{1,0:T(8,128)}, u32[]{:S(2)}, u32[]{:S(2)}) collective-permute-start(f32[32,512]{1,0:T(8,128)} %pad_maximum_fusion.52), channel_id=1, source_target_pairs={{5,0},{6,1},{7,2},{4,3},{1,4},{2,5},{3,6},{0,7},{13,8},{14,9},{15,... | collective-permute-start | bytes 196616 | tf_op jit(solution)/shard_map/ppermute | solution.py:215
  46.7 21.5 %collective-permute-start.16 = (f32[32,512]{1,0:T(8,128)}, f32[32,512]{1,0:T(8,128)}, u32[]{:S(2)}, u32[]{:S(2)}) collective-permute-start(f32[32,512]{1,0:T(8,128)} %pad_maximum_fusion.52), channel_id=1, source_target_pairs={{4,0},{5,1},{6,2},{7,3},{0,4},{1,5},{2,6},{3,7},{12,8},{13,9},{14,... | collective-permute-start | bytes 196616 | tf_op jit(solution)/shard_map/ppermute | solution.py:215
  47.2 22.4 %collective-permute-start.15 = (f32[32,512]{1,0:T(8,128)}, f32[32,512]{1,0:T(8,128)}, u32[]{:S(2)}, u32[]{:S(2)}) collective-permute-start(f32[32,512]{1,0:T(8,128)} %pad_maximum_fusion.52), channel_id=1, source_target_pairs={{3,0},{0,1},{1,2},{2,3},{7,4},{4,5},{5,6},{6,7},{11,8},{8,9},{9,10... | collective-permute-start | bytes 196616 | tf_op jit(solution)/shard_map/ppermute | solution.py:215
  56.9 2.4 %copy-start.17 = (f32[128,128]{1,0:T(8,128)S(1)}, f32[128,128]{1,0:T(8,128)}, u32[]{:S(2)}) copy-start(f32[128,128]{1,0:T(8,128)} %squeeze_reshape.10) | copy-start | bytes 196612
  59.3 3.0 %copy-start.27 = (f32[216,32]{1,0:T(8,128)S(1)}, f32[216,32]{1,0:T(8,128)}, u32[]{:S(2)}) copy-start(f32[216,32]{1,0:T(8,128)} %constant.147) | copy-start | bytes 82948
  61.9 3.5 %copy-start.26 = (f32[216,32]{1,0:T(8,128)S(1)}, f32[216,32]{1,0:T(8,128)}, u32[]{:S(2)}) copy-start(f32[216,32]{1,0:T(8,128)} %constant.146) | copy-start | bytes 82948
  61.9 9.0 %collective-permute-start.14 = (f32[32,512]{1,0:T(8,128)}, f32[32,512]{1,0:T(8,128)S(1)}, u32[]{:S(2)}, u32[]{:S(2)}) collective-permute-start(f32[32,512]{1,0:T(8,128)} %pad_maximum_fusion.52), channel_id=1, source_target_pairs={{2,0},{3,1},{0,2},{1,3},{6,4},{7,5},{4,6},{5,7},{10,8},{11,9},{8,1... | collective-permute-start | bytes 196616 | tf_op jit(solution)/shard_map/ppermute | solution.py:215
  63.7 3.1 %copy-start.25 = (f32[216,32]{1,0:T(8,128)S(1)}, f32[216,32]{1,0:T(8,128)}, u32[]{:S(2)}) copy-start(f32[216,32]{1,0:T(8,128)} %constant.145) | copy-start | bytes 82948
  63.7 7.8 %collective-permute-start.13 = (f32[32,512]{1,0:T(8,128)}, f32[32,512]{1,0:T(8,128)S(1)}, u32[]{:S(2)}, u32[]{:S(2)}) collective-permute-start(f32[32,512]{1,0:T(8,128)} %pad_maximum_fusion.52), channel_id=1, source_target_pairs={{1,0},{2,1},{3,2},{0,3},{5,4},{6,5},{7,6},{4,7},{9,8},{10,9},{11,1... | collective-permute-start | bytes 196616 | tf_op jit(solution)/shard_map/ppermute | solution.py:215
  66.7 1.4 %copy-start.24 = (f32[216,32]{1,0:T(8,128)S(1)}, f32[216,32]{1,0:T(8,128)}, u32[]{:S(2)}) copy-start(f32[216,32]{1,0:T(8,128)} %constant.144) | copy-start | bytes 82948
  68.2 1.4 %copy-start.23 = (f32[216,32]{1,0:T(8,128)S(1)}, f32[216,32]{1,0:T(8,128)}, u32[]{:S(2)}) copy-start(f32[216,32]{1,0:T(8,128)} %constant.143) | copy-start | bytes 82948
  69.6 1.4 %copy-start.22 = (f32[216,32]{1,0:T(8,128)S(1)}, f32[216,32]{1,0:T(8,128)}, u32[]{:S(2)}) copy-start(f32[216,32]{1,0:T(8,128)} %constant.142) | copy-start | bytes 82948
  71.5 1.0 %copy-start.3 = (f32[512,216]{0,1:T(8,128)S(1)}, f32[512,216]{0,1:T(8,128)}, u32[]{:S(2)}) copy-start(f32[512,216]{0,1:T(8,128)} %convolution_add_fusion.1) | copy-start | bytes 1327108
  71.5 1.0 %copy-start.28 = (f32[216,8]{1,0:T(8,128)S(1)}, f32[216,8]{1,0:T(8,128)}, u32[]{:S(2)}) copy-start(f32[216,8]{1,0:T(8,128)} %constant.139) | copy-start | bytes 20740
  77.1 5.7 %collective-permute-start.24 = (f32[4,4,1,4,128]{4,2,3,1,0:T(1,128)S(1)}, f32[4,4,1,4,128]{4,2,3,1,0:T(1,128)S(1)}, u32[]{:S(2)}, u32[]{:S(2)}) collective-permute-start(f32[4,4,1,4,128]{4,2,3,1,0:T(1,128)S(1)} %get-tuple-element.16), channel_id=1, source_target_pairs={{0,1},{1,2},{2,3},{3,0},{4,5},{5,6},{6,7},{7,4},{8,9},{9,10},{10,1... | collective-permute-start | bytes 98312 | tf_op jit(solution)/shard_map/ppermute | solution.py:24
  77.3 11.4 %collective-permute-start.22 = (f32[4,2,4,4,128]{4,2,3,1,0:T(4,128)S(1)}, f32[4,2,4,4,128]{4,2,3,1,0:T(4,128)S(1)}, u32[]{:S(2)}, u32[]{:S(2)}) collective-permute-start(f32[4,2,4,4,128]{4,2,3,1,0:T(4,128)S(1)} %pad_maximum_fusion.53), channel_id=1, source_target_pairs={{0,4},{4,0},{1,5},{5,1},{2,6},{6,2},{3,7},{7,3},{8,12},{12,8},{9,1... | collective-permute-start | bytes 196616 | tf_op jit(solution)/shard_map/ppermute | solution.py:37
  78.8 5.0 %collective-permute-start.20 = (f32[1,4,4,4,128]{4,2,3,1,0:T(4,128)S(1)}, f32[1,4,4,4,128]{4,2,3,1,0:T(4,128)S(1)}, u32[]{:S(2)}, u32[]{:S(2)}) collective-permute-start(f32[1,4,4,4,128]{4,2,3,1,0:T(4,128)S(1)} %get-tuple-element.18), channel_id=1, source_target_pairs={{0,24},{8,0},{16,8},{24,16},{1,25},{9,1},{17,9},{25,17},{2,26},{10... | collective-permute-start | bytes 98312 | tf_op jit(solution)/shard_map/ppermute | solution.py:24
  80.8 5.9 %collective-permute-start.21 = (f32[1,4,4,4,128]{4,2,3,1,0:T(4,128)S(1)}, f32[1,4,4,4,128]{4,2,3,1,0:T(4,128)S(1)}, u32[]{:S(2)}, u32[]{:S(2)}) collective-permute-start(f32[1,4,4,4,128]{4,2,3,1,0:T(4,128)S(1)} %get-tuple-element.17), channel_id=1, source_target_pairs={{0,8},{8,16},{16,24},{24,0},{1,9},{9,17},{17,25},{25,1},{2,10},{10... | collective-permute-start | bytes 98312 | tf_op jit(solution)/shard_map/ppermute | solution.py:24
  80.9 6.8 %collective-permute-start.23 = (f32[4,4,1,4,128]{4,2,3,1,0:T(1,128)S(1)}, f32[4,4,1,4,128]{4,2,3,1,0:T(1,128)S(1)}, u32[]{:S(2)}, u32[]{:S(2)}) collective-permute-start(f32[4,4,1,4,128]{4,2,3,1,0:T(1,128)S(1)} %get-tuple-element.15), channel_id=1, source_target_pairs={{0,3},{1,0},{2,1},{3,2},{4,7},{5,4},{6,5},{7,6},{8,11},{9,8},{10,9... | collective-permute-start | bytes 98312 | tf_op jit(solution)/shard_map/ppermute | solution.py:24
  88.7 1.0 %copy-start.5 = (f32[8,2,8,4,128]{4,2,3,1,0:T(8,128)S(1)}, f32[8,2,8,4,128]{4,2,3,1,0:T(8,128)}, u32[]{:S(2)}) copy-start(f32[8,2,8,4,128]{4,2,3,1,0:T(8,128)} %copy-done.4) | copy-start | bytes 786436
  (11 other events, 9.0 us)

commit v11 on v9

--- a/solution.py
+++ b/solution.py
@@ -183,15 +183,17 @@
     starts.extend(joint_starts)
     grid = extended.shape[:3]
     orbs = extended.shape[3:]
-    operator = jnp.asarray(coarse_matrix(grid, tuple(starts), rhs_two.shape[:3]))
-    flat = extended.reshape((-1,) + (int(np.prod(orbs)),))
-    post = jnp.dot(operator, flat, precision=lax.Precision.HIGHEST, preferred_element_type=jnp.float32)
-    return post.reshape(tuple(size + 2 for size in rhs_two.shape[:3]) + orbs), tiles_by_step
+    operator = coarse_matrix(grid, tuple(starts), rhs_two.shape[:3])
+    operator = jnp.asarray(operator.reshape((-1,) + tuple(grid)))
+    post = jnp.einsum(
+        "qxyz,xyzgl->qgl", operator, extended, precision=lax.Precision.HIGHEST, preferred_element_type=jnp.float32
+    )
+    return post.reshape(tuple(2 * size + 2 for size in rhs_two.shape[:3]) + orbs), tiles_by_step
 
 
 def coarse_matrix(grid, starts, block):
     cells = int(np.prod(grid))
-    field = np.eye(cells).reshape(tuple(grid) + (cells,))
+    field = np.eye(cells).reshape(grid + (cells,))
 
     def apply(v, level_id):
         center, coupling = level_coeffs(level_id)
@@ -218,10 +220,18 @@
         correct = correct + omega * (current - apply(correct, top_level)) / center_top
     updated = correct_two + grow(correct)
     post = updated + omega * (field - apply(updated, level_two)) / center
-    for dim, start in enumerate(starts):
-        index = [(start - 1 + k) % grid[dim] for k in range(block[dim] + 2)]
+    padded = [2 * size + 2 for size in block]
+    for dim in range(3):
+        index = [(starts[dim] + (p - 1) // 2) % grid[dim] for p in range(padded[dim])]
         post = np.take(post, index, axis=dim)
-    return post.reshape(-1, cells).astype(np.float32)
+    rim = np.zeros(padded, np.int32)
+    for dim in range(3):
+        edge = np.zeros(padded[dim], np.int32)
+        edge[0] = edge[-1] = 1
+        rim = rim + edge.reshape([-1 if d == dim else 1 for d in range(3)])
+    post = post * (rim <= 1)[..., None]
+    post = post.reshape(-1, cells)
+    return post.astype(np.float32)
 
 
 def prolong_face(face, dim):
@@ -295,11 +305,11 @@
     corr_one = omega * rhs_one / center
     padded_one = pad_with(corr_one, all_faces(corr_one))
     rhs_two = restrict(rhs_one - padded_stencil(padded_one, 1))
-    post_two, tiles_by_step = coarse_solve(rhs_two, inv_tiles)
-    inner_two = post_two[1:-1, 1:-1, 1:-1]
-    post_one = post_smooth_padded(
-        1, padded_one, rhs_one, inner_two, [coarse_faces(post_two, dim) for dim in range(3)]
-    )
+    coarse_padded, tiles_by_step = coarse_solve(rhs_two, inv_tiles)
+    center, coupling = level_coeffs(1)
+    updated_padded = padded_one + coarse_padded
+    updated = updated_padded[1:-1, 1:-1, 1:-1]
+    post_one = updated + omega * (rhs_one - padded_stencil(updated_padded, 1)) / center
     return post_smooth(0, corr_zero, faces_zero, rhs_zero, post_one, all_faces(post_one)), tiles_by_step
 
 

time: 78.6 us -> 69.4 us (0.88)
  local copies, waits for them, and re-layouts: 21.1 us -> 10.2 us
  waiting for transfers between devices: 13 us -> 14.4 us
  starting transfers between devices: 26.2 us -> 27.1 us
    slice x11 -> x0, local copies, waits for them, and re-layouts: 6.22 us -> none  [the longest x5 3.35 us: coarse_faces(): lo = lax.slice_in_dim(inner, 0, 1, axis=dim)]
    unnamed x42 -> x36, local copies, waits for them, and re-layouts: 6.91 us -> 3.34 us
    ppermute x15, waiting for transfers between devices: 10.6 us -> 12.8 us  [shifted(): lax.ppermute(block, axis, [(j, (j - step) % count) for j in range(count)])]
    ppermute x15, starting transfers between devices: 14 us -> 14.9 us  [shifted(): lax.ppermute(block, axis, [(j, (j - step) % count) for j in range(count)])]
  transfers between devices with their start and end apart: 25 -> 25, of which waited for: 7 -> 9; matrix products, arithmetic and copies ran while one was open for 10% -> 11% of each run, Pallas kernels for 0% -> 0%
where the time goes in v11:
time: 69.4 us; the launch traced here: 68.7 us
  starting transfers between devices  27.1 us (39%)
  waiting for transfers between devices  14.4 us (21%)
  local copies, waits for them, and re-layouts  10.2 us (15%)
  other arithmetic  8.92 us (13%)
  between operations  5.58 us (8%)
  matrix products  2.44 us (4%)
    ppermute x15, starting transfers between devices, shifted(): lax.ppermute(block, axis, [(j, (j - step) % count) for j in range(count)])  14.9 us
    ppermute x15, waiting for transfers between devices, shifted(): lax.ppermute(block, axis, [(j, (j - step) % count) for j in range(count)])  12.8 us
    ppermute x7, starting transfers between devices, fetch(): cache[steps] = lax.ppermute(block, tuple(axes), pairs)  7.43 us
    ppermute x3, starting transfers between devices, axis_faces(): lax.ppermute(jnp.concatenate([first, last], axis=dim), axis, [(0, 1), (1,...  4.75 us
    unnamed x36, local copies, waits for them, and re-layouts  3.34 us
    dynamic_update_slice x4, local copies, waits for them, and re-layouts, gram_matrix(): total = lax.dynamic_update_slice(total, piece[slot], (row, col))  2.55 us
    slice x3, local copies, waits for them, and re-layouts, extend_axis(): cache[step] = both[:block.size].reshape(block.shape)  2.17 us
    sub x1, other arithmetic, vcycle(): rhs_one = restrict(rhs_zero - stencil(corr_zero, faces_zero, 0))  1.86 us
  transfers between devices with their start and end apart: 25, of which 9 were waited for; matrix products, arithmetic and copies ran while one was open for 11% of the time, Pallas kernels for 0%

profile of v11, /device:TPU:0, one launch (start us, length us, event | category | flops | bytes accessed | tf_op | source)
XLA Modules:
  0.0 68.7 jit_solution(10979076226111895417)
XLA Ops:
  0.0 1.5 %fusion.36 = (f32[8,8,1,4,128]{4,2,3,1,0:T(1,128)S(1)}, f32[8,8,1,4,128]{4,2,3,1,0:T(1,128)S(1)}) fusion(bf16[8,8,8,4,128]{4,2,3,1,0:T(8,128)(2,1)} %bitcast.82), kind=kLoop, calls=%fused_computation.110 | loop fusion | flops 131072 | bytes 393216 | tf_op jit(solution)/shard_map/div | solution.py:300
  1.5 0.5 collective-permute-start.4
  2.2 2.6 %collective-permute-start.2 = (f32[8,2,8,4,128]{4,2,3,1,0:T(8,128)S(1)}, f32[8,2,8,4,128]{4,2,3,1,0:T(8,128)S(1)}, u32[]{:S(2)}, u32[]{:S(2)}) collective-permute-start(f32[8,2,8,4,128]{4,2,3,1,0:T(8,128)S(1)} %pad_maximum_fusion.32), channel_id=1, source_target_pairs={{0,4},{4,0},{1,5},{5,1},{2,6},{6,2},{3,7},{7,3},{8,12},{12,8},{9,1... | collective-permute-start | bytes 786440 | tf_op jit(solution)/shard_map/ppermute | solution.py:37
  4.8 3.7 %collective-permute-start = (f32[1,8,8,4,128]{4,2,3,1,0:T(8,128)S(1)}, f32[1,8,8,4,128]{4,2,3,1,0:T(8,128)}, u32[]{:S(2)}, u32[]{:S(2)}) collective-permute-start(f32[1,8,8,4,128]{4,2,3,1,0:T(8,128)S(1)} %get-tuple-element.8), channel_id=1, source_target_pairs={{0,24},{8,0},{16,8},{24,16},{1,25},{9,1},{17,9},{25,17},{2,26},{10... | collective-permute-start | bytes 393224 | tf_op jit(solution)/shard_map/ppermute | solution.py:24
  8.4 1.2 %collective-permute-start.3 = (f32[8,8,1,4,128]{4,2,3,1,0:T(1,128)S(1)}, f32[8,8,1,4,128]{4,2,3,1,0:T(1,128)S(1)}, u32[]{:S(2)}, u32[]{:S(2)}) collective-permute-start(f32[8,8,1,4,128]{4,2,3,1,0:T(1,128)S(1)} %get-tuple-element.5), channel_id=1, source_target_pairs={{0,3},{1,0},{2,1},{3,2},{4,7},{5,4},{6,5},{7,6},{8,11},{9,8},{10,9... | collective-permute-start | bytes 393224 | tf_op jit(solution)/shard_map/ppermute | solution.py:24
  9.6 0.7 copy-done.15
  10.3 0.7 constant_dynamic-slice_fusion
  12.8 3.7 %collective-permute-done.1 = f32[1,8,8,4,128]{4,2,3,1,0:T(8,128)S(1)} collective-permute-done((f32[1,8,8,4,128]{4,2,3,1,0:T(8,128)S(1)}, f32[1,8,8,4,128]{4,2,3,1,0:T(8,128)S(1)}, u32[]{:S(2)}, u32[]{:S(2)}) %collective-permute-start.1) | collective-permute-done | bytes 131104 | tf_op jit(solution)/shard_map/ppermute | solution.py:24
  16.6 1.9 %convert_subtract_fusion.1 = f32[8,8,8,4,128]{4,2,3,1,0:T(8,128)S(1)} fusion(f32[8,8,1,4,128]{4,2,3,1,0:T(1,128)S(1)} %collective-permute-done.4, f32[10,1,8,4,128]{4,2,3,1,0:T(8,128)S(1)} %pad.40, f32[10,1,8,4,128]{4,2,3,1,0:T(8,128)S(1)} %pad.41, f32[1,8,8,4,128]{4,2,3,1,0:T(8,128)} %collective-permute-done, ...), kind=kLoop, calls=%fused_computation.1 | loop fusion | flops 8912896 | bytes 3473408 | tf_op jit(solution)/shard_map/sub | solution.py:303
  18.4 0.7 %reduce_sum.18 = f32[4,4,4,4,128]{4,2,3,1,0:T(4,128)S(1)} reduce(f32[4,2,4,2,4,2,4,128]{7,5,4,6,3,2,1,0:T(2,128)S(1)} %bitcast.85, f32[]{:T(128)} %constant.92.clone.1), dimensions={1,3,5}, to_apply=%region_0.1 | reduce | flops 229376 | bytes 1179652 | tf_op jit(solution)/shard_map/reduce_sum | solution.py:170
  19.4 0.6 collective-permute-start.6
  20.1 1.5 %collective-permute-start.8 = (f32[1,4,4,4,128]{4,2,3,1,0:T(4,128)S(1)}, f32[1,4,4,4,128]{4,2,3,1,0:T(4,128)S(1)}, u32[]{:S(2)}, u32[]{:S(2)}) collective-permute-start(f32[1,4,4,4,128]{4,2,3,1,0:T(4,128)S(1)} %get-tuple-element.24), channel_id=1, source_target_pairs={{0,24},{8,0},{16,8},{24,16},{1,25},{9,1},{17,9},{25,17},{2,26},{10... | collective-permute-start | bytes 98312 | tf_op jit(solution)/shard_map/ppermute | solution.py:24
  21.6 0.6 collective-permute-start.7
  22.2 1.1 %collective-permute-done.5 = f32[4,4,1,4,128]{4,2,3,1,0:T(1,128)S(1)} collective-permute-done((f32[4,4,1,4,128]{4,2,3,1,0:T(1,128)S(1)}, f32[4,4,1,4,128]{4,2,3,1,0:T(1,128)S(1)}, u32[]{:S(2)}, u32[]{:S(2)}) %collective-permute-start.5) | collective-permute-done | bytes 32800 | tf_op jit(solution)/shard_map/ppermute | solution.py:24
  23.4 0.6 collective-permute-done.6
  24.1 3.3 %collective-permute-done.7 = f32[1,4,4,4,128]{4,2,3,1,0:T(4,128)S(1)} collective-permute-done((f32[1,4,4,4,128]{4,2,3,1,0:T(4,128)S(1)}, f32[1,4,4,4,128]{4,2,3,1,0:T(4,128)S(1)}, u32[]{:S(2)}, u32[]{:S(2)}) %collective-permute-start.7) | collective-permute-done | bytes 32800 | tf_op jit(solution)/shard_map/ppermute | solution.py:24
  27.6 0.4 copy-done.13
  28.0 0.7 %copy-done.9 = f32[1,128,128]{2,1,0:T(8,128)S(1)} copy-done((f32[1,128,128]{2,1,0:T(8,128)S(1)}, f32[1,128,128]{2,1,0:T(8,128)}, u32[]{:S(2)}) %copy-start.9) | copy-done | bytes 65560
  28.8 0.6 pad_maximum_fusion.51
  29.4 0.6 collective-permute-start.11
  30.0 3.2 %collective-permute-start.10 = (f32[20480]{0:T(1024)}, f32[20480]{0:T(1024)}, u32[]{:S(2)}, u32[]{:S(2)}) collective-permute-start(f32[20480]{0:T(1024)} %pad_maximum_fusion.51), channel_id=1, source_target_pairs={{0,24},{8,0},{16,8},{24,16},{1,25},{9,1},{17,9},{25,17},{2,26},{10... | collective-permute-start | bytes 245768 | tf_op jit(solution)/shard_map/ppermute | solution.py:24
  37.1 0.7 %slice.368 = f32[4096]{0:T(1024)S(1)} slice(f32[20480]{0:T(1024)} %collective-permute-done.12), slice={[0:4096]} | slice | bytes 32768 | tf_op jit(solution)/shard_map/slice | solution.py:72
  37.8 1.7 %collective-permute-done.11 = f32[20480]{0:T(1024)} collective-permute-done((f32[20480]{0:T(1024)}, f32[20480]{0:T(1024)}, u32[]{:S(2)}, u32[]{:S(2)}) %collective-permute-start.11) | collective-permute-done | bytes 81952 | tf_op jit(solution)/shard_map/ppermute | solution.py:24
  39.5 0.7 %slice.367 = f32[4096]{0:T(1024)S(1)} slice(f32[20480]{0:T(1024)} %collective-permute-done.11), slice={[0:4096]} | slice | bytes 32768 | tf_op jit(solution)/shard_map/slice | solution.py:72
  40.3 0.7 %slice.366 = f32[4096]{0:T(1024)S(1)} slice(f32[20480]{0:T(1024)} %collective-permute-done.10), slice={[0:4096]} | slice | bytes 32768 | tf_op jit(solution)/shard_map/slice | solution.py:72
  41.1 1.4 %collective-permute-start.18 = (f32[8,2,2,4,128]{4,3,2,1,0:T(4,128)S(1)}, f32[8,2,2,4,128]{4,3,2,1,0:T(4,128)S(1)}, u32[]{:S(2)}, u32[]{:S(2)}) collective-permute-start(f32[8,2,2,4,128]{4,3,2,1,0:T(4,128)S(1)} %pad_maximum_fusion.53), channel_id=1, source_target_pairs={{6,0},{7,1},{4,2},{5,3},{2,4},{3,5},{0,6},{1,7},{14,8},{15,9},{12,... | collective-permute-start | bytes 196616 | tf_op jit(solution)/shard_map/ppermute | solution.py:101
  42.5 2.3 %collective-permute-start.17 = (f32[8,2,2,4,128]{4,3,2,1,0:T(4,128)S(1)}, f32[8,2,2,4,128]{4,3,2,1,0:T(4,128)S(1)}, u32[]{:S(2)}, u32[]{:S(2)}) collective-permute-start(f32[8,2,2,4,128]{4,3,2,1,0:T(4,128)S(1)} %pad_maximum_fusion.53), channel_id=1, source_target_pairs={{5,0},{6,1},{7,2},{4,3},{1,4},{2,5},{3,6},{0,7},{13,8},{14,9},{15,... | collective-permute-start | bytes 196616 | tf_op jit(solution)/shard_map/ppermute | solution.py:101
  44.8 0.5 collective-permute-start.16
  45.3 0.8 %fusion.39 = f32[512,512]{1,0:T(8,128)S(1)} fusion(f32[512,512]{1,0:T(8,128)S(1)} %bitcast_dynamic-update-slice_fusion, s32[]{:T(128)S(6)} %select_n.65, s32[]{:T(128)S(6)} %select_n.66, f32[20480]{0:T(1024)} %collective-permute-done.10), kind=kLoop, calls=%fused_computation.121 | loop fusion | bytes 131080 | tf_op jit(solution)/shard_map/dynamic_update_slice | solution.py:294
  46.1 0.8 %fusion.38 = f32[512,512]{1,0:T(8,128)S(1)} fusion(f32[512,512]{1,0:T(8,128)S(1)} %fusion.39, s32[]{:T(128)S(6)} %select_n.69, s32[]{:T(128)S(6)} %select_n.70, f32[20480]{0:T(1024)} %collective-permute-done.11), kind=kLoop, calls=%fused_computation.119 | loop fusion | bytes 131080 | tf_op jit(solution)/shard_map/dynamic_update_slice | solution.py:294
  47.0 1.7 %collective-permute-start.14 = (f32[8,2,2,4,128]{4,3,2,1,0:T(4,128)S(1)}, f32[8,2,2,4,128]{4,3,2,1,0:T(4,128)S(1)}, u32[]{:S(2)}, u32[]{:S(2)}) collective-permute-start(f32[8,2,2,4,128]{4,3,2,1,0:T(4,128)S(1)} %pad_maximum_fusion.53), channel_id=1, source_target_pairs={{2,0},{3,1},{0,2},{1,3},{6,4},{7,5},{4,6},{5,7},{10,8},{11,9},{8,1... | collective-permute-start | bytes 196616 | tf_op jit(solution)/shard_map/ppermute | solution.py:101
  48.7 1.5 %collective-permute-start.13 = (f32[8,2,2,4,128]{4,3,2,1,0:T(4,128)S(1)}, f32[8,2,2,4,128]{4,3,2,1,0:T(4,128)S(1)}, u32[]{:S(2)}, u32[]{:S(2)}) collective-permute-start(f32[8,2,2,4,128]{4,3,2,1,0:T(4,128)S(1)} %pad_maximum_fusion.53), channel_id=1, source_target_pairs={{1,0},{2,1},{3,2},{0,3},{5,4},{6,5},{7,6},{4,7},{9,8},{10,9},{11,1... | collective-permute-start | bytes 196616 | tf_op jit(solution)/shard_map/ppermute | solution.py:101
  50.1 0.8 %fusion.37 = f32[512,512]{1,0:T(8,128)S(1)} fusion(f32[512,512]{1,0:T(8,128)S(1)} %fusion.38, s32[]{:T(128)S(6)} %select_n.73, s32[]{:T(128)S(6)} %select_n.74, f32[20480]{0:T(1024)} %collective-permute-done.12), kind=kLoop, calls=%fused_computation.117 | loop fusion | bytes 131080 | tf_op jit(solution)/shard_map/dynamic_update_slice | solution.py:294
  51.0 0.3 collective-permute-done.14
  51.3 0.7 %collective-permute-done.13 = f32[8,2,2,4,128]{4,3,2,1,0:T(4,128)S(1)} collective-permute-done((f32[8,2,2,4,128]{4,3,2,1,0:T(4,128)S(1)}, f32[8,2,2,4,128]{4,3,2,1,0:T(4,128)S(1)}, u32[]{:S(2)}, u32[]{:S(2)}) %collective-permute-start.13) | collective-permute-done | bytes 65568 | tf_op jit(solution)/shard_map/ppermute | solution.py:101
  52.2 0.6 convolution_bitcast_fusion
  53.0 0.6 copy-done.4
  53.7 0.2 maximum_add_fusion
  54.2 0.6 collective-permute-start.24
  54.8 1.6 %collective-permute-start.22 = (f32[4,2,4,4,128]{4,2,3,1,0:T(4,128)S(1)}, f32[4,2,4,4,128]{4,2,3,1,0:T(4,128)S(1)}, u32[]{:S(2)}, u32[]{:S(2)}) collective-permute-start(f32[4,2,4,4,128]{4,2,3,1,0:T(4,128)S(1)} %pad_maximum_fusion.54), channel_id=1, source_target_pairs={{0,4},{4,0},{1,5},{5,1},{2,6},{6,2},{3,7},{7,3},{8,12},{12,8},{9,1... | collective-permute-start | bytes 196616 | tf_op jit(solution)/shard_map/ppermute | solution.py:37
  56.4 2.1 %collective-permute-start.20 = (f32[1,4,4,4,128]{4,2,3,1,0:T(4,128)S(1)}, f32[1,4,4,4,128]{4,2,3,1,0:T(4,128)S(1)}, u32[]{:S(2)}, u32[]{:S(2)}) collective-permute-start(f32[1,4,4,4,128]{4,2,3,1,0:T(4,128)S(1)} %get-tuple-element.18), channel_id=1, source_target_pairs={{0,24},{8,0},{16,8},{24,16},{1,25},{9,1},{17,9},{25,17},{2,26},{10... | collective-permute-start | bytes 98312 | tf_op jit(solution)/shard_map/ppermute | solution.py:24
  58.5 0.7 collective-permute-start.23
  59.3 0.6 broadcast_in_dim.80
  60.4 0.9 %add.227 = f32[1,8,8,4,128]{4,2,3,1,0:T(8,128)S(1)} add(f32[1,8,8,4,128]{4,2,3,1,0:T(8,128)} %collective-permute-done, f32[1,8,8,4,128]{4,2,3,1,0:T(8,128)S(1)} %bitcast.91) | non-fusion elementwise | flops 32768 | bytes 393216 | tf_op jit(solution)/shard_map/add | solution.py:261
  61.3 2.9 %collective-permute-done.21 = f32[1,4,4,4,128]{4,2,3,1,0:T(4,128)S(1)} collective-permute-done((f32[1,4,4,4,128]{4,2,3,1,0:T(4,128)S(1)}, f32[1,4,4,4,128]{4,2,3,1,0:T(4,128)S(1)}, u32[]{:S(2)}, u32[]{:S(2)}) %collective-permute-start.21) | collective-permute-done | bytes 32800 | tf_op jit(solution)/shard_map/ppermute | solution.py:24
  64.3 0.8 %copy-done.2 = f32[1,8,8,4,128]{4,2,3,1,0:T(8,128)S(1)} copy-done((f32[1,8,8,4,128]{4,2,3,1,0:T(8,128)S(1)}, f32[1,8,8,4,128]{4,2,3,1,0:T(8,128)}, u32[]{:S(2)}) %copy-start.2) | copy-done | bytes 131096
  65.6 1.0 %fusion.2 = f32[8,8,8,4,128]{4,2,3,1,0:T(8,128)S(1)} fusion(f32[8,8,8,4,128]{4,2,3,1,0:T(8,128)S(1)} %fusion.21, f32[8,8,1,4,128]{4,2,3,1,0:T(1,128)S(1)} %add.236, f32[10,1,8,4,128]{4,2,3,1,0:T(8,128)S(1)} %pad.48, f32[10,1,8,4,128]{4,2,3,1,0:T(8,128)S(1)} %pad.49, f32[1,8,8,4,128]{4,2,3,1,0:T(8,128)S(1)} %add.227, f32[1,8,8,4,128]{4,2,3,1,0:T(8,128)S(1)} %add.228, ...), kind=kLoop, calls=%fused_computation.8 | loop fusion | flops 9437184 | bytes 3473408 | tf_op jit(solution)/shard_map/add | solution.py:263
  66.9 1.8 %convolution_convert_fusion = bf16[512,512]{1,0:T(8,128)(2,1)} fusion(f32[512,512]{1,0:T(8,128)S(1)} %bitcast_multiply_fusion, f32[512,512]{1,0:T(8,128)S(1)} %fusion.37), kind=kOutput, calls=%fused_computation.4 | convolution fusion | flops 805568512 | bytes 2621440 | tf_op jit(solution)/shard_map/dot_general | solution.py:331
  (116 shorter events, 3.5 us)
Async XLA Ops:
  0.0 2.1 %copy-start = (bf16[8,8,8,512]{3,2,1,0:T(8,128)(2,1)S(1)}, bf16[8,8,8,512]{3,2,1,0:T(8,128)(2,1)}, u32[]{:S(2)}) copy-start(bf16[8,8,8,512]{3,2,1,0:T(8,128)(2,1)} %param.5) | copy-start | bytes 1572868
  1.5 11.2 %collective-permute-start.4 = (f32[8,8,1,4,128]{4,2,3,1,0:T(1,128)S(1)}, f32[8,8,1,4,128]{4,2,3,1,0:T(1,128)S(1)}, u32[]{:S(2)}, u32[]{:S(2)}) collective-permute-start(f32[8,8,1,4,128]{4,2,3,1,0:T(1,128)S(1)} %get-tuple-element.6), channel_id=1, source_target_pairs={{0,1},{1,2},{2,3},{3,0},{4,5},{5,6},{6,7},{7,4},{8,9},{9,10},{10,1... | collective-permute-start | bytes 393224 | tf_op jit(solution)/shard_map/ppermute | solution.py:24
  2.2 10.6 %collective-permute-start.2 = (f32[8,2,8,4,128]{4,2,3,1,0:T(8,128)S(1)}, f32[8,2,8,4,128]{4,2,3,1,0:T(8,128)S(1)}, u32[]{:S(2)}, u32[]{:S(2)}) collective-permute-start(f32[8,2,8,4,128]{4,2,3,1,0:T(8,128)S(1)} %pad_maximum_fusion.32), channel_id=1, source_target_pairs={{0,4},{4,0},{1,5},{5,1},{2,6},{6,2},{3,7},{7,3},{8,12},{12,8},{9,1... | collective-permute-start | bytes 786440 | tf_op jit(solution)/shard_map/ppermute | solution.py:37
  4.8 8.0 %collective-permute-start = (f32[1,8,8,4,128]{4,2,3,1,0:T(8,128)S(1)}, f32[1,8,8,4,128]{4,2,3,1,0:T(8,128)}, u32[]{:S(2)}, u32[]{:S(2)}) collective-permute-start(f32[1,8,8,4,128]{4,2,3,1,0:T(8,128)S(1)} %get-tuple-element.8), channel_id=1, source_target_pairs={{0,24},{8,0},{16,8},{24,16},{1,25},{9,1},{17,9},{25,17},{2,26},{10... | collective-permute-start | bytes 393224 | tf_op jit(solution)/shard_map/ppermute | solution.py:24
  8.4 8.1 %collective-permute-start.1 = (f32[1,8,8,4,128]{4,2,3,1,0:T(8,128)S(1)}, f32[1,8,8,4,128]{4,2,3,1,0:T(8,128)S(1)}, u32[]{:S(2)}, u32[]{:S(2)}) collective-permute-start(f32[1,8,8,4,128]{4,2,3,1,0:T(8,128)S(1)} %get-tuple-element.7), channel_id=1, source_target_pairs={{0,8},{8,16},{16,24},{24,0},{1,9},{9,17},{17,25},{25,1},{2,10},{10... | collective-permute-start | bytes 393224 | tf_op jit(solution)/shard_map/ppermute | solution.py:24
  8.4 8.1 %collective-permute-start.3 = (f32[8,8,1,4,128]{4,2,3,1,0:T(1,128)S(1)}, f32[8,8,1,4,128]{4,2,3,1,0:T(1,128)S(1)}, u32[]{:S(2)}, u32[]{:S(2)}) collective-permute-start(f32[8,8,1,4,128]{4,2,3,1,0:T(1,128)S(1)} %get-tuple-element.5), channel_id=1, source_target_pairs={{0,3},{1,0},{2,1},{3,2},{4,7},{5,4},{6,5},{7,6},{8,11},{9,8},{10,9... | collective-permute-start | bytes 393224 | tf_op jit(solution)/shard_map/ppermute | solution.py:24
  9.6 0.7 copy-start.15
  10.3 1.9 %copy-start.16 = (s32[3,2,512]{2,1,0:T(2,128)S(1)}, s32[3,2,512]{2,1,0:T(2,128)}, u32[]{:S(2)}) copy-start(s32[3,2,512]{2,1,0:T(2,128)} %param.6) | copy-start | bytes 36868
  16.5 1.9 %copy-start.1 = (f32[1,8,8,4,128]{4,2,3,1,0:T(8,128)}, f32[1,8,8,4,128]{4,2,3,1,0:T(8,128)S(1)}, u32[]{:S(2)}) copy-start(f32[1,8,8,4,128]{4,2,3,1,0:T(8,128)S(1)} %collective-permute-done.1) | copy-start | bytes 393220
  19.3 2.9 %collective-permute-start.9 = (f32[4,4,1,4,128]{4,2,3,1,0:T(1,128)S(1)}, f32[4,4,1,4,128]{4,2,3,1,0:T(1,128)S(1)}, u32[]{:S(2)}, u32[]{:S(2)}) collective-permute-start(f32[4,4,1,4,128]{4,2,3,1,0:T(1,128)S(1)} %get-tuple-element.22), channel_id=1, source_target_pairs={{0,3},{1,0},{2,1},{3,2},{4,7},{5,4},{6,5},{7,6},{8,11},{9,8},{10,9... | collective-permute-start | bytes 98312 | tf_op jit(solution)/shard_map/ppermute | solution.py:24
  19.4 4.6 %collective-permute-start.6 = (f32[4,2,4,4,128]{4,2,3,1,0:T(4,128)S(1)}, f32[4,2,4,4,128]{4,2,3,1,0:T(4,128)S(1)}, u32[]{:S(2)}, u32[]{:S(2)}) collective-permute-start(f32[4,2,4,4,128]{4,2,3,1,0:T(4,128)S(1)} %pad_maximum_fusion.52), channel_id=1, source_target_pairs={{0,4},{4,0},{1,5},{5,1},{2,6},{6,2},{3,7},{7,3},{8,12},{12,8},{9,1... | collective-permute-start | bytes 196616 | tf_op jit(solution)/shard_map/ppermute | solution.py:37
  19.9 3.4 %collective-permute-start.5 = (f32[4,4,1,4,128]{4,2,3,1,0:T(1,128)S(1)}, f32[4,4,1,4,128]{4,2,3,1,0:T(1,128)S(1)}, u32[]{:S(2)}, u32[]{:S(2)}) collective-permute-start(f32[4,4,1,4,128]{4,2,3,1,0:T(1,128)S(1)} %get-tuple-element.21), channel_id=1, source_target_pairs={{0,1},{1,2},{2,3},{3,0},{4,5},{5,6},{6,7},{7,4},{8,9},{9,10},{10,1... | collective-permute-start | bytes 98312 | tf_op jit(solution)/shard_map/ppermute | solution.py:24
  20.1 3.9 %collective-permute-start.8 = (f32[1,4,4,4,128]{4,2,3,1,0:T(4,128)S(1)}, f32[1,4,4,4,128]{4,2,3,1,0:T(4,128)S(1)}, u32[]{:S(2)}, u32[]{:S(2)}) collective-permute-start(f32[1,4,4,4,128]{4,2,3,1,0:T(4,128)S(1)} %get-tuple-element.24), channel_id=1, source_target_pairs={{0,24},{8,0},{16,8},{24,16},{1,25},{9,1},{17,9},{25,17},{2,26},{10... | collective-permute-start | bytes 98312 | tf_op jit(solution)/shard_map/ppermute | solution.py:24
  21.6 5.7 %collective-permute-start.7 = (f32[1,4,4,4,128]{4,2,3,1,0:T(4,128)S(1)}, f32[1,4,4,4,128]{4,2,3,1,0:T(4,128)S(1)}, u32[]{:S(2)}, u32[]{:S(2)}) collective-permute-start(f32[1,4,4,4,128]{4,2,3,1,0:T(4,128)S(1)} %get-tuple-element.23), channel_id=1, source_target_pairs={{0,8},{8,16},{16,24},{24,0},{1,9},{9,17},{17,25},{25,1},{2,10},{10... | collective-permute-start | bytes 98312 | tf_op jit(solution)/shard_map/ppermute | solution.py:24
  23.9 3.6 %copy-start.3 = (f32[6,1,4,4,128]{4,2,3,1,0:T(4,128)}, f32[6,1,4,4,128]{4,2,3,1,0:T(4,128)S(1)}, u32[]{:S(2)}) copy-start(f32[6,1,4,4,128]{4,2,3,1,0:T(4,128)S(1)} %pad.46) | copy-start | bytes 147460
  24.0 3.6 %copy-start.5 = (f32[6,1,4,4,128]{4,2,3,1,0:T(4,128)}, f32[6,1,4,4,128]{4,2,3,1,0:T(4,128)S(1)}, u32[]{:S(2)}) copy-start(f32[6,1,4,4,128]{4,2,3,1,0:T(4,128)S(1)} %pad.45) | copy-start | bytes 147460
  24.1 3.5 %copy-start.11 = (f32[1,4,4,4,128]{4,2,3,1,0:T(4,128)}, f32[1,4,4,4,128]{4,2,3,1,0:T(4,128)S(1)}, u32[]{:S(2)}) copy-start(f32[1,4,4,4,128]{4,2,3,1,0:T(4,128)S(1)} %collective-permute-done.8) | copy-start | bytes 98308
  27.3 0.6 copy-start.13
  27.9 0.8 %copy-start.9 = (f32[1,128,128]{2,1,0:T(8,128)S(1)}, f32[1,128,128]{2,1,0:T(8,128)}, u32[]{:S(2)}) copy-start(f32[1,128,128]{2,1,0:T(8,128)} %param.8) | copy-start | bytes 196612
  28.0 1.4 %copy-start.7 = (f32[2,2,2,4,128]{4,3,2,1,0:T(4,128)}, f32[2,2,2,4,128]{4,3,2,1,0:T(4,128)S(1)}, u32[]{:S(2)}) copy-start(f32[2,2,2,4,128]{4,3,2,1,0:T(4,128)S(1)} %copy_multiply_fusion) | copy-start | bytes 49156
  29.4 4.0 %copy-start.10 = (f32[1,128,128]{2,1,0:T(8,128)S(1)}, f32[1,128,128]{2,1,0:T(8,128)}, u32[]{:S(2)}) copy-start(f32[1,128,128]{2,1,0:T(8,128)} %param.8) | copy-start | bytes 196612
  29.4 7.6 %collective-permute-start.12 = (f32[20480]{0:T(1024)}, f32[20480]{0:T(1024)}, u32[]{:S(2)}, u32[]{:S(2)}) collective-permute-start(f32[20480]{0:T(1024)} %pad_maximum_fusion.51), channel_id=1, source_target_pairs={{0,8},{8,16},{16,24},{24,0},{1,9},{9,17},{17,25},{25,1},{2,10},{10... | collective-permute-start | bytes 245768 | tf_op jit(solution)/shard_map/ppermute | solution.py:24
  29.4 10.1 %collective-permute-start.11 = (f32[20480]{0:T(1024)}, f32[20480]{0:T(1024)}, u32[]{:S(2)}, u32[]{:S(2)}) collective-permute-start(f32[20480]{0:T(1024)} %pad_maximum_fusion.51), channel_id=1, source_target_pairs={{0,16},{8,24},{16,0},{24,8},{1,17},{9,25},{17,1},{25,9},{2,18},{10... | collective-permute-start | bytes 245768 | tf_op jit(solution)/shard_map/ppermute | solution.py:24
  30.0 10.2 %collective-permute-start.10 = (f32[20480]{0:T(1024)}, f32[20480]{0:T(1024)}, u32[]{:S(2)}, u32[]{:S(2)}) collective-permute-start(f32[20480]{0:T(1024)} %pad_maximum_fusion.51), channel_id=1, source_target_pairs={{0,24},{8,0},{16,8},{24,16},{1,25},{9,1},{17,9},{25,17},{2,26},{10... | collective-permute-start | bytes 245768 | tf_op jit(solution)/shard_map/ppermute | solution.py:24
  40.2 0.7 %copy-start.8 = (f32[2,2,2,4,128]{4,3,2,1,0:T(4,128)S(1)}, f32[2,2,2,4,128]{4,3,2,1,0:T(4,128)}, u32[]{:S(2)}) copy-start(f32[2,2,2,4,128]{4,3,2,1,0:T(4,128)} %copy-done.7) | copy-start | bytes 49156
  41.0 6.0 %collective-permute-start.19 = (f32[8,2,2,4,128]{4,3,2,1,0:T(4,128)S(1)}, f32[8,2,2,4,128]{4,3,2,1,0:T(4,128)S(1)}, u32[]{:S(2)}, u32[]{:S(2)}) collective-permute-start(f32[8,2,2,4,128]{4,3,2,1,0:T(4,128)S(1)} %pad_maximum_fusion.53), channel_id=1, source_target_pairs={{7,0},{4,1},{5,2},{6,3},{3,4},{0,5},{1,6},{2,7},{15,8},{12,9},{13,... | collective-permute-start | bytes 196616 | tf_op jit(solution)/shard_map/ppermute | solution.py:101
  41.1 7.6 %collective-permute-start.18 = (f32[8,2,2,4,128]{4,3,2,1,0:T(4,128)S(1)}, f32[8,2,2,4,128]{4,3,2,1,0:T(4,128)S(1)}, u32[]{:S(2)}, u32[]{:S(2)}) collective-permute-start(f32[8,2,2,4,128]{4,3,2,1,0:T(4,128)S(1)} %pad_maximum_fusion.53), channel_id=1, source_target_pairs={{6,0},{7,1},{4,2},{5,3},{2,4},{3,5},{0,6},{1,7},{14,8},{15,9},{12,... | collective-permute-start | bytes 196616 | tf_op jit(solution)/shard_map/ppermute | solution.py:101
  42.5 8.5 %collective-permute-start.17 = (f32[8,2,2,4,128]{4,3,2,1,0:T(4,128)S(1)}, f32[8,2,2,4,128]{4,3,2,1,0:T(4,128)S(1)}, u32[]{:S(2)}, u32[]{:S(2)}) collective-permute-start(f32[8,2,2,4,128]{4,3,2,1,0:T(4,128)S(1)} %pad_maximum_fusion.53), channel_id=1, source_target_pairs={{5,0},{6,1},{7,2},{4,3},{1,4},{2,5},{3,6},{0,7},{13,8},{14,9},{15,... | collective-permute-start | bytes 196616 | tf_op jit(solution)/shard_map/ppermute | solution.py:101
  44.8 6.2 %collective-permute-start.16 = (f32[8,2,2,4,128]{4,3,2,1,0:T(4,128)S(1)}, f32[8,2,2,4,128]{4,3,2,1,0:T(4,128)S(1)}, u32[]{:S(2)}, u32[]{:S(2)}) collective-permute-start(f32[8,2,2,4,128]{4,3,2,1,0:T(4,128)S(1)} %pad_maximum_fusion.53), channel_id=1, source_target_pairs={{4,0},{5,1},{6,2},{7,3},{0,4},{1,5},{2,6},{3,7},{12,8},{13,9},{14,... | collective-permute-start | bytes 196616 | tf_op jit(solution)/shard_map/ppermute | solution.py:101
  45.3 5.7 %collective-permute-start.15 = (f32[8,2,2,4,128]{4,3,2,1,0:T(4,128)S(1)}, f32[8,2,2,4,128]{4,3,2,1,0:T(4,128)S(1)}, u32[]{:S(2)}, u32[]{:S(2)}) collective-permute-start(f32[8,2,2,4,128]{4,3,2,1,0:T(4,128)S(1)} %pad_maximum_fusion.53), channel_id=1, source_target_pairs={{3,0},{0,1},{1,2},{2,3},{7,4},{4,5},{5,6},{6,7},{11,8},{8,9},{9,10... | collective-permute-start | bytes 196616 | tf_op jit(solution)/shard_map/ppermute | solution.py:101
  47.0 4.3 %collective-permute-start.14 = (f32[8,2,2,4,128]{4,3,2,1,0:T(4,128)S(1)}, f32[8,2,2,4,128]{4,3,2,1,0:T(4,128)S(1)}, u32[]{:S(2)}, u32[]{:S(2)}) collective-permute-start(f32[8,2,2,4,128]{4,3,2,1,0:T(4,128)S(1)} %pad_maximum_fusion.53), channel_id=1, source_target_pairs={{2,0},{3,1},{0,2},{1,3},{6,4},{7,5},{4,6},{5,7},{10,8},{11,9},{8,1... | collective-permute-start | bytes 196616 | tf_op jit(solution)/shard_map/ppermute | solution.py:101
  48.7 3.4 %collective-permute-start.13 = (f32[8,2,2,4,128]{4,3,2,1,0:T(4,128)S(1)}, f32[8,2,2,4,128]{4,3,2,1,0:T(4,128)S(1)}, u32[]{:S(2)}, u32[]{:S(2)}) collective-permute-start(f32[8,2,2,4,128]{4,3,2,1,0:T(4,128)S(1)} %pad_maximum_fusion.53), channel_id=1, source_target_pairs={{1,0},{2,1},{3,2},{0,3},{5,4},{6,5},{7,6},{4,7},{9,8},{10,9},{11,1... | collective-permute-start | bytes 196616 | tf_op jit(solution)/shard_map/ppermute | solution.py:101
  51.0 1.2 %copy-start.17 = (f32[216,8,4,8,1]{0,3,2,4,1:T(8,128)S(1)}, f32[216,8,4,8,1]{0,3,2,4,1:T(8,128)}, u32[]{:S(2)}) copy-start(f32[216,8,4,8,1]{0,3,2,4,1:T(8,128)} %constant.137) | copy-start | bytes 663556
  52.8 0.8 %copy-start.4 = (f32[6,1,4,4,128]{4,2,3,1,0:T(4,128)S(1)}, f32[6,1,4,4,128]{4,2,3,1,0:T(4,128)}, u32[]{:S(2)}) copy-start(f32[6,1,4,4,128]{4,2,3,1,0:T(4,128)} %copy-done.3) | copy-start | bytes 147460
  52.9 0.8 %copy-start.6 = (f32[6,1,4,4,128]{4,2,3,1,0:T(4,128)S(1)}, f32[6,1,4,4,128]{4,2,3,1,0:T(4,128)}, u32[]{:S(2)}) copy-start(f32[6,1,4,4,128]{4,2,3,1,0:T(4,128)} %copy-done.5) | copy-start | bytes 147460
  52.9 0.8 %copy-start.12 = (f32[1,4,4,4,128]{4,2,3,1,0:T(4,128)S(1)}, f32[1,4,4,4,128]{4,2,3,1,0:T(4,128)}, u32[]{:S(2)}) copy-start(f32[1,4,4,4,128]{4,2,3,1,0:T(4,128)} %copy-done.11) | copy-start | bytes 98308
  52.9 0.8 %copy-start.14 = (f32[1,4,4,4,128]{4,2,3,1,0:T(4,128)S(1)}, f32[1,4,4,4,128]{4,2,3,1,0:T(4,128)}, u32[]{:S(2)}) copy-start(f32[1,4,4,4,128]{4,2,3,1,0:T(4,128)} %copy-done.13) | copy-start | bytes 98308
  54.2 5.9 %collective-permute-start.24 = (f32[4,4,1,4,128]{4,2,3,1,0:T(1,128)S(1)}, f32[4,4,1,4,128]{4,2,3,1,0:T(1,128)S(1)}, u32[]{:S(2)}, u32[]{:S(2)}) collective-permute-start(f32[4,4,1,4,128]{4,2,3,1,0:T(1,128)S(1)} %get-tuple-element.16), channel_id=1, source_target_pairs={{0,1},{1,2},{2,3},{3,0},{4,5},{5,6},{6,7},{7,4},{8,9},{9,10},{10,1... | collective-permute-start | bytes 98312 | tf_op jit(solution)/shard_map/ppermute | solution.py:24
  54.8 10.5 %collective-permute-start.22 = (f32[4,2,4,4,128]{4,2,3,1,0:T(4,128)S(1)}, f32[4,2,4,4,128]{4,2,3,1,0:T(4,128)S(1)}, u32[]{:S(2)}, u32[]{:S(2)}) collective-permute-start(f32[4,2,4,4,128]{4,2,3,1,0:T(4,128)S(1)} %pad_maximum_fusion.54), channel_id=1, source_target_pairs={{0,4},{4,0},{1,5},{5,1},{2,6},{6,2},{3,7},{7,3},{8,12},{12,8},{9,1... | collective-permute-start | bytes 196616 | tf_op jit(solution)/shard_map/ppermute | solution.py:37
  56.4 3.9 %collective-permute-start.20 = (f32[1,4,4,4,128]{4,2,3,1,0:T(4,128)S(1)}, f32[1,4,4,4,128]{4,2,3,1,0:T(4,128)S(1)}, u32[]{:S(2)}, u32[]{:S(2)}) collective-permute-start(f32[1,4,4,4,128]{4,2,3,1,0:T(4,128)S(1)} %get-tuple-element.18), channel_id=1, source_target_pairs={{0,24},{8,0},{16,8},{24,16},{1,25},{9,1},{17,9},{25,17},{2,26},{10... | collective-permute-start | bytes 98312 | tf_op jit(solution)/shard_map/ppermute | solution.py:24
  58.5 5.7 %collective-permute-start.21 = (f32[1,4,4,4,128]{4,2,3,1,0:T(4,128)S(1)}, f32[1,4,4,4,128]{4,2,3,1,0:T(4,128)S(1)}, u32[]{:S(2)}, u32[]{:S(2)}) collective-permute-start(f32[1,4,4,4,128]{4,2,3,1,0:T(4,128)S(1)} %get-tuple-element.17), channel_id=1, source_target_pairs={{0,8},{8,16},{16,24},{24,0},{1,9},{9,17},{17,25},{25,1},{2,10},{10... | collective-permute-start | bytes 98312 | tf_op jit(solution)/shard_map/ppermute | solution.py:24
  58.5 6.6 %collective-permute-start.23 = (f32[4,4,1,4,128]{4,2,3,1,0:T(1,128)S(1)}, f32[4,4,1,4,128]{4,2,3,1,0:T(1,128)S(1)}, u32[]{:S(2)}, u32[]{:S(2)}) collective-permute-start(f32[4,4,1,4,128]{4,2,3,1,0:T(1,128)S(1)} %get-tuple-element.15), channel_id=1, source_target_pairs={{0,3},{1,0},{2,1},{3,2},{4,7},{5,4},{6,5},{7,6},{8,11},{9,8},{10,9... | collective-permute-start | bytes 98312 | tf_op jit(solution)/shard_map/ppermute | solution.py:24
  64.2 0.9 %copy-start.2 = (f32[1,8,8,4,128]{4,2,3,1,0:T(8,128)S(1)}, f32[1,8,8,4,128]{4,2,3,1,0:T(8,128)}, u32[]{:S(2)}) copy-start(f32[1,8,8,4,128]{4,2,3,1,0:T(8,128)} %copy-done.1) | copy-start | bytes 393220

commit v12 on v11

--- a/solution.py
+++ b/solution.py
@@ -67,10 +67,17 @@
                 cache[step] = shifted(block, axis, step)
                 extras[step] = extra
             else:
-                both = jnp.concatenate([block.reshape(-1), extra.reshape(-1)])
-                both = shifted(both, axis, step)
-                cache[step] = both[: block.size].reshape(block.shape)
-                extras[step] = both[block.size :].reshape(extra.shape)
+                trailing = block.shape[1:]
+                if extra.size % int(np.prod(trailing)) == 0:
+                    both = jnp.concatenate([block, extra.reshape((-1,) + trailing)], axis=0)
+                    both = shifted(both, axis, step)
+                    cache[step] = both[: block.shape[0]]
+                    extras[step] = both[block.shape[0] :].reshape(extra.shape)
+                else:
+                    both = jnp.concatenate([block.reshape(-1), extra.reshape(-1)])
+                    both = shifted(both, axis, step)
+                    cache[step] = both[: block.size].reshape(block.shape)
+                    extras[step] = both[block.size :].reshape(extra.shape)
         pieces.append(cache[step])
     return jnp.concatenate(pieces, axis=dim), start, extras
 

time: 69.4 us -> 78.1 us (1.13)
  waiting for transfers between devices: 14.4 us -> 19.1 us
  local copies, waits for them, and re-layouts: 10.2 us -> 14.5 us
  other arithmetic: 8.92 us -> 7 us
  matrix products: 2.44 us -> 3.65 us
    ppermute x15, waiting for transfers between devices: 12.8 us -> 18.3 us  [shifted(): lax.ppermute(block, axis, [(j, (j - step) % count) for j in range(count)])]
    dynamic_update_slice x4, local copies, waits for them, and re-layouts: 2.55 us -> 4.22 us  [gram_matrix(): total = lax.dynamic_update_slice(total, piece[slot], (row, col))]
    unnamed x36 -> x68, local copies, waits for them, and re-layouts: 3.34 us -> 4.91 us
    dot_general x1, matrix products: 0.63 us -> 1.84 us  [coarse_solve(): jnp.einsum('qxyz,xyzgl->qgl', operator, extended, precision=lax.Precision...]
    ppermute x7, waiting for transfers between devices: 1.04 us -> 0.02 us  [fetch(): cache[steps] = lax.ppermute(block, tuple(axes), pairs)]
    sub x1, other arithmetic: 1.86 us -> 0.95 us  [vcycle(): rhs_one = restrict(rhs_zero - stencil(corr_zero, faces_zero, 0))]
    add x2, other arithmetic: 1.06 us -> 0.16 us  [post_smooth(): hi = corr_faces[dim][1] + prolong_face(coarse_face_list[dim][1], dim)]
    slice x3 -> x12, local copies, waits for them, and re-layouts: 2.17 us -> 2.56 us  [the longest x9 2.55 us: extend_axis(): extras[step] = both[block.shape[0]:].reshape(extra.shape)]
  transfers between devices with their start and end apart: 25 -> 25, of which waited for: 9 -> 10; matrix products, arithmetic and copies ran while one was open for 11% -> 10% of each run, Pallas kernels for 0% -> 0%
where the time goes in v12:
time: 78.1 us; the launch traced here: 77.5 us
  starting transfers between devices  27.2 us (35%)
  waiting for transfers between devices  19.1 us (24%)
  local copies, waits for them, and re-layouts  14.5 us (19%)
  other arithmetic  7 us (9%)
  between operations  6.02 us (8%)
  matrix products  3.65 us (5%)
    ppermute x15, waiting for transfers between devices, shifted(): lax.ppermute(block, axis, [(j, (j - step) % count) for j in range(count)])  18.3 us
    ppermute x15, starting transfers between devices, shifted(): lax.ppermute(block, axis, [(j, (j - step) % count) for j in range(count)])  15 us
    ppermute x7, starting transfers between devices, fetch(): cache[steps] = lax.ppermute(block, tuple(axes), pairs)  7.41 us
    unnamed x68, local copies, waits for them, and re-layouts  4.91 us
    ppermute x3, starting transfers between devices, axis_faces(): lax.ppermute(jnp.concatenate([first, last], axis=dim), axis, [(0, 1), (1,...  4.75 us
    dynamic_update_slice x4, local copies, waits for them, and re-layouts, gram_matrix(): total = lax.dynamic_update_slice(total, piece[slot], (row, col))  4.22 us
    slice x9, local copies, waits for them, and re-layouts, extend_axis(): extras[step] = both[block.shape[0]:].reshape(extra.shape)  2.55 us
    dot_general x1, matrix products, coarse_solve(): jnp.einsum('qxyz,xyzgl->qgl', operator, extended, precision=lax.Precision...  1.84 us
  transfers between devices with their start and end apart: 25, of which 10 were waited for; matrix products, arithmetic and copies ran while one was open for 10% of the time, Pallas kernels for 0%

profile of v12, /device:TPU:0, one launch (start us, length us, event | category | flops | bytes accessed | tf_op | source)
XLA Modules:
  0.0 77.5 jit_solution(7387951765654670709)
XLA Ops:
  0.0 1.5 %fusion.56 = (f32[8,8,1,4,128]{4,2,3,1,0:T(1,128)S(1)}, f32[8,8,1,4,128]{4,2,3,1,0:T(1,128)S(1)}) fusion(bf16[8,8,8,4,128]{4,2,3,1,0:T(8,128)(2,1)} %bitcast.69), kind=kLoop, calls=%fused_computation.129 | loop fusion | flops 131072 | bytes 393216 | tf_op jit(solution)/shard_map/div | solution.py:307
  1.5 0.5 collective-permute-start.4
  2.2 2.6 %collective-permute-start.2 = (f32[8,2,8,4,128]{4,2,3,1,0:T(8,128)S(1)}, f32[8,2,8,4,128]{4,2,3,1,0:T(8,128)S(1)}, u32[]{:S(2)}, u32[]{:S(2)}) collective-permute-start(f32[8,2,8,4,128]{4,2,3,1,0:T(8,128)S(1)} %pad_maximum_fusion.32), channel_id=1, source_target_pairs={{0,4},{4,0},{1,5},{5,1},{2,6},{6,2},{3,7},{7,3},{8,12},{12,8},{9,1... | collective-permute-start | bytes 786440 | tf_op jit(solution)/shard_map/ppermute | solution.py:37
  4.8 3.7 %collective-permute-start = (f32[1,8,8,4,128]{4,2,3,1,0:T(8,128)S(1)}, f32[1,8,8,4,128]{4,2,3,1,0:T(8,128)S(1)}, u32[]{:S(2)}, u32[]{:S(2)}) collective-permute-start(f32[1,8,8,4,128]{4,2,3,1,0:T(8,128)S(1)} %get-tuple-element.8), channel_id=1, source_target_pairs={{0,24},{8,0},{16,8},{24,16},{1,25},{9,1},{17,9},{25,17},{2,26},{10... | collective-permute-start | bytes 393224 | tf_op jit(solution)/shard_map/ppermute | solution.py:24
  8.4 1.2 %collective-permute-start.3 = (f32[8,8,1,4,128]{4,2,3,1,0:T(1,128)S(1)}, f32[8,8,1,4,128]{4,2,3,1,0:T(1,128)S(1)}, u32[]{:S(2)}, u32[]{:S(2)}) collective-permute-start(f32[8,8,1,4,128]{4,2,3,1,0:T(1,128)S(1)} %get-tuple-element.5), channel_id=1, source_target_pairs={{0,3},{1,0},{2,1},{3,2},{4,7},{5,4},{6,5},{7,6},{8,11},{9,8},{10,9... | collective-permute-start | bytes 393224 | tf_op jit(solution)/shard_map/ppermute | solution.py:24
  9.6 0.7 copy.25
  10.9 1.1 %collective-permute-done = f32[1,8,8,4,128]{4,2,3,1,0:T(8,128)S(1)} collective-permute-done((f32[1,8,8,4,128]{4,2,3,1,0:T(8,128)S(1)}, f32[1,8,8,4,128]{4,2,3,1,0:T(8,128)S(1)}, u32[]{:S(2)}, u32[]{:S(2)}) %collective-permute-start) | collective-permute-done | bytes 131104 | tf_op jit(solution)/shard_map/ppermute | solution.py:24
  12.0 4.5 %collective-permute-done.1 = f32[1,8,8,4,128]{4,2,3,1,0:T(8,128)S(1)} collective-permute-done((f32[1,8,8,4,128]{4,2,3,1,0:T(8,128)S(1)}, f32[1,8,8,4,128]{4,2,3,1,0:T(8,128)S(1)}, u32[]{:S(2)}, u32[]{:S(2)}) %collective-permute-start.1) | collective-permute-done | bytes 131104 | tf_op jit(solution)/shard_map/ppermute | solution.py:24
  16.6 0.9 %convert_subtract_fusion.1 = f32[8,8,8,4,128]{4,2,3,1,0:T(8,128)S(1)} fusion(f32[8,8,1,4,128]{4,2,3,1,0:T(1,128)S(1)} %collective-permute-done.4, f32[10,1,8,4,128]{4,2,3,1,0:T(8,128)S(1)} %pad.40, f32[10,1,8,4,128]{4,2,3,1,0:T(8,128)S(1)} %pad.41, f32[1,8,8,4,128]{4,2,3,1,0:T(8,128)S(1)} %collective-permute-done, ...), kind=kLoop, calls=%fused_computation.1 | loop fusion | flops 8912896 | bytes 3473408 | tf_op jit(solution)/shard_map/sub | solution.py:310
  17.5 0.7 reduce_sum.18
  18.5 0.6 collective-permute-start.6
  19.3 1.5 %collective-permute-start.8 = (f32[1,4,4,4,128]{4,2,3,1,0:T(4,128)S(1)}, f32[1,4,4,4,128]{4,2,3,1,0:T(4,128)S(1)}, u32[]{:S(2)}, u32[]{:S(2)}) collective-permute-start(f32[1,4,4,4,128]{4,2,3,1,0:T(4,128)S(1)} %get-tuple-element.24), channel_id=1, source_target_pairs={{0,24},{8,0},{16,8},{24,16},{1,25},{9,1},{17,9},{25,17},{2,26},{10... | collective-permute-start | bytes 98312 | tf_op jit(solution)/shard_map/ppermute | solution.py:24
  20.7 0.6 collective-permute-start.7
  21.3 1.1 %collective-permute-done.5 = f32[4,4,1,4,128]{4,2,3,1,0:T(1,128)S(1)} collective-permute-done((f32[4,4,1,4,128]{4,2,3,1,0:T(1,128)S(1)}, f32[4,4,1,4,128]{4,2,3,1,0:T(1,128)S(1)}, u32[]{:S(2)}, u32[]{:S(2)}) %collective-permute-start.5) | collective-permute-done | bytes 32800 | tf_op jit(solution)/shard_map/ppermute | solution.py:24
  22.5 0.6 collective-permute-done.6
  23.2 3.3 %collective-permute-done.7 = f32[1,4,4,4,128]{4,2,3,1,0:T(4,128)S(1)} collective-permute-done((f32[1,4,4,4,128]{4,2,3,1,0:T(4,128)S(1)}, f32[1,4,4,4,128]{4,2,3,1,0:T(4,128)S(1)}, u32[]{:S(2)}, u32[]{:S(2)}) %collective-permute-start.7) | collective-permute-done | bytes 32800 | tf_op jit(solution)/shard_map/ppermute | solution.py:24
  26.7 0.4 copy-done.19
  27.1 0.7 copy-done.11
  28.0 0.6 collective-permute-start.11
  28.6 3.2 %collective-permute-start.10 = (f32[10,2,2,4,128]{4,2,1,3,0:T(2,128)S(1)}, f32[10,2,2,4,128]{4,2,1,3,0:T(2,128)S(1)}, u32[]{:S(2)}, u32[]{:S(2)}) collective-permute-start(f32[10,2,2,4,128]{4,2,1,3,0:T(2,128)S(1)} %pad_maximum_fusion.51), channel_id=1, source_target_pairs={{0,24},{8,0},{16,8},{24,16},{1,25},{9,1},{17,9},{25,17},{2,26},{10... | collective-permute-start | bytes 245768 | tf_op jit(solution)/shard_map/ppermute | solution.py:24
  31.9 3.3 %collective-permute-done.12 = f32[10,2,2,4,128]{4,2,1,3,0:T(2,128)S(1)} collective-permute-done((f32[10,2,2,4,128]{4,2,1,3,0:T(2,128)S(1)}, f32[10,2,2,4,128]{4,2,1,3,0:T(2,128)S(1)}, u32[]{:S(2)}, u32[]{:S(2)}) %collective-permute-start.12) | collective-permute-done | bytes 81952 | tf_op jit(solution)/shard_map/ppermute | solution.py:24
  35.2 2.6 %collective-permute-done.11 = f32[10,2,2,4,128]{4,2,1,3,0:T(2,128)S(1)} collective-permute-done((f32[10,2,2,4,128]{4,2,1,3,0:T(2,128)S(1)}, f32[10,2,2,4,128]{4,2,1,3,0:T(2,128)S(1)}, u32[]{:S(2)}, u32[]{:S(2)}) %collective-permute-start.11) | collective-permute-done | bytes 81952 | tf_op jit(solution)/shard_map/ppermute | solution.py:24
  37.8 0.7 pad_maximum_fusion.53
  38.6 1.4 %collective-permute-start.18 = (f32[8,2,2,4,128]{4,2,1,3,0:T(2,128)}, f32[8,2,2,4,128]{4,2,1,3,0:T(2,128)S(1)}, u32[]{:S(2)}, u32[]{:S(2)}) collective-permute-start(f32[8,2,2,4,128]{4,2,1,3,0:T(2,128)} %pad_maximum_fusion.53), channel_id=1, source_target_pairs={{6,0},{7,1},{4,2},{5,3},{2,4},{3,5},{0,6},{1,7},{14,8},{15,9},{12,... | collective-permute-start | bytes 196616 | tf_op jit(solution)/shard_map/ppermute | solution.py:108
  40.2 0.7 copy-done.27
  40.9 0.7 constant_dynamic-slice_fusion
  42.9 2.3 %collective-permute-start.17 = (f32[8,2,2,4,128]{4,2,1,3,0:T(2,128)}, f32[8,2,2,4,128]{4,2,1,3,0:T(2,128)}, u32[]{:S(2)}, u32[]{:S(2)}) collective-permute-start(f32[8,2,2,4,128]{4,2,1,3,0:T(2,128)} %pad_maximum_fusion.53), channel_id=1, source_target_pairs={{5,0},{6,1},{7,2},{4,3},{1,4},{2,5},{3,6},{0,7},{13,8},{14,9},{15,... | collective-permute-start | bytes 196616 | tf_op jit(solution)/shard_map/ppermute | solution.py:108
  45.2 0.5 collective-permute-start.16
  45.7 1.7 %collective-permute-start.14 = (f32[8,2,2,4,128]{4,2,1,3,0:T(2,128)}, f32[8,2,2,4,128]{4,2,1,3,0:T(2,128)}, u32[]{:S(2)}, u32[]{:S(2)}) collective-permute-start(f32[8,2,2,4,128]{4,2,1,3,0:T(2,128)} %pad_maximum_fusion.53), channel_id=1, source_target_pairs={{2,0},{3,1},{0,2},{1,3},{6,4},{7,5},{4,6},{5,7},{10,8},{11,9},{8,1... | collective-permute-start | bytes 196616 | tf_op jit(solution)/shard_map/ppermute | solution.py:108
  47.4 0.6 copy-done.31
  48.1 1.4 %collective-permute-start.13 = (f32[8,2,2,4,128]{4,2,1,3,0:T(2,128)}, f32[8,2,2,4,128]{4,2,1,3,0:T(2,128)}, u32[]{:S(2)}, u32[]{:S(2)}) collective-permute-start(f32[8,2,2,4,128]{4,2,1,3,0:T(2,128)} %pad_maximum_fusion.53), channel_id=1, source_target_pairs={{1,0},{2,1},{3,2},{0,3},{5,4},{6,5},{7,6},{4,7},{9,8},{10,9},{11,1... | collective-permute-start | bytes 196616 | tf_op jit(solution)/shard_map/ppermute | solution.py:108
  53.4 0.8 %slice-done = f32[8,2,2,4,128]{4,2,1,3,0:T(2,128)S(1)} async-done(((f32[10,2,2,4,128]{4,2,1,3,0:T(2,128)}), f32[8,2,2,4,128]{4,2,1,3,0:T(2,128)S(1)}, s32[]{:S(2)}) %slice-start) | async-done | bytes 65560 | tf_op jit(solution)/shard_map/slice | solution.py:75
  54.2 0.8 %slice-done.1 = f32[8,2,2,4,128]{4,2,1,3,0:T(2,128)S(1)} async-done(((f32[10,2,2,4,128]{4,2,1,3,0:T(2,128)}), f32[8,2,2,4,128]{4,2,1,3,0:T(2,128)S(1)}, s32[]{:S(2)}) %slice-start.1) | async-done | bytes 65560 | tf_op jit(solution)/shard_map/slice | solution.py:75
  55.1 0.8 %slice-done.2 = f32[8,2,2,4,128]{4,2,1,3,0:T(2,128)S(1)} async-done(((f32[10,2,2,4,128]{4,2,1,3,0:T(2,128)}), f32[8,2,2,4,128]{4,2,1,3,0:T(2,128)S(1)}, s32[]{:S(2)}) %slice-start.2) | async-done | bytes 65560 | tf_op jit(solution)/shard_map/slice | solution.py:75
  56.0 0.9 %dynamic_update_slice.13 = f32[512,512]{1,0:T(8,128)S(1)} dynamic-update-slice(f32[512,512]{1,0:T(8,128)S(1)} %bitcast_dynamic-update-slice_fusion, f32[128,128]{1,0:T(8,128)S(1)} %bitcast.92, s32[]{:T(128)S(6)} %select_n.65, s32[]{:T(128)S(6)} %select_n.66) | dynamic-update-slice | bytes 131076 | tf_op jit(solution)/shard_map/dynamic_update_slice | solution.py:301
  56.9 1.7 %dynamic_update_slice.14 = f32[512,512]{1,0:T(8,128)S(1)} dynamic-update-slice(f32[512,512]{1,0:T(8,128)S(1)} %dynamic_update_slice.13, f32[128,128]{1,0:T(8,128)S(1)} %bitcast.93, s32[]{:T(128)S(6)} %select_n.69, s32[]{:T(128)S(6)} %select_n.70) | dynamic-update-slice | bytes 131076 | tf_op jit(solution)/shard_map/dynamic_update_slice | solution.py:301
  58.6 1.7 %dynamic_update_slice.15 = f32[512,512]{1,0:T(8,128)S(1)} dynamic-update-slice(f32[512,512]{1,0:T(8,128)S(1)} %dynamic_update_slice.14, f32[128,128]{1,0:T(8,128)S(1)} %bitcast.91, s32[]{:T(128)S(6)} %select_n.73, s32[]{:T(128)S(6)} %select_n.74) | dynamic-update-slice | bytes 131076 | tf_op jit(solution)/shard_map/dynamic_update_slice | solution.py:301
  60.4 1.8 %convolution_bitcast_fusion = f32[216,4,128]{2,0,1:T(8,128)S(1)} fusion(f32[216,8,4,8,1]{0,3,2,4,1:T(8,128)S(1)} %copy-done.33, f32[8,2,2,4,128]{4,2,1,3,0:T(2,128)S(1)} %copy-done.30, f32[8,2,2,4,128]{4,2,1,3,0:T(2,128)S(1)} %copy-done.32, f32[8,2,2,4,128]{4,2,1,3,0:T(2,128)} %collective-permute-done.17, f32[8,2,2,4,128]{4,2,1,3,0:T(2,128)} %collective-permute-done.16, ...), kind=kOutput, calls=%fused_computation.5 | convolution fusion | flops 341049344 | bytes 1187840 | tf_op jit(solution)/shard_map/qxyz,xyzgl->qgl/dot_general | solution.py:195
  62.4 0.6 copy-done.6
  63.6 1.6 %collective-permute-start.22 = (f32[4,2,4,4,128]{4,2,3,1,0:T(4,128)S(1)}, f32[4,2,4,4,128]{4,2,3,1,0:T(4,128)S(1)}, u32[]{:S(2)}, u32[]{:S(2)}) collective-permute-start(f32[4,2,4,4,128]{4,2,3,1,0:T(4,128)S(1)} %pad_maximum_fusion.54), channel_id=1, source_target_pairs={{0,4},{4,0},{1,5},{5,1},{2,6},{6,2},{3,7},{7,3},{8,12},{12,8},{9,1... | collective-permute-start | bytes 196616 | tf_op jit(solution)/shard_map/ppermute | solution.py:37
  65.2 2.1 %collective-permute-start.20 = (f32[1,4,4,4,128]{4,2,3,1,0:T(4,128)S(1)}, f32[1,4,4,4,128]{4,2,3,1,0:T(4,128)S(1)}, u32[]{:S(2)}, u32[]{:S(2)}) collective-permute-start(f32[1,4,4,4,128]{4,2,3,1,0:T(4,128)S(1)} %get-tuple-element.18), channel_id=1, source_target_pairs={{0,24},{8,0},{16,8},{24,16},{1,25},{9,1},{17,9},{25,17},{2,26},{10... | collective-permute-start | bytes 98312 | tf_op jit(solution)/shard_map/ppermute | solution.py:24
  67.5 1.2 %collective-permute-start.23 = (f32[4,4,1,4,128]{4,2,3,1,0:T(1,128)S(1)}, f32[4,4,1,4,128]{4,2,3,1,0:T(1,128)S(1)}, u32[]{:S(2)}, u32[]{:S(2)}) collective-permute-start(f32[4,4,1,4,128]{4,2,3,1,0:T(1,128)S(1)} %get-tuple-element.15), channel_id=1, source_target_pairs={{0,3},{1,0},{2,1},{3,2},{4,7},{5,4},{6,5},{7,6},{8,11},{9,8},{10,9... | collective-permute-start | bytes 98312 | tf_op jit(solution)/shard_map/ppermute | solution.py:24
  68.8 0.6 broadcast_in_dim.80
  69.9 0.8 %copy-done.4 = f32[1,8,8,4,128]{4,2,3,1,0:T(8,128)S(1)} copy-done((f32[1,8,8,4,128]{4,2,3,1,0:T(8,128)S(1)}, f32[1,8,8,4,128]{4,2,3,1,0:T(8,128)}, u32[]{:S(2)}) %copy-start.4) | copy-done | bytes 131096
  70.7 2.3 %collective-permute-done.21 = f32[1,4,4,4,128]{4,2,3,1,0:T(4,128)S(1)} collective-permute-done((f32[1,4,4,4,128]{4,2,3,1,0:T(4,128)S(1)}, f32[1,4,4,4,128]{4,2,3,1,0:T(4,128)S(1)}, u32[]{:S(2)}, u32[]{:S(2)}) %collective-permute-start.21) | collective-permute-done | bytes 32800 | tf_op jit(solution)/shard_map/ppermute | solution.py:24
  73.1 0.8 %copy-done.2 = f32[1,8,8,4,128]{4,2,3,1,0:T(8,128)S(1)} copy-done((f32[1,8,8,4,128]{4,2,3,1,0:T(8,128)S(1)}, f32[1,8,8,4,128]{4,2,3,1,0:T(8,128)}, u32[]{:S(2)}) %copy-start.2) | copy-done | bytes 131096
  74.4 1.0 %fusion.2 = f32[8,8,8,4,128]{4,2,3,1,0:T(8,128)S(1)} fusion(f32[8,8,8,4,128]{4,2,3,1,0:T(8,128)S(1)} %fusion.41, f32[8,8,1,4,128]{4,2,3,1,0:T(1,128)S(1)} %add.236, f32[10,1,8,4,128]{4,2,3,1,0:T(8,128)S(1)} %pad.48, f32[10,1,8,4,128]{4,2,3,1,0:T(8,128)S(1)} %pad.49, f32[1,8,8,4,128]{4,2,3,1,0:T(8,128)S(1)} %add.227, f32[1,8,8,4,128]{4,2,3,1,0:T(8,128)S(1)} %add.228, ...), kind=kLoop, calls=%fused_computation.8 | loop fusion | flops 9437184 | bytes 3473408 | tf_op jit(solution)/shard_map/add | solution.py:270
  75.7 1.8 %convolution_convert_fusion = bf16[512,512]{1,0:T(8,128)(2,1)} fusion(f32[512,512]{1,0:T(8,128)S(1)} %bitcast_multiply_fusion, f32[512,512]{1,0:T(8,128)S(1)} %dynamic_update_slice.15), kind=kOutput, calls=%fused_computation.4 | convolution fusion | flops 805568512 | bytes 2621440 | tf_op jit(solution)/shard_map/dot_general | solution.py:338
  (157 shorter events, 4.3 us)
Async XLA Ops:
  0.0 2.1 %copy-start = (bf16[8,8,8,512]{3,2,1,0:T(8,128)(2,1)S(1)}, bf16[8,8,8,512]{3,2,1,0:T(8,128)(2,1)}, u32[]{:S(2)}) copy-start(bf16[8,8,8,512]{3,2,1,0:T(8,128)(2,1)} %param.5) | copy-start | bytes 1572868
  1.5 9.4 %collective-permute-start.4 = (f32[8,8,1,4,128]{4,2,3,1,0:T(1,128)S(1)}, f32[8,8,1,4,128]{4,2,3,1,0:T(1,128)S(1)}, u32[]{:S(2)}, u32[]{:S(2)}) collective-permute-start(f32[8,8,1,4,128]{4,2,3,1,0:T(1,128)S(1)} %get-tuple-element.6), channel_id=1, source_target_pairs={{0,1},{1,2},{2,3},{3,0},{4,5},{5,6},{6,7},{7,4},{8,9},{9,10},{10,1... | collective-permute-start | bytes 393224 | tf_op jit(solution)/shard_map/ppermute | solution.py:24
  2.2 7.5 %copy-start.9 = (f32[1,128,128]{2,1,0:T(8,128)S(1)}, f32[1,128,128]{2,1,0:T(8,128)}, u32[]{:S(2)}) copy-start(f32[1,128,128]{2,1,0:T(8,128)} %param.8) | copy-start | bytes 196612
  2.2 8.7 %collective-permute-start.2 = (f32[8,2,8,4,128]{4,2,3,1,0:T(8,128)S(1)}, f32[8,2,8,4,128]{4,2,3,1,0:T(8,128)S(1)}, u32[]{:S(2)}, u32[]{:S(2)}) collective-permute-start(f32[8,2,8,4,128]{4,2,3,1,0:T(8,128)S(1)} %pad_maximum_fusion.32), channel_id=1, source_target_pairs={{0,4},{4,0},{1,5},{5,1},{2,6},{6,2},{3,7},{7,3},{8,12},{12,8},{9,1... | collective-permute-start | bytes 786440 | tf_op jit(solution)/shard_map/ppermute | solution.py:37
  4.8 7.3 %collective-permute-start = (f32[1,8,8,4,128]{4,2,3,1,0:T(8,128)S(1)}, f32[1,8,8,4,128]{4,2,3,1,0:T(8,128)S(1)}, u32[]{:S(2)}, u32[]{:S(2)}) collective-permute-start(f32[1,8,8,4,128]{4,2,3,1,0:T(8,128)S(1)} %get-tuple-element.8), channel_id=1, source_target_pairs={{0,24},{8,0},{16,8},{24,16},{1,25},{9,1},{17,9},{25,17},{2,26},{10... | collective-permute-start | bytes 393224 | tf_op jit(solution)/shard_map/ppermute | solution.py:24
  8.4 8.1 %collective-permute-start.1 = (f32[1,8,8,4,128]{4,2,3,1,0:T(8,128)S(1)}, f32[1,8,8,4,128]{4,2,3,1,0:T(8,128)S(1)}, u32[]{:S(2)}, u32[]{:S(2)}) collective-permute-start(f32[1,8,8,4,128]{4,2,3,1,0:T(8,128)S(1)} %get-tuple-element.7), channel_id=1, source_target_pairs={{0,8},{8,16},{16,24},{24,0},{1,9},{9,17},{17,25},{25,1},{2,10},{10... | collective-permute-start | bytes 393224 | tf_op jit(solution)/shard_map/ppermute | solution.py:24
  8.4 8.1 %collective-permute-start.3 = (f32[8,8,1,4,128]{4,2,3,1,0:T(1,128)S(1)}, f32[8,8,1,4,128]{4,2,3,1,0:T(1,128)S(1)}, u32[]{:S(2)}, u32[]{:S(2)}) collective-permute-start(f32[8,8,1,4,128]{4,2,3,1,0:T(1,128)S(1)} %get-tuple-element.5), channel_id=1, source_target_pairs={{0,3},{1,0},{2,1},{3,2},{4,7},{5,4},{6,5},{7,6},{8,11},{9,8},{10,9... | collective-permute-start | bytes 393224 | tf_op jit(solution)/shard_map/ppermute | solution.py:24
  12.0 5.5 %copy-start.3 = (f32[1,8,8,4,128]{4,2,3,1,0:T(8,128)}, f32[1,8,8,4,128]{4,2,3,1,0:T(8,128)S(1)}, u32[]{:S(2)}) copy-start(f32[1,8,8,4,128]{4,2,3,1,0:T(8,128)S(1)} %collective-permute-done) | copy-start | bytes 393220
  16.6 1.0 %copy-start.1 = (f32[1,8,8,4,128]{4,2,3,1,0:T(8,128)}, f32[1,8,8,4,128]{4,2,3,1,0:T(8,128)S(1)}, u32[]{:S(2)}) copy-start(f32[1,8,8,4,128]{4,2,3,1,0:T(8,128)S(1)} %collective-permute-done.1) | copy-start | bytes 393220
  18.4 2.9 %collective-permute-start.9 = (f32[4,4,1,4,128]{4,2,3,1,0:T(1,128)S(1)}, f32[4,4,1,4,128]{4,2,3,1,0:T(1,128)S(1)}, u32[]{:S(2)}, u32[]{:S(2)}) collective-permute-start(f32[4,4,1,4,128]{4,2,3,1,0:T(1,128)S(1)} %get-tuple-element.22), channel_id=1, source_target_pairs={{0,3},{1,0},{2,1},{3,2},{4,7},{5,4},{6,5},{7,6},{8,11},{9,8},{10,9... | collective-permute-start | bytes 98312 | tf_op jit(solution)/shard_map/ppermute | solution.py:24
  18.5 4.6 %collective-permute-start.6 = (f32[4,2,4,4,128]{4,2,3,1,0:T(4,128)S(1)}, f32[4,2,4,4,128]{4,2,3,1,0:T(4,128)S(1)}, u32[]{:S(2)}, u32[]{:S(2)}) collective-permute-start(f32[4,2,4,4,128]{4,2,3,1,0:T(4,128)S(1)} %pad_maximum_fusion.52), channel_id=1, source_target_pairs={{0,4},{4,0},{1,5},{5,1},{2,6},{6,2},{3,7},{7,3},{8,12},{12,8},{9,1... | collective-permute-start | bytes 196616 | tf_op jit(solution)/shard_map/ppermute | solution.py:37
  19.0 3.4 %collective-permute-start.5 = (f32[4,4,1,4,128]{4,2,3,1,0:T(1,128)S(1)}, f32[4,4,1,4,128]{4,2,3,1,0:T(1,128)S(1)}, u32[]{:S(2)}, u32[]{:S(2)}) collective-permute-start(f32[4,4,1,4,128]{4,2,3,1,0:T(1,128)S(1)} %get-tuple-element.21), channel_id=1, source_target_pairs={{0,1},{1,2},{2,3},{3,0},{4,5},{5,6},{6,7},{7,4},{8,9},{9,10},{10,1... | collective-permute-start | bytes 98312 | tf_op jit(solution)/shard_map/ppermute | solution.py:24
  19.3 3.9 %collective-permute-start.8 = (f32[1,4,4,4,128]{4,2,3,1,0:T(4,128)S(1)}, f32[1,4,4,4,128]{4,2,3,1,0:T(4,128)S(1)}, u32[]{:S(2)}, u32[]{:S(2)}) collective-permute-start(f32[1,4,4,4,128]{4,2,3,1,0:T(4,128)S(1)} %get-tuple-element.24), channel_id=1, source_target_pairs={{0,24},{8,0},{16,8},{24,16},{1,25},{9,1},{17,9},{25,17},{2,26},{10... | collective-permute-start | bytes 98312 | tf_op jit(solution)/shard_map/ppermute | solution.py:24
  20.7 5.7 %collective-permute-start.7 = (f32[1,4,4,4,128]{4,2,3,1,0:T(4,128)S(1)}, f32[1,4,4,4,128]{4,2,3,1,0:T(4,128)S(1)}, u32[]{:S(2)}, u32[]{:S(2)}) collective-permute-start(f32[1,4,4,4,128]{4,2,3,1,0:T(4,128)S(1)} %get-tuple-element.23), channel_id=1, source_target_pairs={{0,8},{8,16},{16,24},{24,0},{1,9},{9,17},{17,25},{25,1},{2,10},{10... | collective-permute-start | bytes 98312 | tf_op jit(solution)/shard_map/ppermute | solution.py:24
  23.0 3.6 %copy-start.5 = (f32[6,1,4,4,128]{4,2,3,1,0:T(4,128)}, f32[6,1,4,4,128]{4,2,3,1,0:T(4,128)S(1)}, u32[]{:S(2)}) copy-start(f32[6,1,4,4,128]{4,2,3,1,0:T(4,128)S(1)} %pad.46) | copy-start | bytes 147460
  23.1 3.6 %copy-start.7 = (f32[6,1,4,4,128]{4,2,3,1,0:T(4,128)}, f32[6,1,4,4,128]{4,2,3,1,0:T(4,128)S(1)}, u32[]{:S(2)}) copy-start(f32[6,1,4,4,128]{4,2,3,1,0:T(4,128)S(1)} %pad.45) | copy-start | bytes 147460
  23.2 3.5 %copy-start.17 = (f32[1,4,4,4,128]{4,2,3,1,0:T(4,128)}, f32[1,4,4,4,128]{4,2,3,1,0:T(4,128)S(1)}, u32[]{:S(2)}) copy-start(f32[1,4,4,4,128]{4,2,3,1,0:T(4,128)S(1)} %collective-permute-done.8) | copy-start | bytes 98308
  27.9 9.9 %copy-start.15 = (f32[2,2,2,4,128]{4,2,1,3,0:T(2,128)}, f32[2,2,2,4,128]{4,2,1,3,0:T(2,128)S(1)}, u32[]{:S(2)}) copy-start(f32[2,2,2,4,128]{4,2,1,3,0:T(2,128)S(1)} %copy_multiply_fusion) | copy-start | bytes 49156
  27.9 7.3 %collective-permute-start.12 = (f32[10,2,2,4,128]{4,2,1,3,0:T(2,128)S(1)}, f32[10,2,2,4,128]{4,2,1,3,0:T(2,128)S(1)}, u32[]{:S(2)}, u32[]{:S(2)}) collective-permute-start(f32[10,2,2,4,128]{4,2,1,3,0:T(2,128)S(1)} %pad_maximum_fusion.51), channel_id=1, source_target_pairs={{0,8},{8,16},{16,24},{24,0},{1,9},{9,17},{17,25},{25,1},{2,10},{10... | collective-permute-start | bytes 245768 | tf_op jit(solution)/shard_map/ppermute | solution.py:24
  28.0 9.8 %collective-permute-start.11 = (f32[10,2,2,4,128]{4,2,1,3,0:T(2,128)S(1)}, f32[10,2,2,4,128]{4,2,1,3,0:T(2,128)S(1)}, u32[]{:S(2)}, u32[]{:S(2)}) collective-permute-start(f32[10,2,2,4,128]{4,2,1,3,0:T(2,128)S(1)} %pad_maximum_fusion.51), channel_id=1, source_target_pairs={{0,16},{8,24},{16,0},{24,8},{1,17},{9,25},{17,1},{25,9},{2,18},{10... | collective-permute-start | bytes 245768 | tf_op jit(solution)/shard_map/ppermute | solution.py:24
  28.6 9.2 %collective-permute-start.10 = (f32[10,2,2,4,128]{4,2,1,3,0:T(2,128)S(1)}, f32[10,2,2,4,128]{4,2,1,3,0:T(2,128)S(1)}, u32[]{:S(2)}, u32[]{:S(2)}) collective-permute-start(f32[10,2,2,4,128]{4,2,1,3,0:T(2,128)S(1)} %pad_maximum_fusion.51), channel_id=1, source_target_pairs={{0,24},{8,0},{16,8},{24,16},{1,25},{9,1},{17,9},{25,17},{2,26},{10... | collective-permute-start | bytes 245768 | tf_op jit(solution)/shard_map/ppermute | solution.py:24
  35.2 3.3 %copy-start.14 = (f32[10,2,2,4,128]{4,2,1,3,0:T(2,128)}, f32[10,2,2,4,128]{4,2,1,3,0:T(2,128)S(1)}, u32[]{:S(2)}) copy-start(f32[10,2,2,4,128]{4,2,1,3,0:T(2,128)S(1)} %collective-permute-done.12) | copy-start | bytes 245764
  35.2 3.3 %copy-start.21 = (f32[2,2,2,4,128]{4,2,1,3,0:T(2,128)}, f32[2,2,2,4,128]{4,2,1,3,0:T(2,128)S(1)}, u32[]{:S(2)}) copy-start(f32[2,2,2,4,128]{4,2,1,3,0:T(2,128)S(1)} %slice.302) | copy-start | bytes 49156
  37.8 2.3 %copy-start.12 = (f32[10,2,2,4,128]{4,2,1,3,0:T(2,128)}, f32[10,2,2,4,128]{4,2,1,3,0:T(2,128)S(1)}, u32[]{:S(2)}) copy-start(f32[10,2,2,4,128]{4,2,1,3,0:T(2,128)S(1)} %collective-permute-done.10) | copy-start | bytes 245764
  38.5 7.2 %collective-permute-start.19 = (f32[8,2,2,4,128]{4,2,1,3,0:T(2,128)}, f32[8,2,2,4,128]{4,2,1,3,0:T(2,128)S(1)}, u32[]{:S(2)}, u32[]{:S(2)}) collective-permute-start(f32[8,2,2,4,128]{4,2,1,3,0:T(2,128)} %pad_maximum_fusion.53), channel_id=1, source_target_pairs={{7,0},{4,1},{5,2},{6,3},{3,4},{0,5},{1,6},{2,7},{15,8},{12,9},{13,... | collective-permute-start | bytes 196616 | tf_op jit(solution)/shard_map/ppermute | solution.py:108
  38.6 8.8 %collective-permute-start.18 = (f32[8,2,2,4,128]{4,2,1,3,0:T(2,128)}, f32[8,2,2,4,128]{4,2,1,3,0:T(2,128)S(1)}, u32[]{:S(2)}, u32[]{:S(2)}) collective-permute-start(f32[8,2,2,4,128]{4,2,1,3,0:T(2,128)} %pad_maximum_fusion.53), channel_id=1, source_target_pairs={{6,0},{7,1},{4,2},{5,3},{2,4},{3,5},{0,6},{1,7},{14,8},{15,9},{12,... | collective-permute-start | bytes 196616 | tf_op jit(solution)/shard_map/ppermute | solution.py:108
  42.9 6.7 %copy-start.10 = (f32[1,128,128]{2,1,0:T(8,128)S(1)}, f32[1,128,128]{2,1,0:T(8,128)}, u32[]{:S(2)}) copy-start(f32[1,128,128]{2,1,0:T(8,128)} %param.8) | copy-start | bytes 196612
  42.9 17.4 %collective-permute-start.17 = (f32[8,2,2,4,128]{4,2,1,3,0:T(2,128)}, f32[8,2,2,4,128]{4,2,1,3,0:T(2,128)}, u32[]{:S(2)}, u32[]{:S(2)}) collective-permute-start(f32[8,2,2,4,128]{4,2,1,3,0:T(2,128)} %pad_maximum_fusion.53), channel_id=1, source_target_pairs={{5,0},{6,1},{7,2},{4,3},{1,4},{2,5},{3,6},{0,7},{13,8},{14,9},{15,... | collective-permute-start | bytes 196616 | tf_op jit(solution)/shard_map/ppermute | solution.py:108
  45.2 15.0 %collective-permute-start.16 = (f32[8,2,2,4,128]{4,2,1,3,0:T(2,128)}, f32[8,2,2,4,128]{4,2,1,3,0:T(2,128)}, u32[]{:S(2)}, u32[]{:S(2)}) collective-permute-start(f32[8,2,2,4,128]{4,2,1,3,0:T(2,128)} %pad_maximum_fusion.53), channel_id=1, source_target_pairs={{4,0},{5,1},{6,2},{7,3},{0,4},{1,5},{2,6},{3,7},{12,8},{13,9},{14,... | collective-permute-start | bytes 196616 | tf_op jit(solution)/shard_map/ppermute | solution.py:108
  45.7 14.6 %collective-permute-start.15 = (f32[8,2,2,4,128]{4,2,1,3,0:T(2,128)}, f32[8,2,2,4,128]{4,2,1,3,0:T(2,128)}, u32[]{:S(2)}, u32[]{:S(2)}) collective-permute-start(f32[8,2,2,4,128]{4,2,1,3,0:T(2,128)} %pad_maximum_fusion.53), channel_id=1, source_target_pairs={{3,0},{0,1},{1,2},{2,3},{7,4},{4,5},{5,6},{6,7},{11,8},{8,9},{9,10... | collective-permute-start | bytes 196616 | tf_op jit(solution)/shard_map/ppermute | solution.py:108
  45.7 1.7 %copy-start.29 = (f32[8,2,2,4,128]{4,2,1,3,0:T(2,128)}, f32[8,2,2,4,128]{4,2,1,3,0:T(2,128)S(1)}, u32[]{:S(2)}) copy-start(f32[8,2,2,4,128]{4,2,1,3,0:T(2,128)S(1)} %collective-permute-done.19) | copy-start | bytes 196612
  45.7 14.6 %collective-permute-start.14 = (f32[8,2,2,4,128]{4,2,1,3,0:T(2,128)}, f32[8,2,2,4,128]{4,2,1,3,0:T(2,128)}, u32[]{:S(2)}, u32[]{:S(2)}) collective-permute-start(f32[8,2,2,4,128]{4,2,1,3,0:T(2,128)} %pad_maximum_fusion.53), channel_id=1, source_target_pairs={{2,0},{3,1},{0,2},{1,3},{6,4},{7,5},{4,6},{5,7},{10,8},{11,9},{8,1... | collective-permute-start | bytes 196616 | tf_op jit(solution)/shard_map/ppermute | solution.py:108
  48.1 12.2 %collective-permute-start.13 = (f32[8,2,2,4,128]{4,2,1,3,0:T(2,128)}, f32[8,2,2,4,128]{4,2,1,3,0:T(2,128)}, u32[]{:S(2)}, u32[]{:S(2)}) collective-permute-start(f32[8,2,2,4,128]{4,2,1,3,0:T(2,128)} %pad_maximum_fusion.53), channel_id=1, source_target_pairs={{1,0},{2,1},{3,2},{0,3},{5,4},{6,5},{7,6},{4,7},{9,8},{10,9},{11,1... | collective-permute-start | bytes 196616 | tf_op jit(solution)/shard_map/ppermute | solution.py:108
  54.2 0.8 %slice-start.1 = ((f32[10,2,2,4,128]{4,2,1,3,0:T(2,128)}), f32[8,2,2,4,128]{4,2,1,3,0:T(2,128)S(1)}, s32[]{:S(2)}) async-start(f32[10,2,2,4,128]{4,2,1,3,0:T(2,128)} %copy-done.13), calls=%async_computation.1 | async-start | bytes 131072 | tf_op jit(solution)/shard_map/slice | solution.py:75
  55.9 4.4 %copy-start.33 = (f32[216,8,4,8,1]{0,3,2,4,1:T(8,128)S(1)}, f32[216,8,4,8,1]{0,3,2,4,1:T(8,128)}, u32[]{:S(2)}) copy-start(f32[216,8,4,8,1]{0,3,2,4,1:T(8,128)} %constant.137) | copy-start | bytes 663556
  56.9 3.5 %copy-start.32 = (f32[8,2,2,4,128]{4,2,1,3,0:T(2,128)S(1)}, f32[8,2,2,4,128]{4,2,1,3,0:T(2,128)}, u32[]{:S(2)}) copy-start(f32[8,2,2,4,128]{4,2,1,3,0:T(2,128)} %copy-done.31) | copy-start | bytes 196612
  58.5 1.8 %copy-start.16 = (f32[2,2,2,4,128]{4,2,1,3,0:T(2,128)S(1)}, f32[2,2,2,4,128]{4,2,1,3,0:T(2,128)}, u32[]{:S(2)}) copy-start(f32[2,2,2,4,128]{4,2,1,3,0:T(2,128)} %copy-done.15) | copy-start | bytes 49156
  58.5 1.8 %copy-start.22 = (f32[2,2,2,4,128]{4,2,1,3,0:T(2,128)S(1)}, f32[2,2,2,4,128]{4,2,1,3,0:T(2,128)}, u32[]{:S(2)}) copy-start(f32[2,2,2,4,128]{4,2,1,3,0:T(2,128)} %copy-done.21) | copy-start | bytes 49156
  58.6 1.8 %copy-start.24 = (f32[2,2,2,4,128]{4,2,1,3,0:T(2,128)S(1)}, f32[2,2,2,4,128]{4,2,1,3,0:T(2,128)}, u32[]{:S(2)}) copy-start(f32[2,2,2,4,128]{4,2,1,3,0:T(2,128)} %copy-done.23) | copy-start | bytes 49156
  58.6 1.8 %copy-start.26 = (f32[2,2,2,4,128]{4,2,1,3,0:T(2,128)S(1)}, f32[2,2,2,4,128]{4,2,1,3,0:T(2,128)}, u32[]{:S(2)}) copy-start(f32[2,2,2,4,128]{4,2,1,3,0:T(2,128)} %copy-done.25) | copy-start | bytes 49156
  58.6 1.8 %copy-start.30 = (f32[8,2,2,4,128]{4,2,1,3,0:T(2,128)S(1)}, f32[8,2,2,4,128]{4,2,1,3,0:T(2,128)}, u32[]{:S(2)}) copy-start(f32[8,2,2,4,128]{4,2,1,3,0:T(2,128)} %copy-done.29) | copy-start | bytes 196612
  63.6 6.0 %collective-permute-start.24 = (f32[4,4,1,4,128]{4,2,3,1,0:T(1,128)S(1)}, f32[4,4,1,4,128]{4,2,3,1,0:T(1,128)S(1)}, u32[]{:S(2)}, u32[]{:S(2)}) collective-permute-start(f32[4,4,1,4,128]{4,2,3,1,0:T(1,128)S(1)} %get-tuple-element.16), channel_id=1, source_target_pairs={{0,1},{1,2},{2,3},{3,0},{4,5},{5,6},{6,7},{7,4},{8,9},{9,10},{10,1... | collective-permute-start | bytes 98312 | tf_op jit(solution)/shard_map/ppermute | solution.py:24
  63.6 10.5 %collective-permute-start.22 = (f32[4,2,4,4,128]{4,2,3,1,0:T(4,128)S(1)}, f32[4,2,4,4,128]{4,2,3,1,0:T(4,128)S(1)}, u32[]{:S(2)}, u32[]{:S(2)}) collective-permute-start(f32[4,2,4,4,128]{4,2,3,1,0:T(4,128)S(1)} %pad_maximum_fusion.54), channel_id=1, source_target_pairs={{0,4},{4,0},{1,5},{5,1},{2,6},{6,2},{3,7},{7,3},{8,12},{12,8},{9,1... | collective-permute-start | bytes 196616 | tf_op jit(solution)/shard_map/ppermute | solution.py:37
  65.2 4.6 %collective-permute-start.20 = (f32[1,4,4,4,128]{4,2,3,1,0:T(4,128)S(1)}, f32[1,4,4,4,128]{4,2,3,1,0:T(4,128)S(1)}, u32[]{:S(2)}, u32[]{:S(2)}) collective-permute-start(f32[1,4,4,4,128]{4,2,3,1,0:T(4,128)S(1)} %get-tuple-element.18), channel_id=1, source_target_pairs={{0,24},{8,0},{16,8},{24,16},{1,25},{9,1},{17,9},{25,17},{2,26},{10... | collective-permute-start | bytes 98312 | tf_op jit(solution)/shard_map/ppermute | solution.py:24
  67.3 5.7 %collective-permute-start.21 = (f32[1,4,4,4,128]{4,2,3,1,0:T(4,128)S(1)}, f32[1,4,4,4,128]{4,2,3,1,0:T(4,128)S(1)}, u32[]{:S(2)}, u32[]{:S(2)}) collective-permute-start(f32[1,4,4,4,128]{4,2,3,1,0:T(4,128)S(1)} %get-tuple-element.17), channel_id=1, source_target_pairs={{0,8},{8,16},{16,24},{24,0},{1,9},{9,17},{17,25},{25,1},{2,10},{10... | collective-permute-start | bytes 98312 | tf_op jit(solution)/shard_map/ppermute | solution.py:24
  67.5 6.5 %collective-permute-start.23 = (f32[4,4,1,4,128]{4,2,3,1,0:T(1,128)S(1)}, f32[4,4,1,4,128]{4,2,3,1,0:T(1,128)S(1)}, u32[]{:S(2)}, u32[]{:S(2)}) collective-permute-start(f32[4,4,1,4,128]{4,2,3,1,0:T(1,128)S(1)} %get-tuple-element.15), channel_id=1, source_target_pairs={{0,3},{1,0},{2,1},{3,2},{4,7},{5,4},{6,5},{7,6},{8,11},{9,8},{10,9... | collective-permute-start | bytes 98312 | tf_op jit(solution)/shard_map/ppermute | solution.py:24
  69.8 0.9 %copy-start.4 = (f32[1,8,8,4,128]{4,2,3,1,0:T(8,128)S(1)}, f32[1,8,8,4,128]{4,2,3,1,0:T(8,128)}, u32[]{:S(2)}) copy-start(f32[1,8,8,4,128]{4,2,3,1,0:T(8,128)} %copy-done.3) | copy-start | bytes 393220
  73.0 0.9 %copy-start.2 = (f32[1,8,8,4,128]{4,2,3,1,0:T(8,128)S(1)}, f32[1,8,8,4,128]{4,2,3,1,0:T(8,128)}, u32[]{:S(2)}) copy-start(f32[1,8,8,4,128]{4,2,3,1,0:T(8,128)} %copy-done.1) | copy-start | bytes 393220
  (14 other events, 10.5 us)

commit v13 on v12

--- a/solution.py
+++ b/solution.py
@@ -283,16 +283,17 @@
     return ((box_part[0][None, :] <= cells) & (cells < box_part[1][None, :])).astype(jnp.float32)
 
 
-def gram_matrix(tiles_by_step, inv_tiles, tile_pairs, orb_count):
+def gram_matrix(tiles_by_step, inv_tiles, tile_pairs, orb_count, later):
     count = lax.axis_size("gx")
     local = inv_tiles.shape[0]
     tile_edge = inv_tiles.shape[1]
     me = lax.axis_index("gx")
-    total = jnp.zeros((orb_count, orb_count), jnp.float32)
+    total = jnp.zeros((orb_count, orb_count), jnp.float32) + later
     for step in range(count):
         piece = tiles_by_step.get(step)
         if piece is None:
             piece = inv_tiles if step == 0 else shifted(inv_tiles, "gx", step)
+        piece = piece + later
         owner = (me + step) % count
         for slot in range(local):
             tile_id = owner * local + slot
@@ -317,16 +318,17 @@
     updated_padded = padded_one + coarse_padded
     updated = updated_padded[1:-1, 1:-1, 1:-1]
     post_one = updated + omega * (rhs_one - padded_stencil(updated_padded, 1)) / center
-    return post_smooth(0, corr_zero, faces_zero, rhs_zero, post_one, all_faces(post_one)), tiles_by_step
+    later = 0.0 * post_one[(0,) * post_one.ndim]
+    return post_smooth(0, corr_zero, faces_zero, rhs_zero, post_one, all_faces(post_one)), tiles_by_step, later
 
 
 def body(residuals, patch_box, tile_pairs, inv_tiles):
     size_a, size_b, size_c, orb_count = residuals.shape
     lanes = LANES if orb_count % LANES == 0 else orb_count
     grouped = residuals.reshape(size_a, size_b, size_c, orb_count // lanes, lanes)
-    correct, tiles_by_step = vcycle(grouped, inv_tiles)
+    correct, tiles_by_step, later = vcycle(grouped, inv_tiles)
     correct = correct.reshape(size_a, size_b, size_c, orb_count)
-    gram = gram_matrix(tiles_by_step, inv_tiles, tile_pairs, orb_count)
+    gram = gram_matrix(tiles_by_step, inv_tiles, tile_pairs, orb_count, later)
     mask_first = dim_mask(patch_box[0], lax.axis_index("gx") * size_a, size_a)
     mask_second = dim_mask(patch_box[1], lax.axis_index("gy") * size_b, size_b)
     mask_third = dim_mask(patch_box[2], lax.axis_index("gz") * size_c, size_c)

time: 78.1 us -> 75.5 us (0.967)
  local copies, waits for them, and re-layouts: 14.5 us -> 10.3 us
  waiting for transfers between devices: 19.1 us -> 20.7 us
  other arithmetic: 7 us -> 8.08 us
  matrix products: 3.65 us -> 2.73 us
    slice x9 -> x1, local copies, waits for them, and re-layouts: 2.55 us -> 0.59 us  [vcycle(): later = 0.0 * post_one[(0,) * post_one.ndim]]
    unnamed x68 -> x22, local copies, waits for them, and re-layouts: 4.91 us -> 3.16 us
    ppermute x15, waiting for transfers between devices: 18.3 us -> 19.3 us  [shifted(): lax.ppermute(block, axis, [(j, (j - step) % count) for j in range(count)])]
    concatenate x0 -> x1, other arithmetic: none -> 0.97 us  [assemble(): return jnp.concatenate(pieces, axis=dims[level])]
    dot_general x1, matrix products: 1.84 us -> 0.89 us  [coarse_solve(): jnp.einsum('qxyz,xyzgl->qgl', operator, extended, precision=lax.Precision...]
    dynamic_update_slice x4 -> x3, local copies, waits for them, and re-layouts: 4.22 us -> 4.2 us  [gram_matrix(): total = lax.dynamic_update_slice(total, piece[slot], (row, col))]
  transfers between devices with their start and end apart: 25 -> 25, of which waited for: 10 -> 10; matrix products, arithmetic and copies ran while one was open for 10% -> 8% of each run, Pallas kernels for 0% -> 0%
where the time goes in v13:
time: 75.5 us; the launch traced here: 75.2 us
  starting transfers between devices  26.9 us (36%)
  waiting for transfers between devices  20.7 us (27%)
  local copies, waits for them, and re-layouts  10.3 us (14%)
  other arithmetic  8.08 us (11%)
  between operations  6.49 us (9%)
  matrix products  2.73 us (4%)
    ppermute x15, waiting for transfers between devices, shifted(): lax.ppermute(block, axis, [(j, (j - step) % count) for j in range(count)])  19.3 us
    ppermute x15, starting transfers between devices, shifted(): lax.ppermute(block, axis, [(j, (j - step) % count) for j in range(count)])  15.4 us
    ppermute x7, starting transfers between devices, fetch(): cache[steps] = lax.ppermute(block, tuple(axes), pairs)  6.8 us
    ppermute x3, starting transfers between devices, axis_faces(): lax.ppermute(jnp.concatenate([first, last], axis=dim), axis, [(0, 1), (1,...  4.75 us
    dynamic_update_slice x3, local copies, waits for them, and re-layouts, gram_matrix(): total = lax.dynamic_update_slice(total, piece[slot], (row, col))  4.2 us
    unnamed x22, local copies, waits for them, and re-layouts  3.16 us
    dot_general x1, matrix products, body(): jnp.dot(rows, gram, precision=lax.Precision.HIGH, preferred_element_type=...  1.84 us
    div x3, other arithmetic, vcycle(): omega * part.astype(jnp.float32) / center  1.67 us
  transfers between devices with their start and end apart: 25, of which 10 were waited for; matrix products, arithmetic and copies ran while one was open for 8% of the time, Pallas kernels for 0%

profile of v13, /device:TPU:0, one launch (start us, length us, event | category | flops | bytes accessed | tf_op | source)
XLA Modules:
  0.0 75.2 jit_solution(7565697189289854467)
XLA Ops:
  0.0 1.6 %fusion.36 = (f32[8,8,1,4,128]{4,2,3,1,0:T(1,128)S(1)}, f32[8,8,1,4,128]{4,2,3,1,0:T(1,128)S(1)}) fusion(bf16[8,8,8,4,128]{4,2,3,1,0:T(8,128)(2,1)} %bitcast.70), kind=kLoop, calls=%fused_computation.110 | loop fusion | flops 131072 | bytes 393216 | tf_op jit(solution)/shard_map/div | solution.py:308
  1.6 0.5 collective-permute-start.4
  2.3 2.6 %collective-permute-start.2 = (f32[8,2,8,4,128]{4,2,3,1,0:T(8,128)S(1)}, f32[8,2,8,4,128]{4,2,3,1,0:T(8,128)S(1)}, u32[]{:S(2)}, u32[]{:S(2)}) collective-permute-start(f32[8,2,8,4,128]{4,2,3,1,0:T(8,128)S(1)} %pad_maximum_fusion.32), channel_id=1, source_target_pairs={{0,4},{4,0},{1,5},{5,1},{2,6},{6,2},{3,7},{7,3},{8,12},{12,8},{9,1... | collective-permute-start | bytes 786440 | tf_op jit(solution)/shard_map/ppermute | solution.py:37
  4.9 3.7 %collective-permute-start = (f32[1,8,8,4,128]{4,2,3,1,0:T(8,128)S(1)}, f32[1,8,8,4,128]{4,2,3,1,0:T(8,128)S(1)}, u32[]{:S(2)}, u32[]{:S(2)}) collective-permute-start(f32[1,8,8,4,128]{4,2,3,1,0:T(8,128)S(1)} %get-tuple-element.8), channel_id=1, source_target_pairs={{0,24},{8,0},{16,8},{24,16},{1,25},{9,1},{17,9},{25,17},{2,26},{10... | collective-permute-start | bytes 393224 | tf_op jit(solution)/shard_map/ppermute | solution.py:24
  8.5 1.2 %collective-permute-start.3 = (f32[8,8,1,4,128]{4,2,3,1,0:T(1,128)S(1)}, f32[8,8,1,4,128]{4,2,3,1,0:T(1,128)S(1)}, u32[]{:S(2)}, u32[]{:S(2)}) collective-permute-start(f32[8,8,1,4,128]{4,2,3,1,0:T(1,128)S(1)} %get-tuple-element.5), channel_id=1, source_target_pairs={{0,3},{1,0},{2,1},{3,2},{4,7},{5,4},{6,5},{7,6},{8,11},{9,8},{10,9... | collective-permute-start | bytes 393224 | tf_op jit(solution)/shard_map/ppermute | solution.py:24
  9.7 0.7 copy-done.9
  10.7 0.2 collective-permute-done.2
  11.0 1.1 %collective-permute-done = f32[1,8,8,4,128]{4,2,3,1,0:T(8,128)S(1)} collective-permute-done((f32[1,8,8,4,128]{4,2,3,1,0:T(8,128)S(1)}, f32[1,8,8,4,128]{4,2,3,1,0:T(8,128)S(1)}, u32[]{:S(2)}, u32[]{:S(2)}) %collective-permute-start) | collective-permute-done | bytes 131104 | tf_op jit(solution)/shard_map/ppermute | solution.py:24
  12.1 4.5 %collective-permute-done.1 = f32[1,8,8,4,128]{4,2,3,1,0:T(8,128)S(1)} collective-permute-done((f32[1,8,8,4,128]{4,2,3,1,0:T(8,128)S(1)}, f32[1,8,8,4,128]{4,2,3,1,0:T(8,128)S(1)}, u32[]{:S(2)}, u32[]{:S(2)}) %collective-permute-start.1) | collective-permute-done | bytes 131104 | tf_op jit(solution)/shard_map/ppermute | solution.py:24
  16.6 0.9 %convert_subtract_fusion.1 = f32[8,8,8,4,128]{4,2,3,1,0:T(8,128)S(1)} fusion(f32[8,8,1,4,128]{4,2,3,1,0:T(1,128)S(1)} %collective-permute-done.4, f32[10,1,8,4,128]{4,2,3,1,0:T(8,128)S(1)} %pad.40, f32[10,1,8,4,128]{4,2,3,1,0:T(8,128)S(1)} %pad.41, f32[1,8,8,4,128]{4,2,3,1,0:T(8,128)S(1)} %collective-permute-done, ...), kind=kLoop, calls=%fused_computation.1 | loop fusion | flops 8912896 | bytes 3473408 | tf_op jit(solution)/shard_map/sub | solution.py:311
  17.6 0.7 reduce_sum.18
  18.5 0.6 collective-permute-start.6
  19.1 0.2 collective-permute-start.5
  19.3 1.5 %collective-permute-start.8 = (f32[1,4,4,4,128]{4,2,3,1,0:T(4,128)S(1)}, f32[1,4,4,4,128]{4,2,3,1,0:T(4,128)S(1)}, u32[]{:S(2)}, u32[]{:S(2)}) collective-permute-start(f32[1,4,4,4,128]{4,2,3,1,0:T(4,128)S(1)} %get-tuple-element.24), channel_id=1, source_target_pairs={{0,24},{8,0},{16,8},{24,16},{1,25},{9,1},{17,9},{25,17},{2,26},{10... | collective-permute-start | bytes 98312 | tf_op jit(solution)/shard_map/ppermute | solution.py:24
  20.8 0.6 collective-permute-start.7
  21.4 1.1 %collective-permute-done.5 = f32[4,4,1,4,128]{4,2,3,1,0:T(1,128)S(1)} collective-permute-done((f32[4,4,1,4,128]{4,2,3,1,0:T(1,128)S(1)}, f32[4,4,1,4,128]{4,2,3,1,0:T(1,128)S(1)}, u32[]{:S(2)}, u32[]{:S(2)}) %collective-permute-start.5) | collective-permute-done | bytes 32800 | tf_op jit(solution)/shard_map/ppermute | solution.py:24
  22.5 0.6 collective-permute-done.6
  23.2 3.3 %collective-permute-done.7 = f32[1,4,4,4,128]{4,2,3,1,0:T(4,128)S(1)} collective-permute-done((f32[1,4,4,4,128]{4,2,3,1,0:T(4,128)S(1)}, f32[1,4,4,4,128]{4,2,3,1,0:T(4,128)S(1)}, u32[]{:S(2)}, u32[]{:S(2)}) %collective-permute-start.7) | collective-permute-done | bytes 32800 | tf_op jit(solution)/shard_map/ppermute | solution.py:24
  26.9 0.6 collective-permute-start.11
  27.5 3.2 %collective-permute-start.10 = (f32[10,2,2,4,128]{4,0,3,2,1:T(8,128)S(1)}, f32[10,2,2,4,128]{4,0,3,2,1:T(8,128)S(1)}, u32[]{:S(2)}, u32[]{:S(2)}) collective-permute-start(f32[10,2,2,4,128]{4,0,3,2,1:T(8,128)S(1)} %pad_maximum_fusion.51), channel_id=1, source_target_pairs={{0,24},{8,0},{16,8},{24,16},{1,25},{9,1},{17,9},{25,17},{2,26},{10... | collective-permute-start | bytes 245768 | tf_op jit(solution)/shard_map/ppermute | solution.py:24
  30.7 4.5 %collective-permute-done.12 = f32[10,2,2,4,128]{4,0,3,2,1:T(8,128)S(1)} collective-permute-done((f32[10,2,2,4,128]{4,0,3,2,1:T(8,128)S(1)}, f32[10,2,2,4,128]{4,0,3,2,1:T(8,128)S(1)}, u32[]{:S(2)}, u32[]{:S(2)}) %collective-permute-start.12) | collective-permute-done | bytes 81952 | tf_op jit(solution)/shard_map/ppermute | solution.py:24
  35.2 4.7 %collective-permute-done.11 = f32[10,2,2,4,128]{4,0,3,2,1:T(8,128)S(1)} collective-permute-done((f32[10,2,2,4,128]{4,0,3,2,1:T(8,128)S(1)}, f32[10,2,2,4,128]{4,0,3,2,1:T(8,128)S(1)}, u32[]{:S(2)}, u32[]{:S(2)}) %collective-permute-start.11) | collective-permute-done | bytes 81952 | tf_op jit(solution)/shard_map/ppermute | solution.py:24
  39.9 0.7 pad_maximum_fusion.53
  40.6 1.4 %collective-permute-start.18 = (f32[8,2,2,4,128]{4,0,3,2,1:T(8,128)}, f32[8,2,2,4,128]{4,0,3,2,1:T(8,128)S(1)}, u32[]{:S(2)}, u32[]{:S(2)}) collective-permute-start(f32[8,2,2,4,128]{4,0,3,2,1:T(8,128)} %pad_maximum_fusion.53), channel_id=1, source_target_pairs={{6,0},{7,1},{4,2},{5,3},{2,4},{3,5},{0,6},{1,7},{14,8},{15,9},{12,... | collective-permute-start | bytes 196616 | tf_op jit(solution)/shard_map/ppermute | solution.py:108
  42.1 2.4 %collective-permute-start.17 = (f32[8,2,2,4,128]{4,0,3,2,1:T(8,128)}, f32[8,2,2,4,128]{4,0,3,2,1:T(8,128)S(1)}, u32[]{:S(2)}, u32[]{:S(2)}) collective-permute-start(f32[8,2,2,4,128]{4,0,3,2,1:T(8,128)} %pad_maximum_fusion.53), channel_id=1, source_target_pairs={{5,0},{6,1},{7,2},{4,3},{1,4},{2,5},{3,6},{0,7},{13,8},{14,9},{15,... | collective-permute-start | bytes 196616 | tf_op jit(solution)/shard_map/ppermute | solution.py:108
  44.4 0.5 collective-permute-start.16
  45.0 0.6 collective-permute-done.19
  45.5 1.0 %collective-permute-start.14 = (f32[8,2,2,4,128]{4,0,3,2,1:T(8,128)}, f32[8,2,2,4,128]{4,0,3,2,1:T(8,128)}, u32[]{:S(2)}, u32[]{:S(2)}) collective-permute-start(f32[8,2,2,4,128]{4,0,3,2,1:T(8,128)} %pad_maximum_fusion.53), channel_id=1, source_target_pairs={{2,0},{3,1},{0,2},{1,3},{6,4},{7,5},{4,6},{5,7},{10,8},{11,9},{8,1... | collective-permute-start | bytes 196616 | tf_op jit(solution)/shard_map/ppermute | solution.py:108
  46.6 1.5 %collective-permute-start.13 = (f32[8,2,2,4,128]{4,0,3,2,1:T(8,128)}, f32[8,2,2,4,128]{4,0,3,2,1:T(8,128)}, u32[]{:S(2)}, u32[]{:S(2)}) collective-permute-start(f32[8,2,2,4,128]{4,0,3,2,1:T(8,128)} %pad_maximum_fusion.53), channel_id=1, source_target_pairs={{1,0},{2,1},{3,2},{0,3},{5,4},{6,5},{7,6},{4,7},{9,8},{10,9},{11,1... | collective-permute-start | bytes 196616 | tf_op jit(solution)/shard_map/ppermute | solution.py:108
  48.3 0.7 copy-done.8
  48.9 0.7 constant_dynamic-slice_fusion
  54.7 1.0 %maximum_maximum_fusion = f32[8,4,8,4,128]{4,0,3,2,1:T(8,128)S(1)} fusion(f32[8,2,2,4,128]{4,0,3,2,1:T(8,128)S(1)} %collective-permute-done.19, f32[8,2,2,4,128]{4,0,3,2,1:T(8,128)S(1)} %collective-permute-done.18, f32[8,2,2,4,128]{4,0,3,2,1:T(8,128)S(1)} %collective-permute-done.17, f32[8,2,2,4,128]{4,0,3,2,1:T(8,128)S(1)} %collective-permute-done.16, ...), kind=kLoop, calls=%fused_computation.66 | loop fusion | flops 1310720 | bytes 1048576 | tf_op jit(solution)/shard_map/concatenate | solution.py:117
  55.7 0.9 %convolution_bitcast_fusion = f32[216,4,128]{2,0,1:T(8,128)S(1)} fusion(f32[216,8,4,8,1]{0,3,2,4,1:T(8,128)S(1)} %copy-done.10, f32[8,4,8,4,128]{4,0,3,2,1:T(8,128)S(1)} %maximum_maximum_fusion), kind=kOutput, calls=%fused_computation.5 | convolution fusion | flops 339738624 | bytes 1187840 | tf_op jit(solution)/shard_map/qxyz,xyzgl->qgl/dot_general | solution.py:195
  56.7 0.2 maximum_add_fusion
  57.2 0.6 slice.322
  57.9 0.6 broadcast_in_dim.77
  58.5 0.2 fusion.21
  58.8 1.6 %collective-permute-start.22 = (f32[4,2,4,4,128]{4,2,3,1,0:T(4,128)S(1)}, f32[4,2,4,4,128]{4,2,3,1,0:T(4,128)S(1)}, u32[]{:S(2)}, u32[]{:S(2)}) collective-permute-start(f32[4,2,4,4,128]{4,2,3,1,0:T(4,128)S(1)} %pad_maximum_fusion.54), channel_id=1, source_target_pairs={{0,4},{4,0},{1,5},{5,1},{2,6},{6,2},{3,7},{7,3},{8,12},{12,8},{9,1... | collective-permute-start | bytes 196616 | tf_op jit(solution)/shard_map/ppermute | solution.py:37
  60.4 2.6 %collective-permute-start.20 = (f32[1,4,4,4,128]{4,2,3,1,0:T(4,128)S(1)}, f32[1,4,4,4,128]{4,2,3,1,0:T(4,128)S(1)}, u32[]{:S(2)}, u32[]{:S(2)}) collective-permute-start(f32[1,4,4,4,128]{4,2,3,1,0:T(4,128)S(1)} %get-tuple-element.18), channel_id=1, source_target_pairs={{0,24},{8,0},{16,8},{24,16},{1,25},{9,1},{17,9},{25,17},{2,26},{10... | collective-permute-start | bytes 98312 | tf_op jit(solution)/shard_map/ppermute | solution.py:24
  63.0 1.2 %collective-permute-start.23 = (f32[4,4,1,4,128]{4,2,3,1,0:T(1,128)S(1)}, f32[4,4,1,4,128]{4,2,3,1,0:T(1,128)S(1)}, u32[]{:S(2)}, u32[]{:S(2)}) collective-permute-start(f32[4,4,1,4,128]{4,2,3,1,0:T(1,128)S(1)} %get-tuple-element.15), channel_id=1, source_target_pairs={{0,3},{1,0},{2,1},{3,2},{4,7},{5,4},{6,5},{7,6},{8,11},{9,8},{10,9... | collective-permute-start | bytes 98312 | tf_op jit(solution)/shard_map/ppermute | solution.py:24
  65.1 0.7 copy-done.7
  66.0 0.9 %copy-done.3 = f32[10,2,2,4,128]{4,0,3,2,1:T(8,128)S(1)} copy-done((f32[10,2,2,4,128]{4,0,3,2,1:T(8,128)S(1)}, f32[10,2,2,4,128]{4,0,3,2,1:T(8,128)}, u32[]{:S(2)}) %copy-start.3) | copy-done | bytes 81944
  66.9 0.9 %dynamic_update_slice.13 = f32[512,512]{1,0:T(8,128)S(1)} dynamic-update-slice(f32[512,512]{1,0:T(8,128)S(1)} %bitcast_dynamic-update-slice_fusion, f32[128,128]{1,0:T(8,128)S(1)} %bitcast.94, s32[]{:T(128)S(6)} %select_n.65, s32[]{:T(128)S(6)} %select_n.66) | dynamic-update-slice | bytes 131076 | tf_op jit(solution)/shard_map/dynamic_update_slice | solution.py:302
  67.8 1.7 %dynamic_update_slice.14 = f32[512,512]{1,0:T(8,128)S(1)} dynamic-update-slice(f32[512,512]{1,0:T(8,128)S(1)} %dynamic_update_slice.13, f32[128,128]{1,0:T(8,128)S(1)} %bitcast.93, s32[]{:T(128)S(6)} %select_n.69, s32[]{:T(128)S(6)} %select_n.70) | dynamic-update-slice | bytes 131076 | tf_op jit(solution)/shard_map/dynamic_update_slice | solution.py:302
  69.5 1.7 %dynamic_update_slice.15 = f32[512,512]{1,0:T(8,128)S(1)} dynamic-update-slice(f32[512,512]{1,0:T(8,128)S(1)} %dynamic_update_slice.14, f32[128,128]{1,0:T(8,128)S(1)} %bitcast.92, s32[]{:T(128)S(6)} %select_n.73, s32[]{:T(128)S(6)} %select_n.74) | dynamic-update-slice | bytes 131076 | tf_op jit(solution)/shard_map/dynamic_update_slice | solution.py:302
  72.1 1.0 %fusion.2 = f32[8,8,8,4,128]{4,2,3,1,0:T(8,128)S(1)} fusion(f32[8,8,8,4,128]{4,2,3,1,0:T(8,128)S(1)} %fusion.21, f32[8,8,1,4,128]{4,2,3,1,0:T(1,128)S(1)} %add.277, f32[10,1,8,4,128]{4,2,3,1,0:T(8,128)S(1)} %pad.48, f32[10,1,8,4,128]{4,2,3,1,0:T(8,128)S(1)} %pad.49, f32[1,8,8,4,128]{4,2,3,1,0:T(8,128)S(1)} %add.268, f32[1,8,8,4,128]{4,2,3,1,0:T(8,128)S(1)} %add.269, ...), kind=kLoop, calls=%fused_computation.8 | loop fusion | flops 9437184 | bytes 3473408 | tf_op jit(solution)/shard_map/add | solution.py:270
  73.1 0.2 bitcast_multiply_fusion
  73.3 1.8 %convolution_convert_fusion = bf16[512,512]{1,0:T(8,128)(2,1)} fusion(f32[512,512]{1,0:T(8,128)S(1)} %bitcast_multiply_fusion, f32[512,512]{1,0:T(8,128)S(1)} %dynamic_update_slice.15), kind=kOutput, calls=%fused_computation.4 | convolution fusion | flops 805568512 | bytes 2621440 | tf_op jit(solution)/shard_map/dot_general | solution.py:340
  (109 shorter events, 3.0 us)
Async XLA Ops:
  0.0 2.2 %copy-start = (bf16[8,8,8,512]{3,2,1,0:T(8,128)(2,1)S(1)}, bf16[8,8,8,512]{3,2,1,0:T(8,128)(2,1)}, u32[]{:S(2)}) copy-start(bf16[8,8,8,512]{3,2,1,0:T(8,128)(2,1)} %param.5) | copy-start | bytes 1572868
  1.6 9.4 %collective-permute-start.4 = (f32[8,8,1,4,128]{4,2,3,1,0:T(1,128)S(1)}, f32[8,8,1,4,128]{4,2,3,1,0:T(1,128)S(1)}, u32[]{:S(2)}, u32[]{:S(2)}) collective-permute-start(f32[8,8,1,4,128]{4,2,3,1,0:T(1,128)S(1)} %get-tuple-element.6), channel_id=1, source_target_pairs={{0,1},{1,2},{2,3},{3,0},{4,5},{5,6},{6,7},{7,4},{8,9},{9,10},{10,1... | collective-permute-start | bytes 393224 | tf_op jit(solution)/shard_map/ppermute | solution.py:24
  2.2 7.5 %copy-start.1 = (f32[1,128,128]{2,1,0:T(8,128)S(1)}, f32[1,128,128]{2,1,0:T(8,128)}, u32[]{:S(2)}) copy-start(f32[1,128,128]{2,1,0:T(8,128)} %param.8) | copy-start | bytes 196612
  2.3 8.7 %collective-permute-start.2 = (f32[8,2,8,4,128]{4,2,3,1,0:T(8,128)S(1)}, f32[8,2,8,4,128]{4,2,3,1,0:T(8,128)S(1)}, u32[]{:S(2)}, u32[]{:S(2)}) collective-permute-start(f32[8,2,8,4,128]{4,2,3,1,0:T(8,128)S(1)} %pad_maximum_fusion.32), channel_id=1, source_target_pairs={{0,4},{4,0},{1,5},{5,1},{2,6},{6,2},{3,7},{7,3},{8,12},{12,8},{9,1... | collective-permute-start | bytes 786440 | tf_op jit(solution)/shard_map/ppermute | solution.py:37
  4.9 7.3 %collective-permute-start = (f32[1,8,8,4,128]{4,2,3,1,0:T(8,128)S(1)}, f32[1,8,8,4,128]{4,2,3,1,0:T(8,128)S(1)}, u32[]{:S(2)}, u32[]{:S(2)}) collective-permute-start(f32[1,8,8,4,128]{4,2,3,1,0:T(8,128)S(1)} %get-tuple-element.8), channel_id=1, source_target_pairs={{0,24},{8,0},{16,8},{24,16},{1,25},{9,1},{17,9},{25,17},{2,26},{10... | collective-permute-start | bytes 393224 | tf_op jit(solution)/shard_map/ppermute | solution.py:24
  8.5 8.1 %collective-permute-start.1 = (f32[1,8,8,4,128]{4,2,3,1,0:T(8,128)S(1)}, f32[1,8,8,4,128]{4,2,3,1,0:T(8,128)S(1)}, u32[]{:S(2)}, u32[]{:S(2)}) collective-permute-start(f32[1,8,8,4,128]{4,2,3,1,0:T(8,128)S(1)} %get-tuple-element.7), channel_id=1, source_target_pairs={{0,8},{8,16},{16,24},{24,0},{1,9},{9,17},{17,25},{25,1},{2,10},{10... | collective-permute-start | bytes 393224 | tf_op jit(solution)/shard_map/ppermute | solution.py:24
  8.5 8.1 %collective-permute-start.3 = (f32[8,8,1,4,128]{4,2,3,1,0:T(1,128)S(1)}, f32[8,8,1,4,128]{4,2,3,1,0:T(1,128)S(1)}, u32[]{:S(2)}, u32[]{:S(2)}) collective-permute-start(f32[8,8,1,4,128]{4,2,3,1,0:T(1,128)S(1)} %get-tuple-element.5), channel_id=1, source_target_pairs={{0,3},{1,0},{2,1},{3,2},{4,7},{5,4},{6,5},{7,6},{8,11},{9,8},{10,9... | collective-permute-start | bytes 393224 | tf_op jit(solution)/shard_map/ppermute | solution.py:24
  9.7 0.7 copy-start.9
  18.4 2.9 %collective-permute-start.9 = (f32[4,4,1,4,128]{4,2,3,1,0:T(1,128)S(1)}, f32[4,4,1,4,128]{4,2,3,1,0:T(1,128)S(1)}, u32[]{:S(2)}, u32[]{:S(2)}) collective-permute-start(f32[4,4,1,4,128]{4,2,3,1,0:T(1,128)S(1)} %get-tuple-element.22), channel_id=1, source_target_pairs={{0,3},{1,0},{2,1},{3,2},{4,7},{5,4},{6,5},{7,6},{8,11},{9,8},{10,9... | collective-permute-start | bytes 98312 | tf_op jit(solution)/shard_map/ppermute | solution.py:24
  18.5 4.6 %collective-permute-start.6 = (f32[4,2,4,4,128]{4,2,3,1,0:T(4,128)S(1)}, f32[4,2,4,4,128]{4,2,3,1,0:T(4,128)S(1)}, u32[]{:S(2)}, u32[]{:S(2)}) collective-permute-start(f32[4,2,4,4,128]{4,2,3,1,0:T(4,128)S(1)} %pad_maximum_fusion.52), channel_id=1, source_target_pairs={{0,4},{4,0},{1,5},{5,1},{2,6},{6,2},{3,7},{7,3},{8,12},{12,8},{9,1... | collective-permute-start | bytes 196616 | tf_op jit(solution)/shard_map/ppermute | solution.py:37
  19.1 3.4 %collective-permute-start.5 = (f32[4,4,1,4,128]{4,2,3,1,0:T(1,128)S(1)}, f32[4,4,1,4,128]{4,2,3,1,0:T(1,128)S(1)}, u32[]{:S(2)}, u32[]{:S(2)}) collective-permute-start(f32[4,4,1,4,128]{4,2,3,1,0:T(1,128)S(1)} %get-tuple-element.21), channel_id=1, source_target_pairs={{0,1},{1,2},{2,3},{3,0},{4,5},{5,6},{6,7},{7,4},{8,9},{9,10},{10,1... | collective-permute-start | bytes 98312 | tf_op jit(solution)/shard_map/ppermute | solution.py:24
  19.3 3.9 %collective-permute-start.8 = (f32[1,4,4,4,128]{4,2,3,1,0:T(4,128)S(1)}, f32[1,4,4,4,128]{4,2,3,1,0:T(4,128)S(1)}, u32[]{:S(2)}, u32[]{:S(2)}) collective-permute-start(f32[1,4,4,4,128]{4,2,3,1,0:T(4,128)S(1)} %get-tuple-element.24), channel_id=1, source_target_pairs={{0,24},{8,0},{16,8},{24,16},{1,25},{9,1},{17,9},{25,17},{2,26},{10... | collective-permute-start | bytes 98312 | tf_op jit(solution)/shard_map/ppermute | solution.py:24
  20.8 5.7 %collective-permute-start.7 = (f32[1,4,4,4,128]{4,2,3,1,0:T(4,128)S(1)}, f32[1,4,4,4,128]{4,2,3,1,0:T(4,128)S(1)}, u32[]{:S(2)}, u32[]{:S(2)}) collective-permute-start(f32[1,4,4,4,128]{4,2,3,1,0:T(4,128)S(1)} %get-tuple-element.23), channel_id=1, source_target_pairs={{0,8},{8,16},{16,24},{24,0},{1,9},{9,17},{17,25},{25,1},{2,10},{10... | collective-permute-start | bytes 98312 | tf_op jit(solution)/shard_map/ppermute | solution.py:24
  26.8 8.4 %collective-permute-start.12 = (f32[10,2,2,4,128]{4,0,3,2,1:T(8,128)S(1)}, f32[10,2,2,4,128]{4,0,3,2,1:T(8,128)S(1)}, u32[]{:S(2)}, u32[]{:S(2)}) collective-permute-start(f32[10,2,2,4,128]{4,0,3,2,1:T(8,128)S(1)} %pad_maximum_fusion.51), channel_id=1, source_target_pairs={{0,8},{8,16},{16,24},{24,0},{1,9},{9,17},{17,25},{25,1},{2,10},{10... | collective-permute-start | bytes 245768 | tf_op jit(solution)/shard_map/ppermute | solution.py:24
  26.9 13.0 %collective-permute-start.11 = (f32[10,2,2,4,128]{4,0,3,2,1:T(8,128)S(1)}, f32[10,2,2,4,128]{4,0,3,2,1:T(8,128)S(1)}, u32[]{:S(2)}, u32[]{:S(2)}) collective-permute-start(f32[10,2,2,4,128]{4,0,3,2,1:T(8,128)S(1)} %pad_maximum_fusion.51), channel_id=1, source_target_pairs={{0,16},{8,24},{16,0},{24,8},{1,17},{9,25},{17,1},{25,9},{2,18},{10... | collective-permute-start | bytes 245768 | tf_op jit(solution)/shard_map/ppermute | solution.py:24
  27.5 12.4 %collective-permute-start.10 = (f32[10,2,2,4,128]{4,0,3,2,1:T(8,128)S(1)}, f32[10,2,2,4,128]{4,0,3,2,1:T(8,128)S(1)}, u32[]{:S(2)}, u32[]{:S(2)}) collective-permute-start(f32[10,2,2,4,128]{4,0,3,2,1:T(8,128)S(1)} %pad_maximum_fusion.51), channel_id=1, source_target_pairs={{0,24},{8,0},{16,8},{24,16},{1,25},{9,1},{17,9},{25,17},{2,26},{10... | collective-permute-start | bytes 245768 | tf_op jit(solution)/shard_map/ppermute | solution.py:24
  35.2 11.3 %copy-start.4 = (f32[10,2,2,4,128]{4,0,3,2,1:T(8,128)}, f32[10,2,2,4,128]{4,0,3,2,1:T(8,128)S(1)}, u32[]{:S(2)}) copy-start(f32[10,2,2,4,128]{4,0,3,2,1:T(8,128)S(1)} %collective-permute-done.12) | copy-start | bytes 245764
  39.9 6.6 %copy-start.6 = (f32[10,2,2,4,128]{4,0,3,2,1:T(8,128)}, f32[10,2,2,4,128]{4,0,3,2,1:T(8,128)S(1)}, u32[]{:S(2)}) copy-start(f32[10,2,2,4,128]{4,0,3,2,1:T(8,128)S(1)} %collective-permute-done.11) | copy-start | bytes 245764
  39.9 6.6 %copy-start.2 = (f32[10,2,2,4,128]{4,0,3,2,1:T(8,128)}, f32[10,2,2,4,128]{4,0,3,2,1:T(8,128)S(1)}, u32[]{:S(2)}) copy-start(f32[10,2,2,4,128]{4,0,3,2,1:T(8,128)S(1)} %collective-permute-done.10) | copy-start | bytes 245764
  40.6 4.9 %collective-permute-start.19 = (f32[8,2,2,4,128]{4,0,3,2,1:T(8,128)}, f32[8,2,2,4,128]{4,0,3,2,1:T(8,128)S(1)}, u32[]{:S(2)}, u32[]{:S(2)}) collective-permute-start(f32[8,2,2,4,128]{4,0,3,2,1:T(8,128)} %pad_maximum_fusion.53), channel_id=1, source_target_pairs={{7,0},{4,1},{5,2},{6,3},{3,4},{0,5},{1,6},{2,7},{15,8},{12,9},{13,... | collective-permute-start | bytes 196616 | tf_op jit(solution)/shard_map/ppermute | solution.py:108
  40.6 5.9 %collective-permute-start.18 = (f32[8,2,2,4,128]{4,0,3,2,1:T(8,128)}, f32[8,2,2,4,128]{4,0,3,2,1:T(8,128)S(1)}, u32[]{:S(2)}, u32[]{:S(2)}) collective-permute-start(f32[8,2,2,4,128]{4,0,3,2,1:T(8,128)} %pad_maximum_fusion.53), channel_id=1, source_target_pairs={{6,0},{7,1},{4,2},{5,3},{2,4},{3,5},{0,6},{1,7},{14,8},{15,9},{12,... | collective-permute-start | bytes 196616 | tf_op jit(solution)/shard_map/ppermute | solution.py:108
  42.1 12.6 %collective-permute-start.17 = (f32[8,2,2,4,128]{4,0,3,2,1:T(8,128)}, f32[8,2,2,4,128]{4,0,3,2,1:T(8,128)S(1)}, u32[]{:S(2)}, u32[]{:S(2)}) collective-permute-start(f32[8,2,2,4,128]{4,0,3,2,1:T(8,128)} %pad_maximum_fusion.53), channel_id=1, source_target_pairs={{5,0},{6,1},{7,2},{4,3},{1,4},{2,5},{3,6},{0,7},{13,8},{14,9},{15,... | collective-permute-start | bytes 196616 | tf_op jit(solution)/shard_map/ppermute | solution.py:108
  44.4 10.2 %collective-permute-start.16 = (f32[8,2,2,4,128]{4,0,3,2,1:T(8,128)}, f32[8,2,2,4,128]{4,0,3,2,1:T(8,128)S(1)}, u32[]{:S(2)}, u32[]{:S(2)}) collective-permute-start(f32[8,2,2,4,128]{4,0,3,2,1:T(8,128)} %pad_maximum_fusion.53), channel_id=1, source_target_pairs={{4,0},{5,1},{6,2},{7,3},{0,4},{1,5},{2,6},{3,7},{12,8},{13,9},{14,... | collective-permute-start | bytes 196616 | tf_op jit(solution)/shard_map/ppermute | solution.py:108
  44.9 9.7 %collective-permute-start.15 = (f32[8,2,2,4,128]{4,0,3,2,1:T(8,128)}, f32[8,2,2,4,128]{4,0,3,2,1:T(8,128)S(1)}, u32[]{:S(2)}, u32[]{:S(2)}) collective-permute-start(f32[8,2,2,4,128]{4,0,3,2,1:T(8,128)} %pad_maximum_fusion.53), channel_id=1, source_target_pairs={{3,0},{0,1},{1,2},{2,3},{7,4},{4,5},{5,6},{6,7},{11,8},{8,9},{9,10... | collective-permute-start | bytes 196616 | tf_op jit(solution)/shard_map/ppermute | solution.py:108
  45.5 9.2 %collective-permute-start.14 = (f32[8,2,2,4,128]{4,0,3,2,1:T(8,128)}, f32[8,2,2,4,128]{4,0,3,2,1:T(8,128)}, u32[]{:S(2)}, u32[]{:S(2)}) collective-permute-start(f32[8,2,2,4,128]{4,0,3,2,1:T(8,128)} %pad_maximum_fusion.53), channel_id=1, source_target_pairs={{2,0},{3,1},{0,2},{1,3},{6,4},{7,5},{4,6},{5,7},{10,8},{11,9},{8,1... | collective-permute-start | bytes 196616 | tf_op jit(solution)/shard_map/ppermute | solution.py:108
  46.6 8.1 %collective-permute-start.13 = (f32[8,2,2,4,128]{4,0,3,2,1:T(8,128)}, f32[8,2,2,4,128]{4,0,3,2,1:T(8,128)}, u32[]{:S(2)}, u32[]{:S(2)}) collective-permute-start(f32[8,2,2,4,128]{4,0,3,2,1:T(8,128)} %pad_maximum_fusion.53), channel_id=1, source_target_pairs={{1,0},{2,1},{3,2},{0,3},{5,4},{6,5},{7,6},{4,7},{9,8},{10,9},{11,1... | collective-permute-start | bytes 196616 | tf_op jit(solution)/shard_map/ppermute | solution.py:108
  48.3 0.7 copy-start.8
  54.6 1.0 %copy-start.10 = (f32[216,8,4,8,1]{0,3,2,4,1:T(8,128)S(1)}, f32[216,8,4,8,1]{0,3,2,4,1:T(8,128)}, u32[]{:S(2)}) copy-start(f32[216,8,4,8,1]{0,3,2,4,1:T(8,128)} %constant.138) | copy-start | bytes 663556
  58.7 12.5 %collective-permute-start.24 = (f32[4,4,1,4,128]{4,2,3,1,0:T(1,128)S(1)}, f32[4,4,1,4,128]{4,2,3,1,0:T(1,128)S(1)}, u32[]{:S(2)}, u32[]{:S(2)}) collective-permute-start(f32[4,4,1,4,128]{4,2,3,1,0:T(1,128)S(1)} %get-tuple-element.16), channel_id=1, source_target_pairs={{0,1},{1,2},{2,3},{3,0},{4,5},{5,6},{6,7},{7,4},{8,9},{9,10},{10,1... | collective-permute-start | bytes 98312 | tf_op jit(solution)/shard_map/ppermute | solution.py:24
  58.8 13.0 %collective-permute-start.22 = (f32[4,2,4,4,128]{4,2,3,1,0:T(4,128)S(1)}, f32[4,2,4,4,128]{4,2,3,1,0:T(4,128)S(1)}, u32[]{:S(2)}, u32[]{:S(2)}) collective-permute-start(f32[4,2,4,4,128]{4,2,3,1,0:T(4,128)S(1)} %pad_maximum_fusion.54), channel_id=1, source_target_pairs={{0,4},{4,0},{1,5},{5,1},{2,6},{6,2},{3,7},{7,3},{8,12},{12,8},{9,1... | collective-permute-start | bytes 196616 | tf_op jit(solution)/shard_map/ppermute | solution.py:37
  60.4 11.0 %collective-permute-start.20 = (f32[1,4,4,4,128]{4,2,3,1,0:T(4,128)S(1)}, f32[1,4,4,4,128]{4,2,3,1,0:T(4,128)S(1)}, u32[]{:S(2)}, u32[]{:S(2)}) collective-permute-start(f32[1,4,4,4,128]{4,2,3,1,0:T(4,128)S(1)} %get-tuple-element.18), channel_id=1, source_target_pairs={{0,24},{8,0},{16,8},{24,16},{1,25},{9,1},{17,9},{25,17},{2,26},{10... | collective-permute-start | bytes 98312 | tf_op jit(solution)/shard_map/ppermute | solution.py:24
  63.0 8.5 %collective-permute-start.21 = (f32[1,4,4,4,128]{4,2,3,1,0:T(4,128)S(1)}, f32[1,4,4,4,128]{4,2,3,1,0:T(4,128)S(1)}, u32[]{:S(2)}, u32[]{:S(2)}) collective-permute-start(f32[1,4,4,4,128]{4,2,3,1,0:T(4,128)S(1)} %get-tuple-element.17), channel_id=1, source_target_pairs={{0,8},{8,16},{16,24},{24,0},{1,9},{9,17},{17,25},{25,1},{2,10},{10... | collective-permute-start | bytes 98312 | tf_op jit(solution)/shard_map/ppermute | solution.py:24
  63.0 8.6 %collective-permute-start.23 = (f32[4,4,1,4,128]{4,2,3,1,0:T(1,128)S(1)}, f32[4,4,1,4,128]{4,2,3,1,0:T(1,128)S(1)}, u32[]{:S(2)}, u32[]{:S(2)}) collective-permute-start(f32[4,4,1,4,128]{4,2,3,1,0:T(1,128)S(1)} %get-tuple-element.15), channel_id=1, source_target_pairs={{0,3},{1,0},{2,1},{3,2},{4,7},{5,4},{6,5},{7,6},{8,11},{9,8},{10,9... | collective-permute-start | bytes 98312 | tf_op jit(solution)/shard_map/ppermute | solution.py:24
  64.9 0.9 %copy-start.7 = (f32[10,2,2,4,128]{4,0,3,2,1:T(8,128)S(1)}, f32[10,2,2,4,128]{4,0,3,2,1:T(8,128)}, u32[]{:S(2)}) copy-start(f32[10,2,2,4,128]{4,0,3,2,1:T(8,128)} %copy-done.6) | copy-start | bytes 245764
  65.0 0.9 %copy-start.5 = (f32[10,2,2,4,128]{4,0,3,2,1:T(8,128)S(1)}, f32[10,2,2,4,128]{4,0,3,2,1:T(8,128)}, u32[]{:S(2)}) copy-start(f32[10,2,2,4,128]{4,0,3,2,1:T(8,128)} %copy-done.4) | copy-start | bytes 245764
  66.0 0.9 %copy-start.3 = (f32[10,2,2,4,128]{4,0,3,2,1:T(8,128)S(1)}, f32[10,2,2,4,128]{4,0,3,2,1:T(8,128)}, u32[]{:S(2)}) copy-start(f32[10,2,2,4,128]{4,0,3,2,1:T(8,128)} %copy-done.2) | copy-start | bytes 245764

commit v14 on v12

--- a/solution.py
+++ b/solution.py
@@ -287,19 +287,23 @@
     count = lax.axis_size("gx")
     local = inv_tiles.shape[0]
     tile_edge = inv_tiles.shape[1]
+    blocks = orb_count // tile_edge
     me = lax.axis_index("gx")
-    total = jnp.zeros((orb_count, orb_count), jnp.float32)
+    pieces = []
+    ids = []
     for step in range(count):
         piece = tiles_by_step.get(step)
         if piece is None:
             piece = inv_tiles if step == 0 else shifted(inv_tiles, "gx", step)
-        owner = (me + step) % count
-        for slot in range(local):
-            tile_id = owner * local + slot
-            row = tile_pairs[tile_id, 0] * tile_edge
-            col = tile_pairs[tile_id, 1] * tile_edge
-            total = lax.dynamic_update_slice(total, piece[slot], (row, col))
-    return total
+        pieces.append(piece)
+        ids.append(((me + step) % count) * local + jnp.arange(local, dtype=jnp.int32))
+    tiles = jnp.concatenate(pieces, axis=0)
+    pairs = jnp.take(tile_pairs, jnp.concatenate(ids), axis=0)
+    block_ids = jnp.arange(blocks, dtype=jnp.int32)
+    rows = (pairs[:, 0][:, None] == block_ids[None, :]).astype(jnp.float32)
+    cols = (pairs[:, 1][:, None] == block_ids[None, :]).astype(jnp.float32)
+    spread = rows[:, :, None, None, None] * cols[:, None, None, :, None] * tiles[:, None, :, None, :]
+    return spread.sum(axis=0).reshape(orb_count, orb_count)
 
 
 def vcycle(residuals, inv_tiles):

time: 78.1 us -> 66.6 us (0.85)
  local copies, waits for them, and re-layouts: 14.5 us -> 6.36 us
  between operations: 6.02 us -> 0.91 us
  other arithmetic: 7 us -> 11.1 us
  waiting for transfers between devices: 19.1 us -> 17.7 us
    unnamed x68 -> x49, local copies, waits for them, and re-layouts: 4.91 us -> 0.19 us
    dynamic_update_slice x4 -> x0, local copies, waits for them, and re-layouts: 4.22 us -> none  [gram_matrix(): total = lax.dynamic_update_slice(total, piece[slot], (row, col))]
    slice x9 -> x6, local copies, waits for them, and re-layouts: 2.55 us -> 0.07 us  [extend_axis(): extras[step] = both[block.shape[0]:].reshape(extra.shape)]
    reduce_sum x0 -> x1, local copies, waits for them, and re-layouts: none -> 1.67 us  [gram_matrix(): return spread.sum(axis=0).reshape(orb_count, orb_count)]
    reshape x0 -> x1, local copies, waits for them, and re-layouts: none -> 1.64 us  [gram_matrix(): return spread.sum(axis=0).reshape(orb_count, orb_count)]
    ppermute x15, waiting for transfers between devices: 18.3 us -> 16.7 us  [shifted(): lax.ppermute(block, axis, [(j, (j - step) % count) for j in range(count)])]
    sub x1, other arithmetic: 0.95 us -> 1.86 us  [vcycle(): rhs_one = restrict(rhs_zero - stencil(corr_zero, faces_zero, 0))]
    add x2, other arithmetic: 0.16 us -> 1.06 us  [post_smooth(): hi = corr_faces[dim][1] + prolong_face(coarse_face_list[dim][1], dim)]
  transfers between devices with their start and end apart: 25 -> 25, of which waited for: 10 -> 9; matrix products, arithmetic and copies ran while one was open for 10% -> 15% of each run, Pallas kernels for 0% -> 0%
where the time goes in v14:
time: 66.6 us; the launch traced here: 66.3 us
  starting transfers between devices  26.5 us (40%)
  waiting for transfers between devices  17.7 us (27%)
  other arithmetic  11.1 us (17%)
  local copies, waits for them, and re-layouts  6.36 us (10%)
  matrix products  3.72 us (6%)
  between operations  0.91 us (1%)
    ppermute x15, waiting for transfers between devices, shifted(): lax.ppermute(block, axis, [(j, (j - step) % count) for j in range(count)])  16.7 us
    ppermute x15, starting transfers between devices, shifted(): lax.ppermute(block, axis, [(j, (j - step) % count) for j in range(count)])  14.9 us
    ppermute x7, starting transfers between devices, fetch(): cache[steps] = lax.ppermute(block, tuple(axes), pairs)  6.89 us
    ppermute x3, starting transfers between devices, axis_faces(): lax.ppermute(jnp.concatenate([first, last], axis=dim), axis, [(0, 1), (1,...  4.75 us
    div x3, other arithmetic, vcycle(): omega * part.astype(jnp.float32) / center  2.46 us
    dot_general x1, matrix products, coarse_solve(): jnp.einsum('qxyz,xyzgl->qgl', operator, extended, precision=lax.Precision...  1.92 us
    sub x1, other arithmetic, vcycle(): rhs_one = restrict(rhs_zero - stencil(corr_zero, faces_zero, 0))  1.86 us
    dot_general x1, matrix products, body(): jnp.dot(rows, gram, precision=lax.Precision.HIGH, preferred_element_type=...  1.8 us
  transfers between devices with their start and end apart: 25, of which 9 were waited for; matrix products, arithmetic and copies ran while one was open for 15% of the time, Pallas kernels for 0%

profile of v14, /device:TPU:0, one launch (start us, length us, event | category | flops | bytes accessed | tf_op | source)
XLA Modules:
  0.0 66.3 jit_solution(8188304920179550868)
XLA Ops:
  0.0 1.5 %fusion.57 = (f32[8,8,1,4,128]{4,2,3,1,0:T(1,128)S(1)}, f32[8,8,1,4,128]{4,2,3,1,0:T(1,128)S(1)}) fusion(bf16[8,8,8,4,128]{4,2,3,1,0:T(8,128)(2,1)} %bitcast.71), kind=kLoop, calls=%fused_computation.133 | loop fusion | flops 131072 | bytes 393216 | tf_op jit(solution)/shard_map/div | solution.py:311
  1.6 0.6 collective-permute-start.4
  2.1 0.9 %convert_multiply_fusion.3 = (f32[8,1,8,4,128]{4,2,3,1,0:T(8,128)S(1)}, f32[8,1,8,4,128]{4,2,3,1,0:T(8,128)S(1)}) fusion(bf16[8,8,8,4,128]{4,2,3,1,0:T(8,128)(2,1)} %bitcast.72), kind=kLoop, calls=%fused_computation.135 | loop fusion | flops 131072 | bytes 393216 | tf_op jit(solution)/shard_map/div | solution.py:311
  3.0 2.6 %collective-permute-start.2 = (f32[8,2,8,4,128]{4,2,3,1,0:T(8,128)S(1)}, f32[8,2,8,4,128]{4,2,3,1,0:T(8,128)S(1)}, u32[]{:S(2)}, u32[]{:S(2)}) collective-permute-start(f32[8,2,8,4,128]{4,2,3,1,0:T(8,128)S(1)} %pad_maximum_fusion.32), channel_id=1, source_target_pairs={{0,4},{4,0},{1,5},{5,1},{2,6},{6,2},{3,7},{7,3},{8,12},{12,8},{9,1... | collective-permute-start | bytes 786440 | tf_op jit(solution)/shard_map/ppermute | solution.py:37
  5.7 3.7 %collective-permute-start = (f32[1,8,8,4,128]{4,2,3,1,0:T(8,128)S(1)}, f32[1,8,8,4,128]{4,2,3,1,0:T(8,128)}, u32[]{:S(2)}, u32[]{:S(2)}) collective-permute-start(f32[1,8,8,4,128]{4,2,3,1,0:T(8,128)S(1)} %get-tuple-element.10), channel_id=1, source_target_pairs={{0,24},{8,0},{16,8},{24,16},{1,25},{9,1},{17,9},{25,17},{2,26},{10... | collective-permute-start | bytes 393224 | tf_op jit(solution)/shard_map/ppermute | solution.py:24
  9.3 1.2 %collective-permute-start.3 = (f32[8,8,1,4,128]{4,2,3,1,0:T(1,128)S(1)}, f32[8,8,1,4,128]{4,2,3,1,0:T(1,128)S(1)}, u32[]{:S(2)}, u32[]{:S(2)}) collective-permute-start(f32[8,8,1,4,128]{4,2,3,1,0:T(1,128)S(1)} %get-tuple-element.7), channel_id=1, source_target_pairs={{0,3},{1,0},{2,1},{3,2},{4,7},{5,4},{6,5},{7,6},{8,11},{9,8},{10,9... | collective-permute-start | bytes 393224 | tf_op jit(solution)/shard_map/ppermute | solution.py:24
  10.5 0.7 copy.45
  11.4 0.6 gather_fusion
  12.1 0.2 slice_reduce_fusion.1
  12.6 0.7 %fusion.58 = (f32[4,4]{1,0:T(4,128)}, f32[4,4]{1,0:T(4,128)}) fusion(s32[4]{0:T(128)S(1)} %get-tuple-element.5, s32[4]{0:T(128)S(1)} %get-tuple-element.6), kind=kLoop, calls=%fused_computation.158 | loop fusion | flops 64 | bytes 160 | tf_op jit(solution)/shard_map/convert_element_type | solution.py:303
  13.5 3.9 %collective-permute-done.1 = f32[1,8,8,4,128]{4,2,3,1,0:T(8,128)S(1)} collective-permute-done((f32[1,8,8,4,128]{4,2,3,1,0:T(8,128)S(1)}, f32[1,8,8,4,128]{4,2,3,1,0:T(8,128)S(1)}, u32[]{:S(2)}, u32[]{:S(2)}) %collective-permute-start.1) | collective-permute-done | bytes 131104 | tf_op jit(solution)/shard_map/ppermute | solution.py:24
  17.4 1.9 %convert_subtract_fusion.1 = f32[8,8,8,4,128]{4,2,3,1,0:T(8,128)S(1)} fusion(f32[8,8,1,4,128]{4,2,3,1,0:T(1,128)S(1)} %collective-permute-done.4, f32[10,1,8,4,128]{4,2,3,1,0:T(8,128)S(1)} %pad.40, f32[10,1,8,4,128]{4,2,3,1,0:T(8,128)S(1)} %pad.41, f32[1,8,8,4,128]{4,2,3,1,0:T(8,128)} %collective-permute-done, ...), kind=kLoop, calls=%fused_computation.3 | loop fusion | flops 8912896 | bytes 3473408 | tf_op jit(solution)/shard_map/sub | solution.py:314
  19.3 0.7 %reduce_sum.27 = f32[4,4,4,4,128]{4,2,3,1,0:T(4,128)S(1)} reduce(f32[4,2,4,2,4,2,4,128]{7,5,4,6,3,2,1,0:T(2,128)S(1)} %bitcast.75, f32[]{:T(128)} %constant.93.clone.1), dimensions={1,3,5}, to_apply=%region_0.1 | reduce | flops 229376 | bytes 1179652 | tf_op jit(solution)/shard_map/reduce_sum | solution.py:177
  20.3 0.6 collective-permute-start.6
  20.8 0.2 collective-permute-start.5
  21.1 1.5 %collective-permute-start.8 = (f32[1,4,4,4,128]{4,2,3,1,0:T(4,128)S(1)}, f32[1,4,4,4,128]{4,2,3,1,0:T(4,128)S(1)}, u32[]{:S(2)}, u32[]{:S(2)}) collective-permute-start(f32[1,4,4,4,128]{4,2,3,1,0:T(4,128)S(1)} %get-tuple-element.26), channel_id=1, source_target_pairs={{0,24},{8,0},{16,8},{24,16},{1,25},{9,1},{17,9},{25,17},{2,26},{10... | collective-permute-start | bytes 98312 | tf_op jit(solution)/shard_map/ppermute | solution.py:24
  22.5 0.6 collective-permute-start.7
  23.1 1.1 %collective-permute-done.5 = f32[4,4,1,4,128]{4,2,3,1,0:T(1,128)S(1)} collective-permute-done((f32[4,4,1,4,128]{4,2,3,1,0:T(1,128)S(1)}, f32[4,4,1,4,128]{4,2,3,1,0:T(1,128)S(1)}, u32[]{:S(2)}, u32[]{:S(2)}) %collective-permute-start.5) | collective-permute-done | bytes 32800 | tf_op jit(solution)/shard_map/ppermute | solution.py:24
  24.3 0.6 collective-permute-done.6
  25.0 3.3 %collective-permute-done.7 = f32[1,4,4,4,128]{4,2,3,1,0:T(4,128)S(1)} collective-permute-done((f32[1,4,4,4,128]{4,2,3,1,0:T(4,128)S(1)}, f32[1,4,4,4,128]{4,2,3,1,0:T(4,128)S(1)}, u32[]{:S(2)}, u32[]{:S(2)}) %collective-permute-start.7) | collective-permute-done | bytes 32800 | tf_op jit(solution)/shard_map/ppermute | solution.py:24
  28.2 0.2 fusion.51
  28.7 1.0 %collective-permute-start.11 = (f32[10,2,2,4,128]{4,2,1,3,0:T(2,128)S(1)}, f32[10,2,2,4,128]{4,2,1,3,0:T(2,128)S(1)}, u32[]{:S(2)}, u32[]{:S(2)}) collective-permute-start(f32[10,2,2,4,128]{4,2,1,3,0:T(2,128)S(1)} %pad_maximum_fusion.52), channel_id=1, source_target_pairs={{0,16},{8,24},{16,0},{24,8},{1,17},{9,25},{17,1},{25,9},{2,18},{10... | collective-permute-start | bytes 245768 | tf_op jit(solution)/shard_map/ppermute | solution.py:24
  29.6 2.9 %collective-permute-start.10 = (f32[10,2,2,4,128]{4,2,1,3,0:T(2,128)S(1)}, f32[10,2,2,4,128]{4,2,1,3,0:T(2,128)S(1)}, u32[]{:S(2)}, u32[]{:S(2)}) collective-permute-start(f32[10,2,2,4,128]{4,2,1,3,0:T(2,128)S(1)} %pad_maximum_fusion.52), channel_id=1, source_target_pairs={{0,24},{8,0},{16,8},{24,16},{1,25},{9,1},{17,9},{25,17},{2,26},{10... | collective-permute-start | bytes 245768 | tf_op jit(solution)/shard_map/ppermute | solution.py:24
  32.6 3.3 %collective-permute-done.12 = f32[10,2,2,4,128]{4,2,1,3,0:T(2,128)S(1)} collective-permute-done((f32[10,2,2,4,128]{4,2,1,3,0:T(2,128)S(1)}, f32[10,2,2,4,128]{4,2,1,3,0:T(2,128)S(1)}, u32[]{:S(2)}, u32[]{:S(2)}) %collective-permute-start.12) | collective-permute-done | bytes 81952 | tf_op jit(solution)/shard_map/ppermute | solution.py:24
  35.9 2.6 %collective-permute-done.11 = f32[10,2,2,4,128]{4,2,1,3,0:T(2,128)S(1)} collective-permute-done((f32[10,2,2,4,128]{4,2,1,3,0:T(2,128)S(1)}, f32[10,2,2,4,128]{4,2,1,3,0:T(2,128)S(1)}, u32[]{:S(2)}, u32[]{:S(2)}) %collective-permute-start.11) | collective-permute-done | bytes 81952 | tf_op jit(solution)/shard_map/ppermute | solution.py:24
  38.5 0.6 pad_maximum_fusion.54
  39.2 1.3 %collective-permute-start.18 = (f32[8,2,2,4,128]{4,2,1,3,0:T(2,128)}, f32[8,2,2,4,128]{4,2,1,3,0:T(2,128)S(1)}, u32[]{:S(2)}, u32[]{:S(2)}) collective-permute-start(f32[8,2,2,4,128]{4,2,1,3,0:T(2,128)} %pad_maximum_fusion.54), channel_id=1, source_target_pairs={{6,0},{7,1},{4,2},{5,3},{2,4},{3,5},{0,6},{1,7},{14,8},{15,9},{12,... | collective-permute-start | bytes 196616 | tf_op jit(solution)/shard_map/ppermute | solution.py:108
  40.5 2.4 %collective-permute-start.17 = (f32[8,2,2,4,128]{4,2,1,3,0:T(2,128)}, f32[8,2,2,4,128]{4,2,1,3,0:T(2,128)}, u32[]{:S(2)}, u32[]{:S(2)}) collective-permute-start(f32[8,2,2,4,128]{4,2,1,3,0:T(2,128)} %pad_maximum_fusion.54), channel_id=1, source_target_pairs={{5,0},{6,1},{7,2},{4,3},{1,4},{2,5},{3,6},{0,7},{13,8},{14,9},{15,... | collective-permute-start | bytes 196616 | tf_op jit(solution)/shard_map/ppermute | solution.py:108
  42.9 0.5 collective-permute-start.16
  43.6 0.5 collective-permute-done.19
  44.1 1.2 %collective-permute-start.14 = (f32[8,2,2,4,128]{4,2,1,3,0:T(2,128)}, f32[8,2,2,4,128]{4,2,1,3,0:T(2,128)}, u32[]{:S(2)}, u32[]{:S(2)}) collective-permute-start(f32[8,2,2,4,128]{4,2,1,3,0:T(2,128)} %pad_maximum_fusion.54), channel_id=1, source_target_pairs={{2,0},{3,1},{0,2},{1,3},{6,4},{7,5},{4,6},{5,7},{10,8},{11,9},{8,1... | collective-permute-start | bytes 196616 | tf_op jit(solution)/shard_map/ppermute | solution.py:108
  45.3 1.4 %collective-permute-start.13 = (f32[8,2,2,4,128]{4,2,1,3,0:T(2,128)}, f32[8,2,2,4,128]{4,2,1,3,0:T(2,128)}, u32[]{:S(2)}, u32[]{:S(2)}) collective-permute-start(f32[8,2,2,4,128]{4,2,1,3,0:T(2,128)} %pad_maximum_fusion.54), channel_id=1, source_target_pairs={{1,0},{2,1},{3,2},{0,3},{5,4},{6,5},{7,6},{4,7},{9,8},{10,9},{11,1... | collective-permute-start | bytes 196616 | tf_op jit(solution)/shard_map/ppermute | solution.py:108
  46.8 0.4 multiply_reduce_fusion
  47.2 1.7 %copy.52 = f32[4,128,4,128]{3,2,1,0:T(4,128)} copy(f32[4,128,4,128]{3,1,2,0:T(8,128)S(1)} %multiply_reduce_fusion) | data formatting | bytes 2097152 | tf_op jit(solution)/shard_map/reduce_sum | solution.py:306
  48.8 1.6 %reshape.603 = f32[512,512,1,1]{1,0,2,3:T(8,128)S(1)} reshape(f32[4,128,4,128]{3,2,1,0:T(4,128)} %copy.52) | data formatting | bytes 2097152 | tf_op jit(solution)/shard_map/reshape | solution.py:306
  50.6 1.9 %convolution_bitcast_fusion = f32[216,4,128]{2,0,1:T(8,128)S(1)} fusion(f32[216,8,4,8,1]{0,3,2,4,1:T(8,128)} %constant.137, f32[8,2,2,4,128]{4,2,1,3,0:T(2,128)} %copy-done.22, f32[8,2,2,4,128]{4,2,1,3,0:T(2,128)} %copy-done.23, f32[8,2,2,4,128]{4,2,1,3,0:T(2,128)} %collective-permute-done.17, f32[8,2,2,4,128]{4,2,1,3,0:T(2,128)} %collective-permute-done.16, ...), kind=kOutput, calls=%fused_computation.7 | convolution fusion | flops 341049344 | bytes 1187840 | tf_op jit(solution)/shard_map/qxyz,xyzgl->qgl/dot_general | solution.py:195
  52.7 0.2 maximum_add_fusion
  52.9 0.2 fusion.47
  53.3 1.6 %collective-permute-start.22 = (f32[4,2,4,4,128]{4,2,3,1,0:T(4,128)S(1)}, f32[4,2,4,4,128]{4,2,3,1,0:T(4,128)S(1)}, u32[]{:S(2)}, u32[]{:S(2)}) collective-permute-start(f32[4,2,4,4,128]{4,2,3,1,0:T(4,128)S(1)} %pad_maximum_fusion.55), channel_id=1, source_target_pairs={{0,4},{4,0},{1,5},{5,1},{2,6},{6,2},{3,7},{7,3},{8,12},{12,8},{9,1... | collective-permute-start | bytes 196616 | tf_op jit(solution)/shard_map/ppermute | solution.py:37
  54.8 2.1 %collective-permute-start.20 = (f32[1,4,4,4,128]{4,2,3,1,0:T(4,128)S(1)}, f32[1,4,4,4,128]{4,2,3,1,0:T(4,128)S(1)}, u32[]{:S(2)}, u32[]{:S(2)}) collective-permute-start(f32[1,4,4,4,128]{4,2,3,1,0:T(4,128)S(1)} %get-tuple-element.20), channel_id=1, source_target_pairs={{0,24},{8,0},{16,8},{24,16},{1,25},{9,1},{17,9},{25,17},{2,26},{10... | collective-permute-start | bytes 98312 | tf_op jit(solution)/shard_map/ppermute | solution.py:24
  56.9 1.2 %collective-permute-start.23 = (f32[4,4,1,4,128]{4,2,3,1,0:T(1,128)S(1)}, f32[4,4,1,4,128]{4,2,3,1,0:T(1,128)S(1)}, u32[]{:S(2)}, u32[]{:S(2)}) collective-permute-start(f32[4,4,1,4,128]{4,2,3,1,0:T(1,128)S(1)} %get-tuple-element.17), channel_id=1, source_target_pairs={{0,3},{1,0},{2,1},{3,2},{4,7},{5,4},{6,5},{7,6},{8,11},{9,8},{10,9... | collective-permute-start | bytes 98312 | tf_op jit(solution)/shard_map/ppermute | solution.py:24
  58.2 0.6 broadcast_in_dim.88
  58.8 0.2 fusion.42
  59.3 0.9 %add.206 = f32[1,8,8,4,128]{4,2,3,1,0:T(8,128)S(1)} add(f32[1,8,8,4,128]{4,2,3,1,0:T(8,128)} %collective-permute-done, f32[1,8,8,4,128]{4,2,3,1,0:T(8,128)S(1)} %bitcast.81) | non-fusion elementwise | flops 32768 | bytes 393216 | tf_op jit(solution)/shard_map/add | solution.py:268
  60.2 2.4 %collective-permute-done.21 = f32[1,4,4,4,128]{4,2,3,1,0:T(4,128)S(1)} collective-permute-done((f32[1,4,4,4,128]{4,2,3,1,0:T(4,128)S(1)}, f32[1,4,4,4,128]{4,2,3,1,0:T(4,128)S(1)}, u32[]{:S(2)}, u32[]{:S(2)}) %collective-permute-start.21) | collective-permute-done | bytes 32800 | tf_op jit(solution)/shard_map/ppermute | solution.py:24
  63.2 1.0 %fusion.2 = f32[8,8,8,4,128]{4,2,3,1,0:T(8,128)S(1)} fusion(f32[8,8,8,4,128]{4,2,3,1,0:T(8,128)S(1)} %fusion.42, f32[8,8,1,4,128]{4,2,3,1,0:T(1,128)S(1)} %add.215, f32[10,1,8,4,128]{4,2,3,1,0:T(8,128)S(1)} %pad.48, f32[10,1,8,4,128]{4,2,3,1,0:T(8,128)S(1)} %pad.49, f32[1,8,8,4,128]{4,2,3,1,0:T(8,128)S(1)} %add.206, f32[1,8,8,4,128]{4,2,3,1,0:T(8,128)S(1)} %add.207, ...), kind=kLoop, calls=%fused_computation.10 | loop fusion | flops 9437184 | bytes 3473408 | tf_op jit(solution)/shard_map/add | solution.py:270
  64.3 0.2 bitcast_multiply_fusion
  64.5 1.8 %convolution_convert_fusion = bf16[8,8,8,512]{3,2,1,0:T(8,128)(2,1)} fusion(f32[8,8,8,512]{3,2,1,0:T(8,128)S(1)} %bitcast.74, f32[512,512,1,1]{1,0,2,3:T(8,128)S(1)} %reshape.603), kind=kOutput, calls=%fused_computation.6 | convolution fusion | flops 805568512 | bytes 2621440 | tf_op jit(solution)/shard_map/dot_general | solution.py:342
  (141 shorter events, 2.8 us)
Async XLA Ops:
  0.0 5.6 %copy-start = (bf16[8,8,8,512]{3,2,1,0:T(8,128)(2,1)S(1)}, bf16[8,8,8,512]{3,2,1,0:T(8,128)(2,1)}, u32[]{:S(2)}) copy-start(bf16[8,8,8,512]{3,2,1,0:T(8,128)(2,1)} %param.5) | copy-start | bytes 1572868
  0.0 10.5 %copy-start.8 = (f32[1,128,128]{2,1,0:T(8,128)S(1)}, f32[1,128,128]{2,1,0:T(8,128)}, u32[]{:S(2)}) copy-start(f32[1,128,128]{2,1,0:T(8,128)} %param.8) | copy-start | bytes 196612
  0.0 11.1 %copy-start.18 = (s32[3,2,512]{2,1,0:T(2,128)S(1)}, s32[3,2,512]{2,1,0:T(2,128)}, u32[]{:S(2)}) copy-start(s32[3,2,512]{2,1,0:T(2,128)} %param.6) | copy-start | bytes 36868
  0.0 11.2 %copy-start.21 = (s32[4,2]{0,1:T(2,128)S(1)}, s32[4,2]{0,1:T(2,128)}, u32[]{:S(2)}) copy-start(s32[4,2]{0,1:T(2,128)} %param.7) | copy-start | bytes 100
  1.6 11.9 %collective-permute-start.4 = (f32[8,8,1,4,128]{4,2,3,1,0:T(1,128)S(1)}, f32[8,8,1,4,128]{4,2,3,1,0:T(1,128)S(1)}, u32[]{:S(2)}, u32[]{:S(2)}) collective-permute-start(f32[8,8,1,4,128]{4,2,3,1,0:T(1,128)S(1)} %get-tuple-element.8), channel_id=1, source_target_pairs={{0,1},{1,2},{2,3},{3,0},{4,5},{5,6},{6,7},{7,4},{8,9},{9,10},{10,1... | collective-permute-start | bytes 393224 | tf_op jit(solution)/shard_map/ppermute | solution.py:24
  3.0 10.4 %collective-permute-start.2 = (f32[8,2,8,4,128]{4,2,3,1,0:T(8,128)S(1)}, f32[8,2,8,4,128]{4,2,3,1,0:T(8,128)S(1)}, u32[]{:S(2)}, u32[]{:S(2)}) collective-permute-start(f32[8,2,8,4,128]{4,2,3,1,0:T(8,128)S(1)} %pad_maximum_fusion.32), channel_id=1, source_target_pairs={{0,4},{4,0},{1,5},{5,1},{2,6},{6,2},{3,7},{7,3},{8,12},{12,8},{9,1... | collective-permute-start | bytes 786440 | tf_op jit(solution)/shard_map/ppermute | solution.py:37
  5.7 7.8 %collective-permute-start = (f32[1,8,8,4,128]{4,2,3,1,0:T(8,128)S(1)}, f32[1,8,8,4,128]{4,2,3,1,0:T(8,128)}, u32[]{:S(2)}, u32[]{:S(2)}) collective-permute-start(f32[1,8,8,4,128]{4,2,3,1,0:T(8,128)S(1)} %get-tuple-element.10), channel_id=1, source_target_pairs={{0,24},{8,0},{16,8},{24,16},{1,25},{9,1},{17,9},{25,17},{2,26},{10... | collective-permute-start | bytes 393224 | tf_op jit(solution)/shard_map/ppermute | solution.py:24
  9.3 8.1 %collective-permute-start.1 = (f32[1,8,8,4,128]{4,2,3,1,0:T(8,128)S(1)}, f32[1,8,8,4,128]{4,2,3,1,0:T(8,128)S(1)}, u32[]{:S(2)}, u32[]{:S(2)}) collective-permute-start(f32[1,8,8,4,128]{4,2,3,1,0:T(8,128)S(1)} %get-tuple-element.9), channel_id=1, source_target_pairs={{0,8},{8,16},{16,24},{24,0},{1,9},{9,17},{17,25},{25,1},{2,10},{10... | collective-permute-start | bytes 393224 | tf_op jit(solution)/shard_map/ppermute | solution.py:24
  9.3 8.1 %collective-permute-start.3 = (f32[8,8,1,4,128]{4,2,3,1,0:T(1,128)S(1)}, f32[8,8,1,4,128]{4,2,3,1,0:T(1,128)S(1)}, u32[]{:S(2)}, u32[]{:S(2)}) collective-permute-start(f32[8,8,1,4,128]{4,2,3,1,0:T(1,128)S(1)} %get-tuple-element.7), channel_id=1, source_target_pairs={{0,3},{1,0},{2,1},{3,2},{4,7},{5,4},{6,5},{7,6},{8,11},{9,8},{10,9... | collective-permute-start | bytes 393224 | tf_op jit(solution)/shard_map/ppermute | solution.py:24
  17.4 1.9 %copy-start.1 = (f32[1,8,8,4,128]{4,2,3,1,0:T(8,128)}, f32[1,8,8,4,128]{4,2,3,1,0:T(8,128)S(1)}, u32[]{:S(2)}) copy-start(f32[1,8,8,4,128]{4,2,3,1,0:T(8,128)S(1)} %collective-permute-done.1) | copy-start | bytes 393220
  20.0 8.5 %copy-start.7 = (f32[8,2,2,4,128]{4,2,1,3,0:T(2,128)S(1)}, f32[8,2,2,4,128]{4,2,1,3,0:T(2,128)}, u32[]{:S(2)}) copy-start(f32[8,2,2,4,128]{4,2,1,3,0:T(2,128)} %copy.45) | copy-start | bytes 196612
  20.1 12.4 %copy-start.19 = (f32[4,4]{1,0:T(4,128)S(1)}, f32[4,4]{1,0:T(4,128)}, u32[]{:S(2)}) copy-start(f32[4,4]{1,0:T(4,128)} %get-tuple-element.41) | copy-start | bytes 196
  20.1 12.4 %copy-start.20 = (f32[4,4]{1,0:T(4,128)S(1)}, f32[4,4]{1,0:T(4,128)}, u32[]{:S(2)}) copy-start(f32[4,4]{1,0:T(4,128)} %get-tuple-element.42) | copy-start | bytes 196
  20.2 2.9 %collective-permute-start.9 = (f32[4,4,1,4,128]{4,2,3,1,0:T(1,128)S(1)}, f32[4,4,1,4,128]{4,2,3,1,0:T(1,128)S(1)}, u32[]{:S(2)}, u32[]{:S(2)}) collective-permute-start(f32[4,4,1,4,128]{4,2,3,1,0:T(1,128)S(1)} %get-tuple-element.24), channel_id=1, source_target_pairs={{0,3},{1,0},{2,1},{3,2},{4,7},{5,4},{6,5},{7,6},{8,11},{9,8},{10,9... | collective-permute-start | bytes 98312 | tf_op jit(solution)/shard_map/ppermute | solution.py:24
  20.3 4.6 %collective-permute-start.6 = (f32[4,2,4,4,128]{4,2,3,1,0:T(4,128)S(1)}, f32[4,2,4,4,128]{4,2,3,1,0:T(4,128)S(1)}, u32[]{:S(2)}, u32[]{:S(2)}) collective-permute-start(f32[4,2,4,4,128]{4,2,3,1,0:T(4,128)S(1)} %pad_maximum_fusion.53), channel_id=1, source_target_pairs={{0,4},{4,0},{1,5},{5,1},{2,6},{6,2},{3,7},{7,3},{8,12},{12,8},{9,1... | collective-permute-start | bytes 196616 | tf_op jit(solution)/shard_map/ppermute | solution.py:37
  20.8 3.4 %collective-permute-start.5 = (f32[4,4,1,4,128]{4,2,3,1,0:T(1,128)S(1)}, f32[4,4,1,4,128]{4,2,3,1,0:T(1,128)S(1)}, u32[]{:S(2)}, u32[]{:S(2)}) collective-permute-start(f32[4,4,1,4,128]{4,2,3,1,0:T(1,128)S(1)} %get-tuple-element.23), channel_id=1, source_target_pairs={{0,1},{1,2},{2,3},{3,0},{4,5},{5,6},{6,7},{7,4},{8,9},{9,10},{10,1... | collective-permute-start | bytes 98312 | tf_op jit(solution)/shard_map/ppermute | solution.py:24
  21.1 3.9 %collective-permute-start.8 = (f32[1,4,4,4,128]{4,2,3,1,0:T(4,128)S(1)}, f32[1,4,4,4,128]{4,2,3,1,0:T(4,128)S(1)}, u32[]{:S(2)}, u32[]{:S(2)}) collective-permute-start(f32[1,4,4,4,128]{4,2,3,1,0:T(4,128)S(1)} %get-tuple-element.26), channel_id=1, source_target_pairs={{0,24},{8,0},{16,8},{24,16},{1,25},{9,1},{17,9},{25,17},{2,26},{10... | collective-permute-start | bytes 98312 | tf_op jit(solution)/shard_map/ppermute | solution.py:24
  22.5 5.7 %collective-permute-start.7 = (f32[1,4,4,4,128]{4,2,3,1,0:T(4,128)S(1)}, f32[1,4,4,4,128]{4,2,3,1,0:T(4,128)S(1)}, u32[]{:S(2)}, u32[]{:S(2)}) collective-permute-start(f32[1,4,4,4,128]{4,2,3,1,0:T(4,128)S(1)} %get-tuple-element.25), channel_id=1, source_target_pairs={{0,8},{8,16},{16,24},{24,0},{1,9},{9,17},{17,25},{25,1},{2,10},{10... | collective-permute-start | bytes 98312 | tf_op jit(solution)/shard_map/ppermute | solution.py:24
  24.8 18.7 %copy-start.3 = (f32[6,1,4,4,128]{4,2,3,1,0:T(4,128)}, f32[6,1,4,4,128]{4,2,3,1,0:T(4,128)S(1)}, u32[]{:S(2)}) copy-start(f32[6,1,4,4,128]{4,2,3,1,0:T(4,128)S(1)} %pad.46) | copy-start | bytes 147460
  24.9 18.7 %copy-start.5 = (f32[6,1,4,4,128]{4,2,3,1,0:T(4,128)}, f32[6,1,4,4,128]{4,2,3,1,0:T(4,128)S(1)}, u32[]{:S(2)}) copy-start(f32[6,1,4,4,128]{4,2,3,1,0:T(4,128)S(1)} %pad.45) | copy-start | bytes 147460
  24.9 18.7 %copy-start.9 = (f32[1,128,128]{2,1,0:T(8,128)S(1)}, f32[1,128,128]{2,1,0:T(8,128)}, u32[]{:S(2)}) copy-start(f32[1,128,128]{2,1,0:T(8,128)} %param.8) | copy-start | bytes 196612
  25.0 3.5 %copy-start.11 = (f32[1,4,4,4,128]{4,2,3,1,0:T(4,128)}, f32[1,4,4,4,128]{4,2,3,1,0:T(4,128)S(1)}, u32[]{:S(2)}) copy-start(f32[1,4,4,4,128]{4,2,3,1,0:T(4,128)S(1)} %collective-permute-done.8) | copy-start | bytes 98308
  28.2 15.1 %copy-start.13 = (f32[1,4,4,4,128]{4,2,3,1,0:T(4,128)}, f32[1,4,4,4,128]{4,2,3,1,0:T(4,128)S(1)}, u32[]{:S(2)}) copy-start(f32[1,4,4,4,128]{4,2,3,1,0:T(4,128)S(1)} %collective-permute-done.7) | copy-start | bytes 98308
  28.6 14.8 %copy-start.10 = (f32[2,2,2,4,128]{4,2,1,3,0:T(2,128)}, f32[2,2,2,4,128]{4,2,1,3,0:T(2,128)S(1)}, u32[]{:S(2)}) copy-start(f32[2,2,2,4,128]{4,2,1,3,0:T(2,128)S(1)} %copy_multiply_fusion) | copy-start | bytes 49156
  28.6 7.3 %collective-permute-start.12 = (f32[10,2,2,4,128]{4,2,1,3,0:T(2,128)S(1)}, f32[10,2,2,4,128]{4,2,1,3,0:T(2,128)S(1)}, u32[]{:S(2)}, u32[]{:S(2)}) collective-permute-start(f32[10,2,2,4,128]{4,2,1,3,0:T(2,128)S(1)} %pad_maximum_fusion.52), channel_id=1, source_target_pairs={{0,8},{8,16},{16,24},{24,0},{1,9},{9,17},{17,25},{25,1},{2,10},{10... | collective-permute-start | bytes 245768 | tf_op jit(solution)/shard_map/ppermute | solution.py:24
  28.7 9.8 %collective-permute-start.11 = (f32[10,2,2,4,128]{4,2,1,3,0:T(2,128)S(1)}, f32[10,2,2,4,128]{4,2,1,3,0:T(2,128)S(1)}, u32[]{:S(2)}, u32[]{:S(2)}) collective-permute-start(f32[10,2,2,4,128]{4,2,1,3,0:T(2,128)S(1)} %pad_maximum_fusion.52), channel_id=1, source_target_pairs={{0,16},{8,24},{16,0},{24,8},{1,17},{9,25},{17,1},{25,9},{2,18},{10... | collective-permute-start | bytes 245768 | tf_op jit(solution)/shard_map/ppermute | solution.py:24
  29.6 8.8 %collective-permute-start.10 = (f32[10,2,2,4,128]{4,2,1,3,0:T(2,128)S(1)}, f32[10,2,2,4,128]{4,2,1,3,0:T(2,128)S(1)}, u32[]{:S(2)}, u32[]{:S(2)}) collective-permute-start(f32[10,2,2,4,128]{4,2,1,3,0:T(2,128)S(1)} %pad_maximum_fusion.52), channel_id=1, source_target_pairs={{0,24},{8,0},{16,8},{24,16},{1,25},{9,1},{17,9},{25,17},{2,26},{10... | collective-permute-start | bytes 245768 | tf_op jit(solution)/shard_map/ppermute | solution.py:24
  35.9 7.5 %copy-start.15 = (f32[2,2,2,4,128]{4,2,1,3,0:T(2,128)}, f32[2,2,2,4,128]{4,2,1,3,0:T(2,128)S(1)}, u32[]{:S(2)}) copy-start(f32[2,2,2,4,128]{4,2,1,3,0:T(2,128)S(1)} %slice.315) | copy-start | bytes 49156
  38.5 4.9 %copy-start.16 = (f32[2,2,2,4,128]{4,2,1,3,0:T(2,128)}, f32[2,2,2,4,128]{4,2,1,3,0:T(2,128)S(1)}, u32[]{:S(2)}) copy-start(f32[2,2,2,4,128]{4,2,1,3,0:T(2,128)S(1)} %slice.314) | copy-start | bytes 49156
  38.5 4.9 %copy-start.17 = (f32[2,2,2,4,128]{4,2,1,3,0:T(2,128)}, f32[2,2,2,4,128]{4,2,1,3,0:T(2,128)S(1)}, u32[]{:S(2)}) copy-start(f32[2,2,2,4,128]{4,2,1,3,0:T(2,128)S(1)} %slice.313) | copy-start | bytes 49156
  39.2 4.9 %collective-permute-start.19 = (f32[8,2,2,4,128]{4,2,1,3,0:T(2,128)}, f32[8,2,2,4,128]{4,2,1,3,0:T(2,128)S(1)}, u32[]{:S(2)}, u32[]{:S(2)}) collective-permute-start(f32[8,2,2,4,128]{4,2,1,3,0:T(2,128)} %pad_maximum_fusion.54), channel_id=1, source_target_pairs={{7,0},{4,1},{5,2},{6,3},{3,4},{0,5},{1,6},{2,7},{15,8},{12,9},{13,... | collective-permute-start | bytes 196616 | tf_op jit(solution)/shard_map/ppermute | solution.py:108
  39.2 6.2 %collective-permute-start.18 = (f32[8,2,2,4,128]{4,2,1,3,0:T(2,128)}, f32[8,2,2,4,128]{4,2,1,3,0:T(2,128)S(1)}, u32[]{:S(2)}, u32[]{:S(2)}) collective-permute-start(f32[8,2,2,4,128]{4,2,1,3,0:T(2,128)} %pad_maximum_fusion.54), channel_id=1, source_target_pairs={{6,0},{7,1},{4,2},{5,3},{2,4},{3,5},{0,6},{1,7},{14,8},{15,9},{12,... | collective-permute-start | bytes 196616 | tf_op jit(solution)/shard_map/ppermute | solution.py:108
  40.5 10.0 %collective-permute-start.17 = (f32[8,2,2,4,128]{4,2,1,3,0:T(2,128)}, f32[8,2,2,4,128]{4,2,1,3,0:T(2,128)}, u32[]{:S(2)}, u32[]{:S(2)}) collective-permute-start(f32[8,2,2,4,128]{4,2,1,3,0:T(2,128)} %pad_maximum_fusion.54), channel_id=1, source_target_pairs={{5,0},{6,1},{7,2},{4,3},{1,4},{2,5},{3,6},{0,7},{13,8},{14,9},{15,... | collective-permute-start | bytes 196616 | tf_op jit(solution)/shard_map/ppermute | solution.py:108
  42.9 7.7 %collective-permute-start.16 = (f32[8,2,2,4,128]{4,2,1,3,0:T(2,128)}, f32[8,2,2,4,128]{4,2,1,3,0:T(2,128)}, u32[]{:S(2)}, u32[]{:S(2)}) collective-permute-start(f32[8,2,2,4,128]{4,2,1,3,0:T(2,128)} %pad_maximum_fusion.54), channel_id=1, source_target_pairs={{4,0},{5,1},{6,2},{7,3},{0,4},{1,5},{2,6},{3,7},{12,8},{13,9},{14,... | collective-permute-start | bytes 196616 | tf_op jit(solution)/shard_map/ppermute | solution.py:108
  43.4 7.2 %collective-permute-start.15 = (f32[8,2,2,4,128]{4,2,1,3,0:T(2,128)}, f32[8,2,2,4,128]{4,2,1,3,0:T(2,128)}, u32[]{:S(2)}, u32[]{:S(2)}) collective-permute-start(f32[8,2,2,4,128]{4,2,1,3,0:T(2,128)} %pad_maximum_fusion.54), channel_id=1, source_target_pairs={{3,0},{0,1},{1,2},{2,3},{7,4},{4,5},{5,6},{6,7},{11,8},{8,9},{9,10... | collective-permute-start | bytes 196616 | tf_op jit(solution)/shard_map/ppermute | solution.py:108
  44.1 3.1 %copy-start.22 = (f32[8,2,2,4,128]{4,2,1,3,0:T(2,128)}, f32[8,2,2,4,128]{4,2,1,3,0:T(2,128)S(1)}, u32[]{:S(2)}) copy-start(f32[8,2,2,4,128]{4,2,1,3,0:T(2,128)S(1)} %collective-permute-done.19) | copy-start | bytes 196612
  44.1 6.5 %collective-permute-start.14 = (f32[8,2,2,4,128]{4,2,1,3,0:T(2,128)}, f32[8,2,2,4,128]{4,2,1,3,0:T(2,128)}, u32[]{:S(2)}, u32[]{:S(2)}) collective-permute-start(f32[8,2,2,4,128]{4,2,1,3,0:T(2,128)} %pad_maximum_fusion.54), channel_id=1, source_target_pairs={{2,0},{3,1},{0,2},{1,3},{6,4},{7,5},{4,6},{5,7},{10,8},{11,9},{8,1... | collective-permute-start | bytes 196616 | tf_op jit(solution)/shard_map/ppermute | solution.py:108
  45.3 5.2 %collective-permute-start.13 = (f32[8,2,2,4,128]{4,2,1,3,0:T(2,128)}, f32[8,2,2,4,128]{4,2,1,3,0:T(2,128)}, u32[]{:S(2)}, u32[]{:S(2)}) collective-permute-start(f32[8,2,2,4,128]{4,2,1,3,0:T(2,128)} %pad_maximum_fusion.54), channel_id=1, source_target_pairs={{1,0},{2,1},{3,2},{0,3},{5,4},{6,5},{7,6},{4,7},{9,8},{10,9},{11,1... | collective-permute-start | bytes 196616 | tf_op jit(solution)/shard_map/ppermute | solution.py:108
  50.5 2.1 %copy-start.4 = (f32[6,1,4,4,128]{4,2,3,1,0:T(4,128)S(1)}, f32[6,1,4,4,128]{4,2,3,1,0:T(4,128)}, u32[]{:S(2)}) copy-start(f32[6,1,4,4,128]{4,2,3,1,0:T(4,128)} %copy-done.3) | copy-start | bytes 147460
  50.5 2.1 %copy-start.6 = (f32[6,1,4,4,128]{4,2,3,1,0:T(4,128)S(1)}, f32[6,1,4,4,128]{4,2,3,1,0:T(4,128)}, u32[]{:S(2)}) copy-start(f32[6,1,4,4,128]{4,2,3,1,0:T(4,128)} %copy-done.5) | copy-start | bytes 147460
  50.5 2.1 %copy-start.12 = (f32[1,4,4,4,128]{4,2,3,1,0:T(4,128)S(1)}, f32[1,4,4,4,128]{4,2,3,1,0:T(4,128)}, u32[]{:S(2)}) copy-start(f32[1,4,4,4,128]{4,2,3,1,0:T(4,128)} %copy-done.11) | copy-start | bytes 98308
  50.5 2.1 %copy-start.14 = (f32[1,4,4,4,128]{4,2,3,1,0:T(4,128)S(1)}, f32[1,4,4,4,128]{4,2,3,1,0:T(4,128)}, u32[]{:S(2)}) copy-start(f32[1,4,4,4,128]{4,2,3,1,0:T(4,128)} %copy-done.13) | copy-start | bytes 98308
  53.2 5.9 %collective-permute-start.24 = (f32[4,4,1,4,128]{4,2,3,1,0:T(1,128)S(1)}, f32[4,4,1,4,128]{4,2,3,1,0:T(1,128)S(1)}, u32[]{:S(2)}, u32[]{:S(2)}) collective-permute-start(f32[4,4,1,4,128]{4,2,3,1,0:T(1,128)S(1)} %get-tuple-element.18), channel_id=1, source_target_pairs={{0,1},{1,2},{2,3},{3,0},{4,5},{5,6},{6,7},{7,4},{8,9},{9,10},{10,1... | collective-permute-start | bytes 98312 | tf_op jit(solution)/shard_map/ppermute | solution.py:24
  53.3 9.7 %collective-permute-start.22 = (f32[4,2,4,4,128]{4,2,3,1,0:T(4,128)S(1)}, f32[4,2,4,4,128]{4,2,3,1,0:T(4,128)S(1)}, u32[]{:S(2)}, u32[]{:S(2)}) collective-permute-start(f32[4,2,4,4,128]{4,2,3,1,0:T(4,128)S(1)} %pad_maximum_fusion.55), channel_id=1, source_target_pairs={{0,4},{4,0},{1,5},{5,1},{2,6},{6,2},{3,7},{7,3},{8,12},{12,8},{9,1... | collective-permute-start | bytes 196616 | tf_op jit(solution)/shard_map/ppermute | solution.py:37
  54.8 4.4 %collective-permute-start.20 = (f32[1,4,4,4,128]{4,2,3,1,0:T(4,128)S(1)}, f32[1,4,4,4,128]{4,2,3,1,0:T(4,128)S(1)}, u32[]{:S(2)}, u32[]{:S(2)}) collective-permute-start(f32[1,4,4,4,128]{4,2,3,1,0:T(4,128)S(1)} %get-tuple-element.20), channel_id=1, source_target_pairs={{0,24},{8,0},{16,8},{24,16},{1,25},{9,1},{17,9},{25,17},{2,26},{10... | collective-permute-start | bytes 98312 | tf_op jit(solution)/shard_map/ppermute | solution.py:24
  56.9 5.7 %collective-permute-start.21 = (f32[1,4,4,4,128]{4,2,3,1,0:T(4,128)S(1)}, f32[1,4,4,4,128]{4,2,3,1,0:T(4,128)S(1)}, u32[]{:S(2)}, u32[]{:S(2)}) collective-permute-start(f32[1,4,4,4,128]{4,2,3,1,0:T(4,128)S(1)} %get-tuple-element.19), channel_id=1, source_target_pairs={{0,8},{8,16},{16,24},{24,0},{1,9},{9,17},{17,25},{25,1},{2,10},{10... | collective-permute-start | bytes 98312 | tf_op jit(solution)/shard_map/ppermute | solution.py:24
  56.9 5.8 %collective-permute-start.23 = (f32[4,4,1,4,128]{4,2,3,1,0:T(1,128)S(1)}, f32[4,4,1,4,128]{4,2,3,1,0:T(1,128)S(1)}, u32[]{:S(2)}, u32[]{:S(2)}) collective-permute-start(f32[4,4,1,4,128]{4,2,3,1,0:T(1,128)S(1)} %get-tuple-element.17), channel_id=1, source_target_pairs={{0,3},{1,0},{2,1},{3,2},{4,7},{5,4},{6,5},{7,6},{8,11},{9,8},{10,9... | collective-permute-start | bytes 98312 | tf_op jit(solution)/shard_map/ppermute | solution.py:24
  59.0 3.7 %copy-start.2 = (f32[1,8,8,4,128]{4,2,3,1,0:T(8,128)S(1)}, f32[1,8,8,4,128]{4,2,3,1,0:T(8,128)}, u32[]{:S(2)}) copy-start(f32[1,8,8,4,128]{4,2,3,1,0:T(8,128)} %copy-done.1) | copy-start | bytes 393220
  (1 other events, 1.8 us)

commit v15 on v10

--- a/solution.py
+++ b/solution.py
@@ -67,10 +67,17 @@
                 cache[step] = shifted(block, axis, step)
                 extras[step] = extra
             else:
-                both = jnp.concatenate([block.reshape(-1), extra.reshape(-1)])
-                both = shifted(both, axis, step)
-                cache[step] = both[: block.size].reshape(block.shape)
-                extras[step] = both[block.size :].reshape(extra.shape)
+                trailing = block.shape[1:]
+                if extra.size % int(np.prod(trailing)) == 0:
+                    both = jnp.concatenate([block, extra.reshape((-1,) + trailing)], axis=0)
+                    both = shifted(both, axis, step)
+                    cache[step] = both[: block.shape[0]]
+                    extras[step] = both[block.shape[0] :].reshape(extra.shape)
+                else:
+                    both = jnp.concatenate([block.reshape(-1), extra.reshape(-1)])
+                    both = shifted(both, axis, step)
+                    cache[step] = both[: block.size].reshape(block.shape)
+                    extras[step] = both[block.size :].reshape(extra.shape)
         pieces.append(cache[step])
     return jnp.concatenate(pieces, axis=dim), start, extras
 
@@ -183,7 +190,7 @@
     count_x = lax.axis_size("gx")
     offsets_x, start_x = axis_offsets(count_x, block[0], COARSE_HALO)
     cache = {}
-    tiles_by_step = {0: tiles}
+    tiles_by_step = {0: tile_rows}
     for offset in offsets_x:
         step = offset % count_x
         if step in cache:
@@ -193,7 +200,7 @@
             continue
         both = shifted(jnp.concatenate([rows, tile_rows], axis=0), "gx", step)
         cache[step] = both[: rows.shape[0]]
-        tiles_by_step[step] = both[rows.shape[0] :].reshape(tiles.shape)
+        tiles_by_step[step] = both[rows.shape[0] :]
     line = jnp.concatenate([cache[offset % count_x] for offset in offsets_x], axis=0)
     axes = ("gy", "gz")
     counts = [lax.axis_size(axis) for axis in axes]
@@ -325,19 +332,28 @@
     count = lax.axis_size("gx")
     local = inv_tiles.shape[0]
     tile_edge = inv_tiles.shape[1]
+    blocks = orb_count // tile_edge
     me = lax.axis_index("gx")
-    total = jnp.zeros((orb_count, orb_count), jnp.float32)
+    pieces = []
+    ids = []
     for step in range(count):
         piece = tiles_by_step.get(step)
         if piece is None:
-            piece = inv_tiles if step == 0 else shifted(inv_tiles, "gx", step)
-        owner = (me + step) % count
-        for slot in range(local):
-            tile_id = owner * local + slot
-            row = tile_pairs[tile_id, 0] * tile_edge
-            col = tile_pairs[tile_id, 1] * tile_edge
-            total = lax.dynamic_update_slice(total, piece[slot], (row, col))
-    return total
+            piece = shifted(inv_tiles, "gx", step)
+        split = orb_count // tile_edge
+        pieces.append(piece.reshape(local, tile_edge // split, split, tile_edge))
+        ids.append(((me + step) % count) * local + jnp.arange(local, dtype=jnp.int32))
+    tiles = jnp.concatenate(pieces, axis=0)
+    pairs = jnp.take(tile_pairs, jnp.concatenate(ids), axis=0)
+    block_ids = jnp.arange(blocks, dtype=jnp.int32)
+    rows = (pairs[:, 0][:, None] == block_ids[None, :]).astype(jnp.float32)
+    cols = (pairs[:, 1][:, None] == block_ids[None, :]).astype(jnp.float32)
+    spread = (
+        rows[:, :, None, None, None, None]
+        * cols[:, None, None, None, :, None]
+        * tiles[:, None, :, :, None, :]
+    )
+    return spread.sum(axis=0).reshape(orb_count, orb_count)
 
 
 def vcycle(residuals, inv_tiles):

time: 93.9 us -> 80.5 us (0.86)
  local copies, waits for them, and re-layouts: 23.6 us -> 7.93 us
  waiting for transfers between devices: 12.2 us -> 17.7 us
  between operations: 6.11 us -> 1.08 us
  other arithmetic: 7.79 us -> 10.1 us
  starting transfers between devices: 29.3 us -> 27.2 us
  matrix products: 13.8 us -> 15.9 us
    unnamed x70 -> x59, local copies, waits for them, and re-layouts: 7.45 us -> 1.3 us
    dynamic_update_slice x4 -> x0, local copies, waits for them, and re-layouts: 4.99 us -> none  [gram_matrix(): total = lax.dynamic_update_slice(total, piece[slot], (row, col))]
    ppermute x15, waiting for transfers between devices: 12.2 us -> 17.1 us  [shifted(): lax.ppermute(block, axis, [(j, (j - step) % count) for j in range(count)])]
    another operation x3 -> x0, local copies, waits for them, and re-layouts: 4.38 us -> none  [gram_matrix(): total = lax.dynamic_update_slice(total, piece[slot], (row, col))]
    slice x3 -> x4, local copies, waits for them, and re-layouts: 3.54 us -> 0.19 us  [the longest x1 0.18 us: gram_matrix(): rows = (pairs[:, 0][:, None] == block_ids[None, :]).astype(jnp.float32)]
    dot_general x11, matrix products: 12 us -> 14.1 us  [coarse_solve(): jnp.dot(jnp.asarray(operator), gathered, precision=lax.Precision.HIGHEST,...]
    ppermute x15, starting transfers between devices: 16.8 us -> 14.9 us  [shifted(): lax.ppermute(block, axis, [(j, (j - step) % count) for j in range(count)])]
    reshape x0 -> x4, local copies, waits for them, and re-layouts: none -> 1.72 us  [the longest x1 1.64 us: gram_matrix(): return spread.sum(axis=0).reshape(orb_count, orb_count)]
  transfers between devices with their start and end apart: 25 -> 25, of which waited for: 5 -> 8; matrix products, arithmetic and copies ran while one was open for 27% -> 25% of each run, Pallas kernels for 0% -> 0%
where the time goes in v15:
time: 80.5 us; the launch traced here: 79.9 us
  starting transfers between devices  27.2 us (34%)
  waiting for transfers between devices  17.7 us (22%)
  matrix products  15.9 us (20%)
  other arithmetic  10.1 us (13%)
  local copies, waits for them, and re-layouts  7.93 us (10%)
  between operations  1.08 us (1%)
    ppermute x15, waiting for transfers between devices, shifted(): lax.ppermute(block, axis, [(j, (j - step) % count) for j in range(count)])  17.1 us
    ppermute x15, starting transfers between devices, shifted(): lax.ppermute(block, axis, [(j, (j - step) % count) for j in range(count)])  14.9 us
    dot_general x11, matrix products, coarse_solve(): jnp.dot(jnp.asarray(operator), gathered, precision=lax.Precision.HIGHEST,...  14.1 us
    ppermute x7, starting transfers between devices, coarse_solve(): moved[steps] = lax.ppermute(line, axes, pairs)  7.61 us
    ppermute x3, starting transfers between devices, axis_faces(): lax.ppermute(jnp.concatenate([first, last], axis=dim), axis, [(0, 1), (1,...  4.68 us
    div x3, other arithmetic, vcycle(): omega * part.astype(jnp.float32) / center  2.49 us
    dot_general x1, matrix products, body(): jnp.dot(rows, gram, precision=lax.Precision.HIGH, preferred_element_type=...  1.8 us
    reduce_sum x1, local copies, waits for them, and re-layouts, gram_matrix(): return spread.sum(axis=0).reshape(orb_count, orb_count)  1.68 us
  transfers between devices with their start and end apart: 25, of which 8 were waited for; matrix products, arithmetic and copies ran while one was open for 25% of the time, Pallas kernels for 0%

profile of v15, /device:TPU:0, one launch (start us, length us, event | category | flops | bytes accessed | tf_op | source)
XLA Modules:
  0.0 79.9 jit_solution(3194329136558572645)
XLA Ops:
  0.0 1.6 %fusion.45 = (f32[8,8,1,4,128]{4,2,3,1,0:T(1,128)S(1)}, f32[8,8,1,4,128]{4,2,3,1,0:T(1,128)S(1)}) fusion(bf16[8,8,8,4,128]{4,2,3,1,0:T(8,128)(2,1)} %bitcast.87), kind=kLoop, calls=%fused_computation.122 | loop fusion | flops 131072 | bytes 393216 | tf_op jit(solution)/shard_map/div | solution.py:361
  1.6 0.6 collective-permute-start.4
  2.1 0.9 %convert_multiply_fusion.3 = (f32[8,1,8,4,128]{4,2,3,1,0:T(8,128)S(1)}, f32[8,1,8,4,128]{4,2,3,1,0:T(8,128)S(1)}) fusion(bf16[8,8,8,4,128]{4,2,3,1,0:T(8,128)(2,1)} %bitcast.88), kind=kLoop, calls=%fused_computation.124 | loop fusion | flops 131072 | bytes 393216 | tf_op jit(solution)/shard_map/div | solution.py:361
  3.1 2.6 %collective-permute-start.2 = (f32[8,2,8,4,128]{4,2,3,1,0:T(8,128)S(1)}, f32[8,2,8,4,128]{4,2,3,1,0:T(8,128)S(1)}, u32[]{:S(2)}, u32[]{:S(2)}) collective-permute-start(f32[8,2,8,4,128]{4,2,3,1,0:T(8,128)S(1)} %pad_maximum_fusion.32), channel_id=1, source_target_pairs={{0,4},{4,0},{1,5},{5,1},{2,6},{6,2},{3,7},{7,3},{8,12},{12,8},{9,1... | collective-permute-start | bytes 786440 | tf_op jit(solution)/shard_map/ppermute | solution.py:37
  5.7 3.7 %collective-permute-start = (f32[1,8,8,4,128]{4,2,3,1,0:T(8,128)S(1)}, f32[1,8,8,4,128]{4,2,3,1,0:T(8,128)S(1)}, u32[]{:S(2)}, u32[]{:S(2)}) collective-permute-start(f32[1,8,8,4,128]{4,2,3,1,0:T(8,128)S(1)} %get-tuple-element.10), channel_id=1, source_target_pairs={{0,24},{8,0},{16,8},{24,16},{1,25},{9,1},{17,9},{25,17},{2,26},{10... | collective-permute-start | bytes 393224 | tf_op jit(solution)/shard_map/ppermute | solution.py:24
  9.4 1.2 %collective-permute-start.3 = (f32[8,8,1,4,128]{4,2,3,1,0:T(1,128)S(1)}, f32[8,8,1,4,128]{4,2,3,1,0:T(1,128)S(1)}, u32[]{:S(2)}, u32[]{:S(2)}) collective-permute-start(f32[8,8,1,4,128]{4,2,3,1,0:T(1,128)S(1)} %get-tuple-element.7), channel_id=1, source_target_pairs={{0,3},{1,0},{2,1},{3,2},{4,7},{5,4},{6,5},{7,6},{8,11},{9,8},{10,9... | collective-permute-start | bytes 393224 | tf_op jit(solution)/shard_map/ppermute | solution.py:24
  10.8 0.6 gather_fusion
  12.1 0.7 broadcast_multiply_fusion.3
  13.0 4.4 %collective-permute-done.1 = f32[1,8,8,4,128]{4,2,3,1,0:T(8,128)S(1)} collective-permute-done((f32[1,8,8,4,128]{4,2,3,1,0:T(8,128)S(1)}, f32[1,8,8,4,128]{4,2,3,1,0:T(8,128)S(1)}, u32[]{:S(2)}, u32[]{:S(2)}) %collective-permute-start.1) | collective-permute-done | bytes 131104 | tf_op jit(solution)/shard_map/ppermute | solution.py:24
  17.5 1.0 %convert_subtract_fusion.1 = f32[8,8,8,4,128]{4,2,3,1,0:T(8,128)S(1)} fusion(f32[8,8,1,4,128]{4,2,3,1,0:T(1,128)S(1)} %collective-permute-done.4, f32[10,1,8,4,128]{4,2,3,1,0:T(8,128)S(1)} %pad.40, f32[10,1,8,4,128]{4,2,3,1,0:T(8,128)S(1)} %pad.41, f32[1,8,8,4,128]{4,2,3,1,0:T(8,128)S(1)} %collective-permute-done, ...), kind=kLoop, calls=%fused_computation.3 | loop fusion | flops 8912896 | bytes 3473408 | tf_op jit(solution)/shard_map/sub | solution.py:364
  18.5 0.7 reduce_sum.27
  19.4 0.6 collective-permute-start.6
  20.2 1.5 %collective-permute-start.8 = (f32[1,4,4,4,128]{4,2,3,1,0:T(4,128)S(1)}, f32[1,4,4,4,128]{4,2,3,1,0:T(4,128)S(1)}, u32[]{:S(2)}, u32[]{:S(2)}) collective-permute-start(f32[1,4,4,4,128]{4,2,3,1,0:T(4,128)S(1)} %get-tuple-element.26), channel_id=1, source_target_pairs={{0,24},{8,0},{16,8},{24,16},{1,25},{9,1},{17,9},{25,17},{2,26},{10... | collective-permute-start | bytes 98312 | tf_op jit(solution)/shard_map/ppermute | solution.py:24
  21.7 0.5 collective-permute-start.7
  22.3 1.1 %collective-permute-done.5 = f32[4,4,1,4,128]{4,2,3,1,0:T(1,128)S(1)} collective-permute-done((f32[4,4,1,4,128]{4,2,3,1,0:T(1,128)S(1)}, f32[4,4,1,4,128]{4,2,3,1,0:T(1,128)S(1)}, u32[]{:S(2)}, u32[]{:S(2)}) %collective-permute-start.5) | collective-permute-done | bytes 32800 | tf_op jit(solution)/shard_map/ppermute | solution.py:24
  23.4 0.6 collective-permute-done.6
  24.1 3.3 %collective-permute-done.7 = f32[1,4,4,4,128]{4,2,3,1,0:T(4,128)S(1)} collective-permute-done((f32[1,4,4,4,128]{4,2,3,1,0:T(4,128)S(1)}, f32[1,4,4,4,128]{4,2,3,1,0:T(4,128)S(1)}, u32[]{:S(2)}, u32[]{:S(2)}) %collective-permute-start.7) | collective-permute-done | bytes 32800 | tf_op jit(solution)/shard_map/ppermute | solution.py:24
  27.9 0.6 collective-permute-start.11
  28.5 3.2 %collective-permute-start.10 = (f32[40,512]{1,0:T(8,128)S(1)}, f32[40,512]{1,0:T(8,128)S(1)}, u32[]{:S(2)}, u32[]{:S(2)}) collective-permute-start(f32[40,512]{1,0:T(8,128)S(1)} %constant_dynamic-update-slice_fusion), channel_id=1, source_target_pairs={{0,24},{8,0},{16,8},{24,16},{1,25},{9,1},{17,9},{25,17},{2,26},{10... | collective-permute-start | bytes 245768 | tf_op jit(solution)/shard_map/ppermute | solution.py:24
  32.2 2.9 %collective-permute-done.12 = f32[40,512]{1,0:T(8,128)S(1)} collective-permute-done((f32[40,512]{1,0:T(8,128)S(1)}, f32[40,512]{1,0:T(8,128)S(1)}, u32[]{:S(2)}, u32[]{:S(2)}) %collective-permute-start.12) | collective-permute-done | bytes 81952 | tf_op jit(solution)/shard_map/ppermute | solution.py:24
  35.1 2.6 %collective-permute-done.11 = f32[40,512]{1,0:T(8,128)S(1)} collective-permute-done((f32[40,512]{1,0:T(8,128)S(1)}, f32[40,512]{1,0:T(8,128)S(1)}, u32[]{:S(2)}, u32[]{:S(2)}) %collective-permute-start.11) | collective-permute-done | bytes 81952 | tf_op jit(solution)/shard_map/ppermute | solution.py:24
  37.7 0.7 pad_maximum_fusion.53
  38.3 1.3 %collective-permute-start.18 = (f32[32,512]{1,0:T(8,128)}, f32[32,512]{1,0:T(8,128)}, u32[]{:S(2)}, u32[]{:S(2)}) collective-permute-start(f32[32,512]{1,0:T(8,128)} %pad_maximum_fusion.53), channel_id=1, source_target_pairs={{6,0},{7,1},{4,2},{5,3},{2,4},{3,5},{0,6},{1,7},{14,8},{15,9},{12,... | collective-permute-start | bytes 196616 | tf_op jit(solution)/shard_map/ppermute | solution.py:222
  39.6 2.4 %collective-permute-start.17 = (f32[32,512]{1,0:T(8,128)}, f32[32,512]{1,0:T(8,128)}, u32[]{:S(2)}, u32[]{:S(2)}) collective-permute-start(f32[32,512]{1,0:T(8,128)} %pad_maximum_fusion.53), channel_id=1, source_target_pairs={{5,0},{6,1},{7,2},{4,3},{1,4},{2,5},{3,6},{0,7},{13,8},{14,9},{15,... | collective-permute-start | bytes 196616 | tf_op jit(solution)/shard_map/ppermute | solution.py:222
  42.0 0.7 collective-permute-start.16
  43.0 1.4 %fusion.49 = f32[512,216]{0,1:T(8,128)S(1)} fusion(f32[216,8]{1,0:T(8,128)} %constant.140, f32[40,512]{1,0:T(8,128)} %copy-done.16), kind=kOutput, calls=%fused_computation.157 | convolution fusion | flops 10616832 | bytes 569344 | tf_op jit(solution)/shard_map/dot_general | solution.py:228
  44.4 2.2 %convolution_add_fusion.1 = f32[512,216]{0,1:T(8,128)} fusion(f32[512,216]{0,1:T(8,128)S(1)} %fusion.53, f32[216,8]{1,0:T(8,128)} %constant.138, f32[40,512]{1,0:T(8,128)} %copy-done.15), kind=kOutput, calls=%fused_computation.8 | convolution fusion | flops 10727424 | bytes 1011712 | tf_op jit(solution)/shard_map/dot_general | solution.py:228
  46.9 1.7 %copy.38 = f32[4,32,4,4,128]{4,3,2,1,0:T(4,128)} copy(f32[4,32,4,4,128]{4,1,3,2,0:T(8,128)S(1)} %multiply_reduce_fusion) | data formatting | bytes 2097152 | tf_op jit(solution)/shard_map/reduce_sum | solution.py:356
  48.6 1.6 %reshape.603 = f32[512,512,1,1]{1,0,2,3:T(8,128)S(1)} reshape(f32[4,32,4,4,128]{4,3,2,1,0:T(4,128)} %copy.38) | data formatting | bytes 2097152 | tf_op jit(solution)/shard_map/reshape | solution.py:356
  50.3 1.6 %collective-permute-start.14 = (f32[32,512]{1,0:T(8,128)}, f32[32,512]{1,0:T(8,128)S(1)}, u32[]{:S(2)}, u32[]{:S(2)}) collective-permute-start(f32[32,512]{1,0:T(8,128)} %pad_maximum_fusion.53), channel_id=1, source_target_pairs={{2,0},{3,1},{0,2},{1,3},{6,4},{7,5},{4,6},{5,7},{10,8},{11,9},{8,1... | collective-permute-start | bytes 196616 | tf_op jit(solution)/shard_map/ppermute | solution.py:222
  51.9 1.4 %fusion.69 = f32[512,216]{0,1:T(8,128)S(1)} fusion(f32[32,512]{1,0:T(8,128)} %collective-permute-done.19, f32[216,32]{1,0:T(8,128)} %constant.147), kind=kOutput, calls=%fused_computation.179 | convolution fusion | flops 42467328 | bytes 535552 | tf_op jit(solution)/shard_map/dot_general | solution.py:228
  53.3 1.7 %collective-permute-start.13 = (f32[32,512]{1,0:T(8,128)}, f32[32,512]{1,0:T(8,128)S(1)}, u32[]{:S(2)}, u32[]{:S(2)}) collective-permute-start(f32[32,512]{1,0:T(8,128)} %pad_maximum_fusion.53), channel_id=1, source_target_pairs={{1,0},{2,1},{3,2},{0,3},{5,4},{6,5},{7,6},{4,7},{9,8},{10,9},{11,1... | collective-permute-start | bytes 196616 | tf_op jit(solution)/shard_map/ppermute | solution.py:222
  55.0 1.4 %fusion.68 = f32[512,216]{0,1:T(8,128)S(1)} fusion(f32[32,512]{1,0:T(8,128)} %collective-permute-done.18, f32[216,32]{1,0:T(8,128)} %constant.146), kind=kOutput, calls=%fused_computation.178 | convolution fusion | flops 42467328 | bytes 535552 | tf_op jit(solution)/shard_map/dot_general | solution.py:228
  56.5 1.4 %fusion.67 = f32[512,216]{0,1:T(8,128)S(1)} fusion(f32[32,512]{1,0:T(8,128)} %collective-permute-done.17, f32[216,32]{1,0:T(8,128)S(1)} %copy-done.22), kind=kOutput, calls=%fused_computation.177 | convolution fusion | flops 42467328 | bytes 535552 | tf_op jit(solution)/shard_map/dot_general | solution.py:228
  57.9 1.4 %fusion.66 = f32[512,216]{0,1:T(8,128)S(1)} fusion(f32[32,512]{1,0:T(8,128)} %collective-permute-done.16, f32[216,32]{1,0:T(8,128)S(1)} %copy-done.21), kind=kOutput, calls=%fused_computation.176 | convolution fusion | flops 42467328 | bytes 535552 | tf_op jit(solution)/shard_map/dot_general | solution.py:228
  59.3 1.4 %fusion.65 = f32[512,216]{0,1:T(8,128)S(1)} fusion(f32[32,512]{1,0:T(8,128)} %collective-permute-done.15, f32[216,32]{1,0:T(8,128)S(1)} %copy-done.20), kind=kOutput, calls=%fused_computation.175 | convolution fusion | flops 42467328 | bytes 535552 | tf_op jit(solution)/shard_map/dot_general | solution.py:228
  60.7 0.5 fusion.64
  61.8 2.1 %fusion.8 = f32[216,512]{1,0:T(8,128)} fusion(f32[512,216]{0,1:T(8,128)S(1)} %fusion.69, f32[512,216]{0,1:T(8,128)S(1)} %fusion.68, f32[512,216]{0,1:T(8,128)S(1)} %fusion.67, f32[512,216]{0,1:T(8,128)S(1)} %fusion.66, f32[512,216]{0,1:T(8,128)S(1)} %fusion.65, f32[512,216]{0,1:T(8,128)S(1)} %fusion.64, f32[512,216]{0,1:T(8,128)S(1)} %fusion.63, ...), kind=kOutput, calls=%fused_computation.17 | convolution fusion | flops 11612160 | bytes 4446976 | tf_op jit(solution)/shard_map/dot_general | solution.py:228
  63.9 1.2 %reshape.586 = f32[6,6,6,4,128]{4,3,2,1,0:T(4,128)S(1)} reshape(f32[216,512]{1,0:T(8,128)} %fusion.8) | data formatting | bytes 884736 | tf_op jit(solution)/shard_map/reshape | solution.py:231
  65.0 1.1 %maximum_add_fusion = f32[6,6,6,4,128]{4,2,3,1,0:T(8,128)S(1)} fusion(f32[6,6,1,4,128]{4,2,3,1,0:T(1,128)S(1)} %pad.47, f32[6,1,4,4,128]{4,2,3,1,0:T(4,128)S(1)} %pad.46, f32[1,4,4,4,128]{4,2,3,1,0:T(4,128)S(1)} %collective-permute-done.8, f32[4,4,4,4,128]{4,2,3,1,0:T(4,128)S(1)} %broadcast_multiply_fusion.2, f32[1,4,4,4,128]{4,2,3,1,0:T(4,128)} %copy-done.14, ...), kind=kLoop, calls=%fused_computation.78 | loop fusion | flops 774144 | bytes 1327104 | tf_op jit(solution)/shard_map/add | solution.py:371
  66.4 1.5 %collective-permute-start.22 = (f32[4,2,4,4,128]{4,2,3,1,0:T(4,128)S(1)}, f32[4,2,4,4,128]{4,2,3,1,0:T(4,128)S(1)}, u32[]{:S(2)}, u32[]{:S(2)}) collective-permute-start(f32[4,2,4,4,128]{4,2,3,1,0:T(4,128)S(1)} %pad_maximum_fusion.54), channel_id=1, source_target_pairs={{0,4},{4,0},{1,5},{5,1},{2,6},{6,2},{3,7},{7,3},{8,12},{12,8},{9,1... | collective-permute-start | bytes 196616 | tf_op jit(solution)/shard_map/ppermute | solution.py:37
  68.0 2.1 %collective-permute-start.20 = (f32[1,4,4,4,128]{4,2,3,1,0:T(4,128)S(1)}, f32[1,4,4,4,128]{4,2,3,1,0:T(4,128)S(1)}, u32[]{:S(2)}, u32[]{:S(2)}) collective-permute-start(f32[1,4,4,4,128]{4,2,3,1,0:T(4,128)S(1)} %get-tuple-element.20), channel_id=1, source_target_pairs={{0,24},{8,0},{16,8},{24,16},{1,25},{9,1},{17,9},{25,17},{2,26},{10... | collective-permute-start | bytes 98312 | tf_op jit(solution)/shard_map/ppermute | solution.py:24
  70.1 1.2 %collective-permute-start.23 = (f32[4,4,1,4,128]{4,2,3,1,0:T(1,128)S(1)}, f32[4,4,1,4,128]{4,2,3,1,0:T(1,128)S(1)}, u32[]{:S(2)}, u32[]{:S(2)}) collective-permute-start(f32[4,4,1,4,128]{4,2,3,1,0:T(1,128)S(1)} %get-tuple-element.17), channel_id=1, source_target_pairs={{0,3},{1,0},{2,1},{3,2},{4,7},{5,4},{6,5},{7,6},{8,11},{9,8},{10,9... | collective-permute-start | bytes 98312 | tf_op jit(solution)/shard_map/ppermute | solution.py:24
  71.4 0.6 broadcast_in_dim.88
  72.2 0.6 copy-done.7
  73.1 2.7 %collective-permute-done.21 = f32[1,4,4,4,128]{4,2,3,1,0:T(4,128)S(1)} collective-permute-done((f32[1,4,4,4,128]{4,2,3,1,0:T(4,128)S(1)}, f32[1,4,4,4,128]{4,2,3,1,0:T(4,128)S(1)}, u32[]{:S(2)}, u32[]{:S(2)}) %collective-permute-start.21) | collective-permute-done | bytes 32800 | tf_op jit(solution)/shard_map/ppermute | solution.py:24
  76.8 1.0 %fusion.11 = f32[8,8,8,4,128]{4,2,3,1,0:T(8,128)S(1)} fusion(f32[8,8,8,4,128]{4,2,3,1,0:T(8,128)S(1)} %fusion.30, f32[8,8,1,4,128]{4,2,3,1,0:T(1,128)S(1)} %add.215, f32[10,1,8,4,128]{4,2,3,1,0:T(8,128)S(1)} %pad.48, f32[10,1,8,4,128]{4,2,3,1,0:T(8,128)S(1)} %pad.49, f32[1,8,8,4,128]{4,2,3,1,0:T(8,128)S(1)} %add.206, f32[1,8,8,4,128]{4,2,3,1,0:T(8,128)S(1)} %add.207, ...), kind=kLoop, calls=%fused_computation.20 | loop fusion | flops 9437184 | bytes 3473408 | tf_op jit(solution)/shard_map/add | solution.py:315
  78.1 1.8 %convolution_convert_fusion = bf16[8,8,8,512]{3,2,1,0:T(8,128)(2,1)} fusion(f32[8,8,8,512]{3,2,1,0:T(8,128)S(1)} %bitcast.90, f32[512,512,1,1]{1,0,2,3:T(8,128)S(1)} %reshape.603), kind=kOutput, calls=%fused_computation.6 | convolution fusion | flops 805568512 | bytes 2621440 | tf_op jit(solution)/shard_map/dot_general | solution.py:392
  (162 shorter events, 5.8 us)
Async XLA Ops:
  0.0 5.7 %copy-start = (bf16[8,8,8,512]{3,2,1,0:T(8,128)(2,1)S(1)}, bf16[8,8,8,512]{3,2,1,0:T(8,128)(2,1)}, u32[]{:S(2)}) copy-start(bf16[8,8,8,512]{3,2,1,0:T(8,128)(2,1)} %param.5) | copy-start | bytes 1572868
  0.0 10.5 %copy-start.13 = (f32[1,128,128]{2,1,0:T(8,128)S(1)}, f32[1,128,128]{2,1,0:T(8,128)}, u32[]{:S(2)}) copy-start(f32[1,128,128]{2,1,0:T(8,128)} %param.8) | copy-start | bytes 196612
  0.0 10.5 %copy-start.26 = (s32[3,2,512]{2,1,0:T(2,128)S(1)}, s32[3,2,512]{2,1,0:T(2,128)}, u32[]{:S(2)}) copy-start(s32[3,2,512]{2,1,0:T(2,128)} %param.6) | copy-start | bytes 36868
  0.0 10.6 %copy-start.27 = (s32[4,2]{0,1:T(2,128)S(1)}, s32[4,2]{0,1:T(2,128)}, u32[]{:S(2)}) copy-start(s32[4,2]{0,1:T(2,128)} %param.7) | copy-start | bytes 100
  1.6 11.4 %collective-permute-start.4 = (f32[8,8,1,4,128]{4,2,3,1,0:T(1,128)S(1)}, f32[8,8,1,4,128]{4,2,3,1,0:T(1,128)S(1)}, u32[]{:S(2)}, u32[]{:S(2)}) collective-permute-start(f32[8,8,1,4,128]{4,2,3,1,0:T(1,128)S(1)} %get-tuple-element.8), channel_id=1, source_target_pairs={{0,1},{1,2},{2,3},{3,0},{4,5},{5,6},{6,7},{7,4},{8,9},{9,10},{10,1... | collective-permute-start | bytes 393224 | tf_op jit(solution)/shard_map/ppermute | solution.py:24
  3.1 9.8 %collective-permute-start.2 = (f32[8,2,8,4,128]{4,2,3,1,0:T(8,128)S(1)}, f32[8,2,8,4,128]{4,2,3,1,0:T(8,128)S(1)}, u32[]{:S(2)}, u32[]{:S(2)}) collective-permute-start(f32[8,2,8,4,128]{4,2,3,1,0:T(8,128)S(1)} %pad_maximum_fusion.32), channel_id=1, source_target_pairs={{0,4},{4,0},{1,5},{5,1},{2,6},{6,2},{3,7},{7,3},{8,12},{12,8},{9,1... | collective-permute-start | bytes 786440 | tf_op jit(solution)/shard_map/ppermute | solution.py:37
  5.7 7.3 %collective-permute-start = (f32[1,8,8,4,128]{4,2,3,1,0:T(8,128)S(1)}, f32[1,8,8,4,128]{4,2,3,1,0:T(8,128)S(1)}, u32[]{:S(2)}, u32[]{:S(2)}) collective-permute-start(f32[1,8,8,4,128]{4,2,3,1,0:T(8,128)S(1)} %get-tuple-element.10), channel_id=1, source_target_pairs={{0,24},{8,0},{16,8},{24,16},{1,25},{9,1},{17,9},{25,17},{2,26},{10... | collective-permute-start | bytes 393224 | tf_op jit(solution)/shard_map/ppermute | solution.py:24
  9.3 8.1 %collective-permute-start.1 = (f32[1,8,8,4,128]{4,2,3,1,0:T(8,128)S(1)}, f32[1,8,8,4,128]{4,2,3,1,0:T(8,128)S(1)}, u32[]{:S(2)}, u32[]{:S(2)}) collective-permute-start(f32[1,8,8,4,128]{4,2,3,1,0:T(8,128)S(1)} %get-tuple-element.9), channel_id=1, source_target_pairs={{0,8},{8,16},{16,24},{24,0},{1,9},{9,17},{17,25},{25,1},{2,10},{10... | collective-permute-start | bytes 393224 | tf_op jit(solution)/shard_map/ppermute | solution.py:24
  9.4 8.1 %collective-permute-start.3 = (f32[8,8,1,4,128]{4,2,3,1,0:T(1,128)S(1)}, f32[8,8,1,4,128]{4,2,3,1,0:T(1,128)S(1)}, u32[]{:S(2)}, u32[]{:S(2)}) collective-permute-start(f32[8,8,1,4,128]{4,2,3,1,0:T(1,128)S(1)} %get-tuple-element.7), channel_id=1, source_target_pairs={{0,3},{1,0},{2,1},{3,2},{4,7},{5,4},{6,5},{7,6},{8,11},{9,8},{10,9... | collective-permute-start | bytes 393224 | tf_op jit(solution)/shard_map/ppermute | solution.py:24
  12.9 4.5 %copy-start.2 = (f32[8,2,8,4,128]{4,2,3,1,0:T(8,128)}, f32[8,2,8,4,128]{4,2,3,1,0:T(8,128)S(1)}, u32[]{:S(2)}) copy-start(f32[8,2,8,4,128]{4,2,3,1,0:T(8,128)S(1)} %collective-permute-done.2) | copy-start | bytes 786436
  13.0 5.5 %copy-start.6 = (f32[8,8,1,4,128]{4,2,3,1,0:T(1,128)}, f32[8,8,1,4,128]{4,2,3,1,0:T(1,128)S(1)}, u32[]{:S(2)}) copy-start(f32[8,8,1,4,128]{4,2,3,1,0:T(1,128)S(1)} %collective-permute-done.4) | copy-start | bytes 393220
  13.0 5.4 %copy-start.10 = (f32[1,8,8,4,128]{4,2,3,1,0:T(8,128)}, f32[1,8,8,4,128]{4,2,3,1,0:T(8,128)S(1)}, u32[]{:S(2)}) copy-start(f32[1,8,8,4,128]{4,2,3,1,0:T(8,128)S(1)} %collective-permute-done) | copy-start | bytes 393220
  19.3 12.4 %copy-start.24 = (f32[216,8]{1,0:T(8,128)S(1)}, f32[216,8]{1,0:T(8,128)}, u32[]{:S(2)}) copy-start(f32[216,8]{1,0:T(8,128)} %constant.137) | copy-start | bytes 20740
  19.4 2.9 %collective-permute-start.9 = (f32[4,4,1,4,128]{4,2,3,1,0:T(1,128)S(1)}, f32[4,4,1,4,128]{4,2,3,1,0:T(1,128)S(1)}, u32[]{:S(2)}, u32[]{:S(2)}) collective-permute-start(f32[4,4,1,4,128]{4,2,3,1,0:T(1,128)S(1)} %get-tuple-element.24), channel_id=1, source_target_pairs={{0,3},{1,0},{2,1},{3,2},{4,7},{5,4},{6,5},{7,6},{8,11},{9,8},{10,9... | collective-permute-start | bytes 98312 | tf_op jit(solution)/shard_map/ppermute | solution.py:24
  19.4 4.6 %collective-permute-start.6 = (f32[4,2,4,4,128]{4,2,3,1,0:T(4,128)S(1)}, f32[4,2,4,4,128]{4,2,3,1,0:T(4,128)S(1)}, u32[]{:S(2)}, u32[]{:S(2)}) collective-permute-start(f32[4,2,4,4,128]{4,2,3,1,0:T(4,128)S(1)} %pad_maximum_fusion.52), channel_id=1, source_target_pairs={{0,4},{4,0},{1,5},{5,1},{2,6},{6,2},{3,7},{7,3},{8,12},{12,8},{9,1... | collective-permute-start | bytes 196616 | tf_op jit(solution)/shard_map/ppermute | solution.py:37
  20.0 3.4 %collective-permute-start.5 = (f32[4,4,1,4,128]{4,2,3,1,0:T(1,128)S(1)}, f32[4,4,1,4,128]{4,2,3,1,0:T(1,128)S(1)}, u32[]{:S(2)}, u32[]{:S(2)}) collective-permute-start(f32[4,4,1,4,128]{4,2,3,1,0:T(1,128)S(1)} %get-tuple-element.23), channel_id=1, source_target_pairs={{0,1},{1,2},{2,3},{3,0},{4,5},{5,6},{6,7},{7,4},{8,9},{9,10},{10,1... | collective-permute-start | bytes 98312 | tf_op jit(solution)/shard_map/ppermute | solution.py:24
  20.2 3.9 %collective-permute-start.8 = (f32[1,4,4,4,128]{4,2,3,1,0:T(4,128)S(1)}, f32[1,4,4,4,128]{4,2,3,1,0:T(4,128)S(1)}, u32[]{:S(2)}, u32[]{:S(2)}) collective-permute-start(f32[1,4,4,4,128]{4,2,3,1,0:T(4,128)S(1)} %get-tuple-element.26), channel_id=1, source_target_pairs={{0,24},{8,0},{16,8},{24,16},{1,25},{9,1},{17,9},{25,17},{2,26},{10... | collective-permute-start | bytes 98312 | tf_op jit(solution)/shard_map/ppermute | solution.py:24
  21.7 5.7 %collective-permute-start.7 = (f32[1,4,4,4,128]{4,2,3,1,0:T(4,128)S(1)}, f32[1,4,4,4,128]{4,2,3,1,0:T(4,128)S(1)}, u32[]{:S(2)}, u32[]{:S(2)}) collective-permute-start(f32[1,4,4,4,128]{4,2,3,1,0:T(4,128)S(1)} %get-tuple-element.25), channel_id=1, source_target_pairs={{0,8},{8,16},{16,24},{24,0},{1,9},{9,17},{17,25},{25,1},{2,10},{10... | collective-permute-start | bytes 98312 | tf_op jit(solution)/shard_map/ppermute | solution.py:24
  24.0 18.9 %copy-start.12 = (f32[6,1,4,4,128]{4,2,3,1,0:T(4,128)}, f32[6,1,4,4,128]{4,2,3,1,0:T(4,128)S(1)}, u32[]{:S(2)}) copy-start(f32[6,1,4,4,128]{4,2,3,1,0:T(4,128)S(1)} %pad.45) | copy-start | bytes 147460
  27.5 15.5 %copy-start.14 = (f32[1,4,4,4,128]{4,2,3,1,0:T(4,128)}, f32[1,4,4,4,128]{4,2,3,1,0:T(4,128)S(1)}, u32[]{:S(2)}) copy-start(f32[1,4,4,4,128]{4,2,3,1,0:T(4,128)S(1)} %collective-permute-done.7) | copy-start | bytes 98308
  27.8 7.3 %collective-permute-start.12 = (f32[40,512]{1,0:T(8,128)S(1)}, f32[40,512]{1,0:T(8,128)S(1)}, u32[]{:S(2)}, u32[]{:S(2)}) collective-permute-start(f32[40,512]{1,0:T(8,128)S(1)} %constant_dynamic-update-slice_fusion), channel_id=1, source_target_pairs={{0,8},{8,16},{16,24},{24,0},{1,9},{9,17},{17,25},{25,1},{2,10},{10... | collective-permute-start | bytes 245768 | tf_op jit(solution)/shard_map/ppermute | solution.py:24
  27.9 9.8 %collective-permute-start.11 = (f32[40,512]{1,0:T(8,128)S(1)}, f32[40,512]{1,0:T(8,128)S(1)}, u32[]{:S(2)}, u32[]{:S(2)}) collective-permute-start(f32[40,512]{1,0:T(8,128)S(1)} %constant_dynamic-update-slice_fusion), channel_id=1, source_target_pairs={{0,16},{8,24},{16,0},{24,8},{1,17},{9,25},{17,1},{25,9},{2,18},{10... | collective-permute-start | bytes 245768 | tf_op jit(solution)/shard_map/ppermute | solution.py:24
  28.5 9.2 %collective-permute-start.10 = (f32[40,512]{1,0:T(8,128)S(1)}, f32[40,512]{1,0:T(8,128)S(1)}, u32[]{:S(2)}, u32[]{:S(2)}) collective-permute-start(f32[40,512]{1,0:T(8,128)S(1)} %constant_dynamic-update-slice_fusion), channel_id=1, source_target_pairs={{0,24},{8,0},{16,8},{24,16},{1,25},{9,1},{17,9},{25,17},{2,26},{10... | collective-permute-start | bytes 245768 | tf_op jit(solution)/shard_map/ppermute | solution.py:24
  35.1 7.8 %copy-start.16 = (f32[40,512]{1,0:T(8,128)}, f32[40,512]{1,0:T(8,128)S(1)}, u32[]{:S(2)}) copy-start(f32[40,512]{1,0:T(8,128)S(1)} %collective-permute-done.12) | copy-start | bytes 245764
  37.6 5.2 %copy-start.17 = (f32[40,512]{1,0:T(8,128)}, f32[40,512]{1,0:T(8,128)S(1)}, u32[]{:S(2)}) copy-start(f32[40,512]{1,0:T(8,128)S(1)} %collective-permute-done.11) | copy-start | bytes 245764
  37.7 5.1 %copy-start.15 = (f32[40,512]{1,0:T(8,128)}, f32[40,512]{1,0:T(8,128)S(1)}, u32[]{:S(2)}) copy-start(f32[40,512]{1,0:T(8,128)S(1)} %collective-permute-done.10) | copy-start | bytes 245764
  38.3 11.9 %collective-permute-start.19 = (f32[32,512]{1,0:T(8,128)}, f32[32,512]{1,0:T(8,128)}, u32[]{:S(2)}, u32[]{:S(2)}) collective-permute-start(f32[32,512]{1,0:T(8,128)} %pad_maximum_fusion.53), channel_id=1, source_target_pairs={{7,0},{4,1},{5,2},{6,3},{3,4},{0,5},{1,6},{2,7},{15,8},{12,9},{13,... | collective-permute-start | bytes 196616 | tf_op jit(solution)/shard_map/ppermute | solution.py:222
  38.3 15.0 %collective-permute-start.18 = (f32[32,512]{1,0:T(8,128)}, f32[32,512]{1,0:T(8,128)}, u32[]{:S(2)}, u32[]{:S(2)}) collective-permute-start(f32[32,512]{1,0:T(8,128)} %pad_maximum_fusion.53), channel_id=1, source_target_pairs={{6,0},{7,1},{4,2},{5,3},{2,4},{3,5},{0,6},{1,7},{14,8},{15,9},{12,... | collective-permute-start | bytes 196616 | tf_op jit(solution)/shard_map/ppermute | solution.py:222
  39.6 16.8 %collective-permute-start.17 = (f32[32,512]{1,0:T(8,128)}, f32[32,512]{1,0:T(8,128)}, u32[]{:S(2)}, u32[]{:S(2)}) collective-permute-start(f32[32,512]{1,0:T(8,128)} %pad_maximum_fusion.53), channel_id=1, source_target_pairs={{5,0},{6,1},{7,2},{4,3},{1,4},{2,5},{3,6},{0,7},{13,8},{14,9},{15,... | collective-permute-start | bytes 196616 | tf_op jit(solution)/shard_map/ppermute | solution.py:222
  42.0 15.9 %collective-permute-start.16 = (f32[32,512]{1,0:T(8,128)}, f32[32,512]{1,0:T(8,128)}, u32[]{:S(2)}, u32[]{:S(2)}) collective-permute-start(f32[32,512]{1,0:T(8,128)} %pad_maximum_fusion.53), channel_id=1, source_target_pairs={{4,0},{5,1},{6,2},{7,3},{0,4},{1,5},{2,6},{3,7},{12,8},{13,9},{14,... | collective-permute-start | bytes 196616 | tf_op jit(solution)/shard_map/ppermute | solution.py:222
  42.7 16.6 %collective-permute-start.15 = (f32[32,512]{1,0:T(8,128)}, f32[32,512]{1,0:T(8,128)}, u32[]{:S(2)}, u32[]{:S(2)}) collective-permute-start(f32[32,512]{1,0:T(8,128)} %pad_maximum_fusion.53), channel_id=1, source_target_pairs={{3,0},{0,1},{1,2},{2,3},{7,4},{4,5},{5,6},{6,7},{11,8},{8,9},{9,10... | collective-permute-start | bytes 196616 | tf_op jit(solution)/shard_map/ppermute | solution.py:222
  42.9 3.6 %copy-start.25 = (f32[4,4,4]{2,1,0:T(4,128)S(1)}, f32[4,4,4]{2,1,0:T(4,128)}, u32[]{:S(2)}) copy-start(f32[4,4,4]{2,1,0:T(4,128)} %broadcast_multiply_fusion.3) | copy-start | bytes 772
  50.3 6.2 %copy-start.22 = (f32[216,32]{1,0:T(8,128)S(1)}, f32[216,32]{1,0:T(8,128)}, u32[]{:S(2)}) copy-start(f32[216,32]{1,0:T(8,128)} %constant.145) | copy-start | bytes 82948
  50.3 7.6 %copy-start.21 = (f32[216,32]{1,0:T(8,128)S(1)}, f32[216,32]{1,0:T(8,128)}, u32[]{:S(2)}) copy-start(f32[216,32]{1,0:T(8,128)} %constant.144) | copy-start | bytes 82948
  50.3 10.4 %collective-permute-start.14 = (f32[32,512]{1,0:T(8,128)}, f32[32,512]{1,0:T(8,128)S(1)}, u32[]{:S(2)}, u32[]{:S(2)}) collective-permute-start(f32[32,512]{1,0:T(8,128)} %pad_maximum_fusion.53), channel_id=1, source_target_pairs={{2,0},{3,1},{0,2},{1,3},{6,4},{7,5},{4,6},{5,7},{10,8},{11,9},{8,1... | collective-permute-start | bytes 196616 | tf_op jit(solution)/shard_map/ppermute | solution.py:222
  53.3 6.0 %copy-start.20 = (f32[216,32]{1,0:T(8,128)S(1)}, f32[216,32]{1,0:T(8,128)}, u32[]{:S(2)}) copy-start(f32[216,32]{1,0:T(8,128)} %constant.143) | copy-start | bytes 82948
  53.3 7.9 %collective-permute-start.13 = (f32[32,512]{1,0:T(8,128)}, f32[32,512]{1,0:T(8,128)S(1)}, u32[]{:S(2)}, u32[]{:S(2)}) collective-permute-start(f32[32,512]{1,0:T(8,128)} %pad_maximum_fusion.53), channel_id=1, source_target_pairs={{1,0},{2,1},{3,2},{0,3},{5,4},{6,5},{7,6},{4,7},{9,8},{10,9},{11,1... | collective-permute-start | bytes 196616 | tf_op jit(solution)/shard_map/ppermute | solution.py:222
  56.5 4.3 %copy-start.19 = (f32[216,32]{1,0:T(8,128)S(1)}, f32[216,32]{1,0:T(8,128)}, u32[]{:S(2)}) copy-start(f32[216,32]{1,0:T(8,128)} %constant.142) | copy-start | bytes 82948
  57.9 3.4 %copy-start.18 = (f32[216,32]{1,0:T(8,128)S(1)}, f32[216,32]{1,0:T(8,128)}, u32[]{:S(2)}) copy-start(f32[216,32]{1,0:T(8,128)} %constant.141) | copy-start | bytes 82948
  59.3 2.5 %copy-start.1 = (f32[512,216]{0,1:T(8,128)S(1)}, f32[512,216]{0,1:T(8,128)}, u32[]{:S(2)}) copy-start(f32[512,216]{0,1:T(8,128)} %convolution_add_fusion.1) | copy-start | bytes 1327108
  59.3 2.5 %copy-start.23 = (f32[216,8]{1,0:T(8,128)S(1)}, f32[216,8]{1,0:T(8,128)}, u32[]{:S(2)}) copy-start(f32[216,8]{1,0:T(8,128)} %constant.139) | copy-start | bytes 20740
  66.3 5.8 %collective-permute-start.24 = (f32[4,4,1,4,128]{4,2,3,1,0:T(1,128)S(1)}, f32[4,4,1,4,128]{4,2,3,1,0:T(1,128)S(1)}, u32[]{:S(2)}, u32[]{:S(2)}) collective-permute-start(f32[4,4,1,4,128]{4,2,3,1,0:T(1,128)S(1)} %get-tuple-element.18), channel_id=1, source_target_pairs={{0,1},{1,2},{2,3},{3,0},{4,5},{5,6},{6,7},{7,4},{8,9},{9,10},{10,1... | collective-permute-start | bytes 98312 | tf_op jit(solution)/shard_map/ppermute | solution.py:24
  66.4 9.7 %collective-permute-start.22 = (f32[4,2,4,4,128]{4,2,3,1,0:T(4,128)S(1)}, f32[4,2,4,4,128]{4,2,3,1,0:T(4,128)S(1)}, u32[]{:S(2)}, u32[]{:S(2)}) collective-permute-start(f32[4,2,4,4,128]{4,2,3,1,0:T(4,128)S(1)} %pad_maximum_fusion.54), channel_id=1, source_target_pairs={{0,4},{4,0},{1,5},{5,1},{2,6},{6,2},{3,7},{7,3},{8,12},{12,8},{9,1... | collective-permute-start | bytes 196616 | tf_op jit(solution)/shard_map/ppermute | solution.py:37
  68.0 5.0 %collective-permute-start.20 = (f32[1,4,4,4,128]{4,2,3,1,0:T(4,128)S(1)}, f32[1,4,4,4,128]{4,2,3,1,0:T(4,128)S(1)}, u32[]{:S(2)}, u32[]{:S(2)}) collective-permute-start(f32[1,4,4,4,128]{4,2,3,1,0:T(4,128)S(1)} %get-tuple-element.20), channel_id=1, source_target_pairs={{0,24},{8,0},{16,8},{24,16},{1,25},{9,1},{17,9},{25,17},{2,26},{10... | collective-permute-start | bytes 98312 | tf_op jit(solution)/shard_map/ppermute | solution.py:24
  70.1 5.7 %collective-permute-start.21 = (f32[1,4,4,4,128]{4,2,3,1,0:T(4,128)S(1)}, f32[1,4,4,4,128]{4,2,3,1,0:T(4,128)S(1)}, u32[]{:S(2)}, u32[]{:S(2)}) collective-permute-start(f32[1,4,4,4,128]{4,2,3,1,0:T(4,128)S(1)} %get-tuple-element.19), channel_id=1, source_target_pairs={{0,8},{8,16},{16,24},{24,0},{1,9},{9,17},{17,25},{25,1},{2,10},{10... | collective-permute-start | bytes 98312 | tf_op jit(solution)/shard_map/ppermute | solution.py:24
  70.1 5.8 %collective-permute-start.23 = (f32[4,4,1,4,128]{4,2,3,1,0:T(1,128)S(1)}, f32[4,4,1,4,128]{4,2,3,1,0:T(1,128)S(1)}, u32[]{:S(2)}, u32[]{:S(2)}) collective-permute-start(f32[4,4,1,4,128]{4,2,3,1,0:T(1,128)S(1)} %get-tuple-element.17), channel_id=1, source_target_pairs={{0,3},{1,0},{2,1},{3,2},{4,7},{5,4},{6,5},{7,6},{8,11},{9,8},{10,9... | collective-permute-start | bytes 98312 | tf_op jit(solution)/shard_map/ppermute | solution.py:24
  72.1 3.7 %copy-start.9 = (f32[1,8,8,4,128]{4,2,3,1,0:T(8,128)S(1)}, f32[1,8,8,4,128]{4,2,3,1,0:T(8,128)}, u32[]{:S(2)}) copy-start(f32[1,8,8,4,128]{4,2,3,1,0:T(8,128)} %copy-done.8) | copy-start | bytes 393220
  72.2 3.7 %copy-start.5 = (f32[8,8,1,4,128]{4,2,3,1,0:T(1,128)S(1)}, f32[8,8,1,4,128]{4,2,3,1,0:T(1,128)}, u32[]{:S(2)}) copy-start(f32[8,8,1,4,128]{4,2,3,1,0:T(1,128)} %copy-done.4) | copy-start | bytes 393220
  (5 other events, 4.8 us)

commit v16 on v15

--- a/solution.py
+++ b/solution.py
@@ -184,9 +184,8 @@
 def coarse_solve(rhs_two, tiles):
     block = rhs_two.shape[:3]
     orbs = rhs_two.shape[3:]
-    width = int(np.prod(orbs))
-    rows = rhs_two.reshape(-1, width)
-    tile_rows = tiles.reshape(-1, width)
+    rows = rhs_two.reshape((-1,) + orbs)
+    tile_rows = tiles.reshape((-1,) + orbs)
     count_x = lax.axis_size("gx")
     offsets_x, start_x = axis_offsets(count_x, block[0], COARSE_HALO)
     cache = {}
@@ -221,12 +220,13 @@
                         pairs.append((source, target))
                     moved[steps] = lax.ppermute(line, axes, pairs)
             pieces.append(moved[steps])
-    gathered = jnp.concatenate(pieces, axis=0)
+    gathered = lax.optimization_barrier(jnp.concatenate(pieces, axis=0))
     operator = coarse_matrix(
         block, (offsets_x, plans[0][0], plans[1][0]), (start_x, plans[0][1], plans[1][1])
     )
-    post = jnp.dot(
-        jnp.asarray(operator), gathered, precision=lax.Precision.HIGHEST, preferred_element_type=jnp.float32
+    post = jnp.einsum(
+        "qe,e...->q...", jnp.asarray(operator), gathered, precision=lax.Precision.HIGHEST,
+        preferred_element_type=jnp.float32,
     )
     return post.reshape(tuple(2 * size + 2 for size in block) + orbs), tiles_by_step
 

time: 80.5 us -> 76.3 us (0.948)
  matrix products: 15.9 us -> 3.44 us
  local copies, waits for them, and re-layouts: 7.93 us -> 16.7 us
  waiting for transfers between devices: 17.7 us -> 21.3 us
  starting transfers between devices: 27.2 us -> 24.4 us
  other arithmetic: 10.1 us -> 9.22 us
    dot_general x11 -> x1, matrix products: 14.1 us -> 1.63 us  [coarse_solve(): jnp.einsum('qe,e...->q...', jnp.asarray(operator), gathered, precision=la...]
    unnamed x59 -> x45, local copies, waits for them, and re-layouts: 1.3 us -> 8.18 us
    ppermute x15, waiting for transfers between devices: 17.1 us -> 20.7 us  [shifted(): lax.ppermute(block, axis, [(j, (j - step) % count) for j in range(count)])]
    slice x3, local copies, waits for them, and re-layouts: 0.01 us -> 1.82 us  [coarse_solve(): cache[step] = both[:rows.shape[0]]]
    ppermute x7, starting transfers between devices: 7.61 us -> 5.98 us  [coarse_solve(): moved[steps] = lax.ppermute(line, axes, pairs)]
    ppermute x15, starting transfers between devices: 14.9 us -> 13.7 us  [shifted(): lax.ppermute(block, axis, [(j, (j - step) % count) for j in range(count)])]
    reshape x2 -> x0, local copies, waits for them, and re-layouts: 1.17 us -> none  [the longest x1 1.16 us: coarse_solve(): post.reshape(tuple((2 * size + 2 for size in block)) + orbs)]
    add x1, other arithmetic: 1.06 us -> 0.25 us  [vcycle(): updated_padded = padded_one + coarse_padded]
  transfers between devices with their start and end apart: 25 -> 25, of which waited for: 8 -> 10; matrix products, arithmetic and copies ran while one was open for 25% -> 23% of each run, Pallas kernels for 0% -> 0%
where the time goes in v16:
time: 76.3 us; the launch traced here: 75.8 us
  starting transfers between devices  24.4 us (32%)
  waiting for transfers between devices  21.3 us (28%)
  local copies, waits for them, and re-layouts  16.7 us (22%)
  other arithmetic  9.22 us (12%)
  matrix products  3.44 us (5%)
    ppermute x15, waiting for transfers between devices, shifted(): lax.ppermute(block, axis, [(j, (j - step) % count) for j in range(count)])  20.7 us
    ppermute x15, starting transfers between devices, shifted(): lax.ppermute(block, axis, [(j, (j - step) % count) for j in range(count)])  13.7 us
    unnamed x45, local copies, waits for them, and re-layouts  8.18 us
    ppermute x7, starting transfers between devices, coarse_solve(): moved[steps] = lax.ppermute(line, axes, pairs)  5.98 us
    ppermute x3, starting transfers between devices, axis_faces(): lax.ppermute(jnp.concatenate([first, last], axis=dim), axis, [(0, 1), (1,...  4.74 us
    div x3, other arithmetic, vcycle(): omega * part.astype(jnp.float32) / center  2.45 us
    slice x3, local copies, waits for them, and re-layouts, coarse_solve(): cache[step] = both[:rows.shape[0]]  1.82 us
    dot_general x1, matrix products, body(): jnp.dot(rows, gram, precision=lax.Precision.HIGH, preferred_element_type=...  1.81 us
  transfers between devices with their start and end apart: 25, of which 10 were waited for; matrix products, arithmetic and copies ran while one was open for 23% of the time, Pallas kernels for 0%

profile of v16, /device:TPU:0, one launch (start us, length us, event | category | flops | bytes accessed | tf_op | source)
XLA Modules:
  0.0 75.8 jit_solution(16430133399451394620)
XLA Ops:
  0.0 1.5 %fusion.36 = (f32[8,8,1,4,128]{4,2,3,1,0:T(1,128)S(1)}, f32[8,8,1,4,128]{4,2,3,1,0:T(1,128)S(1)}) fusion(bf16[8,8,8,4,128]{4,2,3,1,0:T(8,128)(2,1)} %bitcast.71), kind=kLoop, calls=%fused_computation.111 | loop fusion | flops 131072 | bytes 393216 | tf_op jit(solution)/shard_map/div | solution.py:361
  1.6 0.5 collective-permute-start.4
  2.1 0.9 %convert_multiply_fusion.3 = (f32[8,1,8,4,128]{4,2,3,1,0:T(8,128)S(1)}, f32[8,1,8,4,128]{4,2,3,1,0:T(8,128)S(1)}) fusion(bf16[8,8,8,4,128]{4,2,3,1,0:T(8,128)(2,1)} %bitcast.72), kind=kLoop, calls=%fused_computation.113 | loop fusion | flops 131072 | bytes 393216 | tf_op jit(solution)/shard_map/div | solution.py:361
  3.0 2.6 %collective-permute-start.2 = (f32[8,2,8,4,128]{4,2,3,1,0:T(8,128)S(1)}, f32[8,2,8,4,128]{4,2,3,1,0:T(8,128)S(1)}, u32[]{:S(2)}, u32[]{:S(2)}) collective-permute-start(f32[8,2,8,4,128]{4,2,3,1,0:T(8,128)S(1)} %pad_maximum_fusion.32), channel_id=1, source_target_pairs={{0,4},{4,0},{1,5},{5,1},{2,6},{6,2},{3,7},{7,3},{8,12},{12,8},{9,1... | collective-permute-start | bytes 786440 | tf_op jit(solution)/shard_map/ppermute | solution.py:37
  5.6 3.7 %collective-permute-start = (f32[1,8,8,4,128]{4,2,3,1,0:T(8,128)S(1)}, f32[1,8,8,4,128]{4,2,3,1,0:T(8,128)S(1)}, u32[]{:S(2)}, u32[]{:S(2)}) collective-permute-start(f32[1,8,8,4,128]{4,2,3,1,0:T(8,128)S(1)} %get-tuple-element.10), channel_id=1, source_target_pairs={{0,24},{8,0},{16,8},{24,16},{1,25},{9,1},{17,9},{25,17},{2,26},{10... | collective-permute-start | bytes 393224 | tf_op jit(solution)/shard_map/ppermute | solution.py:24
  9.3 1.2 %collective-permute-start.3 = (f32[8,8,1,4,128]{4,2,3,1,0:T(1,128)S(1)}, f32[8,8,1,4,128]{4,2,3,1,0:T(1,128)S(1)}, u32[]{:S(2)}, u32[]{:S(2)}) collective-permute-start(f32[8,8,1,4,128]{4,2,3,1,0:T(1,128)S(1)} %get-tuple-element.7), channel_id=1, source_target_pairs={{0,3},{1,0},{2,1},{3,2},{4,7},{5,4},{6,5},{7,6},{8,11},{9,8},{10,9... | collective-permute-start | bytes 393224 | tf_op jit(solution)/shard_map/ppermute | solution.py:24
  10.7 0.6 gather_fusion
  11.9 0.7 fusion.37
  12.9 4.5 %collective-permute-done.1 = f32[1,8,8,4,128]{4,2,3,1,0:T(8,128)S(1)} collective-permute-done((f32[1,8,8,4,128]{4,2,3,1,0:T(8,128)S(1)}, f32[1,8,8,4,128]{4,2,3,1,0:T(8,128)S(1)}, u32[]{:S(2)}, u32[]{:S(2)}) %collective-permute-start.1) | collective-permute-done | bytes 131104 | tf_op jit(solution)/shard_map/ppermute | solution.py:24
  17.4 0.9 %convert_subtract_fusion.1 = f32[8,8,8,4,128]{4,2,3,1,0:T(8,128)S(1)} fusion(f32[8,8,1,4,128]{4,2,3,1,0:T(1,128)S(1)} %collective-permute-done.4, f32[10,1,8,4,128]{4,2,3,1,0:T(8,128)S(1)} %pad.40, f32[10,1,8,4,128]{4,2,3,1,0:T(8,128)S(1)} %pad.41, f32[1,8,8,4,128]{4,2,3,1,0:T(8,128)S(1)} %collective-permute-done, ...), kind=kLoop, calls=%fused_computation.3 | loop fusion | flops 8912896 | bytes 3473408 | tf_op jit(solution)/shard_map/sub | solution.py:364
  18.4 0.7 reduce_sum.27
  19.4 0.6 collective-permute-start.6
  20.1 1.5 %collective-permute-start.8 = (f32[1,4,4,4,128]{4,2,3,1,0:T(4,128)S(1)}, f32[1,4,4,4,128]{4,2,3,1,0:T(4,128)S(1)}, u32[]{:S(2)}, u32[]{:S(2)}) collective-permute-start(f32[1,4,4,4,128]{4,2,3,1,0:T(4,128)S(1)} %get-tuple-element.26), channel_id=1, source_target_pairs={{0,24},{8,0},{16,8},{24,16},{1,25},{9,1},{17,9},{25,17},{2,26},{10... | collective-permute-start | bytes 98312 | tf_op jit(solution)/shard_map/ppermute | solution.py:24
  21.6 0.6 collective-permute-start.7
  22.2 1.1 %collective-permute-done.5 = f32[4,4,1,4,128]{4,2,3,1,0:T(1,128)S(1)} collective-permute-done((f32[4,4,1,4,128]{4,2,3,1,0:T(1,128)S(1)}, f32[4,4,1,4,128]{4,2,3,1,0:T(1,128)S(1)}, u32[]{:S(2)}, u32[]{:S(2)}) %collective-permute-start.5) | collective-permute-done | bytes 32800 | tf_op jit(solution)/shard_map/ppermute | solution.py:24
  23.3 0.6 collective-permute-done.6
  24.1 3.3 %collective-permute-done.7 = f32[1,4,4,4,128]{4,2,3,1,0:T(4,128)S(1)} collective-permute-done((f32[1,4,4,4,128]{4,2,3,1,0:T(4,128)S(1)}, f32[1,4,4,4,128]{4,2,3,1,0:T(4,128)S(1)}, u32[]{:S(2)}, u32[]{:S(2)}) %collective-permute-start.7) | collective-permute-done | bytes 32800 | tf_op jit(solution)/shard_map/ppermute | solution.py:24
  27.6 0.6 fusion.51
  28.4 2.0 %collective-permute-start.12 = (f32[40,4,128]{2,0,1:T(8,128)S(1)}, f32[40,4,128]{2,0,1:T(8,128)S(1)}, u32[]{:S(2)}, u32[]{:S(2)}) collective-permute-start(f32[40,4,128]{2,0,1:T(8,128)S(1)} %copy_dynamic-update-slice_fusion), channel_id=1, source_target_pairs={{0,8},{8,16},{16,24},{24,0},{1,9},{9,17},{17,25},{25,1},{2,10},{10... | collective-permute-start | bytes 245768 | tf_op jit(solution)/shard_map/ppermute | solution.py:24
  30.6 2.3 %collective-permute-done.10 = f32[40,4,128]{2,0,1:T(8,128)S(1)} collective-permute-done((f32[40,4,128]{2,0,1:T(8,128)S(1)}, f32[40,4,128]{2,0,1:T(8,128)S(1)}, u32[]{:S(2)}, u32[]{:S(2)}) %collective-permute-start.10) | collective-permute-done | bytes 81952 | tf_op jit(solution)/shard_map/ppermute | solution.py:24
  32.9 0.6 fusion.47
  33.5 5.1 %collective-permute-done.11 = f32[40,4,128]{2,0,1:T(8,128)S(1)} collective-permute-done((f32[40,4,128]{2,0,1:T(8,128)S(1)}, f32[40,4,128]{2,0,1:T(8,128)S(1)}, u32[]{:S(2)}, u32[]{:S(2)}) %collective-permute-start.11) | collective-permute-done | bytes 81952 | tf_op jit(solution)/shard_map/ppermute | solution.py:24
  38.6 0.6 fusion.48
  39.2 0.6 fusion.49
  39.8 0.6 pad_maximum_fusion.53
  40.4 1.6 %collective-permute-start.14 = (f32[32,4,128]{2,0,1:T(8,128)}, f32[32,4,128]{2,0,1:T(8,128)}, u32[]{:S(2)}, u32[]{:S(2)}) collective-permute-start(f32[32,4,128]{2,0,1:T(8,128)} %pad_maximum_fusion.53), channel_id=1, source_target_pairs={{2,0},{3,1},{0,2},{1,3},{6,4},{7,5},{4,6},{5,7},{10,8},{11,9},{8,1... | collective-permute-start | bytes 196616 | tf_op jit(solution)/shard_map/ppermute | solution.py:221
  42.1 1.5 %collective-permute-start.16 = (f32[32,4,128]{2,0,1:T(8,128)}, f32[32,4,128]{2,0,1:T(8,128)}, u32[]{:S(2)}, u32[]{:S(2)}) collective-permute-start(f32[32,4,128]{2,0,1:T(8,128)} %pad_maximum_fusion.53), channel_id=1, source_target_pairs={{4,0},{5,1},{6,2},{7,3},{0,4},{1,5},{2,6},{3,7},{12,8},{13,9},{14,... | collective-permute-start | bytes 196616 | tf_op jit(solution)/shard_map/ppermute | solution.py:221
  43.6 1.4 %collective-permute-start.17 = (f32[32,4,128]{2,0,1:T(8,128)}, f32[32,4,128]{2,0,1:T(8,128)}, u32[]{:S(2)}, u32[]{:S(2)}) collective-permute-start(f32[32,4,128]{2,0,1:T(8,128)} %pad_maximum_fusion.53), channel_id=1, source_target_pairs={{5,0},{6,1},{7,2},{4,3},{1,4},{2,5},{3,6},{0,7},{13,8},{14,9},{15,... | collective-permute-start | bytes 196616 | tf_op jit(solution)/shard_map/ppermute | solution.py:221
  45.1 0.4 multiply_reduce_fusion
  45.5 1.7 %copy.55 = f32[4,32,4,4,128]{4,3,2,1,0:T(4,128)} copy(f32[4,32,4,4,128]{4,1,3,2,0:T(8,128)S(1)} %multiply_reduce_fusion) | data formatting | bytes 2097152 | tf_op jit(solution)/shard_map/reduce_sum | solution.py:356
  47.1 1.6 %reshape.604 = f32[512,512,1,1]{1,0,2,3:T(8,128)S(1)} reshape(f32[4,32,4,4,128]{4,3,2,1,0:T(4,128)} %copy.55) | data formatting | bytes 2097152 | tf_op jit(solution)/shard_map/reshape | solution.py:356
  48.8 1.4 %collective-permute-start.18 = (f32[32,4,128]{2,0,1:T(8,128)}, f32[32,4,128]{2,0,1:T(8,128)S(1)}, u32[]{:S(2)}, u32[]{:S(2)}) collective-permute-start(f32[32,4,128]{2,0,1:T(8,128)} %pad_maximum_fusion.53), channel_id=1, source_target_pairs={{6,0},{7,1},{4,2},{5,3},{2,4},{3,5},{0,6},{1,7},{14,8},{15,9},{12,... | collective-permute-start | bytes 196616 | tf_op jit(solution)/shard_map/ppermute | solution.py:221
  50.2 1.5 %constant_dynamic-update-slice_fusion.7 = f32[256,4,128]{2,0,1:T(8,128)} fusion(f32[256,4,128]{2,0,1:T(8,128)} %get-tuple-element.34, f32[32,4,128]{2,0,1:T(8,128)} %collective-permute-done.13), kind=kLoop, calls=%fused_computation.134 | loop fusion | bytes 131072
  51.7 1.5 %constant_dynamic-update-slice_fusion.6 = f32[256,4,128]{2,0,1:T(8,128)} fusion(f32[256,4,128]{2,0,1:T(8,128)} %constant_dynamic-update-slice_fusion.7, f32[32,4,128]{2,0,1:T(8,128)} %collective-permute-done.14), kind=kLoop, calls=%fused_computation.133 | loop fusion | bytes 131072
  53.2 1.5 %constant_dynamic-update-slice_fusion.5 = f32[256,4,128]{2,0,1:T(8,128)} fusion(f32[256,4,128]{2,0,1:T(8,128)} %constant_dynamic-update-slice_fusion.6, f32[32,4,128]{2,0,1:T(8,128)} %collective-permute-done.15), kind=kLoop, calls=%fused_computation.132 | loop fusion | bytes 131072
  54.6 1.5 %constant_dynamic-update-slice_fusion.4 = f32[256,4,128]{2,0,1:T(8,128)} fusion(f32[256,4,128]{2,0,1:T(8,128)} %constant_dynamic-update-slice_fusion.5, f32[32,4,128]{2,0,1:T(8,128)} %collective-permute-done.16), kind=kLoop, calls=%fused_computation.131 | loop fusion | bytes 131072
  56.1 1.5 %constant_dynamic-update-slice_fusion.3 = f32[256,4,128]{2,0,1:T(8,128)} fusion(f32[256,4,128]{2,0,1:T(8,128)} %constant_dynamic-update-slice_fusion.4, f32[32,4,128]{2,0,1:T(8,128)} %collective-permute-done.17), kind=kLoop, calls=%fused_computation.130 | loop fusion | bytes 131072
  57.6 0.6 constant_dynamic-update-slice_fusion.2
  58.2 0.6 constant_dynamic-update-slice_fusion.1
  58.9 1.6 %fusion.53 = f32[216,4,128]{2,0,1:T(8,128)S(1)} fusion(f32[216,256,1]{1,0,2:T(8,128)S(1)} %copy-done.10, f32[256,4,128]{2,0,1:T(8,128)} %constant_dynamic-update-slice_fusion.1), kind=kOutput, calls=%fused_computation.174 | convolution fusion | flops 339738624 | bytes 1187840 | tf_op jit(solution)/shard_map/qe,e...->q.../dot_general | solution.py:227
  61.2 1.7 %collective-permute-start.24 = (f32[4,4,1,4,128]{4,2,3,1,0:T(1,128)S(1)}, f32[4,4,1,4,128]{4,2,3,1,0:T(1,128)S(1)}, u32[]{:S(2)}, u32[]{:S(2)}) collective-permute-start(f32[4,4,1,4,128]{4,2,3,1,0:T(1,128)S(1)} %get-tuple-element.18), channel_id=1, source_target_pairs={{0,1},{1,2},{2,3},{3,0},{4,5},{5,6},{6,7},{7,4},{8,9},{9,10},{10,1... | collective-permute-start | bytes 98312 | tf_op jit(solution)/shard_map/ppermute | solution.py:24
  63.0 1.6 %collective-permute-start.22 = (f32[4,2,4,4,128]{4,2,3,1,0:T(4,128)S(1)}, f32[4,2,4,4,128]{4,2,3,1,0:T(4,128)S(1)}, u32[]{:S(2)}, u32[]{:S(2)}) collective-permute-start(f32[4,2,4,4,128]{4,2,3,1,0:T(4,128)S(1)} %pad_maximum_fusion.54), channel_id=1, source_target_pairs={{0,4},{4,0},{1,5},{5,1},{2,6},{6,2},{3,7},{7,3},{8,12},{12,8},{9,1... | collective-permute-start | bytes 196616 | tf_op jit(solution)/shard_map/ppermute | solution.py:37
  64.6 1.9 %collective-permute-start.20 = (f32[1,4,4,4,128]{4,2,3,1,0:T(4,128)S(1)}, f32[1,4,4,4,128]{4,2,3,1,0:T(4,128)S(1)}, u32[]{:S(2)}, u32[]{:S(2)}) collective-permute-start(f32[1,4,4,4,128]{4,2,3,1,0:T(4,128)S(1)} %get-tuple-element.20), channel_id=1, source_target_pairs={{0,24},{8,0},{16,8},{24,16},{1,25},{9,1},{17,9},{25,17},{2,26},{10... | collective-permute-start | bytes 98312 | tf_op jit(solution)/shard_map/ppermute | solution.py:24
  66.7 0.6 broadcast_in_dim.88
  67.7 0.8 collective-permute-done.20
  68.6 3.6 %collective-permute-done.21 = f32[1,4,4,4,128]{4,2,3,1,0:T(4,128)S(1)} collective-permute-done((f32[1,4,4,4,128]{4,2,3,1,0:T(4,128)S(1)}, f32[1,4,4,4,128]{4,2,3,1,0:T(4,128)S(1)}, u32[]{:S(2)}, u32[]{:S(2)}) %collective-permute-start.21) | collective-permute-done | bytes 32800 | tf_op jit(solution)/shard_map/ppermute | solution.py:24
  72.8 1.0 %fusion.2 = f32[8,8,8,4,128]{4,2,3,1,0:T(8,128)S(1)} fusion(f32[8,8,8,4,128]{4,2,3,1,0:T(8,128)S(1)} %fusion.21, f32[8,8,1,4,128]{4,2,3,1,0:T(1,128)S(1)} %add.215, f32[10,1,8,4,128]{4,2,3,1,0:T(8,128)S(1)} %pad.48, f32[10,1,8,4,128]{4,2,3,1,0:T(8,128)S(1)} %pad.49, f32[1,8,8,4,128]{4,2,3,1,0:T(8,128)S(1)} %add.206, f32[1,8,8,4,128]{4,2,3,1,0:T(8,128)S(1)} %add.207, ...), kind=kLoop, calls=%fused_computation.9 | loop fusion | flops 9437184 | bytes 3473408 | tf_op jit(solution)/shard_map/add | solution.py:315
  74.0 1.8 %convolution_convert_fusion = bf16[8,8,8,512]{3,2,1,0:T(8,128)(2,1)} fusion(f32[8,8,8,512]{3,2,1,0:T(8,128)S(1)} %bitcast.74, f32[512,512,1,1]{1,0,2,3:T(8,128)S(1)} %reshape.604), kind=kOutput, calls=%fused_computation.6 | convolution fusion | flops 805568512 | bytes 2621440 | tf_op jit(solution)/shard_map/dot_general | solution.py:392
  (136 shorter events, 4.4 us)
Async XLA Ops:
  0.0 5.6 %copy-start = (bf16[8,8,8,512]{3,2,1,0:T(8,128)(2,1)S(1)}, bf16[8,8,8,512]{3,2,1,0:T(8,128)(2,1)}, u32[]{:S(2)}) copy-start(bf16[8,8,8,512]{3,2,1,0:T(8,128)(2,1)} %param.5) | copy-start | bytes 1572868
  0.0 10.5 %copy-start.15 = (s32[3,2,512]{2,1,0:T(2,128)S(1)}, s32[3,2,512]{2,1,0:T(2,128)}, u32[]{:S(2)}) copy-start(s32[3,2,512]{2,1,0:T(2,128)} %param.6) | copy-start | bytes 36868
  0.0 10.5 %copy-start.18 = (s32[4,2]{0,1:T(2,128)S(1)}, s32[4,2]{0,1:T(2,128)}, u32[]{:S(2)}) copy-start(s32[4,2]{0,1:T(2,128)} %param.7) | copy-start | bytes 100
  1.6 11.3 %collective-permute-start.4 = (f32[8,8,1,4,128]{4,2,3,1,0:T(1,128)S(1)}, f32[8,8,1,4,128]{4,2,3,1,0:T(1,128)S(1)}, u32[]{:S(2)}, u32[]{:S(2)}) collective-permute-start(f32[8,8,1,4,128]{4,2,3,1,0:T(1,128)S(1)} %get-tuple-element.8), channel_id=1, source_target_pairs={{0,1},{1,2},{2,3},{3,0},{4,5},{5,6},{6,7},{7,4},{8,9},{9,10},{10,1... | collective-permute-start | bytes 393224 | tf_op jit(solution)/shard_map/ppermute | solution.py:24
  3.0 9.7 %collective-permute-start.2 = (f32[8,2,8,4,128]{4,2,3,1,0:T(8,128)S(1)}, f32[8,2,8,4,128]{4,2,3,1,0:T(8,128)S(1)}, u32[]{:S(2)}, u32[]{:S(2)}) collective-permute-start(f32[8,2,8,4,128]{4,2,3,1,0:T(8,128)S(1)} %pad_maximum_fusion.32), channel_id=1, source_target_pairs={{0,4},{4,0},{1,5},{5,1},{2,6},{6,2},{3,7},{7,3},{8,12},{12,8},{9,1... | collective-permute-start | bytes 786440 | tf_op jit(solution)/shard_map/ppermute | solution.py:37
  5.6 7.3 %collective-permute-start = (f32[1,8,8,4,128]{4,2,3,1,0:T(8,128)S(1)}, f32[1,8,8,4,128]{4,2,3,1,0:T(8,128)S(1)}, u32[]{:S(2)}, u32[]{:S(2)}) collective-permute-start(f32[1,8,8,4,128]{4,2,3,1,0:T(8,128)S(1)} %get-tuple-element.10), channel_id=1, source_target_pairs={{0,24},{8,0},{16,8},{24,16},{1,25},{9,1},{17,9},{25,17},{2,26},{10... | collective-permute-start | bytes 393224 | tf_op jit(solution)/shard_map/ppermute | solution.py:24
  9.3 8.1 %collective-permute-start.1 = (f32[1,8,8,4,128]{4,2,3,1,0:T(8,128)S(1)}, f32[1,8,8,4,128]{4,2,3,1,0:T(8,128)S(1)}, u32[]{:S(2)}, u32[]{:S(2)}) collective-permute-start(f32[1,8,8,4,128]{4,2,3,1,0:T(8,128)S(1)} %get-tuple-element.9), channel_id=1, source_target_pairs={{0,8},{8,16},{16,24},{24,0},{1,9},{9,17},{17,25},{25,1},{2,10},{10... | collective-permute-start | bytes 393224 | tf_op jit(solution)/shard_map/ppermute | solution.py:24
  9.3 8.1 %collective-permute-start.3 = (f32[8,8,1,4,128]{4,2,3,1,0:T(1,128)S(1)}, f32[8,8,1,4,128]{4,2,3,1,0:T(1,128)S(1)}, u32[]{:S(2)}, u32[]{:S(2)}) collective-permute-start(f32[8,8,1,4,128]{4,2,3,1,0:T(1,128)S(1)} %get-tuple-element.7), channel_id=1, source_target_pairs={{0,3},{1,0},{2,1},{3,2},{4,7},{5,4},{6,5},{7,6},{8,11},{9,8},{10,9... | collective-permute-start | bytes 393224 | tf_op jit(solution)/shard_map/ppermute | solution.py:24
  12.9 5.5 %copy-start.3 = (f32[1,8,8,4,128]{4,2,3,1,0:T(8,128)}, f32[1,8,8,4,128]{4,2,3,1,0:T(8,128)S(1)}, u32[]{:S(2)}) copy-start(f32[1,8,8,4,128]{4,2,3,1,0:T(8,128)S(1)} %collective-permute-done) | copy-start | bytes 393220
  17.4 1.0 %copy-start.1 = (f32[1,8,8,4,128]{4,2,3,1,0:T(8,128)}, f32[1,8,8,4,128]{4,2,3,1,0:T(8,128)S(1)}, u32[]{:S(2)}) copy-start(f32[1,8,8,4,128]{4,2,3,1,0:T(8,128)S(1)} %collective-permute-done.1) | copy-start | bytes 393220
  19.2 9.1 %copy-start.9 = (f32[1,128,128]{2,1,0:T(8,128)S(1)}, f32[1,128,128]{2,1,0:T(8,128)}, u32[]{:S(2)}) copy-start(f32[1,128,128]{2,1,0:T(8,128)} %param.8) | copy-start | bytes 196612
  19.2 9.2 %copy-start.16 = (f32[4,4]{1,0:T(4,128)S(1)}, f32[4,4]{1,0:T(4,128)}, u32[]{:S(2)}) copy-start(f32[4,4]{1,0:T(4,128)} %get-tuple-element.50) | copy-start | bytes 196
  19.2 9.2 %copy-start.17 = (f32[4,4]{1,0:T(4,128)S(1)}, f32[4,4]{1,0:T(4,128)}, u32[]{:S(2)}) copy-start(f32[4,4]{1,0:T(4,128)} %get-tuple-element.51) | copy-start | bytes 196
  19.3 2.9 %collective-permute-start.9 = (f32[4,4,1,4,128]{4,2,3,1,0:T(1,128)S(1)}, f32[4,4,1,4,128]{4,2,3,1,0:T(1,128)S(1)}, u32[]{:S(2)}, u32[]{:S(2)}) collective-permute-start(f32[4,4,1,4,128]{4,2,3,1,0:T(1,128)S(1)} %get-tuple-element.24), channel_id=1, source_target_pairs={{0,3},{1,0},{2,1},{3,2},{4,7},{5,4},{6,5},{7,6},{8,11},{9,8},{10,9... | collective-permute-start | bytes 98312 | tf_op jit(solution)/shard_map/ppermute | solution.py:24
  19.4 4.6 %collective-permute-start.6 = (f32[4,2,4,4,128]{4,2,3,1,0:T(4,128)S(1)}, f32[4,2,4,4,128]{4,2,3,1,0:T(4,128)S(1)}, u32[]{:S(2)}, u32[]{:S(2)}) collective-permute-start(f32[4,2,4,4,128]{4,2,3,1,0:T(4,128)S(1)} %pad_maximum_fusion.52), channel_id=1, source_target_pairs={{0,4},{4,0},{1,5},{5,1},{2,6},{6,2},{3,7},{7,3},{8,12},{12,8},{9,1... | collective-permute-start | bytes 196616 | tf_op jit(solution)/shard_map/ppermute | solution.py:37
  19.9 3.4 %collective-permute-start.5 = (f32[4,4,1,4,128]{4,2,3,1,0:T(1,128)S(1)}, f32[4,4,1,4,128]{4,2,3,1,0:T(1,128)S(1)}, u32[]{:S(2)}, u32[]{:S(2)}) collective-permute-start(f32[4,4,1,4,128]{4,2,3,1,0:T(1,128)S(1)} %get-tuple-element.23), channel_id=1, source_target_pairs={{0,1},{1,2},{2,3},{3,0},{4,5},{5,6},{6,7},{7,4},{8,9},{9,10},{10,1... | collective-permute-start | bytes 98312 | tf_op jit(solution)/shard_map/ppermute | solution.py:24
  20.1 3.9 %collective-permute-start.8 = (f32[1,4,4,4,128]{4,2,3,1,0:T(4,128)S(1)}, f32[1,4,4,4,128]{4,2,3,1,0:T(4,128)S(1)}, u32[]{:S(2)}, u32[]{:S(2)}) collective-permute-start(f32[1,4,4,4,128]{4,2,3,1,0:T(4,128)S(1)} %get-tuple-element.26), channel_id=1, source_target_pairs={{0,24},{8,0},{16,8},{24,16},{1,25},{9,1},{17,9},{25,17},{2,26},{10... | collective-permute-start | bytes 98312 | tf_op jit(solution)/shard_map/ppermute | solution.py:24
  21.6 5.7 %collective-permute-start.7 = (f32[1,4,4,4,128]{4,2,3,1,0:T(4,128)S(1)}, f32[1,4,4,4,128]{4,2,3,1,0:T(4,128)S(1)}, u32[]{:S(2)}, u32[]{:S(2)}) collective-permute-start(f32[1,4,4,4,128]{4,2,3,1,0:T(4,128)S(1)} %get-tuple-element.25), channel_id=1, source_target_pairs={{0,8},{8,16},{16,24},{24,0},{1,9},{9,17},{17,25},{25,1},{2,10},{10... | collective-permute-start | bytes 98312 | tf_op jit(solution)/shard_map/ppermute | solution.py:24
  23.9 21.1 %copy-start.5 = (f32[6,1,4,4,128]{4,2,3,1,0:T(4,128)}, f32[6,1,4,4,128]{4,2,3,1,0:T(4,128)S(1)}, u32[]{:S(2)}) copy-start(f32[6,1,4,4,128]{4,2,3,1,0:T(4,128)S(1)} %pad.46) | copy-start | bytes 147460
  24.0 21.1 %copy-start.7 = (f32[6,1,4,4,128]{4,2,3,1,0:T(4,128)}, f32[6,1,4,4,128]{4,2,3,1,0:T(4,128)S(1)}, u32[]{:S(2)}) copy-start(f32[6,1,4,4,128]{4,2,3,1,0:T(4,128)S(1)} %pad.45) | copy-start | bytes 147460
  24.1 4.4 %copy-start.11 = (f32[1,4,4,4,128]{4,2,3,1,0:T(4,128)}, f32[1,4,4,4,128]{4,2,3,1,0:T(4,128)S(1)}, u32[]{:S(2)}) copy-start(f32[1,4,4,4,128]{4,2,3,1,0:T(4,128)S(1)} %collective-permute-done.8) | copy-start | bytes 98308
  27.3 1.1 %copy-start.13 = (f32[1,4,4,4,128]{4,2,3,1,0:T(4,128)}, f32[1,4,4,4,128]{4,2,3,1,0:T(4,128)S(1)}, u32[]{:S(2)}) copy-start(f32[1,4,4,4,128]{4,2,3,1,0:T(4,128)S(1)} %collective-permute-done.7) | copy-start | bytes 98308
  28.2 4.6 %collective-permute-start.10 = (f32[40,4,128]{2,0,1:T(8,128)S(1)}, f32[40,4,128]{2,0,1:T(8,128)S(1)}, u32[]{:S(2)}, u32[]{:S(2)}) collective-permute-start(f32[40,4,128]{2,0,1:T(8,128)S(1)} %copy_dynamic-update-slice_fusion), channel_id=1, source_target_pairs={{0,24},{8,0},{16,8},{24,16},{1,25},{9,1},{17,9},{25,17},{2,26},{10... | collective-permute-start | bytes 245768 | tf_op jit(solution)/shard_map/ppermute | solution.py:24
  28.4 10.7 %collective-permute-start.12 = (f32[40,4,128]{2,0,1:T(8,128)S(1)}, f32[40,4,128]{2,0,1:T(8,128)S(1)}, u32[]{:S(2)}, u32[]{:S(2)}) collective-permute-start(f32[40,4,128]{2,0,1:T(8,128)S(1)} %copy_dynamic-update-slice_fusion), channel_id=1, source_target_pairs={{0,8},{8,16},{16,24},{24,0},{1,9},{9,17},{17,25},{25,1},{2,10},{10... | collective-permute-start | bytes 245768 | tf_op jit(solution)/shard_map/ppermute | solution.py:24
  30.5 8.1 %collective-permute-start.11 = (f32[40,4,128]{2,0,1:T(8,128)S(1)}, f32[40,4,128]{2,0,1:T(8,128)S(1)}, u32[]{:S(2)}, u32[]{:S(2)}) collective-permute-start(f32[40,4,128]{2,0,1:T(8,128)S(1)} %copy_dynamic-update-slice_fusion), channel_id=1, source_target_pairs={{0,16},{8,24},{16,0},{24,8},{1,17},{9,25},{17,1},{25,9},{2,18},{10... | collective-permute-start | bytes 245768 | tf_op jit(solution)/shard_map/ppermute | solution.py:24
  40.4 8.4 %collective-permute-start.13 = (f32[32,4,128]{2,0,1:T(8,128)}, f32[32,4,128]{2,0,1:T(8,128)}, u32[]{:S(2)}, u32[]{:S(2)}) collective-permute-start(f32[32,4,128]{2,0,1:T(8,128)} %pad_maximum_fusion.53), channel_id=1, source_target_pairs={{1,0},{2,1},{3,2},{0,3},{5,4},{6,5},{7,6},{4,7},{9,8},{10,9},{11,1... | collective-permute-start | bytes 196616 | tf_op jit(solution)/shard_map/ppermute | solution.py:221
  40.4 11.3 %collective-permute-start.14 = (f32[32,4,128]{2,0,1:T(8,128)}, f32[32,4,128]{2,0,1:T(8,128)}, u32[]{:S(2)}, u32[]{:S(2)}) collective-permute-start(f32[32,4,128]{2,0,1:T(8,128)} %pad_maximum_fusion.53), channel_id=1, source_target_pairs={{2,0},{3,1},{0,2},{1,3},{6,4},{7,5},{4,6},{5,7},{10,8},{11,9},{8,1... | collective-permute-start | bytes 196616 | tf_op jit(solution)/shard_map/ppermute | solution.py:221
  42.1 11.1 %collective-permute-start.15 = (f32[32,4,128]{2,0,1:T(8,128)}, f32[32,4,128]{2,0,1:T(8,128)}, u32[]{:S(2)}, u32[]{:S(2)}) collective-permute-start(f32[32,4,128]{2,0,1:T(8,128)} %pad_maximum_fusion.53), channel_id=1, source_target_pairs={{3,0},{0,1},{1,2},{2,3},{7,4},{4,5},{5,6},{6,7},{11,8},{8,9},{9,10... | collective-permute-start | bytes 196616 | tf_op jit(solution)/shard_map/ppermute | solution.py:221
  42.1 12.6 %collective-permute-start.16 = (f32[32,4,128]{2,0,1:T(8,128)}, f32[32,4,128]{2,0,1:T(8,128)}, u32[]{:S(2)}, u32[]{:S(2)}) collective-permute-start(f32[32,4,128]{2,0,1:T(8,128)} %pad_maximum_fusion.53), channel_id=1, source_target_pairs={{4,0},{5,1},{6,2},{7,3},{0,4},{1,5},{2,6},{3,7},{12,8},{13,9},{14,... | collective-permute-start | bytes 196616 | tf_op jit(solution)/shard_map/ppermute | solution.py:221
  43.6 12.5 %collective-permute-start.17 = (f32[32,4,128]{2,0,1:T(8,128)}, f32[32,4,128]{2,0,1:T(8,128)}, u32[]{:S(2)}, u32[]{:S(2)}) collective-permute-start(f32[32,4,128]{2,0,1:T(8,128)} %pad_maximum_fusion.53), channel_id=1, source_target_pairs={{5,0},{6,1},{7,2},{4,3},{1,4},{2,5},{3,6},{0,7},{13,8},{14,9},{15,... | collective-permute-start | bytes 196616 | tf_op jit(solution)/shard_map/ppermute | solution.py:221
  48.8 10.1 %copy-start.10 = (f32[216,256,1]{1,0,2:T(8,128)S(1)}, f32[216,256,1]{1,0,2:T(8,128)}, u32[]{:S(2)}) copy-start(f32[216,256,1]{1,0,2:T(8,128)} %constant.137) | copy-start | bytes 663556
  48.8 8.8 %collective-permute-start.18 = (f32[32,4,128]{2,0,1:T(8,128)}, f32[32,4,128]{2,0,1:T(8,128)S(1)}, u32[]{:S(2)}, u32[]{:S(2)}) collective-permute-start(f32[32,4,128]{2,0,1:T(8,128)} %pad_maximum_fusion.53), channel_id=1, source_target_pairs={{6,0},{7,1},{4,2},{5,3},{2,4},{3,5},{0,6},{1,7},{14,8},{15,9},{12,... | collective-permute-start | bytes 196616 | tf_op jit(solution)/shard_map/ppermute | solution.py:221
  51.7 6.6 %collective-permute-start.19 = (f32[32,4,128]{2,0,1:T(8,128)}, f32[32,4,128]{2,0,1:T(8,128)S(1)}, u32[]{:S(2)}, u32[]{:S(2)}) collective-permute-start(f32[32,4,128]{2,0,1:T(8,128)} %pad_maximum_fusion.53), channel_id=1, source_target_pairs={{7,0},{4,1},{5,2},{6,3},{3,4},{0,5},{1,6},{2,7},{15,8},{12,9},{13,... | collective-permute-start | bytes 196616 | tf_op jit(solution)/shard_map/ppermute | solution.py:221
  58.9 1.8 %copy-start.6 = (f32[6,1,4,4,128]{4,2,3,1,0:T(4,128)S(1)}, f32[6,1,4,4,128]{4,2,3,1,0:T(4,128)}, u32[]{:S(2)}) copy-start(f32[6,1,4,4,128]{4,2,3,1,0:T(4,128)} %copy-done.5) | copy-start | bytes 147460
  58.9 1.8 %copy-start.8 = (f32[6,1,4,4,128]{4,2,3,1,0:T(4,128)S(1)}, f32[6,1,4,4,128]{4,2,3,1,0:T(4,128)}, u32[]{:S(2)}) copy-start(f32[6,1,4,4,128]{4,2,3,1,0:T(4,128)} %copy-done.7) | copy-start | bytes 147460
  58.9 1.8 %copy-start.12 = (f32[1,4,4,4,128]{4,2,3,1,0:T(4,128)S(1)}, f32[1,4,4,4,128]{4,2,3,1,0:T(4,128)}, u32[]{:S(2)}) copy-start(f32[1,4,4,4,128]{4,2,3,1,0:T(4,128)} %copy-done.11) | copy-start | bytes 98308
  58.9 1.8 %copy-start.14 = (f32[1,4,4,4,128]{4,2,3,1,0:T(4,128)S(1)}, f32[1,4,4,4,128]{4,2,3,1,0:T(4,128)}, u32[]{:S(2)}) copy-start(f32[1,4,4,4,128]{4,2,3,1,0:T(4,128)} %copy-done.13) | copy-start | bytes 98308
  61.2 6.3 %collective-permute-start.24 = (f32[4,4,1,4,128]{4,2,3,1,0:T(1,128)S(1)}, f32[4,4,1,4,128]{4,2,3,1,0:T(1,128)S(1)}, u32[]{:S(2)}, u32[]{:S(2)}) collective-permute-start(f32[4,4,1,4,128]{4,2,3,1,0:T(1,128)S(1)} %get-tuple-element.18), channel_id=1, source_target_pairs={{0,1},{1,2},{2,3},{3,0},{4,5},{5,6},{6,7},{7,4},{8,9},{9,10},{10,1... | collective-permute-start | bytes 98312 | tf_op jit(solution)/shard_map/ppermute | solution.py:24
  63.0 9.5 %collective-permute-start.22 = (f32[4,2,4,4,128]{4,2,3,1,0:T(4,128)S(1)}, f32[4,2,4,4,128]{4,2,3,1,0:T(4,128)S(1)}, u32[]{:S(2)}, u32[]{:S(2)}) collective-permute-start(f32[4,2,4,4,128]{4,2,3,1,0:T(4,128)S(1)} %pad_maximum_fusion.54), channel_id=1, source_target_pairs={{0,4},{4,0},{1,5},{5,1},{2,6},{6,2},{3,7},{7,3},{8,12},{12,8},{9,1... | collective-permute-start | bytes 196616 | tf_op jit(solution)/shard_map/ppermute | solution.py:37
  64.6 3.9 %collective-permute-start.20 = (f32[1,4,4,4,128]{4,2,3,1,0:T(4,128)S(1)}, f32[1,4,4,4,128]{4,2,3,1,0:T(4,128)S(1)}, u32[]{:S(2)}, u32[]{:S(2)}) collective-permute-start(f32[1,4,4,4,128]{4,2,3,1,0:T(4,128)S(1)} %get-tuple-element.20), channel_id=1, source_target_pairs={{0,24},{8,0},{16,8},{24,16},{1,25},{9,1},{17,9},{25,17},{2,26},{10... | collective-permute-start | bytes 98312 | tf_op jit(solution)/shard_map/ppermute | solution.py:24
  66.5 5.7 %collective-permute-start.21 = (f32[1,4,4,4,128]{4,2,3,1,0:T(4,128)S(1)}, f32[1,4,4,4,128]{4,2,3,1,0:T(4,128)S(1)}, u32[]{:S(2)}, u32[]{:S(2)}) collective-permute-start(f32[1,4,4,4,128]{4,2,3,1,0:T(4,128)S(1)} %get-tuple-element.19), channel_id=1, source_target_pairs={{0,8},{8,16},{16,24},{24,0},{1,9},{9,17},{17,25},{25,1},{2,10},{10... | collective-permute-start | bytes 98312 | tf_op jit(solution)/shard_map/ppermute | solution.py:24
  66.6 5.7 %collective-permute-start.23 = (f32[4,4,1,4,128]{4,2,3,1,0:T(1,128)S(1)}, f32[4,4,1,4,128]{4,2,3,1,0:T(1,128)S(1)}, u32[]{:S(2)}, u32[]{:S(2)}) collective-permute-start(f32[4,4,1,4,128]{4,2,3,1,0:T(1,128)S(1)} %get-tuple-element.17), channel_id=1, source_target_pairs={{0,3},{1,0},{2,1},{3,2},{4,7},{5,4},{6,5},{7,6},{8,11},{9,8},{10,9... | collective-permute-start | bytes 98312 | tf_op jit(solution)/shard_map/ppermute | solution.py:24
  67.5 1.1 %copy-start.4 = (f32[1,8,8,4,128]{4,2,3,1,0:T(8,128)S(1)}, f32[1,8,8,4,128]{4,2,3,1,0:T(8,128)}, u32[]{:S(2)}) copy-start(f32[1,8,8,4,128]{4,2,3,1,0:T(8,128)} %copy-done.3) | copy-start | bytes 393220
  67.5 4.8 %copy-start.2 = (f32[1,8,8,4,128]{4,2,3,1,0:T(8,128)S(1)}, f32[1,8,8,4,128]{4,2,3,1,0:T(8,128)}, u32[]{:S(2)}) copy-start(f32[1,8,8,4,128]{4,2,3,1,0:T(8,128)} %copy-done.1) | copy-start | bytes 393220

commit v17 on v14

--- a/solution.py
+++ b/solution.py
@@ -182,18 +182,18 @@
 
 
 def coarse_solve(rhs_two, tiles):
-    extended = rhs_two
+    orbs = rhs_two.shape[3:]
+    extended = rhs_two.reshape(rhs_two.shape[:3] + (-1,))
     starts = []
     extended, start, tiles_by_step = extend_axis(extended, "gx", 0, COARSE_HALO, tiles)
     starts.append(start)
     extended, joint_starts = extend_joint(extended, ("gy", "gz"), (1, 2), COARSE_HALO)
     starts.extend(joint_starts)
     grid = extended.shape[:3]
-    orbs = extended.shape[3:]
     operator = coarse_matrix(grid, tuple(starts), rhs_two.shape[:3])
     operator = jnp.asarray(operator.reshape((-1,) + tuple(grid)))
     post = jnp.einsum(
-        "qxyz,xyzgl->qgl", operator, extended, precision=lax.Precision.HIGHEST, preferred_element_type=jnp.float32
+        "qxyz,xyzw->qw", operator, extended, precision=lax.Precision.HIGHEST, preferred_element_type=jnp.float32
     )
     return post.reshape(tuple(2 * size + 2 for size in rhs_two.shape[:3]) + orbs), tiles_by_step
 

time: 66.6 us -> 69.2 us (1.039)
  local copies, waits for them, and re-layouts: 6.36 us -> 8.39 us
  other arithmetic: 11.1 us -> 10.1 us
  waiting for transfers between devices: 17.7 us -> 18.5 us
    unnamed x49 -> x45, local copies, waits for them, and re-layouts: 0.19 us -> 1.65 us
    reshape x0 -> x4, local copies, waits for them, and re-layouts: none -> 1.32 us  [the longest x1 1.16 us: coarse_solve(): post.reshape(tuple((2 * size + 2 for size in rhs_two.shape[:3])) + orbs)]
    ppermute x15, waiting for transfers between devices: 16.7 us -> 17.6 us  [shifted(): lax.ppermute(block, axis, [(j, (j - step) % count) for j in range(count)])]
    add x2, other arithmetic: 1.06 us -> 0.16 us  [post_smooth(): hi = corr_faces[dim][1] + prolong_face(coarse_face_list[dim][1], dim)]
    sub x1, other arithmetic: 1.86 us -> 0.97 us  [vcycle(): rhs_one = restrict(rhs_zero - stencil(corr_zero, faces_zero, 0))]
    add x1, other arithmetic: 0.25 us -> 1.06 us  [vcycle(): updated_padded = padded_one + coarse_padded]
  transfers between devices with their start and end apart: 25 -> 25, of which waited for: 9 -> 9; matrix products, arithmetic and copies ran while one was open for 15% -> 13% of each run, Pallas kernels for 0% -> 0%
where the time goes in v17:
time: 69.2 us; the launch traced here: 68.8 us
  starting transfers between devices  26.6 us (38%)
  waiting for transfers between devices  18.5 us (27%)
  other arithmetic  10.1 us (15%)
  local copies, waits for them, and re-layouts  8.39 us (12%)
  matrix products  4.38 us (6%)
  between operations  0.85 us (1%)
    ppermute x15, waiting for transfers between devices, shifted(): lax.ppermute(block, axis, [(j, (j - step) % count) for j in range(count)])  17.6 us
    ppermute x15, starting transfers between devices, shifted(): lax.ppermute(block, axis, [(j, (j - step) % count) for j in range(count)])  14.9 us
    ppermute x7, starting transfers between devices, fetch(): cache[steps] = lax.ppermute(block, tuple(axes), pairs)  7.06 us
    ppermute x3, starting transfers between devices, axis_faces(): lax.ppermute(jnp.concatenate([first, last], axis=dim), axis, [(0, 1), (1,...  4.68 us
    dot_general x1, matrix products, coarse_solve(): jnp.einsum('qxyz,xyzw->qw', operator, extended, precision=lax.Precision.H...  2.57 us
    div x3, other arithmetic, vcycle(): omega * part.astype(jnp.float32) / center  2.45 us
    dot_general x1, matrix products, body(): jnp.dot(rows, gram, precision=lax.Precision.HIGH, preferred_element_type=...  1.81 us
    reshape x1, local copies, waits for them, and re-layouts, gram_matrix(): return spread.sum(axis=0).reshape(orb_count, orb_count)  1.68 us
  transfers between devices with their start and end apart: 25, of which 9 were waited for; matrix products, arithmetic and copies ran while one was open for 13% of the time, Pallas kernels for 0%

profile of v17, /device:TPU:0, one launch (start us, length us, event | category | flops | bytes accessed | tf_op | source)
XLA Modules:
  0.0 68.8 jit_solution(8105539945618952320)
XLA Ops:
  0.0 1.5 %fusion.57 = (f32[8,8,1,4,128]{4,2,3,1,0:T(1,128)S(1)}, f32[8,8,1,4,128]{4,2,3,1,0:T(1,128)S(1)}) fusion(bf16[8,8,8,4,128]{4,2,3,1,0:T(8,128)(2,1)} %bitcast.65), kind=kLoop, calls=%fused_computation.133 | loop fusion | flops 131072 | bytes 393216 | tf_op jit(solution)/shard_map/div | solution.py:311
  1.5 0.6 collective-permute-start.4
  2.1 0.9 %convert_multiply_fusion.3 = (f32[8,1,8,4,128]{4,2,3,1,0:T(8,128)S(1)}, f32[8,1,8,4,128]{4,2,3,1,0:T(8,128)S(1)}) fusion(bf16[8,8,8,4,128]{4,2,3,1,0:T(8,128)(2,1)} %bitcast.66), kind=kLoop, calls=%fused_computation.135 | loop fusion | flops 131072 | bytes 393216 | tf_op jit(solution)/shard_map/div | solution.py:311
  3.0 2.6 %collective-permute-start.2 = (f32[8,2,8,4,128]{4,2,3,1,0:T(8,128)S(1)}, f32[8,2,8,4,128]{4,2,3,1,0:T(8,128)S(1)}, u32[]{:S(2)}, u32[]{:S(2)}) collective-permute-start(f32[8,2,8,4,128]{4,2,3,1,0:T(8,128)S(1)} %pad_maximum_fusion.32), channel_id=1, source_target_pairs={{0,4},{4,0},{1,5},{5,1},{2,6},{6,2},{3,7},{7,3},{8,12},{12,8},{9,1... | collective-permute-start | bytes 786440 | tf_op jit(solution)/shard_map/ppermute | solution.py:37
  5.6 3.7 %collective-permute-start = (f32[1,8,8,4,128]{4,2,3,1,0:T(8,128)S(1)}, f32[1,8,8,4,128]{4,2,3,1,0:T(8,128)S(1)}, u32[]{:S(2)}, u32[]{:S(2)}) collective-permute-start(f32[1,8,8,4,128]{4,2,3,1,0:T(8,128)S(1)} %get-tuple-element.10), channel_id=1, source_target_pairs={{0,24},{8,0},{16,8},{24,16},{1,25},{9,1},{17,9},{25,17},{2,26},{10... | collective-permute-start | bytes 393224 | tf_op jit(solution)/shard_map/ppermute | solution.py:24
  9.3 1.2 %collective-permute-start.3 = (f32[8,8,1,4,128]{4,2,3,1,0:T(1,128)S(1)}, f32[8,8,1,4,128]{4,2,3,1,0:T(1,128)S(1)}, u32[]{:S(2)}, u32[]{:S(2)}) collective-permute-start(f32[8,8,1,4,128]{4,2,3,1,0:T(1,128)S(1)} %get-tuple-element.7), channel_id=1, source_target_pairs={{0,3},{1,0},{2,1},{3,2},{4,7},{5,4},{6,5},{7,6},{8,11},{9,8},{10,9... | collective-permute-start | bytes 393224 | tf_op jit(solution)/shard_map/ppermute | solution.py:24
  10.8 0.6 gather_fusion
  12.0 0.7 fusion.58
  12.9 4.5 %collective-permute-done.1 = f32[1,8,8,4,128]{4,2,3,1,0:T(8,128)S(1)} collective-permute-done((f32[1,8,8,4,128]{4,2,3,1,0:T(8,128)S(1)}, f32[1,8,8,4,128]{4,2,3,1,0:T(8,128)S(1)}, u32[]{:S(2)}, u32[]{:S(2)}) %collective-permute-start.1) | collective-permute-done | bytes 131104 | tf_op jit(solution)/shard_map/ppermute | solution.py:24
  17.4 1.0 %convert_subtract_fusion.1 = f32[8,8,8,4,128]{4,2,3,1,0:T(8,128)S(1)} fusion(f32[8,8,1,4,128]{4,2,3,1,0:T(1,128)S(1)} %collective-permute-done.4, f32[10,1,8,4,128]{4,2,3,1,0:T(8,128)S(1)} %pad.40, f32[10,1,8,4,128]{4,2,3,1,0:T(8,128)S(1)} %pad.41, f32[1,8,8,4,128]{4,2,3,1,0:T(8,128)S(1)} %collective-permute-done, ...), kind=kLoop, calls=%fused_computation.3 | loop fusion | flops 8912896 | bytes 3473408 | tf_op jit(solution)/shard_map/sub | solution.py:314
  18.4 0.7 %reduce_sum.27 = f32[4,4,4,4,128]{4,2,3,1,0:T(4,128)S(1)} reduce(f32[4,2,4,2,4,2,4,128]{7,5,4,6,3,2,1,0:T(2,128)S(1)} %bitcast.69, f32[]{:T(128)} %constant.93.clone.1), dimensions={1,3,5}, to_apply=%region_0.1 | reduce | flops 229376 | bytes 1179652 | tf_op jit(solution)/shard_map/reduce_sum | solution.py:177
  19.4 0.6 collective-permute-start.6
  20.0 0.2 collective-permute-start.5
  20.2 1.5 %collective-permute-start.8 = (f32[1,4,4,4,128]{4,2,3,1,0:T(4,128)S(1)}, f32[1,4,4,4,128]{4,2,3,1,0:T(4,128)S(1)}, u32[]{:S(2)}, u32[]{:S(2)}) collective-permute-start(f32[1,4,4,4,128]{4,2,3,1,0:T(4,128)S(1)} %get-tuple-element.26), channel_id=1, source_target_pairs={{0,24},{8,0},{16,8},{24,16},{1,25},{9,1},{17,9},{25,17},{2,26},{10... | collective-permute-start | bytes 98312 | tf_op jit(solution)/shard_map/ppermute | solution.py:24
  21.7 0.5 collective-permute-start.7
  22.3 1.1 %collective-permute-done.5 = f32[4,4,1,4,128]{4,2,3,1,0:T(1,128)S(1)} collective-permute-done((f32[4,4,1,4,128]{4,2,3,1,0:T(1,128)S(1)}, f32[4,4,1,4,128]{4,2,3,1,0:T(1,128)S(1)}, u32[]{:S(2)}, u32[]{:S(2)}) %collective-permute-start.5) | collective-permute-done | bytes 32800 | tf_op jit(solution)/shard_map/ppermute | solution.py:24
  23.4 0.6 collective-permute-done.6
  24.1 3.3 %collective-permute-done.7 = f32[1,4,4,4,128]{4,2,3,1,0:T(4,128)S(1)} collective-permute-done((f32[1,4,4,4,128]{4,2,3,1,0:T(4,128)S(1)}, f32[1,4,4,4,128]{4,2,3,1,0:T(4,128)S(1)}, u32[]{:S(2)}, u32[]{:S(2)}) %collective-permute-start.7) | collective-permute-done | bytes 32800 | tf_op jit(solution)/shard_map/ppermute | solution.py:24
  27.4 0.2 fusion.51
  27.6 0.4 copy-done.13
  28.2 0.6 collective-permute-start.11
  28.9 3.2 %collective-permute-start.10 = (f32[10,2,2,512]{3,2,1,0:T(2,128)S(1)}, f32[10,2,2,512]{3,2,1,0:T(2,128)S(1)}, u32[]{:S(2)}, u32[]{:S(2)}) collective-permute-start(f32[10,2,2,512]{3,2,1,0:T(2,128)S(1)} %pad_maximum_fusion.52), channel_id=1, source_target_pairs={{0,24},{8,0},{16,8},{24,16},{1,25},{9,1},{17,9},{25,17},{2,26},{10... | collective-permute-start | bytes 245768 | tf_op jit(solution)/shard_map/ppermute | solution.py:24
  32.1 3.3 %collective-permute-done.12 = f32[10,2,2,512]{3,2,1,0:T(2,128)S(1)} collective-permute-done((f32[10,2,2,512]{3,2,1,0:T(2,128)S(1)}, f32[10,2,2,512]{3,2,1,0:T(2,128)S(1)}, u32[]{:S(2)}, u32[]{:S(2)}) %collective-permute-start.12) | collective-permute-done | bytes 81952 | tf_op jit(solution)/shard_map/ppermute | solution.py:24
  35.5 2.6 %collective-permute-done.11 = f32[10,2,2,512]{3,2,1,0:T(2,128)S(1)} collective-permute-done((f32[10,2,2,512]{3,2,1,0:T(2,128)S(1)}, f32[10,2,2,512]{3,2,1,0:T(2,128)S(1)}, u32[]{:S(2)}, u32[]{:S(2)}) %collective-permute-start.11) | collective-permute-done | bytes 81952 | tf_op jit(solution)/shard_map/ppermute | solution.py:24
  38.1 0.7 pad_maximum_fusion.54
  38.7 1.3 %collective-permute-start.18 = (f32[8,2,2,512]{3,2,1,0:T(2,128)}, f32[8,2,2,512]{3,2,1,0:T(2,128)S(1)}, u32[]{:S(2)}, u32[]{:S(2)}) collective-permute-start(f32[8,2,2,512]{3,2,1,0:T(2,128)} %pad_maximum_fusion.54), channel_id=1, source_target_pairs={{6,0},{7,1},{4,2},{5,3},{2,4},{3,5},{0,6},{1,7},{14,8},{15,9},{12,... | collective-permute-start | bytes 196616 | tf_op jit(solution)/shard_map/ppermute | solution.py:108
  40.0 2.4 %collective-permute-start.17 = (f32[8,2,2,512]{3,2,1,0:T(2,128)}, f32[8,2,2,512]{3,2,1,0:T(2,128)}, u32[]{:S(2)}, u32[]{:S(2)}) collective-permute-start(f32[8,2,2,512]{3,2,1,0:T(2,128)} %pad_maximum_fusion.54), channel_id=1, source_target_pairs={{5,0},{6,1},{7,2},{4,3},{1,4},{2,5},{3,6},{0,7},{13,8},{14,9},{15,... | collective-permute-start | bytes 196616 | tf_op jit(solution)/shard_map/ppermute | solution.py:108
  42.4 0.7 collective-permute-start.16
  43.3 0.3 collective-permute-done.19
  43.6 1.3 %collective-permute-start.14 = (f32[8,2,2,512]{3,2,1,0:T(2,128)}, f32[8,2,2,512]{3,2,1,0:T(2,128)S(1)}, u32[]{:S(2)}, u32[]{:S(2)}) collective-permute-start(f32[8,2,2,512]{3,2,1,0:T(2,128)} %pad_maximum_fusion.54), channel_id=1, source_target_pairs={{2,0},{3,1},{0,2},{1,3},{6,4},{7,5},{4,6},{5,7},{10,8},{11,9},{8,1... | collective-permute-start | bytes 196616 | tf_op jit(solution)/shard_map/ppermute | solution.py:108
  44.9 1.5 %collective-permute-start.13 = (f32[8,2,2,512]{3,2,1,0:T(2,128)}, f32[8,2,2,512]{3,2,1,0:T(2,128)S(1)}, u32[]{:S(2)}, u32[]{:S(2)}) collective-permute-start(f32[8,2,2,512]{3,2,1,0:T(2,128)} %pad_maximum_fusion.54), channel_id=1, source_target_pairs={{1,0},{2,1},{3,2},{0,3},{5,4},{6,5},{7,6},{4,7},{9,8},{10,9},{11,1... | collective-permute-start | bytes 196616 | tf_op jit(solution)/shard_map/ppermute | solution.py:108
  46.4 0.4 multiply_reduce_fusion
  46.8 1.7 %copy.26 = f32[4,128,4,128]{3,2,1,0:T(4,128)} copy(f32[4,128,4,128]{3,1,2,0:T(8,128)S(1)} %multiply_reduce_fusion) | data formatting | bytes 2097152 | tf_op jit(solution)/shard_map/reduce_sum | solution.py:306
  48.5 1.7 %reshape.606 = f32[512,512,1,1]{1,0,2,3:T(8,128)S(1)} reshape(f32[4,128,4,128]{3,2,1,0:T(4,128)} %copy.26) | data formatting | bytes 2097152 | tf_op jit(solution)/shard_map/reshape | solution.py:306
  50.2 2.6 %convolution_bitcast_fusion = f32[216,512]{1,0:T(8,128)} fusion(f32[216,8,4,8]{0,3,2,1:T(8,128)} %constant.111.clone, f32[8,2,2,512]{3,2,1,0:T(2,128)S(1)} %copy-done.19, f32[8,2,2,512]{3,2,1,0:T(2,128)S(1)} %copy-done.21, f32[8,2,2,512]{3,2,1,0:T(2,128)} %collective-permute-done.17, f32[8,2,2,512]{3,2,1,0:T(2,128)} %collective-permute-done.16, ...), kind=kOutput, calls=%fused_computation.7 | convolution fusion | flops 341049344 | bytes 1187840 | tf_op jit(solution)/shard_map/qxyz,xyzw->qw/dot_general | solution.py:195
  52.8 1.2 %reshape.588 = f32[6,6,6,4,128]{4,3,2,1,0:T(4,128)S(1)} reshape(f32[216,512]{1,0:T(8,128)} %convolution_bitcast_fusion) | data formatting | bytes 884736 | tf_op jit(solution)/shard_map/reshape | solution.py:198
  54.0 1.1 %maximum_add_fusion = f32[6,6,6,4,128]{4,2,3,1,0:T(8,128)S(1)} fusion(f32[6,6,1,4,128]{4,2,3,1,0:T(1,128)S(1)} %pad.47, f32[6,1,4,4,128]{4,2,3,1,0:T(4,128)S(1)} %pad.46, f32[1,4,4,4,128]{4,2,3,1,0:T(4,128)S(1)} %collective-permute-done.8, f32[4,4,4,4,128]{4,2,3,1,0:T(4,128)S(1)} %broadcast_multiply_fusion.2, f32[1,4,4,4,128]{4,2,3,1,0:T(4,128)} %copy-done.13, ...), kind=kLoop, calls=%fused_computation.68 | loop fusion | flops 774144 | bytes 1327104 | tf_op jit(solution)/shard_map/add | solution.py:321
  55.4 1.5 %collective-permute-start.22 = (f32[4,2,4,4,128]{4,2,3,1,0:T(4,128)S(1)}, f32[4,2,4,4,128]{4,2,3,1,0:T(4,128)S(1)}, u32[]{:S(2)}, u32[]{:S(2)}) collective-permute-start(f32[4,2,4,4,128]{4,2,3,1,0:T(4,128)S(1)} %pad_maximum_fusion.55), channel_id=1, source_target_pairs={{0,4},{4,0},{1,5},{5,1},{2,6},{6,2},{3,7},{7,3},{8,12},{12,8},{9,1... | collective-permute-start | bytes 196616 | tf_op jit(solution)/shard_map/ppermute | solution.py:37
  56.9 2.1 %collective-permute-start.20 = (f32[1,4,4,4,128]{4,2,3,1,0:T(4,128)S(1)}, f32[1,4,4,4,128]{4,2,3,1,0:T(4,128)S(1)}, u32[]{:S(2)}, u32[]{:S(2)}) collective-permute-start(f32[1,4,4,4,128]{4,2,3,1,0:T(4,128)S(1)} %get-tuple-element.20), channel_id=1, source_target_pairs={{0,24},{8,0},{16,8},{24,16},{1,25},{9,1},{17,9},{25,17},{2,26},{10... | collective-permute-start | bytes 98312 | tf_op jit(solution)/shard_map/ppermute | solution.py:24
  59.0 1.2 %collective-permute-start.23 = (f32[4,4,1,4,128]{4,2,3,1,0:T(1,128)S(1)}, f32[4,4,1,4,128]{4,2,3,1,0:T(1,128)S(1)}, u32[]{:S(2)}, u32[]{:S(2)}) collective-permute-start(f32[4,4,1,4,128]{4,2,3,1,0:T(1,128)S(1)} %get-tuple-element.17), channel_id=1, source_target_pairs={{0,3},{1,0},{2,1},{3,2},{4,7},{5,4},{6,5},{7,6},{8,11},{9,8},{10,9... | collective-permute-start | bytes 98312 | tf_op jit(solution)/shard_map/ppermute | solution.py:24
  60.3 0.6 broadcast_in_dim.88
  60.9 0.2 fusion.42
  61.2 0.6 copy-done.6
  62.0 2.7 %collective-permute-done.21 = f32[1,4,4,4,128]{4,2,3,1,0:T(4,128)S(1)} collective-permute-done((f32[1,4,4,4,128]{4,2,3,1,0:T(4,128)S(1)}, f32[1,4,4,4,128]{4,2,3,1,0:T(4,128)S(1)}, u32[]{:S(2)}, u32[]{:S(2)}) %collective-permute-start.21) | collective-permute-done | bytes 32800 | tf_op jit(solution)/shard_map/ppermute | solution.py:24
  65.2 0.5 copy-done.2
  65.7 1.0 %fusion.2 = f32[8,8,8,4,128]{4,2,3,1,0:T(8,128)S(1)} fusion(f32[8,8,8,4,128]{4,2,3,1,0:T(8,128)S(1)} %fusion.42, f32[8,8,1,4,128]{4,2,3,1,0:T(1,128)S(1)} %add.215, f32[10,1,8,4,128]{4,2,3,1,0:T(8,128)S(1)} %pad.48, f32[10,1,8,4,128]{4,2,3,1,0:T(8,128)S(1)} %pad.49, f32[1,8,8,4,128]{4,2,3,1,0:T(8,128)S(1)} %add.206, f32[1,8,8,4,128]{4,2,3,1,0:T(8,128)S(1)} %add.207, ...), kind=kLoop, calls=%fused_computation.10 | loop fusion | flops 9437184 | bytes 3473408 | tf_op jit(solution)/shard_map/add | solution.py:270
  66.8 0.2 bitcast_multiply_fusion
  67.0 1.8 %convolution_convert_fusion = bf16[8,8,8,512]{3,2,1,0:T(8,128)(2,1)} fusion(f32[8,8,8,512]{3,2,1,0:T(8,128)S(1)} %bitcast.68, f32[512,512,1,1]{1,0,2,3:T(8,128)S(1)} %reshape.606), kind=kOutput, calls=%fused_computation.6 | convolution fusion | flops 805568512 | bytes 2621440 | tf_op jit(solution)/shard_map/dot_general | solution.py:342
  (137 shorter events, 3.2 us)
Async XLA Ops:
  0.0 5.6 %copy-start = (bf16[8,8,8,512]{3,2,1,0:T(8,128)(2,1)S(1)}, bf16[8,8,8,512]{3,2,1,0:T(8,128)(2,1)}, u32[]{:S(2)}) copy-start(bf16[8,8,8,512]{3,2,1,0:T(8,128)(2,1)} %param.5) | copy-start | bytes 1572868
  0.0 10.5 %copy-start.12 = (f32[1,128,128]{2,1,0:T(8,128)S(1)}, f32[1,128,128]{2,1,0:T(8,128)}, u32[]{:S(2)}) copy-start(f32[1,128,128]{2,1,0:T(8,128)} %param.8) | copy-start | bytes 196612
  0.0 10.5 %copy-start.14 = (s32[3,2,512]{2,1,0:T(2,128)S(1)}, s32[3,2,512]{2,1,0:T(2,128)}, u32[]{:S(2)}) copy-start(s32[3,2,512]{2,1,0:T(2,128)} %param.6) | copy-start | bytes 36868
  0.0 10.6 %copy-start.17 = (s32[4,2]{0,1:T(2,128)S(1)}, s32[4,2]{0,1:T(2,128)}, u32[]{:S(2)}) copy-start(s32[4,2]{0,1:T(2,128)} %param.7) | copy-start | bytes 100
  1.5 11.4 %collective-permute-start.4 = (f32[8,8,1,4,128]{4,2,3,1,0:T(1,128)S(1)}, f32[8,8,1,4,128]{4,2,3,1,0:T(1,128)S(1)}, u32[]{:S(2)}, u32[]{:S(2)}) collective-permute-start(f32[8,8,1,4,128]{4,2,3,1,0:T(1,128)S(1)} %get-tuple-element.8), channel_id=1, source_target_pairs={{0,1},{1,2},{2,3},{3,0},{4,5},{5,6},{6,7},{7,4},{8,9},{9,10},{10,1... | collective-permute-start | bytes 393224 | tf_op jit(solution)/shard_map/ppermute | solution.py:24
  3.0 9.8 %collective-permute-start.2 = (f32[8,2,8,4,128]{4,2,3,1,0:T(8,128)S(1)}, f32[8,2,8,4,128]{4,2,3,1,0:T(8,128)S(1)}, u32[]{:S(2)}, u32[]{:S(2)}) collective-permute-start(f32[8,2,8,4,128]{4,2,3,1,0:T(8,128)S(1)} %pad_maximum_fusion.32), channel_id=1, source_target_pairs={{0,4},{4,0},{1,5},{5,1},{2,6},{6,2},{3,7},{7,3},{8,12},{12,8},{9,1... | collective-permute-start | bytes 786440 | tf_op jit(solution)/shard_map/ppermute | solution.py:37
  5.6 7.3 %collective-permute-start = (f32[1,8,8,4,128]{4,2,3,1,0:T(8,128)S(1)}, f32[1,8,8,4,128]{4,2,3,1,0:T(8,128)S(1)}, u32[]{:S(2)}, u32[]{:S(2)}) collective-permute-start(f32[1,8,8,4,128]{4,2,3,1,0:T(8,128)S(1)} %get-tuple-element.10), channel_id=1, source_target_pairs={{0,24},{8,0},{16,8},{24,16},{1,25},{9,1},{17,9},{25,17},{2,26},{10... | collective-permute-start | bytes 393224 | tf_op jit(solution)/shard_map/ppermute | solution.py:24
  9.3 8.1 %collective-permute-start.1 = (f32[1,8,8,4,128]{4,2,3,1,0:T(8,128)S(1)}, f32[1,8,8,4,128]{4,2,3,1,0:T(8,128)S(1)}, u32[]{:S(2)}, u32[]{:S(2)}) collective-permute-start(f32[1,8,8,4,128]{4,2,3,1,0:T(8,128)S(1)} %get-tuple-element.9), channel_id=1, source_target_pairs={{0,8},{8,16},{16,24},{24,0},{1,9},{9,17},{17,25},{25,1},{2,10},{10... | collective-permute-start | bytes 393224 | tf_op jit(solution)/shard_map/ppermute | solution.py:24
  9.3 8.1 %collective-permute-start.3 = (f32[8,8,1,4,128]{4,2,3,1,0:T(1,128)S(1)}, f32[8,8,1,4,128]{4,2,3,1,0:T(1,128)S(1)}, u32[]{:S(2)}, u32[]{:S(2)}) collective-permute-start(f32[8,8,1,4,128]{4,2,3,1,0:T(1,128)S(1)} %get-tuple-element.7), channel_id=1, source_target_pairs={{0,3},{1,0},{2,1},{3,2},{4,7},{5,4},{6,5},{7,6},{8,11},{9,8},{10,9... | collective-permute-start | bytes 393224 | tf_op jit(solution)/shard_map/ppermute | solution.py:24
  12.8 4.6 %copy-start.1 = (f32[8,2,8,4,128]{4,2,3,1,0:T(8,128)}, f32[8,2,8,4,128]{4,2,3,1,0:T(8,128)S(1)}, u32[]{:S(2)}) copy-start(f32[8,2,8,4,128]{4,2,3,1,0:T(8,128)S(1)} %collective-permute-done.2) | copy-start | bytes 786436
  12.9 5.5 %copy-start.5 = (f32[8,8,1,4,128]{4,2,3,1,0:T(1,128)}, f32[8,8,1,4,128]{4,2,3,1,0:T(1,128)S(1)}, u32[]{:S(2)}) copy-start(f32[8,8,1,4,128]{4,2,3,1,0:T(1,128)S(1)} %collective-permute-done.4) | copy-start | bytes 393220
  12.9 5.5 %copy-start.9 = (f32[1,8,8,4,128]{4,2,3,1,0:T(8,128)}, f32[1,8,8,4,128]{4,2,3,1,0:T(8,128)S(1)}, u32[]{:S(2)}) copy-start(f32[1,8,8,4,128]{4,2,3,1,0:T(8,128)S(1)} %collective-permute-done) | copy-start | bytes 393220
  17.4 1.0 %copy-start.7 = (f32[1,8,8,4,128]{4,2,3,1,0:T(8,128)}, f32[1,8,8,4,128]{4,2,3,1,0:T(8,128)S(1)}, u32[]{:S(2)}) copy-start(f32[1,8,8,4,128]{4,2,3,1,0:T(8,128)S(1)} %collective-permute-done.1) | copy-start | bytes 393220
  17.4 1.0 %copy-start.3 = (f32[8,8,1,4,128]{4,2,3,1,0:T(1,128)}, f32[8,8,1,4,128]{4,2,3,1,0:T(1,128)S(1)}, u32[]{:S(2)}) copy-start(f32[8,8,1,4,128]{4,2,3,1,0:T(1,128)S(1)} %collective-permute-done.3) | copy-start | bytes 393220
  19.2 12.8 %copy-start.15 = (f32[4,4]{1,0:T(4,128)S(1)}, f32[4,4]{1,0:T(4,128)}, u32[]{:S(2)}) copy-start(f32[4,4]{1,0:T(4,128)} %get-tuple-element.41) | copy-start | bytes 196
  19.2 12.8 %copy-start.16 = (f32[4,4]{1,0:T(4,128)S(1)}, f32[4,4]{1,0:T(4,128)}, u32[]{:S(2)}) copy-start(f32[4,4]{1,0:T(4,128)} %get-tuple-element.42) | copy-start | bytes 196
  19.3 2.9 %collective-permute-start.9 = (f32[4,4,1,4,128]{4,2,3,1,0:T(1,128)S(1)}, f32[4,4,1,4,128]{4,2,3,1,0:T(1,128)S(1)}, u32[]{:S(2)}, u32[]{:S(2)}) collective-permute-start(f32[4,4,1,4,128]{4,2,3,1,0:T(1,128)S(1)} %get-tuple-element.24), channel_id=1, source_target_pairs={{0,3},{1,0},{2,1},{3,2},{4,7},{5,4},{6,5},{7,6},{8,11},{9,8},{10,9... | collective-permute-start | bytes 98312 | tf_op jit(solution)/shard_map/ppermute | solution.py:24
  19.4 4.6 %collective-permute-start.6 = (f32[4,2,4,4,128]{4,2,3,1,0:T(4,128)S(1)}, f32[4,2,4,4,128]{4,2,3,1,0:T(4,128)S(1)}, u32[]{:S(2)}, u32[]{:S(2)}) collective-permute-start(f32[4,2,4,4,128]{4,2,3,1,0:T(4,128)S(1)} %pad_maximum_fusion.53), channel_id=1, source_target_pairs={{0,4},{4,0},{1,5},{5,1},{2,6},{6,2},{3,7},{7,3},{8,12},{12,8},{9,1... | collective-permute-start | bytes 196616 | tf_op jit(solution)/shard_map/ppermute | solution.py:37
  20.0 3.4 %collective-permute-start.5 = (f32[4,4,1,4,128]{4,2,3,1,0:T(1,128)S(1)}, f32[4,4,1,4,128]{4,2,3,1,0:T(1,128)S(1)}, u32[]{:S(2)}, u32[]{:S(2)}) collective-permute-start(f32[4,4,1,4,128]{4,2,3,1,0:T(1,128)S(1)} %get-tuple-element.23), channel_id=1, source_target_pairs={{0,1},{1,2},{2,3},{3,0},{4,5},{5,6},{6,7},{7,4},{8,9},{9,10},{10,1... | collective-permute-start | bytes 98312 | tf_op jit(solution)/shard_map/ppermute | solution.py:24
  20.2 3.9 %collective-permute-start.8 = (f32[1,4,4,4,128]{4,2,3,1,0:T(4,128)S(1)}, f32[1,4,4,4,128]{4,2,3,1,0:T(4,128)S(1)}, u32[]{:S(2)}, u32[]{:S(2)}) collective-permute-start(f32[1,4,4,4,128]{4,2,3,1,0:T(4,128)S(1)} %get-tuple-element.26), channel_id=1, source_target_pairs={{0,24},{8,0},{16,8},{24,16},{1,25},{9,1},{17,9},{25,17},{2,26},{10... | collective-permute-start | bytes 98312 | tf_op jit(solution)/shard_map/ppermute | solution.py:24
  21.7 5.7 %collective-permute-start.7 = (f32[1,4,4,4,128]{4,2,3,1,0:T(4,128)S(1)}, f32[1,4,4,4,128]{4,2,3,1,0:T(4,128)S(1)}, u32[]{:S(2)}, u32[]{:S(2)}) collective-permute-start(f32[1,4,4,4,128]{4,2,3,1,0:T(4,128)S(1)} %get-tuple-element.25), channel_id=1, source_target_pairs={{0,8},{8,16},{16,24},{24,0},{1,9},{9,17},{17,25},{25,1},{2,10},{10... | collective-permute-start | bytes 98312 | tf_op jit(solution)/shard_map/ppermute | solution.py:24
  24.0 26.2 %copy-start.11 = (f32[6,1,4,4,128]{4,2,3,1,0:T(4,128)}, f32[6,1,4,4,128]{4,2,3,1,0:T(4,128)S(1)}, u32[]{:S(2)}) copy-start(f32[6,1,4,4,128]{4,2,3,1,0:T(4,128)S(1)} %pad.45) | copy-start | bytes 147460
  27.4 0.6 copy-start.13
  28.2 7.3 %collective-permute-start.12 = (f32[10,2,2,512]{3,2,1,0:T(2,128)S(1)}, f32[10,2,2,512]{3,2,1,0:T(2,128)S(1)}, u32[]{:S(2)}, u32[]{:S(2)}) collective-permute-start(f32[10,2,2,512]{3,2,1,0:T(2,128)S(1)} %pad_maximum_fusion.52), channel_id=1, source_target_pairs={{0,8},{8,16},{16,24},{24,0},{1,9},{9,17},{17,25},{25,1},{2,10},{10... | collective-permute-start | bytes 245768 | tf_op jit(solution)/shard_map/ppermute | solution.py:24
  28.2 9.8 %collective-permute-start.11 = (f32[10,2,2,512]{3,2,1,0:T(2,128)S(1)}, f32[10,2,2,512]{3,2,1,0:T(2,128)S(1)}, u32[]{:S(2)}, u32[]{:S(2)}) collective-permute-start(f32[10,2,2,512]{3,2,1,0:T(2,128)S(1)} %pad_maximum_fusion.52), channel_id=1, source_target_pairs={{0,16},{8,24},{16,0},{24,8},{1,17},{9,25},{17,1},{25,9},{2,18},{10... | collective-permute-start | bytes 245768 | tf_op jit(solution)/shard_map/ppermute | solution.py:24
  28.9 9.2 %collective-permute-start.10 = (f32[10,2,2,512]{3,2,1,0:T(2,128)S(1)}, f32[10,2,2,512]{3,2,1,0:T(2,128)S(1)}, u32[]{:S(2)}, u32[]{:S(2)}) collective-permute-start(f32[10,2,2,512]{3,2,1,0:T(2,128)S(1)} %pad_maximum_fusion.52), channel_id=1, source_target_pairs={{0,24},{8,0},{16,8},{24,16},{1,25},{9,1},{17,9},{25,17},{2,26},{10... | collective-permute-start | bytes 245768 | tf_op jit(solution)/shard_map/ppermute | solution.py:24
  38.7 4.9 %collective-permute-start.19 = (f32[8,2,2,512]{3,2,1,0:T(2,128)}, f32[8,2,2,512]{3,2,1,0:T(2,128)S(1)}, u32[]{:S(2)}, u32[]{:S(2)}) collective-permute-start(f32[8,2,2,512]{3,2,1,0:T(2,128)} %pad_maximum_fusion.54), channel_id=1, source_target_pairs={{7,0},{4,1},{5,2},{6,3},{3,4},{0,5},{1,6},{2,7},{15,8},{12,9},{13,... | collective-permute-start | bytes 196616 | tf_op jit(solution)/shard_map/ppermute | solution.py:108
  38.7 6.2 %collective-permute-start.18 = (f32[8,2,2,512]{3,2,1,0:T(2,128)}, f32[8,2,2,512]{3,2,1,0:T(2,128)S(1)}, u32[]{:S(2)}, u32[]{:S(2)}) collective-permute-start(f32[8,2,2,512]{3,2,1,0:T(2,128)} %pad_maximum_fusion.54), channel_id=1, source_target_pairs={{6,0},{7,1},{4,2},{5,3},{2,4},{3,5},{0,6},{1,7},{14,8},{15,9},{12,... | collective-permute-start | bytes 196616 | tf_op jit(solution)/shard_map/ppermute | solution.py:108
  40.0 10.2 %collective-permute-start.17 = (f32[8,2,2,512]{3,2,1,0:T(2,128)}, f32[8,2,2,512]{3,2,1,0:T(2,128)}, u32[]{:S(2)}, u32[]{:S(2)}) collective-permute-start(f32[8,2,2,512]{3,2,1,0:T(2,128)} %pad_maximum_fusion.54), channel_id=1, source_target_pairs={{5,0},{6,1},{7,2},{4,3},{1,4},{2,5},{3,6},{0,7},{13,8},{14,9},{15,... | collective-permute-start | bytes 196616 | tf_op jit(solution)/shard_map/ppermute | solution.py:108
  42.4 7.8 %collective-permute-start.16 = (f32[8,2,2,512]{3,2,1,0:T(2,128)}, f32[8,2,2,512]{3,2,1,0:T(2,128)}, u32[]{:S(2)}, u32[]{:S(2)}) collective-permute-start(f32[8,2,2,512]{3,2,1,0:T(2,128)} %pad_maximum_fusion.54), channel_id=1, source_target_pairs={{4,0},{5,1},{6,2},{7,3},{0,4},{1,5},{2,6},{3,7},{12,8},{13,9},{14,... | collective-permute-start | bytes 196616 | tf_op jit(solution)/shard_map/ppermute | solution.py:108
  43.0 7.1 %collective-permute-start.15 = (f32[8,2,2,512]{3,2,1,0:T(2,128)}, f32[8,2,2,512]{3,2,1,0:T(2,128)}, u32[]{:S(2)}, u32[]{:S(2)}) collective-permute-start(f32[8,2,2,512]{3,2,1,0:T(2,128)} %pad_maximum_fusion.54), channel_id=1, source_target_pairs={{3,0},{0,1},{1,2},{2,3},{7,4},{4,5},{5,6},{6,7},{11,8},{8,9},{9,10... | collective-permute-start | bytes 196616 | tf_op jit(solution)/shard_map/ppermute | solution.py:108
  43.6 3.1 %copy-start.18 = (f32[8,2,2,512]{3,2,1,0:T(2,128)}, f32[8,2,2,512]{3,2,1,0:T(2,128)S(1)}, u32[]{:S(2)}) copy-start(f32[8,2,2,512]{3,2,1,0:T(2,128)S(1)} %collective-permute-done.19) | copy-start | bytes 196612
  43.6 6.6 %collective-permute-start.14 = (f32[8,2,2,512]{3,2,1,0:T(2,128)}, f32[8,2,2,512]{3,2,1,0:T(2,128)S(1)}, u32[]{:S(2)}, u32[]{:S(2)}) collective-permute-start(f32[8,2,2,512]{3,2,1,0:T(2,128)} %pad_maximum_fusion.54), channel_id=1, source_target_pairs={{2,0},{3,1},{0,2},{1,3},{6,4},{7,5},{4,6},{5,7},{10,8},{11,9},{8,1... | collective-permute-start | bytes 196616 | tf_op jit(solution)/shard_map/ppermute | solution.py:108
  44.9 1.9 %copy-start.20 = (f32[8,2,2,512]{3,2,1,0:T(2,128)}, f32[8,2,2,512]{3,2,1,0:T(2,128)S(1)}, u32[]{:S(2)}) copy-start(f32[8,2,2,512]{3,2,1,0:T(2,128)S(1)} %collective-permute-done.18) | copy-start | bytes 196612
  44.9 5.3 %collective-permute-start.13 = (f32[8,2,2,512]{3,2,1,0:T(2,128)}, f32[8,2,2,512]{3,2,1,0:T(2,128)S(1)}, u32[]{:S(2)}, u32[]{:S(2)}) collective-permute-start(f32[8,2,2,512]{3,2,1,0:T(2,128)} %pad_maximum_fusion.54), channel_id=1, source_target_pairs={{1,0},{2,1},{3,2},{0,3},{5,4},{6,5},{7,6},{4,7},{9,8},{10,9},{11,1... | collective-permute-start | bytes 196616 | tf_op jit(solution)/shard_map/ppermute | solution.py:108
  48.5 1.8 %copy-start.19 = (f32[8,2,2,512]{3,2,1,0:T(2,128)S(1)}, f32[8,2,2,512]{3,2,1,0:T(2,128)}, u32[]{:S(2)}) copy-start(f32[8,2,2,512]{3,2,1,0:T(2,128)} %copy-done.18) | copy-start | bytes 196612
  48.5 1.8 %copy-start.21 = (f32[8,2,2,512]{3,2,1,0:T(2,128)S(1)}, f32[8,2,2,512]{3,2,1,0:T(2,128)}, u32[]{:S(2)}) copy-start(f32[8,2,2,512]{3,2,1,0:T(2,128)} %copy-done.20) | copy-start | bytes 196612
  55.3 5.8 %collective-permute-start.24 = (f32[4,4,1,4,128]{4,2,3,1,0:T(1,128)S(1)}, f32[4,4,1,4,128]{4,2,3,1,0:T(1,128)S(1)}, u32[]{:S(2)}, u32[]{:S(2)}) collective-permute-start(f32[4,4,1,4,128]{4,2,3,1,0:T(1,128)S(1)} %get-tuple-element.18), channel_id=1, source_target_pairs={{0,1},{1,2},{2,3},{3,0},{4,5},{5,6},{6,7},{7,4},{8,9},{9,10},{10,1... | collective-permute-start | bytes 98312 | tf_op jit(solution)/shard_map/ppermute | solution.py:24
  55.4 9.7 %collective-permute-start.22 = (f32[4,2,4,4,128]{4,2,3,1,0:T(4,128)S(1)}, f32[4,2,4,4,128]{4,2,3,1,0:T(4,128)S(1)}, u32[]{:S(2)}, u32[]{:S(2)}) collective-permute-start(f32[4,2,4,4,128]{4,2,3,1,0:T(4,128)S(1)} %pad_maximum_fusion.55), channel_id=1, source_target_pairs={{0,4},{4,0},{1,5},{5,1},{2,6},{6,2},{3,7},{7,3},{8,12},{12,8},{9,1... | collective-permute-start | bytes 196616 | tf_op jit(solution)/shard_map/ppermute | solution.py:37
  56.9 5.0 %collective-permute-start.20 = (f32[1,4,4,4,128]{4,2,3,1,0:T(4,128)S(1)}, f32[1,4,4,4,128]{4,2,3,1,0:T(4,128)S(1)}, u32[]{:S(2)}, u32[]{:S(2)}) collective-permute-start(f32[1,4,4,4,128]{4,2,3,1,0:T(4,128)S(1)} %get-tuple-element.20), channel_id=1, source_target_pairs={{0,24},{8,0},{16,8},{24,16},{1,25},{9,1},{17,9},{25,17},{2,26},{10... | collective-permute-start | bytes 98312 | tf_op jit(solution)/shard_map/ppermute | solution.py:24
  59.0 5.7 %collective-permute-start.21 = (f32[1,4,4,4,128]{4,2,3,1,0:T(4,128)S(1)}, f32[1,4,4,4,128]{4,2,3,1,0:T(4,128)S(1)}, u32[]{:S(2)}, u32[]{:S(2)}) collective-permute-start(f32[1,4,4,4,128]{4,2,3,1,0:T(4,128)S(1)} %get-tuple-element.19), channel_id=1, source_target_pairs={{0,8},{8,16},{16,24},{24,0},{1,9},{9,17},{17,25},{25,1},{2,10},{10... | collective-permute-start | bytes 98312 | tf_op jit(solution)/shard_map/ppermute | solution.py:24
  59.0 5.8 %collective-permute-start.23 = (f32[4,4,1,4,128]{4,2,3,1,0:T(1,128)S(1)}, f32[4,4,1,4,128]{4,2,3,1,0:T(1,128)S(1)}, u32[]{:S(2)}, u32[]{:S(2)}) collective-permute-start(f32[4,4,1,4,128]{4,2,3,1,0:T(1,128)S(1)} %get-tuple-element.17), channel_id=1, source_target_pairs={{0,3},{1,0},{2,1},{3,2},{4,7},{5,4},{6,5},{7,6},{8,11},{9,8},{10,9... | collective-permute-start | bytes 98312 | tf_op jit(solution)/shard_map/ppermute | solution.py:24
  60.9 0.9 %copy-start.6 = (f32[8,8,1,4,128]{4,2,3,1,0:T(1,128)S(1)}, f32[8,8,1,4,128]{4,2,3,1,0:T(1,128)}, u32[]{:S(2)}) copy-start(f32[8,8,1,4,128]{4,2,3,1,0:T(1,128)} %copy-done.5) | copy-start | bytes 393220
  61.1 0.9 %copy-start.10 = (f32[1,8,8,4,128]{4,2,3,1,0:T(8,128)S(1)}, f32[1,8,8,4,128]{4,2,3,1,0:T(8,128)}, u32[]{:S(2)}) copy-start(f32[1,8,8,4,128]{4,2,3,1,0:T(8,128)} %copy-done.9) | copy-start | bytes 393220
  61.1 3.7 %copy-start.8 = (f32[1,8,8,4,128]{4,2,3,1,0:T(8,128)S(1)}, f32[1,8,8,4,128]{4,2,3,1,0:T(8,128)}, u32[]{:S(2)}) copy-start(f32[1,8,8,4,128]{4,2,3,1,0:T(8,128)} %copy-done.7) | copy-start | bytes 393220
  61.1 3.7 %copy-start.4 = (f32[8,8,1,4,128]{4,2,3,1,0:T(1,128)S(1)}, f32[8,8,1,4,128]{4,2,3,1,0:T(1,128)}, u32[]{:S(2)}) copy-start(f32[8,8,1,4,128]{4,2,3,1,0:T(1,128)} %copy-done.3) | copy-start | bytes 393220
  64.7 1.0 %copy-start.2 = (f32[8,2,8,4,128]{4,2,3,1,0:T(8,128)S(1)}, f32[8,2,8,4,128]{4,2,3,1,0:T(8,128)}, u32[]{:S(2)}) copy-start(f32[8,2,8,4,128]{4,2,3,1,0:T(8,128)} %copy-done.1) | copy-start | bytes 786436

commit v18 on v14

--- a/solution.py
+++ b/solution.py
@@ -193,7 +193,7 @@
     operator = coarse_matrix(grid, tuple(starts), rhs_two.shape[:3])
     operator = jnp.asarray(operator.reshape((-1,) + tuple(grid)))
     post = jnp.einsum(
-        "qxyz,xyzgl->qgl", operator, extended, precision=lax.Precision.HIGHEST, preferred_element_type=jnp.float32
+        "qxyz,xyzgl->qgl", operator, extended, precision=lax.Precision.HIGH, preferred_element_type=jnp.float32
     )
     return post.reshape(tuple(2 * size + 2 for size in rhs_two.shape[:3]) + orbs), tiles_by_step
 

time: 66.6 us -> 66.4 us (level)
  no operation moved by 1% of the time
where the time goes in v18:
time: 66.4 us; the launch traced here: 66.1 us
  starting transfers between devices  26.5 us (40%)
  waiting for transfers between devices  17.7 us (27%)
  other arithmetic  11.1 us (17%)
  local copies, waits for them, and re-layouts  6.36 us (10%)
  matrix products  3.49 us (5%)
  between operations  0.91 us (1%)
    ppermute x15, waiting for transfers between devices, shifted(): lax.ppermute(block, axis, [(j, (j - step) % count) for j in range(count)])  16.7 us
    ppermute x15, starting transfers between devices, shifted(): lax.ppermute(block, axis, [(j, (j - step) % count) for j in range(count)])  14.9 us
    ppermute x7, starting transfers between devices, fetch(): cache[steps] = lax.ppermute(block, tuple(axes), pairs)  6.89 us
    ppermute x3, starting transfers between devices, axis_faces(): lax.ppermute(jnp.concatenate([first, last], axis=dim), axis, [(0, 1), (1,...  4.74 us
    div x3, other arithmetic, vcycle(): omega * part.astype(jnp.float32) / center  2.46 us
    sub x1, other arithmetic, vcycle(): rhs_one = restrict(rhs_zero - stencil(corr_zero, faces_zero, 0))  1.86 us
    dot_general x1, matrix products, body(): jnp.dot(rows, gram, precision=lax.Precision.HIGH, preferred_element_type=...  1.81 us
    dot_general x1, matrix products, coarse_solve(): jnp.einsum('qxyz,xyzgl->qgl', operator, extended, precision=lax.Precision...  1.69 us
  transfers between devices with their start and end apart: 25, of which 9 were waited for; matrix products, arithmetic and copies ran while one was open for 15% of the time, Pallas kernels for 0%

profile of v18, /device:TPU:0, one launch (start us, length us, event | category | flops | bytes accessed | tf_op | source)
XLA Modules:
  0.0 66.1 jit_solution(11185019241843515042)
XLA Ops:
  0.0 1.5 %fusion.57 = (f32[8,8,1,4,128]{4,2,3,1,0:T(1,128)S(1)}, f32[8,8,1,4,128]{4,2,3,1,0:T(1,128)S(1)}) fusion(bf16[8,8,8,4,128]{4,2,3,1,0:T(8,128)(2,1)} %bitcast.71), kind=kLoop, calls=%fused_computation.133 | loop fusion | flops 131072 | bytes 393216 | tf_op jit(solution)/shard_map/div | solution.py:311
  1.6 0.6 collective-permute-start.4
  2.1 0.9 %convert_multiply_fusion.3 = (f32[8,1,8,4,128]{4,2,3,1,0:T(8,128)S(1)}, f32[8,1,8,4,128]{4,2,3,1,0:T(8,128)S(1)}) fusion(bf16[8,8,8,4,128]{4,2,3,1,0:T(8,128)(2,1)} %bitcast.72), kind=kLoop, calls=%fused_computation.135 | loop fusion | flops 131072 | bytes 393216 | tf_op jit(solution)/shard_map/div | solution.py:311
  3.0 2.6 %collective-permute-start.2 = (f32[8,2,8,4,128]{4,2,3,1,0:T(8,128)S(1)}, f32[8,2,8,4,128]{4,2,3,1,0:T(8,128)S(1)}, u32[]{:S(2)}, u32[]{:S(2)}) collective-permute-start(f32[8,2,8,4,128]{4,2,3,1,0:T(8,128)S(1)} %pad_maximum_fusion.32), channel_id=1, source_target_pairs={{0,4},{4,0},{1,5},{5,1},{2,6},{6,2},{3,7},{7,3},{8,12},{12,8},{9,1... | collective-permute-start | bytes 786440 | tf_op jit(solution)/shard_map/ppermute | solution.py:37
  5.7 3.7 %collective-permute-start = (f32[1,8,8,4,128]{4,2,3,1,0:T(8,128)S(1)}, f32[1,8,8,4,128]{4,2,3,1,0:T(8,128)}, u32[]{:S(2)}, u32[]{:S(2)}) collective-permute-start(f32[1,8,8,4,128]{4,2,3,1,0:T(8,128)S(1)} %get-tuple-element.10), channel_id=1, source_target_pairs={{0,24},{8,0},{16,8},{24,16},{1,25},{9,1},{17,9},{25,17},{2,26},{10... | collective-permute-start | bytes 393224 | tf_op jit(solution)/shard_map/ppermute | solution.py:24
  9.3 1.2 %collective-permute-start.3 = (f32[8,8,1,4,128]{4,2,3,1,0:T(1,128)S(1)}, f32[8,8,1,4,128]{4,2,3,1,0:T(1,128)S(1)}, u32[]{:S(2)}, u32[]{:S(2)}) collective-permute-start(f32[8,8,1,4,128]{4,2,3,1,0:T(1,128)S(1)} %get-tuple-element.7), channel_id=1, source_target_pairs={{0,3},{1,0},{2,1},{3,2},{4,7},{5,4},{6,5},{7,6},{8,11},{9,8},{10,9... | collective-permute-start | bytes 393224 | tf_op jit(solution)/shard_map/ppermute | solution.py:24
  10.5 0.7 copy.45
  11.4 0.6 gather_fusion
  12.1 0.2 slice_reduce_fusion.1
  12.6 0.7 %fusion.58 = (f32[4,4]{1,0:T(4,128)}, f32[4,4]{1,0:T(4,128)}) fusion(s32[4]{0:T(128)S(1)} %get-tuple-element.5, s32[4]{0:T(128)S(1)} %get-tuple-element.6), kind=kLoop, calls=%fused_computation.158 | loop fusion | flops 64 | bytes 160 | tf_op jit(solution)/shard_map/convert_element_type | solution.py:303
  13.5 3.9 %collective-permute-done.1 = f32[1,8,8,4,128]{4,2,3,1,0:T(8,128)S(1)} collective-permute-done((f32[1,8,8,4,128]{4,2,3,1,0:T(8,128)S(1)}, f32[1,8,8,4,128]{4,2,3,1,0:T(8,128)S(1)}, u32[]{:S(2)}, u32[]{:S(2)}) %collective-permute-start.1) | collective-permute-done | bytes 131104 | tf_op jit(solution)/shard_map/ppermute | solution.py:24
  17.4 1.9 %convert_subtract_fusion.1 = f32[8,8,8,4,128]{4,2,3,1,0:T(8,128)S(1)} fusion(f32[8,8,1,4,128]{4,2,3,1,0:T(1,128)S(1)} %collective-permute-done.4, f32[10,1,8,4,128]{4,2,3,1,0:T(8,128)S(1)} %pad.40, f32[10,1,8,4,128]{4,2,3,1,0:T(8,128)S(1)} %pad.41, f32[1,8,8,4,128]{4,2,3,1,0:T(8,128)} %collective-permute-done, ...), kind=kLoop, calls=%fused_computation.3 | loop fusion | flops 8912896 | bytes 3473408 | tf_op jit(solution)/shard_map/sub | solution.py:314
  19.3 0.7 %reduce_sum.27 = f32[4,4,4,4,128]{4,2,3,1,0:T(4,128)S(1)} reduce(f32[4,2,4,2,4,2,4,128]{7,5,4,6,3,2,1,0:T(2,128)S(1)} %bitcast.75, f32[]{:T(128)} %constant.93.clone.1), dimensions={1,3,5}, to_apply=%region_0.1 | reduce | flops 229376 | bytes 1179652 | tf_op jit(solution)/shard_map/reduce_sum | solution.py:177
  20.3 0.6 collective-permute-start.6
  20.8 0.2 collective-permute-start.5
  21.1 1.5 %collective-permute-start.8 = (f32[1,4,4,4,128]{4,2,3,1,0:T(4,128)S(1)}, f32[1,4,4,4,128]{4,2,3,1,0:T(4,128)S(1)}, u32[]{:S(2)}, u32[]{:S(2)}) collective-permute-start(f32[1,4,4,4,128]{4,2,3,1,0:T(4,128)S(1)} %get-tuple-element.26), channel_id=1, source_target_pairs={{0,24},{8,0},{16,8},{24,16},{1,25},{9,1},{17,9},{25,17},{2,26},{10... | collective-permute-start | bytes 98312 | tf_op jit(solution)/shard_map/ppermute | solution.py:24
  22.5 0.6 collective-permute-start.7
  23.1 1.1 %collective-permute-done.5 = f32[4,4,1,4,128]{4,2,3,1,0:T(1,128)S(1)} collective-permute-done((f32[4,4,1,4,128]{4,2,3,1,0:T(1,128)S(1)}, f32[4,4,1,4,128]{4,2,3,1,0:T(1,128)S(1)}, u32[]{:S(2)}, u32[]{:S(2)}) %collective-permute-start.5) | collective-permute-done | bytes 32800 | tf_op jit(solution)/shard_map/ppermute | solution.py:24
  24.3 0.6 collective-permute-done.6
  25.0 3.3 %collective-permute-done.7 = f32[1,4,4,4,128]{4,2,3,1,0:T(4,128)S(1)} collective-permute-done((f32[1,4,4,4,128]{4,2,3,1,0:T(4,128)S(1)}, f32[1,4,4,4,128]{4,2,3,1,0:T(4,128)S(1)}, u32[]{:S(2)}, u32[]{:S(2)}) %collective-permute-start.7) | collective-permute-done | bytes 32800 | tf_op jit(solution)/shard_map/ppermute | solution.py:24
  28.2 0.2 fusion.51
  28.7 1.0 %collective-permute-start.11 = (f32[10,2,2,4,128]{4,2,1,3,0:T(2,128)S(1)}, f32[10,2,2,4,128]{4,2,1,3,0:T(2,128)S(1)}, u32[]{:S(2)}, u32[]{:S(2)}) collective-permute-start(f32[10,2,2,4,128]{4,2,1,3,0:T(2,128)S(1)} %pad_maximum_fusion.52), channel_id=1, source_target_pairs={{0,16},{8,24},{16,0},{24,8},{1,17},{9,25},{17,1},{25,9},{2,18},{10... | collective-permute-start | bytes 245768 | tf_op jit(solution)/shard_map/ppermute | solution.py:24
  29.6 2.9 %collective-permute-start.10 = (f32[10,2,2,4,128]{4,2,1,3,0:T(2,128)S(1)}, f32[10,2,2,4,128]{4,2,1,3,0:T(2,128)S(1)}, u32[]{:S(2)}, u32[]{:S(2)}) collective-permute-start(f32[10,2,2,4,128]{4,2,1,3,0:T(2,128)S(1)} %pad_maximum_fusion.52), channel_id=1, source_target_pairs={{0,24},{8,0},{16,8},{24,16},{1,25},{9,1},{17,9},{25,17},{2,26},{10... | collective-permute-start | bytes 245768 | tf_op jit(solution)/shard_map/ppermute | solution.py:24
  32.6 3.3 %collective-permute-done.12 = f32[10,2,2,4,128]{4,2,1,3,0:T(2,128)S(1)} collective-permute-done((f32[10,2,2,4,128]{4,2,1,3,0:T(2,128)S(1)}, f32[10,2,2,4,128]{4,2,1,3,0:T(2,128)S(1)}, u32[]{:S(2)}, u32[]{:S(2)}) %collective-permute-start.12) | collective-permute-done | bytes 81952 | tf_op jit(solution)/shard_map/ppermute | solution.py:24
  35.9 2.6 %collective-permute-done.11 = f32[10,2,2,4,128]{4,2,1,3,0:T(2,128)S(1)} collective-permute-done((f32[10,2,2,4,128]{4,2,1,3,0:T(2,128)S(1)}, f32[10,2,2,4,128]{4,2,1,3,0:T(2,128)S(1)}, u32[]{:S(2)}, u32[]{:S(2)}) %collective-permute-start.11) | collective-permute-done | bytes 81952 | tf_op jit(solution)/shard_map/ppermute | solution.py:24
  38.5 0.6 pad_maximum_fusion.54
  39.2 1.3 %collective-permute-start.18 = (f32[8,2,2,4,128]{4,2,1,3,0:T(2,128)}, f32[8,2,2,4,128]{4,2,1,3,0:T(2,128)S(1)}, u32[]{:S(2)}, u32[]{:S(2)}) collective-permute-start(f32[8,2,2,4,128]{4,2,1,3,0:T(2,128)} %pad_maximum_fusion.54), channel_id=1, source_target_pairs={{6,0},{7,1},{4,2},{5,3},{2,4},{3,5},{0,6},{1,7},{14,8},{15,9},{12,... | collective-permute-start | bytes 196616 | tf_op jit(solution)/shard_map/ppermute | solution.py:108
  40.5 2.4 %collective-permute-start.17 = (f32[8,2,2,4,128]{4,2,1,3,0:T(2,128)}, f32[8,2,2,4,128]{4,2,1,3,0:T(2,128)}, u32[]{:S(2)}, u32[]{:S(2)}) collective-permute-start(f32[8,2,2,4,128]{4,2,1,3,0:T(2,128)} %pad_maximum_fusion.54), channel_id=1, source_target_pairs={{5,0},{6,1},{7,2},{4,3},{1,4},{2,5},{3,6},{0,7},{13,8},{14,9},{15,... | collective-permute-start | bytes 196616 | tf_op jit(solution)/shard_map/ppermute | solution.py:108
  42.9 0.5 collective-permute-start.16
  43.6 0.5 collective-permute-done.19
  44.1 1.2 %collective-permute-start.14 = (f32[8,2,2,4,128]{4,2,1,3,0:T(2,128)}, f32[8,2,2,4,128]{4,2,1,3,0:T(2,128)}, u32[]{:S(2)}, u32[]{:S(2)}) collective-permute-start(f32[8,2,2,4,128]{4,2,1,3,0:T(2,128)} %pad_maximum_fusion.54), channel_id=1, source_target_pairs={{2,0},{3,1},{0,2},{1,3},{6,4},{7,5},{4,6},{5,7},{10,8},{11,9},{8,1... | collective-permute-start | bytes 196616 | tf_op jit(solution)/shard_map/ppermute | solution.py:108
  45.3 1.4 %collective-permute-start.13 = (f32[8,2,2,4,128]{4,2,1,3,0:T(2,128)}, f32[8,2,2,4,128]{4,2,1,3,0:T(2,128)}, u32[]{:S(2)}, u32[]{:S(2)}) collective-permute-start(f32[8,2,2,4,128]{4,2,1,3,0:T(2,128)} %pad_maximum_fusion.54), channel_id=1, source_target_pairs={{1,0},{2,1},{3,2},{0,3},{5,4},{6,5},{7,6},{4,7},{9,8},{10,9},{11,1... | collective-permute-start | bytes 196616 | tf_op jit(solution)/shard_map/ppermute | solution.py:108
  46.8 0.4 multiply_reduce_fusion
  47.2 1.7 %copy.52 = f32[4,128,4,128]{3,2,1,0:T(4,128)} copy(f32[4,128,4,128]{3,1,2,0:T(8,128)S(1)} %multiply_reduce_fusion) | data formatting | bytes 2097152 | tf_op jit(solution)/shard_map/reduce_sum | solution.py:306
  48.8 1.6 %reshape.603 = f32[512,512,1,1]{1,0,2,3:T(8,128)S(1)} reshape(f32[4,128,4,128]{3,2,1,0:T(4,128)} %copy.52) | data formatting | bytes 2097152 | tf_op jit(solution)/shard_map/reshape | solution.py:306
  50.6 1.7 %convolution_bitcast_fusion = f32[216,4,128]{2,0,1:T(8,128)S(1)} fusion(f32[216,8,4,8,1]{0,3,2,4,1:T(8,128)} %constant.137, f32[8,2,2,4,128]{4,2,1,3,0:T(2,128)} %copy-done.22, f32[8,2,2,4,128]{4,2,1,3,0:T(2,128)} %copy-done.23, f32[8,2,2,4,128]{4,2,1,3,0:T(2,128)} %collective-permute-done.17, f32[8,2,2,4,128]{4,2,1,3,0:T(2,128)} %collective-permute-done.16, ...), kind=kOutput, calls=%fused_computation.7 | convolution fusion | flops 171180032 | bytes 1187840 | tf_op jit(solution)/shard_map/qxyz,xyzgl->qgl/dot_general | solution.py:195
  52.4 0.2 maximum_add_fusion
  52.7 0.2 fusion.47
  53.0 1.6 %collective-permute-start.22 = (f32[4,2,4,4,128]{4,2,3,1,0:T(4,128)S(1)}, f32[4,2,4,4,128]{4,2,3,1,0:T(4,128)S(1)}, u32[]{:S(2)}, u32[]{:S(2)}) collective-permute-start(f32[4,2,4,4,128]{4,2,3,1,0:T(4,128)S(1)} %pad_maximum_fusion.55), channel_id=1, source_target_pairs={{0,4},{4,0},{1,5},{5,1},{2,6},{6,2},{3,7},{7,3},{8,12},{12,8},{9,1... | collective-permute-start | bytes 196616 | tf_op jit(solution)/shard_map/ppermute | solution.py:37
  54.6 2.1 %collective-permute-start.20 = (f32[1,4,4,4,128]{4,2,3,1,0:T(4,128)S(1)}, f32[1,4,4,4,128]{4,2,3,1,0:T(4,128)S(1)}, u32[]{:S(2)}, u32[]{:S(2)}) collective-permute-start(f32[1,4,4,4,128]{4,2,3,1,0:T(4,128)S(1)} %get-tuple-element.20), channel_id=1, source_target_pairs={{0,24},{8,0},{16,8},{24,16},{1,25},{9,1},{17,9},{25,17},{2,26},{10... | collective-permute-start | bytes 98312 | tf_op jit(solution)/shard_map/ppermute | solution.py:24
  56.7 1.2 %collective-permute-start.23 = (f32[4,4,1,4,128]{4,2,3,1,0:T(1,128)S(1)}, f32[4,4,1,4,128]{4,2,3,1,0:T(1,128)S(1)}, u32[]{:S(2)}, u32[]{:S(2)}) collective-permute-start(f32[4,4,1,4,128]{4,2,3,1,0:T(1,128)S(1)} %get-tuple-element.17), channel_id=1, source_target_pairs={{0,3},{1,0},{2,1},{3,2},{4,7},{5,4},{6,5},{7,6},{8,11},{9,8},{10,9... | collective-permute-start | bytes 98312 | tf_op jit(solution)/shard_map/ppermute | solution.py:24
  58.0 0.6 broadcast_in_dim.88
  58.6 0.2 fusion.42
  59.1 0.9 %add.206 = f32[1,8,8,4,128]{4,2,3,1,0:T(8,128)S(1)} add(f32[1,8,8,4,128]{4,2,3,1,0:T(8,128)} %collective-permute-done, f32[1,8,8,4,128]{4,2,3,1,0:T(8,128)S(1)} %bitcast.81) | non-fusion elementwise | flops 32768 | bytes 393216 | tf_op jit(solution)/shard_map/add | solution.py:268
  60.0 2.4 %collective-permute-done.21 = f32[1,4,4,4,128]{4,2,3,1,0:T(4,128)S(1)} collective-permute-done((f32[1,4,4,4,128]{4,2,3,1,0:T(4,128)S(1)}, f32[1,4,4,4,128]{4,2,3,1,0:T(4,128)S(1)}, u32[]{:S(2)}, u32[]{:S(2)}) %collective-permute-start.21) | collective-permute-done | bytes 32800 | tf_op jit(solution)/shard_map/ppermute | solution.py:24
  63.0 1.0 %fusion.2 = f32[8,8,8,4,128]{4,2,3,1,0:T(8,128)S(1)} fusion(f32[8,8,8,4,128]{4,2,3,1,0:T(8,128)S(1)} %fusion.42, f32[8,8,1,4,128]{4,2,3,1,0:T(1,128)S(1)} %add.215, f32[10,1,8,4,128]{4,2,3,1,0:T(8,128)S(1)} %pad.48, f32[10,1,8,4,128]{4,2,3,1,0:T(8,128)S(1)} %pad.49, f32[1,8,8,4,128]{4,2,3,1,0:T(8,128)S(1)} %add.206, f32[1,8,8,4,128]{4,2,3,1,0:T(8,128)S(1)} %add.207, ...), kind=kLoop, calls=%fused_computation.10 | loop fusion | flops 9437184 | bytes 3473408 | tf_op jit(solution)/shard_map/add | solution.py:270
  64.0 0.2 bitcast_multiply_fusion
  64.3 1.8 %convolution_convert_fusion = bf16[8,8,8,512]{3,2,1,0:T(8,128)(2,1)} fusion(f32[8,8,8,512]{3,2,1,0:T(8,128)S(1)} %bitcast.74, f32[512,512,1,1]{1,0,2,3:T(8,128)S(1)} %reshape.603), kind=kOutput, calls=%fused_computation.6 | convolution fusion | flops 805568512 | bytes 2621440 | tf_op jit(solution)/shard_map/dot_general | solution.py:342
  (141 shorter events, 2.8 us)
Async XLA Ops:
  0.0 5.6 %copy-start = (bf16[8,8,8,512]{3,2,1,0:T(8,128)(2,1)S(1)}, bf16[8,8,8,512]{3,2,1,0:T(8,128)(2,1)}, u32[]{:S(2)}) copy-start(bf16[8,8,8,512]{3,2,1,0:T(8,128)(2,1)} %param.5) | copy-start | bytes 1572868
  0.0 10.5 %copy-start.8 = (f32[1,128,128]{2,1,0:T(8,128)S(1)}, f32[1,128,128]{2,1,0:T(8,128)}, u32[]{:S(2)}) copy-start(f32[1,128,128]{2,1,0:T(8,128)} %param.8) | copy-start | bytes 196612
  0.0 11.1 %copy-start.18 = (s32[3,2,512]{2,1,0:T(2,128)S(1)}, s32[3,2,512]{2,1,0:T(2,128)}, u32[]{:S(2)}) copy-start(s32[3,2,512]{2,1,0:T(2,128)} %param.6) | copy-start | bytes 36868
  0.0 11.2 %copy-start.21 = (s32[4,2]{0,1:T(2,128)S(1)}, s32[4,2]{0,1:T(2,128)}, u32[]{:S(2)}) copy-start(s32[4,2]{0,1:T(2,128)} %param.7) | copy-start | bytes 100
  1.6 11.9 %collective-permute-start.4 = (f32[8,8,1,4,128]{4,2,3,1,0:T(1,128)S(1)}, f32[8,8,1,4,128]{4,2,3,1,0:T(1,128)S(1)}, u32[]{:S(2)}, u32[]{:S(2)}) collective-permute-start(f32[8,8,1,4,128]{4,2,3,1,0:T(1,128)S(1)} %get-tuple-element.8), channel_id=1, source_target_pairs={{0,1},{1,2},{2,3},{3,0},{4,5},{5,6},{6,7},{7,4},{8,9},{9,10},{10,1... | collective-permute-start | bytes 393224 | tf_op jit(solution)/shard_map/ppermute | solution.py:24
  3.0 10.4 %collective-permute-start.2 = (f32[8,2,8,4,128]{4,2,3,1,0:T(8,128)S(1)}, f32[8,2,8,4,128]{4,2,3,1,0:T(8,128)S(1)}, u32[]{:S(2)}, u32[]{:S(2)}) collective-permute-start(f32[8,2,8,4,128]{4,2,3,1,0:T(8,128)S(1)} %pad_maximum_fusion.32), channel_id=1, source_target_pairs={{0,4},{4,0},{1,5},{5,1},{2,6},{6,2},{3,7},{7,3},{8,12},{12,8},{9,1... | collective-permute-start | bytes 786440 | tf_op jit(solution)/shard_map/ppermute | solution.py:37
  5.7 7.8 %collective-permute-start = (f32[1,8,8,4,128]{4,2,3,1,0:T(8,128)S(1)}, f32[1,8,8,4,128]{4,2,3,1,0:T(8,128)}, u32[]{:S(2)}, u32[]{:S(2)}) collective-permute-start(f32[1,8,8,4,128]{4,2,3,1,0:T(8,128)S(1)} %get-tuple-element.10), channel_id=1, source_target_pairs={{0,24},{8,0},{16,8},{24,16},{1,25},{9,1},{17,9},{25,17},{2,26},{10... | collective-permute-start | bytes 393224 | tf_op jit(solution)/shard_map/ppermute | solution.py:24
  9.3 8.1 %collective-permute-start.1 = (f32[1,8,8,4,128]{4,2,3,1,0:T(8,128)S(1)}, f32[1,8,8,4,128]{4,2,3,1,0:T(8,128)S(1)}, u32[]{:S(2)}, u32[]{:S(2)}) collective-permute-start(f32[1,8,8,4,128]{4,2,3,1,0:T(8,128)S(1)} %get-tuple-element.9), channel_id=1, source_target_pairs={{0,8},{8,16},{16,24},{24,0},{1,9},{9,17},{17,25},{25,1},{2,10},{10... | collective-permute-start | bytes 393224 | tf_op jit(solution)/shard_map/ppermute | solution.py:24
  9.3 8.1 %collective-permute-start.3 = (f32[8,8,1,4,128]{4,2,3,1,0:T(1,128)S(1)}, f32[8,8,1,4,128]{4,2,3,1,0:T(1,128)S(1)}, u32[]{:S(2)}, u32[]{:S(2)}) collective-permute-start(f32[8,8,1,4,128]{4,2,3,1,0:T(1,128)S(1)} %get-tuple-element.7), channel_id=1, source_target_pairs={{0,3},{1,0},{2,1},{3,2},{4,7},{5,4},{6,5},{7,6},{8,11},{9,8},{10,9... | collective-permute-start | bytes 393224 | tf_op jit(solution)/shard_map/ppermute | solution.py:24
  17.4 1.9 %copy-start.1 = (f32[1,8,8,4,128]{4,2,3,1,0:T(8,128)}, f32[1,8,8,4,128]{4,2,3,1,0:T(8,128)S(1)}, u32[]{:S(2)}) copy-start(f32[1,8,8,4,128]{4,2,3,1,0:T(8,128)S(1)} %collective-permute-done.1) | copy-start | bytes 393220
  20.0 8.5 %copy-start.7 = (f32[8,2,2,4,128]{4,2,1,3,0:T(2,128)S(1)}, f32[8,2,2,4,128]{4,2,1,3,0:T(2,128)}, u32[]{:S(2)}) copy-start(f32[8,2,2,4,128]{4,2,1,3,0:T(2,128)} %copy.45) | copy-start | bytes 196612
  20.1 12.4 %copy-start.19 = (f32[4,4]{1,0:T(4,128)S(1)}, f32[4,4]{1,0:T(4,128)}, u32[]{:S(2)}) copy-start(f32[4,4]{1,0:T(4,128)} %get-tuple-element.41) | copy-start | bytes 196
  20.1 12.4 %copy-start.20 = (f32[4,4]{1,0:T(4,128)S(1)}, f32[4,4]{1,0:T(4,128)}, u32[]{:S(2)}) copy-start(f32[4,4]{1,0:T(4,128)} %get-tuple-element.42) | copy-start | bytes 196
  20.2 2.9 %collective-permute-start.9 = (f32[4,4,1,4,128]{4,2,3,1,0:T(1,128)S(1)}, f32[4,4,1,4,128]{4,2,3,1,0:T(1,128)S(1)}, u32[]{:S(2)}, u32[]{:S(2)}) collective-permute-start(f32[4,4,1,4,128]{4,2,3,1,0:T(1,128)S(1)} %get-tuple-element.24), channel_id=1, source_target_pairs={{0,3},{1,0},{2,1},{3,2},{4,7},{5,4},{6,5},{7,6},{8,11},{9,8},{10,9... | collective-permute-start | bytes 98312 | tf_op jit(solution)/shard_map/ppermute | solution.py:24
  20.3 4.6 %collective-permute-start.6 = (f32[4,2,4,4,128]{4,2,3,1,0:T(4,128)S(1)}, f32[4,2,4,4,128]{4,2,3,1,0:T(4,128)S(1)}, u32[]{:S(2)}, u32[]{:S(2)}) collective-permute-start(f32[4,2,4,4,128]{4,2,3,1,0:T(4,128)S(1)} %pad_maximum_fusion.53), channel_id=1, source_target_pairs={{0,4},{4,0},{1,5},{5,1},{2,6},{6,2},{3,7},{7,3},{8,12},{12,8},{9,1... | collective-permute-start | bytes 196616 | tf_op jit(solution)/shard_map/ppermute | solution.py:37
  20.8 3.4 %collective-permute-start.5 = (f32[4,4,1,4,128]{4,2,3,1,0:T(1,128)S(1)}, f32[4,4,1,4,128]{4,2,3,1,0:T(1,128)S(1)}, u32[]{:S(2)}, u32[]{:S(2)}) collective-permute-start(f32[4,4,1,4,128]{4,2,3,1,0:T(1,128)S(1)} %get-tuple-element.23), channel_id=1, source_target_pairs={{0,1},{1,2},{2,3},{3,0},{4,5},{5,6},{6,7},{7,4},{8,9},{9,10},{10,1... | collective-permute-start | bytes 98312 | tf_op jit(solution)/shard_map/ppermute | solution.py:24
  21.1 3.9 %collective-permute-start.8 = (f32[1,4,4,4,128]{4,2,3,1,0:T(4,128)S(1)}, f32[1,4,4,4,128]{4,2,3,1,0:T(4,128)S(1)}, u32[]{:S(2)}, u32[]{:S(2)}) collective-permute-start(f32[1,4,4,4,128]{4,2,3,1,0:T(4,128)S(1)} %get-tuple-element.26), channel_id=1, source_target_pairs={{0,24},{8,0},{16,8},{24,16},{1,25},{9,1},{17,9},{25,17},{2,26},{10... | collective-permute-start | bytes 98312 | tf_op jit(solution)/shard_map/ppermute | solution.py:24
  22.5 5.7 %collective-permute-start.7 = (f32[1,4,4,4,128]{4,2,3,1,0:T(4,128)S(1)}, f32[1,4,4,4,128]{4,2,3,1,0:T(4,128)S(1)}, u32[]{:S(2)}, u32[]{:S(2)}) collective-permute-start(f32[1,4,4,4,128]{4,2,3,1,0:T(4,128)S(1)} %get-tuple-element.25), channel_id=1, source_target_pairs={{0,8},{8,16},{16,24},{24,0},{1,9},{9,17},{17,25},{25,1},{2,10},{10... | collective-permute-start | bytes 98312 | tf_op jit(solution)/shard_map/ppermute | solution.py:24
  24.8 18.7 %copy-start.3 = (f32[6,1,4,4,128]{4,2,3,1,0:T(4,128)}, f32[6,1,4,4,128]{4,2,3,1,0:T(4,128)S(1)}, u32[]{:S(2)}) copy-start(f32[6,1,4,4,128]{4,2,3,1,0:T(4,128)S(1)} %pad.46) | copy-start | bytes 147460
  24.9 18.7 %copy-start.5 = (f32[6,1,4,4,128]{4,2,3,1,0:T(4,128)}, f32[6,1,4,4,128]{4,2,3,1,0:T(4,128)S(1)}, u32[]{:S(2)}) copy-start(f32[6,1,4,4,128]{4,2,3,1,0:T(4,128)S(1)} %pad.45) | copy-start | bytes 147460
  24.9 18.7 %copy-start.9 = (f32[1,128,128]{2,1,0:T(8,128)S(1)}, f32[1,128,128]{2,1,0:T(8,128)}, u32[]{:S(2)}) copy-start(f32[1,128,128]{2,1,0:T(8,128)} %param.8) | copy-start | bytes 196612
  25.0 3.5 %copy-start.11 = (f32[1,4,4,4,128]{4,2,3,1,0:T(4,128)}, f32[1,4,4,4,128]{4,2,3,1,0:T(4,128)S(1)}, u32[]{:S(2)}) copy-start(f32[1,4,4,4,128]{4,2,3,1,0:T(4,128)S(1)} %collective-permute-done.8) | copy-start | bytes 98308
  28.2 15.1 %copy-start.13 = (f32[1,4,4,4,128]{4,2,3,1,0:T(4,128)}, f32[1,4,4,4,128]{4,2,3,1,0:T(4,128)S(1)}, u32[]{:S(2)}) copy-start(f32[1,4,4,4,128]{4,2,3,1,0:T(4,128)S(1)} %collective-permute-done.7) | copy-start | bytes 98308
  28.6 14.8 %copy-start.10 = (f32[2,2,2,4,128]{4,2,1,3,0:T(2,128)}, f32[2,2,2,4,128]{4,2,1,3,0:T(2,128)S(1)}, u32[]{:S(2)}) copy-start(f32[2,2,2,4,128]{4,2,1,3,0:T(2,128)S(1)} %copy_multiply_fusion) | copy-start | bytes 49156
  28.6 7.3 %collective-permute-start.12 = (f32[10,2,2,4,128]{4,2,1,3,0:T(2,128)S(1)}, f32[10,2,2,4,128]{4,2,1,3,0:T(2,128)S(1)}, u32[]{:S(2)}, u32[]{:S(2)}) collective-permute-start(f32[10,2,2,4,128]{4,2,1,3,0:T(2,128)S(1)} %pad_maximum_fusion.52), channel_id=1, source_target_pairs={{0,8},{8,16},{16,24},{24,0},{1,9},{9,17},{17,25},{25,1},{2,10},{10... | collective-permute-start | bytes 245768 | tf_op jit(solution)/shard_map/ppermute | solution.py:24
  28.7 9.8 %collective-permute-start.11 = (f32[10,2,2,4,128]{4,2,1,3,0:T(2,128)S(1)}, f32[10,2,2,4,128]{4,2,1,3,0:T(2,128)S(1)}, u32[]{:S(2)}, u32[]{:S(2)}) collective-permute-start(f32[10,2,2,4,128]{4,2,1,3,0:T(2,128)S(1)} %pad_maximum_fusion.52), channel_id=1, source_target_pairs={{0,16},{8,24},{16,0},{24,8},{1,17},{9,25},{17,1},{25,9},{2,18},{10... | collective-permute-start | bytes 245768 | tf_op jit(solution)/shard_map/ppermute | solution.py:24
  29.6 8.8 %collective-permute-start.10 = (f32[10,2,2,4,128]{4,2,1,3,0:T(2,128)S(1)}, f32[10,2,2,4,128]{4,2,1,3,0:T(2,128)S(1)}, u32[]{:S(2)}, u32[]{:S(2)}) collective-permute-start(f32[10,2,2,4,128]{4,2,1,3,0:T(2,128)S(1)} %pad_maximum_fusion.52), channel_id=1, source_target_pairs={{0,24},{8,0},{16,8},{24,16},{1,25},{9,1},{17,9},{25,17},{2,26},{10... | collective-permute-start | bytes 245768 | tf_op jit(solution)/shard_map/ppermute | solution.py:24
  35.9 7.5 %copy-start.15 = (f32[2,2,2,4,128]{4,2,1,3,0:T(2,128)}, f32[2,2,2,4,128]{4,2,1,3,0:T(2,128)S(1)}, u32[]{:S(2)}) copy-start(f32[2,2,2,4,128]{4,2,1,3,0:T(2,128)S(1)} %slice.315) | copy-start | bytes 49156
  38.5 4.9 %copy-start.16 = (f32[2,2,2,4,128]{4,2,1,3,0:T(2,128)}, f32[2,2,2,4,128]{4,2,1,3,0:T(2,128)S(1)}, u32[]{:S(2)}) copy-start(f32[2,2,2,4,128]{4,2,1,3,0:T(2,128)S(1)} %slice.314) | copy-start | bytes 49156
  38.5 4.9 %copy-start.17 = (f32[2,2,2,4,128]{4,2,1,3,0:T(2,128)}, f32[2,2,2,4,128]{4,2,1,3,0:T(2,128)S(1)}, u32[]{:S(2)}) copy-start(f32[2,2,2,4,128]{4,2,1,3,0:T(2,128)S(1)} %slice.313) | copy-start | bytes 49156
  39.2 4.9 %collective-permute-start.19 = (f32[8,2,2,4,128]{4,2,1,3,0:T(2,128)}, f32[8,2,2,4,128]{4,2,1,3,0:T(2,128)S(1)}, u32[]{:S(2)}, u32[]{:S(2)}) collective-permute-start(f32[8,2,2,4,128]{4,2,1,3,0:T(2,128)} %pad_maximum_fusion.54), channel_id=1, source_target_pairs={{7,0},{4,1},{5,2},{6,3},{3,4},{0,5},{1,6},{2,7},{15,8},{12,9},{13,... | collective-permute-start | bytes 196616 | tf_op jit(solution)/shard_map/ppermute | solution.py:108
  39.2 6.2 %collective-permute-start.18 = (f32[8,2,2,4,128]{4,2,1,3,0:T(2,128)}, f32[8,2,2,4,128]{4,2,1,3,0:T(2,128)S(1)}, u32[]{:S(2)}, u32[]{:S(2)}) collective-permute-start(f32[8,2,2,4,128]{4,2,1,3,0:T(2,128)} %pad_maximum_fusion.54), channel_id=1, source_target_pairs={{6,0},{7,1},{4,2},{5,3},{2,4},{3,5},{0,6},{1,7},{14,8},{15,9},{12,... | collective-permute-start | bytes 196616 | tf_op jit(solution)/shard_map/ppermute | solution.py:108
  40.5 10.0 %collective-permute-start.17 = (f32[8,2,2,4,128]{4,2,1,3,0:T(2,128)}, f32[8,2,2,4,128]{4,2,1,3,0:T(2,128)}, u32[]{:S(2)}, u32[]{:S(2)}) collective-permute-start(f32[8,2,2,4,128]{4,2,1,3,0:T(2,128)} %pad_maximum_fusion.54), channel_id=1, source_target_pairs={{5,0},{6,1},{7,2},{4,3},{1,4},{2,5},{3,6},{0,7},{13,8},{14,9},{15,... | collective-permute-start | bytes 196616 | tf_op jit(solution)/shard_map/ppermute | solution.py:108
  42.9 7.7 %collective-permute-start.16 = (f32[8,2,2,4,128]{4,2,1,3,0:T(2,128)}, f32[8,2,2,4,128]{4,2,1,3,0:T(2,128)}, u32[]{:S(2)}, u32[]{:S(2)}) collective-permute-start(f32[8,2,2,4,128]{4,2,1,3,0:T(2,128)} %pad_maximum_fusion.54), channel_id=1, source_target_pairs={{4,0},{5,1},{6,2},{7,3},{0,4},{1,5},{2,6},{3,7},{12,8},{13,9},{14,... | collective-permute-start | bytes 196616 | tf_op jit(solution)/shard_map/ppermute | solution.py:108
  43.4 7.2 %collective-permute-start.15 = (f32[8,2,2,4,128]{4,2,1,3,0:T(2,128)}, f32[8,2,2,4,128]{4,2,1,3,0:T(2,128)}, u32[]{:S(2)}, u32[]{:S(2)}) collective-permute-start(f32[8,2,2,4,128]{4,2,1,3,0:T(2,128)} %pad_maximum_fusion.54), channel_id=1, source_target_pairs={{3,0},{0,1},{1,2},{2,3},{7,4},{4,5},{5,6},{6,7},{11,8},{8,9},{9,10... | collective-permute-start | bytes 196616 | tf_op jit(solution)/shard_map/ppermute | solution.py:108
  44.1 3.1 %copy-start.22 = (f32[8,2,2,4,128]{4,2,1,3,0:T(2,128)}, f32[8,2,2,4,128]{4,2,1,3,0:T(2,128)S(1)}, u32[]{:S(2)}) copy-start(f32[8,2,2,4,128]{4,2,1,3,0:T(2,128)S(1)} %collective-permute-done.19) | copy-start | bytes 196612
  44.1 6.5 %collective-permute-start.14 = (f32[8,2,2,4,128]{4,2,1,3,0:T(2,128)}, f32[8,2,2,4,128]{4,2,1,3,0:T(2,128)}, u32[]{:S(2)}, u32[]{:S(2)}) collective-permute-start(f32[8,2,2,4,128]{4,2,1,3,0:T(2,128)} %pad_maximum_fusion.54), channel_id=1, source_target_pairs={{2,0},{3,1},{0,2},{1,3},{6,4},{7,5},{4,6},{5,7},{10,8},{11,9},{8,1... | collective-permute-start | bytes 196616 | tf_op jit(solution)/shard_map/ppermute | solution.py:108
  45.3 5.2 %collective-permute-start.13 = (f32[8,2,2,4,128]{4,2,1,3,0:T(2,128)}, f32[8,2,2,4,128]{4,2,1,3,0:T(2,128)}, u32[]{:S(2)}, u32[]{:S(2)}) collective-permute-start(f32[8,2,2,4,128]{4,2,1,3,0:T(2,128)} %pad_maximum_fusion.54), channel_id=1, source_target_pairs={{1,0},{2,1},{3,2},{0,3},{5,4},{6,5},{7,6},{4,7},{9,8},{10,9},{11,1... | collective-permute-start | bytes 196616 | tf_op jit(solution)/shard_map/ppermute | solution.py:108
  50.5 1.9 %copy-start.4 = (f32[6,1,4,4,128]{4,2,3,1,0:T(4,128)S(1)}, f32[6,1,4,4,128]{4,2,3,1,0:T(4,128)}, u32[]{:S(2)}) copy-start(f32[6,1,4,4,128]{4,2,3,1,0:T(4,128)} %copy-done.3) | copy-start | bytes 147460
  50.5 1.9 %copy-start.6 = (f32[6,1,4,4,128]{4,2,3,1,0:T(4,128)S(1)}, f32[6,1,4,4,128]{4,2,3,1,0:T(4,128)}, u32[]{:S(2)}) copy-start(f32[6,1,4,4,128]{4,2,3,1,0:T(4,128)} %copy-done.5) | copy-start | bytes 147460
  50.5 1.9 %copy-start.12 = (f32[1,4,4,4,128]{4,2,3,1,0:T(4,128)S(1)}, f32[1,4,4,4,128]{4,2,3,1,0:T(4,128)}, u32[]{:S(2)}) copy-start(f32[1,4,4,4,128]{4,2,3,1,0:T(4,128)} %copy-done.11) | copy-start | bytes 98308
  50.5 1.9 %copy-start.14 = (f32[1,4,4,4,128]{4,2,3,1,0:T(4,128)S(1)}, f32[1,4,4,4,128]{4,2,3,1,0:T(4,128)}, u32[]{:S(2)}) copy-start(f32[1,4,4,4,128]{4,2,3,1,0:T(4,128)} %copy-done.13) | copy-start | bytes 98308
  52.9 5.9 %collective-permute-start.24 = (f32[4,4,1,4,128]{4,2,3,1,0:T(1,128)S(1)}, f32[4,4,1,4,128]{4,2,3,1,0:T(1,128)S(1)}, u32[]{:S(2)}, u32[]{:S(2)}) collective-permute-start(f32[4,4,1,4,128]{4,2,3,1,0:T(1,128)S(1)} %get-tuple-element.18), channel_id=1, source_target_pairs={{0,1},{1,2},{2,3},{3,0},{4,5},{5,6},{6,7},{7,4},{8,9},{9,10},{10,1... | collective-permute-start | bytes 98312 | tf_op jit(solution)/shard_map/ppermute | solution.py:24
  53.0 9.7 %collective-permute-start.22 = (f32[4,2,4,4,128]{4,2,3,1,0:T(4,128)S(1)}, f32[4,2,4,4,128]{4,2,3,1,0:T(4,128)S(1)}, u32[]{:S(2)}, u32[]{:S(2)}) collective-permute-start(f32[4,2,4,4,128]{4,2,3,1,0:T(4,128)S(1)} %pad_maximum_fusion.55), channel_id=1, source_target_pairs={{0,4},{4,0},{1,5},{5,1},{2,6},{6,2},{3,7},{7,3},{8,12},{12,8},{9,1... | collective-permute-start | bytes 196616 | tf_op jit(solution)/shard_map/ppermute | solution.py:37
  54.6 4.4 %collective-permute-start.20 = (f32[1,4,4,4,128]{4,2,3,1,0:T(4,128)S(1)}, f32[1,4,4,4,128]{4,2,3,1,0:T(4,128)S(1)}, u32[]{:S(2)}, u32[]{:S(2)}) collective-permute-start(f32[1,4,4,4,128]{4,2,3,1,0:T(4,128)S(1)} %get-tuple-element.20), channel_id=1, source_target_pairs={{0,24},{8,0},{16,8},{24,16},{1,25},{9,1},{17,9},{25,17},{2,26},{10... | collective-permute-start | bytes 98312 | tf_op jit(solution)/shard_map/ppermute | solution.py:24
  56.7 5.7 %collective-permute-start.21 = (f32[1,4,4,4,128]{4,2,3,1,0:T(4,128)S(1)}, f32[1,4,4,4,128]{4,2,3,1,0:T(4,128)S(1)}, u32[]{:S(2)}, u32[]{:S(2)}) collective-permute-start(f32[1,4,4,4,128]{4,2,3,1,0:T(4,128)S(1)} %get-tuple-element.19), channel_id=1, source_target_pairs={{0,8},{8,16},{16,24},{24,0},{1,9},{9,17},{17,25},{25,1},{2,10},{10... | collective-permute-start | bytes 98312 | tf_op jit(solution)/shard_map/ppermute | solution.py:24
  56.7 5.8 %collective-permute-start.23 = (f32[4,4,1,4,128]{4,2,3,1,0:T(1,128)S(1)}, f32[4,4,1,4,128]{4,2,3,1,0:T(1,128)S(1)}, u32[]{:S(2)}, u32[]{:S(2)}) collective-permute-start(f32[4,4,1,4,128]{4,2,3,1,0:T(1,128)S(1)} %get-tuple-element.17), channel_id=1, source_target_pairs={{0,3},{1,0},{2,1},{3,2},{4,7},{5,4},{6,5},{7,6},{8,11},{9,8},{10,9... | collective-permute-start | bytes 98312 | tf_op jit(solution)/shard_map/ppermute | solution.py:24
  58.8 3.7 %copy-start.2 = (f32[1,8,8,4,128]{4,2,3,1,0:T(8,128)S(1)}, f32[1,8,8,4,128]{4,2,3,1,0:T(8,128)}, u32[]{:S(2)}) copy-start(f32[1,8,8,4,128]{4,2,3,1,0:T(8,128)} %copy-done.1) | copy-start | bytes 393220
  (1 other events, 1.8 us)

commit v19 on v14

--- a/solution.py
+++ b/solution.py
@@ -172,9 +172,12 @@
 
 
 def restrict(field):
-    size_a, size_b, size_c = field.shape[:3]
-    rest = field.shape[3:]
-    return field.reshape((size_a // 2, 2, size_b // 2, 2, size_c // 2, 2) + rest).mean(axis=(1, 3, 5))
+    for dim in range(3):
+        size = field.shape[dim]
+        even = lax.slice_in_dim(field, 0, size, stride=2, axis=dim)
+        odd = lax.slice_in_dim(field, 1, size, stride=2, axis=dim)
+        field = even + odd
+    return field * 0.125
 
 
 def prolong(field):

time: 66.6 us -> 66.4 us (level)
  other arithmetic: 11.1 us -> 7.7 us
  local copies, waits for them, and re-layouts: 6.36 us -> 8.42 us
  waiting for transfers between devices: 17.7 us -> 18.8 us
    slice x0 -> x4, local copies, waits for them, and re-layouts: none -> 1.33 us  [the longest x2 0.67 us: restrict(): even = lax.slice_in_dim(field, 0, size, stride=2, axis=dim)]
    unnamed x49 -> x53, local copies, waits for them, and re-layouts: 0.19 us -> 1.46 us
    ppermute x15, waiting for transfers between devices: 16.7 us -> 17.6 us  [shifted(): lax.ppermute(block, axis, [(j, (j - step) % count) for j in range(count)])]
    add x2, other arithmetic: 1.06 us -> 0.16 us  [post_smooth(): hi = corr_faces[dim][1] + prolong_face(coarse_face_list[dim][1], dim)]
    sub x1, other arithmetic: 1.86 us -> 0.96 us  [vcycle(): rhs_one = restrict(rhs_zero - stencil(corr_zero, faces_zero, 0))]
    div x3, other arithmetic: 2.46 us -> 1.57 us  [vcycle(): omega * part.astype(jnp.float32) / center]
    reduce_sum x2 -> x0, other arithmetic: 0.8 us -> none  [restrict(): field.reshape((size_a // 2, 2, size_b // 2, 2, size_c // 2, 2) + rest)]
  transfers between devices with their start and end apart: 25 -> 25, of which waited for: 9 -> 9; matrix products, arithmetic and copies ran while one was open for 15% -> 11% of each run, Pallas kernels for 0% -> 0%
where the time goes in v19:
time: 66.4 us; the launch traced here: 66.2 us
  starting transfers between devices  26.6 us (40%)
  waiting for transfers between devices  18.8 us (28%)
  local copies, waits for them, and re-layouts  8.42 us (13%)
  other arithmetic  7.7 us (12%)
  matrix products  3.72 us (6%)
  between operations  1.07 us (2%)
    ppermute x15, waiting for transfers between devices, shifted(): lax.ppermute(block, axis, [(j, (j - step) % count) for j in range(count)])  17.6 us
    ppermute x15, starting transfers between devices, shifted(): lax.ppermute(block, axis, [(j, (j - step) % count) for j in range(count)])  15 us
    ppermute x7, starting transfers between devices, fetch(): cache[steps] = lax.ppermute(block, tuple(axes), pairs)  6.86 us
    ppermute x3, starting transfers between devices, axis_faces(): lax.ppermute(jnp.concatenate([first, last], axis=dim), axis, [(0, 1), (1,...  4.75 us
    dot_general x1, matrix products, coarse_solve(): jnp.einsum('qxyz,xyzgl->qgl', operator, extended, precision=lax.Precision...  1.92 us
    dot_general x1, matrix products, body(): jnp.dot(rows, gram, precision=lax.Precision.HIGH, preferred_element_type=...  1.8 us
    reduce_sum x1, local copies, waits for them, and re-layouts, gram_matrix(): return spread.sum(axis=0).reshape(orb_count, orb_count)  1.7 us
    reshape x1, local copies, waits for them, and re-layouts, gram_matrix(): return spread.sum(axis=0).reshape(orb_count, orb_count)  1.64 us
  transfers between devices with their start and end apart: 25, of which 9 were waited for; matrix products, arithmetic and copies ran while one was open for 11% of the time, Pallas kernels for 0%

profile of v19, /device:TPU:0, one launch (start us, length us, event | category | flops | bytes accessed | tf_op | source)
XLA Modules:
  0.0 66.2 jit_solution(8320753241461590936)
XLA Ops:
  0.0 1.5 %fusion.57 = (f32[8,8,1,4,128]{4,2,1,3,0:T(1,128)S(1)}, f32[8,8,1,4,128]{4,2,1,3,0:T(1,128)S(1)}) fusion(bf16[8,8,8,512]{3,2,1,0:T(8,128)(2,1)} %param.5), kind=kLoop, calls=%fused_computation.135 | loop fusion | flops 131072 | bytes 786432 | tf_op jit(solution)/shard_map/div | solution.py:314
  1.6 0.5 collective-permute-start.4
  2.2 2.6 %collective-permute-start.2 = (f32[8,2,8,4,128]{4,2,1,3,0:T(8,128)S(1)}, f32[8,2,8,4,128]{4,2,1,3,0:T(8,128)S(1)}, u32[]{:S(2)}, u32[]{:S(2)}) collective-permute-start(f32[8,2,8,4,128]{4,2,1,3,0:T(8,128)S(1)} %pad_maximum_fusion.32), channel_id=1, source_target_pairs={{0,4},{4,0},{1,5},{5,1},{2,6},{6,2},{3,7},{7,3},{8,12},{12,8},{9,1... | collective-permute-start | bytes 786440 | tf_op jit(solution)/shard_map/ppermute | solution.py:37
  4.8 3.7 %collective-permute-start = (f32[1,8,8,4,128]{4,2,1,3,0:T(8,128)S(1)}, f32[1,8,8,4,128]{4,2,1,3,0:T(8,128)S(1)}, u32[]{:S(2)}, u32[]{:S(2)}) collective-permute-start(f32[1,8,8,4,128]{4,2,1,3,0:T(8,128)S(1)} %copy.38), channel_id=1, source_target_pairs={{0,24},{8,0},{16,8},{24,16},{1,25},{9,1},{17,9},{25,17},{2,26},{10... | collective-permute-start | bytes 393224 | tf_op jit(solution)/shard_map/ppermute | solution.py:24
  8.6 1.2 %collective-permute-start.3 = (f32[8,8,1,4,128]{4,2,1,3,0:T(1,128)S(1)}, f32[8,8,1,4,128]{4,2,1,3,0:T(1,128)S(1)}, u32[]{:S(2)}, u32[]{:S(2)}) collective-permute-start(f32[8,8,1,4,128]{4,2,1,3,0:T(1,128)S(1)} %get-tuple-element.7), channel_id=1, source_target_pairs={{0,3},{1,0},{2,1},{3,2},{4,7},{5,4},{6,5},{7,6},{8,11},{9,8},{10,9... | collective-permute-start | bytes 393224 | tf_op jit(solution)/shard_map/ppermute | solution.py:24
  10.1 0.6 gather_fusion
  11.3 0.7 %fusion.58 = (f32[4,4]{1,0:T(4,128)}, f32[4,4]{1,0:T(4,128)}) fusion(s32[4]{0:T(128)S(1)} %get-tuple-element.5, s32[4]{0:T(128)S(1)} %get-tuple-element.6), kind=kLoop, calls=%fused_computation.164 | loop fusion | flops 64 | bytes 160 | tf_op jit(solution)/shard_map/convert_element_type | solution.py:306
  12.2 4.4 %collective-permute-done.1 = f32[1,8,8,4,128]{4,2,1,3,0:T(8,128)S(1)} collective-permute-done((f32[1,8,8,4,128]{4,2,1,3,0:T(8,128)S(1)}, f32[1,8,8,4,128]{4,2,1,3,0:T(8,128)S(1)}, u32[]{:S(2)}, u32[]{:S(2)}) %collective-permute-start.1) | collective-permute-done | bytes 131104 | tf_op jit(solution)/shard_map/ppermute | solution.py:24
  16.7 1.0 %convert_subtract_fusion.1 = f32[8,8,8,4,128]{4,2,1,3,0:T(8,128)S(1)} fusion(f32[8,8,1,4,128]{4,2,1,3,0:T(1,128)S(1)} %collective-permute-done.4, f32[10,1,8,4,128]{4,2,1,3,0:T(8,128)S(1)} %pad.40, f32[10,1,8,4,128]{4,2,1,3,0:T(8,128)S(1)} %pad.41, f32[1,8,8,4,128]{4,2,1,3,0:T(8,128)S(1)} %collective-permute-done, ...), kind=kLoop, calls=%fused_computation.3 | loop fusion | flops 8912896 | bytes 3473408 | tf_op jit(solution)/shard_map/sub | solution.py:317
  17.8 0.4 slice.285
  18.2 0.4 slice.286
  18.9 0.6 collective-permute-start.6
  19.5 0.2 collective-permute-start.5
  19.7 1.5 %collective-permute-start.8 = (f32[1,4,4,4,128]{4,2,1,3,0:T(4,128)S(1)}, f32[1,4,4,4,128]{4,2,1,3,0:T(4,128)S(1)}, u32[]{:S(2)}, u32[]{:S(2)}) collective-permute-start(f32[1,4,4,4,128]{4,2,1,3,0:T(4,128)S(1)} %get-tuple-element.26), channel_id=1, source_target_pairs={{0,24},{8,0},{16,8},{24,16},{1,25},{9,1},{17,9},{25,17},{2,26},{10... | collective-permute-start | bytes 98312 | tf_op jit(solution)/shard_map/ppermute | solution.py:24
  21.2 0.6 collective-permute-start.7
  21.8 1.1 %collective-permute-done.5 = f32[4,4,1,4,128]{4,2,1,3,0:T(1,128)S(1)} collective-permute-done((f32[4,4,1,4,128]{4,2,1,3,0:T(1,128)S(1)}, f32[4,4,1,4,128]{4,2,1,3,0:T(1,128)S(1)}, u32[]{:S(2)}, u32[]{:S(2)}) %collective-permute-start.5) | collective-permute-done | bytes 32800 | tf_op jit(solution)/shard_map/ppermute | solution.py:24
  22.9 0.6 collective-permute-done.6
  23.6 3.3 %collective-permute-done.7 = f32[1,4,4,4,128]{4,2,1,3,0:T(4,128)S(1)} collective-permute-done((f32[1,4,4,4,128]{4,2,1,3,0:T(4,128)S(1)}, f32[1,4,4,4,128]{4,2,1,3,0:T(4,128)S(1)}, u32[]{:S(2)}, u32[]{:S(2)}) %collective-permute-start.7) | collective-permute-done | bytes 32800 | tf_op jit(solution)/shard_map/ppermute | solution.py:24
  26.9 0.2 fusion.51
  27.2 0.2 slice.305
  27.4 0.2 slice.306
  27.8 0.7 %collective-permute-start.11 = (f32[10,2,2,4,128]{4,2,1,3,0:T(2,128)S(1)}, f32[10,2,2,4,128]{4,2,1,3,0:T(2,128)S(1)}, u32[]{:S(2)}, u32[]{:S(2)}) collective-permute-start(f32[10,2,2,4,128]{4,2,1,3,0:T(2,128)S(1)} %pad_maximum_fusion.52), channel_id=1, source_target_pairs={{0,16},{8,24},{16,0},{24,8},{1,17},{9,25},{17,1},{25,9},{2,18},{10... | collective-permute-start | bytes 245768 | tf_op jit(solution)/shard_map/ppermute | solution.py:24
  28.5 3.1 %collective-permute-start.10 = (f32[10,2,2,4,128]{4,2,1,3,0:T(2,128)S(1)}, f32[10,2,2,4,128]{4,2,1,3,0:T(2,128)S(1)}, u32[]{:S(2)}, u32[]{:S(2)}) collective-permute-start(f32[10,2,2,4,128]{4,2,1,3,0:T(2,128)S(1)} %pad_maximum_fusion.52), channel_id=1, source_target_pairs={{0,24},{8,0},{16,8},{24,16},{1,25},{9,1},{17,9},{25,17},{2,26},{10... | collective-permute-start | bytes 245768 | tf_op jit(solution)/shard_map/ppermute | solution.py:24
  31.7 3.3 %collective-permute-done.12 = f32[10,2,2,4,128]{4,2,1,3,0:T(2,128)S(1)} collective-permute-done((f32[10,2,2,4,128]{4,2,1,3,0:T(2,128)S(1)}, f32[10,2,2,4,128]{4,2,1,3,0:T(2,128)S(1)}, u32[]{:S(2)}, u32[]{:S(2)}) %collective-permute-start.12) | collective-permute-done | bytes 81952 | tf_op jit(solution)/shard_map/ppermute | solution.py:24
  35.0 2.6 %collective-permute-done.11 = f32[10,2,2,4,128]{4,2,1,3,0:T(2,128)S(1)} collective-permute-done((f32[10,2,2,4,128]{4,2,1,3,0:T(2,128)S(1)}, f32[10,2,2,4,128]{4,2,1,3,0:T(2,128)S(1)}, u32[]{:S(2)}, u32[]{:S(2)}) %collective-permute-start.11) | collective-permute-done | bytes 81952 | tf_op jit(solution)/shard_map/ppermute | solution.py:24
  37.6 0.6 pad_maximum_fusion.54
  38.3 1.3 %collective-permute-start.18 = (f32[8,2,2,4,128]{4,2,1,3,0:T(2,128)}, f32[8,2,2,4,128]{4,2,1,3,0:T(2,128)S(1)}, u32[]{:S(2)}, u32[]{:S(2)}) collective-permute-start(f32[8,2,2,4,128]{4,2,1,3,0:T(2,128)} %pad_maximum_fusion.54), channel_id=1, source_target_pairs={{6,0},{7,1},{4,2},{5,3},{2,4},{3,5},{0,6},{1,7},{14,8},{15,9},{12,... | collective-permute-start | bytes 196616 | tf_op jit(solution)/shard_map/ppermute | solution.py:108
  39.6 2.4 %collective-permute-start.17 = (f32[8,2,2,4,128]{4,2,1,3,0:T(2,128)}, f32[8,2,2,4,128]{4,2,1,3,0:T(2,128)}, u32[]{:S(2)}, u32[]{:S(2)}) collective-permute-start(f32[8,2,2,4,128]{4,2,1,3,0:T(2,128)} %pad_maximum_fusion.54), channel_id=1, source_target_pairs={{5,0},{6,1},{7,2},{4,3},{1,4},{2,5},{3,6},{0,7},{13,8},{14,9},{15,... | collective-permute-start | bytes 196616 | tf_op jit(solution)/shard_map/ppermute | solution.py:108
  42.0 0.5 collective-permute-start.16
  42.7 0.5 collective-permute-done.19
  43.2 1.2 %collective-permute-start.14 = (f32[8,2,2,4,128]{4,2,1,3,0:T(2,128)}, f32[8,2,2,4,128]{4,2,1,3,0:T(2,128)}, u32[]{:S(2)}, u32[]{:S(2)}) collective-permute-start(f32[8,2,2,4,128]{4,2,1,3,0:T(2,128)} %pad_maximum_fusion.54), channel_id=1, source_target_pairs={{2,0},{3,1},{0,2},{1,3},{6,4},{7,5},{4,6},{5,7},{10,8},{11,9},{8,1... | collective-permute-start | bytes 196616 | tf_op jit(solution)/shard_map/ppermute | solution.py:108
  44.4 0.6 copy-done.25
  45.0 1.4 %collective-permute-start.13 = (f32[8,2,2,4,128]{4,2,1,3,0:T(2,128)}, f32[8,2,2,4,128]{4,2,1,3,0:T(2,128)}, u32[]{:S(2)}, u32[]{:S(2)}) collective-permute-start(f32[8,2,2,4,128]{4,2,1,3,0:T(2,128)} %pad_maximum_fusion.54), channel_id=1, source_target_pairs={{1,0},{2,1},{3,2},{0,3},{5,4},{6,5},{7,6},{4,7},{9,8},{10,9},{11,1... | collective-permute-start | bytes 196616 | tf_op jit(solution)/shard_map/ppermute | solution.py:108
  46.4 0.4 multiply_reduce_fusion
  46.9 1.7 %copy.52 = f32[4,128,4,128]{3,2,1,0:T(4,128)} copy(f32[4,128,4,128]{3,1,2,0:T(8,128)S(1)} %multiply_reduce_fusion) | data formatting | bytes 2097152 | tf_op jit(solution)/shard_map/reduce_sum | solution.py:309
  48.6 1.6 %reshape.595 = f32[512,512,1,1]{1,0,2,3:T(8,128)S(1)} reshape(f32[4,128,4,128]{3,2,1,0:T(4,128)} %copy.52) | data formatting | bytes 2097152 | tf_op jit(solution)/shard_map/reshape | solution.py:309
  50.3 1.9 %convolution_bitcast_fusion = f32[216,4,128]{2,0,1:T(8,128)S(1)} fusion(f32[216,8,4,8,1]{0,3,2,4,1:T(8,128)} %constant.134, f32[8,2,2,4,128]{4,2,1,3,0:T(2,128)} %copy-done.24, f32[8,2,2,4,128]{4,2,1,3,0:T(2,128)} %copy-done.25, f32[8,2,2,4,128]{4,2,1,3,0:T(2,128)} %collective-permute-done.17, f32[8,2,2,4,128]{4,2,1,3,0:T(2,128)} %collective-permute-done.16, ...), kind=kOutput, calls=%fused_computation.7 | convolution fusion | flops 341049344 | bytes 1187840 | tf_op jit(solution)/shard_map/qxyz,xyzgl->qgl/dot_general | solution.py:198
  52.4 0.2 maximum_add_fusion
  52.6 0.2 fusion.47
  53.0 1.6 %collective-permute-start.22 = (f32[4,2,4,4,128]{4,2,1,3,0:T(4,128)S(1)}, f32[4,2,4,4,128]{4,2,1,3,0:T(4,128)S(1)}, u32[]{:S(2)}, u32[]{:S(2)}) collective-permute-start(f32[4,2,4,4,128]{4,2,1,3,0:T(4,128)S(1)} %pad_maximum_fusion.55), channel_id=1, source_target_pairs={{0,4},{4,0},{1,5},{5,1},{2,6},{6,2},{3,7},{7,3},{8,12},{12,8},{9,1... | collective-permute-start | bytes 196616 | tf_op jit(solution)/shard_map/ppermute | solution.py:37
  54.6 2.1 %collective-permute-start.20 = (f32[1,4,4,4,128]{4,2,1,3,0:T(4,128)S(1)}, f32[1,4,4,4,128]{4,2,1,3,0:T(4,128)S(1)}, u32[]{:S(2)}, u32[]{:S(2)}) collective-permute-start(f32[1,4,4,4,128]{4,2,1,3,0:T(4,128)S(1)} %get-tuple-element.20), channel_id=1, source_target_pairs={{0,24},{8,0},{16,8},{24,16},{1,25},{9,1},{17,9},{25,17},{2,26},{10... | collective-permute-start | bytes 98312 | tf_op jit(solution)/shard_map/ppermute | solution.py:24
  56.7 1.2 %collective-permute-start.23 = (f32[4,4,1,4,128]{4,2,1,3,0:T(1,128)S(1)}, f32[4,4,1,4,128]{4,2,1,3,0:T(1,128)S(1)}, u32[]{:S(2)}, u32[]{:S(2)}) collective-permute-start(f32[4,4,1,4,128]{4,2,1,3,0:T(1,128)S(1)} %get-tuple-element.17), channel_id=1, source_target_pairs={{0,3},{1,0},{2,1},{3,2},{4,7},{5,4},{6,5},{7,6},{8,11},{9,8},{10,9... | collective-permute-start | bytes 98312 | tf_op jit(solution)/shard_map/ppermute | solution.py:24
  58.0 0.4 broadcast_in_dim.88
  58.6 0.6 copy-done.2
  59.5 2.9 %collective-permute-done.21 = f32[1,4,4,4,128]{4,2,1,3,0:T(4,128)S(1)} collective-permute-done((f32[1,4,4,4,128]{4,2,1,3,0:T(4,128)S(1)}, f32[1,4,4,4,128]{4,2,1,3,0:T(4,128)S(1)}, u32[]{:S(2)}, u32[]{:S(2)}) %collective-permute-start.21) | collective-permute-done | bytes 32800 | tf_op jit(solution)/shard_map/ppermute | solution.py:24
  63.0 1.0 %fusion.2 = f32[8,8,8,4,128]{4,2,1,3,0:T(8,128)S(1)} fusion(f32[8,8,8,4,128]{4,2,1,3,0:T(8,128)S(1)} %fusion.42, f32[8,8,1,4,128]{4,2,1,3,0:T(1,128)S(1)} %add.239, f32[10,1,8,4,128]{4,2,1,3,0:T(8,128)S(1)} %pad.48, f32[10,1,8,4,128]{4,2,1,3,0:T(8,128)S(1)} %pad.49, f32[1,8,8,4,128]{4,2,1,3,0:T(8,128)S(1)} %add.230, f32[1,8,8,4,128]{4,2,1,3,0:T(8,128)S(1)} %add.231, ...), kind=kLoop, calls=%fused_computation.10 | loop fusion | flops 9437184 | bytes 3473408 | tf_op jit(solution)/shard_map/add | solution.py:273
  64.2 0.2 bitcast_multiply_fusion
  64.4 1.8 %convolution_convert_fusion = bf16[8,8,8,512]{3,2,1,0:T(8,128)(2,1)} fusion(f32[8,8,8,512]{3,2,1,0:T(8,128)S(1)} %bitcast.82, f32[512,512,1,1]{1,0,2,3:T(8,128)S(1)} %reshape.595), kind=kOutput, calls=%fused_computation.6 | convolution fusion | flops 805568512 | bytes 2621440 | tf_op jit(solution)/shard_map/dot_general | solution.py:345
  (154 shorter events, 3.5 us)
Async XLA Ops:
  0.0 2.1 %copy-start = (bf16[8,8,8,512]{3,2,1,0:T(8,128)(2,1)S(1)}, bf16[8,8,8,512]{3,2,1,0:T(8,128)(2,1)}, u32[]{:S(2)}) copy-start(bf16[8,8,8,512]{3,2,1,0:T(8,128)(2,1)} %param.5) | copy-start | bytes 1572868
  1.5 8.2 %copy-start.11 = (f32[1,128,128]{2,1,0:T(8,128)S(1)}, f32[1,128,128]{2,1,0:T(8,128)}, u32[]{:S(2)}) copy-start(f32[1,128,128]{2,1,0:T(8,128)} %param.8) | copy-start | bytes 196612
  1.6 8.3 %copy-start.20 = (s32[3,2,512]{2,1,0:T(2,128)S(1)}, s32[3,2,512]{2,1,0:T(2,128)}, u32[]{:S(2)}) copy-start(s32[3,2,512]{2,1,0:T(2,128)} %param.6) | copy-start | bytes 36868
  1.6 10.6 %collective-permute-start.4 = (f32[8,8,1,4,128]{4,2,1,3,0:T(1,128)S(1)}, f32[8,8,1,4,128]{4,2,1,3,0:T(1,128)S(1)}, u32[]{:S(2)}, u32[]{:S(2)}) collective-permute-start(f32[8,8,1,4,128]{4,2,1,3,0:T(1,128)S(1)} %get-tuple-element.8), channel_id=1, source_target_pairs={{0,1},{1,2},{2,3},{3,0},{4,5},{5,6},{6,7},{7,4},{8,9},{9,10},{10,1... | collective-permute-start | bytes 393224 | tf_op jit(solution)/shard_map/ppermute | solution.py:24
  2.1 7.7 %copy-start.23 = (s32[4,2]{0,1:T(2,128)S(1)}, s32[4,2]{0,1:T(2,128)}, u32[]{:S(2)}) copy-start(s32[4,2]{0,1:T(2,128)} %param.7) | copy-start | bytes 100
  2.2 9.9 %collective-permute-start.2 = (f32[8,2,8,4,128]{4,2,1,3,0:T(8,128)S(1)}, f32[8,2,8,4,128]{4,2,1,3,0:T(8,128)S(1)}, u32[]{:S(2)}, u32[]{:S(2)}) collective-permute-start(f32[8,2,8,4,128]{4,2,1,3,0:T(8,128)S(1)} %pad_maximum_fusion.32), channel_id=1, source_target_pairs={{0,4},{4,0},{1,5},{5,1},{2,6},{6,2},{3,7},{7,3},{8,12},{12,8},{9,1... | collective-permute-start | bytes 786440 | tf_op jit(solution)/shard_map/ppermute | solution.py:37
  4.8 7.4 %collective-permute-start = (f32[1,8,8,4,128]{4,2,1,3,0:T(8,128)S(1)}, f32[1,8,8,4,128]{4,2,1,3,0:T(8,128)S(1)}, u32[]{:S(2)}, u32[]{:S(2)}) collective-permute-start(f32[1,8,8,4,128]{4,2,1,3,0:T(8,128)S(1)} %copy.38), channel_id=1, source_target_pairs={{0,24},{8,0},{16,8},{24,16},{1,25},{9,1},{17,9},{25,17},{2,26},{10... | collective-permute-start | bytes 393224 | tf_op jit(solution)/shard_map/ppermute | solution.py:24
  8.5 8.2 %collective-permute-start.1 = (f32[1,8,8,4,128]{4,2,1,3,0:T(8,128)S(1)}, f32[1,8,8,4,128]{4,2,1,3,0:T(8,128)S(1)}, u32[]{:S(2)}, u32[]{:S(2)}) collective-permute-start(f32[1,8,8,4,128]{4,2,1,3,0:T(8,128)S(1)} %copy.39), channel_id=1, source_target_pairs={{0,8},{8,16},{16,24},{24,0},{1,9},{9,17},{17,25},{25,1},{2,10},{10... | collective-permute-start | bytes 393224 | tf_op jit(solution)/shard_map/ppermute | solution.py:24
  8.6 8.1 %collective-permute-start.3 = (f32[8,8,1,4,128]{4,2,1,3,0:T(1,128)S(1)}, f32[8,8,1,4,128]{4,2,1,3,0:T(1,128)S(1)}, u32[]{:S(2)}, u32[]{:S(2)}) collective-permute-start(f32[8,8,1,4,128]{4,2,1,3,0:T(1,128)S(1)} %get-tuple-element.7), channel_id=1, source_target_pairs={{0,3},{1,0},{2,1},{3,2},{4,7},{5,4},{6,5},{7,6},{8,11},{9,8},{10,9... | collective-permute-start | bytes 393224 | tf_op jit(solution)/shard_map/ppermute | solution.py:24
  12.2 5.4 %copy-start.1 = (f32[8,8,1,4,128]{4,2,1,3,0:T(1,128)}, f32[8,8,1,4,128]{4,2,1,3,0:T(1,128)S(1)}, u32[]{:S(2)}) copy-start(f32[8,8,1,4,128]{4,2,1,3,0:T(1,128)S(1)} %collective-permute-done.4) | copy-start | bytes 393220
  12.2 5.4 %copy-start.5 = (f32[1,8,8,4,128]{4,2,1,3,0:T(8,128)}, f32[1,8,8,4,128]{4,2,1,3,0:T(8,128)S(1)}, u32[]{:S(2)}) copy-start(f32[1,8,8,4,128]{4,2,1,3,0:T(8,128)S(1)} %collective-permute-done) | copy-start | bytes 393220
  16.7 1.0 %copy-start.3 = (f32[1,8,8,4,128]{4,2,1,3,0:T(8,128)}, f32[1,8,8,4,128]{4,2,1,3,0:T(8,128)S(1)}, u32[]{:S(2)}) copy-start(f32[1,8,8,4,128]{4,2,1,3,0:T(8,128)S(1)} %collective-permute-done.1) | copy-start | bytes 393220
  18.8 2.9 %collective-permute-start.9 = (f32[4,4,1,4,128]{4,2,1,3,0:T(1,128)S(1)}, f32[4,4,1,4,128]{4,2,1,3,0:T(1,128)S(1)}, u32[]{:S(2)}, u32[]{:S(2)}) collective-permute-start(f32[4,4,1,4,128]{4,2,1,3,0:T(1,128)S(1)} %get-tuple-element.24), channel_id=1, source_target_pairs={{0,3},{1,0},{2,1},{3,2},{4,7},{5,4},{6,5},{7,6},{8,11},{9,8},{10,9... | collective-permute-start | bytes 98312 | tf_op jit(solution)/shard_map/ppermute | solution.py:24
  18.9 12.7 %copy-start.21 = (f32[4,4]{1,0:T(4,128)S(1)}, f32[4,4]{1,0:T(4,128)}, u32[]{:S(2)}) copy-start(f32[4,4]{1,0:T(4,128)} %get-tuple-element.41) | copy-start | bytes 196
  18.9 12.7 %copy-start.22 = (f32[4,4]{1,0:T(4,128)S(1)}, f32[4,4]{1,0:T(4,128)}, u32[]{:S(2)}) copy-start(f32[4,4]{1,0:T(4,128)} %get-tuple-element.42) | copy-start | bytes 196
  18.9 4.6 %collective-permute-start.6 = (f32[4,2,4,4,128]{4,2,1,3,0:T(4,128)S(1)}, f32[4,2,4,4,128]{4,2,1,3,0:T(4,128)S(1)}, u32[]{:S(2)}, u32[]{:S(2)}) collective-permute-start(f32[4,2,4,4,128]{4,2,1,3,0:T(4,128)S(1)} %pad_maximum_fusion.53), channel_id=1, source_target_pairs={{0,4},{4,0},{1,5},{5,1},{2,6},{6,2},{3,7},{7,3},{8,12},{12,8},{9,1... | collective-permute-start | bytes 196616 | tf_op jit(solution)/shard_map/ppermute | solution.py:37
  19.5 3.4 %collective-permute-start.5 = (f32[4,4,1,4,128]{4,2,1,3,0:T(1,128)S(1)}, f32[4,4,1,4,128]{4,2,1,3,0:T(1,128)S(1)}, u32[]{:S(2)}, u32[]{:S(2)}) collective-permute-start(f32[4,4,1,4,128]{4,2,1,3,0:T(1,128)S(1)} %get-tuple-element.23), channel_id=1, source_target_pairs={{0,1},{1,2},{2,3},{3,0},{4,5},{5,6},{6,7},{7,4},{8,9},{9,10},{10,1... | collective-permute-start | bytes 98312 | tf_op jit(solution)/shard_map/ppermute | solution.py:24
  19.7 3.9 %collective-permute-start.8 = (f32[1,4,4,4,128]{4,2,1,3,0:T(4,128)S(1)}, f32[1,4,4,4,128]{4,2,1,3,0:T(4,128)S(1)}, u32[]{:S(2)}, u32[]{:S(2)}) collective-permute-start(f32[1,4,4,4,128]{4,2,1,3,0:T(4,128)S(1)} %get-tuple-element.26), channel_id=1, source_target_pairs={{0,24},{8,0},{16,8},{24,16},{1,25},{9,1},{17,9},{25,17},{2,26},{10... | collective-permute-start | bytes 98312 | tf_op jit(solution)/shard_map/ppermute | solution.py:24
  21.2 5.7 %collective-permute-start.7 = (f32[1,4,4,4,128]{4,2,1,3,0:T(4,128)S(1)}, f32[1,4,4,4,128]{4,2,1,3,0:T(4,128)S(1)}, u32[]{:S(2)}, u32[]{:S(2)}) collective-permute-start(f32[1,4,4,4,128]{4,2,1,3,0:T(4,128)S(1)} %get-tuple-element.25), channel_id=1, source_target_pairs={{0,8},{8,16},{16,24},{24,0},{1,9},{9,17},{17,25},{25,1},{2,10},{10... | collective-permute-start | bytes 98312 | tf_op jit(solution)/shard_map/ppermute | solution.py:24
  23.5 3.6 %copy-start.7 = (f32[6,1,4,4,128]{4,2,1,3,0:T(4,128)}, f32[6,1,4,4,128]{4,2,1,3,0:T(4,128)S(1)}, u32[]{:S(2)}) copy-start(f32[6,1,4,4,128]{4,2,1,3,0:T(4,128)S(1)} %pad.46) | copy-start | bytes 147460
  23.5 3.6 %copy-start.9 = (f32[6,1,4,4,128]{4,2,1,3,0:T(4,128)}, f32[6,1,4,4,128]{4,2,1,3,0:T(4,128)S(1)}, u32[]{:S(2)}) copy-start(f32[6,1,4,4,128]{4,2,1,3,0:T(4,128)S(1)} %pad.45) | copy-start | bytes 147460
  23.6 3.8 %copy-start.13 = (f32[1,4,4,4,128]{4,2,1,3,0:T(4,128)}, f32[1,4,4,4,128]{4,2,1,3,0:T(4,128)S(1)}, u32[]{:S(2)}) copy-start(f32[1,4,4,4,128]{4,2,1,3,0:T(4,128)S(1)} %collective-permute-done.8) | copy-start | bytes 98308
  26.9 15.6 %copy-start.15 = (f32[1,4,4,4,128]{4,2,1,3,0:T(4,128)}, f32[1,4,4,4,128]{4,2,1,3,0:T(4,128)S(1)}, u32[]{:S(2)}) copy-start(f32[1,4,4,4,128]{4,2,1,3,0:T(4,128)S(1)} %collective-permute-done.7) | copy-start | bytes 98308
  27.7 14.8 %copy-start.12 = (f32[2,2,2,4,128]{4,2,1,3,0:T(2,128)}, f32[2,2,2,4,128]{4,2,1,3,0:T(2,128)S(1)}, u32[]{:S(2)}) copy-start(f32[2,2,2,4,128]{4,2,1,3,0:T(2,128)S(1)} %add_multiply_fusion) | copy-start | bytes 49156
  27.7 7.3 %collective-permute-start.12 = (f32[10,2,2,4,128]{4,2,1,3,0:T(2,128)S(1)}, f32[10,2,2,4,128]{4,2,1,3,0:T(2,128)S(1)}, u32[]{:S(2)}, u32[]{:S(2)}) collective-permute-start(f32[10,2,2,4,128]{4,2,1,3,0:T(2,128)S(1)} %pad_maximum_fusion.52), channel_id=1, source_target_pairs={{0,8},{8,16},{16,24},{24,0},{1,9},{9,17},{17,25},{25,1},{2,10},{10... | collective-permute-start | bytes 245768 | tf_op jit(solution)/shard_map/ppermute | solution.py:24
  27.8 9.8 %collective-permute-start.11 = (f32[10,2,2,4,128]{4,2,1,3,0:T(2,128)S(1)}, f32[10,2,2,4,128]{4,2,1,3,0:T(2,128)S(1)}, u32[]{:S(2)}, u32[]{:S(2)}) collective-permute-start(f32[10,2,2,4,128]{4,2,1,3,0:T(2,128)S(1)} %pad_maximum_fusion.52), channel_id=1, source_target_pairs={{0,16},{8,24},{16,0},{24,8},{1,17},{9,25},{17,1},{25,9},{2,18},{10... | collective-permute-start | bytes 245768 | tf_op jit(solution)/shard_map/ppermute | solution.py:24
  28.5 9.1 %collective-permute-start.10 = (f32[10,2,2,4,128]{4,2,1,3,0:T(2,128)S(1)}, f32[10,2,2,4,128]{4,2,1,3,0:T(2,128)S(1)}, u32[]{:S(2)}, u32[]{:S(2)}) collective-permute-start(f32[10,2,2,4,128]{4,2,1,3,0:T(2,128)S(1)} %pad_maximum_fusion.52), channel_id=1, source_target_pairs={{0,24},{8,0},{16,8},{24,16},{1,25},{9,1},{17,9},{25,17},{2,26},{10... | collective-permute-start | bytes 245768 | tf_op jit(solution)/shard_map/ppermute | solution.py:24
  35.0 7.5 %copy-start.17 = (f32[2,2,2,4,128]{4,2,1,3,0:T(2,128)}, f32[2,2,2,4,128]{4,2,1,3,0:T(2,128)S(1)}, u32[]{:S(2)}) copy-start(f32[2,2,2,4,128]{4,2,1,3,0:T(2,128)S(1)} %slice.363) | copy-start | bytes 49156
  37.6 4.9 %copy-start.18 = (f32[2,2,2,4,128]{4,2,1,3,0:T(2,128)}, f32[2,2,2,4,128]{4,2,1,3,0:T(2,128)S(1)}, u32[]{:S(2)}) copy-start(f32[2,2,2,4,128]{4,2,1,3,0:T(2,128)S(1)} %slice.362) | copy-start | bytes 49156
  37.6 9.2 %copy-start.19 = (f32[2,2,2,4,128]{4,2,1,3,0:T(2,128)}, f32[2,2,2,4,128]{4,2,1,3,0:T(2,128)S(1)}, u32[]{:S(2)}) copy-start(f32[2,2,2,4,128]{4,2,1,3,0:T(2,128)S(1)} %slice.361) | copy-start | bytes 49156
  38.3 4.9 %collective-permute-start.19 = (f32[8,2,2,4,128]{4,2,1,3,0:T(2,128)}, f32[8,2,2,4,128]{4,2,1,3,0:T(2,128)S(1)}, u32[]{:S(2)}, u32[]{:S(2)}) collective-permute-start(f32[8,2,2,4,128]{4,2,1,3,0:T(2,128)} %pad_maximum_fusion.54), channel_id=1, source_target_pairs={{7,0},{4,1},{5,2},{6,3},{3,4},{0,5},{1,6},{2,7},{15,8},{12,9},{13,... | collective-permute-start | bytes 196616 | tf_op jit(solution)/shard_map/ppermute | solution.py:108
  38.3 6.1 %collective-permute-start.18 = (f32[8,2,2,4,128]{4,2,1,3,0:T(2,128)}, f32[8,2,2,4,128]{4,2,1,3,0:T(2,128)S(1)}, u32[]{:S(2)}, u32[]{:S(2)}) collective-permute-start(f32[8,2,2,4,128]{4,2,1,3,0:T(2,128)} %pad_maximum_fusion.54), channel_id=1, source_target_pairs={{6,0},{7,1},{4,2},{5,3},{2,4},{3,5},{0,6},{1,7},{14,8},{15,9},{12,... | collective-permute-start | bytes 196616 | tf_op jit(solution)/shard_map/ppermute | solution.py:108
  39.6 10.6 %collective-permute-start.17 = (f32[8,2,2,4,128]{4,2,1,3,0:T(2,128)}, f32[8,2,2,4,128]{4,2,1,3,0:T(2,128)}, u32[]{:S(2)}, u32[]{:S(2)}) collective-permute-start(f32[8,2,2,4,128]{4,2,1,3,0:T(2,128)} %pad_maximum_fusion.54), channel_id=1, source_target_pairs={{5,0},{6,1},{7,2},{4,3},{1,4},{2,5},{3,6},{0,7},{13,8},{14,9},{15,... | collective-permute-start | bytes 196616 | tf_op jit(solution)/shard_map/ppermute | solution.py:108
  42.0 8.3 %collective-permute-start.16 = (f32[8,2,2,4,128]{4,2,1,3,0:T(2,128)}, f32[8,2,2,4,128]{4,2,1,3,0:T(2,128)}, u32[]{:S(2)}, u32[]{:S(2)}) collective-permute-start(f32[8,2,2,4,128]{4,2,1,3,0:T(2,128)} %pad_maximum_fusion.54), channel_id=1, source_target_pairs={{4,0},{5,1},{6,2},{7,3},{0,4},{1,5},{2,6},{3,7},{12,8},{13,9},{14,... | collective-permute-start | bytes 196616 | tf_op jit(solution)/shard_map/ppermute | solution.py:108
  42.5 7.8 %collective-permute-start.15 = (f32[8,2,2,4,128]{4,2,1,3,0:T(2,128)}, f32[8,2,2,4,128]{4,2,1,3,0:T(2,128)}, u32[]{:S(2)}, u32[]{:S(2)}) collective-permute-start(f32[8,2,2,4,128]{4,2,1,3,0:T(2,128)} %pad_maximum_fusion.54), channel_id=1, source_target_pairs={{3,0},{0,1},{1,2},{2,3},{7,4},{4,5},{5,6},{6,7},{11,8},{8,9},{9,10... | collective-permute-start | bytes 196616 | tf_op jit(solution)/shard_map/ppermute | solution.py:108
  43.2 3.7 %copy-start.24 = (f32[8,2,2,4,128]{4,2,1,3,0:T(2,128)}, f32[8,2,2,4,128]{4,2,1,3,0:T(2,128)S(1)}, u32[]{:S(2)}) copy-start(f32[8,2,2,4,128]{4,2,1,3,0:T(2,128)S(1)} %collective-permute-done.19) | copy-start | bytes 196612
  43.2 7.1 %collective-permute-start.14 = (f32[8,2,2,4,128]{4,2,1,3,0:T(2,128)}, f32[8,2,2,4,128]{4,2,1,3,0:T(2,128)}, u32[]{:S(2)}, u32[]{:S(2)}) collective-permute-start(f32[8,2,2,4,128]{4,2,1,3,0:T(2,128)} %pad_maximum_fusion.54), channel_id=1, source_target_pairs={{2,0},{3,1},{0,2},{1,3},{6,4},{7,5},{4,6},{5,7},{10,8},{11,9},{8,1... | collective-permute-start | bytes 196616 | tf_op jit(solution)/shard_map/ppermute | solution.py:108
  45.0 5.3 %collective-permute-start.13 = (f32[8,2,2,4,128]{4,2,1,3,0:T(2,128)}, f32[8,2,2,4,128]{4,2,1,3,0:T(2,128)}, u32[]{:S(2)}, u32[]{:S(2)}) collective-permute-start(f32[8,2,2,4,128]{4,2,1,3,0:T(2,128)} %pad_maximum_fusion.54), channel_id=1, source_target_pairs={{1,0},{2,1},{3,2},{0,3},{5,4},{6,5},{7,6},{4,7},{9,8},{10,9},{11,1... | collective-permute-start | bytes 196616 | tf_op jit(solution)/shard_map/ppermute | solution.py:108
  50.2 2.1 %copy-start.8 = (f32[6,1,4,4,128]{4,2,1,3,0:T(4,128)S(1)}, f32[6,1,4,4,128]{4,2,1,3,0:T(4,128)}, u32[]{:S(2)}) copy-start(f32[6,1,4,4,128]{4,2,1,3,0:T(4,128)} %copy-done.7) | copy-start | bytes 147460
  50.2 2.1 %copy-start.10 = (f32[6,1,4,4,128]{4,2,1,3,0:T(4,128)S(1)}, f32[6,1,4,4,128]{4,2,1,3,0:T(4,128)}, u32[]{:S(2)}) copy-start(f32[6,1,4,4,128]{4,2,1,3,0:T(4,128)} %copy-done.9) | copy-start | bytes 147460
  50.2 2.1 %copy-start.14 = (f32[1,4,4,4,128]{4,2,1,3,0:T(4,128)S(1)}, f32[1,4,4,4,128]{4,2,1,3,0:T(4,128)}, u32[]{:S(2)}) copy-start(f32[1,4,4,4,128]{4,2,1,3,0:T(4,128)} %copy-done.13) | copy-start | bytes 98308
  50.2 2.1 %copy-start.16 = (f32[1,4,4,4,128]{4,2,1,3,0:T(4,128)S(1)}, f32[1,4,4,4,128]{4,2,1,3,0:T(4,128)}, u32[]{:S(2)}) copy-start(f32[1,4,4,4,128]{4,2,1,3,0:T(4,128)} %copy-done.15) | copy-start | bytes 98308
  52.9 5.6 %collective-permute-start.24 = (f32[4,4,1,4,128]{4,2,1,3,0:T(1,128)S(1)}, f32[4,4,1,4,128]{4,2,1,3,0:T(1,128)S(1)}, u32[]{:S(2)}, u32[]{:S(2)}) collective-permute-start(f32[4,4,1,4,128]{4,2,1,3,0:T(1,128)S(1)} %get-tuple-element.18), channel_id=1, source_target_pairs={{0,1},{1,2},{2,3},{3,0},{4,5},{5,6},{6,7},{7,4},{8,9},{9,10},{10,1... | collective-permute-start | bytes 98312 | tf_op jit(solution)/shard_map/ppermute | solution.py:24
  53.0 9.7 %collective-permute-start.22 = (f32[4,2,4,4,128]{4,2,1,3,0:T(4,128)S(1)}, f32[4,2,4,4,128]{4,2,1,3,0:T(4,128)S(1)}, u32[]{:S(2)}, u32[]{:S(2)}) collective-permute-start(f32[4,2,4,4,128]{4,2,1,3,0:T(4,128)S(1)} %pad_maximum_fusion.55), channel_id=1, source_target_pairs={{0,4},{4,0},{1,5},{5,1},{2,6},{6,2},{3,7},{7,3},{8,12},{12,8},{9,1... | collective-permute-start | bytes 196616 | tf_op jit(solution)/shard_map/ppermute | solution.py:37
  54.6 4.8 %collective-permute-start.20 = (f32[1,4,4,4,128]{4,2,1,3,0:T(4,128)S(1)}, f32[1,4,4,4,128]{4,2,1,3,0:T(4,128)S(1)}, u32[]{:S(2)}, u32[]{:S(2)}) collective-permute-start(f32[1,4,4,4,128]{4,2,1,3,0:T(4,128)S(1)} %get-tuple-element.20), channel_id=1, source_target_pairs={{0,24},{8,0},{16,8},{24,16},{1,25},{9,1},{17,9},{25,17},{2,26},{10... | collective-permute-start | bytes 98312 | tf_op jit(solution)/shard_map/ppermute | solution.py:24
  56.7 5.7 %collective-permute-start.21 = (f32[1,4,4,4,128]{4,2,1,3,0:T(4,128)S(1)}, f32[1,4,4,4,128]{4,2,1,3,0:T(4,128)S(1)}, u32[]{:S(2)}, u32[]{:S(2)}) collective-permute-start(f32[1,4,4,4,128]{4,2,1,3,0:T(4,128)S(1)} %get-tuple-element.19), channel_id=1, source_target_pairs={{0,8},{8,16},{16,24},{24,0},{1,9},{9,17},{17,25},{25,1},{2,10},{10... | collective-permute-start | bytes 98312 | tf_op jit(solution)/shard_map/ppermute | solution.py:24
  56.7 5.8 %collective-permute-start.23 = (f32[4,4,1,4,128]{4,2,1,3,0:T(1,128)S(1)}, f32[4,4,1,4,128]{4,2,1,3,0:T(1,128)S(1)}, u32[]{:S(2)}, u32[]{:S(2)}) collective-permute-start(f32[4,4,1,4,128]{4,2,1,3,0:T(1,128)S(1)} %get-tuple-element.17), channel_id=1, source_target_pairs={{0,3},{1,0},{2,1},{3,2},{4,7},{5,4},{6,5},{7,6},{8,11},{9,8},{10,9... | collective-permute-start | bytes 98312 | tf_op jit(solution)/shard_map/ppermute | solution.py:24
  58.5 3.9 %copy-start.4 = (f32[1,8,8,4,128]{4,2,1,3,0:T(8,128)S(1)}, f32[1,8,8,4,128]{4,2,1,3,0:T(8,128)}, u32[]{:S(2)}) copy-start(f32[1,8,8,4,128]{4,2,1,3,0:T(8,128)} %copy-done.3) | copy-start | bytes 393220
  (3 other events, 2.5 us)

commit v20 on v19

--- a/solution.py
+++ b/solution.py
@@ -185,12 +185,9 @@
 
 
 def coarse_solve(rhs_two, tiles):
-    extended = rhs_two
-    starts = []
+    extended, joint_starts = extend_joint(rhs_two, ("gy", "gz"), (1, 2), COARSE_HALO)
     extended, start, tiles_by_step = extend_axis(extended, "gx", 0, COARSE_HALO, tiles)
-    starts.append(start)
-    extended, joint_starts = extend_joint(extended, ("gy", "gz"), (1, 2), COARSE_HALO)
-    starts.extend(joint_starts)
+    starts = [start] + list(joint_starts)
     grid = extended.shape[:3]
     orbs = extended.shape[3:]
     operator = coarse_matrix(grid, tuple(starts), rhs_two.shape[:3])

time: 66.4 us -> 79.1 us (1.19)
  waiting for transfers between devices: 18.8 us -> 25.1 us
  local copies, waits for them, and re-layouts: 8.42 us -> 13.4 us
  starting transfers between devices: 26.6 us -> 29.7 us
  matrix products: 3.72 us -> 2.48 us
    ppermute x15, waiting for transfers between devices: 17.6 us -> 22.8 us  [shifted(): lax.ppermute(block, axis, [(j, (j - step) % count) for j in range(count)])]
    broadcast_in_dim x12, local copies, waits for them, and re-layouts: 0.34 us -> 3.38 us  [prolong_face(): face = jnp.repeat(face, 2, other)]
    ppermute x15, starting transfers between devices: 15 us -> 17.6 us  [shifted(): lax.ppermute(block, axis, [(j, (j - step) % count) for j in range(count)])]
    dot_general x1, matrix products: 1.92 us -> 0.68 us  [coarse_solve(): jnp.einsum('qxyz,xyzgl->qgl', operator, extended, precision=lax.Precision...]
    ppermute x7, waiting for transfers between devices: 0.54 us -> 1.73 us  [fetch(): cache[steps] = lax.ppermute(block, tuple(axes), pairs)]
    reshape x1, local copies, waits for them, and re-layouts: 1.64 us -> 2.62 us  [gram_matrix(): return spread.sum(axis=0).reshape(orb_count, orb_count)]
  transfers between devices with their start and end apart: 25 -> 25, of which waited for: 9 -> 10; matrix products, arithmetic and copies ran while one was open for 11% -> 14% of each run, Pallas kernels for 0% -> 0%
where the time goes in v20:
time: 79.1 us; the launch traced here: 78.7 us
  starting transfers between devices  29.7 us (38%)
  waiting for transfers between devices  25.1 us (32%)
  local copies, waits for them, and re-layouts  13.4 us (17%)
  other arithmetic  7.25 us (9%)
  matrix products  2.48 us (3%)
    ppermute x15, waiting for transfers between devices, shifted(): lax.ppermute(block, axis, [(j, (j - step) % count) for j in range(count)])  22.8 us
    ppermute x15, starting transfers between devices, shifted(): lax.ppermute(block, axis, [(j, (j - step) % count) for j in range(count)])  17.6 us
    ppermute x7, starting transfers between devices, fetch(): cache[steps] = lax.ppermute(block, tuple(axes), pairs)  7.42 us
    ppermute x3, starting transfers between devices, axis_faces(): lax.ppermute(jnp.concatenate([first, last], axis=dim), axis, [(0, 1), (1,...  4.68 us
    broadcast_in_dim x12, local copies, waits for them, and re-layouts, prolong_face(): face = jnp.repeat(face, 2, other)  3.38 us
    reshape x1, local copies, waits for them, and re-layouts, gram_matrix(): return spread.sum(axis=0).reshape(orb_count, orb_count)  2.62 us
    dot_general x1, matrix products, body(): jnp.dot(rows, gram, precision=lax.Precision.HIGH, preferred_element_type=...  1.8 us
    ppermute x7, waiting for transfers between devices, fetch(): cache[steps] = lax.ppermute(block, tuple(axes), pairs)  1.73 us
  transfers between devices with their start and end apart: 25, of which 10 were waited for; matrix products, arithmetic and copies ran while one was open for 14% of the time, Pallas kernels for 0%

profile of v20, /device:TPU:0, one launch (start us, length us, event | category | flops | bytes accessed | tf_op | source)
XLA Modules:
  0.0 78.7 jit_solution(10877750504239107202)
XLA Ops:
  0.0 1.5 %fusion.57 = (f32[8,8,1,4,128]{4,2,1,3,0:T(1,128)S(1)}, f32[8,8,1,4,128]{4,2,1,3,0:T(1,128)S(1)}) fusion(bf16[8,8,8,512]{3,2,1,0:T(8,128)(2,1)} %param.5), kind=kLoop, calls=%fused_computation.136 | loop fusion | flops 131072 | bytes 786432 | tf_op jit(solution)/shard_map/div | solution.py:311
  1.6 0.5 collective-permute-start.4
  2.2 2.6 %collective-permute-start.2 = (f32[8,2,8,4,128]{4,2,1,3,0:T(8,128)S(1)}, f32[8,2,8,4,128]{4,2,1,3,0:T(8,128)S(1)}, u32[]{:S(2)}, u32[]{:S(2)}) collective-permute-start(f32[8,2,8,4,128]{4,2,1,3,0:T(8,128)S(1)} %pad_maximum_fusion.32), channel_id=1, source_target_pairs={{0,4},{4,0},{1,5},{5,1},{2,6},{6,2},{3,7},{7,3},{8,12},{12,8},{9,1... | collective-permute-start | bytes 786440 | tf_op jit(solution)/shard_map/ppermute | solution.py:37
  4.8 3.7 %collective-permute-start = (f32[1,8,8,4,128]{4,2,1,3,0:T(8,128)S(1)}, f32[1,8,8,4,128]{4,2,1,3,0:T(8,128)S(1)}, u32[]{:S(2)}, u32[]{:S(2)}) collective-permute-start(f32[1,8,8,4,128]{4,2,1,3,0:T(8,128)S(1)} %copy.38), channel_id=1, source_target_pairs={{0,24},{8,0},{16,8},{24,16},{1,25},{9,1},{17,9},{25,17},{2,26},{10... | collective-permute-start | bytes 393224 | tf_op jit(solution)/shard_map/ppermute | solution.py:24
  8.5 1.2 %collective-permute-start.3 = (f32[8,8,1,4,128]{4,2,1,3,0:T(1,128)S(1)}, f32[8,8,1,4,128]{4,2,1,3,0:T(1,128)S(1)}, u32[]{:S(2)}, u32[]{:S(2)}) collective-permute-start(f32[8,8,1,4,128]{4,2,1,3,0:T(1,128)S(1)} %get-tuple-element.7), channel_id=1, source_target_pairs={{0,3},{1,0},{2,1},{3,2},{4,7},{5,4},{6,5},{7,6},{8,11},{9,8},{10,9... | collective-permute-start | bytes 393224 | tf_op jit(solution)/shard_map/ppermute | solution.py:24
  10.3 0.6 gather_fusion
  11.3 0.8 %collective-permute-done = f32[1,8,8,4,128]{4,2,1,3,0:T(8,128)S(1)} collective-permute-done((f32[1,8,8,4,128]{4,2,1,3,0:T(8,128)S(1)}, f32[1,8,8,4,128]{4,2,1,3,0:T(8,128)S(1)}, u32[]{:S(2)}, u32[]{:S(2)}) %collective-permute-start) | collective-permute-done | bytes 131104 | tf_op jit(solution)/shard_map/ppermute | solution.py:24
  12.1 4.6 %collective-permute-done.1 = f32[1,8,8,4,128]{4,2,1,3,0:T(8,128)S(1)} collective-permute-done((f32[1,8,8,4,128]{4,2,1,3,0:T(8,128)S(1)}, f32[1,8,8,4,128]{4,2,1,3,0:T(8,128)S(1)}, u32[]{:S(2)}, u32[]{:S(2)}) %collective-permute-start.1) | collective-permute-done | bytes 131104 | tf_op jit(solution)/shard_map/ppermute | solution.py:24
  16.6 1.0 %convert_subtract_fusion.1 = f32[8,8,8,4,128]{4,2,1,3,0:T(8,128)S(1)} fusion(f32[8,8,1,4,128]{4,2,1,3,0:T(1,128)S(1)} %collective-permute-done.4, f32[10,1,8,4,128]{4,2,1,3,0:T(8,128)S(1)} %pad.40, f32[10,1,8,4,128]{4,2,1,3,0:T(8,128)S(1)} %pad.41, f32[1,8,8,4,128]{4,2,1,3,0:T(8,128)S(1)} %collective-permute-done, ...), kind=kLoop, calls=%fused_computation.3 | loop fusion | flops 8912896 | bytes 3473408 | tf_op jit(solution)/shard_map/sub | solution.py:314
  17.7 0.4 slice.285
  18.2 0.4 slice.286
  18.9 0.6 collective-permute-start.6
  19.7 1.5 %collective-permute-start.8 = (f32[1,4,4,4,128]{4,2,1,3,0:T(4,128)S(1)}, f32[1,4,4,4,128]{4,2,1,3,0:T(4,128)S(1)}, u32[]{:S(2)}, u32[]{:S(2)}) collective-permute-start(f32[1,4,4,4,128]{4,2,1,3,0:T(4,128)S(1)} %get-tuple-element.26), channel_id=1, source_target_pairs={{0,24},{8,0},{16,8},{24,16},{1,25},{9,1},{17,9},{25,17},{2,26},{10... | collective-permute-start | bytes 98312 | tf_op jit(solution)/shard_map/ppermute | solution.py:24
  21.1 0.6 collective-permute-start.7
  21.7 1.1 %collective-permute-done.5 = f32[4,4,1,4,128]{4,2,1,3,0:T(1,128)S(1)} collective-permute-done((f32[4,4,1,4,128]{4,2,1,3,0:T(1,128)S(1)}, f32[4,4,1,4,128]{4,2,1,3,0:T(1,128)S(1)}, u32[]{:S(2)}, u32[]{:S(2)}) %collective-permute-start.5) | collective-permute-done | bytes 32800 | tf_op jit(solution)/shard_map/ppermute | solution.py:24
  22.9 0.6 collective-permute-done.6
  23.6 3.3 %collective-permute-done.7 = f32[1,4,4,4,128]{4,2,1,3,0:T(4,128)S(1)} collective-permute-done((f32[1,4,4,4,128]{4,2,1,3,0:T(4,128)S(1)}, f32[1,4,4,4,128]{4,2,1,3,0:T(4,128)S(1)}, u32[]{:S(2)}, u32[]{:S(2)}) %collective-permute-start.7) | collective-permute-done | bytes 32800 | tf_op jit(solution)/shard_map/ppermute | solution.py:24
  27.6 1.4 %collective-permute-start.16 = (f32[2,2,2,4,128]{4,2,1,3,0:T(2,128)S(1)}, f32[2,2,2,4,128]{4,2,1,3,0:T(2,128)S(1)}, u32[]{:S(2)}, u32[]{:S(2)}) collective-permute-start(f32[2,2,2,4,128]{4,2,1,3,0:T(2,128)S(1)} %add_multiply_fusion), channel_id=1, source_target_pairs={{7,0},{4,1},{5,2},{6,3},{3,4},{0,5},{1,6},{2,7},{15,8},{12,9},{13,... | collective-permute-start | bytes 49160 | tf_op jit(solution)/shard_map/ppermute | solution.py:108
  29.0 1.3 %collective-permute-start.15 = (f32[2,2,2,4,128]{4,2,1,3,0:T(2,128)S(1)}, f32[2,2,2,4,128]{4,2,1,3,0:T(2,128)S(1)}, u32[]{:S(2)}, u32[]{:S(2)}) collective-permute-start(f32[2,2,2,4,128]{4,2,1,3,0:T(2,128)S(1)} %add_multiply_fusion), channel_id=1, source_target_pairs={{6,0},{7,1},{4,2},{5,3},{2,4},{3,5},{0,6},{1,7},{14,8},{15,9},{12,... | collective-permute-start | bytes 49160 | tf_op jit(solution)/shard_map/ppermute | solution.py:108
  30.4 2.3 %collective-permute-start.14 = (f32[2,2,2,4,128]{4,2,1,3,0:T(2,128)S(1)}, f32[2,2,2,4,128]{4,2,1,3,0:T(2,128)S(1)}, u32[]{:S(2)}, u32[]{:S(2)}) collective-permute-start(f32[2,2,2,4,128]{4,2,1,3,0:T(2,128)S(1)} %add_multiply_fusion), channel_id=1, source_target_pairs={{5,0},{6,1},{7,2},{4,3},{1,4},{2,5},{3,6},{0,7},{13,8},{14,9},{15,... | collective-permute-start | bytes 49160 | tf_op jit(solution)/shard_map/ppermute | solution.py:108
  32.8 0.5 collective-permute-start.13
  33.3 0.5 collective-permute-start.11
  33.7 1.5 %collective-permute-start.10 = (f32[2,2,2,4,128]{4,2,1,3,0:T(2,128)S(1)}, f32[2,2,2,4,128]{4,2,1,3,0:T(2,128)S(1)}, u32[]{:S(2)}, u32[]{:S(2)}) collective-permute-start(f32[2,2,2,4,128]{4,2,1,3,0:T(2,128)S(1)} %add_multiply_fusion), channel_id=1, source_target_pairs={{1,0},{2,1},{3,2},{0,3},{5,4},{6,5},{7,6},{4,7},{9,8},{10,9},{11,1... | collective-permute-start | bytes 49160 | tf_op jit(solution)/shard_map/ppermute | solution.py:108
  35.3 1.2 %collective-permute-done.13 = f32[2,2,2,4,128]{4,2,1,3,0:T(2,128)S(1)} collective-permute-done((f32[2,2,2,4,128]{4,2,1,3,0:T(2,128)S(1)}, f32[2,2,2,4,128]{4,2,1,3,0:T(2,128)S(1)}, u32[]{:S(2)}, u32[]{:S(2)}) %collective-permute-start.13) | collective-permute-done | bytes 16416 | tf_op jit(solution)/shard_map/ppermute | solution.py:108
  36.5 0.5 collective-permute-done.11
  37.2 0.6 collective-permute-start.18
  37.8 3.2 %collective-permute-start.17 = (f32[3,4,8,4,128]{4,2,1,3,0:T(8,128)S(1)}, f32[3,4,8,4,128]{4,2,1,3,0:T(8,128)S(1)}, u32[]{:S(2)}, u32[]{:S(2)}) collective-permute-start(f32[3,4,8,4,128]{4,2,1,3,0:T(8,128)S(1)} %pad_maximum_fusion.34), channel_id=1, source_target_pairs={{0,24},{8,0},{16,8},{24,16},{1,25},{9,1},{17,9},{25,17},{2,26},{10... | collective-permute-start | bytes 589832 | tf_op jit(solution)/shard_map/ppermute | solution.py:24
  41.0 5.6 %collective-permute-done.19 = f32[3,4,8,4,128]{4,2,1,3,0:T(8,128)S(1)} collective-permute-done((f32[3,4,8,4,128]{4,2,1,3,0:T(8,128)S(1)}, f32[3,4,8,4,128]{4,2,1,3,0:T(8,128)S(1)}, u32[]{:S(2)}, u32[]{:S(2)}) %collective-permute-start.19) | collective-permute-done | bytes 196640 | tf_op jit(solution)/shard_map/ppermute | solution.py:24
  46.6 7.4 %collective-permute-done.18 = f32[3,4,8,4,128]{4,2,1,3,0:T(8,128)S(1)} collective-permute-done((f32[3,4,8,4,128]{4,2,1,3,0:T(8,128)S(1)}, f32[3,4,8,4,128]{4,2,1,3,0:T(8,128)S(1)}, u32[]{:S(2)}, u32[]{:S(2)}) %collective-permute-start.18) | collective-permute-done | bytes 196640 | tf_op jit(solution)/shard_map/ppermute | solution.py:24
  54.1 0.7 convolution_bitcast_fusion
  55.4 0.7 fusion.63
  56.1 0.6 fusion.64
  57.4 0.5 collective-permute-start.24
  57.9 0.6 pad_maximum_fusion.54
  58.5 1.5 %collective-permute-start.22 = (f32[4,2,4,4,128]{4,2,1,3,0:T(4,128)}, f32[4,2,4,4,128]{4,2,1,3,0:T(4,128)S(1)}, u32[]{:S(2)}, u32[]{:S(2)}) collective-permute-start(f32[4,2,4,4,128]{4,2,1,3,0:T(4,128)} %pad_maximum_fusion.54), channel_id=1, source_target_pairs={{0,4},{4,0},{1,5},{5,1},{2,6},{6,2},{3,7},{7,3},{8,12},{12,8},{9,1... | collective-permute-start | bytes 196616 | tf_op jit(solution)/shard_map/ppermute | solution.py:37
  60.1 3.6 %collective-permute-start.20 = (f32[1,4,4,4,128]{4,2,1,3,0:T(4,128)}, f32[1,4,4,4,128]{4,2,1,3,0:T(4,128)}, u32[]{:S(2)}, u32[]{:S(2)}) collective-permute-start(f32[1,4,4,4,128]{4,2,1,3,0:T(4,128)} %get-tuple-element.20), channel_id=1, source_target_pairs={{0,24},{8,0},{16,8},{24,16},{1,25},{9,1},{17,9},{25,17},{2,26},{10... | collective-permute-start | bytes 98312 | tf_op jit(solution)/shard_map/ppermute | solution.py:24
  63.7 0.8 %collective-permute-start.21 = (f32[1,4,4,4,128]{4,2,1,3,0:T(4,128)}, f32[1,4,4,4,128]{4,2,1,3,0:T(4,128)}, u32[]{:S(2)}, u32[]{:S(2)}) collective-permute-start(f32[1,4,4,4,128]{4,2,1,3,0:T(4,128)} %get-tuple-element.19), channel_id=1, source_target_pairs={{0,8},{8,16},{16,24},{24,0},{1,9},{9,17},{17,25},{25,1},{2,10},{10... | collective-permute-start | bytes 98312 | tf_op jit(solution)/shard_map/ppermute | solution.py:24
  64.5 1.0 %collective-permute-start.23 = (f32[4,4,1,4,128]{4,2,1,3,0:T(1,128)}, f32[4,4,1,4,128]{4,2,1,3,0:T(1,128)}, u32[]{:S(2)}, u32[]{:S(2)}) collective-permute-start(f32[4,4,1,4,128]{4,2,1,3,0:T(1,128)} %get-tuple-element.17), channel_id=1, source_target_pairs={{0,3},{1,0},{2,1},{3,2},{4,7},{5,4},{6,5},{7,6},{8,11},{9,8},{10,9... | collective-permute-start | bytes 98312 | tf_op jit(solution)/shard_map/ppermute | solution.py:24
  65.8 0.4 multiply_reduce_fusion
  66.2 1.7 %copy.52 = f32[4,128,4,128]{3,2,1,0:T(4,128)} copy(f32[4,128,4,128]{3,1,2,0:T(8,128)S(1)} %multiply_reduce_fusion) | data formatting | bytes 2097152 | tf_op jit(solution)/shard_map/reduce_sum | solution.py:306
  67.8 2.6 %reshape.595 = f32[512,512,1,1]{1,0,2,3:T(8,128)} reshape(f32[4,128,4,128]{3,2,1,0:T(4,128)} %copy.52) | data formatting | bytes 2097152 | tf_op jit(solution)/shard_map/reshape | solution.py:306
  70.4 0.8 broadcast_in_dim.109
  71.5 0.8 broadcast_in_dim.89
  72.3 0.8 broadcast_in_dim.93
  73.2 0.8 broadcast_in_dim.105
  74.4 1.0 %fusion.2 = f32[8,8,8,4,128]{4,2,1,3,0:T(8,128)S(1)} fusion(f32[8,8,8,4,128]{4,2,1,3,0:T(8,128)S(1)} %fusion.42, f32[8,8,1,4,128]{4,2,1,3,0:T(1,128)S(1)} %add.239, f32[10,1,8,4,128]{4,2,1,3,0:T(8,128)S(1)} %pad.48, f32[10,1,8,4,128]{4,2,1,3,0:T(8,128)S(1)} %pad.49, f32[1,8,8,4,128]{4,2,1,3,0:T(8,128)S(1)} %add.230, f32[1,8,8,4,128]{4,2,1,3,0:T(8,128)S(1)} %add.231, ...), kind=kLoop, calls=%fused_computation.10 | loop fusion | flops 9437184 | bytes 3473408 | tf_op jit(solution)/shard_map/add | solution.py:270
  75.9 1.0 %copy-done.1 = f32[512,512,1,1]{1,0,2,3:T(8,128)S(1)} copy-done((f32[512,512,1,1]{1,0,2,3:T(8,128)S(1)}, f32[512,512,1,1]{1,0,2,3:T(8,128)}, u32[]{:S(2)}) %copy-start.1) | copy-done | bytes 1048600
  76.9 1.8 %convolution_convert_fusion = bf16[8,8,8,512]{3,2,1,0:T(8,128)(2,1)} fusion(f32[8,8,8,512]{3,2,1,0:T(8,128)S(1)} %bitcast.82, f32[512,512,1,1]{1,0,2,3:T(8,128)S(1)} %copy-done.1), kind=kOutput, calls=%fused_computation.6 | convolution fusion | flops 805568512 | bytes 2621440 | tf_op jit(solution)/shard_map/dot_general | solution.py:342
  (113 shorter events, 5.5 us)
Async XLA Ops:
  0.0 2.1 %copy-start = (bf16[8,8,8,512]{3,2,1,0:T(8,128)(2,1)S(1)}, bf16[8,8,8,512]{3,2,1,0:T(8,128)(2,1)}, u32[]{:S(2)}) copy-start(bf16[8,8,8,512]{3,2,1,0:T(8,128)(2,1)} %param.5) | copy-start | bytes 1572868
  1.5 8.2 %copy-start.3 = (s32[3,2,512]{2,1,0:T(2,128)S(1)}, s32[3,2,512]{2,1,0:T(2,128)}, u32[]{:S(2)}) copy-start(s32[3,2,512]{2,1,0:T(2,128)} %param.6) | copy-start | bytes 36868
  1.6 8.3 %copy-start.4 = (s32[4,2]{0,1:T(2,128)S(1)}, s32[4,2]{0,1:T(2,128)}, u32[]{:S(2)}) copy-start(s32[4,2]{0,1:T(2,128)} %param.7) | copy-start | bytes 100
  1.6 9.7 %collective-permute-start.4 = (f32[8,8,1,4,128]{4,2,1,3,0:T(1,128)S(1)}, f32[8,8,1,4,128]{4,2,1,3,0:T(1,128)S(1)}, u32[]{:S(2)}, u32[]{:S(2)}) collective-permute-start(f32[8,8,1,4,128]{4,2,1,3,0:T(1,128)S(1)} %get-tuple-element.8), channel_id=1, source_target_pairs={{0,1},{1,2},{2,3},{3,0},{4,5},{5,6},{6,7},{7,4},{8,9},{9,10},{10,1... | collective-permute-start | bytes 393224 | tf_op jit(solution)/shard_map/ppermute | solution.py:24
  2.2 9.0 %collective-permute-start.2 = (f32[8,2,8,4,128]{4,2,1,3,0:T(8,128)S(1)}, f32[8,2,8,4,128]{4,2,1,3,0:T(8,128)S(1)}, u32[]{:S(2)}, u32[]{:S(2)}) collective-permute-start(f32[8,2,8,4,128]{4,2,1,3,0:T(8,128)S(1)} %pad_maximum_fusion.32), channel_id=1, source_target_pairs={{0,4},{4,0},{1,5},{5,1},{2,6},{6,2},{3,7},{7,3},{8,12},{12,8},{9,1... | collective-permute-start | bytes 786440 | tf_op jit(solution)/shard_map/ppermute | solution.py:37
  4.8 7.3 %collective-permute-start = (f32[1,8,8,4,128]{4,2,1,3,0:T(8,128)S(1)}, f32[1,8,8,4,128]{4,2,1,3,0:T(8,128)S(1)}, u32[]{:S(2)}, u32[]{:S(2)}) collective-permute-start(f32[1,8,8,4,128]{4,2,1,3,0:T(8,128)S(1)} %copy.38), channel_id=1, source_target_pairs={{0,24},{8,0},{16,8},{24,16},{1,25},{9,1},{17,9},{25,17},{2,26},{10... | collective-permute-start | bytes 393224 | tf_op jit(solution)/shard_map/ppermute | solution.py:24
  8.5 8.2 %collective-permute-start.1 = (f32[1,8,8,4,128]{4,2,1,3,0:T(8,128)S(1)}, f32[1,8,8,4,128]{4,2,1,3,0:T(8,128)S(1)}, u32[]{:S(2)}, u32[]{:S(2)}) collective-permute-start(f32[1,8,8,4,128]{4,2,1,3,0:T(8,128)S(1)} %copy.39), channel_id=1, source_target_pairs={{0,8},{8,16},{16,24},{24,0},{1,9},{9,17},{17,25},{25,1},{2,10},{10... | collective-permute-start | bytes 393224 | tf_op jit(solution)/shard_map/ppermute | solution.py:24
  8.5 8.1 %collective-permute-start.3 = (f32[8,8,1,4,128]{4,2,1,3,0:T(1,128)S(1)}, f32[8,8,1,4,128]{4,2,1,3,0:T(1,128)S(1)}, u32[]{:S(2)}, u32[]{:S(2)}) collective-permute-start(f32[8,8,1,4,128]{4,2,1,3,0:T(1,128)S(1)} %get-tuple-element.7), channel_id=1, source_target_pairs={{0,3},{1,0},{2,1},{3,2},{4,7},{5,4},{6,5},{7,6},{8,11},{9,8},{10,9... | collective-permute-start | bytes 393224 | tf_op jit(solution)/shard_map/ppermute | solution.py:24
  18.8 16.5 %copy-start.2 = (f32[1,128,128]{2,1,0:T(8,128)S(1)}, f32[1,128,128]{2,1,0:T(8,128)}, u32[]{:S(2)}) copy-start(f32[1,128,128]{2,1,0:T(8,128)} %param.8) | copy-start | bytes 196612
  18.8 2.9 %collective-permute-start.9 = (f32[4,4,1,4,128]{4,2,1,3,0:T(1,128)S(1)}, f32[4,4,1,4,128]{4,2,1,3,0:T(1,128)S(1)}, u32[]{:S(2)}, u32[]{:S(2)}) collective-permute-start(f32[4,4,1,4,128]{4,2,1,3,0:T(1,128)S(1)} %get-tuple-element.24), channel_id=1, source_target_pairs={{0,3},{1,0},{2,1},{3,2},{4,7},{5,4},{6,5},{7,6},{8,11},{9,8},{10,9... | collective-permute-start | bytes 98312 | tf_op jit(solution)/shard_map/ppermute | solution.py:24
  18.9 4.6 %collective-permute-start.6 = (f32[4,2,4,4,128]{4,2,1,3,0:T(4,128)S(1)}, f32[4,2,4,4,128]{4,2,1,3,0:T(4,128)S(1)}, u32[]{:S(2)}, u32[]{:S(2)}) collective-permute-start(f32[4,2,4,4,128]{4,2,1,3,0:T(4,128)S(1)} %pad_maximum_fusion.53), channel_id=1, source_target_pairs={{0,4},{4,0},{1,5},{5,1},{2,6},{6,2},{3,7},{7,3},{8,12},{12,8},{9,1... | collective-permute-start | bytes 196616 | tf_op jit(solution)/shard_map/ppermute | solution.py:37
  19.4 3.4 %collective-permute-start.5 = (f32[4,4,1,4,128]{4,2,1,3,0:T(1,128)S(1)}, f32[4,4,1,4,128]{4,2,1,3,0:T(1,128)S(1)}, u32[]{:S(2)}, u32[]{:S(2)}) collective-permute-start(f32[4,4,1,4,128]{4,2,1,3,0:T(1,128)S(1)} %get-tuple-element.23), channel_id=1, source_target_pairs={{0,1},{1,2},{2,3},{3,0},{4,5},{5,6},{6,7},{7,4},{8,9},{9,10},{10,1... | collective-permute-start | bytes 98312 | tf_op jit(solution)/shard_map/ppermute | solution.py:24
  19.7 3.9 %collective-permute-start.8 = (f32[1,4,4,4,128]{4,2,1,3,0:T(4,128)S(1)}, f32[1,4,4,4,128]{4,2,1,3,0:T(4,128)S(1)}, u32[]{:S(2)}, u32[]{:S(2)}) collective-permute-start(f32[1,4,4,4,128]{4,2,1,3,0:T(4,128)S(1)} %get-tuple-element.26), channel_id=1, source_target_pairs={{0,24},{8,0},{16,8},{24,16},{1,25},{9,1},{17,9},{25,17},{2,26},{10... | collective-permute-start | bytes 98312 | tf_op jit(solution)/shard_map/ppermute | solution.py:24
  21.1 5.7 %collective-permute-start.7 = (f32[1,4,4,4,128]{4,2,1,3,0:T(4,128)S(1)}, f32[1,4,4,4,128]{4,2,1,3,0:T(4,128)S(1)}, u32[]{:S(2)}, u32[]{:S(2)}) collective-permute-start(f32[1,4,4,4,128]{4,2,1,3,0:T(4,128)S(1)} %get-tuple-element.25), channel_id=1, source_target_pairs={{0,8},{8,16},{16,24},{24,0},{1,9},{9,17},{17,25},{25,1},{2,10},{10... | collective-permute-start | bytes 98312 | tf_op jit(solution)/shard_map/ppermute | solution.py:24
  27.1 27.0 %copy-start.5 = (f32[216,8,4,8,1]{0,3,2,4,1:T(8,128)S(1)}, f32[216,8,4,8,1]{0,3,2,4,1:T(8,128)}, u32[]{:S(2)}) copy-start(f32[216,8,4,8,1]{0,3,2,4,1:T(8,128)} %constant.134) | copy-start | bytes 663556
  27.6 5.7 %collective-permute-start.16 = (f32[2,2,2,4,128]{4,2,1,3,0:T(2,128)S(1)}, f32[2,2,2,4,128]{4,2,1,3,0:T(2,128)S(1)}, u32[]{:S(2)}, u32[]{:S(2)}) collective-permute-start(f32[2,2,2,4,128]{4,2,1,3,0:T(2,128)S(1)} %add_multiply_fusion), channel_id=1, source_target_pairs={{7,0},{4,1},{5,2},{6,3},{3,4},{0,5},{1,6},{2,7},{15,8},{12,9},{13,... | collective-permute-start | bytes 49160 | tf_op jit(solution)/shard_map/ppermute | solution.py:108
  29.0 4.8 %collective-permute-start.15 = (f32[2,2,2,4,128]{4,2,1,3,0:T(2,128)S(1)}, f32[2,2,2,4,128]{4,2,1,3,0:T(2,128)S(1)}, u32[]{:S(2)}, u32[]{:S(2)}) collective-permute-start(f32[2,2,2,4,128]{4,2,1,3,0:T(2,128)S(1)} %add_multiply_fusion), channel_id=1, source_target_pairs={{6,0},{7,1},{4,2},{5,3},{2,4},{3,5},{0,6},{1,7},{14,8},{15,9},{12,... | collective-permute-start | bytes 49160 | tf_op jit(solution)/shard_map/ppermute | solution.py:108
  30.4 4.9 %collective-permute-start.14 = (f32[2,2,2,4,128]{4,2,1,3,0:T(2,128)S(1)}, f32[2,2,2,4,128]{4,2,1,3,0:T(2,128)S(1)}, u32[]{:S(2)}, u32[]{:S(2)}) collective-permute-start(f32[2,2,2,4,128]{4,2,1,3,0:T(2,128)S(1)} %add_multiply_fusion), channel_id=1, source_target_pairs={{5,0},{6,1},{7,2},{4,3},{1,4},{2,5},{3,6},{0,7},{13,8},{14,9},{15,... | collective-permute-start | bytes 49160 | tf_op jit(solution)/shard_map/ppermute | solution.py:108
  32.8 3.7 %collective-permute-start.13 = (f32[2,2,2,4,128]{4,2,1,3,0:T(2,128)S(1)}, f32[2,2,2,4,128]{4,2,1,3,0:T(2,128)S(1)}, u32[]{:S(2)}, u32[]{:S(2)}) collective-permute-start(f32[2,2,2,4,128]{4,2,1,3,0:T(2,128)S(1)} %add_multiply_fusion), channel_id=1, source_target_pairs={{4,0},{5,1},{6,2},{7,3},{0,4},{1,5},{2,6},{3,7},{12,8},{13,9},{14,... | collective-permute-start | bytes 49160 | tf_op jit(solution)/shard_map/ppermute | solution.py:108
  33.3 3.2 %collective-permute-start.12 = (f32[2,2,2,4,128]{4,2,1,3,0:T(2,128)S(1)}, f32[2,2,2,4,128]{4,2,1,3,0:T(2,128)S(1)}, u32[]{:S(2)}, u32[]{:S(2)}) collective-permute-start(f32[2,2,2,4,128]{4,2,1,3,0:T(2,128)S(1)} %add_multiply_fusion), channel_id=1, source_target_pairs={{3,0},{0,1},{1,2},{2,3},{7,4},{4,5},{5,6},{6,7},{11,8},{8,9},{9,10... | collective-permute-start | bytes 49160 | tf_op jit(solution)/shard_map/ppermute | solution.py:108
  33.3 3.7 %collective-permute-start.11 = (f32[2,2,2,4,128]{4,2,1,3,0:T(2,128)S(1)}, f32[2,2,2,4,128]{4,2,1,3,0:T(2,128)S(1)}, u32[]{:S(2)}, u32[]{:S(2)}) collective-permute-start(f32[2,2,2,4,128]{4,2,1,3,0:T(2,128)S(1)} %add_multiply_fusion), channel_id=1, source_target_pairs={{2,0},{3,1},{0,2},{1,3},{6,4},{7,5},{4,6},{5,7},{10,8},{11,9},{8,1... | collective-permute-start | bytes 49160 | tf_op jit(solution)/shard_map/ppermute | solution.py:108
  33.7 3.3 %collective-permute-start.10 = (f32[2,2,2,4,128]{4,2,1,3,0:T(2,128)S(1)}, f32[2,2,2,4,128]{4,2,1,3,0:T(2,128)S(1)}, u32[]{:S(2)}, u32[]{:S(2)}) collective-permute-start(f32[2,2,2,4,128]{4,2,1,3,0:T(2,128)S(1)} %add_multiply_fusion), channel_id=1, source_target_pairs={{1,0},{2,1},{3,2},{0,3},{5,4},{6,5},{7,6},{4,7},{9,8},{10,9},{11,1... | collective-permute-start | bytes 49160 | tf_op jit(solution)/shard_map/ppermute | solution.py:108
  37.1 9.5 %collective-permute-start.19 = (f32[3,4,8,4,128]{4,2,1,3,0:T(8,128)S(1)}, f32[3,4,8,4,128]{4,2,1,3,0:T(8,128)S(1)}, u32[]{:S(2)}, u32[]{:S(2)}) collective-permute-start(f32[3,4,8,4,128]{4,2,1,3,0:T(8,128)S(1)} %pad_maximum_fusion.34), channel_id=1, source_target_pairs={{0,8},{8,16},{16,24},{24,0},{1,9},{9,17},{17,25},{25,1},{2,10},{10... | collective-permute-start | bytes 589832 | tf_op jit(solution)/shard_map/ppermute | solution.py:24
  37.2 16.9 %collective-permute-start.18 = (f32[3,4,8,4,128]{4,2,1,3,0:T(8,128)S(1)}, f32[3,4,8,4,128]{4,2,1,3,0:T(8,128)S(1)}, u32[]{:S(2)}, u32[]{:S(2)}) collective-permute-start(f32[3,4,8,4,128]{4,2,1,3,0:T(8,128)S(1)} %pad_maximum_fusion.34), channel_id=1, source_target_pairs={{0,16},{8,24},{16,0},{24,8},{1,17},{9,25},{17,1},{25,9},{2,18},{10... | collective-permute-start | bytes 589832 | tf_op jit(solution)/shard_map/ppermute | solution.py:24
  37.8 16.3 %collective-permute-start.17 = (f32[3,4,8,4,128]{4,2,1,3,0:T(8,128)S(1)}, f32[3,4,8,4,128]{4,2,1,3,0:T(8,128)S(1)}, u32[]{:S(2)}, u32[]{:S(2)}) collective-permute-start(f32[3,4,8,4,128]{4,2,1,3,0:T(8,128)S(1)} %pad_maximum_fusion.34), channel_id=1, source_target_pairs={{0,24},{8,0},{16,8},{24,16},{1,25},{9,1},{17,9},{25,17},{2,26},{10... | collective-permute-start | bytes 589832 | tf_op jit(solution)/shard_map/ppermute | solution.py:24
  57.4 13.0 %collective-permute-start.24 = (f32[4,4,1,4,128]{4,2,1,3,0:T(1,128)}, f32[4,4,1,4,128]{4,2,1,3,0:T(1,128)}, u32[]{:S(2)}, u32[]{:S(2)}) collective-permute-start(f32[4,4,1,4,128]{4,2,1,3,0:T(1,128)} %get-tuple-element.18), channel_id=1, source_target_pairs={{0,1},{1,2},{2,3},{3,0},{4,5},{5,6},{6,7},{7,4},{8,9},{9,10},{10,1... | collective-permute-start | bytes 98312 | tf_op jit(solution)/shard_map/ppermute | solution.py:24
  58.5 15.6 %collective-permute-start.22 = (f32[4,2,4,4,128]{4,2,1,3,0:T(4,128)}, f32[4,2,4,4,128]{4,2,1,3,0:T(4,128)S(1)}, u32[]{:S(2)}, u32[]{:S(2)}) collective-permute-start(f32[4,2,4,4,128]{4,2,1,3,0:T(4,128)} %pad_maximum_fusion.54), channel_id=1, source_target_pairs={{0,4},{4,0},{1,5},{5,1},{2,6},{6,2},{3,7},{7,3},{8,12},{12,8},{9,1... | collective-permute-start | bytes 196616 | tf_op jit(solution)/shard_map/ppermute | solution.py:37
  60.1 11.4 %collective-permute-start.20 = (f32[1,4,4,4,128]{4,2,1,3,0:T(4,128)}, f32[1,4,4,4,128]{4,2,1,3,0:T(4,128)}, u32[]{:S(2)}, u32[]{:S(2)}) collective-permute-start(f32[1,4,4,4,128]{4,2,1,3,0:T(4,128)} %get-tuple-element.20), channel_id=1, source_target_pairs={{0,24},{8,0},{16,8},{24,16},{1,25},{9,1},{17,9},{25,17},{2,26},{10... | collective-permute-start | bytes 98312 | tf_op jit(solution)/shard_map/ppermute | solution.py:24
  63.7 8.6 %collective-permute-start.21 = (f32[1,4,4,4,128]{4,2,1,3,0:T(4,128)}, f32[1,4,4,4,128]{4,2,1,3,0:T(4,128)}, u32[]{:S(2)}, u32[]{:S(2)}) collective-permute-start(f32[1,4,4,4,128]{4,2,1,3,0:T(4,128)} %get-tuple-element.19), channel_id=1, source_target_pairs={{0,8},{8,16},{16,24},{24,0},{1,9},{9,17},{17,25},{25,1},{2,10},{10... | collective-permute-start | bytes 98312 | tf_op jit(solution)/shard_map/ppermute | solution.py:24
  64.5 8.7 %collective-permute-start.23 = (f32[4,4,1,4,128]{4,2,1,3,0:T(1,128)}, f32[4,4,1,4,128]{4,2,1,3,0:T(1,128)}, u32[]{:S(2)}, u32[]{:S(2)}) collective-permute-start(f32[4,4,1,4,128]{4,2,1,3,0:T(1,128)} %get-tuple-element.17), channel_id=1, source_target_pairs={{0,3},{1,0},{2,1},{3,2},{4,7},{5,4},{6,5},{7,6},{8,11},{9,8},{10,9... | collective-permute-start | bytes 98312 | tf_op jit(solution)/shard_map/ppermute | solution.py:24
  75.6 1.2 %copy-start.1 = (f32[512,512,1,1]{1,0,2,3:T(8,128)S(1)}, f32[512,512,1,1]{1,0,2,3:T(8,128)}, u32[]{:S(2)}) copy-start(f32[512,512,1,1]{1,0,2,3:T(8,128)} %reshape.595) | copy-start | bytes 3145732

commit v21 on v19

--- a/solution.py
+++ b/solution.py
@@ -29,8 +29,7 @@
     first = lax.slice_in_dim(block, 0, 1, axis=dim)
     last = lax.slice_in_dim(block, block.shape[dim] - 1, None, axis=dim)
     if prepare is not None:
-        first = prepare(first)
-        last = prepare(last)
+        first, last = lax.optimization_barrier((prepare(first), prepare(last)))
     if count == 1:
         return last, first
     if count == 2:

time: 66.4 us -> 66.4 us (level)
  no operation moved by 1% of the time
where the time goes in v21:
time: 66.4 us; the launch traced here: 66.2 us
  starting transfers between devices  26.6 us (40%)
  waiting for transfers between devices  18.8 us (28%)
  local copies, waits for them, and re-layouts  8.42 us (13%)
  other arithmetic  7.7 us (12%)
  matrix products  3.73 us (6%)
  between operations  1.07 us (2%)
    ppermute x15, waiting for transfers between devices, shifted(): lax.ppermute(block, axis, [(j, (j - step) % count) for j in range(count)])  17.6 us
    ppermute x15, starting transfers between devices, shifted(): lax.ppermute(block, axis, [(j, (j - step) % count) for j in range(count)])  15 us
    ppermute x7, starting transfers between devices, fetch(): cache[steps] = lax.ppermute(block, tuple(axes), pairs)  6.86 us
    ppermute x3, starting transfers between devices, axis_faces(): lax.ppermute(jnp.concatenate([first, last], axis=dim), axis, [(0, 1), (1,...  4.75 us
    dot_general x1, matrix products, coarse_solve(): jnp.einsum('qxyz,xyzgl->qgl', operator, extended, precision=lax.Precision...  1.92 us
    dot_general x1, matrix products, body(): jnp.dot(rows, gram, precision=lax.Precision.HIGH, preferred_element_type=...  1.81 us
    reduce_sum x1, local copies, waits for them, and re-layouts, gram_matrix(): return spread.sum(axis=0).reshape(orb_count, orb_count)  1.7 us
    reshape x1, local copies, waits for them, and re-layouts, gram_matrix(): return spread.sum(axis=0).reshape(orb_count, orb_count)  1.64 us
  transfers between devices with their start and end apart: 25, of which 9 were waited for; matrix products, arithmetic and copies ran while one was open for 11% of the time, Pallas kernels for 0%

profile of v21, /device:TPU:0, one launch (start us, length us, event | category | flops | bytes accessed | tf_op | source)
XLA Modules:
  0.0 66.2 jit_solution(5785423341005408469)
XLA Ops:
  0.0 1.5 %fusion.56 = (f32[8,8,1,4,128]{4,2,1,3,0:T(1,128)S(1)}, f32[8,8,1,4,128]{4,2,1,3,0:T(1,128)S(1)}) fusion(bf16[8,8,8,512]{3,2,1,0:T(8,128)(2,1)} %param.5), kind=kLoop, calls=%fused_computation.133 | loop fusion | flops 131072 | bytes 786432 | tf_op jit(solution)/shard_map/div | solution.py:313
  1.6 0.5 collective-permute-start.4
  2.2 2.6 %collective-permute-start.2 = (f32[8,2,8,4,128]{4,2,1,3,0:T(8,128)S(1)}, f32[8,2,8,4,128]{4,2,1,3,0:T(8,128)S(1)}, u32[]{:S(2)}, u32[]{:S(2)}) collective-permute-start(f32[8,2,8,4,128]{4,2,1,3,0:T(8,128)S(1)} %pad_maximum_fusion.32), channel_id=1, source_target_pairs={{0,4},{4,0},{1,5},{5,1},{2,6},{6,2},{3,7},{7,3},{8,12},{12,8},{9,1... | collective-permute-start | bytes 786440 | tf_op jit(solution)/shard_map/ppermute | solution.py:36
  4.8 3.7 %collective-permute-start = (f32[1,8,8,4,128]{4,2,1,3,0:T(8,128)S(1)}, f32[1,8,8,4,128]{4,2,1,3,0:T(8,128)S(1)}, u32[]{:S(2)}, u32[]{:S(2)}) collective-permute-start(f32[1,8,8,4,128]{4,2,1,3,0:T(8,128)S(1)} %copy.38), channel_id=1, source_target_pairs={{0,24},{8,0},{16,8},{24,16},{1,25},{9,1},{17,9},{25,17},{2,26},{10... | collective-permute-start | bytes 393224 | tf_op jit(solution)/shard_map/ppermute | solution.py:24
  8.6 1.2 %collective-permute-start.3 = (f32[8,8,1,4,128]{4,2,1,3,0:T(1,128)S(1)}, f32[8,8,1,4,128]{4,2,1,3,0:T(1,128)S(1)}, u32[]{:S(2)}, u32[]{:S(2)}) collective-permute-start(f32[8,8,1,4,128]{4,2,1,3,0:T(1,128)S(1)} %get-tuple-element.15), channel_id=1, source_target_pairs={{0,3},{1,0},{2,1},{3,2},{4,7},{5,4},{6,5},{7,6},{8,11},{9,8},{10,9... | collective-permute-start | bytes 393224 | tf_op jit(solution)/shard_map/ppermute | solution.py:24
  10.1 0.6 gather_fusion
  11.3 0.7 %fusion.58 = (f32[4,4]{1,0:T(4,128)}, f32[4,4]{1,0:T(4,128)}) fusion(s32[4]{0:T(128)S(1)} %get-tuple-element.17, s32[4]{0:T(128)S(1)} %get-tuple-element.18), kind=kLoop, calls=%fused_computation.164 | loop fusion | flops 64 | bytes 160 | tf_op jit(solution)/shard_map/convert_element_type | solution.py:305
  12.2 4.4 %collective-permute-done.1 = f32[1,8,8,4,128]{4,2,1,3,0:T(8,128)S(1)} collective-permute-done((f32[1,8,8,4,128]{4,2,1,3,0:T(8,128)S(1)}, f32[1,8,8,4,128]{4,2,1,3,0:T(8,128)S(1)}, u32[]{:S(2)}, u32[]{:S(2)}) %collective-permute-start.1) | collective-permute-done | bytes 131104 | tf_op jit(solution)/shard_map/ppermute | solution.py:24
  16.7 1.0 %convert_subtract_fusion.1 = f32[8,8,8,4,128]{4,2,1,3,0:T(8,128)S(1)} fusion(f32[8,8,1,4,128]{4,2,1,3,0:T(1,128)S(1)} %collective-permute-done.4, f32[10,1,8,4,128]{4,2,1,3,0:T(8,128)S(1)} %pad.40, f32[10,1,8,4,128]{4,2,1,3,0:T(8,128)S(1)} %pad.41, f32[1,8,8,4,128]{4,2,1,3,0:T(8,128)S(1)} %collective-permute-done, ...), kind=kLoop, calls=%fused_computation.3 | loop fusion | flops 8912896 | bytes 3473408 | tf_op jit(solution)/shard_map/sub | solution.py:316
  17.8 0.4 slice.285
  18.2 0.4 slice.286
  18.9 0.6 collective-permute-start.6
  19.5 0.2 collective-permute-start.5
  19.7 1.5 %collective-permute-start.8 = (f32[1,4,4,4,128]{4,2,1,3,0:T(4,128)S(1)}, f32[1,4,4,4,128]{4,2,1,3,0:T(4,128)S(1)}, u32[]{:S(2)}, u32[]{:S(2)}) collective-permute-start(f32[1,4,4,4,128]{4,2,1,3,0:T(4,128)S(1)} %get-tuple-element.38), channel_id=1, source_target_pairs={{0,24},{8,0},{16,8},{24,16},{1,25},{9,1},{17,9},{25,17},{2,26},{10... | collective-permute-start | bytes 98312 | tf_op jit(solution)/shard_map/ppermute | solution.py:24
  21.2 0.6 collective-permute-start.7
  21.8 1.1 %collective-permute-done.5 = f32[4,4,1,4,128]{4,2,1,3,0:T(1,128)S(1)} collective-permute-done((f32[4,4,1,4,128]{4,2,1,3,0:T(1,128)S(1)}, f32[4,4,1,4,128]{4,2,1,3,0:T(1,128)S(1)}, u32[]{:S(2)}, u32[]{:S(2)}) %collective-permute-start.5) | collective-permute-done | bytes 32800 | tf_op jit(solution)/shard_map/ppermute | solution.py:24
  22.9 0.6 collective-permute-done.6
  23.6 3.3 %collective-permute-done.7 = f32[1,4,4,4,128]{4,2,1,3,0:T(4,128)S(1)} collective-permute-done((f32[1,4,4,4,128]{4,2,1,3,0:T(4,128)S(1)}, f32[1,4,4,4,128]{4,2,1,3,0:T(4,128)S(1)}, u32[]{:S(2)}, u32[]{:S(2)}) %collective-permute-start.7) | collective-permute-done | bytes 32800 | tf_op jit(solution)/shard_map/ppermute | solution.py:24
  26.9 0.2 fusion.51
  27.2 0.2 slice.305
  27.4 0.2 slice.306
  27.8 0.7 %collective-permute-start.11 = (f32[10,2,2,4,128]{4,2,1,3,0:T(2,128)S(1)}, f32[10,2,2,4,128]{4,2,1,3,0:T(2,128)S(1)}, u32[]{:S(2)}, u32[]{:S(2)}) collective-permute-start(f32[10,2,2,4,128]{4,2,1,3,0:T(2,128)S(1)} %pad_maximum_fusion.52), channel_id=1, source_target_pairs={{0,16},{8,24},{16,0},{24,8},{1,17},{9,25},{17,1},{25,9},{2,18},{10... | collective-permute-start | bytes 245768 | tf_op jit(solution)/shard_map/ppermute | solution.py:24
  28.5 3.1 %collective-permute-start.10 = (f32[10,2,2,4,128]{4,2,1,3,0:T(2,128)S(1)}, f32[10,2,2,4,128]{4,2,1,3,0:T(2,128)S(1)}, u32[]{:S(2)}, u32[]{:S(2)}) collective-permute-start(f32[10,2,2,4,128]{4,2,1,3,0:T(2,128)S(1)} %pad_maximum_fusion.52), channel_id=1, source_target_pairs={{0,24},{8,0},{16,8},{24,16},{1,25},{9,1},{17,9},{25,17},{2,26},{10... | collective-permute-start | bytes 245768 | tf_op jit(solution)/shard_map/ppermute | solution.py:24
  31.7 3.3 %collective-permute-done.12 = f32[10,2,2,4,128]{4,2,1,3,0:T(2,128)S(1)} collective-permute-done((f32[10,2,2,4,128]{4,2,1,3,0:T(2,128)S(1)}, f32[10,2,2,4,128]{4,2,1,3,0:T(2,128)S(1)}, u32[]{:S(2)}, u32[]{:S(2)}) %collective-permute-start.12) | collective-permute-done | bytes 81952 | tf_op jit(solution)/shard_map/ppermute | solution.py:24
  35.0 2.6 %collective-permute-done.11 = f32[10,2,2,4,128]{4,2,1,3,0:T(2,128)S(1)} collective-permute-done((f32[10,2,2,4,128]{4,2,1,3,0:T(2,128)S(1)}, f32[10,2,2,4,128]{4,2,1,3,0:T(2,128)S(1)}, u32[]{:S(2)}, u32[]{:S(2)}) %collective-permute-start.11) | collective-permute-done | bytes 81952 | tf_op jit(solution)/shard_map/ppermute | solution.py:24
  37.6 0.6 pad_maximum_fusion.54
  38.3 1.3 %collective-permute-start.18 = (f32[8,2,2,4,128]{4,2,1,3,0:T(2,128)}, f32[8,2,2,4,128]{4,2,1,3,0:T(2,128)S(1)}, u32[]{:S(2)}, u32[]{:S(2)}) collective-permute-start(f32[8,2,2,4,128]{4,2,1,3,0:T(2,128)} %pad_maximum_fusion.54), channel_id=1, source_target_pairs={{6,0},{7,1},{4,2},{5,3},{2,4},{3,5},{0,6},{1,7},{14,8},{15,9},{12,... | collective-permute-start | bytes 196616 | tf_op jit(solution)/shard_map/ppermute | solution.py:107
  39.6 2.4 %collective-permute-start.17 = (f32[8,2,2,4,128]{4,2,1,3,0:T(2,128)}, f32[8,2,2,4,128]{4,2,1,3,0:T(2,128)}, u32[]{:S(2)}, u32[]{:S(2)}) collective-permute-start(f32[8,2,2,4,128]{4,2,1,3,0:T(2,128)} %pad_maximum_fusion.54), channel_id=1, source_target_pairs={{5,0},{6,1},{7,2},{4,3},{1,4},{2,5},{3,6},{0,7},{13,8},{14,9},{15,... | collective-permute-start | bytes 196616 | tf_op jit(solution)/shard_map/ppermute | solution.py:107
  42.0 0.5 collective-permute-start.16
  42.7 0.5 collective-permute-done.19
  43.2 1.2 %collective-permute-start.14 = (f32[8,2,2,4,128]{4,2,1,3,0:T(2,128)}, f32[8,2,2,4,128]{4,2,1,3,0:T(2,128)}, u32[]{:S(2)}, u32[]{:S(2)}) collective-permute-start(f32[8,2,2,4,128]{4,2,1,3,0:T(2,128)} %pad_maximum_fusion.54), channel_id=1, source_target_pairs={{2,0},{3,1},{0,2},{1,3},{6,4},{7,5},{4,6},{5,7},{10,8},{11,9},{8,1... | collective-permute-start | bytes 196616 | tf_op jit(solution)/shard_map/ppermute | solution.py:107
  44.4 0.6 copy-done.25
  45.0 1.4 %collective-permute-start.13 = (f32[8,2,2,4,128]{4,2,1,3,0:T(2,128)}, f32[8,2,2,4,128]{4,2,1,3,0:T(2,128)}, u32[]{:S(2)}, u32[]{:S(2)}) collective-permute-start(f32[8,2,2,4,128]{4,2,1,3,0:T(2,128)} %pad_maximum_fusion.54), channel_id=1, source_target_pairs={{1,0},{2,1},{3,2},{0,3},{5,4},{6,5},{7,6},{4,7},{9,8},{10,9},{11,1... | collective-permute-start | bytes 196616 | tf_op jit(solution)/shard_map/ppermute | solution.py:107
  46.4 0.4 multiply_reduce_fusion
  46.9 1.7 %copy.52 = f32[4,128,4,128]{3,2,1,0:T(4,128)} copy(f32[4,128,4,128]{3,1,2,0:T(8,128)S(1)} %multiply_reduce_fusion) | data formatting | bytes 2097152 | tf_op jit(solution)/shard_map/reduce_sum | solution.py:308
  48.6 1.6 %reshape.595 = f32[512,512,1,1]{1,0,2,3:T(8,128)S(1)} reshape(f32[4,128,4,128]{3,2,1,0:T(4,128)} %copy.52) | data formatting | bytes 2097152 | tf_op jit(solution)/shard_map/reshape | solution.py:308
  50.3 1.9 %convolution_bitcast_fusion = f32[216,4,128]{2,0,1:T(8,128)S(1)} fusion(f32[216,8,4,8,1]{0,3,2,4,1:T(8,128)} %constant.134, f32[8,2,2,4,128]{4,2,1,3,0:T(2,128)} %copy-done.24, f32[8,2,2,4,128]{4,2,1,3,0:T(2,128)} %copy-done.25, f32[8,2,2,4,128]{4,2,1,3,0:T(2,128)} %collective-permute-done.17, f32[8,2,2,4,128]{4,2,1,3,0:T(2,128)} %collective-permute-done.16, ...), kind=kOutput, calls=%fused_computation.7 | convolution fusion | flops 341049344 | bytes 1187840 | tf_op jit(solution)/shard_map/qxyz,xyzgl->qgl/dot_general | solution.py:197
  52.4 0.2 maximum_add_fusion
  52.6 0.2 fusion.47
  53.0 1.6 %collective-permute-start.22 = (f32[4,2,4,4,128]{4,2,1,3,0:T(4,128)S(1)}, f32[4,2,4,4,128]{4,2,1,3,0:T(4,128)S(1)}, u32[]{:S(2)}, u32[]{:S(2)}) collective-permute-start(f32[4,2,4,4,128]{4,2,1,3,0:T(4,128)S(1)} %pad_maximum_fusion.55), channel_id=1, source_target_pairs={{0,4},{4,0},{1,5},{5,1},{2,6},{6,2},{3,7},{7,3},{8,12},{12,8},{9,1... | collective-permute-start | bytes 196616 | tf_op jit(solution)/shard_map/ppermute | solution.py:36
  54.6 2.1 %collective-permute-start.20 = (f32[1,4,4,4,128]{4,2,1,3,0:T(4,128)S(1)}, f32[1,4,4,4,128]{4,2,1,3,0:T(4,128)S(1)}, u32[]{:S(2)}, u32[]{:S(2)}) collective-permute-start(f32[1,4,4,4,128]{4,2,1,3,0:T(4,128)S(1)} %get-tuple-element.32), channel_id=1, source_target_pairs={{0,24},{8,0},{16,8},{24,16},{1,25},{9,1},{17,9},{25,17},{2,26},{10... | collective-permute-start | bytes 98312 | tf_op jit(solution)/shard_map/ppermute | solution.py:24
  56.7 1.2 %collective-permute-start.23 = (f32[4,4,1,4,128]{4,2,1,3,0:T(1,128)S(1)}, f32[4,4,1,4,128]{4,2,1,3,0:T(1,128)S(1)}, u32[]{:S(2)}, u32[]{:S(2)}) collective-permute-start(f32[4,4,1,4,128]{4,2,1,3,0:T(1,128)S(1)} %get-tuple-element.29), channel_id=1, source_target_pairs={{0,3},{1,0},{2,1},{3,2},{4,7},{5,4},{6,5},{7,6},{8,11},{9,8},{10,9... | collective-permute-start | bytes 98312 | tf_op jit(solution)/shard_map/ppermute | solution.py:24
  58.0 0.4 broadcast_in_dim.88
  58.6 0.6 copy-done.2
  59.5 2.9 %collective-permute-done.21 = f32[1,4,4,4,128]{4,2,1,3,0:T(4,128)S(1)} collective-permute-done((f32[1,4,4,4,128]{4,2,1,3,0:T(4,128)S(1)}, f32[1,4,4,4,128]{4,2,1,3,0:T(4,128)S(1)}, u32[]{:S(2)}, u32[]{:S(2)}) %collective-permute-start.21) | collective-permute-done | bytes 32800 | tf_op jit(solution)/shard_map/ppermute | solution.py:24
  63.0 1.0 %fusion.2 = f32[8,8,8,4,128]{4,2,1,3,0:T(8,128)S(1)} fusion(f32[8,8,8,4,128]{4,2,1,3,0:T(8,128)S(1)} %fusion.42, f32[8,8,1,4,128]{4,2,1,3,0:T(1,128)S(1)} %add.239, f32[10,1,8,4,128]{4,2,1,3,0:T(8,128)S(1)} %pad.48, f32[10,1,8,4,128]{4,2,1,3,0:T(8,128)S(1)} %pad.49, f32[1,8,8,4,128]{4,2,1,3,0:T(8,128)S(1)} %add.230, f32[1,8,8,4,128]{4,2,1,3,0:T(8,128)S(1)} %add.231, ...), kind=kLoop, calls=%fused_computation.10 | loop fusion | flops 9437184 | bytes 3473408 | tf_op jit(solution)/shard_map/add | solution.py:272
  64.2 0.2 bitcast_multiply_fusion
  64.4 1.8 %convolution_convert_fusion = bf16[8,8,8,512]{3,2,1,0:T(8,128)(2,1)} fusion(f32[8,8,8,512]{3,2,1,0:T(8,128)S(1)} %bitcast.82, f32[512,512,1,1]{1,0,2,3:T(8,128)S(1)} %reshape.595), kind=kOutput, calls=%fused_computation.6 | convolution fusion | flops 805568512 | bytes 2621440 | tf_op jit(solution)/shard_map/dot_general | solution.py:344
  (154 shorter events, 3.5 us)
Async XLA Ops:
  0.0 2.1 %copy-start = (bf16[8,8,8,512]{3,2,1,0:T(8,128)(2,1)S(1)}, bf16[8,8,8,512]{3,2,1,0:T(8,128)(2,1)}, u32[]{:S(2)}) copy-start(bf16[8,8,8,512]{3,2,1,0:T(8,128)(2,1)} %param.5) | copy-start | bytes 1572868
  1.5 8.2 %copy-start.11 = (f32[1,128,128]{2,1,0:T(8,128)S(1)}, f32[1,128,128]{2,1,0:T(8,128)}, u32[]{:S(2)}) copy-start(f32[1,128,128]{2,1,0:T(8,128)} %param.8) | copy-start | bytes 196612
  1.6 8.3 %copy-start.20 = (s32[3,2,512]{2,1,0:T(2,128)S(1)}, s32[3,2,512]{2,1,0:T(2,128)}, u32[]{:S(2)}) copy-start(s32[3,2,512]{2,1,0:T(2,128)} %param.6) | copy-start | bytes 36868
  1.6 10.6 %collective-permute-start.4 = (f32[8,8,1,4,128]{4,2,1,3,0:T(1,128)S(1)}, f32[8,8,1,4,128]{4,2,1,3,0:T(1,128)S(1)}, u32[]{:S(2)}, u32[]{:S(2)}) collective-permute-start(f32[8,8,1,4,128]{4,2,1,3,0:T(1,128)S(1)} %get-tuple-element.16), channel_id=1, source_target_pairs={{0,1},{1,2},{2,3},{3,0},{4,5},{5,6},{6,7},{7,4},{8,9},{9,10},{10,1... | collective-permute-start | bytes 393224 | tf_op jit(solution)/shard_map/ppermute | solution.py:24
  2.1 7.7 %copy-start.23 = (s32[4,2]{0,1:T(2,128)S(1)}, s32[4,2]{0,1:T(2,128)}, u32[]{:S(2)}) copy-start(s32[4,2]{0,1:T(2,128)} %param.7) | copy-start | bytes 100
  2.2 9.9 %collective-permute-start.2 = (f32[8,2,8,4,128]{4,2,1,3,0:T(8,128)S(1)}, f32[8,2,8,4,128]{4,2,1,3,0:T(8,128)S(1)}, u32[]{:S(2)}, u32[]{:S(2)}) collective-permute-start(f32[8,2,8,4,128]{4,2,1,3,0:T(8,128)S(1)} %pad_maximum_fusion.32), channel_id=1, source_target_pairs={{0,4},{4,0},{1,5},{5,1},{2,6},{6,2},{3,7},{7,3},{8,12},{12,8},{9,1... | collective-permute-start | bytes 786440 | tf_op jit(solution)/shard_map/ppermute | solution.py:36
  4.8 7.4 %collective-permute-start = (f32[1,8,8,4,128]{4,2,1,3,0:T(8,128)S(1)}, f32[1,8,8,4,128]{4,2,1,3,0:T(8,128)S(1)}, u32[]{:S(2)}, u32[]{:S(2)}) collective-permute-start(f32[1,8,8,4,128]{4,2,1,3,0:T(8,128)S(1)} %copy.38), channel_id=1, source_target_pairs={{0,24},{8,0},{16,8},{24,16},{1,25},{9,1},{17,9},{25,17},{2,26},{10... | collective-permute-start | bytes 393224 | tf_op jit(solution)/shard_map/ppermute | solution.py:24
  8.5 8.2 %collective-permute-start.1 = (f32[1,8,8,4,128]{4,2,1,3,0:T(8,128)S(1)}, f32[1,8,8,4,128]{4,2,1,3,0:T(8,128)S(1)}, u32[]{:S(2)}, u32[]{:S(2)}) collective-permute-start(f32[1,8,8,4,128]{4,2,1,3,0:T(8,128)S(1)} %copy.39), channel_id=1, source_target_pairs={{0,8},{8,16},{16,24},{24,0},{1,9},{9,17},{17,25},{25,1},{2,10},{10... | collective-permute-start | bytes 393224 | tf_op jit(solution)/shard_map/ppermute | solution.py:24
  8.6 8.1 %collective-permute-start.3 = (f32[8,8,1,4,128]{4,2,1,3,0:T(1,128)S(1)}, f32[8,8,1,4,128]{4,2,1,3,0:T(1,128)S(1)}, u32[]{:S(2)}, u32[]{:S(2)}) collective-permute-start(f32[8,8,1,4,128]{4,2,1,3,0:T(1,128)S(1)} %get-tuple-element.15), channel_id=1, source_target_pairs={{0,3},{1,0},{2,1},{3,2},{4,7},{5,4},{6,5},{7,6},{8,11},{9,8},{10,9... | collective-permute-start | bytes 393224 | tf_op jit(solution)/shard_map/ppermute | solution.py:24
  12.2 5.4 %copy-start.1 = (f32[8,8,1,4,128]{4,2,1,3,0:T(1,128)}, f32[8,8,1,4,128]{4,2,1,3,0:T(1,128)S(1)}, u32[]{:S(2)}) copy-start(f32[8,8,1,4,128]{4,2,1,3,0:T(1,128)S(1)} %collective-permute-done.4) | copy-start | bytes 393220
  12.2 5.4 %copy-start.5 = (f32[1,8,8,4,128]{4,2,1,3,0:T(8,128)}, f32[1,8,8,4,128]{4,2,1,3,0:T(8,128)S(1)}, u32[]{:S(2)}) copy-start(f32[1,8,8,4,128]{4,2,1,3,0:T(8,128)S(1)} %collective-permute-done) | copy-start | bytes 393220
  16.7 1.0 %copy-start.3 = (f32[1,8,8,4,128]{4,2,1,3,0:T(8,128)}, f32[1,8,8,4,128]{4,2,1,3,0:T(8,128)S(1)}, u32[]{:S(2)}) copy-start(f32[1,8,8,4,128]{4,2,1,3,0:T(8,128)S(1)} %collective-permute-done.1) | copy-start | bytes 393220
  18.8 2.9 %collective-permute-start.9 = (f32[4,4,1,4,128]{4,2,1,3,0:T(1,128)S(1)}, f32[4,4,1,4,128]{4,2,1,3,0:T(1,128)S(1)}, u32[]{:S(2)}, u32[]{:S(2)}) collective-permute-start(f32[4,4,1,4,128]{4,2,1,3,0:T(1,128)S(1)} %get-tuple-element.36), channel_id=1, source_target_pairs={{0,3},{1,0},{2,1},{3,2},{4,7},{5,4},{6,5},{7,6},{8,11},{9,8},{10,9... | collective-permute-start | bytes 98312 | tf_op jit(solution)/shard_map/ppermute | solution.py:24
  18.9 12.7 %copy-start.21 = (f32[4,4]{1,0:T(4,128)S(1)}, f32[4,4]{1,0:T(4,128)}, u32[]{:S(2)}) copy-start(f32[4,4]{1,0:T(4,128)} %get-tuple-element.53) | copy-start | bytes 196
  18.9 12.7 %copy-start.22 = (f32[4,4]{1,0:T(4,128)S(1)}, f32[4,4]{1,0:T(4,128)}, u32[]{:S(2)}) copy-start(f32[4,4]{1,0:T(4,128)} %get-tuple-element.54) | copy-start | bytes 196
  18.9 4.6 %collective-permute-start.6 = (f32[4,2,4,4,128]{4,2,1,3,0:T(4,128)S(1)}, f32[4,2,4,4,128]{4,2,1,3,0:T(4,128)S(1)}, u32[]{:S(2)}, u32[]{:S(2)}) collective-permute-start(f32[4,2,4,4,128]{4,2,1,3,0:T(4,128)S(1)} %pad_maximum_fusion.53), channel_id=1, source_target_pairs={{0,4},{4,0},{1,5},{5,1},{2,6},{6,2},{3,7},{7,3},{8,12},{12,8},{9,1... | collective-permute-start | bytes 196616 | tf_op jit(solution)/shard_map/ppermute | solution.py:36
  19.5 3.4 %collective-permute-start.5 = (f32[4,4,1,4,128]{4,2,1,3,0:T(1,128)S(1)}, f32[4,4,1,4,128]{4,2,1,3,0:T(1,128)S(1)}, u32[]{:S(2)}, u32[]{:S(2)}) collective-permute-start(f32[4,4,1,4,128]{4,2,1,3,0:T(1,128)S(1)} %get-tuple-element.35), channel_id=1, source_target_pairs={{0,1},{1,2},{2,3},{3,0},{4,5},{5,6},{6,7},{7,4},{8,9},{9,10},{10,1... | collective-permute-start | bytes 98312 | tf_op jit(solution)/shard_map/ppermute | solution.py:24
  19.7 3.9 %collective-permute-start.8 = (f32[1,4,4,4,128]{4,2,1,3,0:T(4,128)S(1)}, f32[1,4,4,4,128]{4,2,1,3,0:T(4,128)S(1)}, u32[]{:S(2)}, u32[]{:S(2)}) collective-permute-start(f32[1,4,4,4,128]{4,2,1,3,0:T(4,128)S(1)} %get-tuple-element.38), channel_id=1, source_target_pairs={{0,24},{8,0},{16,8},{24,16},{1,25},{9,1},{17,9},{25,17},{2,26},{10... | collective-permute-start | bytes 98312 | tf_op jit(solution)/shard_map/ppermute | solution.py:24
  21.2 5.7 %collective-permute-start.7 = (f32[1,4,4,4,128]{4,2,1,3,0:T(4,128)S(1)}, f32[1,4,4,4,128]{4,2,1,3,0:T(4,128)S(1)}, u32[]{:S(2)}, u32[]{:S(2)}) collective-permute-start(f32[1,4,4,4,128]{4,2,1,3,0:T(4,128)S(1)} %get-tuple-element.37), channel_id=1, source_target_pairs={{0,8},{8,16},{16,24},{24,0},{1,9},{9,17},{17,25},{25,1},{2,10},{10... | collective-permute-start | bytes 98312 | tf_op jit(solution)/shard_map/ppermute | solution.py:24
  23.5 3.6 %copy-start.7 = (f32[6,1,4,4,128]{4,2,1,3,0:T(4,128)}, f32[6,1,4,4,128]{4,2,1,3,0:T(4,128)S(1)}, u32[]{:S(2)}) copy-start(f32[6,1,4,4,128]{4,2,1,3,0:T(4,128)S(1)} %pad.46) | copy-start | bytes 147460
  23.5 3.6 %copy-start.9 = (f32[6,1,4,4,128]{4,2,1,3,0:T(4,128)}, f32[6,1,4,4,128]{4,2,1,3,0:T(4,128)S(1)}, u32[]{:S(2)}) copy-start(f32[6,1,4,4,128]{4,2,1,3,0:T(4,128)S(1)} %pad.45) | copy-start | bytes 147460
  23.6 3.8 %copy-start.13 = (f32[1,4,4,4,128]{4,2,1,3,0:T(4,128)}, f32[1,4,4,4,128]{4,2,1,3,0:T(4,128)S(1)}, u32[]{:S(2)}) copy-start(f32[1,4,4,4,128]{4,2,1,3,0:T(4,128)S(1)} %collective-permute-done.8) | copy-start | bytes 98308
  26.9 15.6 %copy-start.15 = (f32[1,4,4,4,128]{4,2,1,3,0:T(4,128)}, f32[1,4,4,4,128]{4,2,1,3,0:T(4,128)S(1)}, u32[]{:S(2)}) copy-start(f32[1,4,4,4,128]{4,2,1,3,0:T(4,128)S(1)} %collective-permute-done.7) | copy-start | bytes 98308
  27.7 14.8 %copy-start.12 = (f32[2,2,2,4,128]{4,2,1,3,0:T(2,128)}, f32[2,2,2,4,128]{4,2,1,3,0:T(2,128)S(1)}, u32[]{:S(2)}) copy-start(f32[2,2,2,4,128]{4,2,1,3,0:T(2,128)S(1)} %add_multiply_fusion) | copy-start | bytes 49156
  27.7 7.3 %collective-permute-start.12 = (f32[10,2,2,4,128]{4,2,1,3,0:T(2,128)S(1)}, f32[10,2,2,4,128]{4,2,1,3,0:T(2,128)S(1)}, u32[]{:S(2)}, u32[]{:S(2)}) collective-permute-start(f32[10,2,2,4,128]{4,2,1,3,0:T(2,128)S(1)} %pad_maximum_fusion.52), channel_id=1, source_target_pairs={{0,8},{8,16},{16,24},{24,0},{1,9},{9,17},{17,25},{25,1},{2,10},{10... | collective-permute-start | bytes 245768 | tf_op jit(solution)/shard_map/ppermute | solution.py:24
  27.8 9.8 %collective-permute-start.11 = (f32[10,2,2,4,128]{4,2,1,3,0:T(2,128)S(1)}, f32[10,2,2,4,128]{4,2,1,3,0:T(2,128)S(1)}, u32[]{:S(2)}, u32[]{:S(2)}) collective-permute-start(f32[10,2,2,4,128]{4,2,1,3,0:T(2,128)S(1)} %pad_maximum_fusion.52), channel_id=1, source_target_pairs={{0,16},{8,24},{16,0},{24,8},{1,17},{9,25},{17,1},{25,9},{2,18},{10... | collective-permute-start | bytes 245768 | tf_op jit(solution)/shard_map/ppermute | solution.py:24
  28.5 9.1 %collective-permute-start.10 = (f32[10,2,2,4,128]{4,2,1,3,0:T(2,128)S(1)}, f32[10,2,2,4,128]{4,2,1,3,0:T(2,128)S(1)}, u32[]{:S(2)}, u32[]{:S(2)}) collective-permute-start(f32[10,2,2,4,128]{4,2,1,3,0:T(2,128)S(1)} %pad_maximum_fusion.52), channel_id=1, source_target_pairs={{0,24},{8,0},{16,8},{24,16},{1,25},{9,1},{17,9},{25,17},{2,26},{10... | collective-permute-start | bytes 245768 | tf_op jit(solution)/shard_map/ppermute | solution.py:24
  35.0 7.5 %copy-start.17 = (f32[2,2,2,4,128]{4,2,1,3,0:T(2,128)}, f32[2,2,2,4,128]{4,2,1,3,0:T(2,128)S(1)}, u32[]{:S(2)}) copy-start(f32[2,2,2,4,128]{4,2,1,3,0:T(2,128)S(1)} %slice.363) | copy-start | bytes 49156
  37.6 4.9 %copy-start.18 = (f32[2,2,2,4,128]{4,2,1,3,0:T(2,128)}, f32[2,2,2,4,128]{4,2,1,3,0:T(2,128)S(1)}, u32[]{:S(2)}) copy-start(f32[2,2,2,4,128]{4,2,1,3,0:T(2,128)S(1)} %slice.362) | copy-start | bytes 49156
  37.6 9.2 %copy-start.19 = (f32[2,2,2,4,128]{4,2,1,3,0:T(2,128)}, f32[2,2,2,4,128]{4,2,1,3,0:T(2,128)S(1)}, u32[]{:S(2)}) copy-start(f32[2,2,2,4,128]{4,2,1,3,0:T(2,128)S(1)} %slice.361) | copy-start | bytes 49156
  38.3 4.9 %collective-permute-start.19 = (f32[8,2,2,4,128]{4,2,1,3,0:T(2,128)}, f32[8,2,2,4,128]{4,2,1,3,0:T(2,128)S(1)}, u32[]{:S(2)}, u32[]{:S(2)}) collective-permute-start(f32[8,2,2,4,128]{4,2,1,3,0:T(2,128)} %pad_maximum_fusion.54), channel_id=1, source_target_pairs={{7,0},{4,1},{5,2},{6,3},{3,4},{0,5},{1,6},{2,7},{15,8},{12,9},{13,... | collective-permute-start | bytes 196616 | tf_op jit(solution)/shard_map/ppermute | solution.py:107
  38.3 6.1 %collective-permute-start.18 = (f32[8,2,2,4,128]{4,2,1,3,0:T(2,128)}, f32[8,2,2,4,128]{4,2,1,3,0:T(2,128)S(1)}, u32[]{:S(2)}, u32[]{:S(2)}) collective-permute-start(f32[8,2,2,4,128]{4,2,1,3,0:T(2,128)} %pad_maximum_fusion.54), channel_id=1, source_target_pairs={{6,0},{7,1},{4,2},{5,3},{2,4},{3,5},{0,6},{1,7},{14,8},{15,9},{12,... | collective-permute-start | bytes 196616 | tf_op jit(solution)/shard_map/ppermute | solution.py:107
  39.6 10.6 %collective-permute-start.17 = (f32[8,2,2,4,128]{4,2,1,3,0:T(2,128)}, f32[8,2,2,4,128]{4,2,1,3,0:T(2,128)}, u32[]{:S(2)}, u32[]{:S(2)}) collective-permute-start(f32[8,2,2,4,128]{4,2,1,3,0:T(2,128)} %pad_maximum_fusion.54), channel_id=1, source_target_pairs={{5,0},{6,1},{7,2},{4,3},{1,4},{2,5},{3,6},{0,7},{13,8},{14,9},{15,... | collective-permute-start | bytes 196616 | tf_op jit(solution)/shard_map/ppermute | solution.py:107
  42.0 8.3 %collective-permute-start.16 = (f32[8,2,2,4,128]{4,2,1,3,0:T(2,128)}, f32[8,2,2,4,128]{4,2,1,3,0:T(2,128)}, u32[]{:S(2)}, u32[]{:S(2)}) collective-permute-start(f32[8,2,2,4,128]{4,2,1,3,0:T(2,128)} %pad_maximum_fusion.54), channel_id=1, source_target_pairs={{4,0},{5,1},{6,2},{7,3},{0,4},{1,5},{2,6},{3,7},{12,8},{13,9},{14,... | collective-permute-start | bytes 196616 | tf_op jit(solution)/shard_map/ppermute | solution.py:107
  42.5 7.8 %collective-permute-start.15 = (f32[8,2,2,4,128]{4,2,1,3,0:T(2,128)}, f32[8,2,2,4,128]{4,2,1,3,0:T(2,128)}, u32[]{:S(2)}, u32[]{:S(2)}) collective-permute-start(f32[8,2,2,4,128]{4,2,1,3,0:T(2,128)} %pad_maximum_fusion.54), channel_id=1, source_target_pairs={{3,0},{0,1},{1,2},{2,3},{7,4},{4,5},{5,6},{6,7},{11,8},{8,9},{9,10... | collective-permute-start | bytes 196616 | tf_op jit(solution)/shard_map/ppermute | solution.py:107
  43.2 3.7 %copy-start.24 = (f32[8,2,2,4,128]{4,2,1,3,0:T(2,128)}, f32[8,2,2,4,128]{4,2,1,3,0:T(2,128)S(1)}, u32[]{:S(2)}) copy-start(f32[8,2,2,4,128]{4,2,1,3,0:T(2,128)S(1)} %collective-permute-done.19) | copy-start | bytes 196612
  43.2 7.1 %collective-permute-start.14 = (f32[8,2,2,4,128]{4,2,1,3,0:T(2,128)}, f32[8,2,2,4,128]{4,2,1,3,0:T(2,128)}, u32[]{:S(2)}, u32[]{:S(2)}) collective-permute-start(f32[8,2,2,4,128]{4,2,1,3,0:T(2,128)} %pad_maximum_fusion.54), channel_id=1, source_target_pairs={{2,0},{3,1},{0,2},{1,3},{6,4},{7,5},{4,6},{5,7},{10,8},{11,9},{8,1... | collective-permute-start | bytes 196616 | tf_op jit(solution)/shard_map/ppermute | solution.py:107
  45.0 5.3 %collective-permute-start.13 = (f32[8,2,2,4,128]{4,2,1,3,0:T(2,128)}, f32[8,2,2,4,128]{4,2,1,3,0:T(2,128)}, u32[]{:S(2)}, u32[]{:S(2)}) collective-permute-start(f32[8,2,2,4,128]{4,2,1,3,0:T(2,128)} %pad_maximum_fusion.54), channel_id=1, source_target_pairs={{1,0},{2,1},{3,2},{0,3},{5,4},{6,5},{7,6},{4,7},{9,8},{10,9},{11,1... | collective-permute-start | bytes 196616 | tf_op jit(solution)/shard_map/ppermute | solution.py:107
  50.2 2.1 %copy-start.8 = (f32[6,1,4,4,128]{4,2,1,3,0:T(4,128)S(1)}, f32[6,1,4,4,128]{4,2,1,3,0:T(4,128)}, u32[]{:S(2)}) copy-start(f32[6,1,4,4,128]{4,2,1,3,0:T(4,128)} %copy-done.7) | copy-start | bytes 147460
  50.2 2.1 %copy-start.10 = (f32[6,1,4,4,128]{4,2,1,3,0:T(4,128)S(1)}, f32[6,1,4,4,128]{4,2,1,3,0:T(4,128)}, u32[]{:S(2)}) copy-start(f32[6,1,4,4,128]{4,2,1,3,0:T(4,128)} %copy-done.9) | copy-start | bytes 147460
  50.2 2.1 %copy-start.14 = (f32[1,4,4,4,128]{4,2,1,3,0:T(4,128)S(1)}, f32[1,4,4,4,128]{4,2,1,3,0:T(4,128)}, u32[]{:S(2)}) copy-start(f32[1,4,4,4,128]{4,2,1,3,0:T(4,128)} %copy-done.13) | copy-start | bytes 98308
  50.2 2.1 %copy-start.16 = (f32[1,4,4,4,128]{4,2,1,3,0:T(4,128)S(1)}, f32[1,4,4,4,128]{4,2,1,3,0:T(4,128)}, u32[]{:S(2)}) copy-start(f32[1,4,4,4,128]{4,2,1,3,0:T(4,128)} %copy-done.15) | copy-start | bytes 98308
  52.9 5.6 %collective-permute-start.24 = (f32[4,4,1,4,128]{4,2,1,3,0:T(1,128)S(1)}, f32[4,4,1,4,128]{4,2,1,3,0:T(1,128)S(1)}, u32[]{:S(2)}, u32[]{:S(2)}) collective-permute-start(f32[4,4,1,4,128]{4,2,1,3,0:T(1,128)S(1)} %get-tuple-element.30), channel_id=1, source_target_pairs={{0,1},{1,2},{2,3},{3,0},{4,5},{5,6},{6,7},{7,4},{8,9},{9,10},{10,1... | collective-permute-start | bytes 98312 | tf_op jit(solution)/shard_map/ppermute | solution.py:24
  53.0 9.7 %collective-permute-start.22 = (f32[4,2,4,4,128]{4,2,1,3,0:T(4,128)S(1)}, f32[4,2,4,4,128]{4,2,1,3,0:T(4,128)S(1)}, u32[]{:S(2)}, u32[]{:S(2)}) collective-permute-start(f32[4,2,4,4,128]{4,2,1,3,0:T(4,128)S(1)} %pad_maximum_fusion.55), channel_id=1, source_target_pairs={{0,4},{4,0},{1,5},{5,1},{2,6},{6,2},{3,7},{7,3},{8,12},{12,8},{9,1... | collective-permute-start | bytes 196616 | tf_op jit(solution)/shard_map/ppermute | solution.py:36
  54.6 4.8 %collective-permute-start.20 = (f32[1,4,4,4,128]{4,2,1,3,0:T(4,128)S(1)}, f32[1,4,4,4,128]{4,2,1,3,0:T(4,128)S(1)}, u32[]{:S(2)}, u32[]{:S(2)}) collective-permute-start(f32[1,4,4,4,128]{4,2,1,3,0:T(4,128)S(1)} %get-tuple-element.32), channel_id=1, source_target_pairs={{0,24},{8,0},{16,8},{24,16},{1,25},{9,1},{17,9},{25,17},{2,26},{10... | collective-permute-start | bytes 98312 | tf_op jit(solution)/shard_map/ppermute | solution.py:24
  56.7 5.7 %collective-permute-start.21 = (f32[1,4,4,4,128]{4,2,1,3,0:T(4,128)S(1)}, f32[1,4,4,4,128]{4,2,1,3,0:T(4,128)S(1)}, u32[]{:S(2)}, u32[]{:S(2)}) collective-permute-start(f32[1,4,4,4,128]{4,2,1,3,0:T(4,128)S(1)} %get-tuple-element.31), channel_id=1, source_target_pairs={{0,8},{8,16},{16,24},{24,0},{1,9},{9,17},{17,25},{25,1},{2,10},{10... | collective-permute-start | bytes 98312 | tf_op jit(solution)/shard_map/ppermute | solution.py:24
  56.7 5.8 %collective-permute-start.23 = (f32[4,4,1,4,128]{4,2,1,3,0:T(1,128)S(1)}, f32[4,4,1,4,128]{4,2,1,3,0:T(1,128)S(1)}, u32[]{:S(2)}, u32[]{:S(2)}) collective-permute-start(f32[4,4,1,4,128]{4,2,1,3,0:T(1,128)S(1)} %get-tuple-element.29), channel_id=1, source_target_pairs={{0,3},{1,0},{2,1},{3,2},{4,7},{5,4},{6,5},{7,6},{8,11},{9,8},{10,9... | collective-permute-start | bytes 98312 | tf_op jit(solution)/shard_map/ppermute | solution.py:24
  58.5 3.9 %copy-start.4 = (f32[1,8,8,4,128]{4,2,1,3,0:T(8,128)S(1)}, f32[1,8,8,4,128]{4,2,1,3,0:T(8,128)}, u32[]{:S(2)}) copy-start(f32[1,8,8,4,128]{4,2,1,3,0:T(8,128)} %copy-done.3) | copy-start | bytes 393220
  (3 other events, 2.5 us)

commit v22 on v19

--- a/solution.py
+++ b/solution.py
@@ -24,10 +24,13 @@
     return lax.ppermute(block, axis, [(j, (j - step) % count) for j in range(count)])
 
 
-def axis_faces(block, axis, dim, prepare=None):
+def axis_faces(block, axis, dim, prepare=None, slabs=None):
     count = lax.axis_size(axis)
-    first = lax.slice_in_dim(block, 0, 1, axis=dim)
-    last = lax.slice_in_dim(block, block.shape[dim] - 1, None, axis=dim)
+    if slabs is not None:
+        first, last = slabs
+    else:
+        first = lax.slice_in_dim(block, 0, 1, axis=dim)
+        last = lax.slice_in_dim(block, block.shape[dim] - 1, None, axis=dim)
     if prepare is not None:
         first = prepare(first)
         last = prepare(last)
@@ -324,7 +327,19 @@
     updated_padded = padded_one + coarse_padded
     updated = updated_padded[1:-1, 1:-1, 1:-1]
     post_one = updated + omega * (rhs_one - padded_stencil(updated_padded, 1)) / center
-    return post_smooth(0, corr_zero, faces_zero, rhs_zero, post_one, all_faces(post_one)), tiles_by_step
+    slabs = []
+    for dim in range(3):
+        pair = []
+        for lo_side in (True, False):
+            size = updated_padded.shape[dim]
+            part = lax.slice_in_dim(updated_padded, 0 if lo_side else size - 3, 3 if lo_side else size, axis=dim)
+            inner = rhs_one.shape[dim]
+            rhs = lax.slice_in_dim(rhs_one, 0 if lo_side else inner - 1, 1 if lo_side else inner, axis=dim)
+            mid = part[1:-1, 1:-1, 1:-1]
+            pair.append(mid + omega * (rhs - padded_stencil(part, 1)) / center)
+        slabs.append(tuple(pair))
+    faces_one = [axis_faces(None, axis, dim, slabs=slabs[dim]) for axis, dim in GRID_AXES]
+    return post_smooth(0, corr_zero, faces_zero, rhs_zero, post_one, faces_one), tiles_by_step
 
 
 def body(residuals, patch_box, tile_pairs, inv_tiles):

time: 66.4 us -> 67 us (level)
  no operation moved by 1% of the time
where the time goes in v22:
time: 67 us; the launch traced here: 66.8 us
  starting transfers between devices  26.6 us (40%)
  waiting for transfers between devices  18.7 us (28%)
  local copies, waits for them, and re-layouts  8.34 us (12%)
  other arithmetic  8.33 us (12%)
  matrix products  3.73 us (6%)
  between operations  1.06 us (2%)
    ppermute x15, waiting for transfers between devices, shifted(): lax.ppermute(block, axis, [(j, (j - step) % count) for j in range(count)])  17.6 us
    ppermute x15, starting transfers between devices, shifted(): lax.ppermute(block, axis, [(j, (j - step) % count) for j in range(count)])  15 us
    ppermute x7, starting transfers between devices, fetch(): cache[steps] = lax.ppermute(block, tuple(axes), pairs)  6.86 us
    ppermute x3, starting transfers between devices, axis_faces(): lax.ppermute(jnp.concatenate([first, last], axis=dim), axis, [(0, 1), (1,...  4.75 us
    dot_general x1, matrix products, coarse_solve(): jnp.einsum('qxyz,xyzgl->qgl', operator, extended, precision=lax.Precision...  1.92 us
    dot_general x1, matrix products, body(): jnp.dot(rows, gram, precision=lax.Precision.HIGH, preferred_element_type=...  1.81 us
    reduce_sum x1, local copies, waits for them, and re-layouts, gram_matrix(): return spread.sum(axis=0).reshape(orb_count, orb_count)  1.69 us
    reshape x1, local copies, waits for them, and re-layouts, gram_matrix(): return spread.sum(axis=0).reshape(orb_count, orb_count)  1.64 us
  transfers between devices with their start and end apart: 25, of which 9 were waited for; matrix products, arithmetic and copies ran while one was open for 11% of the time, Pallas kernels for 0%

profile of v22, /device:TPU:0, one launch (start us, length us, event | category | flops | bytes accessed | tf_op | source)
XLA Modules:
  0.0 66.8 jit_solution(11288039232376294707)
XLA Ops:
  0.0 1.5 %fusion.57 = (f32[8,8,1,4,128]{4,2,1,3,0:T(1,128)S(1)}, f32[8,8,1,4,128]{4,2,1,3,0:T(1,128)S(1)}) fusion(bf16[8,8,8,512]{3,2,1,0:T(8,128)(2,1)} %param.5), kind=kLoop, calls=%fused_computation.135 | loop fusion | flops 131072 | bytes 786432 | tf_op jit(solution)/shard_map/div | solution.py:317
  1.6 0.5 collective-permute-start.4
  2.2 2.6 %collective-permute-start.2 = (f32[8,2,8,4,128]{4,2,1,3,0:T(8,128)S(1)}, f32[8,2,8,4,128]{4,2,1,3,0:T(8,128)S(1)}, u32[]{:S(2)}, u32[]{:S(2)}) collective-permute-start(f32[8,2,8,4,128]{4,2,1,3,0:T(8,128)S(1)} %pad_maximum_fusion.32), channel_id=1, source_target_pairs={{0,4},{4,0},{1,5},{5,1},{2,6},{6,2},{3,7},{7,3},{8,12},{12,8},{9,1... | collective-permute-start | bytes 786440 | tf_op jit(solution)/shard_map/ppermute | solution.py:40
  4.8 3.7 %collective-permute-start = (f32[1,8,8,4,128]{4,2,1,3,0:T(8,128)S(1)}, f32[1,8,8,4,128]{4,2,1,3,0:T(8,128)S(1)}, u32[]{:S(2)}, u32[]{:S(2)}) collective-permute-start(f32[1,8,8,4,128]{4,2,1,3,0:T(8,128)S(1)} %copy.38), channel_id=1, source_target_pairs={{0,24},{8,0},{16,8},{24,16},{1,25},{9,1},{17,9},{25,17},{2,26},{10... | collective-permute-start | bytes 393224 | tf_op jit(solution)/shard_map/ppermute | solution.py:24
  8.6 1.2 %collective-permute-start.3 = (f32[8,8,1,4,128]{4,2,1,3,0:T(1,128)S(1)}, f32[8,8,1,4,128]{4,2,1,3,0:T(1,128)S(1)}, u32[]{:S(2)}, u32[]{:S(2)}) collective-permute-start(f32[8,8,1,4,128]{4,2,1,3,0:T(1,128)S(1)} %get-tuple-element.15), channel_id=1, source_target_pairs={{0,3},{1,0},{2,1},{3,2},{4,7},{5,4},{6,5},{7,6},{8,11},{9,8},{10,9... | collective-permute-start | bytes 393224 | tf_op jit(solution)/shard_map/ppermute | solution.py:24
  10.1 0.6 gather_fusion
  11.3 0.7 %fusion.86 = (f32[4,4]{1,0:T(4,128)}, f32[4,4]{1,0:T(4,128)}) fusion(s32[4]{0:T(128)S(1)} %get-tuple-element.5, s32[4]{0:T(128)S(1)} %get-tuple-element.6), kind=kLoop, calls=%fused_computation.225 | loop fusion | flops 64 | bytes 160 | tf_op jit(solution)/shard_map/convert_element_type | solution.py:309
  12.2 4.4 %collective-permute-done.1 = f32[1,8,8,4,128]{4,2,1,3,0:T(8,128)S(1)} collective-permute-done((f32[1,8,8,4,128]{4,2,1,3,0:T(8,128)S(1)}, f32[1,8,8,4,128]{4,2,1,3,0:T(8,128)S(1)}, u32[]{:S(2)}, u32[]{:S(2)}) %collective-permute-start.1) | collective-permute-done | bytes 131104 | tf_op jit(solution)/shard_map/ppermute | solution.py:24
  16.7 1.0 %convert_subtract_fusion.1 = f32[8,8,8,4,128]{4,2,1,3,0:T(8,128)S(1)} fusion(f32[8,8,1,4,128]{4,2,1,3,0:T(1,128)S(1)} %collective-permute-done.4, f32[10,1,8,4,128]{4,2,1,3,0:T(8,128)S(1)} %pad.40, f32[10,1,8,4,128]{4,2,1,3,0:T(8,128)S(1)} %pad.41, f32[1,8,8,4,128]{4,2,1,3,0:T(8,128)S(1)} %collective-permute-done, ...), kind=kLoop, calls=%fused_computation.3 | loop fusion | flops 8912896 | bytes 3473408 | tf_op jit(solution)/shard_map/sub | solution.py:320
  17.8 0.4 slice.465
  18.2 0.4 slice.466
  19.0 0.6 collective-permute-start.6
  19.5 0.2 collective-permute-start.5
  19.8 1.5 %collective-permute-start.8 = (f32[1,4,4,4,128]{4,2,1,3,0:T(4,128)S(1)}, f32[1,4,4,4,128]{4,2,1,3,0:T(4,128)S(1)}, u32[]{:S(2)}, u32[]{:S(2)}) collective-permute-start(f32[1,4,4,4,128]{4,2,1,3,0:T(4,128)S(1)} %get-tuple-element.28), channel_id=1, source_target_pairs={{0,24},{8,0},{16,8},{24,16},{1,25},{9,1},{17,9},{25,17},{2,26},{10... | collective-permute-start | bytes 98312 | tf_op jit(solution)/shard_map/ppermute | solution.py:24
  21.2 0.6 collective-permute-start.7
  21.8 1.1 %collective-permute-done.5 = f32[4,4,1,4,128]{4,2,1,3,0:T(1,128)S(1)} collective-permute-done((f32[4,4,1,4,128]{4,2,1,3,0:T(1,128)S(1)}, f32[4,4,1,4,128]{4,2,1,3,0:T(1,128)S(1)}, u32[]{:S(2)}, u32[]{:S(2)}) %collective-permute-start.5) | collective-permute-done | bytes 32800 | tf_op jit(solution)/shard_map/ppermute | solution.py:24
  23.0 0.6 collective-permute-done.6
  23.7 3.3 %collective-permute-done.7 = f32[1,4,4,4,128]{4,2,1,3,0:T(4,128)S(1)} collective-permute-done((f32[1,4,4,4,128]{4,2,1,3,0:T(4,128)S(1)}, f32[1,4,4,4,128]{4,2,1,3,0:T(4,128)S(1)}, u32[]{:S(2)}, u32[]{:S(2)}) %collective-permute-start.7) | collective-permute-done | bytes 32800 | tf_op jit(solution)/shard_map/ppermute | solution.py:24
  26.9 0.2 fusion.51
  27.2 0.2 slice.485
  27.5 0.2 slice.486
  27.8 0.7 %collective-permute-start.11 = (f32[10,2,2,4,128]{4,2,1,3,0:T(2,128)S(1)}, f32[10,2,2,4,128]{4,2,1,3,0:T(2,128)S(1)}, u32[]{:S(2)}, u32[]{:S(2)}) collective-permute-start(f32[10,2,2,4,128]{4,2,1,3,0:T(2,128)S(1)} %pad_maximum_fusion.52), channel_id=1, source_target_pairs={{0,16},{8,24},{16,0},{24,8},{1,17},{9,25},{17,1},{25,9},{2,18},{10... | collective-permute-start | bytes 245768 | tf_op jit(solution)/shard_map/ppermute | solution.py:24
  28.5 3.1 %collective-permute-start.10 = (f32[10,2,2,4,128]{4,2,1,3,0:T(2,128)S(1)}, f32[10,2,2,4,128]{4,2,1,3,0:T(2,128)S(1)}, u32[]{:S(2)}, u32[]{:S(2)}) collective-permute-start(f32[10,2,2,4,128]{4,2,1,3,0:T(2,128)S(1)} %pad_maximum_fusion.52), channel_id=1, source_target_pairs={{0,24},{8,0},{16,8},{24,16},{1,25},{9,1},{17,9},{25,17},{2,26},{10... | collective-permute-start | bytes 245768 | tf_op jit(solution)/shard_map/ppermute | solution.py:24
  31.7 3.3 %collective-permute-done.12 = f32[10,2,2,4,128]{4,2,1,3,0:T(2,128)S(1)} collective-permute-done((f32[10,2,2,4,128]{4,2,1,3,0:T(2,128)S(1)}, f32[10,2,2,4,128]{4,2,1,3,0:T(2,128)S(1)}, u32[]{:S(2)}, u32[]{:S(2)}) %collective-permute-start.12) | collective-permute-done | bytes 81952 | tf_op jit(solution)/shard_map/ppermute | solution.py:24
  35.0 2.6 %collective-permute-done.11 = f32[10,2,2,4,128]{4,2,1,3,0:T(2,128)S(1)} collective-permute-done((f32[10,2,2,4,128]{4,2,1,3,0:T(2,128)S(1)}, f32[10,2,2,4,128]{4,2,1,3,0:T(2,128)S(1)}, u32[]{:S(2)}, u32[]{:S(2)}) %collective-permute-start.11) | collective-permute-done | bytes 81952 | tf_op jit(solution)/shard_map/ppermute | solution.py:24
  37.7 0.7 pad_maximum_fusion.54
  38.3 1.3 %collective-permute-start.18 = (f32[8,2,2,4,128]{4,2,1,3,0:T(2,128)}, f32[8,2,2,4,128]{4,2,1,3,0:T(2,128)S(1)}, u32[]{:S(2)}, u32[]{:S(2)}) collective-permute-start(f32[8,2,2,4,128]{4,2,1,3,0:T(2,128)} %pad_maximum_fusion.54), channel_id=1, source_target_pairs={{6,0},{7,1},{4,2},{5,3},{2,4},{3,5},{0,6},{1,7},{14,8},{15,9},{12,... | collective-permute-start | bytes 196616 | tf_op jit(solution)/shard_map/ppermute | solution.py:111
  39.7 2.4 %collective-permute-start.17 = (f32[8,2,2,4,128]{4,2,1,3,0:T(2,128)}, f32[8,2,2,4,128]{4,2,1,3,0:T(2,128)}, u32[]{:S(2)}, u32[]{:S(2)}) collective-permute-start(f32[8,2,2,4,128]{4,2,1,3,0:T(2,128)} %pad_maximum_fusion.54), channel_id=1, source_target_pairs={{5,0},{6,1},{7,2},{4,3},{1,4},{2,5},{3,6},{0,7},{13,8},{14,9},{15,... | collective-permute-start | bytes 196616 | tf_op jit(solution)/shard_map/ppermute | solution.py:111
  42.0 0.5 collective-permute-start.16
  42.7 0.5 collective-permute-done.19
  43.2 1.2 %collective-permute-start.14 = (f32[8,2,2,4,128]{4,2,1,3,0:T(2,128)}, f32[8,2,2,4,128]{4,2,1,3,0:T(2,128)}, u32[]{:S(2)}, u32[]{:S(2)}) collective-permute-start(f32[8,2,2,4,128]{4,2,1,3,0:T(2,128)} %pad_maximum_fusion.54), channel_id=1, source_target_pairs={{2,0},{3,1},{0,2},{1,3},{6,4},{7,5},{4,6},{5,7},{10,8},{11,9},{8,1... | collective-permute-start | bytes 196616 | tf_op jit(solution)/shard_map/ppermute | solution.py:111
  44.4 0.6 copy-done.25
  45.1 1.4 %collective-permute-start.13 = (f32[8,2,2,4,128]{4,2,1,3,0:T(2,128)}, f32[8,2,2,4,128]{4,2,1,3,0:T(2,128)}, u32[]{:S(2)}, u32[]{:S(2)}) collective-permute-start(f32[8,2,2,4,128]{4,2,1,3,0:T(2,128)} %pad_maximum_fusion.54), channel_id=1, source_target_pairs={{1,0},{2,1},{3,2},{0,3},{5,4},{6,5},{7,6},{4,7},{9,8},{10,9},{11,1... | collective-permute-start | bytes 196616 | tf_op jit(solution)/shard_map/ppermute | solution.py:111
  46.5 0.4 multiply_reduce_fusion
  46.9 1.7 %copy.52 = f32[4,128,4,128]{3,2,1,0:T(4,128)} copy(f32[4,128,4,128]{3,1,2,0:T(8,128)S(1)} %multiply_reduce_fusion) | data formatting | bytes 2097152 | tf_op jit(solution)/shard_map/reduce_sum | solution.py:312
  48.6 1.6 %reshape.595 = f32[512,512,1,1]{1,0,2,3:T(8,128)S(1)} reshape(f32[4,128,4,128]{3,2,1,0:T(4,128)} %copy.52) | data formatting | bytes 2097152 | tf_op jit(solution)/shard_map/reshape | solution.py:312
  50.3 1.9 %convolution_bitcast_fusion = f32[216,4,128]{2,0,1:T(8,128)S(1)} fusion(f32[216,8,4,8,1]{0,3,2,4,1:T(8,128)} %constant.155, f32[8,2,2,4,128]{4,2,1,3,0:T(2,128)} %copy-done.24, f32[8,2,2,4,128]{4,2,1,3,0:T(2,128)} %copy-done.25, f32[8,2,2,4,128]{4,2,1,3,0:T(2,128)} %collective-permute-done.17, f32[8,2,2,4,128]{4,2,1,3,0:T(2,128)} %collective-permute-done.16, ...), kind=kOutput, calls=%fused_computation.7 | convolution fusion | flops 341049344 | bytes 1187840 | tf_op jit(solution)/shard_map/qxyz,xyzgl->qgl/dot_general | solution.py:201
  52.4 0.2 maximum_add_fusion
  52.9 0.4 fusion.65
  53.5 1.6 %collective-permute-start.22 = (f32[4,2,4,4,128]{4,2,1,3,0:T(4,128)S(1)}, f32[4,2,4,4,128]{4,2,1,3,0:T(4,128)S(1)}, u32[]{:S(2)}, u32[]{:S(2)}) collective-permute-start(f32[4,2,4,4,128]{4,2,1,3,0:T(4,128)S(1)} %pad_maximum_fusion.55), channel_id=1, source_target_pairs={{0,4},{4,0},{1,5},{5,1},{2,6},{6,2},{3,7},{7,3},{8,12},{12,8},{9,1... | collective-permute-start | bytes 196616 | tf_op jit(solution)/shard_map/ppermute | solution.py:40
  55.1 2.1 %collective-permute-start.20 = (f32[1,4,4,4,128]{4,2,1,3,0:T(4,128)S(1)}, f32[1,4,4,4,128]{4,2,1,3,0:T(4,128)S(1)}, u32[]{:S(2)}, u32[]{:S(2)}) collective-permute-start(f32[1,4,4,4,128]{4,2,1,3,0:T(4,128)S(1)} %get-tuple-element.12), channel_id=1, source_target_pairs={{0,24},{8,0},{16,8},{24,16},{1,25},{9,1},{17,9},{25,17},{2,26},{10... | collective-permute-start | bytes 98312 | tf_op jit(solution)/shard_map/ppermute | solution.py:24
  57.2 1.2 %collective-permute-start.23 = (f32[4,4,1,4,128]{4,2,1,3,0:T(1,128)S(1)}, f32[4,4,1,4,128]{4,2,1,3,0:T(1,128)S(1)}, u32[]{:S(2)}, u32[]{:S(2)}) collective-permute-start(f32[4,4,1,4,128]{4,2,1,3,0:T(1,128)S(1)} %get-tuple-element.9), channel_id=1, source_target_pairs={{0,3},{1,0},{2,1},{3,2},{4,7},{5,4},{6,5},{7,6},{8,11},{9,8},{10,9... | collective-permute-start | bytes 98312 | tf_op jit(solution)/shard_map/ppermute | solution.py:24
  58.5 0.4 broadcast_in_dim.88
  59.2 0.6 copy-done.2
  60.1 2.9 %collective-permute-done.21 = f32[1,4,4,4,128]{4,2,1,3,0:T(4,128)S(1)} collective-permute-done((f32[1,4,4,4,128]{4,2,1,3,0:T(4,128)S(1)}, f32[1,4,4,4,128]{4,2,1,3,0:T(4,128)S(1)}, u32[]{:S(2)}, u32[]{:S(2)}) %collective-permute-start.21) | collective-permute-done | bytes 32800 | tf_op jit(solution)/shard_map/ppermute | solution.py:24
  63.5 1.0 %fusion.2 = f32[8,8,8,4,128]{4,2,1,3,0:T(8,128)S(1)} fusion(f32[8,8,8,4,128]{4,2,1,3,0:T(8,128)S(1)} %fusion.42, f32[8,8,1,4,128]{4,2,1,3,0:T(1,128)S(1)} %add.383, f32[10,1,8,4,128]{4,2,1,3,0:T(8,128)S(1)} %pad.48, f32[10,1,8,4,128]{4,2,1,3,0:T(8,128)S(1)} %pad.49, f32[1,8,8,4,128]{4,2,1,3,0:T(8,128)S(1)} %add.344, f32[1,8,8,4,128]{4,2,1,3,0:T(8,128)S(1)} %add.351, ...), kind=kLoop, calls=%fused_computation.10 | loop fusion | flops 9437184 | bytes 3473408 | tf_op jit(solution)/shard_map/add | solution.py:276
  64.7 0.2 bitcast_multiply_fusion
  64.9 1.8 %convolution_convert_fusion = bf16[8,8,8,512]{3,2,1,0:T(8,128)(2,1)} fusion(f32[8,8,8,512]{3,2,1,0:T(8,128)S(1)} %bitcast.82, f32[512,512,1,1]{1,0,2,3:T(8,128)S(1)} %reshape.595), kind=kOutput, calls=%fused_computation.6 | convolution fusion | flops 805568512 | bytes 2621440 | tf_op jit(solution)/shard_map/dot_general | solution.py:360
  (155 shorter events, 3.9 us)
Async XLA Ops:
  0.0 2.1 %copy-start = (bf16[8,8,8,512]{3,2,1,0:T(8,128)(2,1)S(1)}, bf16[8,8,8,512]{3,2,1,0:T(8,128)(2,1)}, u32[]{:S(2)}) copy-start(bf16[8,8,8,512]{3,2,1,0:T(8,128)(2,1)} %param.5) | copy-start | bytes 1572868
  1.5 8.2 %copy-start.11 = (f32[1,128,128]{2,1,0:T(8,128)S(1)}, f32[1,128,128]{2,1,0:T(8,128)}, u32[]{:S(2)}) copy-start(f32[1,128,128]{2,1,0:T(8,128)} %param.8) | copy-start | bytes 196612
  1.6 8.3 %copy-start.20 = (s32[3,2,512]{2,1,0:T(2,128)S(1)}, s32[3,2,512]{2,1,0:T(2,128)}, u32[]{:S(2)}) copy-start(s32[3,2,512]{2,1,0:T(2,128)} %param.6) | copy-start | bytes 36868
  1.6 10.6 %collective-permute-start.4 = (f32[8,8,1,4,128]{4,2,1,3,0:T(1,128)S(1)}, f32[8,8,1,4,128]{4,2,1,3,0:T(1,128)S(1)}, u32[]{:S(2)}, u32[]{:S(2)}) collective-permute-start(f32[8,8,1,4,128]{4,2,1,3,0:T(1,128)S(1)} %get-tuple-element.16), channel_id=1, source_target_pairs={{0,1},{1,2},{2,3},{3,0},{4,5},{5,6},{6,7},{7,4},{8,9},{9,10},{10,1... | collective-permute-start | bytes 393224 | tf_op jit(solution)/shard_map/ppermute | solution.py:24
  2.1 7.7 %copy-start.23 = (s32[4,2]{0,1:T(2,128)S(1)}, s32[4,2]{0,1:T(2,128)}, u32[]{:S(2)}) copy-start(s32[4,2]{0,1:T(2,128)} %param.7) | copy-start | bytes 100
  2.2 9.9 %collective-permute-start.2 = (f32[8,2,8,4,128]{4,2,1,3,0:T(8,128)S(1)}, f32[8,2,8,4,128]{4,2,1,3,0:T(8,128)S(1)}, u32[]{:S(2)}, u32[]{:S(2)}) collective-permute-start(f32[8,2,8,4,128]{4,2,1,3,0:T(8,128)S(1)} %pad_maximum_fusion.32), channel_id=1, source_target_pairs={{0,4},{4,0},{1,5},{5,1},{2,6},{6,2},{3,7},{7,3},{8,12},{12,8},{9,1... | collective-permute-start | bytes 786440 | tf_op jit(solution)/shard_map/ppermute | solution.py:40
  4.8 7.4 %collective-permute-start = (f32[1,8,8,4,128]{4,2,1,3,0:T(8,128)S(1)}, f32[1,8,8,4,128]{4,2,1,3,0:T(8,128)S(1)}, u32[]{:S(2)}, u32[]{:S(2)}) collective-permute-start(f32[1,8,8,4,128]{4,2,1,3,0:T(8,128)S(1)} %copy.38), channel_id=1, source_target_pairs={{0,24},{8,0},{16,8},{24,16},{1,25},{9,1},{17,9},{25,17},{2,26},{10... | collective-permute-start | bytes 393224 | tf_op jit(solution)/shard_map/ppermute | solution.py:24
  8.5 8.2 %collective-permute-start.1 = (f32[1,8,8,4,128]{4,2,1,3,0:T(8,128)S(1)}, f32[1,8,8,4,128]{4,2,1,3,0:T(8,128)S(1)}, u32[]{:S(2)}, u32[]{:S(2)}) collective-permute-start(f32[1,8,8,4,128]{4,2,1,3,0:T(8,128)S(1)} %copy.39), channel_id=1, source_target_pairs={{0,8},{8,16},{16,24},{24,0},{1,9},{9,17},{17,25},{25,1},{2,10},{10... | collective-permute-start | bytes 393224 | tf_op jit(solution)/shard_map/ppermute | solution.py:24
  8.6 8.1 %collective-permute-start.3 = (f32[8,8,1,4,128]{4,2,1,3,0:T(1,128)S(1)}, f32[8,8,1,4,128]{4,2,1,3,0:T(1,128)S(1)}, u32[]{:S(2)}, u32[]{:S(2)}) collective-permute-start(f32[8,8,1,4,128]{4,2,1,3,0:T(1,128)S(1)} %get-tuple-element.15), channel_id=1, source_target_pairs={{0,3},{1,0},{2,1},{3,2},{4,7},{5,4},{6,5},{7,6},{8,11},{9,8},{10,9... | collective-permute-start | bytes 393224 | tf_op jit(solution)/shard_map/ppermute | solution.py:24
  12.2 5.4 %copy-start.1 = (f32[8,8,1,4,128]{4,2,1,3,0:T(1,128)}, f32[8,8,1,4,128]{4,2,1,3,0:T(1,128)S(1)}, u32[]{:S(2)}) copy-start(f32[8,8,1,4,128]{4,2,1,3,0:T(1,128)S(1)} %collective-permute-done.4) | copy-start | bytes 393220
  12.2 5.4 %copy-start.5 = (f32[1,8,8,4,128]{4,2,1,3,0:T(8,128)}, f32[1,8,8,4,128]{4,2,1,3,0:T(8,128)S(1)}, u32[]{:S(2)}) copy-start(f32[1,8,8,4,128]{4,2,1,3,0:T(8,128)S(1)} %collective-permute-done) | copy-start | bytes 393220
  16.7 1.0 %copy-start.3 = (f32[1,8,8,4,128]{4,2,1,3,0:T(8,128)}, f32[1,8,8,4,128]{4,2,1,3,0:T(8,128)S(1)}, u32[]{:S(2)}) copy-start(f32[1,8,8,4,128]{4,2,1,3,0:T(8,128)S(1)} %collective-permute-done.1) | copy-start | bytes 393220
  18.9 12.8 %copy-start.21 = (f32[4,4]{1,0:T(4,128)S(1)}, f32[4,4]{1,0:T(4,128)}, u32[]{:S(2)}) copy-start(f32[4,4]{1,0:T(4,128)} %get-tuple-element.43) | copy-start | bytes 196
  18.9 12.8 %copy-start.22 = (f32[4,4]{1,0:T(4,128)S(1)}, f32[4,4]{1,0:T(4,128)}, u32[]{:S(2)}) copy-start(f32[4,4]{1,0:T(4,128)} %get-tuple-element.44) | copy-start | bytes 196
  18.9 2.9 %collective-permute-start.9 = (f32[4,4,1,4,128]{4,2,1,3,0:T(1,128)S(1)}, f32[4,4,1,4,128]{4,2,1,3,0:T(1,128)S(1)}, u32[]{:S(2)}, u32[]{:S(2)}) collective-permute-start(f32[4,4,1,4,128]{4,2,1,3,0:T(1,128)S(1)} %get-tuple-element.26), channel_id=1, source_target_pairs={{0,3},{1,0},{2,1},{3,2},{4,7},{5,4},{6,5},{7,6},{8,11},{9,8},{10,9... | collective-permute-start | bytes 98312 | tf_op jit(solution)/shard_map/ppermute | solution.py:24
  19.0 4.6 %collective-permute-start.6 = (f32[4,2,4,4,128]{4,2,1,3,0:T(4,128)S(1)}, f32[4,2,4,4,128]{4,2,1,3,0:T(4,128)S(1)}, u32[]{:S(2)}, u32[]{:S(2)}) collective-permute-start(f32[4,2,4,4,128]{4,2,1,3,0:T(4,128)S(1)} %pad_maximum_fusion.53), channel_id=1, source_target_pairs={{0,4},{4,0},{1,5},{5,1},{2,6},{6,2},{3,7},{7,3},{8,12},{12,8},{9,1... | collective-permute-start | bytes 196616 | tf_op jit(solution)/shard_map/ppermute | solution.py:40
  19.5 3.4 %collective-permute-start.5 = (f32[4,4,1,4,128]{4,2,1,3,0:T(1,128)S(1)}, f32[4,4,1,4,128]{4,2,1,3,0:T(1,128)S(1)}, u32[]{:S(2)}, u32[]{:S(2)}) collective-permute-start(f32[4,4,1,4,128]{4,2,1,3,0:T(1,128)S(1)} %get-tuple-element.25), channel_id=1, source_target_pairs={{0,1},{1,2},{2,3},{3,0},{4,5},{5,6},{6,7},{7,4},{8,9},{9,10},{10,1... | collective-permute-start | bytes 98312 | tf_op jit(solution)/shard_map/ppermute | solution.py:24
  19.8 3.9 %collective-permute-start.8 = (f32[1,4,4,4,128]{4,2,1,3,0:T(4,128)S(1)}, f32[1,4,4,4,128]{4,2,1,3,0:T(4,128)S(1)}, u32[]{:S(2)}, u32[]{:S(2)}) collective-permute-start(f32[1,4,4,4,128]{4,2,1,3,0:T(4,128)S(1)} %get-tuple-element.28), channel_id=1, source_target_pairs={{0,24},{8,0},{16,8},{24,16},{1,25},{9,1},{17,9},{25,17},{2,26},{10... | collective-permute-start | bytes 98312 | tf_op jit(solution)/shard_map/ppermute | solution.py:24
  21.2 5.7 %collective-permute-start.7 = (f32[1,4,4,4,128]{4,2,1,3,0:T(4,128)S(1)}, f32[1,4,4,4,128]{4,2,1,3,0:T(4,128)S(1)}, u32[]{:S(2)}, u32[]{:S(2)}) collective-permute-start(f32[1,4,4,4,128]{4,2,1,3,0:T(4,128)S(1)} %get-tuple-element.27), channel_id=1, source_target_pairs={{0,8},{8,16},{16,24},{24,0},{1,9},{9,17},{17,25},{25,1},{2,10},{10... | collective-permute-start | bytes 98312 | tf_op jit(solution)/shard_map/ppermute | solution.py:24
  23.6 3.6 %copy-start.7 = (f32[6,1,4,4,128]{4,2,1,3,0:T(4,128)}, f32[6,1,4,4,128]{4,2,1,3,0:T(4,128)S(1)}, u32[]{:S(2)}) copy-start(f32[6,1,4,4,128]{4,2,1,3,0:T(4,128)S(1)} %pad.46) | copy-start | bytes 147460
  23.6 3.6 %copy-start.9 = (f32[6,1,4,4,128]{4,2,1,3,0:T(4,128)}, f32[6,1,4,4,128]{4,2,1,3,0:T(4,128)S(1)}, u32[]{:S(2)}) copy-start(f32[6,1,4,4,128]{4,2,1,3,0:T(4,128)S(1)} %pad.45) | copy-start | bytes 147460
  23.7 3.8 %copy-start.13 = (f32[1,4,4,4,128]{4,2,1,3,0:T(4,128)}, f32[1,4,4,4,128]{4,2,1,3,0:T(4,128)S(1)}, u32[]{:S(2)}) copy-start(f32[1,4,4,4,128]{4,2,1,3,0:T(4,128)S(1)} %collective-permute-done.8) | copy-start | bytes 98308
  26.9 15.6 %copy-start.15 = (f32[1,4,4,4,128]{4,2,1,3,0:T(4,128)}, f32[1,4,4,4,128]{4,2,1,3,0:T(4,128)S(1)}, u32[]{:S(2)}) copy-start(f32[1,4,4,4,128]{4,2,1,3,0:T(4,128)S(1)} %collective-permute-done.7) | copy-start | bytes 98308
  27.7 14.8 %copy-start.12 = (f32[2,2,2,4,128]{4,2,1,3,0:T(2,128)}, f32[2,2,2,4,128]{4,2,1,3,0:T(2,128)S(1)}, u32[]{:S(2)}) copy-start(f32[2,2,2,4,128]{4,2,1,3,0:T(2,128)S(1)} %add_multiply_fusion) | copy-start | bytes 49156
  27.8 7.3 %collective-permute-start.12 = (f32[10,2,2,4,128]{4,2,1,3,0:T(2,128)S(1)}, f32[10,2,2,4,128]{4,2,1,3,0:T(2,128)S(1)}, u32[]{:S(2)}, u32[]{:S(2)}) collective-permute-start(f32[10,2,2,4,128]{4,2,1,3,0:T(2,128)S(1)} %pad_maximum_fusion.52), channel_id=1, source_target_pairs={{0,8},{8,16},{16,24},{24,0},{1,9},{9,17},{17,25},{25,1},{2,10},{10... | collective-permute-start | bytes 245768 | tf_op jit(solution)/shard_map/ppermute | solution.py:24
  27.8 9.8 %collective-permute-start.11 = (f32[10,2,2,4,128]{4,2,1,3,0:T(2,128)S(1)}, f32[10,2,2,4,128]{4,2,1,3,0:T(2,128)S(1)}, u32[]{:S(2)}, u32[]{:S(2)}) collective-permute-start(f32[10,2,2,4,128]{4,2,1,3,0:T(2,128)S(1)} %pad_maximum_fusion.52), channel_id=1, source_target_pairs={{0,16},{8,24},{16,0},{24,8},{1,17},{9,25},{17,1},{25,9},{2,18},{10... | collective-permute-start | bytes 245768 | tf_op jit(solution)/shard_map/ppermute | solution.py:24
  28.5 9.1 %collective-permute-start.10 = (f32[10,2,2,4,128]{4,2,1,3,0:T(2,128)S(1)}, f32[10,2,2,4,128]{4,2,1,3,0:T(2,128)S(1)}, u32[]{:S(2)}, u32[]{:S(2)}) collective-permute-start(f32[10,2,2,4,128]{4,2,1,3,0:T(2,128)S(1)} %pad_maximum_fusion.52), channel_id=1, source_target_pairs={{0,24},{8,0},{16,8},{24,16},{1,25},{9,1},{17,9},{25,17},{2,26},{10... | collective-permute-start | bytes 245768 | tf_op jit(solution)/shard_map/ppermute | solution.py:24
  35.0 7.5 %copy-start.17 = (f32[2,2,2,4,128]{4,2,1,3,0:T(2,128)}, f32[2,2,2,4,128]{4,2,1,3,0:T(2,128)S(1)}, u32[]{:S(2)}) copy-start(f32[2,2,2,4,128]{4,2,1,3,0:T(2,128)S(1)} %slice.585) | copy-start | bytes 49156
  37.6 4.9 %copy-start.18 = (f32[2,2,2,4,128]{4,2,1,3,0:T(2,128)}, f32[2,2,2,4,128]{4,2,1,3,0:T(2,128)S(1)}, u32[]{:S(2)}) copy-start(f32[2,2,2,4,128]{4,2,1,3,0:T(2,128)S(1)} %slice.584) | copy-start | bytes 49156
  37.6 9.2 %copy-start.19 = (f32[2,2,2,4,128]{4,2,1,3,0:T(2,128)}, f32[2,2,2,4,128]{4,2,1,3,0:T(2,128)S(1)}, u32[]{:S(2)}) copy-start(f32[2,2,2,4,128]{4,2,1,3,0:T(2,128)S(1)} %slice.583) | copy-start | bytes 49156
  38.3 4.9 %collective-permute-start.19 = (f32[8,2,2,4,128]{4,2,1,3,0:T(2,128)}, f32[8,2,2,4,128]{4,2,1,3,0:T(2,128)S(1)}, u32[]{:S(2)}, u32[]{:S(2)}) collective-permute-start(f32[8,2,2,4,128]{4,2,1,3,0:T(2,128)} %pad_maximum_fusion.54), channel_id=1, source_target_pairs={{7,0},{4,1},{5,2},{6,3},{3,4},{0,5},{1,6},{2,7},{15,8},{12,9},{13,... | collective-permute-start | bytes 196616 | tf_op jit(solution)/shard_map/ppermute | solution.py:111
  38.3 6.1 %collective-permute-start.18 = (f32[8,2,2,4,128]{4,2,1,3,0:T(2,128)}, f32[8,2,2,4,128]{4,2,1,3,0:T(2,128)S(1)}, u32[]{:S(2)}, u32[]{:S(2)}) collective-permute-start(f32[8,2,2,4,128]{4,2,1,3,0:T(2,128)} %pad_maximum_fusion.54), channel_id=1, source_target_pairs={{6,0},{7,1},{4,2},{5,3},{2,4},{3,5},{0,6},{1,7},{14,8},{15,9},{12,... | collective-permute-start | bytes 196616 | tf_op jit(solution)/shard_map/ppermute | solution.py:111
  39.7 10.6 %collective-permute-start.17 = (f32[8,2,2,4,128]{4,2,1,3,0:T(2,128)}, f32[8,2,2,4,128]{4,2,1,3,0:T(2,128)}, u32[]{:S(2)}, u32[]{:S(2)}) collective-permute-start(f32[8,2,2,4,128]{4,2,1,3,0:T(2,128)} %pad_maximum_fusion.54), channel_id=1, source_target_pairs={{5,0},{6,1},{7,2},{4,3},{1,4},{2,5},{3,6},{0,7},{13,8},{14,9},{15,... | collective-permute-start | bytes 196616 | tf_op jit(solution)/shard_map/ppermute | solution.py:111
  42.0 8.3 %collective-permute-start.16 = (f32[8,2,2,4,128]{4,2,1,3,0:T(2,128)}, f32[8,2,2,4,128]{4,2,1,3,0:T(2,128)}, u32[]{:S(2)}, u32[]{:S(2)}) collective-permute-start(f32[8,2,2,4,128]{4,2,1,3,0:T(2,128)} %pad_maximum_fusion.54), channel_id=1, source_target_pairs={{4,0},{5,1},{6,2},{7,3},{0,4},{1,5},{2,6},{3,7},{12,8},{13,9},{14,... | collective-permute-start | bytes 196616 | tf_op jit(solution)/shard_map/ppermute | solution.py:111
  42.5 7.8 %collective-permute-start.15 = (f32[8,2,2,4,128]{4,2,1,3,0:T(2,128)}, f32[8,2,2,4,128]{4,2,1,3,0:T(2,128)}, u32[]{:S(2)}, u32[]{:S(2)}) collective-permute-start(f32[8,2,2,4,128]{4,2,1,3,0:T(2,128)} %pad_maximum_fusion.54), channel_id=1, source_target_pairs={{3,0},{0,1},{1,2},{2,3},{7,4},{4,5},{5,6},{6,7},{11,8},{8,9},{9,10... | collective-permute-start | bytes 196616 | tf_op jit(solution)/shard_map/ppermute | solution.py:111
  43.2 3.7 %copy-start.24 = (f32[8,2,2,4,128]{4,2,1,3,0:T(2,128)}, f32[8,2,2,4,128]{4,2,1,3,0:T(2,128)S(1)}, u32[]{:S(2)}) copy-start(f32[8,2,2,4,128]{4,2,1,3,0:T(2,128)S(1)} %collective-permute-done.19) | copy-start | bytes 196612
  43.2 7.1 %collective-permute-start.14 = (f32[8,2,2,4,128]{4,2,1,3,0:T(2,128)}, f32[8,2,2,4,128]{4,2,1,3,0:T(2,128)}, u32[]{:S(2)}, u32[]{:S(2)}) collective-permute-start(f32[8,2,2,4,128]{4,2,1,3,0:T(2,128)} %pad_maximum_fusion.54), channel_id=1, source_target_pairs={{2,0},{3,1},{0,2},{1,3},{6,4},{7,5},{4,6},{5,7},{10,8},{11,9},{8,1... | collective-permute-start | bytes 196616 | tf_op jit(solution)/shard_map/ppermute | solution.py:111
  45.1 5.3 %collective-permute-start.13 = (f32[8,2,2,4,128]{4,2,1,3,0:T(2,128)}, f32[8,2,2,4,128]{4,2,1,3,0:T(2,128)}, u32[]{:S(2)}, u32[]{:S(2)}) collective-permute-start(f32[8,2,2,4,128]{4,2,1,3,0:T(2,128)} %pad_maximum_fusion.54), channel_id=1, source_target_pairs={{1,0},{2,1},{3,2},{0,3},{5,4},{6,5},{7,6},{4,7},{9,8},{10,9},{11,1... | collective-permute-start | bytes 196616 | tf_op jit(solution)/shard_map/ppermute | solution.py:111
  50.2 2.1 %copy-start.8 = (f32[6,1,4,4,128]{4,2,1,3,0:T(4,128)S(1)}, f32[6,1,4,4,128]{4,2,1,3,0:T(4,128)}, u32[]{:S(2)}) copy-start(f32[6,1,4,4,128]{4,2,1,3,0:T(4,128)} %copy-done.7) | copy-start | bytes 147460
  50.3 2.1 %copy-start.10 = (f32[6,1,4,4,128]{4,2,1,3,0:T(4,128)S(1)}, f32[6,1,4,4,128]{4,2,1,3,0:T(4,128)}, u32[]{:S(2)}) copy-start(f32[6,1,4,4,128]{4,2,1,3,0:T(4,128)} %copy-done.9) | copy-start | bytes 147460
  50.3 2.1 %copy-start.14 = (f32[1,4,4,4,128]{4,2,1,3,0:T(4,128)S(1)}, f32[1,4,4,4,128]{4,2,1,3,0:T(4,128)}, u32[]{:S(2)}) copy-start(f32[1,4,4,4,128]{4,2,1,3,0:T(4,128)} %copy-done.13) | copy-start | bytes 98308
  50.3 2.1 %copy-start.16 = (f32[1,4,4,4,128]{4,2,1,3,0:T(4,128)S(1)}, f32[1,4,4,4,128]{4,2,1,3,0:T(4,128)}, u32[]{:S(2)}) copy-start(f32[1,4,4,4,128]{4,2,1,3,0:T(4,128)} %copy-done.15) | copy-start | bytes 98308
  53.5 5.6 %collective-permute-start.24 = (f32[4,4,1,4,128]{4,2,1,3,0:T(1,128)S(1)}, f32[4,4,1,4,128]{4,2,1,3,0:T(1,128)S(1)}, u32[]{:S(2)}, u32[]{:S(2)}) collective-permute-start(f32[4,4,1,4,128]{4,2,1,3,0:T(1,128)S(1)} %get-tuple-element.10), channel_id=1, source_target_pairs={{0,1},{1,2},{2,3},{3,0},{4,5},{5,6},{6,7},{7,4},{8,9},{9,10},{10,1... | collective-permute-start | bytes 98312 | tf_op jit(solution)/shard_map/ppermute | solution.py:24
  53.5 9.7 %collective-permute-start.22 = (f32[4,2,4,4,128]{4,2,1,3,0:T(4,128)S(1)}, f32[4,2,4,4,128]{4,2,1,3,0:T(4,128)S(1)}, u32[]{:S(2)}, u32[]{:S(2)}) collective-permute-start(f32[4,2,4,4,128]{4,2,1,3,0:T(4,128)S(1)} %pad_maximum_fusion.55), channel_id=1, source_target_pairs={{0,4},{4,0},{1,5},{5,1},{2,6},{6,2},{3,7},{7,3},{8,12},{12,8},{9,1... | collective-permute-start | bytes 196616 | tf_op jit(solution)/shard_map/ppermute | solution.py:40
  55.1 4.8 %collective-permute-start.20 = (f32[1,4,4,4,128]{4,2,1,3,0:T(4,128)S(1)}, f32[1,4,4,4,128]{4,2,1,3,0:T(4,128)S(1)}, u32[]{:S(2)}, u32[]{:S(2)}) collective-permute-start(f32[1,4,4,4,128]{4,2,1,3,0:T(4,128)S(1)} %get-tuple-element.12), channel_id=1, source_target_pairs={{0,24},{8,0},{16,8},{24,16},{1,25},{9,1},{17,9},{25,17},{2,26},{10... | collective-permute-start | bytes 98312 | tf_op jit(solution)/shard_map/ppermute | solution.py:24
  57.2 5.7 %collective-permute-start.21 = (f32[1,4,4,4,128]{4,2,1,3,0:T(4,128)S(1)}, f32[1,4,4,4,128]{4,2,1,3,0:T(4,128)S(1)}, u32[]{:S(2)}, u32[]{:S(2)}) collective-permute-start(f32[1,4,4,4,128]{4,2,1,3,0:T(4,128)S(1)} %get-tuple-element.11), channel_id=1, source_target_pairs={{0,8},{8,16},{16,24},{24,0},{1,9},{9,17},{17,25},{25,1},{2,10},{10... | collective-permute-start | bytes 98312 | tf_op jit(solution)/shard_map/ppermute | solution.py:24
  57.2 5.8 %collective-permute-start.23 = (f32[4,4,1,4,128]{4,2,1,3,0:T(1,128)S(1)}, f32[4,4,1,4,128]{4,2,1,3,0:T(1,128)S(1)}, u32[]{:S(2)}, u32[]{:S(2)}) collective-permute-start(f32[4,4,1,4,128]{4,2,1,3,0:T(1,128)S(1)} %get-tuple-element.9), channel_id=1, source_target_pairs={{0,3},{1,0},{2,1},{3,2},{4,7},{5,4},{6,5},{7,6},{8,11},{9,8},{10,9... | collective-permute-start | bytes 98312 | tf_op jit(solution)/shard_map/ppermute | solution.py:24
  59.1 3.9 %copy-start.4 = (f32[1,8,8,4,128]{4,2,1,3,0:T(8,128)S(1)}, f32[1,8,8,4,128]{4,2,1,3,0:T(8,128)}, u32[]{:S(2)}) copy-start(f32[1,8,8,4,128]{4,2,1,3,0:T(8,128)} %copy-done.3) | copy-start | bytes 393220
  (3 other events, 2.5 us)

commit v23 on v19

--- a/solution.py
+++ b/solution.py
@@ -196,7 +196,7 @@
     operator = coarse_matrix(grid, tuple(starts), rhs_two.shape[:3])
     operator = jnp.asarray(operator.reshape((-1,) + tuple(grid)))
     post = jnp.einsum(
-        "qxyz,xyzgl->qgl", operator, extended, precision=lax.Precision.HIGHEST, preferred_element_type=jnp.float32
+        "qxyz,xyzgl->qgl", operator, extended, precision=lax.Precision.HIGH, preferred_element_type=jnp.float32
     )
     return post.reshape(tuple(2 * size + 2 for size in rhs_two.shape[:3]) + orbs), tiles_by_step
 

time: 66.4 us -> 66.2 us (level)
  no operation moved by 1% of the time
where the time goes in v23:
time: 66.2 us; the launch traced here: 66 us
  starting transfers between devices  26.6 us (40%)
  waiting for transfers between devices  18.8 us (28%)
  local copies, waits for them, and re-layouts  8.42 us (13%)
  other arithmetic  7.7 us (12%)
  matrix products  3.5 us (5%)
  between operations  1.07 us (2%)
    ppermute x15, waiting for transfers between devices, shifted(): lax.ppermute(block, axis, [(j, (j - step) % count) for j in range(count)])  17.6 us
    ppermute x15, starting transfers between devices, shifted(): lax.ppermute(block, axis, [(j, (j - step) % count) for j in range(count)])  15 us
    ppermute x7, starting transfers between devices, fetch(): cache[steps] = lax.ppermute(block, tuple(axes), pairs)  6.86 us
    ppermute x3, starting transfers between devices, axis_faces(): lax.ppermute(jnp.concatenate([first, last], axis=dim), axis, [(0, 1), (1,...  4.75 us
    dot_general x1, matrix products, body(): jnp.dot(rows, gram, precision=lax.Precision.HIGH, preferred_element_type=...  1.81 us
    reduce_sum x1, local copies, waits for them, and re-layouts, gram_matrix(): return spread.sum(axis=0).reshape(orb_count, orb_count)  1.7 us
    dot_general x1, matrix products, coarse_solve(): jnp.einsum('qxyz,xyzgl->qgl', operator, extended, precision=lax.Precision...  1.69 us
    reshape x1, local copies, waits for them, and re-layouts, gram_matrix(): return spread.sum(axis=0).reshape(orb_count, orb_count)  1.64 us
  transfers between devices with their start and end apart: 25, of which 9 were waited for; matrix products, arithmetic and copies ran while one was open for 11% of the time, Pallas kernels for 0%

profile of v23, /device:TPU:0, one launch (start us, length us, event | category | flops | bytes accessed | tf_op | source)
XLA Modules:
  0.0 66.0 jit_solution(1538463742031429111)
XLA Ops:
  0.0 1.5 %fusion.57 = (f32[8,8,1,4,128]{4,2,1,3,0:T(1,128)S(1)}, f32[8,8,1,4,128]{4,2,1,3,0:T(1,128)S(1)}) fusion(bf16[8,8,8,512]{3,2,1,0:T(8,128)(2,1)} %param.5), kind=kLoop, calls=%fused_computation.135 | loop fusion | flops 131072 | bytes 786432 | tf_op jit(solution)/shard_map/div | solution.py:314
  1.6 0.5 collective-permute-start.4
  2.2 2.6 %collective-permute-start.2 = (f32[8,2,8,4,128]{4,2,1,3,0:T(8,128)S(1)}, f32[8,2,8,4,128]{4,2,1,3,0:T(8,128)S(1)}, u32[]{:S(2)}, u32[]{:S(2)}) collective-permute-start(f32[8,2,8,4,128]{4,2,1,3,0:T(8,128)S(1)} %pad_maximum_fusion.32), channel_id=1, source_target_pairs={{0,4},{4,0},{1,5},{5,1},{2,6},{6,2},{3,7},{7,3},{8,12},{12,8},{9,1... | collective-permute-start | bytes 786440 | tf_op jit(solution)/shard_map/ppermute | solution.py:37
  4.8 3.7 %collective-permute-start = (f32[1,8,8,4,128]{4,2,1,3,0:T(8,128)S(1)}, f32[1,8,8,4,128]{4,2,1,3,0:T(8,128)S(1)}, u32[]{:S(2)}, u32[]{:S(2)}) collective-permute-start(f32[1,8,8,4,128]{4,2,1,3,0:T(8,128)S(1)} %copy.38), channel_id=1, source_target_pairs={{0,24},{8,0},{16,8},{24,16},{1,25},{9,1},{17,9},{25,17},{2,26},{10... | collective-permute-start | bytes 393224 | tf_op jit(solution)/shard_map/ppermute | solution.py:24
  8.6 1.2 %collective-permute-start.3 = (f32[8,8,1,4,128]{4,2,1,3,0:T(1,128)S(1)}, f32[8,8,1,4,128]{4,2,1,3,0:T(1,128)S(1)}, u32[]{:S(2)}, u32[]{:S(2)}) collective-permute-start(f32[8,8,1,4,128]{4,2,1,3,0:T(1,128)S(1)} %get-tuple-element.7), channel_id=1, source_target_pairs={{0,3},{1,0},{2,1},{3,2},{4,7},{5,4},{6,5},{7,6},{8,11},{9,8},{10,9... | collective-permute-start | bytes 393224 | tf_op jit(solution)/shard_map/ppermute | solution.py:24
  10.1 0.6 gather_fusion
  11.3 0.7 %fusion.58 = (f32[4,4]{1,0:T(4,128)}, f32[4,4]{1,0:T(4,128)}) fusion(s32[4]{0:T(128)S(1)} %get-tuple-element.5, s32[4]{0:T(128)S(1)} %get-tuple-element.6), kind=kLoop, calls=%fused_computation.164 | loop fusion | flops 64 | bytes 160 | tf_op jit(solution)/shard_map/convert_element_type | solution.py:306
  12.2 4.4 %collective-permute-done.1 = f32[1,8,8,4,128]{4,2,1,3,0:T(8,128)S(1)} collective-permute-done((f32[1,8,8,4,128]{4,2,1,3,0:T(8,128)S(1)}, f32[1,8,8,4,128]{4,2,1,3,0:T(8,128)S(1)}, u32[]{:S(2)}, u32[]{:S(2)}) %collective-permute-start.1) | collective-permute-done | bytes 131104 | tf_op jit(solution)/shard_map/ppermute | solution.py:24
  16.7 1.0 %convert_subtract_fusion.1 = f32[8,8,8,4,128]{4,2,1,3,0:T(8,128)S(1)} fusion(f32[8,8,1,4,128]{4,2,1,3,0:T(1,128)S(1)} %collective-permute-done.4, f32[10,1,8,4,128]{4,2,1,3,0:T(8,128)S(1)} %pad.40, f32[10,1,8,4,128]{4,2,1,3,0:T(8,128)S(1)} %pad.41, f32[1,8,8,4,128]{4,2,1,3,0:T(8,128)S(1)} %collective-permute-done, ...), kind=kLoop, calls=%fused_computation.3 | loop fusion | flops 8912896 | bytes 3473408 | tf_op jit(solution)/shard_map/sub | solution.py:317
  17.8 0.4 slice.285
  18.2 0.4 slice.286
  18.9 0.6 collective-permute-start.6
  19.5 0.2 collective-permute-start.5
  19.7 1.5 %collective-permute-start.8 = (f32[1,4,4,4,128]{4,2,1,3,0:T(4,128)S(1)}, f32[1,4,4,4,128]{4,2,1,3,0:T(4,128)S(1)}, u32[]{:S(2)}, u32[]{:S(2)}) collective-permute-start(f32[1,4,4,4,128]{4,2,1,3,0:T(4,128)S(1)} %get-tuple-element.26), channel_id=1, source_target_pairs={{0,24},{8,0},{16,8},{24,16},{1,25},{9,1},{17,9},{25,17},{2,26},{10... | collective-permute-start | bytes 98312 | tf_op jit(solution)/shard_map/ppermute | solution.py:24
  21.2 0.6 collective-permute-start.7
  21.8 1.1 %collective-permute-done.5 = f32[4,4,1,4,128]{4,2,1,3,0:T(1,128)S(1)} collective-permute-done((f32[4,4,1,4,128]{4,2,1,3,0:T(1,128)S(1)}, f32[4,4,1,4,128]{4,2,1,3,0:T(1,128)S(1)}, u32[]{:S(2)}, u32[]{:S(2)}) %collective-permute-start.5) | collective-permute-done | bytes 32800 | tf_op jit(solution)/shard_map/ppermute | solution.py:24
  22.9 0.6 collective-permute-done.6
  23.6 3.3 %collective-permute-done.7 = f32[1,4,4,4,128]{4,2,1,3,0:T(4,128)S(1)} collective-permute-done((f32[1,4,4,4,128]{4,2,1,3,0:T(4,128)S(1)}, f32[1,4,4,4,128]{4,2,1,3,0:T(4,128)S(1)}, u32[]{:S(2)}, u32[]{:S(2)}) %collective-permute-start.7) | collective-permute-done | bytes 32800 | tf_op jit(solution)/shard_map/ppermute | solution.py:24
  26.9 0.2 fusion.51
  27.2 0.2 slice.305
  27.4 0.2 slice.306
  27.8 0.7 %collective-permute-start.11 = (f32[10,2,2,4,128]{4,2,1,3,0:T(2,128)S(1)}, f32[10,2,2,4,128]{4,2,1,3,0:T(2,128)S(1)}, u32[]{:S(2)}, u32[]{:S(2)}) collective-permute-start(f32[10,2,2,4,128]{4,2,1,3,0:T(2,128)S(1)} %pad_maximum_fusion.52), channel_id=1, source_target_pairs={{0,16},{8,24},{16,0},{24,8},{1,17},{9,25},{17,1},{25,9},{2,18},{10... | collective-permute-start | bytes 245768 | tf_op jit(solution)/shard_map/ppermute | solution.py:24
  28.5 3.1 %collective-permute-start.10 = (f32[10,2,2,4,128]{4,2,1,3,0:T(2,128)S(1)}, f32[10,2,2,4,128]{4,2,1,3,0:T(2,128)S(1)}, u32[]{:S(2)}, u32[]{:S(2)}) collective-permute-start(f32[10,2,2,4,128]{4,2,1,3,0:T(2,128)S(1)} %pad_maximum_fusion.52), channel_id=1, source_target_pairs={{0,24},{8,0},{16,8},{24,16},{1,25},{9,1},{17,9},{25,17},{2,26},{10... | collective-permute-start | bytes 245768 | tf_op jit(solution)/shard_map/ppermute | solution.py:24
  31.7 3.3 %collective-permute-done.12 = f32[10,2,2,4,128]{4,2,1,3,0:T(2,128)S(1)} collective-permute-done((f32[10,2,2,4,128]{4,2,1,3,0:T(2,128)S(1)}, f32[10,2,2,4,128]{4,2,1,3,0:T(2,128)S(1)}, u32[]{:S(2)}, u32[]{:S(2)}) %collective-permute-start.12) | collective-permute-done | bytes 81952 | tf_op jit(solution)/shard_map/ppermute | solution.py:24
  35.0 2.6 %collective-permute-done.11 = f32[10,2,2,4,128]{4,2,1,3,0:T(2,128)S(1)} collective-permute-done((f32[10,2,2,4,128]{4,2,1,3,0:T(2,128)S(1)}, f32[10,2,2,4,128]{4,2,1,3,0:T(2,128)S(1)}, u32[]{:S(2)}, u32[]{:S(2)}) %collective-permute-start.11) | collective-permute-done | bytes 81952 | tf_op jit(solution)/shard_map/ppermute | solution.py:24
  37.6 0.6 pad_maximum_fusion.54
  38.3 1.3 %collective-permute-start.18 = (f32[8,2,2,4,128]{4,2,1,3,0:T(2,128)}, f32[8,2,2,4,128]{4,2,1,3,0:T(2,128)S(1)}, u32[]{:S(2)}, u32[]{:S(2)}) collective-permute-start(f32[8,2,2,4,128]{4,2,1,3,0:T(2,128)} %pad_maximum_fusion.54), channel_id=1, source_target_pairs={{6,0},{7,1},{4,2},{5,3},{2,4},{3,5},{0,6},{1,7},{14,8},{15,9},{12,... | collective-permute-start | bytes 196616 | tf_op jit(solution)/shard_map/ppermute | solution.py:108
  39.6 2.4 %collective-permute-start.17 = (f32[8,2,2,4,128]{4,2,1,3,0:T(2,128)}, f32[8,2,2,4,128]{4,2,1,3,0:T(2,128)}, u32[]{:S(2)}, u32[]{:S(2)}) collective-permute-start(f32[8,2,2,4,128]{4,2,1,3,0:T(2,128)} %pad_maximum_fusion.54), channel_id=1, source_target_pairs={{5,0},{6,1},{7,2},{4,3},{1,4},{2,5},{3,6},{0,7},{13,8},{14,9},{15,... | collective-permute-start | bytes 196616 | tf_op jit(solution)/shard_map/ppermute | solution.py:108
  42.0 0.5 collective-permute-start.16
  42.7 0.5 collective-permute-done.19
  43.2 1.2 %collective-permute-start.14 = (f32[8,2,2,4,128]{4,2,1,3,0:T(2,128)}, f32[8,2,2,4,128]{4,2,1,3,0:T(2,128)}, u32[]{:S(2)}, u32[]{:S(2)}) collective-permute-start(f32[8,2,2,4,128]{4,2,1,3,0:T(2,128)} %pad_maximum_fusion.54), channel_id=1, source_target_pairs={{2,0},{3,1},{0,2},{1,3},{6,4},{7,5},{4,6},{5,7},{10,8},{11,9},{8,1... | collective-permute-start | bytes 196616 | tf_op jit(solution)/shard_map/ppermute | solution.py:108
  44.4 0.6 copy-done.25
  45.0 1.4 %collective-permute-start.13 = (f32[8,2,2,4,128]{4,2,1,3,0:T(2,128)}, f32[8,2,2,4,128]{4,2,1,3,0:T(2,128)}, u32[]{:S(2)}, u32[]{:S(2)}) collective-permute-start(f32[8,2,2,4,128]{4,2,1,3,0:T(2,128)} %pad_maximum_fusion.54), channel_id=1, source_target_pairs={{1,0},{2,1},{3,2},{0,3},{5,4},{6,5},{7,6},{4,7},{9,8},{10,9},{11,1... | collective-permute-start | bytes 196616 | tf_op jit(solution)/shard_map/ppermute | solution.py:108
  46.4 0.4 multiply_reduce_fusion
  46.9 1.7 %copy.52 = f32[4,128,4,128]{3,2,1,0:T(4,128)} copy(f32[4,128,4,128]{3,1,2,0:T(8,128)S(1)} %multiply_reduce_fusion) | data formatting | bytes 2097152 | tf_op jit(solution)/shard_map/reduce_sum | solution.py:309
  48.6 1.6 %reshape.595 = f32[512,512,1,1]{1,0,2,3:T(8,128)S(1)} reshape(f32[4,128,4,128]{3,2,1,0:T(4,128)} %copy.52) | data formatting | bytes 2097152 | tf_op jit(solution)/shard_map/reshape | solution.py:309
  50.3 1.7 %convolution_bitcast_fusion = f32[216,4,128]{2,0,1:T(8,128)S(1)} fusion(f32[216,8,4,8,1]{0,3,2,4,1:T(8,128)} %constant.134, f32[8,2,2,4,128]{4,2,1,3,0:T(2,128)} %copy-done.24, f32[8,2,2,4,128]{4,2,1,3,0:T(2,128)} %copy-done.25, f32[8,2,2,4,128]{4,2,1,3,0:T(2,128)} %collective-permute-done.17, f32[8,2,2,4,128]{4,2,1,3,0:T(2,128)} %collective-permute-done.16, ...), kind=kOutput, calls=%fused_computation.7 | convolution fusion | flops 171180032 | bytes 1187840 | tf_op jit(solution)/shard_map/qxyz,xyzgl->qgl/dot_general | solution.py:198
  52.2 0.2 maximum_add_fusion
  52.4 0.2 fusion.47
  52.8 1.6 %collective-permute-start.22 = (f32[4,2,4,4,128]{4,2,1,3,0:T(4,128)S(1)}, f32[4,2,4,4,128]{4,2,1,3,0:T(4,128)S(1)}, u32[]{:S(2)}, u32[]{:S(2)}) collective-permute-start(f32[4,2,4,4,128]{4,2,1,3,0:T(4,128)S(1)} %pad_maximum_fusion.55), channel_id=1, source_target_pairs={{0,4},{4,0},{1,5},{5,1},{2,6},{6,2},{3,7},{7,3},{8,12},{12,8},{9,1... | collective-permute-start | bytes 196616 | tf_op jit(solution)/shard_map/ppermute | solution.py:37
  54.4 2.1 %collective-permute-start.20 = (f32[1,4,4,4,128]{4,2,1,3,0:T(4,128)S(1)}, f32[1,4,4,4,128]{4,2,1,3,0:T(4,128)S(1)}, u32[]{:S(2)}, u32[]{:S(2)}) collective-permute-start(f32[1,4,4,4,128]{4,2,1,3,0:T(4,128)S(1)} %get-tuple-element.20), channel_id=1, source_target_pairs={{0,24},{8,0},{16,8},{24,16},{1,25},{9,1},{17,9},{25,17},{2,26},{10... | collective-permute-start | bytes 98312 | tf_op jit(solution)/shard_map/ppermute | solution.py:24
  56.5 1.2 %collective-permute-start.23 = (f32[4,4,1,4,128]{4,2,1,3,0:T(1,128)S(1)}, f32[4,4,1,4,128]{4,2,1,3,0:T(1,128)S(1)}, u32[]{:S(2)}, u32[]{:S(2)}) collective-permute-start(f32[4,4,1,4,128]{4,2,1,3,0:T(1,128)S(1)} %get-tuple-element.17), channel_id=1, source_target_pairs={{0,3},{1,0},{2,1},{3,2},{4,7},{5,4},{6,5},{7,6},{8,11},{9,8},{10,9... | collective-permute-start | bytes 98312 | tf_op jit(solution)/shard_map/ppermute | solution.py:24
  57.8 0.4 broadcast_in_dim.88
  58.4 0.6 copy-done.2
  59.3 2.9 %collective-permute-done.21 = f32[1,4,4,4,128]{4,2,1,3,0:T(4,128)S(1)} collective-permute-done((f32[1,4,4,4,128]{4,2,1,3,0:T(4,128)S(1)}, f32[1,4,4,4,128]{4,2,1,3,0:T(4,128)S(1)}, u32[]{:S(2)}, u32[]{:S(2)}) %collective-permute-start.21) | collective-permute-done | bytes 32800 | tf_op jit(solution)/shard_map/ppermute | solution.py:24
  62.8 1.0 %fusion.2 = f32[8,8,8,4,128]{4,2,1,3,0:T(8,128)S(1)} fusion(f32[8,8,8,4,128]{4,2,1,3,0:T(8,128)S(1)} %fusion.42, f32[8,8,1,4,128]{4,2,1,3,0:T(1,128)S(1)} %add.239, f32[10,1,8,4,128]{4,2,1,3,0:T(8,128)S(1)} %pad.48, f32[10,1,8,4,128]{4,2,1,3,0:T(8,128)S(1)} %pad.49, f32[1,8,8,4,128]{4,2,1,3,0:T(8,128)S(1)} %add.230, f32[1,8,8,4,128]{4,2,1,3,0:T(8,128)S(1)} %add.231, ...), kind=kLoop, calls=%fused_computation.10 | loop fusion | flops 9437184 | bytes 3473408 | tf_op jit(solution)/shard_map/add | solution.py:273
  64.0 0.2 bitcast_multiply_fusion
  64.2 1.8 %convolution_convert_fusion = bf16[8,8,8,512]{3,2,1,0:T(8,128)(2,1)} fusion(f32[8,8,8,512]{3,2,1,0:T(8,128)S(1)} %bitcast.82, f32[512,512,1,1]{1,0,2,3:T(8,128)S(1)} %reshape.595), kind=kOutput, calls=%fused_computation.6 | convolution fusion | flops 805568512 | bytes 2621440 | tf_op jit(solution)/shard_map/dot_general | solution.py:345
  (154 shorter events, 3.5 us)
Async XLA Ops:
  0.0 2.1 %copy-start = (bf16[8,8,8,512]{3,2,1,0:T(8,128)(2,1)S(1)}, bf16[8,8,8,512]{3,2,1,0:T(8,128)(2,1)}, u32[]{:S(2)}) copy-start(bf16[8,8,8,512]{3,2,1,0:T(8,128)(2,1)} %param.5) | copy-start | bytes 1572868
  1.5 8.2 %copy-start.11 = (f32[1,128,128]{2,1,0:T(8,128)S(1)}, f32[1,128,128]{2,1,0:T(8,128)}, u32[]{:S(2)}) copy-start(f32[1,128,128]{2,1,0:T(8,128)} %param.8) | copy-start | bytes 196612
  1.6 8.3 %copy-start.20 = (s32[3,2,512]{2,1,0:T(2,128)S(1)}, s32[3,2,512]{2,1,0:T(2,128)}, u32[]{:S(2)}) copy-start(s32[3,2,512]{2,1,0:T(2,128)} %param.6) | copy-start | bytes 36868
  1.6 10.6 %collective-permute-start.4 = (f32[8,8,1,4,128]{4,2,1,3,0:T(1,128)S(1)}, f32[8,8,1,4,128]{4,2,1,3,0:T(1,128)S(1)}, u32[]{:S(2)}, u32[]{:S(2)}) collective-permute-start(f32[8,8,1,4,128]{4,2,1,3,0:T(1,128)S(1)} %get-tuple-element.8), channel_id=1, source_target_pairs={{0,1},{1,2},{2,3},{3,0},{4,5},{5,6},{6,7},{7,4},{8,9},{9,10},{10,1... | collective-permute-start | bytes 393224 | tf_op jit(solution)/shard_map/ppermute | solution.py:24
  2.1 7.7 %copy-start.23 = (s32[4,2]{0,1:T(2,128)S(1)}, s32[4,2]{0,1:T(2,128)}, u32[]{:S(2)}) copy-start(s32[4,2]{0,1:T(2,128)} %param.7) | copy-start | bytes 100
  2.2 9.9 %collective-permute-start.2 = (f32[8,2,8,4,128]{4,2,1,3,0:T(8,128)S(1)}, f32[8,2,8,4,128]{4,2,1,3,0:T(8,128)S(1)}, u32[]{:S(2)}, u32[]{:S(2)}) collective-permute-start(f32[8,2,8,4,128]{4,2,1,3,0:T(8,128)S(1)} %pad_maximum_fusion.32), channel_id=1, source_target_pairs={{0,4},{4,0},{1,5},{5,1},{2,6},{6,2},{3,7},{7,3},{8,12},{12,8},{9,1... | collective-permute-start | bytes 786440 | tf_op jit(solution)/shard_map/ppermute | solution.py:37
  4.8 7.4 %collective-permute-start = (f32[1,8,8,4,128]{4,2,1,3,0:T(8,128)S(1)}, f32[1,8,8,4,128]{4,2,1,3,0:T(8,128)S(1)}, u32[]{:S(2)}, u32[]{:S(2)}) collective-permute-start(f32[1,8,8,4,128]{4,2,1,3,0:T(8,128)S(1)} %copy.38), channel_id=1, source_target_pairs={{0,24},{8,0},{16,8},{24,16},{1,25},{9,1},{17,9},{25,17},{2,26},{10... | collective-permute-start | bytes 393224 | tf_op jit(solution)/shard_map/ppermute | solution.py:24
  8.5 8.2 %collective-permute-start.1 = (f32[1,8,8,4,128]{4,2,1,3,0:T(8,128)S(1)}, f32[1,8,8,4,128]{4,2,1,3,0:T(8,128)S(1)}, u32[]{:S(2)}, u32[]{:S(2)}) collective-permute-start(f32[1,8,8,4,128]{4,2,1,3,0:T(8,128)S(1)} %copy.39), channel_id=1, source_target_pairs={{0,8},{8,16},{16,24},{24,0},{1,9},{9,17},{17,25},{25,1},{2,10},{10... | collective-permute-start | bytes 393224 | tf_op jit(solution)/shard_map/ppermute | solution.py:24
  8.6 8.1 %collective-permute-start.3 = (f32[8,8,1,4,128]{4,2,1,3,0:T(1,128)S(1)}, f32[8,8,1,4,128]{4,2,1,3,0:T(1,128)S(1)}, u32[]{:S(2)}, u32[]{:S(2)}) collective-permute-start(f32[8,8,1,4,128]{4,2,1,3,0:T(1,128)S(1)} %get-tuple-element.7), channel_id=1, source_target_pairs={{0,3},{1,0},{2,1},{3,2},{4,7},{5,4},{6,5},{7,6},{8,11},{9,8},{10,9... | collective-permute-start | bytes 393224 | tf_op jit(solution)/shard_map/ppermute | solution.py:24
  12.2 5.4 %copy-start.1 = (f32[8,8,1,4,128]{4,2,1,3,0:T(1,128)}, f32[8,8,1,4,128]{4,2,1,3,0:T(1,128)S(1)}, u32[]{:S(2)}) copy-start(f32[8,8,1,4,128]{4,2,1,3,0:T(1,128)S(1)} %collective-permute-done.4) | copy-start | bytes 393220
  12.2 5.4 %copy-start.5 = (f32[1,8,8,4,128]{4,2,1,3,0:T(8,128)}, f32[1,8,8,4,128]{4,2,1,3,0:T(8,128)S(1)}, u32[]{:S(2)}) copy-start(f32[1,8,8,4,128]{4,2,1,3,0:T(8,128)S(1)} %collective-permute-done) | copy-start | bytes 393220
  16.7 1.0 %copy-start.3 = (f32[1,8,8,4,128]{4,2,1,3,0:T(8,128)}, f32[1,8,8,4,128]{4,2,1,3,0:T(8,128)S(1)}, u32[]{:S(2)}) copy-start(f32[1,8,8,4,128]{4,2,1,3,0:T(8,128)S(1)} %collective-permute-done.1) | copy-start | bytes 393220
  18.8 2.9 %collective-permute-start.9 = (f32[4,4,1,4,128]{4,2,1,3,0:T(1,128)S(1)}, f32[4,4,1,4,128]{4,2,1,3,0:T(1,128)S(1)}, u32[]{:S(2)}, u32[]{:S(2)}) collective-permute-start(f32[4,4,1,4,128]{4,2,1,3,0:T(1,128)S(1)} %get-tuple-element.24), channel_id=1, source_target_pairs={{0,3},{1,0},{2,1},{3,2},{4,7},{5,4},{6,5},{7,6},{8,11},{9,8},{10,9... | collective-permute-start | bytes 98312 | tf_op jit(solution)/shard_map/ppermute | solution.py:24
  18.9 12.7 %copy-start.21 = (f32[4,4]{1,0:T(4,128)S(1)}, f32[4,4]{1,0:T(4,128)}, u32[]{:S(2)}) copy-start(f32[4,4]{1,0:T(4,128)} %get-tuple-element.41) | copy-start | bytes 196
  18.9 12.7 %copy-start.22 = (f32[4,4]{1,0:T(4,128)S(1)}, f32[4,4]{1,0:T(4,128)}, u32[]{:S(2)}) copy-start(f32[4,4]{1,0:T(4,128)} %get-tuple-element.42) | copy-start | bytes 196
  18.9 4.6 %collective-permute-start.6 = (f32[4,2,4,4,128]{4,2,1,3,0:T(4,128)S(1)}, f32[4,2,4,4,128]{4,2,1,3,0:T(4,128)S(1)}, u32[]{:S(2)}, u32[]{:S(2)}) collective-permute-start(f32[4,2,4,4,128]{4,2,1,3,0:T(4,128)S(1)} %pad_maximum_fusion.53), channel_id=1, source_target_pairs={{0,4},{4,0},{1,5},{5,1},{2,6},{6,2},{3,7},{7,3},{8,12},{12,8},{9,1... | collective-permute-start | bytes 196616 | tf_op jit(solution)/shard_map/ppermute | solution.py:37
  19.5 3.4 %collective-permute-start.5 = (f32[4,4,1,4,128]{4,2,1,3,0:T(1,128)S(1)}, f32[4,4,1,4,128]{4,2,1,3,0:T(1,128)S(1)}, u32[]{:S(2)}, u32[]{:S(2)}) collective-permute-start(f32[4,4,1,4,128]{4,2,1,3,0:T(1,128)S(1)} %get-tuple-element.23), channel_id=1, source_target_pairs={{0,1},{1,2},{2,3},{3,0},{4,5},{5,6},{6,7},{7,4},{8,9},{9,10},{10,1... | collective-permute-start | bytes 98312 | tf_op jit(solution)/shard_map/ppermute | solution.py:24
  19.7 3.9 %collective-permute-start.8 = (f32[1,4,4,4,128]{4,2,1,3,0:T(4,128)S(1)}, f32[1,4,4,4,128]{4,2,1,3,0:T(4,128)S(1)}, u32[]{:S(2)}, u32[]{:S(2)}) collective-permute-start(f32[1,4,4,4,128]{4,2,1,3,0:T(4,128)S(1)} %get-tuple-element.26), channel_id=1, source_target_pairs={{0,24},{8,0},{16,8},{24,16},{1,25},{9,1},{17,9},{25,17},{2,26},{10... | collective-permute-start | bytes 98312 | tf_op jit(solution)/shard_map/ppermute | solution.py:24
  21.2 5.7 %collective-permute-start.7 = (f32[1,4,4,4,128]{4,2,1,3,0:T(4,128)S(1)}, f32[1,4,4,4,128]{4,2,1,3,0:T(4,128)S(1)}, u32[]{:S(2)}, u32[]{:S(2)}) collective-permute-start(f32[1,4,4,4,128]{4,2,1,3,0:T(4,128)S(1)} %get-tuple-element.25), channel_id=1, source_target_pairs={{0,8},{8,16},{16,24},{24,0},{1,9},{9,17},{17,25},{25,1},{2,10},{10... | collective-permute-start | bytes 98312 | tf_op jit(solution)/shard_map/ppermute | solution.py:24
  23.5 3.6 %copy-start.7 = (f32[6,1,4,4,128]{4,2,1,3,0:T(4,128)}, f32[6,1,4,4,128]{4,2,1,3,0:T(4,128)S(1)}, u32[]{:S(2)}) copy-start(f32[6,1,4,4,128]{4,2,1,3,0:T(4,128)S(1)} %pad.46) | copy-start | bytes 147460
  23.5 3.6 %copy-start.9 = (f32[6,1,4,4,128]{4,2,1,3,0:T(4,128)}, f32[6,1,4,4,128]{4,2,1,3,0:T(4,128)S(1)}, u32[]{:S(2)}) copy-start(f32[6,1,4,4,128]{4,2,1,3,0:T(4,128)S(1)} %pad.45) | copy-start | bytes 147460
  23.6 3.8 %copy-start.13 = (f32[1,4,4,4,128]{4,2,1,3,0:T(4,128)}, f32[1,4,4,4,128]{4,2,1,3,0:T(4,128)S(1)}, u32[]{:S(2)}) copy-start(f32[1,4,4,4,128]{4,2,1,3,0:T(4,128)S(1)} %collective-permute-done.8) | copy-start | bytes 98308
  26.9 15.6 %copy-start.15 = (f32[1,4,4,4,128]{4,2,1,3,0:T(4,128)}, f32[1,4,4,4,128]{4,2,1,3,0:T(4,128)S(1)}, u32[]{:S(2)}) copy-start(f32[1,4,4,4,128]{4,2,1,3,0:T(4,128)S(1)} %collective-permute-done.7) | copy-start | bytes 98308
  27.7 14.8 %copy-start.12 = (f32[2,2,2,4,128]{4,2,1,3,0:T(2,128)}, f32[2,2,2,4,128]{4,2,1,3,0:T(2,128)S(1)}, u32[]{:S(2)}) copy-start(f32[2,2,2,4,128]{4,2,1,3,0:T(2,128)S(1)} %add_multiply_fusion) | copy-start | bytes 49156
  27.7 7.3 %collective-permute-start.12 = (f32[10,2,2,4,128]{4,2,1,3,0:T(2,128)S(1)}, f32[10,2,2,4,128]{4,2,1,3,0:T(2,128)S(1)}, u32[]{:S(2)}, u32[]{:S(2)}) collective-permute-start(f32[10,2,2,4,128]{4,2,1,3,0:T(2,128)S(1)} %pad_maximum_fusion.52), channel_id=1, source_target_pairs={{0,8},{8,16},{16,24},{24,0},{1,9},{9,17},{17,25},{25,1},{2,10},{10... | collective-permute-start | bytes 245768 | tf_op jit(solution)/shard_map/ppermute | solution.py:24
  27.8 9.8 %collective-permute-start.11 = (f32[10,2,2,4,128]{4,2,1,3,0:T(2,128)S(1)}, f32[10,2,2,4,128]{4,2,1,3,0:T(2,128)S(1)}, u32[]{:S(2)}, u32[]{:S(2)}) collective-permute-start(f32[10,2,2,4,128]{4,2,1,3,0:T(2,128)S(1)} %pad_maximum_fusion.52), channel_id=1, source_target_pairs={{0,16},{8,24},{16,0},{24,8},{1,17},{9,25},{17,1},{25,9},{2,18},{10... | collective-permute-start | bytes 245768 | tf_op jit(solution)/shard_map/ppermute | solution.py:24
  28.5 9.1 %collective-permute-start.10 = (f32[10,2,2,4,128]{4,2,1,3,0:T(2,128)S(1)}, f32[10,2,2,4,128]{4,2,1,3,0:T(2,128)S(1)}, u32[]{:S(2)}, u32[]{:S(2)}) collective-permute-start(f32[10,2,2,4,128]{4,2,1,3,0:T(2,128)S(1)} %pad_maximum_fusion.52), channel_id=1, source_target_pairs={{0,24},{8,0},{16,8},{24,16},{1,25},{9,1},{17,9},{25,17},{2,26},{10... | collective-permute-start | bytes 245768 | tf_op jit(solution)/shard_map/ppermute | solution.py:24
  35.0 7.5 %copy-start.17 = (f32[2,2,2,4,128]{4,2,1,3,0:T(2,128)}, f32[2,2,2,4,128]{4,2,1,3,0:T(2,128)S(1)}, u32[]{:S(2)}) copy-start(f32[2,2,2,4,128]{4,2,1,3,0:T(2,128)S(1)} %slice.363) | copy-start | bytes 49156
  37.6 4.9 %copy-start.18 = (f32[2,2,2,4,128]{4,2,1,3,0:T(2,128)}, f32[2,2,2,4,128]{4,2,1,3,0:T(2,128)S(1)}, u32[]{:S(2)}) copy-start(f32[2,2,2,4,128]{4,2,1,3,0:T(2,128)S(1)} %slice.362) | copy-start | bytes 49156
  37.6 9.2 %copy-start.19 = (f32[2,2,2,4,128]{4,2,1,3,0:T(2,128)}, f32[2,2,2,4,128]{4,2,1,3,0:T(2,128)S(1)}, u32[]{:S(2)}) copy-start(f32[2,2,2,4,128]{4,2,1,3,0:T(2,128)S(1)} %slice.361) | copy-start | bytes 49156
  38.3 4.9 %collective-permute-start.19 = (f32[8,2,2,4,128]{4,2,1,3,0:T(2,128)}, f32[8,2,2,4,128]{4,2,1,3,0:T(2,128)S(1)}, u32[]{:S(2)}, u32[]{:S(2)}) collective-permute-start(f32[8,2,2,4,128]{4,2,1,3,0:T(2,128)} %pad_maximum_fusion.54), channel_id=1, source_target_pairs={{7,0},{4,1},{5,2},{6,3},{3,4},{0,5},{1,6},{2,7},{15,8},{12,9},{13,... | collective-permute-start | bytes 196616 | tf_op jit(solution)/shard_map/ppermute | solution.py:108
  38.3 6.1 %collective-permute-start.18 = (f32[8,2,2,4,128]{4,2,1,3,0:T(2,128)}, f32[8,2,2,4,128]{4,2,1,3,0:T(2,128)S(1)}, u32[]{:S(2)}, u32[]{:S(2)}) collective-permute-start(f32[8,2,2,4,128]{4,2,1,3,0:T(2,128)} %pad_maximum_fusion.54), channel_id=1, source_target_pairs={{6,0},{7,1},{4,2},{5,3},{2,4},{3,5},{0,6},{1,7},{14,8},{15,9},{12,... | collective-permute-start | bytes 196616 | tf_op jit(solution)/shard_map/ppermute | solution.py:108
  39.6 10.6 %collective-permute-start.17 = (f32[8,2,2,4,128]{4,2,1,3,0:T(2,128)}, f32[8,2,2,4,128]{4,2,1,3,0:T(2,128)}, u32[]{:S(2)}, u32[]{:S(2)}) collective-permute-start(f32[8,2,2,4,128]{4,2,1,3,0:T(2,128)} %pad_maximum_fusion.54), channel_id=1, source_target_pairs={{5,0},{6,1},{7,2},{4,3},{1,4},{2,5},{3,6},{0,7},{13,8},{14,9},{15,... | collective-permute-start | bytes 196616 | tf_op jit(solution)/shard_map/ppermute | solution.py:108
  42.0 8.3 %collective-permute-start.16 = (f32[8,2,2,4,128]{4,2,1,3,0:T(2,128)}, f32[8,2,2,4,128]{4,2,1,3,0:T(2,128)}, u32[]{:S(2)}, u32[]{:S(2)}) collective-permute-start(f32[8,2,2,4,128]{4,2,1,3,0:T(2,128)} %pad_maximum_fusion.54), channel_id=1, source_target_pairs={{4,0},{5,1},{6,2},{7,3},{0,4},{1,5},{2,6},{3,7},{12,8},{13,9},{14,... | collective-permute-start | bytes 196616 | tf_op jit(solution)/shard_map/ppermute | solution.py:108
  42.5 7.8 %collective-permute-start.15 = (f32[8,2,2,4,128]{4,2,1,3,0:T(2,128)}, f32[8,2,2,4,128]{4,2,1,3,0:T(2,128)}, u32[]{:S(2)}, u32[]{:S(2)}) collective-permute-start(f32[8,2,2,4,128]{4,2,1,3,0:T(2,128)} %pad_maximum_fusion.54), channel_id=1, source_target_pairs={{3,0},{0,1},{1,2},{2,3},{7,4},{4,5},{5,6},{6,7},{11,8},{8,9},{9,10... | collective-permute-start | bytes 196616 | tf_op jit(solution)/shard_map/ppermute | solution.py:108
  43.2 3.7 %copy-start.24 = (f32[8,2,2,4,128]{4,2,1,3,0:T(2,128)}, f32[8,2,2,4,128]{4,2,1,3,0:T(2,128)S(1)}, u32[]{:S(2)}) copy-start(f32[8,2,2,4,128]{4,2,1,3,0:T(2,128)S(1)} %collective-permute-done.19) | copy-start | bytes 196612
  43.2 7.1 %collective-permute-start.14 = (f32[8,2,2,4,128]{4,2,1,3,0:T(2,128)}, f32[8,2,2,4,128]{4,2,1,3,0:T(2,128)}, u32[]{:S(2)}, u32[]{:S(2)}) collective-permute-start(f32[8,2,2,4,128]{4,2,1,3,0:T(2,128)} %pad_maximum_fusion.54), channel_id=1, source_target_pairs={{2,0},{3,1},{0,2},{1,3},{6,4},{7,5},{4,6},{5,7},{10,8},{11,9},{8,1... | collective-permute-start | bytes 196616 | tf_op jit(solution)/shard_map/ppermute | solution.py:108
  45.0 5.3 %collective-permute-start.13 = (f32[8,2,2,4,128]{4,2,1,3,0:T(2,128)}, f32[8,2,2,4,128]{4,2,1,3,0:T(2,128)}, u32[]{:S(2)}, u32[]{:S(2)}) collective-permute-start(f32[8,2,2,4,128]{4,2,1,3,0:T(2,128)} %pad_maximum_fusion.54), channel_id=1, source_target_pairs={{1,0},{2,1},{3,2},{0,3},{5,4},{6,5},{7,6},{4,7},{9,8},{10,9},{11,1... | collective-permute-start | bytes 196616 | tf_op jit(solution)/shard_map/ppermute | solution.py:108
  50.2 1.9 %copy-start.8 = (f32[6,1,4,4,128]{4,2,1,3,0:T(4,128)S(1)}, f32[6,1,4,4,128]{4,2,1,3,0:T(4,128)}, u32[]{:S(2)}) copy-start(f32[6,1,4,4,128]{4,2,1,3,0:T(4,128)} %copy-done.7) | copy-start | bytes 147460
  50.2 1.9 %copy-start.10 = (f32[6,1,4,4,128]{4,2,1,3,0:T(4,128)S(1)}, f32[6,1,4,4,128]{4,2,1,3,0:T(4,128)}, u32[]{:S(2)}) copy-start(f32[6,1,4,4,128]{4,2,1,3,0:T(4,128)} %copy-done.9) | copy-start | bytes 147460
  50.2 1.9 %copy-start.14 = (f32[1,4,4,4,128]{4,2,1,3,0:T(4,128)S(1)}, f32[1,4,4,4,128]{4,2,1,3,0:T(4,128)}, u32[]{:S(2)}) copy-start(f32[1,4,4,4,128]{4,2,1,3,0:T(4,128)} %copy-done.13) | copy-start | bytes 98308
  50.2 1.9 %copy-start.16 = (f32[1,4,4,4,128]{4,2,1,3,0:T(4,128)S(1)}, f32[1,4,4,4,128]{4,2,1,3,0:T(4,128)}, u32[]{:S(2)}) copy-start(f32[1,4,4,4,128]{4,2,1,3,0:T(4,128)} %copy-done.15) | copy-start | bytes 98308
  52.7 5.6 %collective-permute-start.24 = (f32[4,4,1,4,128]{4,2,1,3,0:T(1,128)S(1)}, f32[4,4,1,4,128]{4,2,1,3,0:T(1,128)S(1)}, u32[]{:S(2)}, u32[]{:S(2)}) collective-permute-start(f32[4,4,1,4,128]{4,2,1,3,0:T(1,128)S(1)} %get-tuple-element.18), channel_id=1, source_target_pairs={{0,1},{1,2},{2,3},{3,0},{4,5},{5,6},{6,7},{7,4},{8,9},{9,10},{10,1... | collective-permute-start | bytes 98312 | tf_op jit(solution)/shard_map/ppermute | solution.py:24
  52.8 9.7 %collective-permute-start.22 = (f32[4,2,4,4,128]{4,2,1,3,0:T(4,128)S(1)}, f32[4,2,4,4,128]{4,2,1,3,0:T(4,128)S(1)}, u32[]{:S(2)}, u32[]{:S(2)}) collective-permute-start(f32[4,2,4,4,128]{4,2,1,3,0:T(4,128)S(1)} %pad_maximum_fusion.55), channel_id=1, source_target_pairs={{0,4},{4,0},{1,5},{5,1},{2,6},{6,2},{3,7},{7,3},{8,12},{12,8},{9,1... | collective-permute-start | bytes 196616 | tf_op jit(solution)/shard_map/ppermute | solution.py:37
  54.4 4.8 %collective-permute-start.20 = (f32[1,4,4,4,128]{4,2,1,3,0:T(4,128)S(1)}, f32[1,4,4,4,128]{4,2,1,3,0:T(4,128)S(1)}, u32[]{:S(2)}, u32[]{:S(2)}) collective-permute-start(f32[1,4,4,4,128]{4,2,1,3,0:T(4,128)S(1)} %get-tuple-element.20), channel_id=1, source_target_pairs={{0,24},{8,0},{16,8},{24,16},{1,25},{9,1},{17,9},{25,17},{2,26},{10... | collective-permute-start | bytes 98312 | tf_op jit(solution)/shard_map/ppermute | solution.py:24
  56.5 5.7 %collective-permute-start.21 = (f32[1,4,4,4,128]{4,2,1,3,0:T(4,128)S(1)}, f32[1,4,4,4,128]{4,2,1,3,0:T(4,128)S(1)}, u32[]{:S(2)}, u32[]{:S(2)}) collective-permute-start(f32[1,4,4,4,128]{4,2,1,3,0:T(4,128)S(1)} %get-tuple-element.19), channel_id=1, source_target_pairs={{0,8},{8,16},{16,24},{24,0},{1,9},{9,17},{17,25},{25,1},{2,10},{10... | collective-permute-start | bytes 98312 | tf_op jit(solution)/shard_map/ppermute | solution.py:24
  56.5 5.8 %collective-permute-start.23 = (f32[4,4,1,4,128]{4,2,1,3,0:T(1,128)S(1)}, f32[4,4,1,4,128]{4,2,1,3,0:T(1,128)S(1)}, u32[]{:S(2)}, u32[]{:S(2)}) collective-permute-start(f32[4,4,1,4,128]{4,2,1,3,0:T(1,128)S(1)} %get-tuple-element.17), channel_id=1, source_target_pairs={{0,3},{1,0},{2,1},{3,2},{4,7},{5,4},{6,5},{7,6},{8,11},{9,8},{10,9... | collective-permute-start | bytes 98312 | tf_op jit(solution)/shard_map/ppermute | solution.py:24
  58.3 3.9 %copy-start.4 = (f32[1,8,8,4,128]{4,2,1,3,0:T(8,128)S(1)}, f32[1,8,8,4,128]{4,2,1,3,0:T(8,128)}, u32[]{:S(2)}) copy-start(f32[1,8,8,4,128]{4,2,1,3,0:T(8,128)} %copy-done.3) | copy-start | bytes 393220
  (3 other events, 2.5 us)
